TPU v7x, 32 devices: a whole 2x2x4 slice. The times are simulated.
32 devices in a mesh: ctx: 8 (over y, x, core), uly: 4 (over z).
Axes of the slice: x: 2, y: 2, z: 4, core: 2. Of those that a mesh axis runs over, the one named last changes fastest.
Arguments:
- query_states: bfloat16 [1024, 2048], P(('ctx', 'uly')), may hold values from -8 to 8
- key_states: bfloat16 [1024, 2048], P(('ctx', 'uly')), may hold values from -8 to 8
- value_states: bfloat16 [1024, 2048], P(('ctx', 'uly')), may hold values from -6 to 6
- score_kernel: float32 [16, 6, 11], P('uly'), may hold values from -0.4 to 1.2
- head_mixing: float32 [16, 4], P('uly'), may hold values from 0.25 to 1
- head_gain: float32 [2048], P('uly'), may hold values from 0.5 to 1.5
Outputs:
- attended: bfloat16 [1024, 2048], P(('ctx', 'uly'))
All inputs are finite; a program needn't handle non-finite values.
Results may differ from a plain program's by a relative error of at most 0.0049.
Values may be sent and summed in bfloat16 or wider, within the bound.
No kernel may reach another device: no remote copies, remote signals or barrier semaphores. Data moves between devices by JAX's collectives and lax.ppermute only.
A program may use at most 64 MiB of HBM per device.

v0:
```python
import jax
import jax.numpy as jnp
from jax import lax
from jax.sharding import PartitionSpec as P

GROUP = 4
QCONV = 6
KCONV = 11


lowest = -1e30
epsilon = 1e-06


def passed_along(shard, axis, by):
    peers = lax.axis_size(axis)
    pairs = [(i, i + by) for i in range(peers) if 0 <= i + by < peers]
    return lax.ppermute(shard, axis, pairs)


def partner_2(shard, axis, bit):
    return lax.ppermute(shard, axis, [(i, i ^ 1 << bit) for i in range(lax.axis_size(axis))])


def unchanged(carried):
    return carried


def group_span(shard_count, shard_rows):
    span_size = 1
    while span_size * 2 * shard_rows <= 512 and shard_count % (span_size * 2) == 0:
        span_size = span_size * 2
    return span_size


def tile_logits(query_rows, query_first, key_rows, key_first, score_kernel):
    row_lead = QCONV - 1
    col_lead = KCONV - 1
    heads = score_kernel.shape[0]
    row_count = query_rows.shape[0] - row_lead
    span_size = key_rows.shape[0]
    padded_cols = key_rows.shape[1]
    col_count = padded_cols - col_lead
    query_heads = query_rows.reshape(query_rows.shape[0], heads, -1)
    key_heads = key_rows.reshape(span_size, padded_cols, heads, -1)
    dot_scores = jnp.einsum(
        "qhd,nkhd->nhqk", query_heads, key_heads, preferred_element_type=jnp.float32
    )
    dot_scores = dot_scores * query_heads.shape[2] ** (-0.5)
    query_pos = query_first - row_lead + lax.iota(jnp.int32, query_rows.shape[0])
    key_pos = (
        key_first
        - col_lead
        + col_count * lax.iota(jnp.int32, span_size)[:, None]
        + lax.iota(jnp.int32, padded_cols)[None, :]
    )
    inside = (
        (key_pos[:, None, :] <= query_pos[None, :, None])
        & (key_pos[:, None, :] >= 0)
        & (query_pos[None, :, None] >= 0)
    )
    dot_scores = jnp.where(inside[:, None], dot_scores, 0.0)
    convolved = jnp.zeros((span_size, heads, row_count, col_count), jnp.float32)
    for row_lag in range(QCONV):
        for col_lag in range(KCONV):
            window = dot_scores[
                :,
                :,
                row_lead - row_lag : row_lead - row_lag + row_count,
                col_lead - col_lag : col_lead - col_lag + col_count,
            ]
            convolved = convolved + score_kernel[None, :, row_lag, col_lag, None, None] * window
    causal = key_pos[:, None, col_lead:] <= query_pos[None, row_lead:, None]
    return jnp.where(causal[:, None], convolved, lowest)


def stats_block(query_block, key_rows, key_first, stats_pair, score_kernel):
    query_rows, query_first = query_block
    last_query = query_first + query_rows.shape[0] - QCONV

    def stats_compute(current):
        logits = tile_logits(query_rows, query_first, key_rows, key_first, score_kernel)
        running_max, running_sum = current
        fresh_max = jnp.maximum(running_max, jnp.max(logits, axis=(0, 3)))
        rescaled = running_sum * jnp.exp(running_max - fresh_max)
        return (
            fresh_max,
            rescaled + jnp.sum(jnp.exp(logits - fresh_max[None, :, :, None]), axis=(0, 3)),
        )

    return lax.cond(key_first <= last_query, stats_compute, unchanged, stats_pair)


def output_block(
    query_block, key_rows, value_rows, key_first, weighted, stats_pair, score_kernel, head_mixing
):
    query_rows, query_first = query_block
    last_query = query_first + query_rows.shape[0] - QCONV

    def output_compute(current):
        logits = tile_logits(query_rows, query_first, key_rows, key_first, score_kernel)
        running_max, running_sum = stats_pair
        probabilities = (
            jnp.exp(logits - running_max[None, :, :, None]) / running_sum[None, :, :, None]
        )
        span_size, heads, row_count, col_count = probabilities.shape
        grouped = probabilities.reshape(span_size, heads // GROUP, GROUP, row_count, col_count)
        weights = head_mixing.reshape(heads // GROUP, GROUP, GROUP)
        mixed_probs = jnp.zeros_like(grouped)
        for source in range(GROUP):
            mixed_probs = (
                mixed_probs + weights[None, :, :, source, None, None] * grouped[:, :, source, None]
            )
        mixed_probs = mixed_probs.reshape(probabilities.shape).astype(jnp.bfloat16)
        value_heads = value_rows.reshape(span_size, col_count, heads, -1)
        return current + jnp.einsum(
            "nhqk,nkhd->qhd", mixed_probs, value_heads, preferred_element_type=jnp.float32
        )

    return lax.cond(key_first <= last_query, output_compute, unchanged, weighted)


def stats_sweep(query_blocks, key_stack, stats_all, score_kernel):
    shard_rows = key_stack.shape[1] - (KCONV - 1)
    span_size = group_span(key_stack.shape[0], shard_rows)
    spans = key_stack.reshape((key_stack.shape[0] // span_size, span_size) + key_stack.shape[1:])

    def stats_advance(step_index, carried):
        key_rows = lax.dynamic_index_in_dim(spans, step_index, 0, keepdims=False)
        key_first = step_index * span_size * shard_rows
        return tuple(
            (
                stats_block(query_block, key_rows, key_first, stats_pair, score_kernel)
                for query_block, stats_pair in zip(query_blocks, carried)
            )
        )

    return lax.fori_loop(0, spans.shape[0], stats_advance, stats_all)


def output_sweep(
    query_blocks, key_stack, value_stack, weighted_all, stats_all, score_kernel, head_mixing
):
    shard_rows = value_stack.shape[1]
    span_size = group_span(key_stack.shape[0], shard_rows)
    key_spans = key_stack.reshape(
        (key_stack.shape[0] // span_size, span_size) + key_stack.shape[1:]
    )
    value_spans = value_stack.reshape(
        (value_stack.shape[0] // span_size, span_size) + value_stack.shape[1:]
    )

    def output_advance(step_index, carried):
        key_rows = lax.dynamic_index_in_dim(key_spans, step_index, 0, keepdims=False)
        value_rows = lax.dynamic_index_in_dim(value_spans, step_index, 0, keepdims=False)
        key_first = step_index * span_size * shard_rows
        return tuple(
            (
                output_block(
                    query_block,
                    key_rows,
                    value_rows,
                    key_first,
                    weighted,
                    stats_pair,
                    score_kernel,
                    head_mixing,
                )
                for query_block, weighted, stats_pair in zip(query_blocks, carried, stats_all)
            )
        )

    return lax.fori_loop(0, key_spans.shape[0], output_advance, weighted_all)


def normalize(weighted, gain_local):
    factor = lax.rsqrt(jnp.mean(weighted * weighted, axis=2, keepdims=True) + epsilon)
    return (
        (weighted * factor * gain_local[None]).astype(jnp.bfloat16).reshape(weighted.shape[0], -1)
    )


def shards(query_states, key_states, value_states, score_kernel, head_mixing, head_gain):
    query_local, key_local, value_local = (
        lax.all_to_all(query_states, "uly", split_axis=1, concat_axis=0, tiled=True),
        lax.all_to_all(key_states, "uly", split_axis=1, concat_axis=0, tiled=True),
        lax.all_to_all(value_states, "uly", split_axis=1, concat_axis=0, tiled=True),
    )
    shard_rows = query_local.shape[0]
    row_lead = QCONV - 1
    col_lead = KCONV - 1
    heads = score_kernel.shape[0]
    head_dim = query_local.shape[1] // heads
    ctx_count = lax.axis_size("ctx")
    ctx_place = lax.axis_index("ctx")
    tails = jnp.concatenate(
        [query_local[shard_rows - row_lead :], key_local[shard_rows - col_lead :]], axis=0
    )
    earlier = passed_along(tails, "ctx", 1)
    query_ext = jnp.concatenate([earlier[:row_lead], query_local], axis=0)
    key_ext = jnp.concatenate([earlier[row_lead:], key_local], axis=0)
    query_first = ctx_place * shard_rows
    half_rows = shard_rows // 2
    top_bit = ctx_count.bit_length() - 2
    far_rows = partner_2(query_ext[half_rows:], "ctx", top_bit)
    partner = jnp.where(
        ctx_place < ctx_count // 2, ctx_place + ctx_count // 2, ctx_place - ctx_count // 2
    )
    query_blocks = [
        (query_ext[: half_rows + row_lead], query_first),
        (far_rows, partner * shard_rows + half_rows),
    ]
    stats_all = tuple(
        (
            (
                jnp.full((heads, block_rows.shape[0] - row_lead), lowest, jnp.float32),
                jnp.zeros((heads, block_rows.shape[0] - row_lead), jnp.float32),
            )
            for block_rows, block_first in query_blocks
        )
    )
    weighted_all = tuple(
        (
            jnp.zeros((block_rows.shape[0] - row_lead, heads, head_dim), jnp.float32)
            for block_rows, block_first in query_blocks
        )
    )
    key_stack = key_ext[None]
    value_stack = value_local[None]
    stats_all = stats_sweep(
        query_blocks, lax.all_gather(key_stack, "ctx", axis=0, tiled=True), stats_all, score_kernel
    )
    weighted_all = output_sweep(
        query_blocks,
        lax.all_gather(key_stack, "ctx", axis=0, tiled=True),
        lax.all_gather(value_stack, "ctx", axis=0, tiled=True),
        weighted_all,
        stats_all,
        score_kernel,
        head_mixing,
    )
    gain_local = head_gain.reshape(heads, head_dim)
    finished = [normalize(weighted, gain_local) for weighted in weighted_all]
    returned = partner_2(finished[1], "ctx", top_bit)
    attended = jnp.concatenate([finished[0], returned], axis=0)
    return lax.all_to_all(attended, "uly", split_axis=0, concat_axis=1, tiled=True)


def solution(mesh):
    placed = (
        P(("ctx", "uly"), None),
        P(("ctx", "uly"), None),
        P(("ctx", "uly"), None),
        P("uly", None, None),
        P("uly", None),
        P("uly"),
    )
    return jax.shard_map(
        shards, mesh=mesh, in_specs=placed, out_specs=P(("ctx", "uly"), None), check_vma=False
    )
```

profile of v0, /device:TPU:0, one launch (start us, length us, event | category | flops | bytes accessed | tf_op | source)
XLA Modules:
  0.0 152.9 jit_solution(973212687336004941)
XLA Ops:
  6.5 1.6 %copy.144 = bf16[4,4,8,512]{3,2,0,1:T(8,128)(2,1)} copy(bf16[4,4,8,512]{3,2,1,0:T(8,128)(2,1)} %bitcast.667) | data formatting | bytes 262144 | tf_op jit(solution)/shard_map/all_to_all | solution.py:186
  8.1 6.4 %all-to-all-start.1 = ((bf16[32,4,512]{2,0,1:T(8,128)(2,1)}), bf16[32,4,512]{2,0,1:T(8,128)(2,1)S(1)}, u32[]{:S(2)}, u32[]{:S(2)}) async-start(bf16[32,4,512]{2,0,1:T(8,128)(2,1)} %bitcast.640), calls=%async_computation.1 | async-start | bytes 262144 | tf_op jit(solution)/shard_map/all_to_all | solution.py:186
  14.6 1.6 %copy.145 = bf16[4,4,8,512]{3,2,0,1:T(8,128)(2,1)} copy(bf16[4,4,8,512]{3,2,1,0:T(8,128)(2,1)} %bitcast.668) | data formatting | bytes 262144 | tf_op jit(solution)/shard_map/all_to_all | solution.py:185
  16.2 4.5 %all-to-all-done.1 = bf16[32,4,512]{2,0,1:T(8,128)(2,1)S(1)} async-done(((bf16[32,4,512]{2,0,1:T(8,128)(2,1)}), bf16[32,4,512]{2,0,1:T(8,128)(2,1)S(1)}, u32[]{:S(2)}, u32[]{:S(2)}) %all-to-all-start.1) | async-done | bytes 131104 | tf_op jit(solution)/shard_map/all_to_all | solution.py:186
  20.7 3.3 %all-to-all-start = ((bf16[32,4,512]{2,0,1:T(8,128)(2,1)}), bf16[32,4,512]{2,0,1:T(8,128)(2,1)S(1)}, u32[]{:S(2)}, u32[]{:S(2)}) async-start(bf16[32,4,512]{2,0,1:T(8,128)(2,1)} %bitcast.641), calls=%async_computation | async-start | bytes 262144 | tf_op jit(solution)/shard_map/all_to_all | solution.py:185
  24.1 5.8 %all-to-all-done = bf16[32,4,512]{2,0,1:T(8,128)(2,1)S(1)} async-done(((bf16[32,4,512]{2,0,1:T(8,128)(2,1)}), bf16[32,4,512]{2,0,1:T(8,128)(2,1)S(1)}, u32[]{:S(2)}, u32[]{:S(2)}) %all-to-all-start) | async-done | bytes 131104 | tf_op jit(solution)/shard_map/all_to_all | solution.py:185
  29.9 1.3 collective-permute-start
  31.2 0.8 collective-permute-done
  32.0 0.7 maximum_bitcast_fusion
  32.8 9.0 %all_to_all.73 = bf16[32,4,512]{2,0,1:T(8,128)(2,1)} all-to-all(bf16[32,4,512]{2,0,1:T(8,128)(2,1)S(1)} %bitcast.665), channel_id=1, replica_groups=mesh['ctx'=8,'uly'=4] {'uly'}, dimensions={1} | all-to-all | bytes 262144 | tf_op jit(solution)/shard_map/all_to_all | solution.py:187
  41.9 5.4 %collective-permute-start.1 = (bf16[69,512]{1,0:T(8,128)(2,1)S(1)}, bf16[69,512]{1,0:T(8,128)(2,1)S(1)}, u32[]{:S(2)}, u32[]{:S(2)}) collective-permute-start(bf16[69,512]{1,0:T(8,128)(2,1)S(1)} %get-tuple-element.1401), channel_id=1, source_target_pairs={{0,16},{4,20},{8,24},{12,28},{16,0},{20,4},{24,8},{28,12},{1,17},{... | collective-permute-start | bytes 211976 | tf_op jit(solution)/shard_map/ppermute | solution.py:22
  47.4 2.2 %collective-permute-done.1 = bf16[69,512]{1,0:T(8,128)(2,1)S(1)} collective-permute-done((bf16[69,512]{1,0:T(8,128)(2,1)S(1)}, bf16[69,512]{1,0:T(8,128)(2,1)S(1)}, u32[]{:S(2)}, u32[]{:S(2)}) %collective-permute-start.1) | collective-permute-done | bytes 70688 | tf_op jit(solution)/shard_map/ppermute | solution.py:22
  49.6 9.5 %all-gather.7.cloned.1.call-done = bf16[8,138,512]{2,1,0:T(8,128)(2,1)} async-done(((bf16[1,138,512]{2,1,0:T(8,128)(2,1)}), bf16[8,138,512]{2,1,0:T(8,128)(2,1)}) %all-gather.7.cloned.1.call-update) | async-done | bytes 1130512 | tf_op jit(solution)/shard_map/all_gather | solution.py:235
  59.1 34.9 %while.46 = (s32[]{:T(128)}, f32[4,64]{1,0:T(4,128)S(1)}, f32[4,64]{1,0:T(4,128)S(1)}, f32[4,64]{1,0:T(4,128)S(1)}, f32[4,64]{1,0:T(4,128)S(1)}, /*index=5*/s32[...) while((s32[]{:T(128)}, f32[4,64]{1,0:T(4,128)S(1)}, ...), condition=%wide.region_9.10_spmd, body=%wide.region_0.9_spmd.sunk | while | flops 114301904 | bytes 77811088 | solution.py:138
  59.1 1.1 dynamic-slice_bitcast_fusion.6
  60.2 10.9 %conditional.8 = ((f32[4,64]{1,0:T(4,128)S(1)}, f32[4,64]{1,0:T(4,128)S(1)})) conditional(s32[]{:T(128)} %convert_element_type.72, (f32[4,64]{1,0:T(4,128)S(1)}, f32[4,64]{1,0:T(4,128)S(1)}) %tuple.395, (s32[]{:T(128)}, s32[]{:T(128)}, f32[4,6,11]{0,2,1:T(8,128)S(1)}, bf16[4,138,512]{2,1,0:T(8,128)(2,1)S(1)}, bf16[69,512]{1,0:T(8,128)(2,1)S(1)}, ...), branch_computations={%region_1.1_spmd, %region_2.4_spmd} | conditional | flops 57150952 | bytes 38340128 | solution.py:91
  60.3 0.2 reshape.613
  60.6 0.1 and_and_fusion
  60.8 0.5 fusion.1
  61.7 9.2 %fusion.312 = (f32[4,64]{1,0:T(4,128)S(1)}, f32[4,4,64,128]{3,2,0,1:T(8,128)S(1)}) fusion(f32[4,4,69,138]{3,2,0,1:T(8,128)S(1)} %fusion.1, f32[4]{0:T(128)S(1)} %get-tuple-element.1270, f32[4]{0:T(128)S(1)} %get-tuple-element.1271, f32[4]{0:T(128)S(1)} %get-tuple-element.1272, f32[4]{0:T(128)S(1)} %get-tuple-element.1273, f32[4]{0:T(128)S(1)} %get-tuple-element.1274, ...), kind=kLoop, calls=%fused_computation.914 | loop fusion | flops 17432320 | bytes 35162144 | tf_op jit(solution)/shard_map/while/body/eval_jaxpr/cond/branch_1_fun/reduce_max | solution.py:84
  70.8 0.2 exponential_reduce_fusion
  71.1 10.9 %conditional.9 = ((f32[4,64]{1,0:T(4,128)S(1)}, f32[4,64]{1,0:T(4,128)S(1)})) conditional(s32[]{:T(128)} %convert_element_type.73, (f32[4,64]{1,0:T(4,128)S(1)}, f32[4,64]{1,0:T(4,128)S(1)}) %tuple.397, (s32[]{:T(128)}, s32[]{:T(128)}, f32[4,6,11]{0,2,1:T(8,128)S(1)}, bf16[4,138,512]{2,1,0:T(8,128)(2,1)S(1)}, bf16[69,512]{1,0:T(8,128)(2,1)S(1)}, ...), branch_computations={%region_5.5_spmd, %region_6.8_spmd} | conditional | flops 57150952 | bytes 38340128 | solution.py:91
  71.1 0.2 reshape.615
  71.5 0.1 and_and_fusion.1
  71.7 0.5 fusion.71
  72.5 9.2 %fusion.314 = (f32[4,64]{1,0:T(4,128)S(1)}, f32[4,4,64,128]{3,2,0,1:T(8,128)S(1)}) fusion(f32[4,4,69,138]{3,2,0,1:T(8,128)S(1)} %fusion.71, f32[4]{0:T(128)S(1)} %get-tuple-element.1336, f32[4]{0:T(128)S(1)} %get-tuple-element.1337, f32[4]{0:T(128)S(1)} %get-tuple-element.1338, f32[4]{0:T(128)S(1)} %get-tuple-element.1339, f32[4]{0:T(128)S(1)} %get-tuple-element.1340, ...), kind=kLoop, calls=%fused_computation.915 | loop fusion | flops 17432320 | bytes 35162144 | tf_op jit(solution)/shard_map/while/body/eval_jaxpr/cond/branch_1_fun/reduce_max | solution.py:84
  81.7 0.2 exponential_reduce_fusion.1
  82.0 1.1 dynamic-slice_bitcast_fusion.6
  83.2 10.9 %conditional.9 = ((f32[4,64]{1,0:T(4,128)S(1)}, f32[4,64]{1,0:T(4,128)S(1)})) conditional(s32[]{:T(128)} %convert_element_type.73, (f32[4,64]{1,0:T(4,128)S(1)}, f32[4,64]{1,0:T(4,128)S(1)}) %tuple.397, (s32[]{:T(128)}, s32[]{:T(128)}, f32[4,6,11]{0,2,1:T(8,128)S(1)}, bf16[4,138,512]{2,1,0:T(8,128)(2,1)S(1)}, bf16[69,512]{1,0:T(8,128)(2,1)S(1)}, ...), branch_computations={%region_5.5_spmd, %region_6.8_spmd} | conditional | flops 57150952 | bytes 38340128 | solution.py:91
  83.2 0.2 reshape.615
  83.5 0.1 and_and_fusion.1
  83.7 0.5 fusion.71
  84.6 9.2 %fusion.314 = (f32[4,64]{1,0:T(4,128)S(1)}, f32[4,4,64,128]{3,2,0,1:T(8,128)S(1)}) fusion(f32[4,4,69,138]{3,2,0,1:T(8,128)S(1)} %fusion.71, f32[4]{0:T(128)S(1)} %get-tuple-element.1336, f32[4]{0:T(128)S(1)} %get-tuple-element.1337, f32[4]{0:T(128)S(1)} %get-tuple-element.1338, f32[4]{0:T(128)S(1)} %get-tuple-element.1339, f32[4]{0:T(128)S(1)} %get-tuple-element.1340, ...), kind=kLoop, calls=%fused_computation.915 | loop fusion | flops 17432320 | bytes 35162144 | tf_op jit(solution)/shard_map/while/body/eval_jaxpr/cond/branch_1_fun/reduce_max | solution.py:84
  93.7 0.2 exponential_reduce_fusion.1
  94.1 36.3 %while.47 = (s32[]{:T(128)}, f32[64,4,128]{2,0,1:T(8,128)S(1)}, f32[64,4,128]{2,0,1:T(8,128)S(1)}, s32[]{:T(128)}, bf16[2,4,138,512]{3,2,1,0:T(8,128)(2,1)}, /*i...) while((s32[]{:T(128)}, f32[64,4,128]{2,0,1:T(8,128)S(1)}, ...), condition=%wide.region_15.16_spmd, body=%wide.region_10.15_spmd.sunk | while | flops 183310304 | bytes 86701888 | solution.py:173
  94.3 1.2 dynamic-slice_bitcast_fusion.7
  95.5 0.2 copy-done
  95.8 11.1 %conditional.10 = (f32[64,4,128]{2,0,1:T(8,128)S(1)}) conditional(s32[]{:T(128)} %convert_element_type.74, f32[64,4,128]{2,0,1:T(8,128)S(1)} %get-tuple-element.1670, (f32[4,4]{1,0:T(4,128)S(1)}, s32[]{:T(128)}, s32[]{:T(128)}, f32[4,6,11]{0,2,1:T(8,128)S(1)}, bf16[4,138,512]{2,1,0:T(8,128)(2,1)S(1)}, /*index=5*/bf16[69,512]{1,0:T(8,128)(2,1)S(1)}, ...), branch_computations={%region_11.11_spmd, %region_12.12_spmd} | conditional | flops 91655144 | bytes 40164048 | solution.py:120
  95.8 0.2 reshape.618
  96.1 0.1 and_and_fusion.2
  96.3 0.5 fusion.141
  97.2 9.0 %fusion.151 = f32[4,1,4,64,128]{4,3,0,2,1:T(8,128)S(1)} fusion(f32[4,4,69,138]{3,2,0,1:T(8,128)S(1)} %fusion.141, f32[4,64]{1,0:T(4,128)S(1)} %get-tuple-element.865, f32[4,64]{1,0:T(4,128)S(1)} %get-tuple-element.864, f32[4]{0:T(128)S(1)} %get-tuple-element.1134, f32[4]{0:T(128)S(1)} %get-tuple-element.1135, f32[4]{0:T(128)S(1)} %get-tuple-element.1136, ...), kind=kLoop, calls=%fused_computation.439 | loop fusion | flops 17563648 | bytes 35163168 | tf_op jit(solution)/shard_map/while/body/eval_jaxpr/cond/branch_1_fun/reshape | solution.py:107
  106.2 0.2 slice_reduce_fusion.3
  106.5 0.4 fusion.142
  106.8 11.0 %conditional.11 = (f32[64,4,128]{2,0,1:T(8,128)S(1)}) conditional(s32[]{:T(128)} %convert_element_type.75, f32[64,4,128]{2,0,1:T(8,128)S(1)} %get-tuple-element.1671, (f32[4,4]{1,0:T(4,128)S(1)}, s32[]{:T(128)}, s32[]{:T(128)}, f32[4,6,11]{0,2,1:T(8,128)S(1)}, bf16[4,138,512]{2,1,0:T(8,128)(2,1)S(1)}, /*index=5*/bf16[69,512]{1,0:T(8,128)(2,1)S(1)}, ...), branch_computations={%region_13.13_spmd, %region_14.14_spmd} | conditional | flops 91655144 | bytes 40164048 | solution.py:120
  106.8 0.2 reshape.623
  107.4 0.5 fusion.226
  108.2 9.0 %fusion.236 = f32[4,1,4,64,128]{4,3,0,2,1:T(8,128)S(1)} fusion(f32[4,4,69,138]{3,2,0,1:T(8,128)S(1)} %fusion.226, f32[4,64]{1,0:T(4,128)S(1)} %get-tuple-element.875, f32[4,64]{1,0:T(4,128)S(1)} %get-tuple-element.874, f32[4]{0:T(128)S(1)} %get-tuple-element.1204, f32[4]{0:T(128)S(1)} %get-tuple-element.1205, f32[4]{0:T(128)S(1)} %get-tuple-element.1206, ...), kind=kLoop, calls=%fused_computation.674 | loop fusion | flops 17563648 | bytes 35163168 | tf_op jit(solution)/shard_map/while/body/eval_jaxpr/cond/branch_1_fun/reshape | solution.py:107
  117.3 0.2 slice_reduce_fusion.7
  117.5 0.4 fusion.227
  117.9 1.2 dynamic-slice_bitcast_fusion.7
  119.1 0.2 copy-done
  119.4 11.0 %conditional.11 = (f32[64,4,128]{2,0,1:T(8,128)S(1)}) conditional(s32[]{:T(128)} %convert_element_type.75, f32[64,4,128]{2,0,1:T(8,128)S(1)} %get-tuple-element.1671, (f32[4,4]{1,0:T(4,128)S(1)}, s32[]{:T(128)}, s32[]{:T(128)}, f32[4,6,11]{0,2,1:T(8,128)S(1)}, bf16[4,138,512]{2,1,0:T(8,128)(2,1)S(1)}, /*index=5*/bf16[69,512]{1,0:T(8,128)(2,1)S(1)}, ...), branch_computations={%region_13.13_spmd, %region_14.14_spmd} | conditional | flops 91655144 | bytes 40164048 | solution.py:120
  119.4 0.2 reshape.623
  119.9 0.5 fusion.226
  120.8 9.0 %fusion.236 = f32[4,1,4,64,128]{4,3,0,2,1:T(8,128)S(1)} fusion(f32[4,4,69,138]{3,2,0,1:T(8,128)S(1)} %fusion.226, f32[4,64]{1,0:T(4,128)S(1)} %get-tuple-element.875, f32[4,64]{1,0:T(4,128)S(1)} %get-tuple-element.874, f32[4]{0:T(128)S(1)} %get-tuple-element.1204, f32[4]{0:T(128)S(1)} %get-tuple-element.1205, f32[4]{0:T(128)S(1)} %get-tuple-element.1206, ...), kind=kLoop, calls=%fused_computation.674 | loop fusion | flops 17563648 | bytes 35163168 | tf_op jit(solution)/shard_map/while/body/eval_jaxpr/cond/branch_1_fun/reshape | solution.py:107
  129.8 0.2 slice_reduce_fusion.7
  130.1 0.4 fusion.227
  130.4 0.1 multiply_reduce_fusion
  130.6 0.1 fusion.310
  130.8 1.5 collective-permute-start.2
  132.3 2.8 %collective-permute-done.2 = bf16[64,512]{1,0:T(8,128)(2,1)S(1)} collective-permute-done((bf16[64,512]{1,0:T(8,128)(2,1)S(1)}, bf16[64,512]{1,0:T(8,128)(2,1)S(1)}, u32[]{:S(2)}, u32[]{:S(2)}) %collective-permute-start.2) | collective-permute-done | bytes 65568 | tf_op jit(solution)/shard_map/ppermute | solution.py:22
  135.1 10.3 %all_to_all.74 = bf16[4,32,512]{2,1,0:T(8,128)(2,1)S(1)} all-to-all(bf16[4,32,512]{2,1,0:T(8,128)(2,1)S(1)} %bitcast.663), channel_id=1, replica_groups=mesh['ctx'=8,'uly'=4] {'uly'}, dimensions={0} | all-to-all | bytes 262144 | tf_op jit(solution)/shard_map/all_to_all | solution.py:246
  145.4 0.7 copy.113
  (130 shorter events, 3.9 us)
Async XLA Ops:
  6.5 26.3 %copy-start.2 = (bf16[32,2048]{1,0:T(8,128)(2,1)S(1)}, bf16[32,2048]{1,0:T(8,128)(2,1)}, u32[]{:S(2)}) copy-start(bf16[32,2048]{1,0:T(8,128)(2,1)} %param.20) | copy-start | bytes 393220
  8.1 39.2 %copy-start.3 = (f32[4,6,11]{2,0,1:T(4,128)S(1)}, f32[4,6,11]{2,0,1:T(4,128)}, u32[]{:S(2)}) copy-start(f32[4,6,11]{2,0,1:T(4,128)} %param.21) | copy-start | bytes 3172
  8.1 12.5 %all-to-all-start.1 = ((bf16[32,4,512]{2,0,1:T(8,128)(2,1)}), bf16[32,4,512]{2,0,1:T(8,128)(2,1)S(1)}, u32[]{:S(2)}, u32[]{:S(2)}) async-start(bf16[32,4,512]{2,0,1:T(8,128)(2,1)} %bitcast.640), calls=%async_computation.1 | async-start | bytes 262144 | tf_op jit(solution)/shard_map/all_to_all | solution.py:186
  20.7 9.2 %all-to-all-start = ((bf16[32,4,512]{2,0,1:T(8,128)(2,1)}), bf16[32,4,512]{2,0,1:T(8,128)(2,1)S(1)}, u32[]{:S(2)}, u32[]{:S(2)}) async-start(bf16[32,4,512]{2,0,1:T(8,128)(2,1)} %bitcast.641), calls=%async_computation | async-start | bytes 262144 | tf_op jit(solution)/shard_map/all_to_all | solution.py:185
  24.0 35.1 %all-gather.7.cloned.1.call-start = ((), (), s32[]{:S(2)}) async-start(), calls=%async_computation.5 | async-start | bytes 1327104 | tf_op jit(solution)/shard_map/all_gather | solution.py:235
  29.9 2.1 %collective-permute-start = (bf16[15,512]{1,0:T(8,128)(2,1)S(1)}, bf16[15,512]{1,0:T(8,128)(2,1)S(1)}, u32[]{:S(2)}, u32[]{:S(2)}) collective-permute-start(bf16[15,512]{1,0:T(8,128)(2,1)S(1)} %pad_maximum_fusion.2), channel_id=1, source_target_pairs={{0,4},{4,8},{8,12},{12,16},{16,20},{20,24},{24,28},{1,5},{5,9},{9,... | collective-permute-start | bytes 46088 | tf_op jit(solution)/shard_map/ppermute | solution.py:18
  32.8 61.3 %all-gather.5.cloned.1.call-start = ((), (), s32[]{:S(2)}) async-start(), calls=%async_computation.4 | async-start | bytes 1179648 | tf_op jit(solution)/shard_map/all_gather | solution.py:236
  41.9 7.7 %collective-permute-start.1 = (bf16[69,512]{1,0:T(8,128)(2,1)S(1)}, bf16[69,512]{1,0:T(8,128)(2,1)S(1)}, u32[]{:S(2)}, u32[]{:S(2)}) collective-permute-start(bf16[69,512]{1,0:T(8,128)(2,1)S(1)} %get-tuple-element.1401), channel_id=1, source_target_pairs={{0,16},{4,20},{8,24},{12,28},{16,0},{20,4},{24,8},{28,12},{1,17},{... | collective-permute-start | bytes 211976 | tf_op jit(solution)/shard_map/ppermute | solution.py:22
  59.1 35.0 %copy-start.1 = (f32[4,4]{1,0:T(4,128)S(1)}, f32[4,4]{1,0:T(4,128)}, u32[]{:S(2)}) copy-start(f32[4,4]{1,0:T(4,128)} %param.22) | copy-start | bytes 196
  94.1 36.5 %copy-start.4 = (f32[512]{0:T(512)S(1)}, f32[512]{0:T(512)}, u32[]{:S(2)}) copy-start(f32[512]{0:T(512)} %param.23) | copy-start | bytes 6148
  94.3 1.4 copy-start
  117.9 1.4 copy-start
  130.8 4.3 %collective-permute-start.2 = (bf16[64,512]{1,0:T(8,128)(2,1)S(1)}, bf16[64,512]{1,0:T(8,128)(2,1)S(1)}, u32[]{:S(2)}, u32[]{:S(2)}) collective-permute-start(bf16[64,512]{1,0:T(8,128)(2,1)S(1)} %bitcast.670), channel_id=1, source_target_pairs={{0,16},{4,20},{8,24},{12,28},{16,0},{20,4},{24,8},{28,12},{1,17},{... | collective-permute-start | bytes 196616 | tf_op jit(solution)/shard_map/ppermute | solution.py:22
Sparse Core Ops, SparseCore 0:
  32.9 26.1 all-gather.6
  61.0 23.6 all-gather.4
where the time goes:
time: 154 us; the launch traced here: 153 us
  other arithmetic  58.6 us (38%)
  waiting for transfers between devices  25.7 us (17%)
  blocking collectives  19.3 us (13%)
  starting transfers between devices  18 us (12%)
  between operations  13.6 us (9%)
  local copies, waits for them, and re-layouts  12.4 us (8%)
  matrix products  4.27 us (3%)
    reduce_max x3, other arithmetic, stats_compute(): fresh_max = jnp.maximum(running_max, jnp.max(logits, axis=(0, 3)))  27.5 us
    reshape x3, other arithmetic, output_compute(): probabilities.reshape(span_size, heads // GROUP, GROUP, row_count, col_co...  27 us
    all_to_all x1, blocking collectives, shards(): lax.all_to_all(attended, 'uly', split_axis=0, concat_axis=1, tiled=True)  10.3 us
    all_gather x1, waiting for transfers between devices, shards(): lax.all_gather(key_stack, 'ctx', axis=0, tiled=True)  9.46 us
    all_to_all x1, blocking collectives, shards(): lax.all_to_all(value_states, 'uly', split_axis=1, concat_axis=0, tiled=True)  9.01 us
    ppermute x2, starting transfers between devices, partner_2(): lax.ppermute(shard, axis, [(i, i ^ 1 << bit) for i in range(lax.axis_size...  6.88 us
    all_to_all x1, starting transfers between devices, shards(): lax.all_to_all(key_states, 'uly', split_axis=1, concat_axis=0, tiled=True)  6.45 us
    all_to_all x1, waiting for transfers between devices, shards(): lax.all_to_all(query_states, 'uly', split_axis=1, concat_axis=0, tiled=True)  5.82 us
  transfers between devices with their start and end apart: 7, of which 6 were waited for; matrix products, arithmetic and copies ran while one was open for 24% of the time, Pallas kernels for 0%

commit v1 on v0

v1 whole, which is shorter than its diff:
```python
import jax
import jax.numpy as jnp
from jax import lax
from jax.sharding import PartitionSpec as P

GROUP = 4
QCONV = 6
KCONV = 11
KEY_BLOCK = 128
ROW_CHUNK = 128
KEY_GROUP = 8


lowest = -1e30
epsilon = 1e-06


def passed_along(shard, axis, by):
    peers = lax.axis_size(axis)
    pairs = [(i, i + by) for i in range(peers) if 0 <= i + by < peers]
    return lax.ppermute(shard, axis, pairs)


def split_bf16(values):
    high = lax.reduce_precision(values, exponent_bits=8, mantissa_bits=7)
    low = values - high
    return high.astype(jnp.bfloat16), low.astype(jnp.bfloat16)


def toeplitz_terms(score_kernel, head_dim):
    col_lead = KCONV - 1
    scaled = score_kernel * head_dim ** (-0.5)
    lag = (
        lax.iota(jnp.int32, KEY_BLOCK)[:, None]
        + col_lead
        - lax.iota(jnp.int32, KEY_BLOCK + col_lead)[None, :]
    )
    toeplitz = jnp.zeros(score_kernel.shape[:2] + lag.shape, jnp.float32)
    for col_lag in range(KCONV):
        toeplitz = jnp.where(lag == col_lag, scaled[:, :, col_lag, None, None], toeplitz)
    return split_bf16(toeplitz)


def convolved_keys(key_windows, terms):
    high, low = terms
    heads = high.shape[0]
    key_heads = key_windows.reshape(key_windows.shape[:2] + (heads, -1))
    conv_keys = jnp.einsum(
        "harc,nchd->nhard", high, key_heads, preferred_element_type=jnp.float32
    ) + jnp.einsum("harc,nchd->nhard", low, key_heads, preferred_element_type=jnp.float32)
    return split_bf16(conv_keys)


def band_terms(query_rows, query_first, key_flat, score_kernel):
    row_lead = QCONV - 1
    heads = score_kernel.shape[0]
    ext_count = query_rows.shape[0]
    row_count = ext_count - row_lead
    near = lax.dynamic_slice_in_dim(key_flat, query_first + 4, ext_count + QCONV - 2, 0)
    query_heads = query_rows.reshape(ext_count, heads, -1).astype(jnp.float32)
    near_heads = near.reshape(near.shape[0], heads, -1).astype(jnp.float32)
    scale = query_heads.shape[2] ** (-0.5)
    diagonals = [
        jnp.sum(query_heads * near_heads[lag - 1 : lag - 1 + ext_count], axis=2) * scale
        for lag in range(1, QCONV)
    ]
    band = []
    for gap in range(QCONV - 1):
        acc = jnp.zeros((row_count, heads), jnp.float32)
        for row_lag in range(gap + 1, QCONV):
            for col_lag in range(row_lag - gap):
                lag = row_lag - col_lag - gap
                acc = acc - score_kernel[None, :, row_lag, col_lag] * diagonals[lag - 1][
                    row_lead - row_lag : row_lead - row_lag + row_count
                ]
        band.append(acc.T)
    return jnp.stack(band)


def group_logits(shifted, key_windows, terms):
    keys_high, keys_low = convolved_keys(key_windows, terms)
    return jnp.einsum(
        "ihad,nhard->hinr", shifted, keys_high, preferred_element_type=jnp.float32
    ) + jnp.einsum("ihad,nhard->hinr", shifted, keys_low, preferred_element_type=jnp.float32)


def attend_chunk(shifted, band, query_first, key_windows, terms, value_heads, head_mixing):
    row_count, heads = shifted.shape[:2]
    seq_len = value_heads.shape[0]
    window_count = key_windows.shape[0]
    if window_count <= KEY_GROUP:
        convolved = group_logits(shifted, key_windows, terms)
    else:
        grouped_windows = key_windows.reshape(
            (window_count // KEY_GROUP, KEY_GROUP) + key_windows.shape[1:]
        )
        convolved = lax.map(lambda windows: group_logits(shifted, windows, terms), grouped_windows)
        convolved = jnp.moveaxis(convolved, 0, 2)
    convolved = convolved.reshape(heads, row_count, seq_len)
    query_pos = query_first + lax.iota(jnp.int32, row_count)
    gap = query_pos[:, None] - lax.iota(jnp.int32, seq_len)[None, :]
    for lag in range(QCONV - 1):
        convolved = convolved + jnp.where(gap == lag, band[lag][:, :, None], 0.0)
    logits = jnp.where(gap >= 0, convolved, lowest)
    peak = jnp.max(logits, axis=2, keepdims=True)
    expd = jnp.exp(logits - peak)
    probabilities = expd / jnp.sum(expd, axis=2, keepdims=True)
    grouped = probabilities.reshape(heads // GROUP, GROUP, row_count, seq_len)
    weights = head_mixing.reshape(heads // GROUP, GROUP, GROUP)
    mixed_probs = jnp.zeros_like(grouped)
    for source in range(GROUP):
        mixed_probs = mixed_probs + weights[:, :, source, None, None] * grouped[:, source, None]
    mixed_probs = mixed_probs.reshape(heads, row_count, seq_len).astype(jnp.bfloat16)
    return jnp.einsum(
        "hik,khd->ihd", mixed_probs, value_heads, preferred_element_type=jnp.float32
    )


def normalize(weighted, gain_local):
    factor = lax.rsqrt(jnp.mean(weighted * weighted, axis=2, keepdims=True) + epsilon)
    return (
        (weighted * factor * gain_local[None]).astype(jnp.bfloat16).reshape(weighted.shape[0], -1)
    )


def shards(query_states, key_states, value_states, score_kernel, head_mixing, head_gain):
    query_local, key_local, value_local = (
        lax.all_to_all(query_states, "uly", split_axis=1, concat_axis=0, tiled=True),
        lax.all_to_all(key_states, "uly", split_axis=1, concat_axis=0, tiled=True),
        lax.all_to_all(value_states, "uly", split_axis=1, concat_axis=0, tiled=True),
    )
    shard_rows = query_local.shape[0]
    width = query_local.shape[1]
    row_lead = QCONV - 1
    col_lead = KCONV - 1
    heads = score_kernel.shape[0]
    head_dim = width // heads
    ctx_place = lax.axis_index("ctx")
    query_first = ctx_place * shard_rows
    earlier = passed_along(query_local[shard_rows - row_lead :], "ctx", 1)
    query_ext = jnp.concatenate([earlier, query_local], axis=0)
    key_all = lax.all_gather(key_local, "ctx", axis=0, tiled=True)
    value_all = lax.all_gather(value_local, "ctx", axis=0, tiled=True)
    seq_len = key_all.shape[0]
    key_pad = jnp.concatenate([jnp.zeros((col_lead, width), key_all.dtype), key_all], axis=0)
    key_windows = jnp.stack(
        [
            key_pad[start : start + KEY_BLOCK + col_lead]
            for start in range(0, seq_len, KEY_BLOCK)
        ]
    )
    terms = toeplitz_terms(score_kernel, head_dim)
    edge = jnp.zeros((8, width), key_all.dtype)
    key_flat = jnp.concatenate([edge, key_all, edge], axis=0)
    band = band_terms(query_ext, query_first, key_flat, score_kernel)
    query_heads = query_ext.reshape(shard_rows + row_lead, heads, head_dim)
    shifted = jnp.stack(
        [query_heads[row_lead - lag : row_lead - lag + shard_rows] for lag in range(QCONV)], axis=2
    )
    value_heads = value_all.reshape(seq_len, heads, head_dim)
    chunk = min(ROW_CHUNK * KEY_BLOCK * 8 // seq_len, shard_rows)
    if chunk == shard_rows:
        weighted = attend_chunk(
            shifted, band, query_first, key_windows, terms, value_heads, head_mixing
        )
    else:
        chunks = shard_rows // chunk

        def one_chunk(index):
            start = index * chunk
            return attend_chunk(
                lax.dynamic_slice_in_dim(shifted, start, chunk, 0),
                lax.dynamic_slice_in_dim(band, start, chunk, 2),
                query_first + start,
                key_windows,
                terms,
                value_heads,
                head_mixing,
            )

        weighted = lax.map(one_chunk, jnp.arange(chunks, dtype=jnp.int32))
        weighted = weighted.reshape((shard_rows,) + weighted.shape[2:])
    gain_local = head_gain.reshape(heads, head_dim)
    attended = normalize(weighted, gain_local)
    return lax.all_to_all(attended, "uly", split_axis=0, concat_axis=1, tiled=True)


def solution(mesh):
    placed = (
        P(("ctx", "uly"), None),
        P(("ctx", "uly"), None),
        P(("ctx", "uly"), None),
        P("uly", None, None),
        P("uly", None),
        P("uly"),
    )
    return jax.shard_map(
        shards, mesh=mesh, in_specs=placed, out_specs=P(("ctx", "uly"), None), check_vma=False
    )
```

time: 154 us -> 129 us (0.84)
  other arithmetic: 58.6 us -> 8.16 us
  matrix products: 4.27 us -> 36.7 us
  local copies, waits for them, and re-layouts: 12.4 us -> 34.2 us
  waiting for transfers between devices: 25.7 us -> 9.09 us
  blocking collectives: 19.3 us -> 8.88 us
  starting transfers between devices: 18 us -> 16 us
    dot_general x9 -> x5, matrix products: 4.27 us -> 36.7 us  [the longest x1 10.8 us: group_logits(): jnp.einsum('ihad,nhard->hinr', shifted, keys_low, preferred_element_type=...]
    reduce_max x3 -> x0, other arithmetic: 27.5 us -> none  [stats_compute(): fresh_max = jnp.maximum(running_max, jnp.max(logits, axis=(0, 3)))]
    reshape x3 -> x0, other arithmetic: 27 us -> none  [output_compute(): probabilities.reshape(span_size, heads // GROUP, GROUP, row_count, col_co...]
    slice x19 -> x28, local copies, waits for them, and re-layouts: 1.53 us -> 14.1 us  [the longest x12 7.05 us: toeplitz_terms(): scaled[:, :, col_lag, None, None]]
    all_gather x2, waiting for transfers between devices: 9.48 us -> 0.02 us  [the longest x1 0.02 us: shards(): value_all = lax.all_gather(value_local, 'ctx', axis=0, tiled=True)]
    all_to_all x1 -> x0, blocking collectives: 9.01 us -> none  [shards(): lax.all_to_all(value_states, 'uly', split_axis=1, concat_axis=0, tiled=True)]
    ppermute x2 -> x0, starting transfers between devices: 6.88 us -> none  [partner_2(): lax.ppermute(shard, axis, [(i, i ^ 1 << bit) for i in range(lax.axis_size...]
    all_to_all x1, waiting for transfers between devices: 5.82 us -> 0.01 us  [shards(): lax.all_to_all(query_states, 'uly', split_axis=1, concat_axis=0, tiled=True)]
  transfers between devices with their start and end apart: 7 -> 6, of which waited for: 6 -> 2; matrix products, arithmetic and copies ran while one was open for 24% -> 57% of each run, Pallas kernels for 0% -> 0%
where the time goes in v1:
time: 129 us; the launch traced here: 128 us
  matrix products  36.7 us (28%)
  local copies, waits for them, and re-layouts  34.2 us (27%)
  starting transfers between devices  16 us (12%)
  between operations  14.5 us (11%)
  waiting for transfers between devices  9.09 us (7%)
  blocking collectives  8.88 us (7%)
  other arithmetic  8.16 us (6%)
    dot_general x1, matrix products, group_logits(): jnp.einsum('ihad,nhard->hinr', shifted, keys_low, preferred_element_type=...  10.8 us
    dot_general x1, matrix products, group_logits(): jnp.einsum('ihad,nhard->hinr', shifted, keys_high, preferred_element_type...  10.4 us
    all_to_all x1, blocking collectives, shards(): lax.all_to_all(attended, 'uly', split_axis=0, concat_axis=1, tiled=True)  8.88 us
    dot_general x1, matrix products, convolved_keys(): jnp.einsum('harc,nchd->nhard', low, key_heads, preferred_element_type=jnp...  7.5 us
    dot_general x1, matrix products, convolved_keys(): jnp.einsum('harc,nchd->nhard', high, key_heads, preferred_element_type=jn...  7.16 us
    slice x12, local copies, waits for them, and re-layouts, toeplitz_terms(): scaled[:, :, col_lag, None, None]  7.05 us
    all_to_all x1, starting transfers between devices, shards(): lax.all_to_all(key_states, 'uly', split_axis=1, concat_axis=0, tiled=True)  6.32 us
    all_to_all x1, starting transfers between devices, shards(): lax.all_to_all(value_states, 'uly', split_axis=1, concat_axis=0, tiled=True)  5.04 us
  transfers between devices with their start and end apart: 6, of which 2 were waited for; matrix products, arithmetic and copies ran while one was open for 57% of the time, Pallas kernels for 0%

profile of v1, /device:TPU:0, one launch (start us, length us, event | category | flops | bytes accessed | tf_op | source)
XLA Modules:
  0.0 127.6 jit_solution(4574001588323531412)
XLA Ops:
  6.5 1.6 %copy.233 = bf16[4,4,8,512]{3,2,0,1:T(8,128)(2,1)} copy(bf16[4,4,8,512]{3,2,1,0:T(8,128)(2,1)} %bitcast.136) | data formatting | bytes 262144 | tf_op jit(solution)/shard_map/all_to_all | solution.py:129
  8.1 6.3 %all-to-all-start.1 = ((bf16[32,4,512]{2,0,1:T(8,128)(2,1)}), bf16[32,4,512]{2,0,1:T(8,128)(2,1)S(1)}, u32[]{:S(2)}, u32[]{:S(2)}) async-start(bf16[32,4,512]{2,0,1:T(8,128)(2,1)} %bitcast.121), calls=%async_computation.1 | async-start | bytes 262144 | tf_op jit(solution)/shard_map/all_to_all | solution.py:129
  14.4 1.6 %copy.234 = bf16[4,4,8,512]{3,2,0,1:T(8,128)(2,1)} copy(bf16[4,4,8,512]{3,2,1,0:T(8,128)(2,1)} %bitcast.137) | data formatting | bytes 262144 | tf_op jit(solution)/shard_map/all_to_all | solution.py:128
  16.0 4.5 %all-to-all-done.1 = bf16[32,4,512]{2,0,1:T(8,128)(2,1)S(1)} async-done(((bf16[32,4,512]{2,0,1:T(8,128)(2,1)}), bf16[32,4,512]{2,0,1:T(8,128)(2,1)S(1)}, u32[]{:S(2)}, u32[]{:S(2)}) %all-to-all-start.1) | async-done | bytes 131104 | tf_op jit(solution)/shard_map/all_to_all | solution.py:129
  20.5 3.3 %all-to-all-start = ((bf16[32,4,512]{2,0,1:T(8,128)(2,1)}), bf16[32,4,512]{2,0,1:T(8,128)(2,1)S(1)}, u32[]{:S(2)}, u32[]{:S(2)}) async-start(bf16[32,4,512]{2,0,1:T(8,128)(2,1)} %bitcast.122), calls=%async_computation | async-start | bytes 262144 | tf_op jit(solution)/shard_map/all_to_all | solution.py:128
  23.9 0.7 all-gather.3.cloned.1.call-update
  24.6 0.7 broadcast_multiply_fusion
  25.5 0.7 copy.182
  26.2 0.7 copy.183
  26.9 0.6 copy.184
  27.5 0.6 copy.185
  28.2 0.7 copy.186
  28.9 0.7 copy.187
  29.6 0.7 copy.188
  30.3 0.7 copy.189
  31.0 0.7 copy.190
  31.6 0.7 copy.191
  32.3 1.6 %copy.232 = bf16[4,4,8,512]{3,2,0,1:T(8,128)(2,1)} copy(bf16[4,4,8,512]{3,2,1,0:T(8,128)(2,1)} %bitcast.138) | data formatting | bytes 262144 | tf_op jit(solution)/shard_map/all_to_all | solution.py:130
  33.9 1.7 %slice_reduce_fusion.18 = (f32[4]{0:T(128)}, f32[4]{0:T(128)}, f32[4]{0:T(128)}, f32[4]{0:T(128)}) fusion(f32[1,4,4]{2,1,0:T(4,128)} %bitcast.161), kind=kLoop, calls=%fused_computation.211 | loop fusion | bytes 128 | tf_op jit(solution)/shard_map/slice | solution.py:112
  35.6 1.9 %slice_reduce_fusion.17 = (f32[4]{0:T(128)}, f32[4]{0:T(128)}, f32[4]{0:T(128)}, f32[4]{0:T(128)}, f32[4]{0:T(128)}, /*index=5*/f32[4]{0:T(128)}, f32[4]{0:T(128...) fusion(f32[4,6,11]{2,0,1:T(4,128)} %param.9), kind=kLoop, calls=%fused_computation.210 | loop fusion | bytes 480 | tf_op jit(solution)/shard_map/slice | solution.py:73
  37.5 1.2 fusion.84
  38.7 0.6 subtract_compare_fusion.5
  39.3 0.8 fusion.108
  40.1 5.0 %all-to-all-start.2 = ((bf16[32,4,512]{2,0,1:T(8,128)(2,1)}), bf16[32,4,512]{2,0,1:T(8,128)(2,1)S(1)}, u32[]{:S(2)}, u32[]{:S(2)}) async-start(bf16[32,4,512]{2,0,1:T(8,128)(2,1)} %bitcast.120), calls=%async_computation.2 | async-start | bytes 262144 | tf_op jit(solution)/shard_map/all_to_all | solution.py:130
  45.1 1.3 %collective-permute-start = (bf16[5,512]{1,0:T(8,128)(2,1)S(1)}, bf16[5,512]{1,0:T(8,128)(2,1)S(1)}, u32[]{:S(2)}, u32[]{:S(2)}) collective-permute-start(bf16[5,512]{1,0:T(8,128)(2,1)S(1)} %slice.339), channel_id=1, source_target_pairs={{0,4},{4,8},{8,12},{12,16},{16,20},{20,24},{24,28},{1,5},{5,9},{9,... | collective-permute-start | bytes 15368 | tf_op jit(solution)/shard_map/ppermute | solution.py:21
  46.5 0.7 concatenate.20
  47.1 3.9 %all-to-all-done.2 = bf16[32,4,512]{2,0,1:T(8,128)(2,1)S(1)} async-done(((bf16[32,4,512]{2,0,1:T(8,128)(2,1)}), bf16[32,4,512]{2,0,1:T(8,128)(2,1)S(1)}, u32[]{:S(2)}, u32[]{:S(2)}) %all-to-all-start.2) | async-done | bytes 131104 | tf_op jit(solution)/shard_map/all_to_all | solution.py:130
  51.0 0.7 copy-done.1
  51.7 0.1 pad_maximum_fusion.1
  52.0 0.1 copy.167
  52.2 0.1 copy.168
  52.5 0.1 copy.169
  52.6 0.1 copy.164
  52.8 0.1 copy.170
  52.9 0.1 copy.165
  53.0 0.1 copy.171
  53.3 0.6 concatenate.19
  53.9 2.3 %fusion.127 = (bf16[138,512]{1,0:T(8,128)(2,1)S(1)}, bf16[138,512]{1,0:T(8,128)(2,1)S(1)}, bf16[138,512]{1,0:T(8,128)(2,1)S(1)}, bf16[138,512]{1,0:T(8,128)(2,1)...) fusion(bf16[1024,512]{1,0:T(8,128)(2,1)} %all-gather.3.cloned.1, ...), kind=kLoop, calls=%fused_computation.217 | loop fusion | bytes 3211264 | tf_op jit(solution)/shard_map/slice | solution.py:148
  56.3 0.7 stack.55
  57.0 0.9 copy_dynamic-update-slice_fusion.7
  57.9 1.6 %stack.56 = bf16[1,138,4,128]{3,2,1,0:T(4,128)(2,1)} reshape(bf16[138,512]{1,0:T(8,128)(2,1)} %get-tuple-element.39) | data formatting | bytes 282624 | tf_op jit(solution)/shard_map/stack | solution.py:146
  59.5 1.6 %stack.57 = bf16[1,138,4,128]{3,2,1,0:T(4,128)(2,1)} reshape(bf16[138,512]{1,0:T(8,128)(2,1)} %get-tuple-element.38) | data formatting | bytes 282624 | tf_op jit(solution)/shard_map/stack | solution.py:146
  61.1 0.7 stack.58
  62.0 1.0 copy_dynamic-update-slice_fusion.6
  62.9 1.0 copy_dynamic-update-slice_fusion.5
  63.9 1.0 copy_dynamic-update-slice_fusion.4
  65.2 7.5 %fusion.15 = f32[4,8,128,6,128]{4,2,3,1,0:T(8,128)} fusion(bf16[8,138,4,128]{3,1,0,2:T(8,128)(2,1)S(1)} %copy_dynamic-update-slice_fusion, f32[4,6]{1,0:T(4,128)} %bitcast.159, f32[4,6]{1,0:T(4,128)} %bitcast.157, f32[4,6]{1,0:T(4,128)} %bitcast.155, f32[4,6]{1,0:T(4,128)} %bitcast.153, f32[4,6]{1,0:T(4,128)} %bitcast.151, f32[4,6]{1,0:T(4,128)} %bitcast.149, ...), kind=kOutput, calls=%fused_computation.30 | convolution fusion | flops 874156032 | bytes 13908768 | tf_op jit(solution)/shard_map/harc,nchd->nhard/dot_general | solution.py:50
  72.9 7.2 %fusion.17 = f32[4,8,128,6,128]{4,2,3,1,0:T(8,128)} fusion(bf16[8,138,4,128]{3,1,0,2:T(8,128)(2,1)S(1)} %copy_dynamic-update-slice_fusion, f32[4,6]{1,0:T(4,128)S(1)} %bitcast.160, f32[4,6]{1,0:T(4,128)S(1)} %bitcast.158, f32[4,6]{1,0:T(4,128)S(1)} %bitcast.156, f32[4,6]{1,0:T(4,128)S(1)} %bitcast.154, f32[4,6]{1,0:T(4,128)S(1)} %bitcast.152, ...), kind=kOutput, calls=%fused_computation.32 | convolution fusion | flops 873732096 | bytes 13908768 | tf_op jit(solution)/shard_map/harc,nchd->nhard/dot_general | solution.py:48
  80.8 1.7 %fusion.90 = (f32[133,4]{1,0:T(8,128)S(1)}, f32[133,4]{1,0:T(8,128)S(1)}, f32[133,4]{1,0:T(8,128)S(1)}, f32[133,4]{1,0:T(8,128)S(1)}, f32[133,4]{1,0:T(8,128)S(1)}) fusion(f32[133,4,128]{2,1,0:T(4,128)S(1)} %slice.322, bf16[128,4,128]{2,1,0:T(4,128)(2,1)} %concatenate.20, bf16[5,4,128]{2,1,0:T(4,128)(2,1)S(1)} %copy-done.27, f32[133,4,128]{2,1,0:T(4,128)S(1)} %slice.312, ...), kind=kLoop, calls=%fused_computation.122 | loop fusion | flops 814492 | bytes 1508752 | tf_op jit(solution)/shard_map/reduce_sum | solution.py:64
  83.1 10.8 %fusion.1 = f32[4,128,8,128,1]{1,3,4,2,0:T(8,128)S(1)} fusion(f32[4,8,128,6,128]{4,2,3,1,0:T(8,128)} %fusion.17, f32[4,8,128,6,128]{4,2,3,1,0:T(8,128)} %fusion.15, bf16[128,4,6,128]{3,0,2,1:T(8,128)(2,1)S(1)} %constant_dynamic-update-slice_fusion), kind=kOutput, calls=%fused_computation.3 | convolution fusion | flops 817889280 | bytes 28049408 | tf_op jit(solution)/shard_map/ihad,nhard->hinr/dot_general | solution.py:84
  94.4 10.4 %fusion.85 = (f32[4,128]{1,0:T(4,128)S(1)}, f32[4,128,8,128]{1,3,2,0:T(8,128)S(1)}) fusion(f32[4,128]{1,0:T(4,128)S(1)} %get-tuple-element.70, pred[128,8,128]{0,2,1:T(8,128)(4,1)S(1)} %get-tuple-element.65, f32[4,128]{1,0:T(4,128)S(1)} %get-tuple-element.63, pred[128,8,128]{0,2,1:T(8,128)(4,1)S(1)} %get-tuple-element.66, ...), kind=kOutput, calls=%fused_computation.113 | convolution fusion | flops 821558784 | bytes 30945280 | tf_op jit(solution)/shard_map/ihad,nhard->hinr/dot_general | solution.py:82
  104.9 1.3 exponential_reduce_fusion
  106.2 1.2 fusion.13
  107.5 0.1 slice_bitcast_fusion.3
  107.6 0.2 copy.199
  107.8 0.2 copy.200
  108.1 0.2 copy.201
  108.3 0.2 copy.202
  108.5 1.5 %copy.204 = bf16[1024,512]{0,1:T(8,128)(2,1)S(1)} copy(bf16[1024,512]{1,0:T(8,128)(2,1)} %all-gather.5.cloned.1.call-done) | data formatting | bytes 2097152 | tf_op jit(solution)/shard_map/all_gather | solution.py:143
  110.0 0.8 multiply_reduce_fusion
  110.9 0.1 multiply_convert_fusion
  111.0 0.1 copy.205
  111.2 8.9 %all_to_all.76 = bf16[4,32,512]{2,1,0:T(8,128)(2,1)S(1)} all-to-all(bf16[4,32,512]{2,1,0:T(8,128)(2,1)S(1)} %all_to_all.68), channel_id=1, replica_groups=mesh['ctx'=8,'uly'=4] {'uly'}, dimensions={0} | all-to-all | bytes 262144 | tf_op jit(solution)/shard_map/all_to_all | solution.py:185
  120.1 0.7 copy.219
  (147 shorter events, 2.9 us)
Async XLA Ops:
  8.1 12.4 %all-to-all-start.1 = ((bf16[32,4,512]{2,0,1:T(8,128)(2,1)}), bf16[32,4,512]{2,0,1:T(8,128)(2,1)S(1)}, u32[]{:S(2)}, u32[]{:S(2)}) async-start(bf16[32,4,512]{2,0,1:T(8,128)(2,1)} %bitcast.121), calls=%async_computation.1 | async-start | bytes 262144 | tf_op jit(solution)/shard_map/all_to_all | solution.py:129
  20.5 3.4 %copy-start.2 = (bf16[32,4,512]{2,0,1:T(8,128)(2,1)}, bf16[32,4,512]{2,0,1:T(8,128)(2,1)S(1)}, u32[]{:S(2)}) copy-start(bf16[32,4,512]{2,0,1:T(8,128)(2,1)S(1)} %all-to-all-done.1) | copy-start | bytes 393220
  20.5 19.6 %all-to-all-start = ((bf16[32,4,512]{2,0,1:T(8,128)(2,1)}), bf16[32,4,512]{2,0,1:T(8,128)(2,1)S(1)}, u32[]{:S(2)}, u32[]{:S(2)}) async-start(bf16[32,4,512]{2,0,1:T(8,128)(2,1)} %bitcast.122), calls=%async_computation | async-start | bytes 262144 | tf_op jit(solution)/shard_map/all_to_all | solution.py:128
  23.8 30.1 %all-gather.3.cloned.1.call-start = ((), (), s32[]{:S(2)}) async-start(), calls=%async_computation.4 | async-start | bytes 1179648 | tf_op jit(solution)/shard_map/all_gather | solution.py:142
  40.1 11.0 %all-to-all-start.2 = ((bf16[32,4,512]{2,0,1:T(8,128)(2,1)}), bf16[32,4,512]{2,0,1:T(8,128)(2,1)S(1)}, u32[]{:S(2)}, u32[]{:S(2)}) async-start(bf16[32,4,512]{2,0,1:T(8,128)(2,1)} %bitcast.120), calls=%async_computation.2 | async-start | bytes 262144 | tf_op jit(solution)/shard_map/all_to_all | solution.py:130
  45.1 63.4 %all-gather.5.cloned.1.call-start = ((), (), s32[]{:S(2)}) async-start(), calls=%async_computation.5 | async-start | bytes 1179648 | tf_op jit(solution)/shard_map/all_gather | solution.py:143
  45.1 6.6 %collective-permute-start = (bf16[5,512]{1,0:T(8,128)(2,1)S(1)}, bf16[5,512]{1,0:T(8,128)(2,1)S(1)}, u32[]{:S(2)}, u32[]{:S(2)}) collective-permute-start(bf16[5,512]{1,0:T(8,128)(2,1)S(1)} %slice.339), channel_id=1, source_target_pairs={{0,4},{4,8},{8,12},{12,16},{16,20},{20,24},{24,28},{1,5},{5,9},{9,... | collective-permute-start | bytes 15368 | tf_op jit(solution)/shard_map/ppermute | solution.py:21
  51.0 0.7 copy-start.1
  65.0 7.7 %copy-start.9 = (pred[128,138]{0,1:T(8,128)(4,1)S(1)}, pred[128,138]{0,1:T(8,128)(4,1)}, u32[]{:S(2)}) copy-start(pred[128,138]{0,1:T(8,128)(4,1)} %get-tuple-element.80) | copy-start | bytes 52996
  65.0 7.7 %copy-start.10 = (pred[128,138]{0,1:T(8,128)(4,1)S(1)}, pred[128,138]{0,1:T(8,128)(4,1)}, u32[]{:S(2)}) copy-start(pred[128,138]{0,1:T(8,128)(4,1)} %get-tuple-element.81) | copy-start | bytes 52996
  65.0 7.7 %copy-start.11 = (pred[128,138]{0,1:T(8,128)(4,1)S(1)}, pred[128,138]{0,1:T(8,128)(4,1)}, u32[]{:S(2)}) copy-start(pred[128,138]{0,1:T(8,128)(4,1)} %get-tuple-element.82) | copy-start | bytes 52996
  65.0 7.7 %copy-start.12 = (pred[128,138]{0,1:T(8,128)(4,1)S(1)}, pred[128,138]{0,1:T(8,128)(4,1)}, u32[]{:S(2)}) copy-start(pred[128,138]{0,1:T(8,128)(4,1)} %get-tuple-element.83) | copy-start | bytes 52996
  65.0 7.7 %copy-start.13 = (pred[128,138]{0,1:T(8,128)(4,1)S(1)}, pred[128,138]{0,1:T(8,128)(4,1)}, u32[]{:S(2)}) copy-start(pred[128,138]{0,1:T(8,128)(4,1)} %get-tuple-element.84) | copy-start | bytes 52996
  65.1 7.7 %copy-start.14 = (pred[128,138]{0,1:T(8,128)(4,1)S(1)}, pred[128,138]{0,1:T(8,128)(4,1)}, u32[]{:S(2)}) copy-start(pred[128,138]{0,1:T(8,128)(4,1)} %get-tuple-element.85) | copy-start | bytes 52996
  65.1 7.7 %copy-start.15 = (pred[128,138]{0,1:T(8,128)(4,1)S(1)}, pred[128,138]{0,1:T(8,128)(4,1)}, u32[]{:S(2)}) copy-start(pred[128,138]{0,1:T(8,128)(4,1)} %get-tuple-element.86) | copy-start | bytes 52996
  65.1 7.7 %copy-start.16 = (pred[128,138]{0,1:T(8,128)(4,1)S(1)}, pred[128,138]{0,1:T(8,128)(4,1)}, u32[]{:S(2)}) copy-start(pred[128,138]{0,1:T(8,128)(4,1)} %get-tuple-element.87) | copy-start | bytes 52996
  65.1 7.7 %copy-start.17 = (f32[4,6,1]{1,0,2:T(4,128)S(1)}, f32[4,6,1]{1,0,2:T(4,128)}, u32[]{:S(2)}) copy-start(f32[4,6,1]{1,0,2:T(4,128)} %copy.182) | copy-start | bytes 292
  65.1 7.7 %copy-start.18 = (f32[4,6,1]{1,0,2:T(4,128)S(1)}, f32[4,6,1]{1,0,2:T(4,128)}, u32[]{:S(2)}) copy-start(f32[4,6,1]{1,0,2:T(4,128)} %copy.183) | copy-start | bytes 292
  65.1 7.7 %copy-start.19 = (f32[4,6,1]{1,0,2:T(4,128)S(1)}, f32[4,6,1]{1,0,2:T(4,128)}, u32[]{:S(2)}) copy-start(f32[4,6,1]{1,0,2:T(4,128)} %copy.184) | copy-start | bytes 292
  65.1 7.7 %copy-start.20 = (f32[4,6,1]{1,0,2:T(4,128)S(1)}, f32[4,6,1]{1,0,2:T(4,128)}, u32[]{:S(2)}) copy-start(f32[4,6,1]{1,0,2:T(4,128)} %copy.185) | copy-start | bytes 292
  65.1 7.7 %copy-start.21 = (f32[4,6,1]{1,0,2:T(4,128)S(1)}, f32[4,6,1]{1,0,2:T(4,128)}, u32[]{:S(2)}) copy-start(f32[4,6,1]{1,0,2:T(4,128)} %copy.186) | copy-start | bytes 292
  65.1 7.7 %copy-start.22 = (f32[4,6,1]{1,0,2:T(4,128)S(1)}, f32[4,6,1]{1,0,2:T(4,128)}, u32[]{:S(2)}) copy-start(f32[4,6,1]{1,0,2:T(4,128)} %copy.187) | copy-start | bytes 292
  65.1 7.7 %copy-start.23 = (f32[4,6,1]{1,0,2:T(4,128)S(1)}, f32[4,6,1]{1,0,2:T(4,128)}, u32[]{:S(2)}) copy-start(f32[4,6,1]{1,0,2:T(4,128)} %copy.188) | copy-start | bytes 292
  65.2 7.7 %copy-start.24 = (f32[4,6,1]{1,0,2:T(4,128)S(1)}, f32[4,6,1]{1,0,2:T(4,128)}, u32[]{:S(2)}) copy-start(f32[4,6,1]{1,0,2:T(4,128)} %copy.189) | copy-start | bytes 292
  65.2 7.7 %copy-start.25 = (f32[4,6,1]{1,0,2:T(4,128)S(1)}, f32[4,6,1]{1,0,2:T(4,128)}, u32[]{:S(2)}) copy-start(f32[4,6,1]{1,0,2:T(4,128)} %copy.190) | copy-start | bytes 292
  65.2 7.7 %copy-start.26 = (f32[4,6,1]{1,0,2:T(4,128)S(1)}, f32[4,6,1]{1,0,2:T(4,128)}, u32[]{:S(2)}) copy-start(f32[4,6,1]{1,0,2:T(4,128)} %copy.191) | copy-start | bytes 292
  72.9 7.2 %copy-start = (bf16[1024,512]{1,0:T(8,128)(2,1)S(1)}, bf16[1024,512]{1,0:T(8,128)(2,1)}, u32[]{:S(2)}) copy-start(bf16[1024,512]{1,0:T(8,128)(2,1)} %all-gather.3.cloned.1.call-done) | copy-start | bytes 3145732
  80.1 0.7 copy-start.27
  83.0 11.0 %copy-start.28 = (f32[4]{0:T(128)S(1)}, f32[4]{0:T(128)}, u32[]{:S(2)}) copy-start(f32[4]{0:T(128)} %get-tuple-element.11) | copy-start | bytes 52
  83.0 11.0 %copy-start.29 = (f32[4]{0:T(128)S(1)}, f32[4]{0:T(128)}, u32[]{:S(2)}) copy-start(f32[4]{0:T(128)} %get-tuple-element.12) | copy-start | bytes 52
  83.0 11.0 %copy-start.30 = (f32[4]{0:T(128)S(1)}, f32[4]{0:T(128)}, u32[]{:S(2)}) copy-start(f32[4]{0:T(128)} %get-tuple-element.13) | copy-start | bytes 52
  83.0 11.0 %copy-start.31 = (f32[4]{0:T(128)S(1)}, f32[4]{0:T(128)}, u32[]{:S(2)}) copy-start(f32[4]{0:T(128)} %get-tuple-element.16) | copy-start | bytes 52
  83.0 11.0 %copy-start.32 = (f32[4]{0:T(128)S(1)}, f32[4]{0:T(128)}, u32[]{:S(2)}) copy-start(f32[4]{0:T(128)} %get-tuple-element.17) | copy-start | bytes 52
  83.0 11.0 %copy-start.33 = (f32[4]{0:T(128)S(1)}, f32[4]{0:T(128)}, u32[]{:S(2)}) copy-start(f32[4]{0:T(128)} %get-tuple-element.20) | copy-start | bytes 52
  83.0 11.1 %copy-start.34 = (f32[4]{0:T(128)S(1)}, f32[4]{0:T(128)}, u32[]{:S(2)}) copy-start(f32[4]{0:T(128)} %get-tuple-element.15) | copy-start | bytes 52
  83.1 11.1 %copy-start.35 = (f32[4]{0:T(128)S(1)}, f32[4]{0:T(128)}, u32[]{:S(2)}) copy-start(f32[4]{0:T(128)} %get-tuple-element.19) | copy-start | bytes 52
  83.1 11.1 %copy-start.36 = (f32[4]{0:T(128)S(1)}, f32[4]{0:T(128)}, u32[]{:S(2)}) copy-start(f32[4]{0:T(128)} %get-tuple-element.22) | copy-start | bytes 52
  83.1 11.1 %copy-start.37 = (f32[4]{0:T(128)S(1)}, f32[4]{0:T(128)}, u32[]{:S(2)}) copy-start(f32[4]{0:T(128)} %get-tuple-element.24) | copy-start | bytes 52
  83.1 11.2 %copy-start.39 = (f32[4]{0:T(128)S(1)}, f32[4]{0:T(128)}, u32[]{:S(2)}) copy-start(f32[4]{0:T(128)} %get-tuple-element.10) | copy-start | bytes 52
  83.1 11.2 %copy-start.40 = (f32[4]{0:T(128)S(1)}, f32[4]{0:T(128)}, u32[]{:S(2)}) copy-start(f32[4]{0:T(128)} %get-tuple-element.14) | copy-start | bytes 52
  83.1 11.2 %copy-start.41 = (f32[4]{0:T(128)S(1)}, f32[4]{0:T(128)}, u32[]{:S(2)}) copy-start(f32[4]{0:T(128)} %get-tuple-element.18) | copy-start | bytes 52
  83.1 11.2 %copy-start.42 = (f32[4]{0:T(128)S(1)}, f32[4]{0:T(128)}, u32[]{:S(2)}) copy-start(f32[4]{0:T(128)} %get-tuple-element.21) | copy-start | bytes 52
  83.1 11.2 %copy-start.43 = (f32[4]{0:T(128)S(1)}, f32[4]{0:T(128)}, u32[]{:S(2)}) copy-start(f32[4]{0:T(128)} %get-tuple-element.23) | copy-start | bytes 52
  104.8 1.3 %copy-start.3 = (pred[128,1024]{0,1:T(8,128)(4,1)S(1)}, pred[128,1024]{0,1:T(8,128)(4,1)}, u32[]{:S(2)}) copy-start(pred[128,1024]{0,1:T(8,128)(4,1)} %get-tuple-element.71) | copy-start | bytes 393220
  104.8 1.3 %copy-start.4 = (pred[128,1024]{0,1:T(8,128)(4,1)S(1)}, pred[128,1024]{0,1:T(8,128)(4,1)}, u32[]{:S(2)}) copy-start(pred[128,1024]{0,1:T(8,128)(4,1)} %get-tuple-element.72) | copy-start | bytes 393220
  104.8 1.3 %copy-start.5 = (pred[128,1024]{0,1:T(8,128)(4,1)S(1)}, pred[128,1024]{0,1:T(8,128)(4,1)}, u32[]{:S(2)}) copy-start(pred[128,1024]{0,1:T(8,128)(4,1)} %get-tuple-element.73) | copy-start | bytes 393220
  104.9 1.3 %copy-start.6 = (pred[128,1024]{0,1:T(8,128)(4,1)S(1)}, pred[128,1024]{0,1:T(8,128)(4,1)}, u32[]{:S(2)}) copy-start(pred[128,1024]{0,1:T(8,128)(4,1)} %get-tuple-element.74) | copy-start | bytes 393220
  104.9 1.3 %copy-start.7 = (pred[128,1024]{0,1:T(8,128)(4,1)S(1)}, pred[128,1024]{0,1:T(8,128)(4,1)}, u32[]{:S(2)}) copy-start(pred[128,1024]{0,1:T(8,128)(4,1)} %get-tuple-element.75) | copy-start | bytes 393220
  104.9 1.3 %copy-start.8 = (pred[128,1024]{0,1:T(8,128)(4,1)S(1)}, pred[128,1024]{0,1:T(8,128)(4,1)}, u32[]{:S(2)}) copy-start(pred[128,1024]{0,1:T(8,128)(4,1)} %get-tuple-element.76) | copy-start | bytes 393220
  108.0 2.0 %copy-start.44 = (f32[4]{0:T(128)S(1)}, f32[4]{0:T(128)}, u32[]{:S(2)}) copy-start(f32[4]{0:T(128)} %get-tuple-element.25) | copy-start | bytes 52
  108.0 2.0 %copy-start.45 = (f32[4]{0:T(128)S(1)}, f32[4]{0:T(128)}, u32[]{:S(2)}) copy-start(f32[4]{0:T(128)} %get-tuple-element.26) | copy-start | bytes 52
  108.0 2.0 %copy-start.46 = (f32[4]{0:T(128)S(1)}, f32[4]{0:T(128)}, u32[]{:S(2)}) copy-start(f32[4]{0:T(128)} %get-tuple-element.27) | copy-start | bytes 52
  108.0 2.0 %copy-start.47 = (f32[4]{0:T(128)S(1)}, f32[4]{0:T(128)}, u32[]{:S(2)}) copy-start(f32[4]{0:T(128)} %get-tuple-element.28) | copy-start | bytes 52
  110.0 0.8 copy-start.38
Sparse Core Ops, SparseCore 0:
  26.6 24.9 all-gather.2
  53.4 23.4 all-gather.4

commit v2 on v1

--- a/solution.py
+++ b/solution.py
@@ -124,10 +124,9 @@
 
 
 def shards(query_states, key_states, value_states, score_kernel, head_mixing, head_gain):
-    query_local, key_local, value_local = (
-        lax.all_to_all(query_states, "uly", split_axis=1, concat_axis=0, tiled=True),
-        lax.all_to_all(key_states, "uly", split_axis=1, concat_axis=0, tiled=True),
-        lax.all_to_all(value_states, "uly", split_axis=1, concat_axis=0, tiled=True),
+    stacked = jnp.stack([query_states, key_states, value_states])
+    query_local, key_local, value_local = lax.all_to_all(
+        stacked, "uly", split_axis=2, concat_axis=1, tiled=True
     )
     shard_rows = query_local.shape[0]
     width = query_local.shape[1]
@@ -139,8 +138,9 @@
     query_first = ctx_place * shard_rows
     earlier = passed_along(query_local[shard_rows - row_lead :], "ctx", 1)
     query_ext = jnp.concatenate([earlier, query_local], axis=0)
-    key_all = lax.all_gather(key_local, "ctx", axis=0, tiled=True)
-    value_all = lax.all_gather(value_local, "ctx", axis=0, tiled=True)
+    key_all, value_all = lax.all_gather(
+        jnp.stack([key_local, value_local]), "ctx", axis=1, tiled=True
+    )
     seq_len = key_all.shape[0]
     key_pad = jnp.concatenate([jnp.zeros((col_lead, width), key_all.dtype), key_all], axis=0)
     key_windows = jnp.stack(

time: 129 us -> 158 us (1.22)
  blocking collectives: 8.88 us -> 28.5 us
  local copies, waits for them, and re-layouts: 34.2 us -> 52.8 us
  starting transfers between devices: 16 us -> 1.29 us
  waiting for transfers between devices: 9.09 us -> 12.6 us
    all_to_all x0 -> x1, blocking collectives: none -> 17.8 us  [shards(): lax.all_to_all(stacked, 'uly', split_axis=2, concat_axis=1, tiled=True)]
    all_to_all x3 -> x0, starting transfers between devices: 14.7 us -> none  [the longest x1 6.32 us: shards(): lax.all_to_all(key_states, 'uly', split_axis=1, concat_axis=0, tiled=True)]
    all_gather x2 -> x1, waiting for transfers between devices: 0.02 us -> 12.5 us  [shards(): lax.all_gather(jnp.stack([key_local, value_local]), 'ctx', axis=1, tiled=...]
    unnamed x109 -> x121, local copies, waits for them, and re-layouts: 4.98 us -> 14.7 us
    another operation x9, local copies, waits for them, and re-layouts: 4.81 us -> 14.4 us  [shards(): jnp.stack([key_pad[start:start + KEY_BLOCK + col_lead] for start in range...]
    all_to_all x3 -> x0, waiting for transfers between devices: 8.38 us -> none  [the longest x1 4.51 us: shards(): lax.all_to_all(key_states, 'uly', split_axis=1, concat_axis=0, tiled=True)]
    another operation x0 -> x7, local copies, waits for them, and re-layouts: none -> 4.63 us  [the longest x2 3.06 us: shards(): key_all, value_all = lax.all_gather(jnp.stack([key_local, value_local]),...]
    all_to_all x3 -> x1, local copies, waits for them, and re-layouts: 4.7 us -> 1.18 us  [shards(): lax.all_to_all(stacked, 'uly', split_axis=2, concat_axis=1, tiled=True)]
  transfers between devices with their start and end apart: 6 -> 2, of which waited for: 2 -> 2; matrix products, arithmetic and copies ran while one was open for 57% -> 8% of each run, Pallas kernels for 0% -> 0%
where the time goes in v2:
time: 158 us; the launch traced here: 157 us
  local copies, waits for them, and re-layouts  52.8 us (33%)
  matrix products  38.1 us (24%)
  blocking collectives  28.5 us (18%)
  between operations  14.5 us (9%)
  waiting for transfers between devices  12.6 us (8%)
  other arithmetic  9 us (6%)
    all_to_all x1, blocking collectives, shards(): lax.all_to_all(stacked, 'uly', split_axis=2, concat_axis=1, tiled=True)  17.8 us
    unnamed x121, local copies, waits for them, and re-layouts  14.7 us
    another operation x9, local copies, waits for them, and re-layouts, shards(): jnp.stack([key_pad[start:start + KEY_BLOCK + col_lead] for start in range...  14.4 us
    all_gather x1, waiting for transfers between devices, shards(): lax.all_gather(jnp.stack([key_local, value_local]), 'ctx', axis=1, tiled=...  12.5 us
    dot_general x1, matrix products, group_logits(): jnp.einsum('ihad,nhard->hinr', shifted, keys_low, preferred_element_type=...  10.9 us
    all_to_all x1, blocking collectives, shards(): lax.all_to_all(attended, 'uly', split_axis=0, concat_axis=1, tiled=True)  10.7 us
    dot_general x1, matrix products, group_logits(): jnp.einsum('ihad,nhard->hinr', shifted, keys_high, preferred_element_type...  10.4 us
    dot_general x1, matrix products, convolved_keys(): jnp.einsum('harc,nchd->nhard', high, key_heads, preferred_element_type=jn...  8.7 us
  transfers between devices with their start and end apart: 2, of which 2 were waited for; matrix products, arithmetic and copies ran while one was open for 8% of the time, Pallas kernels for 0%

profile of v2, /device:TPU:0, one launch (start us, length us, event | category | flops | bytes accessed | tf_op | source)
XLA Modules:
  0.0 156.9 jit_solution(3671239521716522393)
XLA Ops:
  6.5 1.1 pad_maximum_fusion
  7.6 1.4 copy.223
  9.0 1.6 %reshape.295 = bf16[4,2,24576]{2,1,0:T(2,128)(2,1)S(1)} reshape(bf16[2048,3,32]{2,1,0:T(4,128)(2,1)S(1)} %bitcast.118) | data formatting | bytes 786432
  10.6 17.8 %all_to_all.34 = bf16[4,2,24576]{2,1,0:T(2,128)(2,1)S(1)} all-to-all(bf16[4,2,24576]{2,1,0:T(2,128)(2,1)S(1)} %reshape.295), channel_id=1, replica_groups=mesh['ctx'=8,'uly'=4] {'uly'}, dimensions={0} | all-to-all | bytes 786432 | tf_op jit(solution)/shard_map/all_to_all | solution.py:128
  28.4 1.3 reshape.296
  29.7 1.2 copy.282
  30.9 0.1 fusion.128
  31.1 0.8 pad_maximum_fusion.1
  32.5 0.7 copy.255
  33.2 0.6 copy.254
  33.8 0.7 copy.253
  34.5 0.7 copy.252
  35.2 0.7 copy.251
  35.9 0.7 copy.250
  36.5 0.7 copy.249
  37.2 0.7 slice_reduce_fusion.18
  38.0 1.0 slice_reduce_fusion.17
  39.0 0.8 fusion.108
  39.7 1.2 fusion.84
  41.0 1.2 subtract_compare_fusion.5
  42.3 1.3 collective-permute-start
  43.6 0.7 concatenate.20
  45.2 0.1 copy.238
  45.7 0.1 copy.240
  45.8 0.6 concatenate.19
  46.6 12.5 %all-gather.2.cloned.1.call-done = bf16[2,1024,512]{2,1,0:T(8,128)(2,1)} async-done(((bf16[2,128,512]{2,1,0:T(8,128)(2,1)}), bf16[2,1024,512]{2,1,0:T(8,128)(2,1)}) %all-gather.2.cloned.1.call-update) | async-done | bytes 2097168 | tf_op jit(solution)/shard_map/all_gather | solution.py:141
  59.1 1.7 %slice_bitcast_fusion = (bf16[1024,512]{1,0:T(8,128)(2,1)S(1)}, bf16[1,1024,512]{2,1,0:T(8,128)(2,1)S(1)}) fusion(bf16[2,1024,512]{2,1,0:T(8,128)(2,1)} %all-gather.2.cloned.1.call-done), kind=kLoop, calls=%fused_computation.39 | loop fusion | bytes 4194304 | tf_op jit(solution)/shard_map/unstack | solution.py:141
  60.8 0.7 pad_slice_fusion
  61.5 1.6 %stack.75 = bf16[1,138,4,128]{3,2,1,0:T(4,128)(2,1)} reshape(bf16[138,512]{1,0:T(8,128)(2,1)} %pad_slice_fusion) | data formatting | bytes 282624 | tf_op jit(solution)/shard_map/stack | solution.py:146
  63.1 1.6 %copy_dynamic-update-slice_fusion.7 = bf16[8,138,4,128]{3,1,0,2:T(8,128)(2,1)} fusion(bf16[1,138,4,128]{3,2,1,0:T(4,128)(2,1)} %stack.75), kind=kLoop, calls=%fused_computation.138 | loop fusion | bytes 288768
  64.7 2.4 %fusion.127 = (bf16[1,138,512]{2,1,0:T(8,128)(2,1)}, bf16[1,138,512]{2,1,0:T(8,128)(2,1)}, bf16[1,138,512]{2,1,0:T(8,128)(2,1)}, bf16[1,138,512]{2,1,0:T(8,128)(...) fusion(bf16[2,1024,512]{2,1,0:T(8,128)(2,1)} %all-gather.2.cloned.1.call-done), kind=kLoop, calls=%fused_computation.217 | loop fusion | bytes 1978368 | tf_op jit(solution)/shard_map/slice | solution.py:148
  67.1 1.6 %stack.76 = bf16[1,138,4,128]{3,2,1,0:T(4,128)(2,1)} reshape(bf16[1,138,512]{2,1,0:T(8,128)(2,1)} %get-tuple-element.39) | data formatting | bytes 282624 | tf_op jit(solution)/shard_map/stack | solution.py:146
  68.7 1.6 %stack.77 = bf16[1,138,4,128]{3,2,1,0:T(4,128)(2,1)} reshape(bf16[1,138,512]{2,1,0:T(8,128)(2,1)} %get-tuple-element.38) | data formatting | bytes 282624 | tf_op jit(solution)/shard_map/stack | solution.py:146
  70.3 1.6 %stack.78 = bf16[1,138,4,128]{3,2,1,0:T(4,128)(2,1)} reshape(bf16[1,138,512]{2,1,0:T(8,128)(2,1)} %get-tuple-element.37) | data formatting | bytes 282624 | tf_op jit(solution)/shard_map/stack | solution.py:146
  71.9 1.6 %stack.79 = bf16[1,138,4,128]{3,2,1,0:T(4,128)(2,1)} reshape(bf16[1,138,512]{2,1,0:T(8,128)(2,1)} %get-tuple-element.36) | data formatting | bytes 282624 | tf_op jit(solution)/shard_map/stack | solution.py:146
  73.5 1.6 %stack.80 = bf16[1,138,4,128]{3,2,1,0:T(4,128)(2,1)} reshape(bf16[1,138,512]{2,1,0:T(8,128)(2,1)} %get-tuple-element.35) | data formatting | bytes 282624 | tf_op jit(solution)/shard_map/stack | solution.py:146
  75.1 1.6 %stack.81 = bf16[1,138,4,128]{3,2,1,0:T(4,128)(2,1)} reshape(bf16[1,138,512]{2,1,0:T(8,128)(2,1)} %get-tuple-element.34) | data formatting | bytes 282624 | tf_op jit(solution)/shard_map/stack | solution.py:146
  76.7 1.6 %stack.82 = bf16[1,138,4,128]{3,2,1,0:T(4,128)(2,1)} reshape(bf16[1,138,512]{2,1,0:T(8,128)(2,1)} %get-tuple-element.33) | data formatting | bytes 282624 | tf_op jit(solution)/shard_map/stack | solution.py:146
  78.3 1.6 %copy_dynamic-update-slice_fusion.6 = bf16[8,138,4,128]{3,1,0,2:T(8,128)(2,1)} fusion(bf16[8,138,4,128]{3,1,0,2:T(8,128)(2,1)} %copy_dynamic-update-slice_fusion.7, bf16[1,138,4,128]{3,2,1,0:T(4,128)(2,1)} %stack.76), kind=kLoop, calls=%fused_computation.137 | loop fusion | bytes 288768
  79.9 1.6 %copy_dynamic-update-slice_fusion.5 = bf16[8,138,4,128]{3,1,0,2:T(8,128)(2,1)} fusion(bf16[8,138,4,128]{3,1,0,2:T(8,128)(2,1)} %copy_dynamic-update-slice_fusion.6, bf16[1,138,4,128]{3,2,1,0:T(4,128)(2,1)} %stack.77), kind=kLoop, calls=%fused_computation.136 | loop fusion | bytes 288768
  81.5 1.6 %copy_dynamic-update-slice_fusion.4 = bf16[8,138,4,128]{3,1,0,2:T(8,128)(2,1)} fusion(bf16[8,138,4,128]{3,1,0,2:T(8,128)(2,1)} %copy_dynamic-update-slice_fusion.5, bf16[1,138,4,128]{3,2,1,0:T(4,128)(2,1)} %stack.78), kind=kLoop, calls=%fused_computation.135 | loop fusion | bytes 288768
  83.1 1.6 %copy_dynamic-update-slice_fusion.3 = bf16[8,138,4,128]{3,1,0,2:T(8,128)(2,1)} fusion(bf16[8,138,4,128]{3,1,0,2:T(8,128)(2,1)} %copy_dynamic-update-slice_fusion.4, bf16[1,138,4,128]{3,2,1,0:T(4,128)(2,1)} %stack.79), kind=kLoop, calls=%fused_computation.134 | loop fusion | bytes 288768
  84.7 1.6 %copy_dynamic-update-slice_fusion.2 = bf16[8,138,4,128]{3,1,0,2:T(8,128)(2,1)} fusion(bf16[8,138,4,128]{3,1,0,2:T(8,128)(2,1)} %copy_dynamic-update-slice_fusion.3, bf16[1,138,4,128]{3,2,1,0:T(4,128)(2,1)} %stack.80), kind=kLoop, calls=%fused_computation.133 | loop fusion | bytes 288768
  86.3 1.6 %copy_dynamic-update-slice_fusion.1 = bf16[8,138,4,128]{3,1,0,2:T(8,128)(2,1)} fusion(bf16[8,138,4,128]{3,1,0,2:T(8,128)(2,1)} %copy_dynamic-update-slice_fusion.2, bf16[1,138,4,128]{3,2,1,0:T(4,128)(2,1)} %stack.81), kind=kLoop, calls=%fused_computation.132 | loop fusion | bytes 288768
  87.9 1.6 %copy_dynamic-update-slice_fusion = bf16[8,138,4,128]{3,1,0,2:T(8,128)(2,1)} fusion(bf16[8,138,4,128]{3,1,0,2:T(8,128)(2,1)} %copy_dynamic-update-slice_fusion.1, bf16[1,138,4,128]{3,2,1,0:T(4,128)(2,1)} %stack.82), kind=kLoop, calls=%fused_computation.131 | loop fusion | bytes 288768 | tf_op jit(solution)/shard_map/stack | solution.py:146
  89.6 8.7 %fusion.17 = f32[4,8,128,6,128]{4,2,3,1,0:T(8,128)} fusion(bf16[8,138,4,128]{3,1,0,2:T(8,128)(2,1)} %copy_dynamic-update-slice_fusion, f32[4,6]{1,0:T(4,128)S(1)} %bitcast.135, f32[4,6]{1,0:T(4,128)S(1)} %bitcast.137, f32[4,6]{1,0:T(4,128)S(1)} %bitcast.139, f32[4,6]{1,0:T(4,128)S(1)} %bitcast.141, f32[4,6]{1,0:T(4,128)} %bitcast.143, ...), kind=kOutput, calls=%fused_computation.32 | convolution fusion | flops 873732096 | bytes 13908768 | tf_op jit(solution)/shard_map/harc,nchd->nhard/dot_general | solution.py:48
  98.5 6.3 %fusion.15 = f32[4,8,128,6,128]{4,2,3,1,0:T(8,128)} fusion(bf16[8,138,4,128]{3,1,0,2:T(8,128)(2,1)S(1)} %copy-done, f32[4,6]{1,0:T(4,128)S(1)} %bitcast.136, f32[4,6]{1,0:T(4,128)S(1)} %bitcast.138, f32[4,6]{1,0:T(4,128)S(1)} %bitcast.140, f32[4,6]{1,0:T(4,128)S(1)} %bitcast.142, f32[4,6]{1,0:T(4,128)S(1)} %bitcast.144, f32[4,6]{1,0:T(4,128)S(1)} %bitcast.146, ...), kind=kOutput, calls=%fused_computation.30 | convolution fusion | flops 874156032 | bytes 13908768 | tf_op jit(solution)/shard_map/harc,nchd->nhard/dot_general | solution.py:50
  104.8 1.4 copy.227
  106.3 0.1 fusion.129
  107.0 0.2 copy-done.5
  107.2 0.8 fusion.90
  108.6 10.9 %fusion.1 = f32[4,128,8,128,1]{1,3,4,2,0:T(8,128)S(1)} fusion(f32[4,8,128,6,128]{4,2,3,1,0:T(8,128)} %fusion.17, f32[4,8,128,6,128]{4,2,3,1,0:T(8,128)} %fusion.15, bf16[128,4,6,128]{3,0,2,1:T(8,128)(2,1)S(1)} %constant_dynamic-update-slice_fusion), kind=kOutput, calls=%fused_computation.3 | convolution fusion | flops 817889280 | bytes 28049408 | tf_op jit(solution)/shard_map/ihad,nhard->hinr/dot_general | solution.py:84
  119.9 10.4 %fusion.85 = (f32[4,128]{1,0:T(4,128)S(1)}, f32[4,128,8,128]{1,3,2,0:T(8,128)S(1)}) fusion(f32[4,128]{1,0:T(4,128)S(1)} %get-tuple-element.74, pred[128,8,128]{0,2,1:T(8,128)(4,1)S(1)} %get-tuple-element.69, f32[4,128]{1,0:T(4,128)S(1)} %get-tuple-element.67, pred[128,8,128]{0,2,1:T(8,128)(4,1)S(1)} %get-tuple-element.70, ...), kind=kOutput, calls=%fused_computation.115 | convolution fusion | flops 821558784 | bytes 30945280 | tf_op jit(solution)/shard_map/ihad,nhard->hinr/dot_general | solution.py:82
  130.4 1.3 exponential_reduce_fusion
  131.7 1.3 fusion.13
  133.0 0.1 slice_bitcast_fusion.4
  133.1 1.0 copy.271
  134.1 1.0 copy.270
  135.2 1.0 copy.269
  136.2 0.2 copy.268
  136.5 1.8 %multiply_reduce_fusion = (f32[128,4]{0,1:T(4,128)S(1)}, f32[128,4,128]{0,2,1:T(8,128)S(1)}) fusion(bf16[1024,4,128]{0,2,1:T(8,128)(2,1)S(1)} %bitcast.123, f32[128,1024]{1,0:T(8,128)S(1)} %copy-done.3, f32[4]{0:T(128)S(1)} %copy-done.50, f32[128,1024]{1,0:T(8,128)S(1)} %copy-done.4, f32[4]{0:T(128)S(1)} %copy-done.51, f32[128,1024]{1,0:T(8,128)} %copy.269, ...), kind=kOutput, calls=%fused_computation.127 | convolution fusion | flops 138542592 | bytes 3409984 | tf_op jit(solution)/shard_map/hik,khd->ihd/dot_general | solution.py:114
  138.5 0.1 copy.272
  138.7 10.7 %all_to_all.35 = bf16[4,32,512]{2,1,0:T(8,128)(2,1)S(1)} all-to-all(bf16[4,32,512]{2,1,0:T(8,128)(2,1)S(1)} %all_to_all.28), channel_id=1, replica_groups=mesh['ctx'=8,'uly'=4] {'uly'}, dimensions={0} | all-to-all | bytes 262144 | tf_op jit(solution)/shard_map/all_to_all | solution.py:185
  149.4 0.7 copy.284
  (158 shorter events, 3.8 us)
Async XLA Ops:
  6.5 52.5 %all-gather.2.cloned.1.call-start = ((), (), s32[]{:S(2)}) async-start(), calls=%async_computation.2 | async-start | bytes 2359296 | tf_op jit(solution)/shard_map/all_gather | solution.py:141
  29.7 2.2 %copy-start.23 = (f32[4,6,11]{2,0,1:T(4,128)S(1)}, f32[4,6,11]{2,0,1:T(4,128)}, u32[]{:S(2)}) copy-start(f32[4,6,11]{2,0,1:T(4,128)} %param.9) | copy-start | bytes 3172
  29.7 7.5 %copy-start.31 = (f32[4,4]{1,0:T(4,128)S(1)}, f32[4,4]{1,0:T(4,128)}, u32[]{:S(2)}) copy-start(f32[4,4]{1,0:T(4,128)} %param.10) | copy-start | bytes 196
  42.3 2.1 %collective-permute-start = (bf16[5,512]{1,0:T(8,128)(2,1)S(1)}, bf16[5,512]{1,0:T(8,128)(2,1)S(1)}, u32[]{:S(2)}, u32[]{:S(2)}) collective-permute-start(bf16[5,512]{1,0:T(8,128)(2,1)S(1)} %slice.356), channel_id=1, source_target_pairs={{0,4},{4,8},{8,12},{12,16},{16,20},{20,24},{24,28},{1,5},{5,9},{9,... | collective-permute-start | bytes 15368 | tf_op jit(solution)/shard_map/ppermute | solution.py:21
  89.5 8.9 %copy-start = (bf16[8,138,4,128]{3,1,0,2:T(8,128)(2,1)S(1)}, bf16[8,138,4,128]{3,1,0,2:T(8,128)(2,1)}, u32[]{:S(2)}) copy-start(bf16[8,138,4,128]{3,1,0,2:T(8,128)(2,1)} %copy_dynamic-update-slice_fusion) | copy-start | bytes 3391492
  89.5 8.9 %copy-start.12 = (pred[128,138]{0,1:T(8,128)(4,1)S(1)}, pred[128,138]{0,1:T(8,128)(4,1)}, u32[]{:S(2)}) copy-start(pred[128,138]{0,1:T(8,128)(4,1)} %get-tuple-element.81) | copy-start | bytes 52996
  89.5 8.9 %copy-start.13 = (pred[128,138]{0,1:T(8,128)(4,1)S(1)}, pred[128,138]{0,1:T(8,128)(4,1)}, u32[]{:S(2)}) copy-start(pred[128,138]{0,1:T(8,128)(4,1)} %get-tuple-element.82) | copy-start | bytes 52996
  89.5 8.9 %copy-start.14 = (pred[128,138]{0,1:T(8,128)(4,1)S(1)}, pred[128,138]{0,1:T(8,128)(4,1)}, u32[]{:S(2)}) copy-start(pred[128,138]{0,1:T(8,128)(4,1)} %get-tuple-element.83) | copy-start | bytes 52996
  89.5 8.9 %copy-start.15 = (pred[128,138]{0,1:T(8,128)(4,1)S(1)}, pred[128,138]{0,1:T(8,128)(4,1)}, u32[]{:S(2)}) copy-start(pred[128,138]{0,1:T(8,128)(4,1)} %get-tuple-element.84) | copy-start | bytes 52996
  89.5 8.9 %copy-start.16 = (pred[128,138]{0,1:T(8,128)(4,1)S(1)}, pred[128,138]{0,1:T(8,128)(4,1)}, u32[]{:S(2)}) copy-start(pred[128,138]{0,1:T(8,128)(4,1)} %get-tuple-element.85) | copy-start | bytes 52996
  89.5 8.9 %copy-start.17 = (pred[128,138]{0,1:T(8,128)(4,1)S(1)}, pred[128,138]{0,1:T(8,128)(4,1)}, u32[]{:S(2)}) copy-start(pred[128,138]{0,1:T(8,128)(4,1)} %get-tuple-element.86) | copy-start | bytes 52996
  89.5 8.9 %copy-start.18 = (pred[128,138]{0,1:T(8,128)(4,1)S(1)}, pred[128,138]{0,1:T(8,128)(4,1)}, u32[]{:S(2)}) copy-start(pred[128,138]{0,1:T(8,128)(4,1)} %get-tuple-element.87) | copy-start | bytes 52996
  89.5 8.9 %copy-start.19 = (pred[128,138]{0,1:T(8,128)(4,1)S(1)}, pred[128,138]{0,1:T(8,128)(4,1)}, u32[]{:S(2)}) copy-start(pred[128,138]{0,1:T(8,128)(4,1)} %get-tuple-element.88) | copy-start | bytes 52996
  89.5 8.9 %copy-start.20 = (pred[128,138]{0,1:T(8,128)(4,1)S(1)}, pred[128,138]{0,1:T(8,128)(4,1)}, u32[]{:S(2)}) copy-start(pred[128,138]{0,1:T(8,128)(4,1)} %get-tuple-element.89) | copy-start | bytes 52996
  89.5 8.9 %copy-start.21 = (pred[128,138]{0,1:T(8,128)(4,1)S(1)}, pred[128,138]{0,1:T(8,128)(4,1)}, u32[]{:S(2)}) copy-start(pred[128,138]{0,1:T(8,128)(4,1)} %get-tuple-element.90) | copy-start | bytes 52996
  89.6 8.9 %copy-start.22 = (pred[128,138]{0,1:T(8,128)(4,1)S(1)}, pred[128,138]{0,1:T(8,128)(4,1)}, u32[]{:S(2)}) copy-start(pred[128,138]{0,1:T(8,128)(4,1)} %get-tuple-element.91) | copy-start | bytes 52996
  89.6 8.9 %copy-start.24 = (f32[4,6,1]{1,0,2:T(4,128)S(1)}, f32[4,6,1]{1,0,2:T(4,128)}, u32[]{:S(2)}) copy-start(f32[4,6,1]{1,0,2:T(4,128)} %copy.255) | copy-start | bytes 292
  89.6 8.9 %copy-start.25 = (f32[4,6,1]{1,0,2:T(4,128)S(1)}, f32[4,6,1]{1,0,2:T(4,128)}, u32[]{:S(2)}) copy-start(f32[4,6,1]{1,0,2:T(4,128)} %copy.254) | copy-start | bytes 292
  89.6 8.9 %copy-start.26 = (f32[4,6,1]{1,0,2:T(4,128)S(1)}, f32[4,6,1]{1,0,2:T(4,128)}, u32[]{:S(2)}) copy-start(f32[4,6,1]{1,0,2:T(4,128)} %copy.253) | copy-start | bytes 292
  89.6 8.9 %copy-start.27 = (f32[4,6,1]{1,0,2:T(4,128)S(1)}, f32[4,6,1]{1,0,2:T(4,128)}, u32[]{:S(2)}) copy-start(f32[4,6,1]{1,0,2:T(4,128)} %copy.252) | copy-start | bytes 292
  89.6 8.9 %copy-start.28 = (f32[4,6,1]{1,0,2:T(4,128)S(1)}, f32[4,6,1]{1,0,2:T(4,128)}, u32[]{:S(2)}) copy-start(f32[4,6,1]{1,0,2:T(4,128)} %copy.251) | copy-start | bytes 292
  89.6 8.9 %copy-start.29 = (f32[4,6,1]{1,0,2:T(4,128)S(1)}, f32[4,6,1]{1,0,2:T(4,128)}, u32[]{:S(2)}) copy-start(f32[4,6,1]{1,0,2:T(4,128)} %copy.250) | copy-start | bytes 292
  89.6 8.9 %copy-start.30 = (f32[4,6,1]{1,0,2:T(4,128)S(1)}, f32[4,6,1]{1,0,2:T(4,128)}, u32[]{:S(2)}) copy-start(f32[4,6,1]{1,0,2:T(4,128)} %copy.249) | copy-start | bytes 292
  106.3 0.9 copy-start.5
  106.3 0.9 copy-start.32
  108.4 11.0 %copy-start.33 = (f32[4]{0:T(128)S(1)}, f32[4]{0:T(128)}, u32[]{:S(2)}) copy-start(f32[4]{0:T(128)} %get-tuple-element.11) | copy-start | bytes 52
  108.4 11.0 %copy-start.34 = (f32[4]{0:T(128)S(1)}, f32[4]{0:T(128)}, u32[]{:S(2)}) copy-start(f32[4]{0:T(128)} %get-tuple-element.12) | copy-start | bytes 52
  108.4 11.0 %copy-start.35 = (f32[4]{0:T(128)S(1)}, f32[4]{0:T(128)}, u32[]{:S(2)}) copy-start(f32[4]{0:T(128)} %get-tuple-element.13) | copy-start | bytes 52
  108.5 11.0 %copy-start.36 = (f32[4]{0:T(128)S(1)}, f32[4]{0:T(128)}, u32[]{:S(2)}) copy-start(f32[4]{0:T(128)} %get-tuple-element.16) | copy-start | bytes 52
  108.5 11.0 %copy-start.37 = (f32[4]{0:T(128)S(1)}, f32[4]{0:T(128)}, u32[]{:S(2)}) copy-start(f32[4]{0:T(128)} %get-tuple-element.17) | copy-start | bytes 52
  108.5 11.0 %copy-start.38 = (f32[4]{0:T(128)S(1)}, f32[4]{0:T(128)}, u32[]{:S(2)}) copy-start(f32[4]{0:T(128)} %get-tuple-element.20) | copy-start | bytes 52
  108.5 11.1 %copy-start.39 = (f32[4]{0:T(128)S(1)}, f32[4]{0:T(128)}, u32[]{:S(2)}) copy-start(f32[4]{0:T(128)} %get-tuple-element.15) | copy-start | bytes 52
  108.5 11.1 %copy-start.40 = (f32[4]{0:T(128)S(1)}, f32[4]{0:T(128)}, u32[]{:S(2)}) copy-start(f32[4]{0:T(128)} %get-tuple-element.19) | copy-start | bytes 52
  108.5 11.1 %copy-start.41 = (f32[4]{0:T(128)S(1)}, f32[4]{0:T(128)}, u32[]{:S(2)}) copy-start(f32[4]{0:T(128)} %get-tuple-element.22) | copy-start | bytes 52
  108.5 11.1 %copy-start.42 = (f32[4]{0:T(128)S(1)}, f32[4]{0:T(128)}, u32[]{:S(2)}) copy-start(f32[4]{0:T(128)} %get-tuple-element.24) | copy-start | bytes 52
  108.5 11.2 %copy-start.44 = (f32[4]{0:T(128)S(1)}, f32[4]{0:T(128)}, u32[]{:S(2)}) copy-start(f32[4]{0:T(128)} %get-tuple-element.10) | copy-start | bytes 52
  108.5 11.2 %copy-start.45 = (f32[4]{0:T(128)S(1)}, f32[4]{0:T(128)}, u32[]{:S(2)}) copy-start(f32[4]{0:T(128)} %get-tuple-element.14) | copy-start | bytes 52
  108.5 11.2 %copy-start.46 = (f32[4]{0:T(128)S(1)}, f32[4]{0:T(128)}, u32[]{:S(2)}) copy-start(f32[4]{0:T(128)} %get-tuple-element.18) | copy-start | bytes 52
  108.6 11.2 %copy-start.47 = (f32[4]{0:T(128)S(1)}, f32[4]{0:T(128)}, u32[]{:S(2)}) copy-start(f32[4]{0:T(128)} %get-tuple-element.21) | copy-start | bytes 52
  108.6 11.2 %copy-start.48 = (f32[4]{0:T(128)S(1)}, f32[4]{0:T(128)}, u32[]{:S(2)}) copy-start(f32[4]{0:T(128)} %get-tuple-element.23) | copy-start | bytes 52
  108.6 11.3 %copy-start.1 = (pred[128,8,128]{0,2,1:T(8,128)(4,1)S(1)}, pred[128,8,128]{0,2,1:T(8,128)(4,1)}, u32[]{:S(2)}) copy-start(pred[128,8,128]{0,2,1:T(8,128)(4,1)} %get-tuple-element.73) | copy-start | bytes 393220
  130.3 1.3 copy-start.6
  130.3 1.3 copy-start.7
  130.3 1.3 copy-start.8
  130.4 1.3 copy-start.9
  130.4 1.3 copy-start.10
  130.4 1.3 copy-start.11
  133.1 3.3 %copy-start.2 = (bf16[1,1024,512]{1,2,0:T(8,128)(2,1)S(1)}, bf16[1,1024,512]{1,2,0:T(8,128)(2,1)}, u32[]{:S(2)}) copy-start(bf16[1,1024,512]{1,2,0:T(8,128)(2,1)} %copy.227) | copy-start | bytes 3145732
  133.1 3.3 %copy-start.49 = (f32[4]{0:T(128)S(1)}, f32[4]{0:T(128)}, u32[]{:S(2)}) copy-start(f32[4]{0:T(128)} %get-tuple-element.25) | copy-start | bytes 52
  133.1 3.3 %copy-start.50 = (f32[4]{0:T(128)S(1)}, f32[4]{0:T(128)}, u32[]{:S(2)}) copy-start(f32[4]{0:T(128)} %get-tuple-element.26) | copy-start | bytes 52
  133.1 3.3 %copy-start.51 = (f32[4]{0:T(128)S(1)}, f32[4]{0:T(128)}, u32[]{:S(2)}) copy-start(f32[4]{0:T(128)} %get-tuple-element.27) | copy-start | bytes 52
  133.1 3.3 %copy-start.52 = (f32[4]{0:T(128)S(1)}, f32[4]{0:T(128)}, u32[]{:S(2)}) copy-start(f32[4]{0:T(128)} %get-tuple-element.28) | copy-start | bytes 52
  134.1 2.3 %copy-start.3 = (f32[128,1024]{1,0:T(8,128)S(1)}, f32[128,1024]{1,0:T(8,128)}, u32[]{:S(2)}) copy-start(f32[128,1024]{1,0:T(8,128)} %copy.271) | copy-start | bytes 1572868
  135.2 1.3 copy-start.4
  136.4 1.9 %copy-start.43 = (f32[512]{0:T(512)S(1)}, f32[512]{0:T(512)}, u32[]{:S(2)}) copy-start(f32[512]{0:T(512)} %param.11) | copy-start | bytes 6148
Sparse Core Ops, SparseCore 0:
  32.0 26.9 all-gather.1

commit v3 on v2

--- a/solution.py
+++ b/solution.py
@@ -25,6 +25,38 @@
     high = lax.reduce_precision(values, exponent_bits=8, mantissa_bits=7)
     low = values - high
     return high.astype(jnp.bfloat16), low.astype(jnp.bfloat16)
+
+
+def exchanged(pieces_of, axis):
+    peers = lax.axis_size(axis)
+    place = lax.axis_index(axis)
+    received = [pieces_of(place)]
+    for shift in range(1, peers):
+        outgoing = pieces_of((place + shift) % peers)
+        pairs = [(i, (i + shift) % peers) for i in range(peers)]
+        received.append(lax.ppermute(outgoing, axis, pairs))
+    order = (place - jnp.arange(peers, dtype=jnp.int32)) % peers
+    return jnp.take(jnp.stack(received), order, axis=0)
+
+
+def gathered(shard, axis):
+    peers = lax.axis_size(axis)
+    place = lax.axis_index(axis)
+    if peers & (peers - 1):
+        return lax.all_gather(shard, axis, axis=0, tiled=False)
+    bits = peers.bit_length() - 1
+    held = shard[None]
+    for level in reversed(range(bits)):
+        bit = 1 << level
+        incoming = lax.ppermute(held, axis, [(i, i ^ bit) for i in range(peers)])
+        upper = (place & bit) != 0
+        held = jnp.where(
+            upper,
+            jnp.concatenate([incoming, held], axis=0),
+            jnp.concatenate([held, incoming], axis=0),
+        )
+    held = held.reshape((2,) * bits + shard.shape)
+    return jnp.transpose(held, tuple(reversed(range(bits))) + tuple(range(bits, held.ndim)))
 
 
 def toeplitz_terms(score_kernel, head_dim):
@@ -124,9 +156,16 @@
 
 
 def shards(query_states, key_states, value_states, score_kernel, head_mixing, head_gain):
+    groups = lax.axis_size("uly")
     stacked = jnp.stack([query_states, key_states, value_states])
-    query_local, key_local, value_local = lax.all_to_all(
-        stacked, "uly", split_axis=2, concat_axis=1, tiled=True
+    group_width = stacked.shape[2] // groups
+    pieces = exchanged(
+        lambda group: lax.dynamic_slice_in_dim(stacked, group * group_width, group_width, 2),
+        "uly",
+    )
+    pieces = jnp.moveaxis(pieces, 0, 1)
+    query_local, key_local, value_local = pieces.reshape(
+        (pieces.shape[0], -1, pieces.shape[-1])
     )
     shard_rows = query_local.shape[0]
     width = query_local.shape[1]
@@ -138,9 +177,8 @@
     query_first = ctx_place * shard_rows
     earlier = passed_along(query_local[shard_rows - row_lead :], "ctx", 1)
     query_ext = jnp.concatenate([earlier, query_local], axis=0)
-    key_all, value_all = lax.all_gather(
-        jnp.stack([key_local, value_local]), "ctx", axis=1, tiled=True
-    )
+    key_all = gathered(key_local, "ctx").reshape((-1, width))
+    value_all = gathered(value_local, "ctx").reshape((-1, width))
     seq_len = key_all.shape[0]
     key_pad = jnp.concatenate([jnp.zeros((col_lead, width), key_all.dtype), key_all], axis=0)
     key_windows = jnp.stack(
@@ -182,7 +220,12 @@
         weighted = weighted.reshape((shard_rows,) + weighted.shape[2:])
     gain_local = head_gain.reshape(heads, head_dim)
     attended = normalize(weighted, gain_local)
-    return lax.all_to_all(attended, "uly", split_axis=0, concat_axis=1, tiled=True)
+    block_rows = shard_rows // groups
+    returned = exchanged(
+        lambda group: lax.dynamic_slice_in_dim(attended, group * block_rows, block_rows, 0),
+        "uly",
+    )
+    return jnp.moveaxis(returned, 0, 1).reshape((block_rows, -1))
 
 
 def solution(mesh):

time: 158 us -> 115 us (0.73)
  blocking collectives: 28.5 us -> 0 us
  local copies, waits for them, and re-layouts: 52.8 us -> 26.9 us
  starting transfers between devices: 1.29 us -> 17.1 us
  between operations: 14.5 us -> 1.36 us
  waiting for transfers between devices: 12.6 us -> 19.5 us
  other arithmetic: 9 us -> 12.2 us
    all_to_all x2 -> x0, blocking collectives: 28.5 us -> none  [the longest x1 17.8 us: shards(): lax.all_to_all(stacked, 'uly', split_axis=2, concat_axis=1, tiled=True)]
    ppermute x0 -> x12, waiting for transfers between devices: none -> 19.5 us  [the longest x6 14.1 us: gathered(): incoming = lax.ppermute(held, axis, [(i, i ^ bit) for i in range(peers)])]
    ppermute x0 -> x12, starting transfers between devices: none -> 15.8 us  [the longest x6 10.5 us: exchanged(): received.append(lax.ppermute(outgoing, axis, pairs))]
    another operation x9, local copies, waits for them, and re-layouts: 14.4 us -> 1.01 us  [shards(): jnp.stack([key_pad[start:start + KEY_BLOCK + col_lead] for start in range...]
    all_gather x1 -> x0, waiting for transfers between devices: 12.5 us -> none  [shards(): lax.all_gather(jnp.stack([key_local, value_local]), 'ctx', axis=1, tiled=...]
    unnamed x121 -> x134, local copies, waits for them, and re-layouts: 14.7 us -> 5.65 us
    another operation x7 -> x3, local copies, waits for them, and re-layouts: 4.63 us -> 1.67 us  [the longest x1 1.6 us: shards(): value_heads = value_all.reshape(seq_len, heads, head_dim)]
    select_n x0 -> x8, other arithmetic: none -> 2.9 us  [the longest x6 2.78 us: gathered(): jnp.where(upper, jnp.concatenate([incoming, held], axis=0), jnp.concatena...]
  transfers between devices with their start and end apart: 2 -> 13, of which waited for: 2 -> 6; matrix products, arithmetic and copies ran while one was open for 8% -> 32% of each run, Pallas kernels for 0% -> 0%
where the time goes in v3:
time: 115 us
  matrix products  37.8 us (33%)
  local copies, waits for them, and re-layouts  26.9 us (23%)
  waiting for transfers between devices  19.5 us (17%)
  starting transfers between devices  17.1 us (15%)
  other arithmetic  12.2 us (11%)
  between operations  1.36 us (1%)
    ppermute x6, waiting for transfers between devices, gathered(): incoming = lax.ppermute(held, axis, [(i, i ^ bit) for i in range(peers)])  14.1 us
    dot_general x1, matrix products, group_logits(): jnp.einsum('ihad,nhard->hinr', shifted, keys_low, preferred_element_type=...  10.9 us
    ppermute x6, starting transfers between devices, exchanged(): received.append(lax.ppermute(outgoing, axis, pairs))  10.5 us
    dot_general x1, matrix products, group_logits(): jnp.einsum('ihad,nhard->hinr', shifted, keys_high, preferred_element_type...  10.4 us
    dot_general x1, matrix products, convolved_keys(): jnp.einsum('harc,nchd->nhard', high, key_heads, preferred_element_type=jn...  8.6 us
    dot_general x1, matrix products, convolved_keys(): jnp.einsum('harc,nchd->nhard', low, key_heads, preferred_element_type=jnp...  6.06 us
    unnamed x134, local copies, waits for them, and re-layouts  5.65 us
    slice x12, local copies, waits for them, and re-layouts, toeplitz_terms(): scaled[:, :, col_lag, None, None]  5.4 us
  transfers between devices with their start and end apart: 13, of which 6 were waited for; matrix products, arithmetic and copies ran while one was open for 32% of the time, Pallas kernels for 0%

profile of v3, /device:TPU:0, one launch (start us, length us, event | category | flops | bytes accessed | tf_op | source)
XLA Modules:
  0.0 114.8 jit_solution(8580493284501071752)
XLA Ops:
  0.0 1.1 pad_maximum_fusion
  1.1 5.1 %collective-permute-start.2 = (bf16[3,32,512]{2,1,0:T(8,128)(2,1)S(1)}, bf16[3,32,512]{2,1,0:T(8,128)(2,1)S(1)}, u32[]{:S(2)}, u32[]{:S(2)}) collective-permute-start(bf16[3,32,512]{2,1,0:T(8,128)(2,1)S(1)} %get-tuple-element.45), channel_id=1, source_target_pairs={{0,3},{1,0},{2,1},{3,2},{4,7},{5,4},{6,5},{7,6},{8,11},{9,8},{10,9... | collective-permute-start | bytes 294920 | tf_op jit(solution)/shard_map/ppermute | solution.py:37
  6.2 1.0 collective-permute-start
  7.3 1.9 %slice_reduce_fusion.17 = (f32[4]{0:T(128)}, f32[4]{0:T(128)}, f32[4]{0:T(128)}, f32[4]{0:T(128)}, f32[4]{0:T(128)}, /*index=5*/f32[4]{0:T(128)}, f32[4]{0:T(128...) fusion(f32[4,6,11]{2,0,1:T(4,128)} %param.9), kind=kLoop, calls=%fused_computation.235 | loop fusion | bytes 480 | tf_op jit(solution)/shard_map/slice | solution.py:105
  9.2 0.7 broadcast_multiply_fusion
  9.9 1.2 %fusion.84 = (pred[128,1024]{0,1:T(8,128)(4,1)}, pred[128,1024]{0,1:T(8,128)(4,1)}, pred[128,1024]{0,1:T(8,128)(4,1)}, pred[128,1024]{0,1:T(8,128)(4,1)}, pred[1...) fusion(s32[128]{0:T(128)S(1)} %iota_add_fusion.1), kind=kLoop, calls=%fused_computation.118 | loop fusion | flops 917504 | bytes 786944 | tf_op jit(solution)/shard_map/ge | solution.py:136
  11.2 1.3 %subtract_compare_fusion.5 = (pred[128,8,128]{0,2,1:T(8,128)(4,1)S(1)}, pred[128,8,128]{0,2,1:T(8,128)(4,1)S(1)}, pred[128,8,128]{0,2,1:T(8,128)(4,1)S(1)}, pred...) fusion(s32[8,128]{1,0:T(8,128)S(1)} %multiply_add_fusion, ...), kind=kLoop, calls=%fused_computation.31 | loop fusion | flops 917504 | bytes 791040 | tf_op jit(solution)/shard_map/ge | solution.py:136
  13.1 0.7 copy.271
  13.8 0.7 copy.270
  14.5 0.7 copy.269
  15.2 0.7 copy.268
  15.9 0.7 copy.267
  16.6 0.7 copy.266
  17.2 0.7 copy.265
  17.9 0.8 fusion.108
  18.7 0.8 slice_reduce_fusion.18
  19.6 0.6 gather_fusion
  20.3 0.7 concatenate.68
  21.1 1.6 %collective-permute-start.3 = (bf16[1,128,512]{2,1,0:T(8,128)(2,1)S(1)}, bf16[1,128,512]{2,1,0:T(8,128)(2,1)S(1)}, u32[]{:S(2)}, u32[]{:S(2)}) collective-permute-start(bf16[1,128,512]{2,1,0:T(8,128)(2,1)S(1)} %bitcast.146), channel_id=1, source_target_pairs={{0,16},{4,20},{8,24},{12,28},{16,0},{20,4},{24,8},{28,12},{1,17},{... | collective-permute-start | bytes 393224 | tf_op jit(solution)/shard_map/ppermute | solution.py:51
  22.7 0.5 collective-permute-start.7
  23.2 1.3 %collective-permute-start.6 = (bf16[5,512]{1,0:T(8,128)(2,1)S(1)}, bf16[5,512]{1,0:T(8,128)(2,1)S(1)}, u32[]{:S(2)}, u32[]{:S(2)}) collective-permute-start(bf16[5,512]{1,0:T(8,128)(2,1)S(1)} %slice.346), channel_id=1, source_target_pairs={{0,4},{4,8},{8,12},{12,16},{16,20},{20,24},{24,28},{1,5},{5,9},{9,... | collective-permute-start | bytes 15368 | tf_op jit(solution)/shard_map/ppermute | solution.py:21
  24.5 3.9 %collective-permute-done.7 = bf16[1,128,512]{2,1,0:T(8,128)(2,1)S(1)} collective-permute-done((bf16[1,128,512]{2,1,0:T(8,128)(2,1)S(1)}, bf16[1,128,512]{2,1,0:T(8,128)(2,1)S(1)}, u32[]{:S(2)}, u32[]{:S(2)}) %collective-permute-start.7) | collective-permute-done | bytes 131104 | tf_op jit(solution)/shard_map/ppermute | solution.py:51
  28.4 1.6 %collective-permute-start.8 = (bf16[2,128,512]{2,1,0:T(8,128)(2,1)S(1)}, bf16[2,128,512]{2,1,0:T(8,128)(2,1)S(1)}, u32[]{:S(2)}, u32[]{:S(2)}) collective-permute-start(bf16[2,128,512]{2,1,0:T(8,128)(2,1)S(1)} %maximum_select_fusion.5), channel_id=1, source_target_pairs={{0,8},{4,12},{8,0},{12,4},{16,24},{20,28},{24,16},{28,20},{1,9},{5... | collective-permute-start | bytes 786440 | tf_op jit(solution)/shard_map/ppermute | solution.py:51
  30.9 4.1 %collective-permute-done.8 = bf16[2,128,512]{2,1,0:T(8,128)(2,1)S(1)} collective-permute-done((bf16[2,128,512]{2,1,0:T(8,128)(2,1)S(1)}, bf16[2,128,512]{2,1,0:T(8,128)(2,1)S(1)}, u32[]{:S(2)}, u32[]{:S(2)}) %collective-permute-start.8) | collective-permute-done | bytes 262176 | tf_op jit(solution)/shard_map/ppermute | solution.py:51
  35.2 1.6 %collective-permute-start.4 = (bf16[2,128,512]{2,1,0:T(8,128)(2,1)S(1)}, bf16[2,128,512]{2,1,0:T(8,128)(2,1)}, u32[]{:S(2)}, u32[]{:S(2)}) collective-permute-start(bf16[2,128,512]{2,1,0:T(8,128)(2,1)S(1)} %maximum_select_fusion.4), channel_id=1, source_target_pairs={{0,8},{4,12},{8,0},{12,4},{16,24},{20,28},{24,16},{28,20},{1,9},{5... | collective-permute-start | bytes 786440 | tf_op jit(solution)/shard_map/ppermute | solution.py:51
  37.4 0.6 concatenate.67
  38.0 6.1 %collective-permute-done.4 = bf16[2,128,512]{2,1,0:T(8,128)(2,1)} collective-permute-done((bf16[2,128,512]{2,1,0:T(8,128)(2,1)S(1)}, bf16[2,128,512]{2,1,0:T(8,128)(2,1)}, u32[]{:S(2)}, u32[]{:S(2)}) %collective-permute-start.4) | collective-permute-done | bytes 262176 | tf_op jit(solution)/shard_map/ppermute | solution.py:51
  44.1 1.1 maximum_select_fusion.2
  45.3 0.2 maximum_select_fusion.1
  45.6 0.3 fusion.130
  46.0 0.7 copy_dynamic-update-slice_fusion.7
  47.1 0.7 copy_dynamic-update-slice_fusion.6
  47.8 0.7 copy_dynamic-update-slice_fusion.5
  48.5 0.7 copy_dynamic-update-slice_fusion.4
  49.2 0.7 copy_dynamic-update-slice_fusion.3
  49.8 0.7 copy_dynamic-update-slice_fusion.2
  50.5 0.7 copy_dynamic-update-slice_fusion.1
  51.2 0.7 copy_dynamic-update-slice_fusion
  52.1 8.6 %fusion.17 = f32[4,8,128,6,128]{4,2,3,1,0:T(8,128)} fusion(bf16[8,138,4,128]{3,1,0,2:T(8,128)(2,1)} %copy_dynamic-update-slice_fusion, f32[4,6]{1,0:T(4,128)S(1)} %bitcast.162, f32[4,6]{1,0:T(4,128)S(1)} %bitcast.164, f32[4,6]{1,0:T(4,128)S(1)} %bitcast.166, f32[4,6]{1,0:T(4,128)S(1)} %bitcast.168, f32[4,6]{1,0:T(4,128)S(1)} %bitcast.170, ...), kind=kOutput, calls=%fused_computation.34 | convolution fusion | flops 873732096 | bytes 13908768 | tf_op jit(solution)/shard_map/harc,nchd->nhard/dot_general | solution.py:80
  60.7 6.1 %fusion.15 = f32[4,8,128,6,128]{4,2,3,1,0:T(8,128)} fusion(bf16[8,138,4,128]{3,1,0,2:T(8,128)(2,1)S(1)} %copy-done.2, f32[4,6]{1,0:T(4,128)S(1)} %bitcast.163, f32[4,6]{1,0:T(4,128)S(1)} %bitcast.165, f32[4,6]{1,0:T(4,128)S(1)} %bitcast.167, f32[4,6]{1,0:T(4,128)S(1)} %bitcast.169, f32[4,6]{1,0:T(4,128)S(1)} %bitcast.171, f32[4,6]{1,0:T(4,128)S(1)} %bitcast.173, ...), kind=kOutput, calls=%fused_computation.32 | convolution fusion | flops 874156032 | bytes 13908768 | tf_op jit(solution)/shard_map/harc,nchd->nhard/dot_general | solution.py:82
  66.7 1.4 %maximum_select_fusion = bf16[8,128,512]{2,1,0:T(8,128)(2,1)S(1)} fusion(bf16[4,128,512]{2,1,0:T(8,128)(2,1)S(1)} %maximum_select_fusion.2, bf16[4,128,512]{2,1,0:T(8,128)(2,1)} %collective-permute-done.5, pred[]{:T(512)S(6)} %ne.64), kind=kLoop, calls=%fused_computation.41 | loop fusion | flops 1572864 | bytes 2097153 | tf_op jit(solution)/shard_map/jit(_where)/select_n | solution.py:53
  68.1 0.9 copy.244
  69.0 1.6 %reshape_reshape.3 = bf16[1024,4,128]{0,2,1:T(8,128)(2,1)} reshape(bf16[2,2,2,128,512]{3,2,1,0,4:T(2,128)(2,1)S(1)} %copy.244) | data formatting | bytes 2097152 | tf_op jit(solution)/shard_map/reshape;reshape | solution.py:198
  70.8 0.1 fusion.132
  71.5 0.2 copy-done.9
  71.7 0.8 fusion.90
  73.1 10.9 %fusion.1 = f32[4,128,8,128,1]{1,3,4,2,0:T(8,128)S(1)} fusion(f32[4,8,128,6,128]{4,2,3,1,0:T(8,128)} %fusion.17, f32[4,8,128,6,128]{4,2,3,1,0:T(8,128)} %fusion.15, bf16[128,4,6,128]{3,0,2,1:T(8,128)(2,1)S(1)} %copy-done.1), kind=kOutput, calls=%fused_computation.5 | convolution fusion | flops 817889280 | bytes 28049408 | tf_op jit(solution)/shard_map/ihad,nhard->hinr/dot_general | solution.py:116
  84.4 10.4 %fusion.85 = (f32[4,128]{1,0:T(4,128)S(1)}, f32[4,128,8,128]{1,3,2,0:T(8,128)S(1)}) fusion(f32[4,128]{1,0:T(4,128)S(1)} %get-tuple-element.81, pred[128,8,128]{0,2,1:T(8,128)(4,1)S(1)} %get-tuple-element.76, f32[4,128]{1,0:T(4,128)S(1)} %get-tuple-element.74, pred[128,8,128]{0,2,1:T(8,128)(4,1)S(1)} %get-tuple-element.77, ...), kind=kOutput, calls=%fused_computation.122 | convolution fusion | flops 821558784 | bytes 30945280 | tf_op jit(solution)/shard_map/ihad,nhard->hinr/dot_general | solution.py:114
  94.9 1.3 %exponential_reduce_fusion = f32[4,128]{1,0:T(4,128)S(1)} fusion(f32[4,128]{1,0:T(4,128)S(1)} %get-tuple-element.99, f32[4,128]{1,0:T(4,128)S(1)} %get-tuple-element.81, pred[128,8,128]{0,2,1:T(8,128)(4,1)S(1)} %get-tuple-element.76, f32[4,128]{1,0:T(4,128)S(1)} %get-tuple-element.74, pred[128,8,128]{0,2,1:T(8,128)(4,1)S(1)} %get-tuple-element.77, ...), kind=kLoop, calls=%fused_computation.22 | loop fusion | flops 6815232 | bytes 2897920 | tf_op jit(solution)/shard_map/reduce_sum | solution.py:139
  96.2 1.2 %fusion.13 = f32[1,4,128,1024]{2,3,1,0:T(8,128)S(1)} fusion(f32[4,128,8,128]{1,3,2,0:T(8,128)S(1)} %get-tuple-element.100, f32[4,128]{1,0:T(4,128)S(1)} %exponential_reduce_fusion, f32[4,128]{1,0:T(4,128)S(1)} %get-tuple-element.99, f32[4,128]{1,0:T(4,128)S(1)} %get-tuple-element.81, f32[4,128]{1,0:T(4,128)S(1)} %get-tuple-element.74, ...), kind=kLoop, calls=%fused_computation.19 | loop fusion | flops 6815744 | bytes 4995072 | tf_op jit(solution)/shard_map/div | solution.py:139
  97.5 0.1 slice_bitcast_fusion.3
  97.7 1.0 copy.286
  98.7 1.0 copy.285
  99.6 1.0 copy.284
  100.7 0.2 copy.283
  101.0 1.8 %multiply_reduce_fusion = (f32[128,4]{0,1:T(4,128)S(1)}, f32[128,4,128]{0,2,1:T(8,128)S(1)}) fusion(bf16[1024,4,128]{0,2,1:T(8,128)(2,1)S(1)} %copy-done.6, f32[128,1024]{1,0:T(8,128)S(1)} %copy-done.7, f32[4]{0:T(128)S(1)} %copy-done.56, f32[128,1024]{1,0:T(8,128)S(1)} %copy-done.8, f32[4]{0:T(128)S(1)} %copy-done.57, f32[128,1024]{1,0:T(8,128)} %copy.284, ...), kind=kOutput, calls=%fused_computation.135 | convolution fusion | flops 138542592 | bytes 3409984 | tf_op jit(solution)/shard_map/hik,khd->ihd/dot_general | solution.py:146
  103.0 0.2 constant_dynamic-slice_fusion.3
  103.3 3.1 %collective-permute-start.12 = (bf16[32,512]{1,0:T(8,128)(2,1)S(1)}, bf16[32,512]{1,0:T(8,128)(2,1)S(1)}, u32[]{:S(2)}, u32[]{:S(2)}) collective-permute-start(bf16[32,512]{1,0:T(8,128)(2,1)S(1)} %copy.302), channel_id=1, source_target_pairs={{0,3},{1,0},{2,1},{3,2},{4,7},{5,4},{6,5},{7,6},{8,11},{9,8},{10,9... | collective-permute-start | bytes 98312 | tf_op jit(solution)/shard_map/ppermute | solution.py:37
  106.5 0.9 collective-permute-start.11
  107.5 0.3 collective-permute-start.10
  108.0 3.4 %collective-permute-done.11 = bf16[32,512]{1,0:T(8,128)(2,1)S(1)} collective-permute-done((bf16[32,512]{1,0:T(8,128)(2,1)S(1)}, bf16[32,512]{1,0:T(8,128)(2,1)S(1)}, u32[]{:S(2)}, u32[]{:S(2)}) %collective-permute-start.11) | collective-permute-done | bytes 32800 | tf_op jit(solution)/shard_map/ppermute | solution.py:37
  111.4 1.9 %collective-permute-done.10 = bf16[32,512]{1,0:T(8,128)(2,1)S(1)} collective-permute-done((bf16[32,512]{1,0:T(8,128)(2,1)S(1)}, bf16[32,512]{1,0:T(8,128)(2,1)S(1)}, u32[]{:S(2)}, u32[]{:S(2)}) %collective-permute-start.10) | collective-permute-done | bytes 32800 | tf_op jit(solution)/shard_map/ppermute | solution.py:37
  113.3 0.7 gather_fusion.1
  114.1 0.7 copy.304
  (200 shorter events, 5.3 us)
Async XLA Ops:
  0.0 18.7 %copy-start.34 = (f32[4,4]{1,0:T(4,128)S(1)}, f32[4,4]{1,0:T(4,128)}, u32[]{:S(2)}) copy-start(f32[4,4]{1,0:T(4,128)} %param.10) | copy-start | bytes 196
  1.1 18.4 %collective-permute-start.2 = (bf16[3,32,512]{2,1,0:T(8,128)(2,1)S(1)}, bf16[3,32,512]{2,1,0:T(8,128)(2,1)S(1)}, u32[]{:S(2)}, u32[]{:S(2)}) collective-permute-start(bf16[3,32,512]{2,1,0:T(8,128)(2,1)S(1)} %get-tuple-element.45), channel_id=1, source_target_pairs={{0,3},{1,0},{2,1},{3,2},{4,7},{5,4},{6,5},{7,6},{8,11},{9,8},{10,9... | collective-permute-start | bytes 294920 | tf_op jit(solution)/shard_map/ppermute | solution.py:37
  6.2 13.3 %collective-permute-start.1 = (bf16[3,32,512]{2,1,0:T(8,128)(2,1)S(1)}, bf16[3,32,512]{2,1,0:T(8,128)(2,1)S(1)}, u32[]{:S(2)}, u32[]{:S(2)}) collective-permute-start(bf16[3,32,512]{2,1,0:T(8,128)(2,1)S(1)} %get-tuple-element.46), channel_id=1, source_target_pairs={{0,2},{1,3},{2,0},{3,1},{4,6},{5,7},{6,4},{7,5},{8,10},{9,11},{10,... | collective-permute-start | bytes 294920 | tf_op jit(solution)/shard_map/ppermute | solution.py:37
  6.2 13.3 %collective-permute-start = (bf16[3,32,512]{2,1,0:T(8,128)(2,1)S(1)}, bf16[3,32,512]{2,1,0:T(8,128)(2,1)S(1)}, u32[]{:S(2)}, u32[]{:S(2)}) collective-permute-start(bf16[3,32,512]{2,1,0:T(8,128)(2,1)S(1)} %get-tuple-element.47), channel_id=1, source_target_pairs={{0,1},{1,2},{2,3},{3,0},{4,5},{5,6},{6,7},{7,4},{8,9},{9,10},{10,1... | collective-permute-start | bytes 294920 | tf_op jit(solution)/shard_map/ppermute | solution.py:37
  9.9 10.3 %copy-start.42 = (s32[1024]{0:T(1024)}, s32[1024]{0:T(1024)S(1)}, u32[]{:S(2)}) copy-start(s32[1024]{0:T(1024)S(1)} %pad_clamp_fusion) | copy-start | bytes 12292
  21.1 14.1 %collective-permute-start.3 = (bf16[1,128,512]{2,1,0:T(8,128)(2,1)S(1)}, bf16[1,128,512]{2,1,0:T(8,128)(2,1)S(1)}, u32[]{:S(2)}, u32[]{:S(2)}) collective-permute-start(bf16[1,128,512]{2,1,0:T(8,128)(2,1)S(1)} %bitcast.146), channel_id=1, source_target_pairs={{0,16},{4,20},{8,24},{12,28},{16,0},{20,4},{24,8},{28,12},{1,17},{... | collective-permute-start | bytes 393224 | tf_op jit(solution)/shard_map/ppermute | solution.py:51
  22.7 5.7 %collective-permute-start.7 = (bf16[1,128,512]{2,1,0:T(8,128)(2,1)S(1)}, bf16[1,128,512]{2,1,0:T(8,128)(2,1)S(1)}, u32[]{:S(2)}, u32[]{:S(2)}) collective-permute-start(bf16[1,128,512]{2,1,0:T(8,128)(2,1)S(1)} %bitcast.148), channel_id=1, source_target_pairs={{0,16},{4,20},{8,24},{12,28},{16,0},{20,4},{24,8},{28,12},{1,17},{... | collective-permute-start | bytes 393224 | tf_op jit(solution)/shard_map/ppermute | solution.py:51
  23.2 6.8 %collective-permute-start.6 = (bf16[5,512]{1,0:T(8,128)(2,1)S(1)}, bf16[5,512]{1,0:T(8,128)(2,1)S(1)}, u32[]{:S(2)}, u32[]{:S(2)}) collective-permute-start(bf16[5,512]{1,0:T(8,128)(2,1)S(1)} %slice.346), channel_id=1, source_target_pairs={{0,4},{4,8},{8,12},{12,16},{16,20},{20,24},{24,28},{1,5},{5,9},{9,... | collective-permute-start | bytes 15368 | tf_op jit(solution)/shard_map/ppermute | solution.py:21
  28.4 6.7 %collective-permute-start.8 = (bf16[2,128,512]{2,1,0:T(8,128)(2,1)S(1)}, bf16[2,128,512]{2,1,0:T(8,128)(2,1)S(1)}, u32[]{:S(2)}, u32[]{:S(2)}) collective-permute-start(bf16[2,128,512]{2,1,0:T(8,128)(2,1)S(1)} %maximum_select_fusion.5), channel_id=1, source_target_pairs={{0,8},{4,12},{8,0},{12,4},{16,24},{20,28},{24,16},{28,20},{1,9},{5... | collective-permute-start | bytes 786440 | tf_op jit(solution)/shard_map/ppermute | solution.py:51
  35.1 10.2 %collective-permute-start.9 = (bf16[4,128,512]{2,1,0:T(8,128)(2,1)S(1)}, bf16[4,128,512]{2,1,0:T(8,128)(2,1)S(1)}, u32[]{:S(2)}, u32[]{:S(2)}) collective-permute-start(bf16[4,128,512]{2,1,0:T(8,128)(2,1)S(1)} %maximum_select_fusion.3), channel_id=1, source_target_pairs={{0,4},{4,0},{8,12},{12,8},{16,20},{20,16},{24,28},{28,24},{1,5},{5... | collective-permute-start | bytes 1572872 | tf_op jit(solution)/shard_map/ppermute | solution.py:51
  35.2 8.9 %collective-permute-start.4 = (bf16[2,128,512]{2,1,0:T(8,128)(2,1)S(1)}, bf16[2,128,512]{2,1,0:T(8,128)(2,1)}, u32[]{:S(2)}, u32[]{:S(2)}) collective-permute-start(bf16[2,128,512]{2,1,0:T(8,128)(2,1)S(1)} %maximum_select_fusion.4), channel_id=1, source_target_pairs={{0,8},{4,12},{8,0},{12,4},{16,24},{20,28},{24,16},{28,20},{1,9},{5... | collective-permute-start | bytes 786440 | tf_op jit(solution)/shard_map/ppermute | solution.py:51
  38.0 7.5 %copy-start = (bf16[128,4,6,128]{3,0,2,1:T(8,128)(2,1)}, bf16[128,4,6,128]{3,0,2,1:T(8,128)(2,1)S(1)}, u32[]{:S(2)}) copy-start(bf16[128,4,6,128]{3,0,2,1:T(8,128)(2,1)S(1)} %constant_dynamic-update-slice_fusion) | copy-start | bytes 2359300
  45.2 21.5 %collective-permute-start.5 = (bf16[4,128,512]{2,1,0:T(8,128)(2,1)S(1)}, bf16[4,128,512]{2,1,0:T(8,128)(2,1)}, u32[]{:S(2)}, u32[]{:S(2)}) collective-permute-start(bf16[4,128,512]{2,1,0:T(8,128)(2,1)S(1)} %maximum_select_fusion.2), channel_id=1, source_target_pairs={{0,4},{4,0},{8,12},{12,8},{16,20},{20,16},{24,28},{28,24},{1,5},{5... | collective-permute-start | bytes 1572872 | tf_op jit(solution)/shard_map/ppermute | solution.py:51
  46.6 5.3 %copy-start.16 = (pred[128,138]{0,1:T(8,128)(4,1)S(1)}, pred[128,138]{0,1:T(8,128)(4,1)}, u32[]{:S(2)}) copy-start(pred[128,138]{0,1:T(8,128)(4,1)} %get-tuple-element.88) | copy-start | bytes 52996
  46.6 5.3 %copy-start.17 = (pred[128,138]{0,1:T(8,128)(4,1)S(1)}, pred[128,138]{0,1:T(8,128)(4,1)}, u32[]{:S(2)}) copy-start(pred[128,138]{0,1:T(8,128)(4,1)} %get-tuple-element.89) | copy-start | bytes 52996
  46.6 5.3 %copy-start.18 = (pred[128,138]{0,1:T(8,128)(4,1)S(1)}, pred[128,138]{0,1:T(8,128)(4,1)}, u32[]{:S(2)}) copy-start(pred[128,138]{0,1:T(8,128)(4,1)} %get-tuple-element.90) | copy-start | bytes 52996
  46.6 5.3 %copy-start.19 = (pred[128,138]{0,1:T(8,128)(4,1)S(1)}, pred[128,138]{0,1:T(8,128)(4,1)}, u32[]{:S(2)}) copy-start(pred[128,138]{0,1:T(8,128)(4,1)} %get-tuple-element.91) | copy-start | bytes 52996
  46.6 5.3 %copy-start.20 = (pred[128,138]{0,1:T(8,128)(4,1)S(1)}, pred[128,138]{0,1:T(8,128)(4,1)}, u32[]{:S(2)}) copy-start(pred[128,138]{0,1:T(8,128)(4,1)} %get-tuple-element.92) | copy-start | bytes 52996
  46.7 5.3 %copy-start.21 = (pred[128,138]{0,1:T(8,128)(4,1)S(1)}, pred[128,138]{0,1:T(8,128)(4,1)}, u32[]{:S(2)}) copy-start(pred[128,138]{0,1:T(8,128)(4,1)} %get-tuple-element.93) | copy-start | bytes 52996
  46.7 5.3 %copy-start.22 = (pred[128,138]{0,1:T(8,128)(4,1)S(1)}, pred[128,138]{0,1:T(8,128)(4,1)}, u32[]{:S(2)}) copy-start(pred[128,138]{0,1:T(8,128)(4,1)} %get-tuple-element.94) | copy-start | bytes 52996
  46.7 5.3 %copy-start.23 = (pred[128,138]{0,1:T(8,128)(4,1)S(1)}, pred[128,138]{0,1:T(8,128)(4,1)}, u32[]{:S(2)}) copy-start(pred[128,138]{0,1:T(8,128)(4,1)} %get-tuple-element.95) | copy-start | bytes 52996
  46.7 5.3 %copy-start.24 = (pred[128,138]{0,1:T(8,128)(4,1)S(1)}, pred[128,138]{0,1:T(8,128)(4,1)}, u32[]{:S(2)}) copy-start(pred[128,138]{0,1:T(8,128)(4,1)} %get-tuple-element.96) | copy-start | bytes 52996
  46.7 5.3 %copy-start.25 = (pred[128,138]{0,1:T(8,128)(4,1)S(1)}, pred[128,138]{0,1:T(8,128)(4,1)}, u32[]{:S(2)}) copy-start(pred[128,138]{0,1:T(8,128)(4,1)} %get-tuple-element.97) | copy-start | bytes 52996
  46.7 5.3 %copy-start.26 = (pred[128,138]{0,1:T(8,128)(4,1)S(1)}, pred[128,138]{0,1:T(8,128)(4,1)}, u32[]{:S(2)}) copy-start(pred[128,138]{0,1:T(8,128)(4,1)} %get-tuple-element.98) | copy-start | bytes 52996
  46.7 5.3 %copy-start.27 = (f32[4,6,1]{1,0,2:T(4,128)S(1)}, f32[4,6,1]{1,0,2:T(4,128)}, u32[]{:S(2)}) copy-start(f32[4,6,1]{1,0,2:T(4,128)} %copy.271) | copy-start | bytes 292
  46.7 5.3 %copy-start.28 = (f32[4,6,1]{1,0,2:T(4,128)S(1)}, f32[4,6,1]{1,0,2:T(4,128)}, u32[]{:S(2)}) copy-start(f32[4,6,1]{1,0,2:T(4,128)} %copy.270) | copy-start | bytes 292
  46.7 5.3 %copy-start.29 = (f32[4,6,1]{1,0,2:T(4,128)S(1)}, f32[4,6,1]{1,0,2:T(4,128)}, u32[]{:S(2)}) copy-start(f32[4,6,1]{1,0,2:T(4,128)} %copy.269) | copy-start | bytes 292
  46.7 5.3 %copy-start.30 = (f32[4,6,1]{1,0,2:T(4,128)S(1)}, f32[4,6,1]{1,0,2:T(4,128)}, u32[]{:S(2)}) copy-start(f32[4,6,1]{1,0,2:T(4,128)} %copy.268) | copy-start | bytes 292
  46.8 5.3 %copy-start.31 = (f32[4,6,1]{1,0,2:T(4,128)S(1)}, f32[4,6,1]{1,0,2:T(4,128)}, u32[]{:S(2)}) copy-start(f32[4,6,1]{1,0,2:T(4,128)} %copy.267) | copy-start | bytes 292
  46.8 5.3 %copy-start.32 = (f32[4,6,1]{1,0,2:T(4,128)S(1)}, f32[4,6,1]{1,0,2:T(4,128)}, u32[]{:S(2)}) copy-start(f32[4,6,1]{1,0,2:T(4,128)} %copy.266) | copy-start | bytes 292
  46.8 5.3 %copy-start.33 = (f32[4,6,1]{1,0,2:T(4,128)S(1)}, f32[4,6,1]{1,0,2:T(4,128)}, u32[]{:S(2)}) copy-start(f32[4,6,1]{1,0,2:T(4,128)} %copy.265) | copy-start | bytes 292
  52.1 8.6 %copy-start.2 = (bf16[8,138,4,128]{3,1,0,2:T(8,128)(2,1)S(1)}, bf16[8,138,4,128]{3,1,0,2:T(8,128)(2,1)}, u32[]{:S(2)}) copy-start(bf16[8,138,4,128]{3,1,0,2:T(8,128)(2,1)} %copy_dynamic-update-slice_fusion) | copy-start | bytes 3391492
  71.1 1.8 %copy-start.1 = (bf16[128,4,6,128]{3,0,2,1:T(8,128)(2,1)S(1)}, bf16[128,4,6,128]{3,0,2,1:T(8,128)(2,1)}, u32[]{:S(2)}) copy-start(bf16[128,4,6,128]{3,0,2,1:T(8,128)(2,1)} %copy-done) | copy-start | bytes 2359300
  72.9 11.1 %copy-start.36 = (f32[4]{0:T(128)S(1)}, f32[4]{0:T(128)}, u32[]{:S(2)}) copy-start(f32[4]{0:T(128)} %get-tuple-element.11) | copy-start | bytes 52
  72.9 11.1 %copy-start.37 = (f32[4]{0:T(128)S(1)}, f32[4]{0:T(128)}, u32[]{:S(2)}) copy-start(f32[4]{0:T(128)} %get-tuple-element.12) | copy-start | bytes 52
  72.9 11.1 %copy-start.38 = (f32[4]{0:T(128)S(1)}, f32[4]{0:T(128)}, u32[]{:S(2)}) copy-start(f32[4]{0:T(128)} %get-tuple-element.13) | copy-start | bytes 52
  72.9 11.1 %copy-start.39 = (f32[4]{0:T(128)S(1)}, f32[4]{0:T(128)}, u32[]{:S(2)}) copy-start(f32[4]{0:T(128)} %get-tuple-element.16) | copy-start | bytes 52
  72.9 11.1 %copy-start.40 = (f32[4]{0:T(128)S(1)}, f32[4]{0:T(128)}, u32[]{:S(2)}) copy-start(f32[4]{0:T(128)} %get-tuple-element.17) | copy-start | bytes 52
  72.9 11.1 %copy-start.41 = (f32[4]{0:T(128)S(1)}, f32[4]{0:T(128)}, u32[]{:S(2)}) copy-start(f32[4]{0:T(128)} %get-tuple-element.20) | copy-start | bytes 52
  73.0 11.1 %copy-start.43 = (f32[4]{0:T(128)S(1)}, f32[4]{0:T(128)}, u32[]{:S(2)}) copy-start(f32[4]{0:T(128)} %get-tuple-element.15) | copy-start | bytes 52
  73.0 11.1 %copy-start.44 = (f32[4]{0:T(128)S(1)}, f32[4]{0:T(128)}, u32[]{:S(2)}) copy-start(f32[4]{0:T(128)} %get-tuple-element.19) | copy-start | bytes 52
  73.0 11.1 %copy-start.45 = (f32[4]{0:T(128)S(1)}, f32[4]{0:T(128)}, u32[]{:S(2)}) copy-start(f32[4]{0:T(128)} %get-tuple-element.22) | copy-start | bytes 52
  73.0 11.1 %copy-start.46 = (f32[4]{0:T(128)S(1)}, f32[4]{0:T(128)}, u32[]{:S(2)}) copy-start(f32[4]{0:T(128)} %get-tuple-element.24) | copy-start | bytes 52
  73.0 11.2 %copy-start.48 = (f32[4]{0:T(128)S(1)}, f32[4]{0:T(128)}, u32[]{:S(2)}) copy-start(f32[4]{0:T(128)} %get-tuple-element.10) | copy-start | bytes 52
  73.0 11.2 %copy-start.49 = (f32[4]{0:T(128)S(1)}, f32[4]{0:T(128)}, u32[]{:S(2)}) copy-start(f32[4]{0:T(128)} %get-tuple-element.14) | copy-start | bytes 52
  73.0 11.2 %copy-start.50 = (f32[4]{0:T(128)S(1)}, f32[4]{0:T(128)}, u32[]{:S(2)}) copy-start(f32[4]{0:T(128)} %get-tuple-element.18) | copy-start | bytes 52
  73.0 11.2 %copy-start.51 = (f32[4]{0:T(128)S(1)}, f32[4]{0:T(128)}, u32[]{:S(2)}) copy-start(f32[4]{0:T(128)} %get-tuple-element.21) | copy-start | bytes 52
  73.0 11.2 %copy-start.52 = (f32[4]{0:T(128)S(1)}, f32[4]{0:T(128)}, u32[]{:S(2)}) copy-start(f32[4]{0:T(128)} %get-tuple-element.23) | copy-start | bytes 52
  73.0 11.3 %copy-start.3 = (pred[128,8,128]{0,2,1:T(8,128)(4,1)S(1)}, pred[128,8,128]{0,2,1:T(8,128)(4,1)}, u32[]{:S(2)}) copy-start(pred[128,8,128]{0,2,1:T(8,128)(4,1)} %get-tuple-element.78) | copy-start | bytes 393220
  73.1 11.3 %copy-start.4 = (pred[128,8,128]{0,2,1:T(8,128)(4,1)S(1)}, pred[128,8,128]{0,2,1:T(8,128)(4,1)}, u32[]{:S(2)}) copy-start(pred[128,8,128]{0,2,1:T(8,128)(4,1)} %get-tuple-element.79) | copy-start | bytes 393220
  73.1 11.3 %copy-start.5 = (pred[128,8,128]{0,2,1:T(8,128)(4,1)S(1)}, pred[128,8,128]{0,2,1:T(8,128)(4,1)}, u32[]{:S(2)}) copy-start(pred[128,8,128]{0,2,1:T(8,128)(4,1)} %get-tuple-element.80) | copy-start | bytes 393220
  94.8 1.3 %copy-start.10 = (pred[128,1024]{0,1:T(8,128)(4,1)S(1)}, pred[128,1024]{0,1:T(8,128)(4,1)}, u32[]{:S(2)}) copy-start(pred[128,1024]{0,1:T(8,128)(4,1)} %get-tuple-element.82) | copy-start | bytes 393220
  94.9 1.3 %copy-start.11 = (pred[128,1024]{0,1:T(8,128)(4,1)S(1)}, pred[128,1024]{0,1:T(8,128)(4,1)}, u32[]{:S(2)}) copy-start(pred[128,1024]{0,1:T(8,128)(4,1)} %get-tuple-element.83) | copy-start | bytes 393220
  97.6 3.3 %copy-start.6 = (bf16[1024,4,128]{0,2,1:T(8,128)(2,1)S(1)}, bf16[1024,4,128]{0,2,1:T(8,128)(2,1)}, u32[]{:S(2)}) copy-start(bf16[1024,4,128]{0,2,1:T(8,128)(2,1)} %reshape_reshape.3) | copy-start | bytes 3145732
  97.6 3.3 %copy-start.55 = (f32[4]{0:T(128)S(1)}, f32[4]{0:T(128)}, u32[]{:S(2)}) copy-start(f32[4]{0:T(128)} %get-tuple-element.25) | copy-start | bytes 52
  97.6 3.3 %copy-start.56 = (f32[4]{0:T(128)S(1)}, f32[4]{0:T(128)}, u32[]{:S(2)}) copy-start(f32[4]{0:T(128)} %get-tuple-element.26) | copy-start | bytes 52
  97.6 3.3 %copy-start.57 = (f32[4]{0:T(128)S(1)}, f32[4]{0:T(128)}, u32[]{:S(2)}) copy-start(f32[4]{0:T(128)} %get-tuple-element.27) | copy-start | bytes 52
  97.7 3.3 %copy-start.58 = (f32[4]{0:T(128)S(1)}, f32[4]{0:T(128)}, u32[]{:S(2)}) copy-start(f32[4]{0:T(128)} %get-tuple-element.28) | copy-start | bytes 52
  98.7 2.3 %copy-start.7 = (f32[128,1024]{1,0:T(8,128)S(1)}, f32[128,1024]{1,0:T(8,128)}, u32[]{:S(2)}) copy-start(f32[128,1024]{1,0:T(8,128)} %copy.286) | copy-start | bytes 1572868
  101.0 1.9 %copy-start.47 = (f32[512]{0:T(512)S(1)}, f32[512]{0:T(512)}, u32[]{:S(2)}) copy-start(f32[512]{0:T(512)} %param.11) | copy-start | bytes 6148
  102.8 11.2 %copy-start.54 = (pred[4]{0:T(512)(128)(4,1)S(1)}, pred[4]{0:T(512)(128)(4,1)}, u32[]{:S(2)}) copy-start(pred[4]{0:T(512)(128)(4,1)} %copy-done.53) | copy-start | bytes 16
  103.3 4.7 %collective-permute-start.12 = (bf16[32,512]{1,0:T(8,128)(2,1)S(1)}, bf16[32,512]{1,0:T(8,128)(2,1)S(1)}, u32[]{:S(2)}, u32[]{:S(2)}) collective-permute-start(bf16[32,512]{1,0:T(8,128)(2,1)S(1)} %copy.302), channel_id=1, source_target_pairs={{0,3},{1,0},{2,1},{3,2},{4,7},{5,4},{6,5},{7,6},{8,11},{9,8},{10,9... | collective-permute-start | bytes 98312 | tf_op jit(solution)/shard_map/ppermute | solution.py:37
  106.5 4.9 %collective-permute-start.11 = (bf16[32,512]{1,0:T(8,128)(2,1)S(1)}, bf16[32,512]{1,0:T(8,128)(2,1)S(1)}, u32[]{:S(2)}, u32[]{:S(2)}) collective-permute-start(bf16[32,512]{1,0:T(8,128)(2,1)S(1)} %copy.301), channel_id=1, source_target_pairs={{0,2},{1,3},{2,0},{3,1},{4,6},{5,7},{6,4},{7,5},{8,10},{9,11},{10,... | collective-permute-start | bytes 98312 | tf_op jit(solution)/shard_map/ppermute | solution.py:37
  107.5 5.8 %collective-permute-start.10 = (bf16[32,512]{1,0:T(8,128)(2,1)S(1)}, bf16[32,512]{1,0:T(8,128)(2,1)S(1)}, u32[]{:S(2)}, u32[]{:S(2)}) collective-permute-start(bf16[32,512]{1,0:T(8,128)(2,1)S(1)} %copy.300), channel_id=1, source_target_pairs={{0,1},{1,2},{2,3},{3,0},{4,5},{5,6},{6,7},{7,4},{8,9},{9,10},{10,1... | collective-permute-start | bytes 98312 | tf_op jit(solution)/shard_map/ppermute | solution.py:37
  (8 other events, 9.1 us)

commit v4 on v3

--- a/solution.py
+++ b/solution.py
@@ -1,6 +1,7 @@
 import jax
 import jax.numpy as jnp
 from jax import lax
+from jax.experimental import pallas as pl
 from jax.sharding import PartitionSpec as P
 
 GROUP = 4
@@ -8,7 +9,6 @@
 KCONV = 11
 KEY_BLOCK = 128
 ROW_CHUNK = 128
-KEY_GROUP = 8
 
 
 lowest = -1e30
@@ -60,27 +60,75 @@
 
 
 def toeplitz_terms(score_kernel, head_dim):
-    col_lead = KCONV - 1
     scaled = score_kernel * head_dim ** (-0.5)
     lag = (
         lax.iota(jnp.int32, KEY_BLOCK)[:, None]
-        + col_lead
-        - lax.iota(jnp.int32, KEY_BLOCK + col_lead)[None, :]
+        + KEY_BLOCK
+        - lax.iota(jnp.int32, 2 * KEY_BLOCK)[None, :]
     )
     toeplitz = jnp.zeros(score_kernel.shape[:2] + lag.shape, jnp.float32)
     for col_lag in range(KCONV):
         toeplitz = jnp.where(lag == col_lag, scaled[:, :, col_lag, None, None], toeplitz)
+    toeplitz = toeplitz.reshape((toeplitz.shape[0], -1, toeplitz.shape[3]))
     return split_bf16(toeplitz)
 
 
-def convolved_keys(key_windows, terms):
+def logits_kernel(query_ref, high_ref, low_ref, before_ref, current_ref, out_ref):
+    window = pl.program_id(1)
+    before = jnp.where(
+        window > 0, before_ref[...], jnp.zeros(before_ref.shape, before_ref.dtype)
+    )
+    current = current_ref[...]
+    high = high_ref[0]
+    low = low_ref[0]
+    conv_keys = (
+        jnp.dot(high[:, :KEY_BLOCK], before, preferred_element_type=jnp.float32)
+        + jnp.dot(high[:, KEY_BLOCK:], current, preferred_element_type=jnp.float32)
+        + jnp.dot(low[:, :KEY_BLOCK], before, preferred_element_type=jnp.float32)
+        + jnp.dot(low[:, KEY_BLOCK:], current, preferred_element_type=jnp.float32)
+    )
+    keys_high = conv_keys.astype(jnp.bfloat16)
+    keys_low = (conv_keys - keys_high.astype(jnp.float32)).astype(jnp.bfloat16)
+    query = query_ref[0]
+    head_dim = current.shape[1]
+    dims = (((1,), (1,)), ((), ()))
+    acc = jnp.zeros(out_ref.shape[1:], jnp.float32)
+    for row_lag in range(QCONV):
+        part = query[:, row_lag * head_dim : (row_lag + 1) * head_dim]
+        acc = acc + lax.dot_general(
+            part,
+            keys_high[row_lag * KEY_BLOCK : (row_lag + 1) * KEY_BLOCK],
+            dims,
+            preferred_element_type=jnp.float32,
+        )
+        acc = acc + lax.dot_general(
+            part,
+            keys_low[row_lag * KEY_BLOCK : (row_lag + 1) * KEY_BLOCK],
+            dims,
+            preferred_element_type=jnp.float32,
+        )
+    out_ref[0] = acc
+
+
+def conv_logits(shifted_heads, terms, key_all):
     high, low = terms
-    heads = high.shape[0]
-    key_heads = key_windows.reshape(key_windows.shape[:2] + (heads, -1))
-    conv_keys = jnp.einsum(
-        "harc,nchd->nhard", high, key_heads, preferred_element_type=jnp.float32
-    ) + jnp.einsum("harc,nchd->nhard", low, key_heads, preferred_element_type=jnp.float32)
-    return split_bf16(conv_keys)
+    heads, row_count, contract = shifted_heads.shape
+    seq_len, width = key_all.shape
+    head_dim = width // heads
+    windows = seq_len // KEY_BLOCK
+    return pl.pallas_call(
+        logits_kernel,
+        grid=(heads, windows),
+        in_specs=[
+            pl.BlockSpec((1, row_count, contract), lambda h, n: (h, 0, 0)),
+            pl.BlockSpec((1,) + high.shape[1:], lambda h, n: (h, 0, 0)),
+            pl.BlockSpec((1,) + low.shape[1:], lambda h, n: (h, 0, 0)),
+            pl.BlockSpec((KEY_BLOCK, head_dim), lambda h, n: (jnp.maximum(n - 1, 0), h)),
+            pl.BlockSpec((KEY_BLOCK, head_dim), lambda h, n: (n, h)),
+        ],
+        out_specs=pl.BlockSpec((1, row_count, KEY_BLOCK), lambda h, n: (h, 0, n)),
+        out_shape=jax.ShapeDtypeStruct((heads, row_count, seq_len), jnp.float32),
+    )(shifted_heads, high, low, key_all, key_all)
 
 
 def band_terms(query_rows, query_first, key_flat, score_kernel):
@@ -109,26 +157,11 @@
     return jnp.stack(band)
 
 
-def group_logits(shifted, key_windows, terms):
-    keys_high, keys_low = convolved_keys(key_windows, terms)
-    return jnp.einsum(
-        "ihad,nhard->hinr", shifted, keys_high, preferred_element_type=jnp.float32
-    ) + jnp.einsum("ihad,nhard->hinr", shifted, keys_low, preferred_element_type=jnp.float32)
-
-
-def attend_chunk(shifted, band, query_first, key_windows, terms, value_heads, head_mixing):
+def attend_chunk(shifted, band, query_first, key_all, terms, value_heads, head_mixing):
     row_count, heads = shifted.shape[:2]
     seq_len = value_heads.shape[0]
-    window_count = key_windows.shape[0]
-    if window_count <= KEY_GROUP:
-        convolved = group_logits(shifted, key_windows, terms)
-    else:
-        grouped_windows = key_windows.reshape(
-            (window_count // KEY_GROUP, KEY_GROUP) + key_windows.shape[1:]
-        )
-        convolved = lax.map(lambda windows: group_logits(shifted, windows, terms), grouped_windows)
-        convolved = jnp.moveaxis(convolved, 0, 2)
-    convolved = convolved.reshape(heads, row_count, seq_len)
+    shifted_heads = jnp.transpose(shifted, (1, 0, 2, 3)).reshape((heads, row_count, -1))
+    convolved = conv_logits(shifted_heads, terms, key_all)
     query_pos = query_first + lax.iota(jnp.int32, row_count)
     gap = query_pos[:, None] - lax.iota(jnp.int32, seq_len)[None, :]
     for lag in range(QCONV - 1):
@@ -170,7 +203,6 @@
     shard_rows = query_local.shape[0]
     width = query_local.shape[1]
     row_lead = QCONV - 1
-    col_lead = KCONV - 1
     heads = score_kernel.shape[0]
     head_dim = width // heads
     ctx_place = lax.axis_index("ctx")
@@ -180,13 +212,6 @@
     key_all = gathered(key_local, "ctx").reshape((-1, width))
     value_all = gathered(value_local, "ctx").reshape((-1, width))
     seq_len = key_all.shape[0]
-    key_pad = jnp.concatenate([jnp.zeros((col_lead, width), key_all.dtype), key_all], axis=0)
-    key_windows = jnp.stack(
-        [
-            key_pad[start : start + KEY_BLOCK + col_lead]
-            for start in range(0, seq_len, KEY_BLOCK)
-        ]
-    )
     terms = toeplitz_terms(score_kernel, head_dim)
     edge = jnp.zeros((8, width), key_all.dtype)
     key_flat = jnp.concatenate([edge, key_all, edge], axis=0)
@@ -199,7 +224,7 @@
     chunk = min(ROW_CHUNK * KEY_BLOCK * 8 // seq_len, shard_rows)
     if chunk == shard_rows:
         weighted = attend_chunk(
-            shifted, band, query_first, key_windows, terms, value_heads, head_mixing
+            shifted, band, query_first, key_all, terms, value_heads, head_mixing
         )
     else:
         chunks = shard_rows // chunk
@@ -210,7 +235,7 @@
                 lax.dynamic_slice_in_dim(shifted, start, chunk, 0),
                 lax.dynamic_slice_in_dim(band, start, chunk, 2),
                 query_first + start,
-                key_windows,
+                key_all,
                 terms,
                 value_heads,
                 head_mixing,

time: 115 us -> 116 us (level)
  matrix products: 37.8 us -> 2.01 us
  Pallas kernels: 0 us -> 35.5 us
  other arithmetic: 12.2 us -> 28.4 us
  local copies, waits for them, and re-layouts: 26.9 us -> 16.5 us
  waiting for transfers between devices: 19.5 us -> 14 us
    dot_general x4 -> x0, matrix products: 36 us -> none  [the longest x1 10.9 us: group_logits(): jnp.einsum('ihad,nhard->hinr', shifted, keys_low, preferred_element_type=...]
    pallas_call x0 -> x1, Pallas kernels: none -> 35.5 us  [conv_logits(): pl.pallas_call(logits_kernel, grid=(heads, windows), in_specs=[pl.BlockSp...]
    convert_element_type x0 -> x2, other arithmetic: none -> 14 us  [split_bf16(): return (high.astype(jnp.bfloat16), low.astype(jnp.bfloat16))]
    div x1, other arithmetic: 1.24 us -> 6.39 us  [attend_chunk(): probabilities = expd / jnp.sum(expd, axis=2, keepdims=True)]
    slice x12, local copies, waits for them, and re-layouts: 5.4 us -> 1.33 us  [toeplitz_terms(): scaled[:, :, col_lag, None, None]]
    unnamed x134 -> x69, local copies, waits for them, and re-layouts: 5.65 us -> 2.37 us
    ppermute x6, waiting for transfers between devices: 5.39 us -> 2.56 us  [exchanged(): received.append(lax.ppermute(outgoing, axis, pairs))]
    ppermute x6, waiting for transfers between devices: 14.1 us -> 11.5 us  [gathered(): incoming = lax.ppermute(held, axis, [(i, i ^ bit) for i in range(peers)])]
  transfers between devices with their start and end apart: 13 -> 13, of which waited for: 6 -> 5; matrix products, arithmetic and copies ran while one was open for 32% -> 32% of each run, Pallas kernels for 0% -> 31%
where the time goes in v4:
time: 116 us
  Pallas kernels  35.5 us (31%)
  other arithmetic  28.4 us (24%)
  starting transfers between devices  18 us (16%)
  local copies, waits for them, and re-layouts  16.5 us (14%)
  waiting for transfers between devices  14 us (12%)
  matrix products  2.01 us (2%)
    pallas_call x1, Pallas kernels, conv_logits(): pl.pallas_call(logits_kernel, grid=(heads, windows), in_specs=[pl.BlockSp...  35.5 us
    convert_element_type x2, other arithmetic, split_bf16(): return (high.astype(jnp.bfloat16), low.astype(jnp.bfloat16))  14 us
    ppermute x6, waiting for transfers between devices, gathered(): incoming = lax.ppermute(held, axis, [(i, i ^ bit) for i in range(peers)])  11.5 us
    ppermute x6, starting transfers between devices, exchanged(): received.append(lax.ppermute(outgoing, axis, pairs))  11 us
    div x1, other arithmetic, attend_chunk(): probabilities = expd / jnp.sum(expd, axis=2, keepdims=True)  6.39 us
    ppermute x6, starting transfers between devices, gathered(): incoming = lax.ppermute(held, axis, [(i, i ^ bit) for i in range(peers)])  5.55 us
    select_n x6, other arithmetic, gathered(): jnp.where(upper, jnp.concatenate([incoming, held], axis=0), jnp.concatena...  2.87 us
    ppermute x6, waiting for transfers between devices, exchanged(): received.append(lax.ppermute(outgoing, axis, pairs))  2.56 us
  transfers between devices with their start and end apart: 13, of which 5 were waited for; matrix products, arithmetic and copies ran while one was open for 32% of the time, Pallas kernels for 31%

profile of v4, /device:TPU:0, one launch (start us, length us, event | category | flops | bytes accessed | tf_op | source)
XLA Modules:
  0.0 115.5 jit_solution(1471355935737184692)
XLA Ops:
  0.0 1.1 pad_maximum_fusion
  1.1 3.1 %collective-permute-start = (bf16[3,32,512]{2,1,0:T(8,128)(2,1)S(1)}, bf16[3,32,512]{2,1,0:T(8,128)(2,1)S(1)}, u32[]{:S(2)}, u32[]{:S(2)}) collective-permute-start(bf16[3,32,512]{2,1,0:T(8,128)(2,1)S(1)} %get-tuple-element.39), channel_id=1, source_target_pairs={{0,1},{1,2},{2,3},{3,0},{4,5},{5,6},{6,7},{7,4},{8,9},{9,10},{10,1... | collective-permute-start | bytes 294920 | tf_op jit(solution)/shard_map/ppermute | solution.py:37
  4.2 2.6 %collective-permute-start.1 = (bf16[3,32,512]{2,1,0:T(8,128)(2,1)S(1)}, bf16[3,32,512]{2,1,0:T(8,128)(2,1)S(1)}, u32[]{:S(2)}, u32[]{:S(2)}) collective-permute-start(bf16[3,32,512]{2,1,0:T(8,128)(2,1)S(1)} %get-tuple-element.38), channel_id=1, source_target_pairs={{0,2},{1,3},{2,0},{3,1},{4,6},{5,7},{6,4},{7,5},{8,10},{9,11},{10,... | collective-permute-start | bytes 294920 | tf_op jit(solution)/shard_map/ppermute | solution.py:37
  6.8 1.3 %collective-permute-start.2 = (bf16[3,32,512]{2,1,0:T(8,128)(2,1)S(1)}, bf16[3,32,512]{2,1,0:T(8,128)(2,1)S(1)}, u32[]{:S(2)}, u32[]{:S(2)}) collective-permute-start(bf16[3,32,512]{2,1,0:T(8,128)(2,1)S(1)} %get-tuple-element.37), channel_id=1, source_target_pairs={{0,3},{1,0},{2,1},{3,2},{4,7},{5,4},{6,5},{7,6},{8,11},{9,8},{10,9... | collective-permute-start | bytes 294920 | tf_op jit(solution)/shard_map/ppermute | solution.py:37
  8.2 1.9 %slice_reduce_fusion.17 = (f32[4]{0:T(128)}, f32[4]{0:T(128)S(1)}, f32[4]{0:T(128)S(1)}, f32[4]{0:T(128)}, f32[4]{0:T(128)}, /*index=5*/f32[4]{0:T(128)}, f32[4]...) fusion(f32[4,6,11]{2,0,1:T(4,128)} %param.9), kind=kLoop, calls=%fused_computation.173 | loop fusion | bytes 480 | tf_op jit(solution)/shard_map/slice | solution.py:153
  10.1 0.7 broadcast_multiply_fusion
  10.8 0.1 fusion.64
  10.9 0.1 copy.183
  11.1 0.1 copy.182
  11.3 0.1 copy.181
  11.5 0.1 copy.180
  11.7 0.1 copy.179
  11.9 0.1 copy.178
  12.8 0.3 fusion.40
  13.1 0.1 copy.173
  14.0 7.0 %fusion.2.low_ref = bf16[4,768,256]{2,1,0:T(8,128)(2,1)} fusion(f32[4,768]{1,0:T(4,128)S(1)} %get-tuple-element.87, f32[4,768]{1,0:T(4,128)S(1)} %get-tuple-element.88, f32[4,768]{1,0:T(4,128)S(1)} %get-tuple-element.89, f32[4,768]{1,0:T(4,128)S(1)} %get-tuple-element.90, f32[4,768]{1,0:T(4,128)S(1)} %get-tuple-element.91, ...), kind=kLoop, calls=%fused_computation.6 | loop fusion | flops 11010048 | bytes 3870720 | tf_op jit(solution)/shard_map/convert_element_type | solution.py:27
  21.1 7.0 %reduce-precision_convert_fusion.high_ref = bf16[4,768,256]{2,1,0:T(8,128)(2,1)} fusion(f32[4,768]{1,0:T(4,128)S(1)} %get-tuple-element.87, f32[4,768]{1,0:T(4,128)S(1)} %get-tuple-element.88, f32[4,768]{1,0:T(4,128)S(1)} %get-tuple-element.89, f32[4,768]{1,0:T(4,128)S(1)} %get-tuple-element.90, f32[4,768]{1,0:T(4,128)S(1)} %get-tuple-element.91, ...), kind=kLoop, calls=%fused_computation.5 | loop fusion | flops 10223616 | bytes 3870720 | tf_op jit(solution)/shard_map/convert_element_type | solution.py:27
  28.1 1.3 %fusion.16 = (pred[128,1024]{1,0:T(8,128)(4,1)}, pred[128,1024]{1,0:T(8,128)(4,1)}, pred[128,1024]{1,0:T(8,128)(4,1)}, pred[128,1024]{1,0:T(8,128)(4,1)}, pred[1...) fusion(s32[128]{0:T(128)S(1)} %iota_add_fusion.1), kind=kLoop, calls=%fused_computation.43 | loop fusion | flops 917504 | bytes 786944 | tf_op jit(solution)/shard_map/ge | solution.py:169
  29.5 0.6 gather_fusion
  30.2 1.6 %collective-permute-start.7 = (bf16[1,128,512]{2,1,0:T(8,128)(2,1)S(1)}, bf16[1,128,512]{2,1,0:T(8,128)(2,1)S(1)}, u32[]{:S(2)}, u32[]{:S(2)}) collective-permute-start(bf16[1,128,512]{2,1,0:T(8,128)(2,1)S(1)} %bitcast.174), channel_id=1, source_target_pairs={{0,16},{4,20},{8,24},{12,28},{16,0},{20,4},{24,8},{28,12},{1,17},{... | collective-permute-start | bytes 393224 | tf_op jit(solution)/shard_map/ppermute | solution.py:51
  31.8 0.8 slice_reduce_fusion.18
  32.7 1.5 %collective-permute-start.6 = (bf16[5,512]{1,0:T(8,128)(2,1)S(1)}, bf16[5,512]{1,0:T(8,128)(2,1)S(1)}, u32[]{:S(2)}, u32[]{:S(2)}) collective-permute-start(bf16[5,512]{1,0:T(8,128)(2,1)S(1)} %slice.314), channel_id=1, source_target_pairs={{0,4},{4,8},{8,12},{12,16},{16,20},{20,24},{24,28},{1,5},{5,9},{9,... | collective-permute-start | bytes 15368 | tf_op jit(solution)/shard_map/ppermute | solution.py:21
  34.2 1.2 %collective-permute-start.3 = (bf16[1,128,512]{2,1,0:T(8,128)(2,1)S(1)}, bf16[1,128,512]{2,1,0:T(8,128)(2,1)S(1)}, u32[]{:S(2)}, u32[]{:S(2)}) collective-permute-start(bf16[1,128,512]{2,1,0:T(8,128)(2,1)S(1)} %bitcast.172), channel_id=1, source_target_pairs={{0,16},{4,20},{8,24},{12,28},{16,0},{20,4},{24,8},{28,12},{1,17},{... | collective-permute-start | bytes 393224 | tf_op jit(solution)/shard_map/ppermute | solution.py:51
  35.5 1.6 %collective-permute-start.8 = (bf16[2,128,512]{2,1,0:T(8,128)(2,1)S(1)}, bf16[2,128,512]{2,1,0:T(8,128)(2,1)S(1)}, u32[]{:S(2)}, u32[]{:S(2)}) collective-permute-start(bf16[2,128,512]{2,1,0:T(8,128)(2,1)S(1)} %maximum_select_fusion.5), channel_id=1, source_target_pairs={{0,8},{4,12},{8,0},{12,4},{16,24},{20,28},{24,16},{28,20},{1,9},{5... | collective-permute-start | bytes 786440 | tf_op jit(solution)/shard_map/ppermute | solution.py:51
  37.0 0.1 pad_maximum_fusion.3
  37.2 0.1 copy.162
  37.3 0.1 copy.167
  37.4 0.1 copy.163
  37.6 0.1 copy.168
  37.9 0.1 copy.164
  38.0 0.1 copy.169
  38.1 6.2 %collective-permute-done.8 = bf16[2,128,512]{2,1,0:T(8,128)(2,1)S(1)} collective-permute-done((bf16[2,128,512]{2,1,0:T(8,128)(2,1)S(1)}, bf16[2,128,512]{2,1,0:T(8,128)(2,1)S(1)}, u32[]{:S(2)}, u32[]{:S(2)}) %collective-permute-start.8) | collective-permute-done | bytes 262176 | tf_op jit(solution)/shard_map/ppermute | solution.py:51
  44.5 0.2 collective-permute-start.9
  44.7 0.9 collective-permute-start.4
  45.7 0.1 copy.165
  45.8 0.1 copy.170
  46.0 0.1 copy.166
  46.1 0.1 copy.171
  46.4 0.6 copy.172
  47.0 1.2 %copy.185.query_ref = bf16[4,128,768]{2,1,0:T(8,128)(2,1)} copy(bf16[4,128,768]{1,2,0:T(8,128)(2,1)S(1)} %bitcast.146) | data formatting | bytes 1572864 | tf_op jit(solution)/shard_map/reshape | solution.py:163
  48.2 5.2 %collective-permute-done.4 = bf16[2,128,512]{2,1,0:T(8,128)(2,1)} collective-permute-done((bf16[2,128,512]{2,1,0:T(8,128)(2,1)S(1)}, bf16[2,128,512]{2,1,0:T(8,128)(2,1)}, u32[]{:S(2)}, u32[]{:S(2)}) %collective-permute-start.4) | collective-permute-done | bytes 262176 | tf_op jit(solution)/shard_map/ppermute | solution.py:51
  53.5 1.2 %maximum_select_fusion.2 = bf16[4,128,512]{2,1,0:T(8,128)(2,1)S(1)} fusion(bf16[2,128,512]{2,1,0:T(8,128)(2,1)S(1)} %maximum_select_fusion.4, bf16[2,128,512]{2,1,0:T(8,128)(2,1)} %collective-permute-done.4, pred[]{:T(512)S(6)} %ne.65), kind=kLoop, calls=%fused_computation.35 | loop fusion | flops 786432 | bytes 1048577 | tf_op jit(solution)/shard_map/jit(_where)/select_n | solution.py:53
  54.7 0.2 maximum_select_fusion.1
  55.1 0.1 fusion.63
  55.3 0.6 copy-done
  56.4 0.8 fusion.22
  57.8 35.5 %shard_map.64 = f32[4,128,1024]{2,1,0:T(8,128)} custom-call(bf16[4,128,768]{2,1,0:T(8,128)(2,1)} %copy.185.query_ref, bf16[4,768,256]{2,1,0:T(8,128)(2,1)} %reduce-precision_convert_fusion.high_ref, bf16[4,768,256]{2,1,0:T(8,128)(2,1)} %fusion.2.low_ref, bf16[1024,512]{1,0:T(8,128)(2,1)} %bitcast.141, bf16[1024,512]{1,0:T(8,128)(2,1)} %bitcast.142), custom_call_target="tpu_custom_call" | custom-call | tf_op jit(solution)/shard_map/pallas_call | solution.py:119
  93.7 6.4 %divide_bitcast_fusion = f32[1,4,128,1024]{3,2,1,0:T(8,128)S(1)} fusion(f32[4,128,1024]{2,1,0:T(8,128)} %shard_map.64, f32[4,128]{1,0:T(4,128)S(1)} %get-tuple-element.67, f32[4,128]{1,0:T(4,128)S(1)} %get-tuple-element.66, f32[4,128]{1,0:T(4,128)S(1)} %get-tuple-element.65, f32[4,128]{1,0:T(4,128)S(1)} %subtract_bitcast_fusion.3, f32[4,128]{1,0:T(4,128)S(1)} %fusion.56, ...), kind=kOutput, calls=%fused_computation.9 | output fusion | flops 6818814 | bytes 4990976 | tf_op jit(solution)/shard_map/div | solution.py:172
  100.1 1.2 %slice_bitcast_fusion.3 = (f32[128,1024]{1,0:T(8,128)S(1)}, f32[128,1024]{1,0:T(8,128)}, f32[128,1024]{1,0:T(8,128)}, f32[128,1024]{1,0:T(8,128)}) fusion(f32[1,4,128,1024]{3,2,1,0:T(8,128)S(1)} %divide_bitcast_fusion), kind=kLoop, calls=%fused_computation.34 | loop fusion | bytes 4194304 | tf_op jit(solution)/shard_map/mul | solution.py:177
  101.3 1.4 %maximum_select_fusion = bf16[8,128,512]{2,1,0:T(8,128)(2,1)S(1)} fusion(bf16[4,128,512]{2,1,0:T(8,128)(2,1)S(1)} %maximum_select_fusion.2, bf16[4,128,512]{2,1,0:T(8,128)(2,1)} %collective-permute-done.5, pred[]{:T(512)S(6)} %ne.64), kind=kLoop, calls=%fused_computation.16 | loop fusion | flops 1572864 | bytes 2097153 | tf_op jit(solution)/shard_map/jit(_where)/select_n | solution.py:53
  102.7 0.9 copy.161
  103.7 0.8 reshape_reshape.3
  104.5 0.2 copy-done.1
  104.7 2.0 %multiply_reduce_fusion = (f32[128,4]{0,1:T(4,128)S(1)}, f32[128,4,128]{0,2,1:T(8,128)S(1)}) fusion(bf16[1024,4,128]{0,2,1:T(8,128)(2,1)S(1)} %reshape_reshape.3, f32[128,1024]{1,0:T(8,128)S(1)} %copy-done.1, f32[4]{0:T(128)S(1)} %copy-done.21, f32[128,1024]{1,0:T(8,128)} %get-tuple-element.31, f32[4]{0:T(128)S(1)} %copy-done.22, ...), kind=kOutput, calls=%fused_computation.60 | convolution fusion | flops 138542592 | bytes 3409984 | tf_op jit(solution)/shard_map/hik,khd->ihd/dot_general | solution.py:179
  106.8 0.1 multiply_convert_fusion
  106.9 0.2 constant_dynamic-slice_fusion.3
  107.2 0.7 collective-permute-start.10
  108.0 0.4 collective-permute-start.11
  108.5 2.9 %collective-permute-start.12 = (bf16[32,512]{1,0:T(8,128)(2,1)S(1)}, bf16[32,512]{1,0:T(8,128)(2,1)S(1)}, u32[]{:S(2)}, u32[]{:S(2)}) collective-permute-start(bf16[32,512]{1,0:T(8,128)(2,1)S(1)} %copy.198), channel_id=1, source_target_pairs={{0,3},{1,0},{2,1},{3,2},{4,7},{5,4},{6,5},{7,6},{8,11},{9,8},{10,9... | collective-permute-start | bytes 98312 | tf_op jit(solution)/shard_map/ppermute | solution.py:37
  111.5 1.8 %collective-permute-done.10 = bf16[32,512]{1,0:T(8,128)(2,1)S(1)} collective-permute-done((bf16[32,512]{1,0:T(8,128)(2,1)S(1)}, bf16[32,512]{1,0:T(8,128)(2,1)S(1)}, u32[]{:S(2)}, u32[]{:S(2)}) %collective-permute-start.10) | collective-permute-done | bytes 32800 | tf_op jit(solution)/shard_map/ppermute | solution.py:37
  113.3 0.6 collective-permute-done.11
  113.8 0.2 collective-permute-done.12
  114.1 0.7 gather_fusion.1
  114.8 0.7 copy.200
  (135 shorter events, 4.7 us)
Async XLA Ops:
  1.1 28.3 %collective-permute-start = (bf16[3,32,512]{2,1,0:T(8,128)(2,1)S(1)}, bf16[3,32,512]{2,1,0:T(8,128)(2,1)S(1)}, u32[]{:S(2)}, u32[]{:S(2)}) collective-permute-start(bf16[3,32,512]{2,1,0:T(8,128)(2,1)S(1)} %get-tuple-element.39), channel_id=1, source_target_pairs={{0,1},{1,2},{2,3},{3,0},{4,5},{5,6},{6,7},{7,4},{8,9},{9,10},{10,1... | collective-permute-start | bytes 294920 | tf_op jit(solution)/shard_map/ppermute | solution.py:37
  4.2 25.2 %collective-permute-start.1 = (bf16[3,32,512]{2,1,0:T(8,128)(2,1)S(1)}, bf16[3,32,512]{2,1,0:T(8,128)(2,1)S(1)}, u32[]{:S(2)}, u32[]{:S(2)}) collective-permute-start(bf16[3,32,512]{2,1,0:T(8,128)(2,1)S(1)} %get-tuple-element.38), channel_id=1, source_target_pairs={{0,2},{1,3},{2,0},{3,1},{4,6},{5,7},{6,4},{7,5},{8,10},{9,11},{10,... | collective-permute-start | bytes 294920 | tf_op jit(solution)/shard_map/ppermute | solution.py:37
  6.8 22.7 %collective-permute-start.2 = (bf16[3,32,512]{2,1,0:T(8,128)(2,1)S(1)}, bf16[3,32,512]{2,1,0:T(8,128)(2,1)S(1)}, u32[]{:S(2)}, u32[]{:S(2)}) collective-permute-start(bf16[3,32,512]{2,1,0:T(8,128)(2,1)S(1)} %get-tuple-element.37), channel_id=1, source_target_pairs={{0,3},{1,0},{2,1},{3,2},{4,7},{5,4},{6,5},{7,6},{8,11},{9,8},{10,9... | collective-permute-start | bytes 294920 | tf_op jit(solution)/shard_map/ppermute | solution.py:37
  28.1 3.8 %copy-start.2 = (f32[4,4]{1,0:T(4,128)S(1)}, f32[4,4]{1,0:T(4,128)}, u32[]{:S(2)}) copy-start(f32[4,4]{1,0:T(4,128)} %param.10) | copy-start | bytes 196
  28.1 4.6 %copy-start.7 = (s32[1024]{0:T(1024)}, s32[1024]{0:T(1024)S(1)}, u32[]{:S(2)}) copy-start(s32[1024]{0:T(1024)S(1)} %pad_clamp_fusion) | copy-start | bytes 12292
  29.4 4.8 %copy-start.18 = (pred[4]{0:T(512)(128)(4,1)}, pred[4]{0:T(512)(128)(4,1)S(1)}, u32[]{:S(2)}) copy-start(pred[4]{0:T(512)(128)(4,1)S(1)} %compare_and_fusion) | copy-start | bytes 16
  30.2 5.2 %collective-permute-start.7 = (bf16[1,128,512]{2,1,0:T(8,128)(2,1)S(1)}, bf16[1,128,512]{2,1,0:T(8,128)(2,1)S(1)}, u32[]{:S(2)}, u32[]{:S(2)}) collective-permute-start(bf16[1,128,512]{2,1,0:T(8,128)(2,1)S(1)} %bitcast.174), channel_id=1, source_target_pairs={{0,16},{4,20},{8,24},{12,28},{16,0},{20,4},{24,8},{28,12},{1,17},{... | collective-permute-start | bytes 393224 | tf_op jit(solution)/shard_map/ppermute | solution.py:51
  32.7 4.3 %collective-permute-start.6 = (bf16[5,512]{1,0:T(8,128)(2,1)S(1)}, bf16[5,512]{1,0:T(8,128)(2,1)S(1)}, u32[]{:S(2)}, u32[]{:S(2)}) collective-permute-start(bf16[5,512]{1,0:T(8,128)(2,1)S(1)} %slice.314), channel_id=1, source_target_pairs={{0,4},{4,8},{8,12},{12,16},{16,20},{20,24},{24,28},{1,5},{5,9},{9,... | collective-permute-start | bytes 15368 | tf_op jit(solution)/shard_map/ppermute | solution.py:21
  34.2 10.5 %collective-permute-start.3 = (bf16[1,128,512]{2,1,0:T(8,128)(2,1)S(1)}, bf16[1,128,512]{2,1,0:T(8,128)(2,1)S(1)}, u32[]{:S(2)}, u32[]{:S(2)}) collective-permute-start(bf16[1,128,512]{2,1,0:T(8,128)(2,1)S(1)} %bitcast.172), channel_id=1, source_target_pairs={{0,16},{4,20},{8,24},{12,28},{16,0},{20,4},{24,8},{28,12},{1,17},{... | collective-permute-start | bytes 393224 | tf_op jit(solution)/shard_map/ppermute | solution.py:51
  35.5 8.9 %collective-permute-start.8 = (bf16[2,128,512]{2,1,0:T(8,128)(2,1)S(1)}, bf16[2,128,512]{2,1,0:T(8,128)(2,1)S(1)}, u32[]{:S(2)}, u32[]{:S(2)}) collective-permute-start(bf16[2,128,512]{2,1,0:T(8,128)(2,1)S(1)} %maximum_select_fusion.5), channel_id=1, source_target_pairs={{0,8},{4,12},{8,0},{12,4},{16,24},{20,28},{24,16},{28,20},{1,9},{5... | collective-permute-start | bytes 786440 | tf_op jit(solution)/shard_map/ppermute | solution.py:51
  44.5 10.2 %collective-permute-start.9 = (bf16[4,128,512]{2,1,0:T(8,128)(2,1)S(1)}, bf16[4,128,512]{2,1,0:T(8,128)(2,1)S(1)}, u32[]{:S(2)}, u32[]{:S(2)}) collective-permute-start(bf16[4,128,512]{2,1,0:T(8,128)(2,1)S(1)} %maximum_select_fusion.3), channel_id=1, source_target_pairs={{0,4},{4,0},{8,12},{12,8},{16,20},{20,16},{24,28},{28,24},{1,5},{5... | collective-permute-start | bytes 1572872 | tf_op jit(solution)/shard_map/ppermute | solution.py:51
  44.7 8.7 %collective-permute-start.4 = (bf16[2,128,512]{2,1,0:T(8,128)(2,1)S(1)}, bf16[2,128,512]{2,1,0:T(8,128)(2,1)}, u32[]{:S(2)}, u32[]{:S(2)}) collective-permute-start(bf16[2,128,512]{2,1,0:T(8,128)(2,1)S(1)} %maximum_select_fusion.4), channel_id=1, source_target_pairs={{0,8},{4,12},{8,0},{12,4},{16,24},{20,28},{24,16},{28,20},{1,9},{5... | collective-permute-start | bytes 786440 | tf_op jit(solution)/shard_map/ppermute | solution.py:51
  54.6 46.7 %collective-permute-start.5 = (bf16[4,128,512]{2,1,0:T(8,128)(2,1)S(1)}, bf16[4,128,512]{2,1,0:T(8,128)(2,1)}, u32[]{:S(2)}, u32[]{:S(2)}) collective-permute-start(bf16[4,128,512]{2,1,0:T(8,128)(2,1)S(1)} %maximum_select_fusion.2), channel_id=1, source_target_pairs={{0,4},{4,0},{8,12},{12,8},{16,20},{20,16},{24,28},{28,24},{1,5},{5... | collective-permute-start | bytes 1572872 | tf_op jit(solution)/shard_map/ppermute | solution.py:51
  55.0 1.0 copy-start
  57.6 35.7 %copy-start.3 = (f32[4]{0:T(128)S(1)}, f32[4]{0:T(128)}, u32[]{:S(2)}) copy-start(f32[4]{0:T(128)} %get-tuple-element.13) | copy-start | bytes 52
  57.6 35.7 %copy-start.4 = (f32[4]{0:T(128)S(1)}, f32[4]{0:T(128)}, u32[]{:S(2)}) copy-start(f32[4]{0:T(128)} %get-tuple-element.16) | copy-start | bytes 52
  57.7 35.7 %copy-start.5 = (f32[4]{0:T(128)S(1)}, f32[4]{0:T(128)}, u32[]{:S(2)}) copy-start(f32[4]{0:T(128)} %get-tuple-element.17) | copy-start | bytes 52
  57.7 35.7 %copy-start.6 = (f32[4]{0:T(128)S(1)}, f32[4]{0:T(128)}, u32[]{:S(2)}) copy-start(f32[4]{0:T(128)} %get-tuple-element.20) | copy-start | bytes 52
  57.7 35.7 %copy-start.8 = (f32[4]{0:T(128)S(1)}, f32[4]{0:T(128)}, u32[]{:S(2)}) copy-start(f32[4]{0:T(128)} %get-tuple-element.15) | copy-start | bytes 52
  57.7 35.7 %copy-start.9 = (f32[4]{0:T(128)S(1)}, f32[4]{0:T(128)}, u32[]{:S(2)}) copy-start(f32[4]{0:T(128)} %get-tuple-element.19) | copy-start | bytes 52
  57.7 35.7 %copy-start.10 = (f32[4]{0:T(128)S(1)}, f32[4]{0:T(128)}, u32[]{:S(2)}) copy-start(f32[4]{0:T(128)} %get-tuple-element.22) | copy-start | bytes 52
  57.7 35.7 %copy-start.11 = (f32[4]{0:T(128)S(1)}, f32[4]{0:T(128)}, u32[]{:S(2)}) copy-start(f32[4]{0:T(128)} %get-tuple-element.24) | copy-start | bytes 52
  57.7 35.8 %copy-start.13 = (f32[4]{0:T(128)S(1)}, f32[4]{0:T(128)}, u32[]{:S(2)}) copy-start(f32[4]{0:T(128)} %get-tuple-element.10) | copy-start | bytes 52
  57.7 35.8 %copy-start.14 = (f32[4]{0:T(128)S(1)}, f32[4]{0:T(128)}, u32[]{:S(2)}) copy-start(f32[4]{0:T(128)} %get-tuple-element.14) | copy-start | bytes 52
  57.7 35.8 %copy-start.15 = (f32[4]{0:T(128)S(1)}, f32[4]{0:T(128)}, u32[]{:S(2)}) copy-start(f32[4]{0:T(128)} %get-tuple-element.18) | copy-start | bytes 52
  57.7 35.8 %copy-start.16 = (f32[4]{0:T(128)S(1)}, f32[4]{0:T(128)}, u32[]{:S(2)}) copy-start(f32[4]{0:T(128)} %get-tuple-element.21) | copy-start | bytes 52
  57.8 35.8 %copy-start.17 = (f32[4]{0:T(128)S(1)}, f32[4]{0:T(128)}, u32[]{:S(2)}) copy-start(f32[4]{0:T(128)} %get-tuple-element.23) | copy-start | bytes 52
  102.7 1.8 %copy-start.20 = (f32[4]{0:T(128)S(1)}, f32[4]{0:T(128)}, u32[]{:S(2)}) copy-start(f32[4]{0:T(128)} %get-tuple-element.25) | copy-start | bytes 52
  102.7 1.8 %copy-start.21 = (f32[4]{0:T(128)S(1)}, f32[4]{0:T(128)}, u32[]{:S(2)}) copy-start(f32[4]{0:T(128)} %get-tuple-element.26) | copy-start | bytes 52
  102.7 1.8 %copy-start.22 = (f32[4]{0:T(128)S(1)}, f32[4]{0:T(128)}, u32[]{:S(2)}) copy-start(f32[4]{0:T(128)} %get-tuple-element.27) | copy-start | bytes 52
  102.7 1.8 %copy-start.23 = (f32[4]{0:T(128)S(1)}, f32[4]{0:T(128)}, u32[]{:S(2)}) copy-start(f32[4]{0:T(128)} %get-tuple-element.28) | copy-start | bytes 52
  103.7 1.0 copy-start.1
  104.7 2.0 %copy-start.12 = (f32[512]{0:T(512)S(1)}, f32[512]{0:T(512)}, u32[]{:S(2)}) copy-start(f32[512]{0:T(512)} %param.11) | copy-start | bytes 6148
  106.7 8.0 %copy-start.19 = (pred[4]{0:T(512)(128)(4,1)S(1)}, pred[4]{0:T(512)(128)(4,1)}, u32[]{:S(2)}) copy-start(pred[4]{0:T(512)(128)(4,1)} %copy-done.18) | copy-start | bytes 16
  107.2 6.1 %collective-permute-start.10 = (bf16[32,512]{1,0:T(8,128)(2,1)S(1)}, bf16[32,512]{1,0:T(8,128)(2,1)S(1)}, u32[]{:S(2)}, u32[]{:S(2)}) collective-permute-start(bf16[32,512]{1,0:T(8,128)(2,1)S(1)} %copy.196), channel_id=1, source_target_pairs={{0,1},{1,2},{2,3},{3,0},{4,5},{5,6},{6,7},{7,4},{8,9},{9,10},{10,1... | collective-permute-start | bytes 98312 | tf_op jit(solution)/shard_map/ppermute | solution.py:37
  108.0 5.8 %collective-permute-start.11 = (bf16[32,512]{1,0:T(8,128)(2,1)S(1)}, bf16[32,512]{1,0:T(8,128)(2,1)S(1)}, u32[]{:S(2)}, u32[]{:S(2)}) collective-permute-start(bf16[32,512]{1,0:T(8,128)(2,1)S(1)} %copy.197), channel_id=1, source_target_pairs={{0,2},{1,3},{2,0},{3,1},{4,6},{5,7},{6,4},{7,5},{8,10},{9,11},{10,... | collective-permute-start | bytes 98312 | tf_op jit(solution)/shard_map/ppermute | solution.py:37
  108.5 5.5 %collective-permute-start.12 = (bf16[32,512]{1,0:T(8,128)(2,1)S(1)}, bf16[32,512]{1,0:T(8,128)(2,1)S(1)}, u32[]{:S(2)}, u32[]{:S(2)}) collective-permute-start(bf16[32,512]{1,0:T(8,128)(2,1)S(1)} %copy.198), channel_id=1, source_target_pairs={{0,3},{1,0},{2,1},{3,2},{4,7},{5,4},{6,5},{7,6},{8,11},{9,8},{10,9... | collective-permute-start | bytes 98312 | tf_op jit(solution)/shard_map/ppermute | solution.py:37

commit v5 on v4

--- a/solution.py
+++ b/solution.py
@@ -2,6 +2,7 @@
 import jax.numpy as jnp
 from jax import lax
 from jax.experimental import pallas as pl
+from jax.experimental.pallas import tpu as pltpu
 from jax.sharding import PartitionSpec as P
 
 GROUP = 4
@@ -59,76 +60,72 @@
     return jnp.transpose(held, tuple(reversed(range(bits))) + tuple(range(bits, held.ndim)))
 
 
-def toeplitz_terms(score_kernel, head_dim):
-    scaled = score_kernel * head_dim ** (-0.5)
-    lag = (
-        lax.iota(jnp.int32, KEY_BLOCK)[:, None]
-        + KEY_BLOCK
-        - lax.iota(jnp.int32, 2 * KEY_BLOCK)[None, :]
-    )
-    toeplitz = jnp.zeros(score_kernel.shape[:2] + lag.shape, jnp.float32)
-    for col_lag in range(KCONV):
-        toeplitz = jnp.where(lag == col_lag, scaled[:, :, col_lag, None, None], toeplitz)
-    toeplitz = toeplitz.reshape((toeplitz.shape[0], -1, toeplitz.shape[3]))
-    return split_bf16(toeplitz)
-
-
-def logits_kernel(query_ref, high_ref, low_ref, before_ref, current_ref, out_ref):
+def logits_kernel(taps_ref, query_ref, before_ref, current_ref, out_ref, high_ref, low_ref):
+    head = pl.program_id(0)
     window = pl.program_id(1)
+
+    @pl.when(window == 0)
+    def _():
+        lag = (
+            lax.broadcasted_iota(jnp.int32, (2 * KEY_BLOCK, KEY_BLOCK), 1)
+            + KEY_BLOCK
+            - lax.broadcasted_iota(jnp.int32, (2 * KEY_BLOCK, KEY_BLOCK), 0)
+        )
+        for row_lag in range(QCONV):
+            toeplitz = jnp.zeros(lag.shape, jnp.float32)
+            for col_lag in range(KCONV):
+                tap = taps_ref[(head * QCONV + row_lag) * KCONV + col_lag]
+                toeplitz = jnp.where(lag == col_lag, tap, toeplitz)
+            high = toeplitz.astype(jnp.bfloat16)
+            low = (toeplitz - high.astype(jnp.float32)).astype(jnp.bfloat16)
+            high_ref[:, row_lag * KEY_BLOCK : (row_lag + 1) * KEY_BLOCK] = high
+            low_ref[:, row_lag * KEY_BLOCK : (row_lag + 1) * KEY_BLOCK] = low
+
     before = jnp.where(
         window > 0, before_ref[...], jnp.zeros(before_ref.shape, before_ref.dtype)
     )
     current = current_ref[...]
-    high = high_ref[0]
-    low = low_ref[0]
     conv_keys = (
-        jnp.dot(high[:, :KEY_BLOCK], before, preferred_element_type=jnp.float32)
-        + jnp.dot(high[:, KEY_BLOCK:], current, preferred_element_type=jnp.float32)
-        + jnp.dot(low[:, :KEY_BLOCK], before, preferred_element_type=jnp.float32)
-        + jnp.dot(low[:, KEY_BLOCK:], current, preferred_element_type=jnp.float32)
+        jnp.dot(before, high_ref[:KEY_BLOCK], preferred_element_type=jnp.float32)
+        + jnp.dot(current, high_ref[KEY_BLOCK:], preferred_element_type=jnp.float32)
+        + jnp.dot(before, low_ref[:KEY_BLOCK], preferred_element_type=jnp.float32)
+        + jnp.dot(current, low_ref[KEY_BLOCK:], preferred_element_type=jnp.float32)
     )
     keys_high = conv_keys.astype(jnp.bfloat16)
     keys_low = (conv_keys - keys_high.astype(jnp.float32)).astype(jnp.bfloat16)
     query = query_ref[0]
-    head_dim = current.shape[1]
-    dims = (((1,), (1,)), ((), ()))
+    head_dim = current.shape[0]
     acc = jnp.zeros(out_ref.shape[1:], jnp.float32)
     for row_lag in range(QCONV):
         part = query[:, row_lag * head_dim : (row_lag + 1) * head_dim]
-        acc = acc + lax.dot_general(
-            part,
-            keys_high[row_lag * KEY_BLOCK : (row_lag + 1) * KEY_BLOCK],
-            dims,
-            preferred_element_type=jnp.float32,
-        )
-        acc = acc + lax.dot_general(
-            part,
-            keys_low[row_lag * KEY_BLOCK : (row_lag + 1) * KEY_BLOCK],
-            dims,
-            preferred_element_type=jnp.float32,
-        )
+        cols = slice(row_lag * KEY_BLOCK, (row_lag + 1) * KEY_BLOCK)
+        acc = acc + jnp.dot(part, keys_high[:, cols], preferred_element_type=jnp.float32)
+        acc = acc + jnp.dot(part, keys_low[:, cols], preferred_element_type=jnp.float32)
     out_ref[0] = acc
 
 
-def conv_logits(shifted_heads, terms, key_all):
-    high, low = terms
+def conv_logits(shifted_heads, score_kernel, keys_t):
     heads, row_count, contract = shifted_heads.shape
-    seq_len, width = key_all.shape
+    width, seq_len = keys_t.shape
     head_dim = width // heads
     windows = seq_len // KEY_BLOCK
+    taps = (score_kernel * head_dim ** (-0.5)).reshape(-1)
     return pl.pallas_call(
         logits_kernel,
         grid=(heads, windows),
         in_specs=[
+            pl.BlockSpec(memory_space=pltpu.SMEM),
             pl.BlockSpec((1, row_count, contract), lambda h, n: (h, 0, 0)),
-            pl.BlockSpec((1,) + high.shape[1:], lambda h, n: (h, 0, 0)),
-            pl.BlockSpec((1,) + low.shape[1:], lambda h, n: (h, 0, 0)),
-            pl.BlockSpec((KEY_BLOCK, head_dim), lambda h, n: (jnp.maximum(n - 1, 0), h)),
-            pl.BlockSpec((KEY_BLOCK, head_dim), lambda h, n: (n, h)),
+            pl.BlockSpec((head_dim, KEY_BLOCK), lambda h, n: (h, jnp.maximum(n - 1, 0))),
+            pl.BlockSpec((head_dim, KEY_BLOCK), lambda h, n: (h, n)),
         ],
         out_specs=pl.BlockSpec((1, row_count, KEY_BLOCK), lambda h, n: (h, 0, n)),
         out_shape=jax.ShapeDtypeStruct((heads, row_count, seq_len), jnp.float32),
-    )(shifted_heads, high, low, key_all, key_all)
+        scratch_shapes=[
+            pltpu.VMEM((2 * KEY_BLOCK, QCONV * KEY_BLOCK), jnp.bfloat16),
+            pltpu.VMEM((2 * KEY_BLOCK, QCONV * KEY_BLOCK), jnp.bfloat16),
+        ],
+    )(taps, shifted_heads, keys_t, keys_t)
 
 
 def band_terms(query_rows, query_first, key_flat, score_kernel):
@@ -157,11 +154,11 @@
     return jnp.stack(band)
 
 
-def attend_chunk(shifted, band, query_first, key_all, terms, value_heads, head_mixing):
+def attend_chunk(shifted, band, query_first, keys_t, score_kernel, value_heads, head_mixing):
     row_count, heads = shifted.shape[:2]
     seq_len = value_heads.shape[0]
     shifted_heads = jnp.transpose(shifted, (1, 0, 2, 3)).reshape((heads, row_count, -1))
-    convolved = conv_logits(shifted_heads, terms, key_all)
+    convolved = conv_logits(shifted_heads, score_kernel, keys_t)
     query_pos = query_first + lax.iota(jnp.int32, row_count)
     gap = query_pos[:, None] - lax.iota(jnp.int32, seq_len)[None, :]
     for lag in range(QCONV - 1):
@@ -212,7 +209,7 @@
     key_all = gathered(key_local, "ctx").reshape((-1, width))
     value_all = gathered(value_local, "ctx").reshape((-1, width))
     seq_len = key_all.shape[0]
-    terms = toeplitz_terms(score_kernel, head_dim)
+    keys_t = key_all.T
     edge = jnp.zeros((8, width), key_all.dtype)
     key_flat = jnp.concatenate([edge, key_all, edge], axis=0)
     band = band_terms(query_ext, query_first, key_flat, score_kernel)
@@ -224,7 +221,7 @@
     chunk = min(ROW_CHUNK * KEY_BLOCK * 8 // seq_len, shard_rows)
     if chunk == shard_rows:
         weighted = attend_chunk(
-            shifted, band, query_first, key_all, terms, value_heads, head_mixing
+            shifted, band, query_first, keys_t, score_kernel, value_heads, head_mixing
         )
     else:
         chunks = shard_rows // chunk
@@ -235,8 +232,8 @@
                 lax.dynamic_slice_in_dim(shifted, start, chunk, 0),
                 lax.dynamic_slice_in_dim(band, start, chunk, 2),
                 query_first + start,
-                key_all,
-                terms,
+                keys_t,
+                score_kernel,
                 value_heads,
                 head_mixing,
             )

time: 116 us -> 99.9 us (0.86); the launches traced: 116 us -> 98 us
  other arithmetic: 28.4 us -> 13.7 us
  Pallas kernels: 35.5 us -> 29.5 us
  local copies, waits for them, and re-layouts: 16.5 us -> 18.1 us
    convert_element_type x2 -> x0, other arithmetic: 14 us -> none  [split_bf16(): return (high.astype(jnp.bfloat16), low.astype(jnp.bfloat16))]
    pallas_call x1, Pallas kernels: 35.5 us -> 29.5 us  [conv_logits(): pl.pallas_call(logits_kernel, grid=(heads, windows), in_specs=[pl.BlockSp...]
    concatenate x0 -> x1, local copies, waits for them, and re-layouts: none -> 1.93 us  [shards(): key_flat = jnp.concatenate([edge, key_all, edge], axis=0)]
    ppermute x6, waiting for transfers between devices: 2.56 us -> 4.26 us  [exchanged(): received.append(lax.ppermute(outgoing, axis, pairs))]
    reshape x0 -> x2, local copies, waits for them, and re-layouts: none -> 1.44 us  [the longest x1 0.76 us: shards(): key_all = gathered(key_local, 'ctx').reshape((-1, width))]
    slice x13 -> x0, local copies, waits for them, and re-layouts: 1.34 us -> none  [the longest x12 1.33 us: toeplitz_terms(): scaled[:, :, col_lag, None, None]]
    unnamed x69 -> x58, local copies, waits for them, and re-layouts: 2.37 us -> 1.14 us
  transfers between devices with their start and end apart: 13 -> 13, of which waited for: 5 -> 6; matrix products, arithmetic and copies ran while one was open for 32% -> 25% of each run, Pallas kernels for 31% -> 30%
where the time goes in v5:
time: 99.9 us; the launch traced here: 98 us
  Pallas kernels  29.5 us (30%)
  starting transfers between devices  19 us (19%)
  local copies, waits for them, and re-layouts  18.1 us (18%)
  waiting for transfers between devices  15 us (15%)
  other arithmetic  13.7 us (14%)
  matrix products  2.01 us (2%)
    pallas_call x1, Pallas kernels, conv_logits(): pl.pallas_call(logits_kernel, grid=(heads, windows), in_specs=[pl.BlockSp...  29.5 us
    ppermute x6, starting transfers between devices, exchanged(): received.append(lax.ppermute(outgoing, axis, pairs))  12.1 us
    ppermute x6, waiting for transfers between devices, gathered(): incoming = lax.ppermute(held, axis, [(i, i ^ bit) for i in range(peers)])  10.7 us
    div x1, other arithmetic, attend_chunk(): probabilities = expd / jnp.sum(expd, axis=2, keepdims=True)  6.39 us
    ppermute x6, starting transfers between devices, gathered(): incoming = lax.ppermute(held, axis, [(i, i ^ bit) for i in range(peers)])  5.33 us
    ppermute x6, waiting for transfers between devices, exchanged(): received.append(lax.ppermute(outgoing, axis, pairs))  4.26 us
    select_n x6, other arithmetic, gathered(): jnp.where(upper, jnp.concatenate([incoming, held], axis=0), jnp.concatena...  2.82 us
    dot_general x1, matrix products, attend_chunk(): jnp.einsum('hik,khd->ihd', mixed_probs, value_heads, preferred_element_ty...  2.01 us
  transfers between devices with their start and end apart: 13, of which 6 were waited for; matrix products, arithmetic and copies ran while one was open for 25% of the time, Pallas kernels for 30%

profile of v5, /device:TPU:0, one launch (start us, length us, event | category | flops | bytes accessed | tf_op | source)
XLA Modules:
  0.0 98.0 jit_solution(17051805797227452619)
XLA Ops:
  0.0 1.1 %pad_maximum_fusion = bf16[3,32,2048]{2,1,0:T(8,128)(2,1)S(1)} fusion(bf16[1,32,2048]{2,1,0:T(8,128)(2,1)} %bitcast.105, bf16[1,32,2048]{2,1,0:T(8,128)(2,1)} %bitcast.106, bf16[1,32,2048]{2,1,0:T(8,128)(2,1)} %bitcast.107), kind=kLoop, calls=%fused_computation.42 | loop fusion | flops 393216 | bytes 786432 | tf_op jit(solution)/shard_map/stack | solution.py:190
  1.1 3.1 %collective-permute-start = (bf16[3,32,512]{2,1,0:T(8,128)(2,1)S(1)}, bf16[3,32,512]{2,1,0:T(8,128)(2,1)S(1)}, u32[]{:S(2)}, u32[]{:S(2)}) collective-permute-start(bf16[3,32,512]{2,1,0:T(8,128)(2,1)S(1)} %get-tuple-element.44), channel_id=1, source_target_pairs={{0,1},{1,2},{2,3},{3,0},{4,5},{5,6},{6,7},{7,4},{8,9},{9,10},{10,1... | collective-permute-start | bytes 294920 | tf_op jit(solution)/shard_map/ppermute | solution.py:38
  4.2 2.6 %collective-permute-start.1 = (bf16[3,32,512]{2,1,0:T(8,128)(2,1)S(1)}, bf16[3,32,512]{2,1,0:T(8,128)(2,1)S(1)}, u32[]{:S(2)}, u32[]{:S(2)}) collective-permute-start(bf16[3,32,512]{2,1,0:T(8,128)(2,1)S(1)} %get-tuple-element.43), channel_id=1, source_target_pairs={{0,2},{1,3},{2,0},{3,1},{4,6},{5,7},{6,4},{7,5},{8,10},{9,11},{10,... | collective-permute-start | bytes 294920 | tf_op jit(solution)/shard_map/ppermute | solution.py:38
  6.8 1.3 %collective-permute-start.2 = (bf16[3,32,512]{2,1,0:T(8,128)(2,1)S(1)}, bf16[3,32,512]{2,1,0:T(8,128)(2,1)S(1)}, u32[]{:S(2)}, u32[]{:S(2)}) collective-permute-start(bf16[3,32,512]{2,1,0:T(8,128)(2,1)S(1)} %get-tuple-element.42), channel_id=1, source_target_pairs={{0,3},{1,0},{2,1},{3,2},{4,7},{5,4},{6,5},{7,6},{8,11},{9,8},{10,9... | collective-permute-start | bytes 294920 | tf_op jit(solution)/shard_map/ppermute | solution.py:38
  8.2 1.9 %slice_reduce_fusion.17 = (f32[4]{0:T(128)}, f32[4]{0:T(128)S(1)}, f32[4]{0:T(128)S(1)}, f32[4]{0:T(128)}, f32[4]{0:T(128)}, /*index=5*/f32[4]{0:T(128)}, f32[4]...) fusion(f32[4,6,11]{2,0,1:T(4,128)} %param.9), kind=kLoop, calls=%fused_computation.133 | loop fusion | bytes 480 | tf_op jit(solution)/shard_map/slice | solution.py:150
  10.1 0.7 broadcast_multiply_fusion
  10.8 1.3 %fusion.20 = (pred[128,1024]{1,0:T(8,128)(4,1)}, pred[128,1024]{1,0:T(8,128)(4,1)}, pred[128,1024]{1,0:T(8,128)(4,1)}, pred[128,1024]{1,0:T(8,128)(4,1)}, pred[1...) fusion(s32[128]{0:T(128)S(1)} %iota_add_fusion), kind=kLoop, calls=%fused_computation.41 | loop fusion | flops 917504 | bytes 786944 | tf_op jit(solution)/shard_map/ge | solution.py:166
  12.2 1.2 %collective-permute-done.1 = bf16[3,32,512]{2,1,0:T(8,128)(2,1)S(1)} collective-permute-done((bf16[3,32,512]{2,1,0:T(8,128)(2,1)S(1)}, bf16[3,32,512]{2,1,0:T(8,128)(2,1)S(1)}, u32[]{:S(2)}, u32[]{:S(2)}) %collective-permute-start.1) | collective-permute-done | bytes 98336 | tf_op jit(solution)/shard_map/ppermute | solution.py:38
  13.5 0.6 gather_fusion
  14.1 0.1 select_bitcast_fusion
  14.2 1.6 %collective-permute-start.7 = (bf16[1,128,512]{2,1,0:T(8,128)(2,1)S(1)}, bf16[1,128,512]{2,1,0:T(8,128)(2,1)S(1)}, u32[]{:S(2)}, u32[]{:S(2)}) collective-permute-start(bf16[1,128,512]{2,1,0:T(8,128)(2,1)S(1)} %bitcast.98), channel_id=1, source_target_pairs={{0,16},{4,20},{8,24},{12,28},{16,0},{20,4},{24,8},{28,12},{1,17},{... | collective-permute-start | bytes 393224 | tf_op jit(solution)/shard_map/ppermute | solution.py:52
  15.8 0.7 slice_reduce_fusion.18
  16.5 0.7 reshape.179.taps_ref
  17.3 0.1 copy.94
  17.5 1.5 %collective-permute-start.6 = (bf16[5,512]{1,0:T(8,128)(2,1)S(1)}, bf16[5,512]{1,0:T(8,128)(2,1)S(1)}, u32[]{:S(2)}, u32[]{:S(2)}) collective-permute-start(bf16[5,512]{1,0:T(8,128)(2,1)S(1)} %slice.270), channel_id=1, source_target_pairs={{0,4},{4,8},{8,12},{12,16},{16,20},{20,24},{24,28},{1,5},{5,9},{9,... | collective-permute-start | bytes 15368 | tf_op jit(solution)/shard_map/ppermute | solution.py:22
  19.0 1.0 %collective-permute-start.3 = (bf16[1,128,512]{2,1,0:T(8,128)(2,1)S(1)}, bf16[1,128,512]{2,1,0:T(8,128)(2,1)S(1)}, u32[]{:S(2)}, u32[]{:S(2)}) collective-permute-start(bf16[1,128,512]{2,1,0:T(8,128)(2,1)S(1)} %bitcast.96), channel_id=1, source_target_pairs={{0,16},{4,20},{8,24},{12,28},{16,0},{20,4},{24,8},{28,12},{1,17},{... | collective-permute-start | bytes 393224 | tf_op jit(solution)/shard_map/ppermute | solution.py:52
  20.1 1.6 %collective-permute-start.8 = (bf16[2,128,512]{2,1,0:T(8,128)(2,1)S(1)}, bf16[2,128,512]{2,1,0:T(8,128)(2,1)S(1)}, u32[]{:S(2)}, u32[]{:S(2)}) collective-permute-start(bf16[2,128,512]{2,1,0:T(8,128)(2,1)S(1)} %maximum_select_fusion.5), channel_id=1, source_target_pairs={{0,8},{4,12},{8,0},{12,4},{16,24},{20,28},{24,16},{28,20},{1,9},{5... | collective-permute-start | bytes 786440 | tf_op jit(solution)/shard_map/ppermute | solution.py:52
  21.6 0.1 pad_maximum_fusion.3
  21.7 0.1 copy.80
  21.9 0.1 copy.85
  22.0 0.1 copy.81
  22.1 0.1 copy.86
  22.4 0.1 copy.82
  22.6 0.1 copy.87
  22.7 6.2 %collective-permute-done.8 = bf16[2,128,512]{2,1,0:T(8,128)(2,1)S(1)} collective-permute-done((bf16[2,128,512]{2,1,0:T(8,128)(2,1)S(1)}, bf16[2,128,512]{2,1,0:T(8,128)(2,1)S(1)}, u32[]{:S(2)}, u32[]{:S(2)}) %collective-permute-start.8) | collective-permute-done | bytes 262176 | tf_op jit(solution)/shard_map/ppermute | solution.py:52
  29.0 0.2 collective-permute-start.9
  29.3 0.9 collective-permute-start.4
  30.3 0.1 copy.83
  30.4 0.1 copy.88
  30.5 0.1 copy.84
  30.7 0.1 copy.89
  31.0 0.6 copy.90
  31.6 1.2 %copy.92.query_ref = bf16[4,128,768]{2,1,0:T(8,128)(2,1)} copy(bf16[4,128,768]{1,2,0:T(8,128)(2,1)S(1)} %bitcast.91) | data formatting | bytes 1572864 | tf_op jit(solution)/shard_map/reshape | solution.py:160
  32.8 0.8 copy.100
  33.6 4.5 %collective-permute-done.4 = bf16[2,128,512]{2,1,0:T(8,128)(2,1)} collective-permute-done((bf16[2,128,512]{2,1,0:T(8,128)(2,1)S(1)}, bf16[2,128,512]{2,1,0:T(8,128)(2,1)}, u32[]{:S(2)}, u32[]{:S(2)}) %collective-permute-start.4) | collective-permute-done | bytes 262176 | tf_op jit(solution)/shard_map/ppermute | solution.py:52
  38.0 1.1 %maximum_select_fusion.2 = bf16[4,128,512]{2,1,0:T(8,128)(2,1)S(1)} fusion(bf16[2,128,512]{2,1,0:T(8,128)(2,1)S(1)} %maximum_select_fusion.4, bf16[2,128,512]{2,1,0:T(8,128)(2,1)} %collective-permute-done.4, pred[]{:T(512)S(6)} %ne.65), kind=kLoop, calls=%fused_computation.33 | loop fusion | flops 786432 | bytes 1048577 | tf_op jit(solution)/shard_map/jit(_where)/select_n | solution.py:54
  39.2 0.2 maximum_select_fusion.1
  39.4 0.9 copy.91
  40.4 0.8 reshape.181
  41.2 1.9 %concatenate.65 = bf16[1040,512]{0,1:T(8,128)(2,1)S(1)} concatenate(bf16[8,512]{0,1:T(8,128)(2,1)S(1)} %broadcast_in_dim.93, bf16[1024,512]{0,1:T(8,128)(2,1)S(1)} %reshape.181, bf16[8,512]{0,1:T(8,128)(2,1)S(1)} %broadcast_in_dim.93), dimensions={0} | concatenate | bytes 2129920 | tf_op jit(solution)/shard_map/concatenate | solution.py:214
  43.1 0.2 dynamic-slice_convert_fusion
  43.3 0.6 fusion.48
  43.9 0.3 copy-done.1
  44.2 0.4 fusion.14
  44.7 29.5 %shard_map.64 = f32[4,128,1024]{2,1,0:T(8,128)} custom-call(f32[264]{0:T(512)} %reshape.179.taps_ref, bf16[4,128,768]{2,1,0:T(8,128)(2,1)} %copy.92.query_ref, bf16[512,1024]{1,0:T(8,128)(2,1)} %bitcast.86, bf16[512,1024]{1,0:T(8,128)(2,1)} %bitcast.87), custom_call_target="tpu_custom_call" | custom-call | tf_op jit(solution)/shard_map/pallas_call | solution.py:113
  74.3 0.1 subtract_bitcast_fusion.3
  74.5 0.1 fusion.32
  74.6 6.4 %divide_bitcast_fusion = f32[1,4,128,1024]{3,2,1,0:T(8,128)S(1)} fusion(f32[4,128,1024]{2,1,0:T(8,128)} %shard_map.64, f32[4,128]{1,0:T(4,128)S(1)} %get-tuple-element.56, f32[4,128]{1,0:T(4,128)S(1)} %get-tuple-element.55, f32[4,128]{1,0:T(4,128)S(1)} %get-tuple-element.54, f32[4,128]{1,0:T(4,128)S(1)} %subtract_bitcast_fusion.3, f32[4,128]{1,0:T(4,128)S(1)} %fusion.32, ...), kind=kOutput, calls=%fused_computation.5 | output fusion | flops 6818814 | bytes 4990976 | tf_op jit(solution)/shard_map/div | solution.py:169
  81.0 1.2 %slice_bitcast_fusion.3 = (f32[128,1024]{1,0:T(8,128)S(1)}, f32[128,1024]{1,0:T(8,128)}, f32[128,1024]{1,0:T(8,128)}, f32[128,1024]{1,0:T(8,128)}) fusion(f32[1,4,128,1024]{3,2,1,0:T(8,128)S(1)} %divide_bitcast_fusion), kind=kLoop, calls=%fused_computation.32 | loop fusion | bytes 4194304 | tf_op jit(solution)/shard_map/mul | solution.py:174
  82.2 1.4 %maximum_select_fusion = bf16[8,128,512]{2,1,0:T(8,128)(2,1)S(1)} fusion(bf16[4,128,512]{2,1,0:T(8,128)(2,1)S(1)} %maximum_select_fusion.2, bf16[4,128,512]{2,1,0:T(8,128)(2,1)} %collective-permute-done.5, pred[]{:T(512)S(6)} %ne.64), kind=kLoop, calls=%fused_computation.9 | loop fusion | flops 1572864 | bytes 2097153 | tf_op jit(solution)/shard_map/jit(_where)/select_n | solution.py:54
  83.6 0.9 copy.78
  84.6 0.8 reshape_reshape.3
  85.4 0.2 copy-done.2
  85.6 2.0 %multiply_reduce_fusion = (f32[128,4]{0,1:T(4,128)S(1)}, f32[128,4,128]{0,2,1:T(8,128)S(1)}) fusion(bf16[1024,4,128]{0,2,1:T(8,128)(2,1)S(1)} %reshape_reshape.3, f32[128,1024]{1,0:T(8,128)S(1)} %copy-done.2, f32[4]{0:T(128)S(1)} %copy-done.22, f32[128,1024]{1,0:T(8,128)} %get-tuple-element.31, f32[4]{0:T(128)S(1)} %copy-done.23, ...), kind=kOutput, calls=%fused_computation.54 | convolution fusion | flops 138542592 | bytes 3409984 | tf_op jit(solution)/shard_map/hik,khd->ihd/dot_general | solution.py:176
  87.7 0.1 multiply_convert_fusion
  87.8 0.2 constant_dynamic-slice_fusion.3
  88.1 2.6 %collective-permute-start.10 = (bf16[32,512]{1,0:T(8,128)(2,1)S(1)}, bf16[32,512]{1,0:T(8,128)(2,1)S(1)}, u32[]{:S(2)}, u32[]{:S(2)}) collective-permute-start(bf16[32,512]{1,0:T(8,128)(2,1)S(1)} %copy.101), channel_id=1, source_target_pairs={{0,1},{1,2},{2,3},{3,0},{4,5},{5,6},{6,7},{7,4},{8,9},{9,10},{10,1... | collective-permute-start | bytes 98312 | tf_op jit(solution)/shard_map/ppermute | solution.py:38
  90.8 1.7 %collective-permute-start.11 = (bf16[32,512]{1,0:T(8,128)(2,1)S(1)}, bf16[32,512]{1,0:T(8,128)(2,1)S(1)}, u32[]{:S(2)}, u32[]{:S(2)}) collective-permute-start(bf16[32,512]{1,0:T(8,128)(2,1)S(1)} %copy.102), channel_id=1, source_target_pairs={{0,2},{1,3},{2,0},{3,1},{4,6},{5,7},{6,4},{7,5},{8,10},{9,11},{10,... | collective-permute-start | bytes 98312 | tf_op jit(solution)/shard_map/ppermute | solution.py:38
  92.6 0.8 collective-permute-start.12
  93.5 0.4 collective-permute-done.10
  93.9 2.2 %collective-permute-done.11 = bf16[32,512]{1,0:T(8,128)(2,1)S(1)} collective-permute-done((bf16[32,512]{1,0:T(8,128)(2,1)S(1)}, bf16[32,512]{1,0:T(8,128)(2,1)S(1)}, u32[]{:S(2)}, u32[]{:S(2)}) %collective-permute-start.11) | collective-permute-done | bytes 32800 | tf_op jit(solution)/shard_map/ppermute | solution.py:38
  96.0 0.5 collective-permute-done.12
  96.6 0.7 gather_fusion.1
  97.3 0.7 copy.104
  (87 shorter events, 1.5 us)
Async XLA Ops:
  1.1 14.7 %copy-start.3 = (f32[4,4]{1,0:T(4,128)S(1)}, f32[4,4]{1,0:T(4,128)}, u32[]{:S(2)}) copy-start(f32[4,4]{1,0:T(4,128)} %param.10) | copy-start | bytes 196
  1.1 11.1 %collective-permute-start = (bf16[3,32,512]{2,1,0:T(8,128)(2,1)S(1)}, bf16[3,32,512]{2,1,0:T(8,128)(2,1)S(1)}, u32[]{:S(2)}, u32[]{:S(2)}) collective-permute-start(bf16[3,32,512]{2,1,0:T(8,128)(2,1)S(1)} %get-tuple-element.44), channel_id=1, source_target_pairs={{0,1},{1,2},{2,3},{3,0},{4,5},{5,6},{6,7},{7,4},{8,9},{9,10},{10,1... | collective-permute-start | bytes 294920 | tf_op jit(solution)/shard_map/ppermute | solution.py:38
  4.2 9.2 %collective-permute-start.1 = (bf16[3,32,512]{2,1,0:T(8,128)(2,1)S(1)}, bf16[3,32,512]{2,1,0:T(8,128)(2,1)S(1)}, u32[]{:S(2)}, u32[]{:S(2)}) collective-permute-start(bf16[3,32,512]{2,1,0:T(8,128)(2,1)S(1)} %get-tuple-element.43), channel_id=1, source_target_pairs={{0,2},{1,3},{2,0},{3,1},{4,6},{5,7},{6,4},{7,5},{8,10},{9,11},{10,... | collective-permute-start | bytes 294920 | tf_op jit(solution)/shard_map/ppermute | solution.py:38
  6.8 6.6 %collective-permute-start.2 = (bf16[3,32,512]{2,1,0:T(8,128)(2,1)S(1)}, bf16[3,32,512]{2,1,0:T(8,128)(2,1)S(1)}, u32[]{:S(2)}, u32[]{:S(2)}) collective-permute-start(bf16[3,32,512]{2,1,0:T(8,128)(2,1)S(1)} %get-tuple-element.42), channel_id=1, source_target_pairs={{0,3},{1,0},{2,1},{3,2},{4,7},{5,4},{6,5},{7,6},{8,11},{9,8},{10,9... | collective-permute-start | bytes 294920 | tf_op jit(solution)/shard_map/ppermute | solution.py:38
  10.8 5.7 %copy-start.8 = (s32[1024]{0:T(1024)}, s32[1024]{0:T(1024)S(1)}, u32[]{:S(2)}) copy-start(s32[1024]{0:T(1024)S(1)} %pad_clamp_fusion) | copy-start | bytes 12292
  12.2 4.3 %copy-start.19 = (pred[4]{0:T(512)(128)(4,1)}, pred[4]{0:T(512)(128)(4,1)S(1)}, u32[]{:S(2)}) copy-start(pred[4]{0:T(512)(128)(4,1)S(1)} %compare_and_fusion) | copy-start | bytes 16
  14.2 5.8 %collective-permute-start.7 = (bf16[1,128,512]{2,1,0:T(8,128)(2,1)S(1)}, bf16[1,128,512]{2,1,0:T(8,128)(2,1)S(1)}, u32[]{:S(2)}, u32[]{:S(2)}) collective-permute-start(bf16[1,128,512]{2,1,0:T(8,128)(2,1)S(1)} %bitcast.98), channel_id=1, source_target_pairs={{0,16},{4,20},{8,24},{12,28},{16,0},{20,4},{24,8},{28,12},{1,17},{... | collective-permute-start | bytes 393224 | tf_op jit(solution)/shard_map/ppermute | solution.py:52
  17.5 4.2 %collective-permute-start.6 = (bf16[5,512]{1,0:T(8,128)(2,1)S(1)}, bf16[5,512]{1,0:T(8,128)(2,1)S(1)}, u32[]{:S(2)}, u32[]{:S(2)}) collective-permute-start(bf16[5,512]{1,0:T(8,128)(2,1)S(1)} %slice.270), channel_id=1, source_target_pairs={{0,4},{4,8},{8,12},{12,16},{16,20},{20,24},{24,28},{1,5},{5,9},{9,... | collective-permute-start | bytes 15368 | tf_op jit(solution)/shard_map/ppermute | solution.py:22
  19.0 10.3 %collective-permute-start.3 = (bf16[1,128,512]{2,1,0:T(8,128)(2,1)S(1)}, bf16[1,128,512]{2,1,0:T(8,128)(2,1)S(1)}, u32[]{:S(2)}, u32[]{:S(2)}) collective-permute-start(bf16[1,128,512]{2,1,0:T(8,128)(2,1)S(1)} %bitcast.96), channel_id=1, source_target_pairs={{0,16},{4,20},{8,24},{12,28},{16,0},{20,4},{24,8},{28,12},{1,17},{... | collective-permute-start | bytes 393224 | tf_op jit(solution)/shard_map/ppermute | solution.py:52
  20.1 8.9 %collective-permute-start.8 = (bf16[2,128,512]{2,1,0:T(8,128)(2,1)S(1)}, bf16[2,128,512]{2,1,0:T(8,128)(2,1)S(1)}, u32[]{:S(2)}, u32[]{:S(2)}) collective-permute-start(bf16[2,128,512]{2,1,0:T(8,128)(2,1)S(1)} %maximum_select_fusion.5), channel_id=1, source_target_pairs={{0,8},{4,12},{8,0},{12,4},{16,24},{20,28},{24,16},{28,20},{1,9},{5... | collective-permute-start | bytes 786440 | tf_op jit(solution)/shard_map/ppermute | solution.py:52
  29.0 10.2 %collective-permute-start.9 = (bf16[4,128,512]{2,1,0:T(8,128)(2,1)S(1)}, bf16[4,128,512]{2,1,0:T(8,128)(2,1)S(1)}, u32[]{:S(2)}, u32[]{:S(2)}) collective-permute-start(bf16[4,128,512]{2,1,0:T(8,128)(2,1)S(1)} %maximum_select_fusion.3), channel_id=1, source_target_pairs={{0,4},{4,0},{8,12},{12,8},{16,20},{20,16},{24,28},{28,24},{1,5},{5... | collective-permute-start | bytes 1572872 | tf_op jit(solution)/shard_map/ppermute | solution.py:52
  29.3 8.7 %collective-permute-start.4 = (bf16[2,128,512]{2,1,0:T(8,128)(2,1)S(1)}, bf16[2,128,512]{2,1,0:T(8,128)(2,1)}, u32[]{:S(2)}, u32[]{:S(2)}) collective-permute-start(bf16[2,128,512]{2,1,0:T(8,128)(2,1)S(1)} %maximum_select_fusion.4), channel_id=1, source_target_pairs={{0,8},{4,12},{8,0},{12,4},{16,24},{20,28},{24,16},{28,20},{1,9},{5... | collective-permute-start | bytes 786440 | tf_op jit(solution)/shard_map/ppermute | solution.py:52
  39.2 43.0 %collective-permute-start.5 = (bf16[4,128,512]{2,1,0:T(8,128)(2,1)S(1)}, bf16[4,128,512]{2,1,0:T(8,128)(2,1)}, u32[]{:S(2)}, u32[]{:S(2)}) collective-permute-start(bf16[4,128,512]{2,1,0:T(8,128)(2,1)S(1)} %maximum_select_fusion.2), channel_id=1, source_target_pairs={{0,4},{4,0},{8,12},{12,8},{16,20},{20,16},{24,28},{28,24},{1,5},{5... | collective-permute-start | bytes 1572872 | tf_op jit(solution)/shard_map/ppermute | solution.py:52
  41.1 2.8 %copy-start = (bf16[1024,512]{0,1:T(8,128)(2,1)}, bf16[1024,512]{0,1:T(8,128)(2,1)S(1)}, u32[]{:S(2)}) copy-start(bf16[1024,512]{0,1:T(8,128)(2,1)S(1)} %reshape.181) | copy-start | bytes 3145732
  43.3 0.9 copy-start.1
  44.6 29.6 %copy-start.4 = (f32[4]{0:T(128)S(1)}, f32[4]{0:T(128)}, u32[]{:S(2)}) copy-start(f32[4]{0:T(128)} %get-tuple-element.13) | copy-start | bytes 52
  44.6 29.6 %copy-start.5 = (f32[4]{0:T(128)S(1)}, f32[4]{0:T(128)}, u32[]{:S(2)}) copy-start(f32[4]{0:T(128)} %get-tuple-element.16) | copy-start | bytes 52
  44.6 29.6 %copy-start.6 = (f32[4]{0:T(128)S(1)}, f32[4]{0:T(128)}, u32[]{:S(2)}) copy-start(f32[4]{0:T(128)} %get-tuple-element.17) | copy-start | bytes 52
  44.6 29.6 %copy-start.7 = (f32[4]{0:T(128)S(1)}, f32[4]{0:T(128)}, u32[]{:S(2)}) copy-start(f32[4]{0:T(128)} %get-tuple-element.20) | copy-start | bytes 52
  44.6 29.7 %copy-start.9 = (f32[4]{0:T(128)S(1)}, f32[4]{0:T(128)}, u32[]{:S(2)}) copy-start(f32[4]{0:T(128)} %get-tuple-element.15) | copy-start | bytes 52
  44.6 29.7 %copy-start.10 = (f32[4]{0:T(128)S(1)}, f32[4]{0:T(128)}, u32[]{:S(2)}) copy-start(f32[4]{0:T(128)} %get-tuple-element.19) | copy-start | bytes 52
  44.6 29.7 %copy-start.11 = (f32[4]{0:T(128)S(1)}, f32[4]{0:T(128)}, u32[]{:S(2)}) copy-start(f32[4]{0:T(128)} %get-tuple-element.22) | copy-start | bytes 52
  44.6 29.7 %copy-start.12 = (f32[4]{0:T(128)S(1)}, f32[4]{0:T(128)}, u32[]{:S(2)}) copy-start(f32[4]{0:T(128)} %get-tuple-element.24) | copy-start | bytes 52
  44.6 29.8 %copy-start.14 = (f32[4]{0:T(128)S(1)}, f32[4]{0:T(128)}, u32[]{:S(2)}) copy-start(f32[4]{0:T(128)} %get-tuple-element.10) | copy-start | bytes 52
  44.7 29.8 %copy-start.15 = (f32[4]{0:T(128)S(1)}, f32[4]{0:T(128)}, u32[]{:S(2)}) copy-start(f32[4]{0:T(128)} %get-tuple-element.14) | copy-start | bytes 52
  44.7 29.8 %copy-start.16 = (f32[4]{0:T(128)S(1)}, f32[4]{0:T(128)}, u32[]{:S(2)}) copy-start(f32[4]{0:T(128)} %get-tuple-element.18) | copy-start | bytes 52
  44.7 29.8 %copy-start.17 = (f32[4]{0:T(128)S(1)}, f32[4]{0:T(128)}, u32[]{:S(2)}) copy-start(f32[4]{0:T(128)} %get-tuple-element.21) | copy-start | bytes 52
  44.7 29.8 %copy-start.18 = (f32[4]{0:T(128)S(1)}, f32[4]{0:T(128)}, u32[]{:S(2)}) copy-start(f32[4]{0:T(128)} %get-tuple-element.23) | copy-start | bytes 52
  83.6 1.8 %copy-start.21 = (f32[4]{0:T(128)S(1)}, f32[4]{0:T(128)}, u32[]{:S(2)}) copy-start(f32[4]{0:T(128)} %get-tuple-element.25) | copy-start | bytes 52
  83.6 1.8 %copy-start.22 = (f32[4]{0:T(128)S(1)}, f32[4]{0:T(128)}, u32[]{:S(2)}) copy-start(f32[4]{0:T(128)} %get-tuple-element.26) | copy-start | bytes 52
  83.6 1.8 %copy-start.23 = (f32[4]{0:T(128)S(1)}, f32[4]{0:T(128)}, u32[]{:S(2)}) copy-start(f32[4]{0:T(128)} %get-tuple-element.27) | copy-start | bytes 52
  83.6 1.8 %copy-start.24 = (f32[4]{0:T(128)S(1)}, f32[4]{0:T(128)}, u32[]{:S(2)}) copy-start(f32[4]{0:T(128)} %get-tuple-element.28) | copy-start | bytes 52
  84.6 1.0 %copy-start.2 = (f32[128,1024]{1,0:T(8,128)S(1)}, f32[128,1024]{1,0:T(8,128)}, u32[]{:S(2)}) copy-start(f32[128,1024]{1,0:T(8,128)} %get-tuple-element.30) | copy-start | bytes 1572868
  85.6 2.0 %copy-start.13 = (f32[512]{0:T(512)S(1)}, f32[512]{0:T(512)}, u32[]{:S(2)}) copy-start(f32[512]{0:T(512)} %param.11) | copy-start | bytes 6148
  87.6 9.6 %copy-start.20 = (pred[4]{0:T(512)(128)(4,1)S(1)}, pred[4]{0:T(512)(128)(4,1)}, u32[]{:S(2)}) copy-start(pred[4]{0:T(512)(128)(4,1)} %copy-done.19) | copy-start | bytes 16
  88.1 5.8 %collective-permute-start.10 = (bf16[32,512]{1,0:T(8,128)(2,1)S(1)}, bf16[32,512]{1,0:T(8,128)(2,1)S(1)}, u32[]{:S(2)}, u32[]{:S(2)}) collective-permute-start(bf16[32,512]{1,0:T(8,128)(2,1)S(1)} %copy.101), channel_id=1, source_target_pairs={{0,1},{1,2},{2,3},{3,0},{4,5},{5,6},{6,7},{7,4},{8,9},{9,10},{10,1... | collective-permute-start | bytes 98312 | tf_op jit(solution)/shard_map/ppermute | solution.py:38
  90.8 5.2 %collective-permute-start.11 = (bf16[32,512]{1,0:T(8,128)(2,1)S(1)}, bf16[32,512]{1,0:T(8,128)(2,1)S(1)}, u32[]{:S(2)}, u32[]{:S(2)}) collective-permute-start(bf16[32,512]{1,0:T(8,128)(2,1)S(1)} %copy.102), channel_id=1, source_target_pairs={{0,2},{1,3},{2,0},{3,1},{4,6},{5,7},{6,4},{7,5},{8,10},{9,11},{10,... | collective-permute-start | bytes 98312 | tf_op jit(solution)/shard_map/ppermute | solution.py:38
  92.6 4.0 %collective-permute-start.12 = (bf16[32,512]{1,0:T(8,128)(2,1)S(1)}, bf16[32,512]{1,0:T(8,128)(2,1)S(1)}, u32[]{:S(2)}, u32[]{:S(2)}) collective-permute-start(bf16[32,512]{1,0:T(8,128)(2,1)S(1)} %copy.103), channel_id=1, source_target_pairs={{0,3},{1,0},{2,1},{3,2},{4,7},{5,4},{6,5},{7,6},{8,11},{9,8},{10,9... | collective-permute-start | bytes 98312 | tf_op jit(solution)/shard_map/ppermute | solution.py:38

commit v6 on v5

--- a/solution.py
+++ b/solution.py
@@ -9,6 +9,7 @@
 QCONV = 6
 KCONV = 11
 KEY_BLOCK = 128
+KEY_SPAN = 1024
 ROW_CHUNK = 128
 
 
@@ -20,12 +21,6 @@
     peers = lax.axis_size(axis)
     pairs = [(i, i + by) for i in range(peers) if 0 <= i + by < peers]
     return lax.ppermute(shard, axis, pairs)
-
-
-def split_bf16(values):
-    high = lax.reduce_precision(values, exponent_bits=8, mantissa_bits=7)
-    low = values - high
-    return high.astype(jnp.bfloat16), low.astype(jnp.bfloat16)
 
 
 def exchanged(pieces_of, axis):
@@ -60,16 +55,16 @@
     return jnp.transpose(held, tuple(reversed(range(bits))) + tuple(range(bits, held.ndim)))
 
 
-def logits_kernel(taps_ref, query_ref, before_ref, current_ref, out_ref, high_ref, low_ref):
+def logits_kernel(taps_ref, query_ref, keys_ref, out_ref, high_ref, low_ref, conv_ref):
     head = pl.program_id(0)
-    window = pl.program_id(1)
-
-    @pl.when(window == 0)
+    group = pl.program_id(1)
+
+    @pl.when(group == 0)
     def _():
         lag = (
-            lax.broadcasted_iota(jnp.int32, (2 * KEY_BLOCK, KEY_BLOCK), 1)
+            lax.broadcasted_iota(jnp.int32, (KEY_BLOCK, 2 * KEY_BLOCK), 0)
             + KEY_BLOCK
-            - lax.broadcasted_iota(jnp.int32, (2 * KEY_BLOCK, KEY_BLOCK), 0)
+            - lax.broadcasted_iota(jnp.int32, (KEY_BLOCK, 2 * KEY_BLOCK), 1)
         )
         for row_lag in range(QCONV):
             toeplitz = jnp.zeros(lag.shape, jnp.float32)
@@ -78,54 +73,54 @@
                 toeplitz = jnp.where(lag == col_lag, tap, toeplitz)
             high = toeplitz.astype(jnp.bfloat16)
             low = (toeplitz - high.astype(jnp.float32)).astype(jnp.bfloat16)
-            high_ref[:, row_lag * KEY_BLOCK : (row_lag + 1) * KEY_BLOCK] = high
-            low_ref[:, row_lag * KEY_BLOCK : (row_lag + 1) * KEY_BLOCK] = low
-
-    before = jnp.where(
-        window > 0, before_ref[...], jnp.zeros(before_ref.shape, before_ref.dtype)
-    )
-    current = current_ref[...]
-    conv_keys = (
-        jnp.dot(before, high_ref[:KEY_BLOCK], preferred_element_type=jnp.float32)
-        + jnp.dot(current, high_ref[KEY_BLOCK:], preferred_element_type=jnp.float32)
-        + jnp.dot(before, low_ref[:KEY_BLOCK], preferred_element_type=jnp.float32)
-        + jnp.dot(current, low_ref[KEY_BLOCK:], preferred_element_type=jnp.float32)
-    )
-    keys_high = conv_keys.astype(jnp.bfloat16)
-    keys_low = (conv_keys - keys_high.astype(jnp.float32)).astype(jnp.bfloat16)
-    query = query_ref[0]
-    head_dim = current.shape[0]
+            high_ref[row_lag * KEY_BLOCK : (row_lag + 1) * KEY_BLOCK] = high
+            low_ref[row_lag * KEY_BLOCK : (row_lag + 1) * KEY_BLOCK] = low
+
+    blocks = conv_ref.shape[2] // KEY_BLOCK
+    for block in range(blocks):
+        start = pl.multiple_of((group * blocks + block) * KEY_BLOCK, KEY_BLOCK)
+        window = keys_ref[pl.ds(start, 2 * KEY_BLOCK), :]
+        conv_keys = jnp.dot(
+            high_ref[...], window, preferred_element_type=jnp.float32
+        ) + jnp.dot(low_ref[...], window, preferred_element_type=jnp.float32)
+        keys_high = conv_keys.astype(jnp.bfloat16)
+        keys_low = (conv_keys - keys_high.astype(jnp.float32)).astype(jnp.bfloat16)
+        rows = slice(block * KEY_BLOCK, (block + 1) * KEY_BLOCK)
+        for row_lag in range(QCONV):
+            part = slice(row_lag * KEY_BLOCK, (row_lag + 1) * KEY_BLOCK)
+            conv_ref[0, row_lag, rows] = keys_high[part]
+            conv_ref[1, row_lag, rows] = keys_low[part]
+    head_dim = keys_ref.shape[1]
     acc = jnp.zeros(out_ref.shape[1:], jnp.float32)
     for row_lag in range(QCONV):
-        part = query[:, row_lag * head_dim : (row_lag + 1) * head_dim]
-        cols = slice(row_lag * KEY_BLOCK, (row_lag + 1) * KEY_BLOCK)
-        acc = acc + jnp.dot(part, keys_high[:, cols], preferred_element_type=jnp.float32)
-        acc = acc + jnp.dot(part, keys_low[:, cols], preferred_element_type=jnp.float32)
+        part = query_ref[0, row_lag * head_dim : (row_lag + 1) * head_dim, :]
+        acc = acc + jnp.dot(conv_ref[0, row_lag], part, preferred_element_type=jnp.float32)
+        acc = acc + jnp.dot(conv_ref[1, row_lag], part, preferred_element_type=jnp.float32)
     out_ref[0] = acc
 
 
-def conv_logits(shifted_heads, score_kernel, keys_t):
-    heads, row_count, contract = shifted_heads.shape
-    width, seq_len = keys_t.shape
-    head_dim = width // heads
-    windows = seq_len // KEY_BLOCK
+def conv_logits(shifted_t, score_kernel, key_pad):
+    heads, contract, row_count = shifted_t.shape
+    seq_len = key_pad.shape[0] - KEY_BLOCK
+    head_dim = key_pad.shape[1] // heads
+    span = min(seq_len, KEY_SPAN)
     taps = (score_kernel * head_dim ** (-0.5)).reshape(-1)
     return pl.pallas_call(
         logits_kernel,
-        grid=(heads, windows),
+        grid=(heads, seq_len // span),
         in_specs=[
             pl.BlockSpec(memory_space=pltpu.SMEM),
-            pl.BlockSpec((1, row_count, contract), lambda h, n: (h, 0, 0)),
-            pl.BlockSpec((head_dim, KEY_BLOCK), lambda h, n: (h, jnp.maximum(n - 1, 0))),
-            pl.BlockSpec((head_dim, KEY_BLOCK), lambda h, n: (h, n)),
+            pl.BlockSpec((1, contract, row_count), lambda h, g: (h, 0, 0)),
+            pl.BlockSpec((key_pad.shape[0], head_dim), lambda h, g: (0, h)),
         ],
-        out_specs=pl.BlockSpec((1, row_count, KEY_BLOCK), lambda h, n: (h, 0, n)),
-        out_shape=jax.ShapeDtypeStruct((heads, row_count, seq_len), jnp.float32),
+        out_specs=pl.BlockSpec((1, span, row_count), lambda h, g: (h, g, 0)),
+        out_shape=jax.ShapeDtypeStruct((heads, seq_len, row_count), jnp.float32),
         scratch_shapes=[
-            pltpu.VMEM((2 * KEY_BLOCK, QCONV * KEY_BLOCK), jnp.bfloat16),
-            pltpu.VMEM((2 * KEY_BLOCK, QCONV * KEY_BLOCK), jnp.bfloat16),
+            pltpu.VMEM((QCONV * KEY_BLOCK, 2 * KEY_BLOCK), jnp.bfloat16),
+            pltpu.VMEM((QCONV * KEY_BLOCK, 2 * KEY_BLOCK), jnp.bfloat16),
+            pltpu.VMEM((2, QCONV, span, head_dim), jnp.bfloat16),
         ],
-    )(taps, shifted_heads, keys_t, keys_t)
+    )(taps, shifted_t, key_pad)
 
 
 def band_terms(query_rows, query_first, key_flat, score_kernel):
@@ -154,27 +149,27 @@
     return jnp.stack(band)
 
 
-def attend_chunk(shifted, band, query_first, keys_t, score_kernel, value_heads, head_mixing):
+def attend_chunk(shifted, band, query_first, key_pad, score_kernel, value_heads, head_mixing):
     row_count, heads = shifted.shape[:2]
     seq_len = value_heads.shape[0]
-    shifted_heads = jnp.transpose(shifted, (1, 0, 2, 3)).reshape((heads, row_count, -1))
-    convolved = conv_logits(shifted_heads, score_kernel, keys_t)
+    shifted_t = jnp.transpose(shifted, (1, 2, 3, 0)).reshape((heads, -1, row_count))
+    convolved = conv_logits(shifted_t, score_kernel, key_pad)
     query_pos = query_first + lax.iota(jnp.int32, row_count)
-    gap = query_pos[:, None] - lax.iota(jnp.int32, seq_len)[None, :]
+    gap = query_pos[None, :] - lax.iota(jnp.int32, seq_len)[:, None]
     for lag in range(QCONV - 1):
-        convolved = convolved + jnp.where(gap == lag, band[lag][:, :, None], 0.0)
+        convolved = convolved + jnp.where(gap == lag, band[lag][:, None, :], 0.0)
     logits = jnp.where(gap >= 0, convolved, lowest)
-    peak = jnp.max(logits, axis=2, keepdims=True)
+    peak = jnp.max(logits, axis=1, keepdims=True)
     expd = jnp.exp(logits - peak)
-    probabilities = expd / jnp.sum(expd, axis=2, keepdims=True)
-    grouped = probabilities.reshape(heads // GROUP, GROUP, row_count, seq_len)
+    probabilities = expd / jnp.sum(expd, axis=1, keepdims=True)
+    grouped = probabilities.reshape(heads // GROUP, GROUP, seq_len, row_count)
     weights = head_mixing.reshape(heads // GROUP, GROUP, GROUP)
     mixed_probs = jnp.zeros_like(grouped)
     for source in range(GROUP):
         mixed_probs = mixed_probs + weights[:, :, source, None, None] * grouped[:, source, None]
-    mixed_probs = mixed_probs.reshape(heads, row_count, seq_len).astype(jnp.bfloat16)
+    mixed_probs = mixed_probs.reshape(heads, seq_len, row_count).astype(jnp.bfloat16)
     return jnp.einsum(
-        "hik,khd->ihd", mixed_probs, value_heads, preferred_element_type=jnp.float32
+        "hki,khd->ihd", mixed_probs, value_heads, preferred_element_type=jnp.float32
     )
 
 
@@ -209,7 +204,9 @@
     key_all = gathered(key_local, "ctx").reshape((-1, width))
     value_all = gathered(value_local, "ctx").reshape((-1, width))
     seq_len = key_all.shape[0]
-    keys_t = key_all.T
+    key_pad = jnp.concatenate(
+        [jnp.zeros((KEY_BLOCK, width), key_all.dtype), key_all], axis=0
+    )
     edge = jnp.zeros((8, width), key_all.dtype)
     key_flat = jnp.concatenate([edge, key_all, edge], axis=0)
     band = band_terms(query_ext, query_first, key_flat, score_kernel)
@@ -221,7 +218,7 @@
     chunk = min(ROW_CHUNK * KEY_BLOCK * 8 // seq_len, shard_rows)
     if chunk == shard_rows:
         weighted = attend_chunk(
-            shifted, band, query_first, keys_t, score_kernel, value_heads, head_mixing
+            shifted, band, query_first, key_pad, score_kernel, value_heads, head_mixing
         )
     else:
         chunks = shard_rows // chunk
@@ -232,7 +229,7 @@
                 lax.dynamic_slice_in_dim(shifted, start, chunk, 0),
                 lax.dynamic_slice_in_dim(band, start, chunk, 2),
                 query_first + start,
-                keys_t,
+                key_pad,
                 score_kernel,
                 value_heads,
                 head_mixing,

time: 99.9 us -> 82.8 us (0.83); the launches traced: 98 us -> 82.4 us
  Pallas kernels: 29.5 us -> 19.1 us
  local copies, waits for them, and re-layouts: 18.1 us -> 13.3 us
  other arithmetic: 13.7 us -> 9.53 us
  waiting for transfers between devices: 15 us -> 18.7 us
    pallas_call x1, Pallas kernels: 29.5 us -> 19.1 us  [conv_logits(): pl.pallas_call(logits_kernel, grid=(heads, seq_len // span), in_specs=[pl...]
    ppermute x6, waiting for transfers between devices: 10.7 us -> 14.2 us  [gathered(): incoming = lax.ppermute(held, axis, [(i, i ^ bit) for i in range(peers)])]
    div x1, other arithmetic: 6.39 us -> 3.75 us  [attend_chunk(): probabilities = expd / jnp.sum(expd, axis=1, keepdims=True)]
    select_n x6, other arithmetic: 2.82 us -> 0.55 us  [gathered(): jnp.where(upper, jnp.concatenate([incoming, held], axis=0), jnp.concatena...]
    reshape x2 -> x0, local copies, waits for them, and re-layouts: 1.93 us -> none  [the longest x1 1.16 us: attend_chunk(): jnp.transpose(shifted, (1, 0, 2, 3)).reshape((heads, row_count, -1))]
  transfers between devices with their start and end apart: 13 -> 13, of which waited for: 6 -> 6; matrix products, arithmetic and copies ran while one was open for 25% -> 20% of each run, Pallas kernels for 30% -> 23%
where the time goes in v6:
time: 82.8 us; the launch traced here: 82.4 us
  Pallas kernels  19.1 us (23%)
  starting transfers between devices  18.9 us (23%)
  waiting for transfers between devices  18.7 us (23%)
  local copies, waits for them, and re-layouts  13.3 us (16%)
  other arithmetic  9.53 us (12%)
  matrix products  2.13 us (3%)
    pallas_call x1, Pallas kernels, conv_logits(): pl.pallas_call(logits_kernel, grid=(heads, seq_len // span), in_specs=[pl...  19.1 us
    ppermute x6, waiting for transfers between devices, gathered(): incoming = lax.ppermute(held, axis, [(i, i ^ bit) for i in range(peers)])  14.2 us
    ppermute x6, starting transfers between devices, exchanged(): received.append(lax.ppermute(outgoing, axis, pairs))  12.1 us
    ppermute x6, starting transfers between devices, gathered(): incoming = lax.ppermute(held, axis, [(i, i ^ bit) for i in range(peers)])  5.33 us
    ppermute x6, waiting for transfers between devices, exchanged(): received.append(lax.ppermute(outgoing, axis, pairs))  4.5 us
    div x1, other arithmetic, attend_chunk(): probabilities = expd / jnp.sum(expd, axis=1, keepdims=True)  3.75 us
    dot_general x1, matrix products, attend_chunk(): jnp.einsum('hki,khd->ihd', mixed_probs, value_heads, preferred_element_ty...  2.13 us
    slice x1, local copies, waits for them, and re-layouts, band_terms(): score_kernel[None, :, row_lag, col_lag]  1.89 us
  transfers between devices with their start and end apart: 13, of which 6 were waited for; matrix products, arithmetic and copies ran while one was open for 20% of the time, Pallas kernels for 23%

profile of v6, /device:TPU:0, one launch (start us, length us, event | category | flops | bytes accessed | tf_op | source)
XLA Modules:
  0.0 82.4 jit_solution(9066209902662501978)
XLA Ops:
  0.0 1.1 %pad_maximum_fusion = bf16[3,32,2048]{2,1,0:T(8,128)(2,1)S(1)} fusion(bf16[1,32,2048]{2,1,0:T(8,128)(2,1)} %bitcast.91, bf16[1,32,2048]{2,1,0:T(8,128)(2,1)} %bitcast.92, bf16[1,32,2048]{2,1,0:T(8,128)(2,1)} %bitcast.93), kind=kLoop, calls=%fused_computation.40 | loop fusion | flops 393216 | bytes 786432 | tf_op jit(solution)/shard_map/stack | solution.py:185
  1.1 3.1 %collective-permute-start = (bf16[3,32,512]{2,1,0:T(8,128)(2,1)S(1)}, bf16[3,32,512]{2,1,0:T(8,128)(2,1)S(1)}, u32[]{:S(2)}, u32[]{:S(2)}) collective-permute-start(bf16[3,32,512]{2,1,0:T(8,128)(2,1)S(1)} %get-tuple-element.39), channel_id=1, source_target_pairs={{0,1},{1,2},{2,3},{3,0},{4,5},{5,6},{6,7},{7,4},{8,9},{9,10},{10,1... | collective-permute-start | bytes 294920 | tf_op jit(solution)/shard_map/ppermute | solution.py:33
  4.2 2.6 %collective-permute-start.1 = (bf16[3,32,512]{2,1,0:T(8,128)(2,1)S(1)}, bf16[3,32,512]{2,1,0:T(8,128)(2,1)S(1)}, u32[]{:S(2)}, u32[]{:S(2)}) collective-permute-start(bf16[3,32,512]{2,1,0:T(8,128)(2,1)S(1)} %get-tuple-element.38), channel_id=1, source_target_pairs={{0,2},{1,3},{2,0},{3,1},{4,6},{5,7},{6,4},{7,5},{8,10},{9,11},{10,... | collective-permute-start | bytes 294920 | tf_op jit(solution)/shard_map/ppermute | solution.py:33
  6.8 1.3 %collective-permute-start.2 = (bf16[3,32,512]{2,1,0:T(8,128)(2,1)S(1)}, bf16[3,32,512]{2,1,0:T(8,128)(2,1)S(1)}, u32[]{:S(2)}, u32[]{:S(2)}) collective-permute-start(bf16[3,32,512]{2,1,0:T(8,128)(2,1)S(1)} %get-tuple-element.37), channel_id=1, source_target_pairs={{0,3},{1,0},{2,1},{3,2},{4,7},{5,4},{6,5},{7,6},{8,11},{9,8},{10,9... | collective-permute-start | bytes 294920 | tf_op jit(solution)/shard_map/ppermute | solution.py:33
  8.2 1.9 %slice_reduce_fusion.17 = (f32[4]{0:T(128)}, f32[4]{0:T(128)}, f32[4]{0:T(128)}, f32[4]{0:T(128)}, f32[4]{0:T(128)}, /*index=5*/f32[4]{0:T(128)}, f32[4]{0:T(128...) fusion(f32[4,6,11]{2,0,1:T(4,128)} %param.9), kind=kLoop, calls=%fused_computation.135 | loop fusion | bytes 480 | tf_op jit(solution)/shard_map/slice | solution.py:145
  10.1 0.7 broadcast_multiply_fusion
  10.8 1.2 %fusion.15 = (pred[1024,128]{1,0:T(8,128)(4,1)S(1)}, pred[1024,128]{1,0:T(8,128)(4,1)S(1)}, pred[1024,128]{1,0:T(8,128)(4,1)S(1)}, pred[1024,128]{1,0:T(8,128)(4...) fusion(s32[128]{0:T(128)S(1)} %iota_add_fusion), kind=kLoop, calls=%fused_computation.39 | loop fusion | flops 917504 | bytes 786944 | tf_op jit(solution)/shard_map/ge | solution.py:161
  12.0 1.4 %collective-permute-done.1 = bf16[3,32,512]{2,1,0:T(8,128)(2,1)S(1)} collective-permute-done((bf16[3,32,512]{2,1,0:T(8,128)(2,1)S(1)}, bf16[3,32,512]{2,1,0:T(8,128)(2,1)S(1)}, u32[]{:S(2)}, u32[]{:S(2)}) %collective-permute-start.1) | collective-permute-done | bytes 98336 | tf_op jit(solution)/shard_map/ppermute | solution.py:33
  13.5 0.6 gather_fusion
  14.1 0.1 select_bitcast_fusion
  14.2 1.6 %collective-permute-start.7 = (bf16[1,128,512]{2,1,0:T(8,128)(2,1)S(1)}, bf16[1,128,512]{2,1,0:T(8,128)(2,1)S(1)}, u32[]{:S(2)}, u32[]{:S(2)}) collective-permute-start(bf16[1,128,512]{2,1,0:T(8,128)(2,1)S(1)} %bitcast.84), channel_id=1, source_target_pairs={{0,16},{4,20},{8,24},{12,28},{16,0},{20,4},{24,8},{28,12},{1,17},{... | collective-permute-start | bytes 393224 | tf_op jit(solution)/shard_map/ppermute | solution.py:47
  15.8 0.8 slice_reduce_fusion.18
  16.6 0.7 reshape.179.taps_ref
  17.3 0.7 concatenate.67
  18.0 1.5 %collective-permute-start.6 = (bf16[5,512]{1,0:T(8,128)(2,1)S(1)}, bf16[5,512]{1,0:T(8,128)(2,1)S(1)}, u32[]{:S(2)}, u32[]{:S(2)}) collective-permute-start(bf16[5,512]{1,0:T(8,128)(2,1)S(1)} %slice.270), channel_id=1, source_target_pairs={{0,4},{4,8},{8,12},{12,16},{16,20},{20,24},{24,28},{1,5},{5,9},{9,... | collective-permute-start | bytes 15368 | tf_op jit(solution)/shard_map/ppermute | solution.py:23
  19.6 0.1 copy.69
  19.7 1.0 %collective-permute-start.3 = (bf16[1,128,512]{2,1,0:T(8,128)(2,1)S(1)}, bf16[1,128,512]{2,1,0:T(8,128)(2,1)S(1)}, u32[]{:S(2)}, u32[]{:S(2)}) collective-permute-start(bf16[1,128,512]{2,1,0:T(8,128)(2,1)S(1)} %bitcast.82), channel_id=1, source_target_pairs={{0,16},{4,20},{8,24},{12,28},{16,0},{20,4},{24,8},{28,12},{1,17},{... | collective-permute-start | bytes 393224 | tf_op jit(solution)/shard_map/ppermute | solution.py:47
  20.7 1.6 %collective-permute-start.8 = (bf16[2,128,512]{2,1,0:T(8,128)(2,1)S(1)}, bf16[2,128,512]{2,1,0:T(8,128)(2,1)S(1)}, u32[]{:S(2)}, u32[]{:S(2)}) collective-permute-start(bf16[2,128,512]{2,1,0:T(8,128)(2,1)S(1)} %maximum_select_fusion.5), channel_id=1, source_target_pairs={{0,8},{4,12},{8,0},{12,4},{16,24},{20,28},{24,16},{28,20},{1,9},{5... | collective-permute-start | bytes 786440 | tf_op jit(solution)/shard_map/ppermute | solution.py:47
  22.3 0.1 pad_maximum_fusion.3
  22.4 0.1 copy.64
  22.6 0.1 copy.65
  22.7 0.1 copy.66
  22.9 6.8 %collective-permute-done.8 = bf16[2,128,512]{2,1,0:T(8,128)(2,1)S(1)} collective-permute-done((bf16[2,128,512]{2,1,0:T(8,128)(2,1)S(1)}, bf16[2,128,512]{2,1,0:T(8,128)(2,1)S(1)}, u32[]{:S(2)}, u32[]{:S(2)}) %collective-permute-start.8) | collective-permute-done | bytes 262176 | tf_op jit(solution)/shard_map/ppermute | solution.py:47
  29.7 0.2 collective-permute-start.9
  30.0 0.9 %collective-permute-start.4 = (bf16[2,128,512]{2,1,0:T(8,128)(2,1)S(1)}, bf16[2,128,512]{2,1,0:T(8,128)(2,1)S(1)}, u32[]{:S(2)}, u32[]{:S(2)}) collective-permute-start(bf16[2,128,512]{2,1,0:T(8,128)(2,1)S(1)} %maximum_select_fusion.4), channel_id=1, source_target_pairs={{0,8},{4,12},{8,0},{12,4},{16,24},{20,28},{24,16},{28,20},{1,9},{5... | collective-permute-start | bytes 786440 | tf_op jit(solution)/shard_map/ppermute | solution.py:47
  30.9 0.1 copy.67
  31.0 0.1 copy.68
  31.3 7.4 %collective-permute-done.4 = bf16[2,128,512]{2,1,0:T(8,128)(2,1)S(1)} collective-permute-done((bf16[2,128,512]{2,1,0:T(8,128)(2,1)S(1)}, bf16[2,128,512]{2,1,0:T(8,128)(2,1)S(1)}, u32[]{:S(2)}, u32[]{:S(2)}) %collective-permute-start.4) | collective-permute-done | bytes 262176 | tf_op jit(solution)/shard_map/ppermute | solution.py:47
  38.6 0.1 maximum_select_fusion.2
  38.8 0.2 maximum_select_fusion.1
  39.1 1.1 %concatenate.65.keys_ref = bf16[1152,512]{1,0:T(8,128)(2,1)} pad(bf16[1024,512]{1,0:T(8,128)(2,1)S(1)} %bitcast.74, bf16[]{:T(256)} %constant.106.clone.1), padding=128_0x0_0 | pad | bytes 2228226 | tf_op jit(solution)/shard_map/concatenate | solution.py:207
  40.2 0.1 fusion.24
  40.3 0.1 fusion.56
  40.4 0.1 slice.221
  40.5 0.1 slice.225
  40.6 0.1 slice.231
  40.7 0.1 slice.239
  40.8 0.1 slice.249
  40.9 0.3 copy-done.1
  41.2 0.8 fusion.21
  42.0 0.1 copy.71
  42.1 0.1 copy.74
  42.2 0.1 copy.72
  42.5 19.1 %shard_map.64 = f32[4,1024,128]{2,1,0:T(8,128)} custom-call(f32[264]{0:T(512)} %reshape.179.taps_ref, bf16[4,768,128]{2,1,0:T(8,128)(2,1)} %bitcast.81, bf16[1152,512]{1,0:T(8,128)(2,1)} %concatenate.65.keys_ref), custom_call_target="tpu_custom_call" | custom-call | tf_op jit(solution)/shard_map/pallas_call | solution.py:108
  61.7 0.7 subtract_bitcast_fusion.2
  62.4 0.1 subtract_bitcast_fusion.3
  62.5 0.1 fusion.44
  62.6 3.8 %divide_bitcast_fusion = f32[1,4,1024,128]{3,2,1,0:T(8,128)S(1)} fusion(f32[4,1024,128]{2,1,0:T(8,128)} %shard_map.64, f32[4,128]{1,0:T(4,128)} %get-tuple-element.56, f32[4,128]{1,0:T(4,128)S(1)} %get-tuple-element.55, f32[4,128]{1,0:T(4,128)S(1)} %get-tuple-element.54, f32[4,128]{1,0:T(4,128)S(1)} %subtract_bitcast_fusion.3, f32[4,128]{1,0:T(4,128)S(1)} %fusion.44, ...), kind=kOutput, calls=%fused_computation.5 | output fusion | flops 6818814 | bytes 4990976 | tf_op jit(solution)/shard_map/div | solution.py:164
  66.4 1.4 %slice_bitcast_fusion.3 = (f32[1024,128]{1,0:T(8,128)}, f32[1024,128]{1,0:T(8,128)}, f32[1024,128]{1,0:T(8,128)}, f32[1024,128]{1,0:T(8,128)}) fusion(f32[1,4,1024,128]{3,2,1,0:T(8,128)S(1)} %divide_bitcast_fusion), kind=kLoop, calls=%fused_computation.30 | loop fusion | bytes 4194304 | tf_op jit(solution)/shard_map/mul | solution.py:169
  67.7 0.2 maximum_select_fusion
  68.0 0.9 %copy.62 = bf16[2,2,2,128,512]{3,2,1,0,4:T(2,128)(2,1)S(1)} copy(bf16[2,2,2,128,512]{4,3,0,1,2:T(8,128)(2,1)S(1)} %bitcast.76) | data formatting | bytes 2097152 | tf_op jit(solution)/shard_map/transpose | solution.py:55
  68.9 0.8 reshape_reshape.3
  69.7 0.2 copy-done.3
  70.0 2.1 %multiply_reduce_fusion = (f32[128,4]{0,1:T(4,128)S(1)}, f32[128,4,128]{0,2,1:T(8,128)S(1)}) fusion(bf16[1024,4,128]{0,2,1:T(8,128)(2,1)S(1)} %reshape_reshape.3, f32[1024,128]{1,0:T(8,128)S(1)} %copy-done.3, f32[4]{0:T(128)S(1)} %copy-done.25, f32[1024,128]{1,0:T(8,128)} %get-tuple-element.31, f32[4]{0:T(128)S(1)} %copy-done.26, ...), kind=kOutput, calls=%fused_computation.56 | convolution fusion | flops 138542592 | bytes 3409984 | tf_op jit(solution)/shard_map/hki,khd->ihd/dot_general | solution.py:171
  72.1 0.1 multiply_convert_fusion
  72.3 0.2 constant_dynamic-slice_fusion.3
  72.6 2.6 %collective-permute-start.10 = (bf16[32,512]{1,0:T(8,128)(2,1)S(1)}, bf16[32,512]{1,0:T(8,128)(2,1)S(1)}, u32[]{:S(2)}, u32[]{:S(2)}) collective-permute-start(bf16[32,512]{1,0:T(8,128)(2,1)S(1)} %copy.81), channel_id=1, source_target_pairs={{0,1},{1,2},{2,3},{3,0},{4,5},{5,6},{6,7},{7,4},{8,9},{9,10},{10,1... | collective-permute-start | bytes 98312 | tf_op jit(solution)/shard_map/ppermute | solution.py:33
  75.2 1.7 %collective-permute-start.11 = (bf16[32,512]{1,0:T(8,128)(2,1)S(1)}, bf16[32,512]{1,0:T(8,128)(2,1)S(1)}, u32[]{:S(2)}, u32[]{:S(2)}) collective-permute-start(bf16[32,512]{1,0:T(8,128)(2,1)S(1)} %copy.82), channel_id=1, source_target_pairs={{0,2},{1,3},{2,0},{3,1},{4,6},{5,7},{6,4},{7,5},{8,10},{9,11},{10,... | collective-permute-start | bytes 98312 | tf_op jit(solution)/shard_map/ppermute | solution.py:33
  77.0 0.8 collective-permute-start.12
  77.9 0.4 collective-permute-done.10
  78.3 2.1 %collective-permute-done.11 = bf16[32,512]{1,0:T(8,128)(2,1)S(1)} collective-permute-done((bf16[32,512]{1,0:T(8,128)(2,1)S(1)}, bf16[32,512]{1,0:T(8,128)(2,1)S(1)}, u32[]{:S(2)}, u32[]{:S(2)}) %collective-permute-start.11) | collective-permute-done | bytes 32800 | tf_op jit(solution)/shard_map/ppermute | solution.py:33
  80.5 0.5 collective-permute-done.12
  81.0 0.7 gather_fusion.1
  81.8 0.7 copy.85
  (96 shorter events, 1.3 us)
Async XLA Ops:
  1.1 14.7 %copy-start.4 = (f32[4,4]{1,0:T(4,128)S(1)}, f32[4,4]{1,0:T(4,128)}, u32[]{:S(2)}) copy-start(f32[4,4]{1,0:T(4,128)} %param.10) | copy-start | bytes 196
  1.1 10.9 %collective-permute-start = (bf16[3,32,512]{2,1,0:T(8,128)(2,1)S(1)}, bf16[3,32,512]{2,1,0:T(8,128)(2,1)S(1)}, u32[]{:S(2)}, u32[]{:S(2)}) collective-permute-start(bf16[3,32,512]{2,1,0:T(8,128)(2,1)S(1)} %get-tuple-element.39), channel_id=1, source_target_pairs={{0,1},{1,2},{2,3},{3,0},{4,5},{5,6},{6,7},{7,4},{8,9},{9,10},{10,1... | collective-permute-start | bytes 294920 | tf_op jit(solution)/shard_map/ppermute | solution.py:33
  4.2 9.2 %collective-permute-start.1 = (bf16[3,32,512]{2,1,0:T(8,128)(2,1)S(1)}, bf16[3,32,512]{2,1,0:T(8,128)(2,1)S(1)}, u32[]{:S(2)}, u32[]{:S(2)}) collective-permute-start(bf16[3,32,512]{2,1,0:T(8,128)(2,1)S(1)} %get-tuple-element.38), channel_id=1, source_target_pairs={{0,2},{1,3},{2,0},{3,1},{4,6},{5,7},{6,4},{7,5},{8,10},{9,11},{10,... | collective-permute-start | bytes 294920 | tf_op jit(solution)/shard_map/ppermute | solution.py:33
  6.8 6.6 %collective-permute-start.2 = (bf16[3,32,512]{2,1,0:T(8,128)(2,1)S(1)}, bf16[3,32,512]{2,1,0:T(8,128)(2,1)S(1)}, u32[]{:S(2)}, u32[]{:S(2)}) collective-permute-start(bf16[3,32,512]{2,1,0:T(8,128)(2,1)S(1)} %get-tuple-element.37), channel_id=1, source_target_pairs={{0,3},{1,0},{2,1},{3,2},{4,7},{5,4},{6,5},{7,6},{8,11},{9,8},{10,9... | collective-permute-start | bytes 294920 | tf_op jit(solution)/shard_map/ppermute | solution.py:33
  10.8 7.2 %copy-start.11 = (s32[1024]{0:T(1024)}, s32[1024]{0:T(1024)S(1)}, u32[]{:S(2)}) copy-start(s32[1024]{0:T(1024)S(1)} %pad_clamp_fusion) | copy-start | bytes 12292
  12.0 8.7 %copy-start.22 = (pred[4]{0:T(512)(128)(4,1)}, pred[4]{0:T(512)(128)(4,1)S(1)}, u32[]{:S(2)}) copy-start(pred[4]{0:T(512)(128)(4,1)S(1)} %compare_and_fusion) | copy-start | bytes 16
  14.2 6.5 %collective-permute-start.7 = (bf16[1,128,512]{2,1,0:T(8,128)(2,1)S(1)}, bf16[1,128,512]{2,1,0:T(8,128)(2,1)S(1)}, u32[]{:S(2)}, u32[]{:S(2)}) collective-permute-start(bf16[1,128,512]{2,1,0:T(8,128)(2,1)S(1)} %bitcast.84), channel_id=1, source_target_pairs={{0,16},{4,20},{8,24},{12,28},{16,0},{20,4},{24,8},{28,12},{1,17},{... | collective-permute-start | bytes 393224 | tf_op jit(solution)/shard_map/ppermute | solution.py:47
  18.0 4.3 %collective-permute-start.6 = (bf16[5,512]{1,0:T(8,128)(2,1)S(1)}, bf16[5,512]{1,0:T(8,128)(2,1)S(1)}, u32[]{:S(2)}, u32[]{:S(2)}) collective-permute-start(bf16[5,512]{1,0:T(8,128)(2,1)S(1)} %slice.270), channel_id=1, source_target_pairs={{0,4},{4,8},{8,12},{12,16},{16,20},{20,24},{24,28},{1,5},{5,9},{9,... | collective-permute-start | bytes 15368 | tf_op jit(solution)/shard_map/ppermute | solution.py:23
  19.7 10.3 %collective-permute-start.3 = (bf16[1,128,512]{2,1,0:T(8,128)(2,1)S(1)}, bf16[1,128,512]{2,1,0:T(8,128)(2,1)S(1)}, u32[]{:S(2)}, u32[]{:S(2)}) collective-permute-start(bf16[1,128,512]{2,1,0:T(8,128)(2,1)S(1)} %bitcast.82), channel_id=1, source_target_pairs={{0,16},{4,20},{8,24},{12,28},{16,0},{20,4},{24,8},{28,12},{1,17},{... | collective-permute-start | bytes 393224 | tf_op jit(solution)/shard_map/ppermute | solution.py:47
  20.7 8.9 %collective-permute-start.8 = (bf16[2,128,512]{2,1,0:T(8,128)(2,1)S(1)}, bf16[2,128,512]{2,1,0:T(8,128)(2,1)S(1)}, u32[]{:S(2)}, u32[]{:S(2)}) collective-permute-start(bf16[2,128,512]{2,1,0:T(8,128)(2,1)S(1)} %maximum_select_fusion.5), channel_id=1, source_target_pairs={{0,8},{4,12},{8,0},{12,4},{16,24},{20,28},{24,16},{28,20},{1,9},{5... | collective-permute-start | bytes 786440 | tf_op jit(solution)/shard_map/ppermute | solution.py:47
  29.7 9.1 %collective-permute-start.9 = (bf16[4,128,512]{2,1,0:T(8,128)(2,1)S(1)}, bf16[4,128,512]{2,1,0:T(8,128)(2,1)S(1)}, u32[]{:S(2)}, u32[]{:S(2)}) collective-permute-start(bf16[4,128,512]{2,1,0:T(8,128)(2,1)S(1)} %maximum_select_fusion.3), channel_id=1, source_target_pairs={{0,4},{4,0},{8,12},{12,8},{16,20},{20,16},{24,28},{28,24},{1,5},{5... | collective-permute-start | bytes 1572872 | tf_op jit(solution)/shard_map/ppermute | solution.py:47
  30.0 8.6 %collective-permute-start.4 = (bf16[2,128,512]{2,1,0:T(8,128)(2,1)S(1)}, bf16[2,128,512]{2,1,0:T(8,128)(2,1)S(1)}, u32[]{:S(2)}, u32[]{:S(2)}) collective-permute-start(bf16[2,128,512]{2,1,0:T(8,128)(2,1)S(1)} %maximum_select_fusion.4), channel_id=1, source_target_pairs={{0,8},{4,12},{8,0},{12,4},{16,24},{20,28},{24,16},{28,20},{1,9},{5... | collective-permute-start | bytes 786440 | tf_op jit(solution)/shard_map/ppermute | solution.py:47
  31.2 7.8 %copy-start = (bf16[128,4,6,128]{0,3,2,1:T(8,128)(2,1)}, bf16[128,4,6,128]{0,3,2,1:T(8,128)(2,1)S(1)}, u32[]{:S(2)}) copy-start(bf16[128,4,6,128]{0,3,2,1:T(8,128)(2,1)S(1)} %constant_dynamic-update-slice_fusion) | copy-start | bytes 2359300
  38.7 29.0 %collective-permute-start.5 = (bf16[4,128,512]{2,1,0:T(8,128)(2,1)S(1)}, bf16[4,128,512]{2,1,0:T(8,128)(2,1)S(1)}, u32[]{:S(2)}, u32[]{:S(2)}) collective-permute-start(bf16[4,128,512]{2,1,0:T(8,128)(2,1)S(1)} %maximum_select_fusion.2), channel_id=1, source_target_pairs={{0,4},{4,0},{8,12},{12,8},{16,20},{20,16},{24,28},{28,24},{1,5},{5... | collective-permute-start | bytes 1572872 | tf_op jit(solution)/shard_map/ppermute | solution.py:47
  40.3 0.9 %copy-start.1 = (bf16[128,4,128]{2,1,0:T(4,128)(2,1)S(1)}, bf16[128,4,128]{2,1,0:T(4,128)(2,1)}, u32[]{:S(2)}) copy-start(bf16[128,4,128]{2,1,0:T(4,128)(2,1)} %concatenate.67) | copy-start | bytes 393220
  42.3 19.3 %copy-start.5 = (f32[4]{0:T(128)S(1)}, f32[4]{0:T(128)}, u32[]{:S(2)}) copy-start(f32[4]{0:T(128)} %get-tuple-element.11) | copy-start | bytes 52
  42.3 19.3 %copy-start.6 = (f32[4]{0:T(128)S(1)}, f32[4]{0:T(128)}, u32[]{:S(2)}) copy-start(f32[4]{0:T(128)} %get-tuple-element.12) | copy-start | bytes 52
  42.3 19.3 %copy-start.7 = (f32[4]{0:T(128)S(1)}, f32[4]{0:T(128)}, u32[]{:S(2)}) copy-start(f32[4]{0:T(128)} %get-tuple-element.13) | copy-start | bytes 52
  42.3 19.3 %copy-start.8 = (f32[4]{0:T(128)S(1)}, f32[4]{0:T(128)}, u32[]{:S(2)}) copy-start(f32[4]{0:T(128)} %get-tuple-element.16) | copy-start | bytes 52
  42.3 19.3 %copy-start.9 = (f32[4]{0:T(128)S(1)}, f32[4]{0:T(128)}, u32[]{:S(2)}) copy-start(f32[4]{0:T(128)} %get-tuple-element.17) | copy-start | bytes 52
  42.3 19.3 %copy-start.10 = (f32[4]{0:T(128)S(1)}, f32[4]{0:T(128)}, u32[]{:S(2)}) copy-start(f32[4]{0:T(128)} %get-tuple-element.20) | copy-start | bytes 52
  42.4 20.0 %copy-start.12 = (f32[4]{0:T(128)S(1)}, f32[4]{0:T(128)}, u32[]{:S(2)}) copy-start(f32[4]{0:T(128)} %get-tuple-element.15) | copy-start | bytes 52
  42.4 20.0 %copy-start.13 = (f32[4]{0:T(128)S(1)}, f32[4]{0:T(128)}, u32[]{:S(2)}) copy-start(f32[4]{0:T(128)} %get-tuple-element.19) | copy-start | bytes 52
  42.4 20.0 %copy-start.14 = (f32[4]{0:T(128)S(1)}, f32[4]{0:T(128)}, u32[]{:S(2)}) copy-start(f32[4]{0:T(128)} %get-tuple-element.22) | copy-start | bytes 52
  42.4 20.0 %copy-start.15 = (f32[4]{0:T(128)S(1)}, f32[4]{0:T(128)}, u32[]{:S(2)}) copy-start(f32[4]{0:T(128)} %get-tuple-element.24) | copy-start | bytes 52
  42.5 20.0 %copy-start.17 = (f32[4]{0:T(128)S(1)}, f32[4]{0:T(128)}, u32[]{:S(2)}) copy-start(f32[4]{0:T(128)} %get-tuple-element.10) | copy-start | bytes 52
  42.5 20.0 %copy-start.18 = (f32[4]{0:T(128)S(1)}, f32[4]{0:T(128)}, u32[]{:S(2)}) copy-start(f32[4]{0:T(128)} %get-tuple-element.14) | copy-start | bytes 52
  42.5 20.0 %copy-start.19 = (f32[4]{0:T(128)S(1)}, f32[4]{0:T(128)}, u32[]{:S(2)}) copy-start(f32[4]{0:T(128)} %get-tuple-element.18) | copy-start | bytes 52
  42.5 20.0 %copy-start.20 = (f32[4]{0:T(128)S(1)}, f32[4]{0:T(128)}, u32[]{:S(2)}) copy-start(f32[4]{0:T(128)} %get-tuple-element.21) | copy-start | bytes 52
  42.5 20.0 %copy-start.21 = (f32[4]{0:T(128)S(1)}, f32[4]{0:T(128)}, u32[]{:S(2)}) copy-start(f32[4]{0:T(128)} %get-tuple-element.23) | copy-start | bytes 52
  67.9 1.8 %copy-start.2 = (f32[1024,128]{1,0:T(8,128)S(1)}, f32[1024,128]{1,0:T(8,128)}, u32[]{:S(2)}) copy-start(f32[1024,128]{1,0:T(8,128)} %get-tuple-element.29) | copy-start | bytes 1572868
  67.9 1.8 %copy-start.24 = (f32[4]{0:T(128)S(1)}, f32[4]{0:T(128)}, u32[]{:S(2)}) copy-start(f32[4]{0:T(128)} %get-tuple-element.25) | copy-start | bytes 52
  67.9 1.8 %copy-start.25 = (f32[4]{0:T(128)S(1)}, f32[4]{0:T(128)}, u32[]{:S(2)}) copy-start(f32[4]{0:T(128)} %get-tuple-element.26) | copy-start | bytes 52
  67.9 1.8 %copy-start.26 = (f32[4]{0:T(128)S(1)}, f32[4]{0:T(128)}, u32[]{:S(2)}) copy-start(f32[4]{0:T(128)} %get-tuple-element.27) | copy-start | bytes 52
  67.9 1.8 %copy-start.27 = (f32[4]{0:T(128)S(1)}, f32[4]{0:T(128)}, u32[]{:S(2)}) copy-start(f32[4]{0:T(128)} %get-tuple-element.28) | copy-start | bytes 52
  68.9 1.1 %copy-start.3 = (f32[1024,128]{1,0:T(8,128)S(1)}, f32[1024,128]{1,0:T(8,128)}, u32[]{:S(2)}) copy-start(f32[1024,128]{1,0:T(8,128)} %get-tuple-element.30) | copy-start | bytes 1572868
  70.0 2.2 %copy-start.16 = (f32[512]{0:T(512)S(1)}, f32[512]{0:T(512)}, u32[]{:S(2)}) copy-start(f32[512]{0:T(512)} %param.11) | copy-start | bytes 6148
  72.1 9.6 %copy-start.23 = (pred[4]{0:T(512)(128)(4,1)S(1)}, pred[4]{0:T(512)(128)(4,1)}, u32[]{:S(2)}) copy-start(pred[4]{0:T(512)(128)(4,1)} %copy-done.22) | copy-start | bytes 16
  72.6 5.8 %collective-permute-start.10 = (bf16[32,512]{1,0:T(8,128)(2,1)S(1)}, bf16[32,512]{1,0:T(8,128)(2,1)S(1)}, u32[]{:S(2)}, u32[]{:S(2)}) collective-permute-start(bf16[32,512]{1,0:T(8,128)(2,1)S(1)} %copy.81), channel_id=1, source_target_pairs={{0,1},{1,2},{2,3},{3,0},{4,5},{5,6},{6,7},{7,4},{8,9},{9,10},{10,1... | collective-permute-start | bytes 98312 | tf_op jit(solution)/shard_map/ppermute | solution.py:33
  75.2 5.2 %collective-permute-start.11 = (bf16[32,512]{1,0:T(8,128)(2,1)S(1)}, bf16[32,512]{1,0:T(8,128)(2,1)S(1)}, u32[]{:S(2)}, u32[]{:S(2)}) collective-permute-start(bf16[32,512]{1,0:T(8,128)(2,1)S(1)} %copy.82), channel_id=1, source_target_pairs={{0,2},{1,3},{2,0},{3,1},{4,6},{5,7},{6,4},{7,5},{8,10},{9,11},{10,... | collective-permute-start | bytes 98312 | tf_op jit(solution)/shard_map/ppermute | solution.py:33
  77.0 4.0 %collective-permute-start.12 = (bf16[32,512]{1,0:T(8,128)(2,1)S(1)}, bf16[32,512]{1,0:T(8,128)(2,1)S(1)}, u32[]{:S(2)}, u32[]{:S(2)}) collective-permute-start(bf16[32,512]{1,0:T(8,128)(2,1)S(1)} %copy.83), channel_id=1, source_target_pairs={{0,3},{1,0},{2,1},{3,2},{4,7},{5,4},{6,5},{7,6},{8,11},{9,8},{10,9... | collective-permute-start | bytes 98312 | tf_op jit(solution)/shard_map/ppermute | solution.py:33

commit v7 on v6

--- a/solution.py
+++ b/solution.py
@@ -61,16 +61,15 @@
 
     @pl.when(group == 0)
     def _():
-        lag = (
-            lax.broadcasted_iota(jnp.int32, (KEY_BLOCK, 2 * KEY_BLOCK), 0)
-            + KEY_BLOCK
-            - lax.broadcasted_iota(jnp.int32, (KEY_BLOCK, 2 * KEY_BLOCK), 1)
-        )
+        lane = lax.broadcasted_iota(jnp.int32, (1, 2 * KEY_BLOCK), 1)
         for row_lag in range(QCONV):
-            toeplitz = jnp.zeros(lag.shape, jnp.float32)
+            row = jnp.zeros(lane.shape, jnp.float32)
             for col_lag in range(KCONV):
                 tap = taps_ref[(head * QCONV + row_lag) * KCONV + col_lag]
-                toeplitz = jnp.where(lag == col_lag, tap, toeplitz)
+                row = jnp.where(lane == KEY_BLOCK - col_lag, tap, row)
+            toeplitz = pltpu.roll(
+                jnp.broadcast_to(row, (KEY_BLOCK, 2 * KEY_BLOCK)), 0, 1, stride=1, stride_axis=0
+            )
             high = toeplitz.astype(jnp.bfloat16)
             low = (toeplitz - high.astype(jnp.float32)).astype(jnp.bfloat16)
             high_ref[row_lag * KEY_BLOCK : (row_lag + 1) * KEY_BLOCK] = high

time: 82.8 us -> 82.4 us (level)
  no operation moved by 1% of the time
where the time goes in v7:
time: 82.4 us; the launch traced here: 82 us
  starting transfers between devices  18.9 us (23%)
  waiting for transfers between devices  18.7 us (23%)
  Pallas kernels  18.7 us (23%)
  local copies, waits for them, and re-layouts  13.3 us (16%)
  other arithmetic  9.53 us (12%)
  matrix products  2.13 us (3%)
    pallas_call x1, Pallas kernels, conv_logits(): pl.pallas_call(logits_kernel, grid=(heads, seq_len // span), in_specs=[pl...  18.7 us
    ppermute x6, waiting for transfers between devices, gathered(): incoming = lax.ppermute(held, axis, [(i, i ^ bit) for i in range(peers)])  14.2 us
    ppermute x6, starting transfers between devices, exchanged(): received.append(lax.ppermute(outgoing, axis, pairs))  12.1 us
    ppermute x6, starting transfers between devices, gathered(): incoming = lax.ppermute(held, axis, [(i, i ^ bit) for i in range(peers)])  5.33 us
    ppermute x6, waiting for transfers between devices, exchanged(): received.append(lax.ppermute(outgoing, axis, pairs))  4.51 us
    div x1, other arithmetic, attend_chunk(): probabilities = expd / jnp.sum(expd, axis=1, keepdims=True)  3.75 us
    dot_general x1, matrix products, attend_chunk(): jnp.einsum('hki,khd->ihd', mixed_probs, value_heads, preferred_element_ty...  2.13 us
    slice x1, local copies, waits for them, and re-layouts, band_terms(): score_kernel[None, :, row_lag, col_lag]  1.89 us
  transfers between devices with their start and end apart: 13, of which 6 were waited for; matrix products, arithmetic and copies ran while one was open for 20% of the time, Pallas kernels for 23%

profile of v7, /device:TPU:0, one launch (start us, length us, event | category | flops | bytes accessed | tf_op | source)
XLA Modules:
  0.0 82.0 jit_solution(8750627777067414764)
XLA Ops:
  0.0 1.1 %pad_maximum_fusion = bf16[3,32,2048]{2,1,0:T(8,128)(2,1)S(1)} fusion(bf16[1,32,2048]{2,1,0:T(8,128)(2,1)} %bitcast.91, bf16[1,32,2048]{2,1,0:T(8,128)(2,1)} %bitcast.92, bf16[1,32,2048]{2,1,0:T(8,128)(2,1)} %bitcast.93), kind=kLoop, calls=%fused_computation.40 | loop fusion | flops 393216 | bytes 786432 | tf_op jit(solution)/shard_map/stack | solution.py:184
  1.1 3.1 %collective-permute-start = (bf16[3,32,512]{2,1,0:T(8,128)(2,1)S(1)}, bf16[3,32,512]{2,1,0:T(8,128)(2,1)S(1)}, u32[]{:S(2)}, u32[]{:S(2)}) collective-permute-start(bf16[3,32,512]{2,1,0:T(8,128)(2,1)S(1)} %get-tuple-element.39), channel_id=1, source_target_pairs={{0,1},{1,2},{2,3},{3,0},{4,5},{5,6},{6,7},{7,4},{8,9},{9,10},{10,1... | collective-permute-start | bytes 294920 | tf_op jit(solution)/shard_map/ppermute | solution.py:33
  4.2 2.6 %collective-permute-start.1 = (bf16[3,32,512]{2,1,0:T(8,128)(2,1)S(1)}, bf16[3,32,512]{2,1,0:T(8,128)(2,1)S(1)}, u32[]{:S(2)}, u32[]{:S(2)}) collective-permute-start(bf16[3,32,512]{2,1,0:T(8,128)(2,1)S(1)} %get-tuple-element.38), channel_id=1, source_target_pairs={{0,2},{1,3},{2,0},{3,1},{4,6},{5,7},{6,4},{7,5},{8,10},{9,11},{10,... | collective-permute-start | bytes 294920 | tf_op jit(solution)/shard_map/ppermute | solution.py:33
  6.8 1.3 %collective-permute-start.2 = (bf16[3,32,512]{2,1,0:T(8,128)(2,1)S(1)}, bf16[3,32,512]{2,1,0:T(8,128)(2,1)S(1)}, u32[]{:S(2)}, u32[]{:S(2)}) collective-permute-start(bf16[3,32,512]{2,1,0:T(8,128)(2,1)S(1)} %get-tuple-element.37), channel_id=1, source_target_pairs={{0,3},{1,0},{2,1},{3,2},{4,7},{5,4},{6,5},{7,6},{8,11},{9,8},{10,9... | collective-permute-start | bytes 294920 | tf_op jit(solution)/shard_map/ppermute | solution.py:33
  8.2 1.9 %slice_reduce_fusion.17 = (f32[4]{0:T(128)}, f32[4]{0:T(128)}, f32[4]{0:T(128)}, f32[4]{0:T(128)}, f32[4]{0:T(128)}, /*index=5*/f32[4]{0:T(128)}, f32[4]{0:T(128...) fusion(f32[4,6,11]{2,0,1:T(4,128)} %param.9), kind=kLoop, calls=%fused_computation.135 | loop fusion | bytes 480 | tf_op jit(solution)/shard_map/slice | solution.py:144
  10.1 0.7 broadcast_multiply_fusion
  10.8 1.2 %fusion.15 = (pred[1024,128]{1,0:T(8,128)(4,1)S(1)}, pred[1024,128]{1,0:T(8,128)(4,1)S(1)}, pred[1024,128]{1,0:T(8,128)(4,1)S(1)}, pred[1024,128]{1,0:T(8,128)(4...) fusion(s32[128]{0:T(128)S(1)} %iota_add_fusion), kind=kLoop, calls=%fused_computation.39 | loop fusion | flops 917504 | bytes 786944 | tf_op jit(solution)/shard_map/ge | solution.py:160
  12.0 1.4 %collective-permute-done.1 = bf16[3,32,512]{2,1,0:T(8,128)(2,1)S(1)} collective-permute-done((bf16[3,32,512]{2,1,0:T(8,128)(2,1)S(1)}, bf16[3,32,512]{2,1,0:T(8,128)(2,1)S(1)}, u32[]{:S(2)}, u32[]{:S(2)}) %collective-permute-start.1) | collective-permute-done | bytes 98336 | tf_op jit(solution)/shard_map/ppermute | solution.py:33
  13.5 0.6 gather_fusion
  14.1 0.1 select_bitcast_fusion
  14.2 1.6 %collective-permute-start.7 = (bf16[1,128,512]{2,1,0:T(8,128)(2,1)S(1)}, bf16[1,128,512]{2,1,0:T(8,128)(2,1)S(1)}, u32[]{:S(2)}, u32[]{:S(2)}) collective-permute-start(bf16[1,128,512]{2,1,0:T(8,128)(2,1)S(1)} %bitcast.84), channel_id=1, source_target_pairs={{0,16},{4,20},{8,24},{12,28},{16,0},{20,4},{24,8},{28,12},{1,17},{... | collective-permute-start | bytes 393224 | tf_op jit(solution)/shard_map/ppermute | solution.py:47
  15.8 0.8 slice_reduce_fusion.18
  16.6 0.7 reshape.179.taps_ref
  17.3 0.7 concatenate.67
  18.0 1.5 %collective-permute-start.6 = (bf16[5,512]{1,0:T(8,128)(2,1)S(1)}, bf16[5,512]{1,0:T(8,128)(2,1)S(1)}, u32[]{:S(2)}, u32[]{:S(2)}) collective-permute-start(bf16[5,512]{1,0:T(8,128)(2,1)S(1)} %slice.270), channel_id=1, source_target_pairs={{0,4},{4,8},{8,12},{12,16},{16,20},{20,24},{24,28},{1,5},{5,9},{9,... | collective-permute-start | bytes 15368 | tf_op jit(solution)/shard_map/ppermute | solution.py:23
  19.6 0.1 copy.69
  19.7 1.0 %collective-permute-start.3 = (bf16[1,128,512]{2,1,0:T(8,128)(2,1)S(1)}, bf16[1,128,512]{2,1,0:T(8,128)(2,1)S(1)}, u32[]{:S(2)}, u32[]{:S(2)}) collective-permute-start(bf16[1,128,512]{2,1,0:T(8,128)(2,1)S(1)} %bitcast.82), channel_id=1, source_target_pairs={{0,16},{4,20},{8,24},{12,28},{16,0},{20,4},{24,8},{28,12},{1,17},{... | collective-permute-start | bytes 393224 | tf_op jit(solution)/shard_map/ppermute | solution.py:47
  20.7 1.6 %collective-permute-start.8 = (bf16[2,128,512]{2,1,0:T(8,128)(2,1)S(1)}, bf16[2,128,512]{2,1,0:T(8,128)(2,1)S(1)}, u32[]{:S(2)}, u32[]{:S(2)}) collective-permute-start(bf16[2,128,512]{2,1,0:T(8,128)(2,1)S(1)} %maximum_select_fusion.5), channel_id=1, source_target_pairs={{0,8},{4,12},{8,0},{12,4},{16,24},{20,28},{24,16},{28,20},{1,9},{5... | collective-permute-start | bytes 786440 | tf_op jit(solution)/shard_map/ppermute | solution.py:47
  22.3 0.1 pad_maximum_fusion.3
  22.4 0.1 copy.64
  22.6 0.1 copy.65
  22.7 0.1 copy.66
  22.9 6.8 %collective-permute-done.8 = bf16[2,128,512]{2,1,0:T(8,128)(2,1)S(1)} collective-permute-done((bf16[2,128,512]{2,1,0:T(8,128)(2,1)S(1)}, bf16[2,128,512]{2,1,0:T(8,128)(2,1)S(1)}, u32[]{:S(2)}, u32[]{:S(2)}) %collective-permute-start.8) | collective-permute-done | bytes 262176 | tf_op jit(solution)/shard_map/ppermute | solution.py:47
  29.7 0.2 collective-permute-start.9
  30.0 0.9 %collective-permute-start.4 = (bf16[2,128,512]{2,1,0:T(8,128)(2,1)S(1)}, bf16[2,128,512]{2,1,0:T(8,128)(2,1)S(1)}, u32[]{:S(2)}, u32[]{:S(2)}) collective-permute-start(bf16[2,128,512]{2,1,0:T(8,128)(2,1)S(1)} %maximum_select_fusion.4), channel_id=1, source_target_pairs={{0,8},{4,12},{8,0},{12,4},{16,24},{20,28},{24,16},{28,20},{1,9},{5... | collective-permute-start | bytes 786440 | tf_op jit(solution)/shard_map/ppermute | solution.py:47
  30.9 0.1 copy.67
  31.0 0.1 copy.68
  31.3 7.4 %collective-permute-done.4 = bf16[2,128,512]{2,1,0:T(8,128)(2,1)S(1)} collective-permute-done((bf16[2,128,512]{2,1,0:T(8,128)(2,1)S(1)}, bf16[2,128,512]{2,1,0:T(8,128)(2,1)S(1)}, u32[]{:S(2)}, u32[]{:S(2)}) %collective-permute-start.4) | collective-permute-done | bytes 262176 | tf_op jit(solution)/shard_map/ppermute | solution.py:47
  38.6 0.1 maximum_select_fusion.2
  38.8 0.2 maximum_select_fusion.1
  39.1 1.1 %concatenate.65.keys_ref = bf16[1152,512]{1,0:T(8,128)(2,1)} pad(bf16[1024,512]{1,0:T(8,128)(2,1)S(1)} %bitcast.74, bf16[]{:T(256)} %constant.106.clone.1), padding=128_0x0_0 | pad | bytes 2228226 | tf_op jit(solution)/shard_map/concatenate | solution.py:206
  40.2 0.1 fusion.24
  40.3 0.1 fusion.56
  40.4 0.1 slice.221
  40.5 0.1 slice.225
  40.6 0.1 slice.231
  40.7 0.1 slice.239
  40.8 0.1 slice.249
  40.9 0.3 copy-done.1
  41.2 0.8 fusion.21
  42.0 0.1 copy.71
  42.1 0.1 copy.74
  42.2 0.1 copy.72
  42.5 18.7 %shard_map.64 = f32[4,1024,128]{2,1,0:T(8,128)} custom-call(f32[264]{0:T(512)} %reshape.179.taps_ref, bf16[4,768,128]{2,1,0:T(8,128)(2,1)} %bitcast.81, bf16[1152,512]{1,0:T(8,128)(2,1)} %concatenate.65.keys_ref), custom_call_target="tpu_custom_call" | custom-call | tf_op jit(solution)/shard_map/pallas_call | solution.py:107
  61.3 0.7 subtract_bitcast_fusion.2
  61.9 0.1 subtract_bitcast_fusion.3
  62.1 0.1 fusion.44
  62.2 3.8 %divide_bitcast_fusion = f32[1,4,1024,128]{3,2,1,0:T(8,128)S(1)} fusion(f32[4,1024,128]{2,1,0:T(8,128)} %shard_map.64, f32[4,128]{1,0:T(4,128)} %get-tuple-element.56, f32[4,128]{1,0:T(4,128)S(1)} %get-tuple-element.55, f32[4,128]{1,0:T(4,128)S(1)} %get-tuple-element.54, f32[4,128]{1,0:T(4,128)S(1)} %subtract_bitcast_fusion.3, f32[4,128]{1,0:T(4,128)S(1)} %fusion.44, ...), kind=kOutput, calls=%fused_computation.5 | output fusion | flops 6818814 | bytes 4990976 | tf_op jit(solution)/shard_map/div | solution.py:163
  65.9 1.4 %slice_bitcast_fusion.3 = (f32[1024,128]{1,0:T(8,128)}, f32[1024,128]{1,0:T(8,128)}, f32[1024,128]{1,0:T(8,128)}, f32[1024,128]{1,0:T(8,128)}) fusion(f32[1,4,1024,128]{3,2,1,0:T(8,128)S(1)} %divide_bitcast_fusion), kind=kLoop, calls=%fused_computation.30 | loop fusion | bytes 4194304 | tf_op jit(solution)/shard_map/mul | solution.py:168
  67.3 0.2 maximum_select_fusion
  67.5 0.9 %copy.62 = bf16[2,2,2,128,512]{3,2,1,0,4:T(2,128)(2,1)S(1)} copy(bf16[2,2,2,128,512]{4,3,0,1,2:T(8,128)(2,1)S(1)} %bitcast.76) | data formatting | bytes 2097152 | tf_op jit(solution)/shard_map/transpose | solution.py:55
  68.5 0.8 reshape_reshape.3
  69.3 0.2 copy-done.3
  69.5 2.1 %multiply_reduce_fusion = (f32[128,4]{0,1:T(4,128)S(1)}, f32[128,4,128]{0,2,1:T(8,128)S(1)}) fusion(bf16[1024,4,128]{0,2,1:T(8,128)(2,1)S(1)} %reshape_reshape.3, f32[1024,128]{1,0:T(8,128)S(1)} %copy-done.3, f32[4]{0:T(128)S(1)} %copy-done.25, f32[1024,128]{1,0:T(8,128)} %get-tuple-element.31, f32[4]{0:T(128)S(1)} %copy-done.26, ...), kind=kOutput, calls=%fused_computation.56 | convolution fusion | flops 138542592 | bytes 3409984 | tf_op jit(solution)/shard_map/hki,khd->ihd/dot_general | solution.py:170
  71.7 0.1 multiply_convert_fusion
  71.8 0.2 constant_dynamic-slice_fusion.3
  72.1 2.6 %collective-permute-start.10 = (bf16[32,512]{1,0:T(8,128)(2,1)S(1)}, bf16[32,512]{1,0:T(8,128)(2,1)S(1)}, u32[]{:S(2)}, u32[]{:S(2)}) collective-permute-start(bf16[32,512]{1,0:T(8,128)(2,1)S(1)} %copy.81), channel_id=1, source_target_pairs={{0,1},{1,2},{2,3},{3,0},{4,5},{5,6},{6,7},{7,4},{8,9},{9,10},{10,1... | collective-permute-start | bytes 98312 | tf_op jit(solution)/shard_map/ppermute | solution.py:33
  74.8 1.7 %collective-permute-start.11 = (bf16[32,512]{1,0:T(8,128)(2,1)S(1)}, bf16[32,512]{1,0:T(8,128)(2,1)S(1)}, u32[]{:S(2)}, u32[]{:S(2)}) collective-permute-start(bf16[32,512]{1,0:T(8,128)(2,1)S(1)} %copy.82), channel_id=1, source_target_pairs={{0,2},{1,3},{2,0},{3,1},{4,6},{5,7},{6,4},{7,5},{8,10},{9,11},{10,... | collective-permute-start | bytes 98312 | tf_op jit(solution)/shard_map/ppermute | solution.py:33
  76.6 0.8 collective-permute-start.12
  77.5 0.4 collective-permute-done.10
  77.9 2.1 %collective-permute-done.11 = bf16[32,512]{1,0:T(8,128)(2,1)S(1)} collective-permute-done((bf16[32,512]{1,0:T(8,128)(2,1)S(1)}, bf16[32,512]{1,0:T(8,128)(2,1)S(1)}, u32[]{:S(2)}, u32[]{:S(2)}) %collective-permute-start.11) | collective-permute-done | bytes 32800 | tf_op jit(solution)/shard_map/ppermute | solution.py:33
  80.0 0.5 collective-permute-done.12
  80.6 0.7 gather_fusion.1
  81.4 0.7 copy.85
  (96 shorter events, 1.3 us)
Async XLA Ops:
  1.1 14.7 %copy-start.4 = (f32[4,4]{1,0:T(4,128)S(1)}, f32[4,4]{1,0:T(4,128)}, u32[]{:S(2)}) copy-start(f32[4,4]{1,0:T(4,128)} %param.10) | copy-start | bytes 196
  1.1 10.9 %collective-permute-start = (bf16[3,32,512]{2,1,0:T(8,128)(2,1)S(1)}, bf16[3,32,512]{2,1,0:T(8,128)(2,1)S(1)}, u32[]{:S(2)}, u32[]{:S(2)}) collective-permute-start(bf16[3,32,512]{2,1,0:T(8,128)(2,1)S(1)} %get-tuple-element.39), channel_id=1, source_target_pairs={{0,1},{1,2},{2,3},{3,0},{4,5},{5,6},{6,7},{7,4},{8,9},{9,10},{10,1... | collective-permute-start | bytes 294920 | tf_op jit(solution)/shard_map/ppermute | solution.py:33
  4.2 9.2 %collective-permute-start.1 = (bf16[3,32,512]{2,1,0:T(8,128)(2,1)S(1)}, bf16[3,32,512]{2,1,0:T(8,128)(2,1)S(1)}, u32[]{:S(2)}, u32[]{:S(2)}) collective-permute-start(bf16[3,32,512]{2,1,0:T(8,128)(2,1)S(1)} %get-tuple-element.38), channel_id=1, source_target_pairs={{0,2},{1,3},{2,0},{3,1},{4,6},{5,7},{6,4},{7,5},{8,10},{9,11},{10,... | collective-permute-start | bytes 294920 | tf_op jit(solution)/shard_map/ppermute | solution.py:33
  6.8 6.6 %collective-permute-start.2 = (bf16[3,32,512]{2,1,0:T(8,128)(2,1)S(1)}, bf16[3,32,512]{2,1,0:T(8,128)(2,1)S(1)}, u32[]{:S(2)}, u32[]{:S(2)}) collective-permute-start(bf16[3,32,512]{2,1,0:T(8,128)(2,1)S(1)} %get-tuple-element.37), channel_id=1, source_target_pairs={{0,3},{1,0},{2,1},{3,2},{4,7},{5,4},{6,5},{7,6},{8,11},{9,8},{10,9... | collective-permute-start | bytes 294920 | tf_op jit(solution)/shard_map/ppermute | solution.py:33
  10.8 7.2 %copy-start.11 = (s32[1024]{0:T(1024)}, s32[1024]{0:T(1024)S(1)}, u32[]{:S(2)}) copy-start(s32[1024]{0:T(1024)S(1)} %pad_clamp_fusion) | copy-start | bytes 12292
  12.0 8.7 %copy-start.22 = (pred[4]{0:T(512)(128)(4,1)}, pred[4]{0:T(512)(128)(4,1)S(1)}, u32[]{:S(2)}) copy-start(pred[4]{0:T(512)(128)(4,1)S(1)} %compare_and_fusion) | copy-start | bytes 16
  14.2 6.5 %collective-permute-start.7 = (bf16[1,128,512]{2,1,0:T(8,128)(2,1)S(1)}, bf16[1,128,512]{2,1,0:T(8,128)(2,1)S(1)}, u32[]{:S(2)}, u32[]{:S(2)}) collective-permute-start(bf16[1,128,512]{2,1,0:T(8,128)(2,1)S(1)} %bitcast.84), channel_id=1, source_target_pairs={{0,16},{4,20},{8,24},{12,28},{16,0},{20,4},{24,8},{28,12},{1,17},{... | collective-permute-start | bytes 393224 | tf_op jit(solution)/shard_map/ppermute | solution.py:47
  18.0 4.3 %collective-permute-start.6 = (bf16[5,512]{1,0:T(8,128)(2,1)S(1)}, bf16[5,512]{1,0:T(8,128)(2,1)S(1)}, u32[]{:S(2)}, u32[]{:S(2)}) collective-permute-start(bf16[5,512]{1,0:T(8,128)(2,1)S(1)} %slice.270), channel_id=1, source_target_pairs={{0,4},{4,8},{8,12},{12,16},{16,20},{20,24},{24,28},{1,5},{5,9},{9,... | collective-permute-start | bytes 15368 | tf_op jit(solution)/shard_map/ppermute | solution.py:23
  19.7 10.3 %collective-permute-start.3 = (bf16[1,128,512]{2,1,0:T(8,128)(2,1)S(1)}, bf16[1,128,512]{2,1,0:T(8,128)(2,1)S(1)}, u32[]{:S(2)}, u32[]{:S(2)}) collective-permute-start(bf16[1,128,512]{2,1,0:T(8,128)(2,1)S(1)} %bitcast.82), channel_id=1, source_target_pairs={{0,16},{4,20},{8,24},{12,28},{16,0},{20,4},{24,8},{28,12},{1,17},{... | collective-permute-start | bytes 393224 | tf_op jit(solution)/shard_map/ppermute | solution.py:47
  20.7 8.9 %collective-permute-start.8 = (bf16[2,128,512]{2,1,0:T(8,128)(2,1)S(1)}, bf16[2,128,512]{2,1,0:T(8,128)(2,1)S(1)}, u32[]{:S(2)}, u32[]{:S(2)}) collective-permute-start(bf16[2,128,512]{2,1,0:T(8,128)(2,1)S(1)} %maximum_select_fusion.5), channel_id=1, source_target_pairs={{0,8},{4,12},{8,0},{12,4},{16,24},{20,28},{24,16},{28,20},{1,9},{5... | collective-permute-start | bytes 786440 | tf_op jit(solution)/shard_map/ppermute | solution.py:47
  29.7 9.1 %collective-permute-start.9 = (bf16[4,128,512]{2,1,0:T(8,128)(2,1)S(1)}, bf16[4,128,512]{2,1,0:T(8,128)(2,1)S(1)}, u32[]{:S(2)}, u32[]{:S(2)}) collective-permute-start(bf16[4,128,512]{2,1,0:T(8,128)(2,1)S(1)} %maximum_select_fusion.3), channel_id=1, source_target_pairs={{0,4},{4,0},{8,12},{12,8},{16,20},{20,16},{24,28},{28,24},{1,5},{5... | collective-permute-start | bytes 1572872 | tf_op jit(solution)/shard_map/ppermute | solution.py:47
  30.0 8.6 %collective-permute-start.4 = (bf16[2,128,512]{2,1,0:T(8,128)(2,1)S(1)}, bf16[2,128,512]{2,1,0:T(8,128)(2,1)S(1)}, u32[]{:S(2)}, u32[]{:S(2)}) collective-permute-start(bf16[2,128,512]{2,1,0:T(8,128)(2,1)S(1)} %maximum_select_fusion.4), channel_id=1, source_target_pairs={{0,8},{4,12},{8,0},{12,4},{16,24},{20,28},{24,16},{28,20},{1,9},{5... | collective-permute-start | bytes 786440 | tf_op jit(solution)/shard_map/ppermute | solution.py:47
  31.2 7.8 %copy-start = (bf16[128,4,6,128]{0,3,2,1:T(8,128)(2,1)}, bf16[128,4,6,128]{0,3,2,1:T(8,128)(2,1)S(1)}, u32[]{:S(2)}) copy-start(bf16[128,4,6,128]{0,3,2,1:T(8,128)(2,1)S(1)} %constant_dynamic-update-slice_fusion) | copy-start | bytes 2359300
  38.7 28.6 %collective-permute-start.5 = (bf16[4,128,512]{2,1,0:T(8,128)(2,1)S(1)}, bf16[4,128,512]{2,1,0:T(8,128)(2,1)S(1)}, u32[]{:S(2)}, u32[]{:S(2)}) collective-permute-start(bf16[4,128,512]{2,1,0:T(8,128)(2,1)S(1)} %maximum_select_fusion.2), channel_id=1, source_target_pairs={{0,4},{4,0},{8,12},{12,8},{16,20},{20,16},{24,28},{28,24},{1,5},{5... | collective-permute-start | bytes 1572872 | tf_op jit(solution)/shard_map/ppermute | solution.py:47
  40.3 0.9 %copy-start.1 = (bf16[128,4,128]{2,1,0:T(4,128)(2,1)S(1)}, bf16[128,4,128]{2,1,0:T(4,128)(2,1)}, u32[]{:S(2)}) copy-start(bf16[128,4,128]{2,1,0:T(4,128)(2,1)} %concatenate.67) | copy-start | bytes 393220
  42.3 18.9 %copy-start.5 = (f32[4]{0:T(128)S(1)}, f32[4]{0:T(128)}, u32[]{:S(2)}) copy-start(f32[4]{0:T(128)} %get-tuple-element.11) | copy-start | bytes 52
  42.3 18.9 %copy-start.6 = (f32[4]{0:T(128)S(1)}, f32[4]{0:T(128)}, u32[]{:S(2)}) copy-start(f32[4]{0:T(128)} %get-tuple-element.12) | copy-start | bytes 52
  42.3 18.9 %copy-start.7 = (f32[4]{0:T(128)S(1)}, f32[4]{0:T(128)}, u32[]{:S(2)}) copy-start(f32[4]{0:T(128)} %get-tuple-element.13) | copy-start | bytes 52
  42.3 18.9 %copy-start.8 = (f32[4]{0:T(128)S(1)}, f32[4]{0:T(128)}, u32[]{:S(2)}) copy-start(f32[4]{0:T(128)} %get-tuple-element.16) | copy-start | bytes 52
  42.3 18.9 %copy-start.9 = (f32[4]{0:T(128)S(1)}, f32[4]{0:T(128)}, u32[]{:S(2)}) copy-start(f32[4]{0:T(128)} %get-tuple-element.17) | copy-start | bytes 52
  42.3 18.9 %copy-start.10 = (f32[4]{0:T(128)S(1)}, f32[4]{0:T(128)}, u32[]{:S(2)}) copy-start(f32[4]{0:T(128)} %get-tuple-element.20) | copy-start | bytes 52
  42.4 19.6 %copy-start.12 = (f32[4]{0:T(128)S(1)}, f32[4]{0:T(128)}, u32[]{:S(2)}) copy-start(f32[4]{0:T(128)} %get-tuple-element.15) | copy-start | bytes 52
  42.4 19.5 %copy-start.13 = (f32[4]{0:T(128)S(1)}, f32[4]{0:T(128)}, u32[]{:S(2)}) copy-start(f32[4]{0:T(128)} %get-tuple-element.19) | copy-start | bytes 52
  42.4 19.5 %copy-start.14 = (f32[4]{0:T(128)S(1)}, f32[4]{0:T(128)}, u32[]{:S(2)}) copy-start(f32[4]{0:T(128)} %get-tuple-element.22) | copy-start | bytes 52
  42.4 19.5 %copy-start.15 = (f32[4]{0:T(128)S(1)}, f32[4]{0:T(128)}, u32[]{:S(2)}) copy-start(f32[4]{0:T(128)} %get-tuple-element.24) | copy-start | bytes 52
  42.5 19.5 %copy-start.17 = (f32[4]{0:T(128)S(1)}, f32[4]{0:T(128)}, u32[]{:S(2)}) copy-start(f32[4]{0:T(128)} %get-tuple-element.10) | copy-start | bytes 52
  42.5 19.6 %copy-start.18 = (f32[4]{0:T(128)S(1)}, f32[4]{0:T(128)}, u32[]{:S(2)}) copy-start(f32[4]{0:T(128)} %get-tuple-element.14) | copy-start | bytes 52
  42.5 19.6 %copy-start.19 = (f32[4]{0:T(128)S(1)}, f32[4]{0:T(128)}, u32[]{:S(2)}) copy-start(f32[4]{0:T(128)} %get-tuple-element.18) | copy-start | bytes 52
  42.5 19.6 %copy-start.20 = (f32[4]{0:T(128)S(1)}, f32[4]{0:T(128)}, u32[]{:S(2)}) copy-start(f32[4]{0:T(128)} %get-tuple-element.21) | copy-start | bytes 52
  42.5 19.6 %copy-start.21 = (f32[4]{0:T(128)S(1)}, f32[4]{0:T(128)}, u32[]{:S(2)}) copy-start(f32[4]{0:T(128)} %get-tuple-element.23) | copy-start | bytes 52
  67.5 1.8 %copy-start.2 = (f32[1024,128]{1,0:T(8,128)S(1)}, f32[1024,128]{1,0:T(8,128)}, u32[]{:S(2)}) copy-start(f32[1024,128]{1,0:T(8,128)} %get-tuple-element.29) | copy-start | bytes 1572868
  67.5 1.8 %copy-start.24 = (f32[4]{0:T(128)S(1)}, f32[4]{0:T(128)}, u32[]{:S(2)}) copy-start(f32[4]{0:T(128)} %get-tuple-element.25) | copy-start | bytes 52
  67.5 1.8 %copy-start.25 = (f32[4]{0:T(128)S(1)}, f32[4]{0:T(128)}, u32[]{:S(2)}) copy-start(f32[4]{0:T(128)} %get-tuple-element.26) | copy-start | bytes 52
  67.5 1.8 %copy-start.26 = (f32[4]{0:T(128)S(1)}, f32[4]{0:T(128)}, u32[]{:S(2)}) copy-start(f32[4]{0:T(128)} %get-tuple-element.27) | copy-start | bytes 52
  67.5 1.8 %copy-start.27 = (f32[4]{0:T(128)S(1)}, f32[4]{0:T(128)}, u32[]{:S(2)}) copy-start(f32[4]{0:T(128)} %get-tuple-element.28) | copy-start | bytes 52
  68.5 1.1 %copy-start.3 = (f32[1024,128]{1,0:T(8,128)S(1)}, f32[1024,128]{1,0:T(8,128)}, u32[]{:S(2)}) copy-start(f32[1024,128]{1,0:T(8,128)} %get-tuple-element.30) | copy-start | bytes 1572868
  69.5 2.2 %copy-start.16 = (f32[512]{0:T(512)S(1)}, f32[512]{0:T(512)}, u32[]{:S(2)}) copy-start(f32[512]{0:T(512)} %param.11) | copy-start | bytes 6148
  71.7 9.6 %copy-start.23 = (pred[4]{0:T(512)(128)(4,1)S(1)}, pred[4]{0:T(512)(128)(4,1)}, u32[]{:S(2)}) copy-start(pred[4]{0:T(512)(128)(4,1)} %copy-done.22) | copy-start | bytes 16
  72.1 5.8 %collective-permute-start.10 = (bf16[32,512]{1,0:T(8,128)(2,1)S(1)}, bf16[32,512]{1,0:T(8,128)(2,1)S(1)}, u32[]{:S(2)}, u32[]{:S(2)}) collective-permute-start(bf16[32,512]{1,0:T(8,128)(2,1)S(1)} %copy.81), channel_id=1, source_target_pairs={{0,1},{1,2},{2,3},{3,0},{4,5},{5,6},{6,7},{7,4},{8,9},{9,10},{10,1... | collective-permute-start | bytes 98312 | tf_op jit(solution)/shard_map/ppermute | solution.py:33
  74.8 5.2 %collective-permute-start.11 = (bf16[32,512]{1,0:T(8,128)(2,1)S(1)}, bf16[32,512]{1,0:T(8,128)(2,1)S(1)}, u32[]{:S(2)}, u32[]{:S(2)}) collective-permute-start(bf16[32,512]{1,0:T(8,128)(2,1)S(1)} %copy.82), channel_id=1, source_target_pairs={{0,2},{1,3},{2,0},{3,1},{4,6},{5,7},{6,4},{7,5},{8,10},{9,11},{10,... | collective-permute-start | bytes 98312 | tf_op jit(solution)/shard_map/ppermute | solution.py:33
  76.6 4.0 %collective-permute-start.12 = (bf16[32,512]{1,0:T(8,128)(2,1)S(1)}, bf16[32,512]{1,0:T(8,128)(2,1)S(1)}, u32[]{:S(2)}, u32[]{:S(2)}) collective-permute-start(bf16[32,512]{1,0:T(8,128)(2,1)S(1)} %copy.83), channel_id=1, source_target_pairs={{0,3},{1,0},{2,1},{3,2},{4,7},{5,4},{6,5},{7,6},{8,11},{9,8},{10,9... | collective-permute-start | bytes 98312 | tf_op jit(solution)/shard_map/ppermute | solution.py:33

commit v8 on v7

--- a/solution.py
+++ b/solution.py
@@ -58,6 +58,7 @@
 def logits_kernel(taps_ref, query_ref, keys_ref, out_ref, high_ref, low_ref, conv_ref):
     head = pl.program_id(0)
     group = pl.program_id(1)
+    edge = 16
 
     @pl.when(group == 0)
     def _():
@@ -72,30 +73,42 @@
             )
             high = toeplitz.astype(jnp.bfloat16)
             low = (toeplitz - high.astype(jnp.float32)).astype(jnp.bfloat16)
-            high_ref[row_lag * KEY_BLOCK : (row_lag + 1) * KEY_BLOCK] = high
-            low_ref[row_lag * KEY_BLOCK : (row_lag + 1) * KEY_BLOCK] = low
-
-    blocks = conv_ref.shape[2] // KEY_BLOCK
+            high_ref[row_lag * KEY_BLOCK : (row_lag + 1) * KEY_BLOCK] = high[:, KEY_BLOCK:]
+            low_ref[row_lag * KEY_BLOCK : (row_lag + 1) * KEY_BLOCK] = low[:, KEY_BLOCK:]
+            top = QCONV * KEY_BLOCK + row_lag * edge
+            high_ref[top : top + edge] = high[:edge, :KEY_BLOCK]
+            low_ref[top : top + edge] = low[:edge, :KEY_BLOCK]
+
+    blocks = conv_ref.shape[1] // KEY_BLOCK
+    body = QCONV * KEY_BLOCK
     for block in range(blocks):
         start = pl.multiple_of((group * blocks + block) * KEY_BLOCK, KEY_BLOCK)
-        window = keys_ref[pl.ds(start, 2 * KEY_BLOCK), :]
-        conv_keys = jnp.dot(
-            high_ref[...], window, preferred_element_type=jnp.float32
-        ) + jnp.dot(low_ref[...], window, preferred_element_type=jnp.float32)
-        keys_high = conv_keys.astype(jnp.bfloat16)
-        keys_low = (conv_keys - keys_high.astype(jnp.float32)).astype(jnp.bfloat16)
-        rows = slice(block * KEY_BLOCK, (block + 1) * KEY_BLOCK)
+        before = keys_ref[pl.ds(start, KEY_BLOCK), :]
+        current = keys_ref[pl.ds(start + KEY_BLOCK, KEY_BLOCK), :]
+        conv_body = jnp.dot(
+            high_ref[:body], current, preferred_element_type=jnp.float32
+        ) + jnp.dot(low_ref[:body], current, preferred_element_type=jnp.float32)
+        conv_top = jnp.dot(
+            high_ref[body:], before, preferred_element_type=jnp.float32
+        ) + jnp.dot(low_ref[body:], before, preferred_element_type=jnp.float32)
+        base = block * KEY_BLOCK
         for row_lag in range(QCONV):
-            part = slice(row_lag * KEY_BLOCK, (row_lag + 1) * KEY_BLOCK)
-            conv_ref[0, row_lag, rows] = keys_high[part]
-            conv_ref[1, row_lag, rows] = keys_low[part]
-    head_dim = keys_ref.shape[1]
-    acc = jnp.zeros(out_ref.shape[1:], jnp.float32)
-    for row_lag in range(QCONV):
-        part = query_ref[0, row_lag * head_dim : (row_lag + 1) * head_dim, :]
-        acc = acc + jnp.dot(conv_ref[0, row_lag], part, preferred_element_type=jnp.float32)
-        acc = acc + jnp.dot(conv_ref[1, row_lag], part, preferred_element_type=jnp.float32)
-    out_ref[0] = acc
+            first = row_lag * KEY_BLOCK
+            head_rows = conv_body[first : first + edge] + conv_top[
+                row_lag * edge : (row_lag + 1) * edge
+            ]
+            rest_rows = conv_body[first + edge : first + KEY_BLOCK]
+            cols = slice(row_lag * KEY_BLOCK, (row_lag + 1) * KEY_BLOCK)
+            for part, rows in ((head_rows, slice(base, base + edge)),
+                               (rest_rows, slice(base + edge, base + KEY_BLOCK))):
+                part_high = part.astype(jnp.bfloat16)
+                part_low = (part - part_high.astype(jnp.float32)).astype(jnp.bfloat16)
+                conv_ref[0, rows, cols] = part_high
+                conv_ref[1, rows, cols] = part_low
+    query = query_ref[0]
+    out_ref[0] = jnp.dot(conv_ref[0], query, preferred_element_type=jnp.float32) + jnp.dot(
+        conv_ref[1], query, preferred_element_type=jnp.float32
+    )
 
 
 def conv_logits(shifted_t, score_kernel, key_pad):
@@ -115,9 +128,9 @@
         out_specs=pl.BlockSpec((1, span, row_count), lambda h, g: (h, g, 0)),
         out_shape=jax.ShapeDtypeStruct((heads, seq_len, row_count), jnp.float32),
         scratch_shapes=[
-            pltpu.VMEM((QCONV * KEY_BLOCK, 2 * KEY_BLOCK), jnp.bfloat16),
-            pltpu.VMEM((QCONV * KEY_BLOCK, 2 * KEY_BLOCK), jnp.bfloat16),
-            pltpu.VMEM((2, QCONV, span, head_dim), jnp.bfloat16),
+            pltpu.VMEM((QCONV * (KEY_BLOCK + 16), KEY_BLOCK), jnp.bfloat16),
+            pltpu.VMEM((QCONV * (KEY_BLOCK + 16), KEY_BLOCK), jnp.bfloat16),
+            pltpu.VMEM((2, span, QCONV * head_dim), jnp.bfloat16),
         ],
     )(taps, shifted_t, key_pad)
 

time: 82.4 us -> 74.6 us (0.905)
  Pallas kernels: 18.7 us -> 10.9 us
    pallas_call x1, Pallas kernels: 18.7 us -> 10.9 us  [conv_logits(): pl.pallas_call(logits_kernel, grid=(heads, seq_len // span), in_specs=[pl...]
  transfers between devices with their start and end apart: 13 -> 13, of which waited for: 6 -> 6; matrix products, arithmetic and copies ran while one was open for 20% -> 22% of each run, Pallas kernels for 23% -> 15%
where the time goes in v8:
time: 74.6 us; the launch traced here: 74.2 us
  starting transfers between devices  18.9 us (25%)
  waiting for transfers between devices  18.7 us (25%)
  local copies, waits for them, and re-layouts  13.3 us (18%)
  Pallas kernels  10.9 us (15%)
  other arithmetic  9.53 us (13%)
  matrix products  2.13 us (3%)
  between operations  0.76 us (1%)
    ppermute x6, waiting for transfers between devices, gathered(): incoming = lax.ppermute(held, axis, [(i, i ^ bit) for i in range(peers)])  14.2 us
    ppermute x6, starting transfers between devices, exchanged(): received.append(lax.ppermute(outgoing, axis, pairs))  12.1 us
    pallas_call x1, Pallas kernels, conv_logits(): pl.pallas_call(logits_kernel, grid=(heads, seq_len // span), in_specs=[pl...  10.9 us
    ppermute x6, starting transfers between devices, gathered(): incoming = lax.ppermute(held, axis, [(i, i ^ bit) for i in range(peers)])  5.33 us
    ppermute x6, waiting for transfers between devices, exchanged(): received.append(lax.ppermute(outgoing, axis, pairs))  4.52 us
    div x1, other arithmetic, attend_chunk(): probabilities = expd / jnp.sum(expd, axis=1, keepdims=True)  3.75 us
    dot_general x1, matrix products, attend_chunk(): jnp.einsum('hki,khd->ihd', mixed_probs, value_heads, preferred_element_ty...  2.13 us
    slice x1, local copies, waits for them, and re-layouts, band_terms(): score_kernel[None, :, row_lag, col_lag]  1.89 us
  transfers between devices with their start and end apart: 13, of which 6 were waited for; matrix products, arithmetic and copies ran while one was open for 22% of the time, Pallas kernels for 15%

profile of v8, /device:TPU:0, one launch (start us, length us, event | category | flops | bytes accessed | tf_op | source)
XLA Modules:
  0.0 74.2 jit_solution(15259104484399139531)
XLA Ops:
  0.0 1.1 %pad_maximum_fusion = bf16[3,32,2048]{2,1,0:T(8,128)(2,1)S(1)} fusion(bf16[1,32,2048]{2,1,0:T(8,128)(2,1)} %bitcast.91, bf16[1,32,2048]{2,1,0:T(8,128)(2,1)} %bitcast.92, bf16[1,32,2048]{2,1,0:T(8,128)(2,1)} %bitcast.93), kind=kLoop, calls=%fused_computation.40 | loop fusion | flops 393216 | bytes 786432 | tf_op jit(solution)/shard_map/stack | solution.py:197
  1.1 3.1 %collective-permute-start = (bf16[3,32,512]{2,1,0:T(8,128)(2,1)S(1)}, bf16[3,32,512]{2,1,0:T(8,128)(2,1)S(1)}, u32[]{:S(2)}, u32[]{:S(2)}) collective-permute-start(bf16[3,32,512]{2,1,0:T(8,128)(2,1)S(1)} %get-tuple-element.39), channel_id=1, source_target_pairs={{0,1},{1,2},{2,3},{3,0},{4,5},{5,6},{6,7},{7,4},{8,9},{9,10},{10,1... | collective-permute-start | bytes 294920 | tf_op jit(solution)/shard_map/ppermute | solution.py:33
  4.2 2.6 %collective-permute-start.1 = (bf16[3,32,512]{2,1,0:T(8,128)(2,1)S(1)}, bf16[3,32,512]{2,1,0:T(8,128)(2,1)S(1)}, u32[]{:S(2)}, u32[]{:S(2)}) collective-permute-start(bf16[3,32,512]{2,1,0:T(8,128)(2,1)S(1)} %get-tuple-element.38), channel_id=1, source_target_pairs={{0,2},{1,3},{2,0},{3,1},{4,6},{5,7},{6,4},{7,5},{8,10},{9,11},{10,... | collective-permute-start | bytes 294920 | tf_op jit(solution)/shard_map/ppermute | solution.py:33
  6.8 1.3 %collective-permute-start.2 = (bf16[3,32,512]{2,1,0:T(8,128)(2,1)S(1)}, bf16[3,32,512]{2,1,0:T(8,128)(2,1)S(1)}, u32[]{:S(2)}, u32[]{:S(2)}) collective-permute-start(bf16[3,32,512]{2,1,0:T(8,128)(2,1)S(1)} %get-tuple-element.37), channel_id=1, source_target_pairs={{0,3},{1,0},{2,1},{3,2},{4,7},{5,4},{6,5},{7,6},{8,11},{9,8},{10,9... | collective-permute-start | bytes 294920 | tf_op jit(solution)/shard_map/ppermute | solution.py:33
  8.2 1.9 %slice_reduce_fusion.17 = (f32[4]{0:T(128)}, f32[4]{0:T(128)}, f32[4]{0:T(128)}, f32[4]{0:T(128)}, f32[4]{0:T(128)}, /*index=5*/f32[4]{0:T(128)}, f32[4]{0:T(128...) fusion(f32[4,6,11]{2,0,1:T(4,128)} %param.9), kind=kLoop, calls=%fused_computation.135 | loop fusion | bytes 480 | tf_op jit(solution)/shard_map/slice | solution.py:157
  10.1 0.7 broadcast_multiply_fusion
  10.8 1.2 %fusion.15 = (pred[1024,128]{1,0:T(8,128)(4,1)S(1)}, pred[1024,128]{1,0:T(8,128)(4,1)S(1)}, pred[1024,128]{1,0:T(8,128)(4,1)S(1)}, pred[1024,128]{1,0:T(8,128)(4...) fusion(s32[128]{0:T(128)S(1)} %iota_add_fusion), kind=kLoop, calls=%fused_computation.39 | loop fusion | flops 917504 | bytes 786944 | tf_op jit(solution)/shard_map/ge | solution.py:173
  12.0 1.4 %collective-permute-done.1 = bf16[3,32,512]{2,1,0:T(8,128)(2,1)S(1)} collective-permute-done((bf16[3,32,512]{2,1,0:T(8,128)(2,1)S(1)}, bf16[3,32,512]{2,1,0:T(8,128)(2,1)S(1)}, u32[]{:S(2)}, u32[]{:S(2)}) %collective-permute-start.1) | collective-permute-done | bytes 98336 | tf_op jit(solution)/shard_map/ppermute | solution.py:33
  13.5 0.6 gather_fusion
  14.1 0.1 select_bitcast_fusion
  14.2 1.6 %collective-permute-start.7 = (bf16[1,128,512]{2,1,0:T(8,128)(2,1)S(1)}, bf16[1,128,512]{2,1,0:T(8,128)(2,1)S(1)}, u32[]{:S(2)}, u32[]{:S(2)}) collective-permute-start(bf16[1,128,512]{2,1,0:T(8,128)(2,1)S(1)} %bitcast.84), channel_id=1, source_target_pairs={{0,16},{4,20},{8,24},{12,28},{16,0},{20,4},{24,8},{28,12},{1,17},{... | collective-permute-start | bytes 393224 | tf_op jit(solution)/shard_map/ppermute | solution.py:47
  15.8 0.8 %slice_reduce_fusion.18 = (f32[4]{0:T(128)}, f32[4]{0:T(128)}, f32[4]{0:T(128)}, f32[4]{0:T(128)}) fusion(f32[1,4,4]{2,1,0:T(4,128)S(1)} %bitcast.98), kind=kLoop, calls=%fused_computation.136 | loop fusion | bytes 128 | tf_op jit(solution)/shard_map/slice | solution.py:181
  16.6 0.7 reshape.179.taps_ref
  17.3 0.7 concatenate.67
  18.0 1.5 %collective-permute-start.6 = (bf16[5,512]{1,0:T(8,128)(2,1)S(1)}, bf16[5,512]{1,0:T(8,128)(2,1)S(1)}, u32[]{:S(2)}, u32[]{:S(2)}) collective-permute-start(bf16[5,512]{1,0:T(8,128)(2,1)S(1)} %slice.270), channel_id=1, source_target_pairs={{0,4},{4,8},{8,12},{12,16},{16,20},{20,24},{24,28},{1,5},{5,9},{9,... | collective-permute-start | bytes 15368 | tf_op jit(solution)/shard_map/ppermute | solution.py:23
  19.6 0.1 copy.69
  19.7 1.0 %collective-permute-start.3 = (bf16[1,128,512]{2,1,0:T(8,128)(2,1)S(1)}, bf16[1,128,512]{2,1,0:T(8,128)(2,1)S(1)}, u32[]{:S(2)}, u32[]{:S(2)}) collective-permute-start(bf16[1,128,512]{2,1,0:T(8,128)(2,1)S(1)} %bitcast.82), channel_id=1, source_target_pairs={{0,16},{4,20},{8,24},{12,28},{16,0},{20,4},{24,8},{28,12},{1,17},{... | collective-permute-start | bytes 393224 | tf_op jit(solution)/shard_map/ppermute | solution.py:47
  20.7 1.6 %collective-permute-start.8 = (bf16[2,128,512]{2,1,0:T(8,128)(2,1)S(1)}, bf16[2,128,512]{2,1,0:T(8,128)(2,1)S(1)}, u32[]{:S(2)}, u32[]{:S(2)}) collective-permute-start(bf16[2,128,512]{2,1,0:T(8,128)(2,1)S(1)} %maximum_select_fusion.5), channel_id=1, source_target_pairs={{0,8},{4,12},{8,0},{12,4},{16,24},{20,28},{24,16},{28,20},{1,9},{5... | collective-permute-start | bytes 786440 | tf_op jit(solution)/shard_map/ppermute | solution.py:47
  22.3 0.1 pad_maximum_fusion.3
  22.4 0.1 copy.64
  22.6 0.1 copy.65
  22.7 0.1 copy.66
  22.9 6.8 %collective-permute-done.8 = bf16[2,128,512]{2,1,0:T(8,128)(2,1)S(1)} collective-permute-done((bf16[2,128,512]{2,1,0:T(8,128)(2,1)S(1)}, bf16[2,128,512]{2,1,0:T(8,128)(2,1)S(1)}, u32[]{:S(2)}, u32[]{:S(2)}) %collective-permute-start.8) | collective-permute-done | bytes 262176 | tf_op jit(solution)/shard_map/ppermute | solution.py:47
  29.7 0.2 collective-permute-start.9
  30.0 0.9 %collective-permute-start.4 = (bf16[2,128,512]{2,1,0:T(8,128)(2,1)S(1)}, bf16[2,128,512]{2,1,0:T(8,128)(2,1)S(1)}, u32[]{:S(2)}, u32[]{:S(2)}) collective-permute-start(bf16[2,128,512]{2,1,0:T(8,128)(2,1)S(1)} %maximum_select_fusion.4), channel_id=1, source_target_pairs={{0,8},{4,12},{8,0},{12,4},{16,24},{20,28},{24,16},{28,20},{1,9},{5... | collective-permute-start | bytes 786440 | tf_op jit(solution)/shard_map/ppermute | solution.py:47
  30.9 0.1 copy.67
  31.0 0.1 copy.68
  31.3 7.4 %collective-permute-done.4 = bf16[2,128,512]{2,1,0:T(8,128)(2,1)S(1)} collective-permute-done((bf16[2,128,512]{2,1,0:T(8,128)(2,1)S(1)}, bf16[2,128,512]{2,1,0:T(8,128)(2,1)S(1)}, u32[]{:S(2)}, u32[]{:S(2)}) %collective-permute-start.4) | collective-permute-done | bytes 262176 | tf_op jit(solution)/shard_map/ppermute | solution.py:47
  38.6 0.1 maximum_select_fusion.2
  38.8 0.2 maximum_select_fusion.1
  39.1 1.1 %concatenate.65.keys_ref = bf16[1152,512]{1,0:T(8,128)(2,1)} pad(bf16[1024,512]{1,0:T(8,128)(2,1)S(1)} %bitcast.74, bf16[]{:T(256)} %constant.106.clone.1), padding=128_0x0_0 | pad | bytes 2228226 | tf_op jit(solution)/shard_map/concatenate | solution.py:219
  40.2 0.1 fusion.24
  40.3 0.1 fusion.56
  40.4 0.1 slice.221
  40.5 0.1 slice.225
  40.6 0.1 slice.231
  40.7 0.1 slice.239
  40.8 0.1 slice.249
  40.9 0.3 copy-done.1
  41.2 0.8 %fusion.21 = (f32[133,4]{1,0:T(8,128)S(1)}, f32[133,4]{1,0:T(8,128)S(1)}, f32[133,4]{1,0:T(8,128)S(1)}, f32[133,4]{1,0:T(8,128)S(1)}, f32[133,4]{1,0:T(8,128)S(1)}) fusion(f32[133,4,128]{2,1,0:T(4,128)S(1)} %slice.249, bf16[128,4,128]{2,1,0:T(4,128)(2,1)S(1)} %copy-done.1, bf16[5,4,128]{2,1,0:T(4,128)(2,1)S(1)} %concatenate.66, ...), kind=kLoop, calls=%fused_computation.52 | loop fusion | flops 814492 | bytes 1508752 | tf_op jit(solution)/shard_map/reduce_sum | solution.py:148
  42.0 0.1 copy.71
  42.1 0.1 copy.74
  42.2 0.1 copy.72
  42.5 10.9 %shard_map.64 = f32[4,1024,128]{2,1,0:T(8,128)} custom-call(f32[264]{0:T(512)} %reshape.179.taps_ref, bf16[4,768,128]{2,1,0:T(8,128)(2,1)} %bitcast.81, bf16[1152,512]{1,0:T(8,128)(2,1)} %concatenate.65.keys_ref), custom_call_target="tpu_custom_call" | custom-call | tf_op jit(solution)/shard_map/pallas_call | solution.py:120
  53.4 0.7 subtract_bitcast_fusion.2
  54.1 0.1 subtract_bitcast_fusion.3
  54.3 0.1 fusion.44
  54.4 3.8 %divide_bitcast_fusion = f32[1,4,1024,128]{3,2,1,0:T(8,128)S(1)} fusion(f32[4,1024,128]{2,1,0:T(8,128)} %shard_map.64, f32[4,128]{1,0:T(4,128)} %get-tuple-element.56, f32[4,128]{1,0:T(4,128)S(1)} %get-tuple-element.55, f32[4,128]{1,0:T(4,128)S(1)} %get-tuple-element.54, f32[4,128]{1,0:T(4,128)S(1)} %subtract_bitcast_fusion.3, f32[4,128]{1,0:T(4,128)S(1)} %fusion.44, ...), kind=kOutput, calls=%fused_computation.5 | output fusion | flops 6818814 | bytes 4990976 | tf_op jit(solution)/shard_map/div | solution.py:176
  58.1 1.4 %slice_bitcast_fusion.3 = (f32[1024,128]{1,0:T(8,128)}, f32[1024,128]{1,0:T(8,128)}, f32[1024,128]{1,0:T(8,128)}, f32[1024,128]{1,0:T(8,128)}) fusion(f32[1,4,1024,128]{3,2,1,0:T(8,128)S(1)} %divide_bitcast_fusion), kind=kLoop, calls=%fused_computation.30 | loop fusion | bytes 4194304 | tf_op jit(solution)/shard_map/mul | solution.py:181
  59.5 0.2 maximum_select_fusion
  59.7 0.9 %copy.62 = bf16[2,2,2,128,512]{3,2,1,0,4:T(2,128)(2,1)S(1)} copy(bf16[2,2,2,128,512]{4,3,0,1,2:T(8,128)(2,1)S(1)} %bitcast.76) | data formatting | bytes 2097152 | tf_op jit(solution)/shard_map/transpose | solution.py:55
  60.7 0.8 %reshape_reshape.3 = bf16[1024,4,128]{0,2,1:T(8,128)(2,1)S(1)} reshape(bf16[2,2,2,128,512]{3,2,1,0,4:T(2,128)(2,1)S(1)} %copy.62) | data formatting | bytes 2097152 | tf_op jit(solution)/shard_map/reshape;reshape | solution.py:229
  61.5 0.2 copy-done.3
  61.7 2.1 %multiply_reduce_fusion = (f32[128,4]{0,1:T(4,128)S(1)}, f32[128,4,128]{0,2,1:T(8,128)S(1)}) fusion(bf16[1024,4,128]{0,2,1:T(8,128)(2,1)S(1)} %reshape_reshape.3, f32[1024,128]{1,0:T(8,128)S(1)} %copy-done.3, f32[4]{0:T(128)S(1)} %copy-done.25, f32[1024,128]{1,0:T(8,128)} %get-tuple-element.31, f32[4]{0:T(128)S(1)} %copy-done.26, ...), kind=kOutput, calls=%fused_computation.56 | convolution fusion | flops 138542592 | bytes 3409984 | tf_op jit(solution)/shard_map/hki,khd->ihd/dot_general | solution.py:183
  63.9 0.1 multiply_convert_fusion
  64.0 0.2 constant_dynamic-slice_fusion.3
  64.3 2.6 %collective-permute-start.10 = (bf16[32,512]{1,0:T(8,128)(2,1)S(1)}, bf16[32,512]{1,0:T(8,128)(2,1)S(1)}, u32[]{:S(2)}, u32[]{:S(2)}) collective-permute-start(bf16[32,512]{1,0:T(8,128)(2,1)S(1)} %copy.81), channel_id=1, source_target_pairs={{0,1},{1,2},{2,3},{3,0},{4,5},{5,6},{6,7},{7,4},{8,9},{9,10},{10,1... | collective-permute-start | bytes 98312 | tf_op jit(solution)/shard_map/ppermute | solution.py:33
  67.0 1.7 %collective-permute-start.11 = (bf16[32,512]{1,0:T(8,128)(2,1)S(1)}, bf16[32,512]{1,0:T(8,128)(2,1)S(1)}, u32[]{:S(2)}, u32[]{:S(2)}) collective-permute-start(bf16[32,512]{1,0:T(8,128)(2,1)S(1)} %copy.82), channel_id=1, source_target_pairs={{0,2},{1,3},{2,0},{3,1},{4,6},{5,7},{6,4},{7,5},{8,10},{9,11},{10,... | collective-permute-start | bytes 98312 | tf_op jit(solution)/shard_map/ppermute | solution.py:33
  68.8 0.8 %collective-permute-start.12 = (bf16[32,512]{1,0:T(8,128)(2,1)S(1)}, bf16[32,512]{1,0:T(8,128)(2,1)S(1)}, u32[]{:S(2)}, u32[]{:S(2)}) collective-permute-start(bf16[32,512]{1,0:T(8,128)(2,1)S(1)} %copy.83), channel_id=1, source_target_pairs={{0,3},{1,0},{2,1},{3,2},{4,7},{5,4},{6,5},{7,6},{8,11},{9,8},{10,9... | collective-permute-start | bytes 98312 | tf_op jit(solution)/shard_map/ppermute | solution.py:33
  69.7 0.4 collective-permute-done.10
  70.1 2.1 %collective-permute-done.11 = bf16[32,512]{1,0:T(8,128)(2,1)S(1)} collective-permute-done((bf16[32,512]{1,0:T(8,128)(2,1)S(1)}, bf16[32,512]{1,0:T(8,128)(2,1)S(1)}, u32[]{:S(2)}, u32[]{:S(2)}) %collective-permute-start.11) | collective-permute-done | bytes 32800 | tf_op jit(solution)/shard_map/ppermute | solution.py:33
  72.2 0.5 collective-permute-done.12
  72.8 0.7 gather_fusion.1
  73.5 0.7 copy.85
  (96 shorter events, 1.3 us)
Async XLA Ops:
  1.1 14.7 %copy-start.4 = (f32[4,4]{1,0:T(4,128)S(1)}, f32[4,4]{1,0:T(4,128)}, u32[]{:S(2)}) copy-start(f32[4,4]{1,0:T(4,128)} %param.10) | copy-start | bytes 196
  1.1 10.9 %collective-permute-start = (bf16[3,32,512]{2,1,0:T(8,128)(2,1)S(1)}, bf16[3,32,512]{2,1,0:T(8,128)(2,1)S(1)}, u32[]{:S(2)}, u32[]{:S(2)}) collective-permute-start(bf16[3,32,512]{2,1,0:T(8,128)(2,1)S(1)} %get-tuple-element.39), channel_id=1, source_target_pairs={{0,1},{1,2},{2,3},{3,0},{4,5},{5,6},{6,7},{7,4},{8,9},{9,10},{10,1... | collective-permute-start | bytes 294920 | tf_op jit(solution)/shard_map/ppermute | solution.py:33
  4.2 9.2 %collective-permute-start.1 = (bf16[3,32,512]{2,1,0:T(8,128)(2,1)S(1)}, bf16[3,32,512]{2,1,0:T(8,128)(2,1)S(1)}, u32[]{:S(2)}, u32[]{:S(2)}) collective-permute-start(bf16[3,32,512]{2,1,0:T(8,128)(2,1)S(1)} %get-tuple-element.38), channel_id=1, source_target_pairs={{0,2},{1,3},{2,0},{3,1},{4,6},{5,7},{6,4},{7,5},{8,10},{9,11},{10,... | collective-permute-start | bytes 294920 | tf_op jit(solution)/shard_map/ppermute | solution.py:33
  6.8 6.6 %collective-permute-start.2 = (bf16[3,32,512]{2,1,0:T(8,128)(2,1)S(1)}, bf16[3,32,512]{2,1,0:T(8,128)(2,1)S(1)}, u32[]{:S(2)}, u32[]{:S(2)}) collective-permute-start(bf16[3,32,512]{2,1,0:T(8,128)(2,1)S(1)} %get-tuple-element.37), channel_id=1, source_target_pairs={{0,3},{1,0},{2,1},{3,2},{4,7},{5,4},{6,5},{7,6},{8,11},{9,8},{10,9... | collective-permute-start | bytes 294920 | tf_op jit(solution)/shard_map/ppermute | solution.py:33
  10.8 7.2 %copy-start.11 = (s32[1024]{0:T(1024)}, s32[1024]{0:T(1024)S(1)}, u32[]{:S(2)}) copy-start(s32[1024]{0:T(1024)S(1)} %pad_clamp_fusion) | copy-start | bytes 12292
  12.0 8.7 %copy-start.22 = (pred[4]{0:T(512)(128)(4,1)}, pred[4]{0:T(512)(128)(4,1)S(1)}, u32[]{:S(2)}) copy-start(pred[4]{0:T(512)(128)(4,1)S(1)} %compare_and_fusion) | copy-start | bytes 16
  14.2 6.5 %collective-permute-start.7 = (bf16[1,128,512]{2,1,0:T(8,128)(2,1)S(1)}, bf16[1,128,512]{2,1,0:T(8,128)(2,1)S(1)}, u32[]{:S(2)}, u32[]{:S(2)}) collective-permute-start(bf16[1,128,512]{2,1,0:T(8,128)(2,1)S(1)} %bitcast.84), channel_id=1, source_target_pairs={{0,16},{4,20},{8,24},{12,28},{16,0},{20,4},{24,8},{28,12},{1,17},{... | collective-permute-start | bytes 393224 | tf_op jit(solution)/shard_map/ppermute | solution.py:47
  18.0 4.3 %collective-permute-start.6 = (bf16[5,512]{1,0:T(8,128)(2,1)S(1)}, bf16[5,512]{1,0:T(8,128)(2,1)S(1)}, u32[]{:S(2)}, u32[]{:S(2)}) collective-permute-start(bf16[5,512]{1,0:T(8,128)(2,1)S(1)} %slice.270), channel_id=1, source_target_pairs={{0,4},{4,8},{8,12},{12,16},{16,20},{20,24},{24,28},{1,5},{5,9},{9,... | collective-permute-start | bytes 15368 | tf_op jit(solution)/shard_map/ppermute | solution.py:23
  19.7 10.3 %collective-permute-start.3 = (bf16[1,128,512]{2,1,0:T(8,128)(2,1)S(1)}, bf16[1,128,512]{2,1,0:T(8,128)(2,1)S(1)}, u32[]{:S(2)}, u32[]{:S(2)}) collective-permute-start(bf16[1,128,512]{2,1,0:T(8,128)(2,1)S(1)} %bitcast.82), channel_id=1, source_target_pairs={{0,16},{4,20},{8,24},{12,28},{16,0},{20,4},{24,8},{28,12},{1,17},{... | collective-permute-start | bytes 393224 | tf_op jit(solution)/shard_map/ppermute | solution.py:47
  20.7 8.9 %collective-permute-start.8 = (bf16[2,128,512]{2,1,0:T(8,128)(2,1)S(1)}, bf16[2,128,512]{2,1,0:T(8,128)(2,1)S(1)}, u32[]{:S(2)}, u32[]{:S(2)}) collective-permute-start(bf16[2,128,512]{2,1,0:T(8,128)(2,1)S(1)} %maximum_select_fusion.5), channel_id=1, source_target_pairs={{0,8},{4,12},{8,0},{12,4},{16,24},{20,28},{24,16},{28,20},{1,9},{5... | collective-permute-start | bytes 786440 | tf_op jit(solution)/shard_map/ppermute | solution.py:47
  29.7 9.1 %collective-permute-start.9 = (bf16[4,128,512]{2,1,0:T(8,128)(2,1)S(1)}, bf16[4,128,512]{2,1,0:T(8,128)(2,1)S(1)}, u32[]{:S(2)}, u32[]{:S(2)}) collective-permute-start(bf16[4,128,512]{2,1,0:T(8,128)(2,1)S(1)} %maximum_select_fusion.3), channel_id=1, source_target_pairs={{0,4},{4,0},{8,12},{12,8},{16,20},{20,16},{24,28},{28,24},{1,5},{5... | collective-permute-start | bytes 1572872 | tf_op jit(solution)/shard_map/ppermute | solution.py:47
  30.0 8.6 %collective-permute-start.4 = (bf16[2,128,512]{2,1,0:T(8,128)(2,1)S(1)}, bf16[2,128,512]{2,1,0:T(8,128)(2,1)S(1)}, u32[]{:S(2)}, u32[]{:S(2)}) collective-permute-start(bf16[2,128,512]{2,1,0:T(8,128)(2,1)S(1)} %maximum_select_fusion.4), channel_id=1, source_target_pairs={{0,8},{4,12},{8,0},{12,4},{16,24},{20,28},{24,16},{28,20},{1,9},{5... | collective-permute-start | bytes 786440 | tf_op jit(solution)/shard_map/ppermute | solution.py:47
  31.2 7.8 %copy-start = (bf16[128,4,6,128]{0,3,2,1:T(8,128)(2,1)}, bf16[128,4,6,128]{0,3,2,1:T(8,128)(2,1)S(1)}, u32[]{:S(2)}) copy-start(bf16[128,4,6,128]{0,3,2,1:T(8,128)(2,1)S(1)} %constant_dynamic-update-slice_fusion) | copy-start | bytes 2359300
  38.7 20.8 %collective-permute-start.5 = (bf16[4,128,512]{2,1,0:T(8,128)(2,1)S(1)}, bf16[4,128,512]{2,1,0:T(8,128)(2,1)S(1)}, u32[]{:S(2)}, u32[]{:S(2)}) collective-permute-start(bf16[4,128,512]{2,1,0:T(8,128)(2,1)S(1)} %maximum_select_fusion.2), channel_id=1, source_target_pairs={{0,4},{4,0},{8,12},{12,8},{16,20},{20,16},{24,28},{28,24},{1,5},{5... | collective-permute-start | bytes 1572872 | tf_op jit(solution)/shard_map/ppermute | solution.py:47
  40.3 0.9 %copy-start.1 = (bf16[128,4,128]{2,1,0:T(4,128)(2,1)S(1)}, bf16[128,4,128]{2,1,0:T(4,128)(2,1)}, u32[]{:S(2)}) copy-start(bf16[128,4,128]{2,1,0:T(4,128)(2,1)} %concatenate.67) | copy-start | bytes 393220
  42.3 11.1 %copy-start.5 = (f32[4]{0:T(128)S(1)}, f32[4]{0:T(128)}, u32[]{:S(2)}) copy-start(f32[4]{0:T(128)} %get-tuple-element.11) | copy-start | bytes 52
  42.3 11.1 %copy-start.6 = (f32[4]{0:T(128)S(1)}, f32[4]{0:T(128)}, u32[]{:S(2)}) copy-start(f32[4]{0:T(128)} %get-tuple-element.12) | copy-start | bytes 52
  42.3 11.1 %copy-start.7 = (f32[4]{0:T(128)S(1)}, f32[4]{0:T(128)}, u32[]{:S(2)}) copy-start(f32[4]{0:T(128)} %get-tuple-element.13) | copy-start | bytes 52
  42.3 11.1 %copy-start.8 = (f32[4]{0:T(128)S(1)}, f32[4]{0:T(128)}, u32[]{:S(2)}) copy-start(f32[4]{0:T(128)} %get-tuple-element.16) | copy-start | bytes 52
  42.3 11.1 %copy-start.9 = (f32[4]{0:T(128)S(1)}, f32[4]{0:T(128)}, u32[]{:S(2)}) copy-start(f32[4]{0:T(128)} %get-tuple-element.17) | copy-start | bytes 52
  42.3 11.1 %copy-start.10 = (f32[4]{0:T(128)S(1)}, f32[4]{0:T(128)}, u32[]{:S(2)}) copy-start(f32[4]{0:T(128)} %get-tuple-element.20) | copy-start | bytes 52
  42.4 11.7 %copy-start.12 = (f32[4]{0:T(128)S(1)}, f32[4]{0:T(128)}, u32[]{:S(2)}) copy-start(f32[4]{0:T(128)} %get-tuple-element.15) | copy-start | bytes 52
  42.4 11.7 %copy-start.13 = (f32[4]{0:T(128)S(1)}, f32[4]{0:T(128)}, u32[]{:S(2)}) copy-start(f32[4]{0:T(128)} %get-tuple-element.19) | copy-start | bytes 52
  42.4 11.7 %copy-start.14 = (f32[4]{0:T(128)S(1)}, f32[4]{0:T(128)}, u32[]{:S(2)}) copy-start(f32[4]{0:T(128)} %get-tuple-element.22) | copy-start | bytes 52
  42.4 11.7 %copy-start.15 = (f32[4]{0:T(128)S(1)}, f32[4]{0:T(128)}, u32[]{:S(2)}) copy-start(f32[4]{0:T(128)} %get-tuple-element.24) | copy-start | bytes 52
  42.5 11.7 %copy-start.17 = (f32[4]{0:T(128)S(1)}, f32[4]{0:T(128)}, u32[]{:S(2)}) copy-start(f32[4]{0:T(128)} %get-tuple-element.10) | copy-start | bytes 52
  42.5 11.7 %copy-start.18 = (f32[4]{0:T(128)S(1)}, f32[4]{0:T(128)}, u32[]{:S(2)}) copy-start(f32[4]{0:T(128)} %get-tuple-element.14) | copy-start | bytes 52
  42.5 11.8 %copy-start.19 = (f32[4]{0:T(128)S(1)}, f32[4]{0:T(128)}, u32[]{:S(2)}) copy-start(f32[4]{0:T(128)} %get-tuple-element.18) | copy-start | bytes 52
  42.5 11.8 %copy-start.20 = (f32[4]{0:T(128)S(1)}, f32[4]{0:T(128)}, u32[]{:S(2)}) copy-start(f32[4]{0:T(128)} %get-tuple-element.21) | copy-start | bytes 52
  42.5 11.8 %copy-start.21 = (f32[4]{0:T(128)S(1)}, f32[4]{0:T(128)}, u32[]{:S(2)}) copy-start(f32[4]{0:T(128)} %get-tuple-element.23) | copy-start | bytes 52
  59.7 1.8 %copy-start.2 = (f32[1024,128]{1,0:T(8,128)S(1)}, f32[1024,128]{1,0:T(8,128)}, u32[]{:S(2)}) copy-start(f32[1024,128]{1,0:T(8,128)} %get-tuple-element.29) | copy-start | bytes 1572868
  59.7 1.8 %copy-start.24 = (f32[4]{0:T(128)S(1)}, f32[4]{0:T(128)}, u32[]{:S(2)}) copy-start(f32[4]{0:T(128)} %get-tuple-element.25) | copy-start | bytes 52
  59.7 1.8 %copy-start.25 = (f32[4]{0:T(128)S(1)}, f32[4]{0:T(128)}, u32[]{:S(2)}) copy-start(f32[4]{0:T(128)} %get-tuple-element.26) | copy-start | bytes 52
  59.7 1.8 %copy-start.26 = (f32[4]{0:T(128)S(1)}, f32[4]{0:T(128)}, u32[]{:S(2)}) copy-start(f32[4]{0:T(128)} %get-tuple-element.27) | copy-start | bytes 52
  59.7 1.8 %copy-start.27 = (f32[4]{0:T(128)S(1)}, f32[4]{0:T(128)}, u32[]{:S(2)}) copy-start(f32[4]{0:T(128)} %get-tuple-element.28) | copy-start | bytes 52
  60.7 1.1 %copy-start.3 = (f32[1024,128]{1,0:T(8,128)S(1)}, f32[1024,128]{1,0:T(8,128)}, u32[]{:S(2)}) copy-start(f32[1024,128]{1,0:T(8,128)} %get-tuple-element.30) | copy-start | bytes 1572868
  61.7 2.2 %copy-start.16 = (f32[512]{0:T(512)S(1)}, f32[512]{0:T(512)}, u32[]{:S(2)}) copy-start(f32[512]{0:T(512)} %param.11) | copy-start | bytes 6148
  63.8 9.6 %copy-start.23 = (pred[4]{0:T(512)(128)(4,1)S(1)}, pred[4]{0:T(512)(128)(4,1)}, u32[]{:S(2)}) copy-start(pred[4]{0:T(512)(128)(4,1)} %copy-done.22) | copy-start | bytes 16
  64.3 5.8 %collective-permute-start.10 = (bf16[32,512]{1,0:T(8,128)(2,1)S(1)}, bf16[32,512]{1,0:T(8,128)(2,1)S(1)}, u32[]{:S(2)}, u32[]{:S(2)}) collective-permute-start(bf16[32,512]{1,0:T(8,128)(2,1)S(1)} %copy.81), channel_id=1, source_target_pairs={{0,1},{1,2},{2,3},{3,0},{4,5},{5,6},{6,7},{7,4},{8,9},{9,10},{10,1... | collective-permute-start | bytes 98312 | tf_op jit(solution)/shard_map/ppermute | solution.py:33
  67.0 5.2 %collective-permute-start.11 = (bf16[32,512]{1,0:T(8,128)(2,1)S(1)}, bf16[32,512]{1,0:T(8,128)(2,1)S(1)}, u32[]{:S(2)}, u32[]{:S(2)}) collective-permute-start(bf16[32,512]{1,0:T(8,128)(2,1)S(1)} %copy.82), channel_id=1, source_target_pairs={{0,2},{1,3},{2,0},{3,1},{4,6},{5,7},{6,4},{7,5},{8,10},{9,11},{10,... | collective-permute-start | bytes 98312 | tf_op jit(solution)/shard_map/ppermute | solution.py:33
  68.8 4.0 %collective-permute-start.12 = (bf16[32,512]{1,0:T(8,128)(2,1)S(1)}, bf16[32,512]{1,0:T(8,128)(2,1)S(1)}, u32[]{:S(2)}, u32[]{:S(2)}) collective-permute-start(bf16[32,512]{1,0:T(8,128)(2,1)S(1)} %copy.83), channel_id=1, source_target_pairs={{0,3},{1,0},{2,1},{3,2},{4,7},{5,4},{6,5},{7,6},{8,11},{9,8},{10,9... | collective-permute-start | bytes 98312 | tf_op jit(solution)/shard_map/ppermute | solution.py:33

commit v9 on v8

--- a/solution.py
+++ b/solution.py
@@ -214,6 +214,7 @@
     earlier = passed_along(query_local[shard_rows - row_lead :], "ctx", 1)
     query_ext = jnp.concatenate([earlier, query_local], axis=0)
     key_all = gathered(key_local, "ctx").reshape((-1, width))
+    key_all, value_local = lax.optimization_barrier((key_all, value_local))
     value_all = gathered(value_local, "ctx").reshape((-1, width))
     seq_len = key_all.shape[0]
     key_pad = jnp.concatenate(

time: 74.6 us -> 72.4 us (0.971)
  waiting for transfers between devices: 18.7 us -> 16.3 us
  starting transfers between devices: 18.9 us -> 21 us
  other arithmetic: 9.53 us -> 8.36 us
    ppermute x6, waiting for transfers between devices: 14.2 us -> 9.5 us  [gathered(): incoming = lax.ppermute(held, axis, [(i, i ^ bit) for i in range(peers)])]
    ppermute x6, waiting for transfers between devices: 4.52 us -> 6.75 us  [exchanged(): received.append(lax.ppermute(outgoing, axis, pairs))]
    ppermute x6, starting transfers between devices: 5.33 us -> 7.42 us  [gathered(): incoming = lax.ppermute(held, axis, [(i, i ^ bit) for i in range(peers)])]
    slice x1, local copies, waits for them, and re-layouts: 1.89 us -> 0.96 us  [band_terms(): score_kernel[None, :, row_lag, col_lag]]
  transfers between devices with their start and end apart: 13 -> 13, of which waited for: 6 -> 9; matrix products, arithmetic and copies ran while one was open for 22% -> 17% of each run, Pallas kernels for 15% -> 15%
where the time goes in v9:
time: 72.4 us; the launch traced here: 72.1 us
  starting transfers between devices  21 us (29%)
  waiting for transfers between devices  16.3 us (23%)
  local copies, waits for them, and re-layouts  12.9 us (18%)
  Pallas kernels  10.9 us (15%)
  other arithmetic  8.36 us (12%)
  matrix products  2.13 us (3%)
    ppermute x6, starting transfers between devices, exchanged(): received.append(lax.ppermute(outgoing, axis, pairs))  12.2 us
    pallas_call x1, Pallas kernels, conv_logits(): pl.pallas_call(logits_kernel, grid=(heads, seq_len // span), in_specs=[pl...  10.9 us
    ppermute x6, waiting for transfers between devices, gathered(): incoming = lax.ppermute(held, axis, [(i, i ^ bit) for i in range(peers)])  9.5 us
    ppermute x6, starting transfers between devices, gathered(): incoming = lax.ppermute(held, axis, [(i, i ^ bit) for i in range(peers)])  7.42 us
    ppermute x6, waiting for transfers between devices, exchanged(): received.append(lax.ppermute(outgoing, axis, pairs))  6.75 us
    div x1, other arithmetic, attend_chunk(): probabilities = expd / jnp.sum(expd, axis=1, keepdims=True)  3.81 us
    dot_general x1, matrix products, attend_chunk(): jnp.einsum('hki,khd->ihd', mixed_probs, value_heads, preferred_element_ty...  2.13 us
  transfers between devices with their start and end apart: 13, of which 9 were waited for; matrix products, arithmetic and copies ran while one was open for 17% of the time, Pallas kernels for 15%

profile of v9, /device:TPU:0, one launch (start us, length us, event | category | flops | bytes accessed | tf_op | source)
XLA Modules:
  0.0 72.1 jit_solution(12071961588703042501)
XLA Ops:
  0.0 1.1 %pad_maximum_fusion = bf16[3,32,2048]{2,1,0:T(8,128)(2,1)S(1)} fusion(bf16[1,32,2048]{2,1,0:T(8,128)(2,1)} %bitcast.92, bf16[1,32,2048]{2,1,0:T(8,128)(2,1)} %bitcast.93, bf16[1,32,2048]{2,1,0:T(8,128)(2,1)} %bitcast.94), kind=kLoop, calls=%fused_computation.40 | loop fusion | flops 393216 | bytes 786432 | tf_op jit(solution)/shard_map/stack | solution.py:197
  1.1 3.1 %collective-permute-start = (bf16[3,32,512]{2,1,0:T(8,128)(2,1)S(1)}, bf16[3,32,512]{2,1,0:T(8,128)(2,1)S(1)}, u32[]{:S(2)}, u32[]{:S(2)}) collective-permute-start(bf16[3,32,512]{2,1,0:T(8,128)(2,1)S(1)} %get-tuple-element.43), channel_id=1, source_target_pairs={{0,1},{1,2},{2,3},{3,0},{4,5},{5,6},{6,7},{7,4},{8,9},{9,10},{10,1... | collective-permute-start | bytes 294920 | tf_op jit(solution)/shard_map/ppermute | solution.py:33
  4.2 2.6 %collective-permute-start.1 = (bf16[3,32,512]{2,1,0:T(8,128)(2,1)S(1)}, bf16[3,32,512]{2,1,0:T(8,128)(2,1)S(1)}, u32[]{:S(2)}, u32[]{:S(2)}) collective-permute-start(bf16[3,32,512]{2,1,0:T(8,128)(2,1)S(1)} %get-tuple-element.42), channel_id=1, source_target_pairs={{0,2},{1,3},{2,0},{3,1},{4,6},{5,7},{6,4},{7,5},{8,10},{9,11},{10,... | collective-permute-start | bytes 294920 | tf_op jit(solution)/shard_map/ppermute | solution.py:33
  6.8 1.3 %collective-permute-start.2 = (bf16[3,32,512]{2,1,0:T(8,128)(2,1)S(1)}, bf16[3,32,512]{2,1,0:T(8,128)(2,1)S(1)}, u32[]{:S(2)}, u32[]{:S(2)}) collective-permute-start(bf16[3,32,512]{2,1,0:T(8,128)(2,1)S(1)} %get-tuple-element.41), channel_id=1, source_target_pairs={{0,3},{1,0},{2,1},{3,2},{4,7},{5,4},{6,5},{7,6},{8,11},{9,8},{10,9... | collective-permute-start | bytes 294920 | tf_op jit(solution)/shard_map/ppermute | solution.py:33
  8.2 1.2 %fusion.15 = (pred[1024,128]{1,0:T(8,128)(4,1)S(1)}, pred[1024,128]{1,0:T(8,128)(4,1)S(1)}, pred[1024,128]{1,0:T(8,128)(4,1)}, pred[1024,128]{1,0:T(8,128)(4,1)}...) fusion(s32[128]{0:T(128)S(1)} %iota_add_fusion), kind=kLoop, calls=%fused_computation.39 | loop fusion | flops 917504 | bytes 786944 | tf_op jit(solution)/shard_map/ge | solution.py:173
  9.4 0.4 collective-permute-done
  9.9 3.5 %collective-permute-done.1 = bf16[3,32,512]{2,1,0:T(8,128)(2,1)S(1)} collective-permute-done((bf16[3,32,512]{2,1,0:T(8,128)(2,1)S(1)}, bf16[3,32,512]{2,1,0:T(8,128)(2,1)S(1)}, u32[]{:S(2)}, u32[]{:S(2)}) %collective-permute-start.1) | collective-permute-done | bytes 98336 | tf_op jit(solution)/shard_map/ppermute | solution.py:33
  13.5 0.6 gather_fusion
  14.1 0.1 select_bitcast_fusion
  14.2 0.7 fusion.55
  14.9 1.5 %collective-permute-start.3 = (bf16[1,128,512]{2,1,0:T(8,128)(2,1)S(1)}, bf16[1,128,512]{2,1,0:T(8,128)(2,1)S(1)}, u32[]{:S(2)}, u32[]{:S(2)}) collective-permute-start(bf16[1,128,512]{2,1,0:T(8,128)(2,1)S(1)} %bitcast.85), channel_id=1, source_target_pairs={{0,16},{4,20},{8,24},{12,28},{16,0},{20,4},{24,8},{28,12},{1,17},{... | collective-permute-start | bytes 393224 | tf_op jit(solution)/shard_map/ppermute | solution.py:47
  16.4 1.0 %slice_reduce_fusion.17 = (f32[4]{0:T(128)}, f32[4]{0:T(128)S(1)}, f32[4]{0:T(128)S(1)}, f32[4]{0:T(128)S(1)}, f32[4]{0:T(128)}, /*index=5*/f32[4]{0:T(128)S(1)}...) fusion(f32[4,6,11]{2,0,1:T(4,128)S(1)} %copy-done.5), kind=kLoop, calls=%fused_computation.135 | loop fusion | bytes 480 | tf_op jit(solution)/shard_map/slice | solution.py:157
  17.3 2.8 %collective-permute-done.3 = bf16[1,128,512]{2,1,0:T(8,128)(2,1)S(1)} collective-permute-done((bf16[1,128,512]{2,1,0:T(8,128)(2,1)S(1)}, bf16[1,128,512]{2,1,0:T(8,128)(2,1)S(1)}, u32[]{:S(2)}, u32[]{:S(2)}) %collective-permute-start.3) | collective-permute-done | bytes 131104 | tf_op jit(solution)/shard_map/ppermute | solution.py:47
  20.2 1.6 %collective-permute-start.4 = (bf16[2,128,512]{2,1,0:T(8,128)(2,1)S(1)}, bf16[2,128,512]{2,1,0:T(8,128)(2,1)S(1)}, u32[]{:S(2)}, u32[]{:S(2)}) collective-permute-start(bf16[2,128,512]{2,1,0:T(8,128)(2,1)S(1)} %maximum_select_fusion.4), channel_id=1, source_target_pairs={{0,8},{4,12},{8,0},{12,4},{16,24},{20,28},{24,16},{28,20},{1,9},{5... | collective-permute-start | bytes 786440 | tf_op jit(solution)/shard_map/ppermute | solution.py:47
  21.7 0.8 %slice_reduce_fusion.18 = (f32[4]{0:T(128)}, f32[4]{0:T(128)}, f32[4]{0:T(128)}, f32[4]{0:T(128)}) fusion(f32[1,4,4]{2,1,0:T(4,128)S(1)} %bitcast.99), kind=kLoop, calls=%fused_computation.136 | loop fusion | bytes 128 | tf_op jit(solution)/shard_map/slice | solution.py:181
  22.5 0.7 reshape.181.taps_ref
  23.3 1.3 %collective-permute-start.9 = (bf16[5,512]{1,0:T(8,128)(2,1)S(1)}, bf16[5,512]{1,0:T(8,128)(2,1)S(1)}, u32[]{:S(2)}, u32[]{:S(2)}) collective-permute-start(bf16[5,512]{1,0:T(8,128)(2,1)S(1)} %slice.270), channel_id=1, source_target_pairs={{0,4},{4,8},{8,12},{12,16},{16,20},{20,24},{24,28},{1,5},{5,9},{9,... | collective-permute-start | bytes 15368 | tf_op jit(solution)/shard_map/ppermute | solution.py:23
  24.6 0.1 copy.70
  24.7 0.7 concatenate.67
  25.4 0.1 pad_maximum_fusion.3
  25.6 0.1 copy.65
  25.7 0.1 copy.66
  25.8 0.1 copy.67
  25.9 0.1 copy.68
  26.1 0.1 copy.69
  26.2 1.3 %collective-permute-done.4 = bf16[2,128,512]{2,1,0:T(8,128)(2,1)S(1)} collective-permute-done((bf16[2,128,512]{2,1,0:T(8,128)(2,1)S(1)}, bf16[2,128,512]{2,1,0:T(8,128)(2,1)S(1)}, u32[]{:S(2)}, u32[]{:S(2)}) %collective-permute-start.4) | collective-permute-done | bytes 262176 | tf_op jit(solution)/shard_map/ppermute | solution.py:47
  27.5 0.1 collective-permute-start.5
  27.8 1.7 %collective-permute-done.5 = bf16[4,128,512]{2,1,0:T(8,128)(2,1)S(1)} collective-permute-done((bf16[4,128,512]{2,1,0:T(8,128)(2,1)S(1)}, bf16[4,128,512]{2,1,0:T(8,128)(2,1)S(1)}, u32[]{:S(2)}, u32[]{:S(2)}) %collective-permute-start.5) | collective-permute-done | bytes 524320 | tf_op jit(solution)/shard_map/ppermute | solution.py:47
  29.5 0.2 maximum_select_fusion
  29.7 0.1 copy.62
  29.8 0.1 fusion.24
  29.9 0.1 fusion.56
  30.0 0.1 slice.221
  30.2 0.1 slice.225
  30.3 0.1 slice.231
  30.4 0.1 slice.239
  30.5 0.1 slice.249
  30.6 0.2 copy-done.2
  30.8 0.8 %fusion.21 = (f32[133,4]{1,0:T(8,128)S(1)}, f32[133,4]{1,0:T(8,128)S(1)}, f32[133,4]{1,0:T(8,128)S(1)}, f32[133,4]{1,0:T(8,128)S(1)}, f32[133,4]{1,0:T(8,128)S(1)}) fusion(f32[133,4,128]{2,1,0:T(4,128)S(1)} %slice.249, bf16[128,4,128]{2,1,0:T(4,128)(2,1)S(1)} %copy-done.2, bf16[5,4,128]{2,1,0:T(4,128)(2,1)S(1)} %concatenate.66, ...), kind=kLoop, calls=%fused_computation.52 | loop fusion | flops 814492 | bytes 1508752 | tf_op jit(solution)/shard_map/reduce_sum | solution.py:148
  31.7 0.1 copy.74
  31.8 0.1 copy.72
  32.0 4.0 %collective-permute-start.6 = (bf16[1,128,512]{2,1,0:T(8,128)(2,1)S(1)}, bf16[1,128,512]{2,1,0:T(8,128)(2,1)S(1)}, u32[]{:S(2)}, u32[]{:S(2)}) collective-permute-start(bf16[1,128,512]{2,1,0:T(8,128)(2,1)S(1)} %bitcast.83), channel_id=1, source_target_pairs={{0,16},{4,20},{8,24},{12,28},{16,0},{20,4},{24,8},{28,12},{1,17},{... | collective-permute-start | bytes 393224 | tf_op jit(solution)/shard_map/ppermute | solution.py:47
  36.1 3.7 %collective-permute-done.6 = bf16[1,128,512]{2,1,0:T(8,128)(2,1)S(1)} collective-permute-done((bf16[1,128,512]{2,1,0:T(8,128)(2,1)S(1)}, bf16[1,128,512]{2,1,0:T(8,128)(2,1)S(1)}, u32[]{:S(2)}, u32[]{:S(2)}) %collective-permute-start.6) | collective-permute-done | bytes 131104 | tf_op jit(solution)/shard_map/ppermute | solution.py:47
  39.8 0.1 collective-permute-start.7
  40.1 1.1 %concatenate.65.keys_ref = bf16[1152,512]{1,0:T(8,128)(2,1)} pad(bf16[1024,512]{1,0:T(8,128)(2,1)S(1)} %bitcast.76, bf16[]{:T(256)} %constant.106.clone.1), padding=128_0x0_0 | pad | bytes 2228226 | tf_op jit(solution)/shard_map/concatenate | solution.py:220
  41.3 10.9 %shard_map.64 = f32[4,1024,128]{2,1,0:T(8,128)} custom-call(f32[264]{0:T(512)} %reshape.181.taps_ref, bf16[4,768,128]{2,1,0:T(8,128)(2,1)} %bitcast.82, bf16[1152,512]{1,0:T(8,128)(2,1)} %concatenate.65.keys_ref), custom_call_target="tpu_custom_call" | custom-call | tf_op jit(solution)/shard_map/pallas_call | solution.py:120
  52.2 0.1 fusion.44
  52.5 3.8 %divide_bitcast_fusion = f32[1,4,1024,128]{3,2,1,0:T(8,128)S(1)} fusion(f32[4,1024,128]{2,1,0:T(8,128)} %shard_map.64, f32[4,128]{1,0:T(4,128)S(1)} %get-tuple-element.60, f32[4,128]{1,0:T(4,128)S(1)} %get-tuple-element.59, f32[4,128]{1,0:T(4,128)S(1)} %get-tuple-element.58, f32[4,128]{1,0:T(4,128)S(1)} %subtract_bitcast_fusion.3, f32[4,128]{1,0:T(4,128)S(1)} %fusion.44, ...), kind=kOutput, calls=%fused_computation.5 | output fusion | flops 6818814 | bytes 4990976 | tf_op jit(solution)/shard_map/div | solution.py:176
  56.3 1.4 %slice_bitcast_fusion.3 = (f32[1024,128]{1,0:T(8,128)}, f32[1024,128]{1,0:T(8,128)}, f32[1024,128]{1,0:T(8,128)}, f32[1024,128]{1,0:T(8,128)}) fusion(f32[1,4,1024,128]{3,2,1,0:T(8,128)S(1)} %divide_bitcast_fusion), kind=kLoop, calls=%fused_computation.30 | loop fusion | bytes 4194304 | tf_op jit(solution)/shard_map/mul | solution.py:181
  57.7 0.2 maximum_select_fusion.1
  57.9 0.9 %copy.63 = bf16[2,2,2,128,512]{3,2,1,0,4:T(2,128)(2,1)S(1)} copy(bf16[2,2,2,128,512]{4,3,0,1,2:T(8,128)(2,1)S(1)} %bitcast.77) | data formatting | bytes 2097152 | tf_op jit(solution)/shard_map/transpose | solution.py:55
  58.8 0.8 %reshape_reshape.3 = bf16[1024,4,128]{0,2,1:T(8,128)(2,1)S(1)} reshape(bf16[2,2,2,128,512]{3,2,1,0,4:T(2,128)(2,1)S(1)} %copy.63) | data formatting | bytes 2097152 | tf_op jit(solution)/shard_map/reshape;reshape | solution.py:230
  59.7 0.2 copy-done.4
  59.9 2.1 %multiply_reduce_fusion = (f32[128,4]{0,1:T(4,128)S(1)}, f32[128,4,128]{0,2,1:T(8,128)S(1)}) fusion(bf16[1024,4,128]{0,2,1:T(8,128)(2,1)S(1)} %reshape_reshape.3, f32[1024,128]{1,0:T(8,128)S(1)} %copy-done.4, f32[4]{0:T(128)S(1)} %copy-done.19, f32[1024,128]{1,0:T(8,128)} %get-tuple-element.35, f32[4]{0:T(128)S(1)} %copy-done.20, ...), kind=kOutput, calls=%fused_computation.56 | convolution fusion | flops 138542592 | bytes 3409984 | tf_op jit(solution)/shard_map/hki,khd->ihd/dot_general | solution.py:183
  62.0 0.1 multiply_convert_fusion
  62.2 0.2 constant_dynamic-slice_fusion.3
  62.5 2.7 %collective-permute-start.10 = (bf16[32,512]{1,0:T(8,128)(2,1)S(1)}, bf16[32,512]{1,0:T(8,128)(2,1)S(1)}, u32[]{:S(2)}, u32[]{:S(2)}) collective-permute-start(bf16[32,512]{1,0:T(8,128)(2,1)S(1)} %copy.81), channel_id=1, source_target_pairs={{0,1},{1,2},{2,3},{3,0},{4,5},{5,6},{6,7},{7,4},{8,9},{9,10},{10,1... | collective-permute-start | bytes 98312 | tf_op jit(solution)/shard_map/ppermute | solution.py:33
  65.3 1.2 %collective-permute-start.11 = (bf16[32,512]{1,0:T(8,128)(2,1)S(1)}, bf16[32,512]{1,0:T(8,128)(2,1)S(1)}, u32[]{:S(2)}, u32[]{:S(2)}) collective-permute-start(bf16[32,512]{1,0:T(8,128)(2,1)S(1)} %copy.82), channel_id=1, source_target_pairs={{0,2},{1,3},{2,0},{3,1},{4,6},{5,7},{6,4},{7,5},{8,10},{9,11},{10,... | collective-permute-start | bytes 98312 | tf_op jit(solution)/shard_map/ppermute | solution.py:33
  66.6 1.3 %collective-permute-start.12 = (bf16[32,512]{1,0:T(8,128)(2,1)S(1)}, bf16[32,512]{1,0:T(8,128)(2,1)S(1)}, u32[]{:S(2)}, u32[]{:S(2)}) collective-permute-start(bf16[32,512]{1,0:T(8,128)(2,1)S(1)} %copy.83), channel_id=1, source_target_pairs={{0,3},{1,0},{2,1},{3,2},{4,7},{5,4},{6,5},{7,6},{8,11},{9,8},{10,9... | collective-permute-start | bytes 98312 | tf_op jit(solution)/shard_map/ppermute | solution.py:33
  68.0 0.3 collective-permute-done.10
  68.2 2.3 %collective-permute-done.11 = bf16[32,512]{1,0:T(8,128)(2,1)S(1)} collective-permute-done((bf16[32,512]{1,0:T(8,128)(2,1)S(1)}, bf16[32,512]{1,0:T(8,128)(2,1)S(1)}, u32[]{:S(2)}, u32[]{:S(2)}) %collective-permute-start.11) | collective-permute-done | bytes 32800 | tf_op jit(solution)/shard_map/ppermute | solution.py:33
  70.5 0.2 collective-permute-done.12
  70.8 0.6 gather_fusion.1
  71.4 0.7 copy.85
  (84 shorter events, 1.6 us)
Async XLA Ops:
  1.1 15.3 %copy-start.5 = (f32[4,6,11]{2,0,1:T(4,128)S(1)}, f32[4,6,11]{2,0,1:T(4,128)}, u32[]{:S(2)}) copy-start(f32[4,6,11]{2,0,1:T(4,128)} %param.9) | copy-start | bytes 3172
  1.1 8.8 %collective-permute-start = (bf16[3,32,512]{2,1,0:T(8,128)(2,1)S(1)}, bf16[3,32,512]{2,1,0:T(8,128)(2,1)S(1)}, u32[]{:S(2)}, u32[]{:S(2)}) collective-permute-start(bf16[3,32,512]{2,1,0:T(8,128)(2,1)S(1)} %get-tuple-element.43), channel_id=1, source_target_pairs={{0,1},{1,2},{2,3},{3,0},{4,5},{5,6},{6,7},{7,4},{8,9},{9,10},{10,1... | collective-permute-start | bytes 294920 | tf_op jit(solution)/shard_map/ppermute | solution.py:33
  4.2 9.2 %collective-permute-start.1 = (bf16[3,32,512]{2,1,0:T(8,128)(2,1)S(1)}, bf16[3,32,512]{2,1,0:T(8,128)(2,1)S(1)}, u32[]{:S(2)}, u32[]{:S(2)}) collective-permute-start(bf16[3,32,512]{2,1,0:T(8,128)(2,1)S(1)} %get-tuple-element.42), channel_id=1, source_target_pairs={{0,2},{1,3},{2,0},{3,1},{4,6},{5,7},{6,4},{7,5},{8,10},{9,11},{10,... | collective-permute-start | bytes 294920 | tf_op jit(solution)/shard_map/ppermute | solution.py:33
  6.8 6.6 %collective-permute-start.2 = (bf16[3,32,512]{2,1,0:T(8,128)(2,1)S(1)}, bf16[3,32,512]{2,1,0:T(8,128)(2,1)S(1)}, u32[]{:S(2)}, u32[]{:S(2)}) collective-permute-start(bf16[3,32,512]{2,1,0:T(8,128)(2,1)S(1)} %get-tuple-element.41), channel_id=1, source_target_pairs={{0,3},{1,0},{2,1},{3,2},{4,7},{5,4},{6,5},{7,6},{8,11},{9,8},{10,9... | collective-permute-start | bytes 294920 | tf_op jit(solution)/shard_map/ppermute | solution.py:33
  8.2 13.5 %copy-start.6 = (f32[4,4]{1,0:T(4,128)S(1)}, f32[4,4]{1,0:T(4,128)}, u32[]{:S(2)}) copy-start(f32[4,4]{1,0:T(4,128)} %param.10) | copy-start | bytes 196
  9.4 13.8 %copy-start.16 = (pred[4]{0:T(512)(128)(4,1)}, pred[4]{0:T(512)(128)(4,1)S(1)}, u32[]{:S(2)}) copy-start(pred[4]{0:T(512)(128)(4,1)S(1)} %compare_and_fusion) | copy-start | bytes 16
  14.9 5.3 %collective-permute-start.3 = (bf16[1,128,512]{2,1,0:T(8,128)(2,1)S(1)}, bf16[1,128,512]{2,1,0:T(8,128)(2,1)S(1)}, u32[]{:S(2)}, u32[]{:S(2)}) collective-permute-start(bf16[1,128,512]{2,1,0:T(8,128)(2,1)S(1)} %bitcast.85), channel_id=1, source_target_pairs={{0,16},{4,20},{8,24},{12,28},{16,0},{20,4},{24,8},{28,12},{1,17},{... | collective-permute-start | bytes 393224 | tf_op jit(solution)/shard_map/ppermute | solution.py:47
  20.2 7.3 %collective-permute-start.4 = (bf16[2,128,512]{2,1,0:T(8,128)(2,1)S(1)}, bf16[2,128,512]{2,1,0:T(8,128)(2,1)S(1)}, u32[]{:S(2)}, u32[]{:S(2)}) collective-permute-start(bf16[2,128,512]{2,1,0:T(8,128)(2,1)S(1)} %maximum_select_fusion.4), channel_id=1, source_target_pairs={{0,8},{4,12},{8,0},{12,4},{16,24},{20,28},{24,16},{28,20},{1,9},{5... | collective-permute-start | bytes 786440 | tf_op jit(solution)/shard_map/ppermute | solution.py:47
  23.3 2.1 %collective-permute-start.9 = (bf16[5,512]{1,0:T(8,128)(2,1)S(1)}, bf16[5,512]{1,0:T(8,128)(2,1)S(1)}, u32[]{:S(2)}, u32[]{:S(2)}) collective-permute-start(bf16[5,512]{1,0:T(8,128)(2,1)S(1)} %slice.270), channel_id=1, source_target_pairs={{0,4},{4,8},{8,12},{12,16},{16,20},{20,24},{24,28},{1,5},{5,9},{9,... | collective-permute-start | bytes 15368 | tf_op jit(solution)/shard_map/ppermute | solution.py:23
  27.5 2.0 %collective-permute-start.5 = (bf16[4,128,512]{2,1,0:T(8,128)(2,1)S(1)}, bf16[4,128,512]{2,1,0:T(8,128)(2,1)S(1)}, u32[]{:S(2)}, u32[]{:S(2)}) collective-permute-start(bf16[4,128,512]{2,1,0:T(8,128)(2,1)S(1)} %maximum_select_fusion.2), channel_id=1, source_target_pairs={{0,4},{4,0},{8,12},{12,8},{16,20},{20,16},{24,28},{28,24},{1,5},{5... | collective-permute-start | bytes 1572872 | tf_op jit(solution)/shard_map/ppermute | solution.py:47
  27.8 2.0 %copy-start = (bf16[128,4,6,128]{0,3,2,1:T(8,128)(2,1)}, bf16[128,4,6,128]{0,3,2,1:T(8,128)(2,1)S(1)}, u32[]{:S(2)}) copy-start(bf16[128,4,6,128]{0,3,2,1:T(8,128)(2,1)S(1)} %constant_dynamic-update-slice_fusion) | copy-start | bytes 2359300
  29.9 0.9 %copy-start.2 = (bf16[128,4,128]{2,1,0:T(4,128)(2,1)S(1)}, bf16[128,4,128]{2,1,0:T(4,128)(2,1)}, u32[]{:S(2)}) copy-start(bf16[128,4,128]{2,1,0:T(4,128)(2,1)} %concatenate.67) | copy-start | bytes 393220
  30.1 1.8 %copy-start.1 = (bf16[1,4,32,512]{3,2,0,1:T(8,128)(2,1)S(1)}, bf16[1,4,32,512]{3,2,0,1:T(8,128)(2,1)}, u32[]{:S(2)}) copy-start(bf16[1,4,32,512]{3,2,0,1:T(8,128)(2,1)} %get-tuple-element.38) | copy-start | bytes 393220
  30.3 9.7 %copy-start.7 = (f32[4]{0:T(128)S(1)}, f32[4]{0:T(128)}, u32[]{:S(2)}) copy-start(f32[4]{0:T(128)} %get-tuple-element.23) | copy-start | bytes 52
  30.3 9.7 %copy-start.8 = (f32[4]{0:T(128)S(1)}, f32[4]{0:T(128)}, u32[]{:S(2)}) copy-start(f32[4]{0:T(128)} %get-tuple-element.26) | copy-start | bytes 52
  30.3 9.7 %copy-start.9 = (f32[4]{0:T(128)S(1)}, f32[4]{0:T(128)}, u32[]{:S(2)}) copy-start(f32[4]{0:T(128)} %get-tuple-element.28) | copy-start | bytes 52
  32.0 7.8 %collective-permute-start.6 = (bf16[1,128,512]{2,1,0:T(8,128)(2,1)S(1)}, bf16[1,128,512]{2,1,0:T(8,128)(2,1)S(1)}, u32[]{:S(2)}, u32[]{:S(2)}) collective-permute-start(bf16[1,128,512]{2,1,0:T(8,128)(2,1)S(1)} %bitcast.83), channel_id=1, source_target_pairs={{0,16},{4,20},{8,24},{12,28},{16,0},{20,4},{24,8},{28,12},{1,17},{... | collective-permute-start | bytes 393224 | tf_op jit(solution)/shard_map/ppermute | solution.py:47
  39.8 12.4 %collective-permute-start.7 = (bf16[2,128,512]{2,1,0:T(8,128)(2,1)S(1)}, bf16[2,128,512]{2,1,0:T(8,128)(2,1)S(1)}, u32[]{:S(2)}, u32[]{:S(2)}) collective-permute-start(bf16[2,128,512]{2,1,0:T(8,128)(2,1)S(1)} %maximum_select_fusion.5), channel_id=1, source_target_pairs={{0,8},{4,12},{8,0},{12,4},{16,24},{20,28},{24,16},{28,20},{1,9},{5... | collective-permute-start | bytes 786440 | tf_op jit(solution)/shard_map/ppermute | solution.py:47
  41.2 11.0 %copy-start.11 = (f32[4]{0:T(128)S(1)}, f32[4]{0:T(128)}, u32[]{:S(2)}) copy-start(f32[4]{0:T(128)} %get-tuple-element.14) | copy-start | bytes 52
  41.2 11.0 %copy-start.12 = (f32[4]{0:T(128)S(1)}, f32[4]{0:T(128)}, u32[]{:S(2)}) copy-start(f32[4]{0:T(128)} %get-tuple-element.18) | copy-start | bytes 52
  41.2 11.0 %copy-start.13 = (f32[4]{0:T(128)S(1)}, f32[4]{0:T(128)}, u32[]{:S(2)}) copy-start(f32[4]{0:T(128)} %get-tuple-element.22) | copy-start | bytes 52
  41.2 11.0 %copy-start.14 = (f32[4]{0:T(128)S(1)}, f32[4]{0:T(128)}, u32[]{:S(2)}) copy-start(f32[4]{0:T(128)} %get-tuple-element.25) | copy-start | bytes 52
  41.2 11.0 %copy-start.15 = (f32[4]{0:T(128)S(1)}, f32[4]{0:T(128)}, u32[]{:S(2)}) copy-start(f32[4]{0:T(128)} %get-tuple-element.27) | copy-start | bytes 52
  52.4 5.3 %collective-permute-start.8 = (bf16[4,128,512]{2,1,0:T(8,128)(2,1)S(1)}, bf16[4,128,512]{2,1,0:T(8,128)(2,1)S(1)}, u32[]{:S(2)}, u32[]{:S(2)}) collective-permute-start(bf16[4,128,512]{2,1,0:T(8,128)(2,1)S(1)} %maximum_select_fusion.3), channel_id=1, source_target_pairs={{0,4},{4,0},{8,12},{12,8},{16,20},{20,16},{24,28},{28,24},{1,5},{5... | collective-permute-start | bytes 1572872 | tf_op jit(solution)/shard_map/ppermute | solution.py:47
  57.8 1.8 %copy-start.3 = (f32[1024,128]{1,0:T(8,128)S(1)}, f32[1024,128]{1,0:T(8,128)}, u32[]{:S(2)}) copy-start(f32[1024,128]{1,0:T(8,128)} %get-tuple-element.33) | copy-start | bytes 1572868
  57.8 1.8 %copy-start.18 = (f32[4]{0:T(128)S(1)}, f32[4]{0:T(128)}, u32[]{:S(2)}) copy-start(f32[4]{0:T(128)} %get-tuple-element.29) | copy-start | bytes 52
  57.8 1.8 %copy-start.19 = (f32[4]{0:T(128)S(1)}, f32[4]{0:T(128)}, u32[]{:S(2)}) copy-start(f32[4]{0:T(128)} %get-tuple-element.30) | copy-start | bytes 52
  57.9 1.8 %copy-start.20 = (f32[4]{0:T(128)S(1)}, f32[4]{0:T(128)}, u32[]{:S(2)}) copy-start(f32[4]{0:T(128)} %get-tuple-element.31) | copy-start | bytes 52
  57.9 1.8 %copy-start.21 = (f32[4]{0:T(128)S(1)}, f32[4]{0:T(128)}, u32[]{:S(2)}) copy-start(f32[4]{0:T(128)} %get-tuple-element.32) | copy-start | bytes 52
  58.8 1.1 %copy-start.4 = (f32[1024,128]{1,0:T(8,128)S(1)}, f32[1024,128]{1,0:T(8,128)}, u32[]{:S(2)}) copy-start(f32[1024,128]{1,0:T(8,128)} %get-tuple-element.34) | copy-start | bytes 1572868
  59.9 2.2 %copy-start.10 = (f32[512]{0:T(512)S(1)}, f32[512]{0:T(512)}, u32[]{:S(2)}) copy-start(f32[512]{0:T(512)} %param.11) | copy-start | bytes 6148
  62.0 9.3 %copy-start.17 = (pred[4]{0:T(512)(128)(4,1)S(1)}, pred[4]{0:T(512)(128)(4,1)}, u32[]{:S(2)}) copy-start(pred[4]{0:T(512)(128)(4,1)} %copy-done.16) | copy-start | bytes 16
  62.5 5.8 %collective-permute-start.10 = (bf16[32,512]{1,0:T(8,128)(2,1)S(1)}, bf16[32,512]{1,0:T(8,128)(2,1)S(1)}, u32[]{:S(2)}, u32[]{:S(2)}) collective-permute-start(bf16[32,512]{1,0:T(8,128)(2,1)S(1)} %copy.81), channel_id=1, source_target_pairs={{0,1},{1,2},{2,3},{3,0},{4,5},{5,6},{6,7},{7,4},{8,9},{9,10},{10,1... | collective-permute-start | bytes 98312 | tf_op jit(solution)/shard_map/ppermute | solution.py:33
  65.3 5.2 %collective-permute-start.11 = (bf16[32,512]{1,0:T(8,128)(2,1)S(1)}, bf16[32,512]{1,0:T(8,128)(2,1)S(1)}, u32[]{:S(2)}, u32[]{:S(2)}) collective-permute-start(bf16[32,512]{1,0:T(8,128)(2,1)S(1)} %copy.82), channel_id=1, source_target_pairs={{0,2},{1,3},{2,0},{3,1},{4,6},{5,7},{6,4},{7,5},{8,10},{9,11},{10,... | collective-permute-start | bytes 98312 | tf_op jit(solution)/shard_map/ppermute | solution.py:33
  66.6 4.1 %collective-permute-start.12 = (bf16[32,512]{1,0:T(8,128)(2,1)S(1)}, bf16[32,512]{1,0:T(8,128)(2,1)S(1)}, u32[]{:S(2)}, u32[]{:S(2)}) collective-permute-start(bf16[32,512]{1,0:T(8,128)(2,1)S(1)} %copy.83), channel_id=1, source_target_pairs={{0,3},{1,0},{2,1},{3,2},{4,7},{5,4},{6,5},{7,6},{8,11},{9,8},{10,9... | collective-permute-start | bytes 98312 | tf_op jit(solution)/shard_map/ppermute | solution.py:33

commit v10 on v9

--- a/solution.py
+++ b/solution.py
@@ -10,6 +10,7 @@
 KCONV = 11
 KEY_BLOCK = 128
 KEY_SPAN = 1024
+CAUSAL_PEERS = 8
 ROW_CHUNK = 128
 
 
@@ -53,6 +54,21 @@
         )
     held = held.reshape((2,) * bits + shard.shape)
     return jnp.transpose(held, tuple(reversed(range(bits))) + tuple(range(bits, held.ndim)))
+
+
+def causal_gathered(shard, axis):
+    peers = lax.axis_size(axis)
+    if peers > CAUSAL_PEERS:
+        return gathered(shard, axis)
+    place = lax.axis_index(axis)
+    received = [shard]
+    for shift in range(1, peers):
+        pairs = [(i, i + shift) for i in range(peers - shift)]
+        received.append(lax.ppermute(shard, axis, pairs))
+    received.append(jnp.zeros_like(shard))
+    blocks = jnp.arange(peers, dtype=jnp.int32)
+    order = jnp.where(blocks <= place, place - blocks, peers)
+    return jnp.take(jnp.stack(received), order, axis=0)
 
 
 def logits_kernel(taps_ref, query_ref, keys_ref, out_ref, high_ref, low_ref, conv_ref):
@@ -213,9 +229,9 @@
     query_first = ctx_place * shard_rows
     earlier = passed_along(query_local[shard_rows - row_lead :], "ctx", 1)
     query_ext = jnp.concatenate([earlier, query_local], axis=0)
-    key_all = gathered(key_local, "ctx").reshape((-1, width))
+    key_all = causal_gathered(key_local, "ctx").reshape((-1, width))
     key_all, value_local = lax.optimization_barrier((key_all, value_local))
-    value_all = gathered(value_local, "ctx").reshape((-1, width))
+    value_all = causal_gathered(value_local, "ctx").reshape((-1, width))
     seq_len = key_all.shape[0]
     key_pad = jnp.concatenate(
         [jnp.zeros((KEY_BLOCK, width), key_all.dtype), key_all], axis=0

time: 72.4 us -> 93.8 us (1.30)
  starting transfers between devices: 21 us -> 43.4 us
  waiting for transfers between devices: 16.3 us -> 10.7 us
  local copies, waits for them, and re-layouts: 12.9 us -> 15.6 us
  other arithmetic: 8.36 us -> 9.34 us
    ppermute x6 -> x14, starting transfers between devices: 7.42 us -> 31.6 us  [causal_gathered(): received.append(lax.ppermute(shard, axis, pairs))]
    ppermute x6 -> x14, waiting for transfers between devices: 9.5 us -> 3.51 us  [causal_gathered(): received.append(lax.ppermute(shard, axis, pairs))]
    unnamed x53 -> x81, local copies, waits for them, and re-layouts: 0.92 us -> 4.99 us
    ppermute x6, starting transfers between devices: 12.2 us -> 10.6 us  [exchanged(): received.append(lax.ppermute(outgoing, axis, pairs))]
    gather x0 -> x2, local copies, waits for them, and re-layouts: none -> 1.47 us  [causal_gathered(): return jnp.take(jnp.stack(received), order, axis=0)]
    transpose x2 -> x0, local copies, waits for them, and re-layouts: 1.04 us -> none  [gathered(): jnp.transpose(held, tuple(reversed(range(bits))) + tuple(range(bits, held...]
  transfers between devices with their start and end apart: 13 -> 21, of which waited for: 9 -> 7; matrix products, arithmetic and copies ran while one was open for 17% -> 20% of each run, Pallas kernels for 15% -> 12%
where the time goes in v10:
time: 93.8 us; the launch traced here: 93.2 us
  starting transfers between devices  43.4 us (46%)
  local copies, waits for them, and re-layouts  15.6 us (17%)
  Pallas kernels  10.8 us (12%)
  waiting for transfers between devices  10.7 us (11%)
  other arithmetic  9.34 us (10%)
  matrix products  2.16 us (2%)
  between operations  1.01 us (1%)
    ppermute x14, starting transfers between devices, causal_gathered(): received.append(lax.ppermute(shard, axis, pairs))  31.6 us
    pallas_call x1, Pallas kernels, conv_logits(): pl.pallas_call(logits_kernel, grid=(heads, seq_len // span), in_specs=[pl...  10.8 us
    ppermute x6, starting transfers between devices, exchanged(): received.append(lax.ppermute(outgoing, axis, pairs))  10.6 us
    ppermute x6, waiting for transfers between devices, exchanged(): received.append(lax.ppermute(outgoing, axis, pairs))  6.48 us
    unnamed x81, local copies, waits for them, and re-layouts  4.99 us
    div x1, other arithmetic, attend_chunk(): probabilities = expd / jnp.sum(expd, axis=1, keepdims=True)  3.88 us
    ppermute x14, waiting for transfers between devices, causal_gathered(): received.append(lax.ppermute(shard, axis, pairs))  3.51 us
    dot_general x1, matrix products, attend_chunk(): jnp.einsum('hki,khd->ihd', mixed_probs, value_heads, preferred_element_ty...  2.16 us
  transfers between devices with their start and end apart: 21, of which 7 were waited for; matrix products, arithmetic and copies ran while one was open for 20% of the time, Pallas kernels for 12%

profile of v10, /device:TPU:0, one launch (start us, length us, event | category | flops | bytes accessed | tf_op | source)
XLA Modules:
  0.0 93.2 jit_solution(11349428347351961498)
XLA Ops:
  0.0 1.1 %pad_maximum_fusion = bf16[3,32,2048]{2,1,0:T(8,128)(2,1)S(1)} fusion(bf16[1,32,2048]{2,1,0:T(8,128)(2,1)} %bitcast.123, bf16[1,32,2048]{2,1,0:T(8,128)(2,1)} %bitcast.124, bf16[1,32,2048]{2,1,0:T(8,128)(2,1)} %bitcast.125), kind=kLoop, calls=%fused_computation.41 | loop fusion | flops 393216 | bytes 786432 | tf_op jit(solution)/shard_map/stack | solution.py:213
  1.2 5.1 %collective-permute-start.2 = (bf16[3,32,512]{2,1,0:T(8,128)(2,1)S(1)}, bf16[3,32,512]{2,1,0:T(8,128)(2,1)S(1)}, u32[]{:S(2)}, u32[]{:S(2)}) collective-permute-start(bf16[3,32,512]{2,1,0:T(8,128)(2,1)S(1)} %get-tuple-element.42), channel_id=1, source_target_pairs={{0,3},{1,0},{2,1},{3,2},{4,7},{5,4},{6,5},{7,6},{8,11},{9,8},{10,9... | collective-permute-start | bytes 294920 | tf_op jit(solution)/shard_map/ppermute | solution.py:34
  6.3 1.0 %collective-permute-start = (bf16[3,32,512]{2,1,0:T(8,128)(2,1)S(1)}, bf16[3,32,512]{2,1,0:T(8,128)(2,1)S(1)}, u32[]{:S(2)}, u32[]{:S(2)}) collective-permute-start(bf16[3,32,512]{2,1,0:T(8,128)(2,1)S(1)} %get-tuple-element.44), channel_id=1, source_target_pairs={{0,1},{1,2},{2,3},{3,0},{4,5},{5,6},{6,7},{7,4},{8,9},{9,10},{10,1... | collective-permute-start | bytes 294920 | tf_op jit(solution)/shard_map/ppermute | solution.py:34
  7.3 1.0 %slice_reduce_fusion.17 = (f32[4]{0:T(128)}, f32[4]{0:T(128)}, f32[4]{0:T(128)}, f32[4]{0:T(128)}, f32[4]{0:T(128)}, /*index=5*/f32[4]{0:T(128)}, f32[4]{0:T(128...) fusion(f32[4,6,11]{2,0,1:T(4,128)S(1)} %copy-done.2), kind=kLoop, calls=%fused_computation.154 | loop fusion | bytes 480 | tf_op jit(solution)/shard_map/slice | solution.py:173
  8.3 0.7 reshape.177.taps_ref
  9.0 0.6 pad_clamp_fusion
  9.6 1.2 %fusion.16 = (pred[1024,128]{1,0:T(8,128)(4,1)}, pred[1024,128]{1,0:T(8,128)(4,1)}, pred[1024,128]{1,0:T(8,128)(4,1)}, pred[1024,128]{1,0:T(8,128)(4,1)}, pred[1...) fusion(s32[128]{0:T(128)S(1)} %iota_add_fusion), kind=kLoop, calls=%fused_computation.40 | loop fusion | flops 917504 | bytes 786944 | tf_op jit(solution)/shard_map/ge | solution.py:189
  10.8 0.8 slice_reduce_fusion.18
  11.6 0.5 compare_and_fusion
  12.1 2.9 %collective-permute-done.1 = bf16[3,32,512]{2,1,0:T(8,128)(2,1)S(1)} collective-permute-done((bf16[3,32,512]{2,1,0:T(8,128)(2,1)S(1)}, bf16[3,32,512]{2,1,0:T(8,128)(2,1)S(1)}, u32[]{:S(2)}, u32[]{:S(2)}) %collective-permute-start.1) | collective-permute-done | bytes 98336 | tf_op jit(solution)/shard_map/ppermute | solution.py:34
  15.1 0.6 gather_fusion
  15.7 0.1 select_bitcast_fusion
  15.8 2.1 %collective-permute-start.3 = (bf16[128,512]{1,0:T(8,128)(2,1)S(1)}, bf16[128,512]{1,0:T(8,128)(2,1)}, u32[]{:S(2)}, u32[]{:S(2)}) collective-permute-start(bf16[128,512]{1,0:T(8,128)(2,1)S(1)} %bitcast.115), channel_id=1, source_target_pairs={{0,4},{4,8},{8,12},{12,16},{16,20},{20,24},{24,28},{1,5},{5,9},{9,... | collective-permute-start | bytes 393224 | tf_op jit(solution)/shard_map/ppermute | solution.py:67
  17.9 3.9 %collective-permute-start.4 = (bf16[128,512]{1,0:T(8,128)(2,1)S(1)}, bf16[128,512]{1,0:T(8,128)(2,1)}, u32[]{:S(2)}, u32[]{:S(2)}) collective-permute-start(bf16[128,512]{1,0:T(8,128)(2,1)S(1)} %bitcast.116), channel_id=1, source_target_pairs={{0,8},{4,12},{8,16},{12,20},{16,24},{20,28},{1,9},{5,13},{9,17},{1... | collective-permute-start | bytes 393224 | tf_op jit(solution)/shard_map/ppermute | solution.py:67
  21.8 3.7 %collective-permute-start.5 = (bf16[128,512]{1,0:T(8,128)(2,1)S(1)}, bf16[128,512]{1,0:T(8,128)(2,1)S(1)}, u32[]{:S(2)}, u32[]{:S(2)}) collective-permute-start(bf16[128,512]{1,0:T(8,128)(2,1)S(1)} %bitcast.117), channel_id=1, source_target_pairs={{0,12},{4,16},{8,20},{12,24},{16,28},{1,13},{5,17},{9,21},{13,25},... | collective-permute-start | bytes 393224 | tf_op jit(solution)/shard_map/ppermute | solution.py:67
  25.5 1.3 %collective-permute-start.6 = (bf16[128,512]{1,0:T(8,128)(2,1)S(1)}, bf16[128,512]{1,0:T(8,128)(2,1)S(1)}, u32[]{:S(2)}, u32[]{:S(2)}) collective-permute-start(bf16[128,512]{1,0:T(8,128)(2,1)S(1)} %bitcast.118), channel_id=1, source_target_pairs={{0,16},{4,20},{8,24},{12,28},{1,17},{5,21},{9,25},{13,29},{2,18},{... | collective-permute-start | bytes 393224 | tf_op jit(solution)/shard_map/ppermute | solution.py:67
  26.8 0.1 copy.66
  27.0 1.3 %collective-permute-start.17 = (bf16[5,512]{1,0:T(8,128)(2,1)S(1)}, bf16[5,512]{1,0:T(8,128)(2,1)S(1)}, u32[]{:S(2)}, u32[]{:S(2)}) collective-permute-start(bf16[5,512]{1,0:T(8,128)(2,1)S(1)} %slice.274), channel_id=1, source_target_pairs={{0,4},{4,8},{8,12},{12,16},{16,20},{20,24},{24,28},{1,5},{5,9},{9,... | collective-permute-start | bytes 15368 | tf_op jit(solution)/shard_map/ppermute | solution.py:24
  28.4 0.8 collective-permute-done.17
  29.1 2.2 %collective-permute-start.7 = (bf16[128,512]{1,0:T(8,128)(2,1)S(1)}, bf16[128,512]{1,0:T(8,128)(2,1)}, u32[]{:S(2)}, u32[]{:S(2)}) collective-permute-start(bf16[128,512]{1,0:T(8,128)(2,1)S(1)} %bitcast.120), channel_id=1, source_target_pairs={{0,20},{4,24},{8,28},{1,21},{5,25},{9,29},{2,22},{6,26},{10,30},{3... | collective-permute-start | bytes 393224 | tf_op jit(solution)/shard_map/ppermute | solution.py:67
  31.4 0.1 pad_maximum_fusion.3
  31.5 0.1 copy.61
  31.6 0.1 copy.62
  31.7 0.1 copy.63
  31.9 0.1 copy.64
  32.1 0.1 copy.65
  32.3 1.8 %collective-permute-start.8 = (bf16[128,512]{1,0:T(8,128)(2,1)S(1)}, bf16[128,512]{1,0:T(8,128)(2,1)S(1)}, u32[]{:S(2)}, u32[]{:S(2)}) collective-permute-start(bf16[128,512]{1,0:T(8,128)(2,1)S(1)} %bitcast.121), channel_id=1, source_target_pairs={{0,24},{4,28},{1,25},{5,29},{2,26},{6,30},{3,27},{7,31}} | collective-permute-start | bytes 393224 | tf_op jit(solution)/shard_map/ppermute | solution.py:67
  34.1 0.9 bitcast_dynamic-update-slice_fusion.14
  35.0 1.3 %collective-permute-start.9 = (bf16[128,512]{1,0:T(8,128)(2,1)S(1)}, bf16[128,512]{1,0:T(8,128)(2,1)S(1)}, u32[]{:S(2)}, u32[]{:S(2)}) collective-permute-start(bf16[128,512]{1,0:T(8,128)(2,1)S(1)} %bitcast.122), channel_id=1, source_target_pairs={{0,28},{1,29},{2,30},{3,31}} | collective-permute-start | bytes 393224 | tf_op jit(solution)/shard_map/ppermute | solution.py:67
  36.3 0.9 bitcast_dynamic-update-slice_fusion.13
  37.3 0.9 bitcast_dynamic-update-slice_fusion.10
  38.2 1.1 %collective-permute-done.9 = bf16[128,512]{1,0:T(8,128)(2,1)S(1)} collective-permute-done((bf16[128,512]{1,0:T(8,128)(2,1)S(1)}, bf16[128,512]{1,0:T(8,128)(2,1)S(1)}, u32[]{:S(2)}, u32[]{:S(2)}) %collective-permute-start.9) | collective-permute-done | bytes 131104 | tf_op jit(solution)/shard_map/ppermute | solution.py:67
  39.4 0.7 gather_fusion.2
  40.1 0.2 broadcast_select_fusion
  40.3 2.0 %collective-permute-start.10 = (bf16[128,512]{1,0:T(8,128)(2,1)S(1)}, bf16[128,512]{1,0:T(8,128)(2,1)}, u32[]{:S(2)}, u32[]{:S(2)}) collective-permute-start(bf16[128,512]{1,0:T(8,128)(2,1)S(1)} %bitcast.107), channel_id=1, source_target_pairs={{0,4},{4,8},{8,12},{12,16},{16,20},{20,24},{24,28},{1,5},{5,9},{9,... | collective-permute-start | bytes 393224 | tf_op jit(solution)/shard_map/ppermute | solution.py:67
  42.2 1.9 %collective-permute-start.11 = (bf16[128,512]{1,0:T(8,128)(2,1)S(1)}, bf16[128,512]{1,0:T(8,128)(2,1)S(1)}, u32[]{:S(2)}, u32[]{:S(2)}) collective-permute-start(bf16[128,512]{1,0:T(8,128)(2,1)S(1)} %bitcast.108), channel_id=1, source_target_pairs={{0,8},{4,12},{8,16},{12,20},{16,24},{20,28},{1,9},{5,13},{9,17},{1... | collective-permute-start | bytes 393224 | tf_op jit(solution)/shard_map/ppermute | solution.py:67
  44.2 5.2 %collective-permute-start.12 = (bf16[128,512]{1,0:T(8,128)(2,1)S(1)}, bf16[128,512]{1,0:T(8,128)(2,1)S(1)}, u32[]{:S(2)}, u32[]{:S(2)}) collective-permute-start(bf16[128,512]{1,0:T(8,128)(2,1)S(1)} %bitcast.109), channel_id=1, source_target_pairs={{0,12},{4,16},{8,20},{12,24},{16,28},{1,13},{5,17},{9,21},{13,25},... | collective-permute-start | bytes 393224 | tf_op jit(solution)/shard_map/ppermute | solution.py:67
  49.4 2.3 %collective-permute-start.13 = (bf16[128,512]{1,0:T(8,128)(2,1)S(1)}, bf16[128,512]{1,0:T(8,128)(2,1)S(1)}, u32[]{:S(2)}, u32[]{:S(2)}) collective-permute-start(bf16[128,512]{1,0:T(8,128)(2,1)S(1)} %bitcast.110), channel_id=1, source_target_pairs={{0,16},{4,20},{8,24},{12,28},{1,17},{5,21},{9,25},{13,29},{2,18},{... | collective-permute-start | bytes 393224 | tf_op jit(solution)/shard_map/ppermute | solution.py:67
  51.7 1.3 %collective-permute-start.14 = (bf16[128,512]{1,0:T(8,128)(2,1)S(1)}, bf16[128,512]{1,0:T(8,128)(2,1)S(1)}, u32[]{:S(2)}, u32[]{:S(2)}) collective-permute-start(bf16[128,512]{1,0:T(8,128)(2,1)S(1)} %bitcast.111), channel_id=1, source_target_pairs={{0,20},{4,24},{8,28},{1,21},{5,25},{9,29},{2,22},{6,26},{10,30},{3... | collective-permute-start | bytes 393224 | tf_op jit(solution)/shard_map/ppermute | solution.py:67
  53.0 1.1 %concatenate.17.keys_ref = bf16[1152,512]{1,0:T(8,128)(2,1)} pad(bf16[1024,512]{1,0:T(8,128)(2,1)S(1)} %bitcast.96, bf16[]{:T(256)} %constant.114.clone.1), padding=128_0x0_0 | pad | bytes 2228226 | tf_op jit(solution)/shard_map/concatenate | solution.py:236
  54.3 0.1 fusion.57
  54.9 0.8 fusion.22
  56.3 10.8 %shard_map.64 = f32[4,1024,128]{2,1,0:T(8,128)} custom-call(f32[264]{0:T(512)} %reshape.177.taps_ref, bf16[4,768,128]{2,1,0:T(8,128)(2,1)} %bitcast.101, bf16[1152,512]{1,0:T(8,128)(2,1)} %concatenate.17.keys_ref), custom_call_target="tpu_custom_call" | custom-call | tf_op jit(solution)/shard_map/pallas_call | solution.py:136
  67.6 3.9 %divide_bitcast_fusion = f32[1,4,1024,128]{3,2,1,0:T(8,128)S(1)} fusion(f32[4,1024,128]{2,1,0:T(8,128)} %shard_map.64, f32[4,128]{1,0:T(4,128)S(1)} %get-tuple-element.61, f32[4,128]{1,0:T(4,128)S(1)} %get-tuple-element.60, f32[4,128]{1,0:T(4,128)S(1)} %get-tuple-element.59, f32[4,128]{1,0:T(4,128)S(1)} %subtract_bitcast_fusion.3, f32[4,128]{1,0:T(4,128)S(1)} %fusion.45, ...), kind=kOutput, calls=%fused_computation.7 | output fusion | flops 6818814 | bytes 4990976 | tf_op jit(solution)/shard_map/div | solution.py:192
  71.5 1.2 %slice_bitcast_fusion.3 = (f32[1024,128]{1,0:T(8,128)S(1)}, f32[1024,128]{1,0:T(8,128)}, f32[1024,128]{1,0:T(8,128)}, f32[1024,128]{1,0:T(8,128)}) fusion(f32[1,4,1024,128]{3,2,1,0:T(8,128)S(1)} %divide_bitcast_fusion), kind=kLoop, calls=%fused_computation.33 | loop fusion | bytes 4194304 | tf_op jit(solution)/shard_map/mul | solution.py:197
  72.7 1.3 %collective-permute-start.15 = (bf16[128,512]{1,0:T(8,128)(2,1)S(1)}, bf16[128,512]{1,0:T(8,128)(2,1)S(1)}, u32[]{:S(2)}, u32[]{:S(2)}) collective-permute-start(bf16[128,512]{1,0:T(8,128)(2,1)S(1)} %bitcast.113), channel_id=1, source_target_pairs={{0,24},{4,28},{1,25},{5,29},{2,26},{6,30},{3,27},{7,31}} | collective-permute-start | bytes 393224 | tf_op jit(solution)/shard_map/ppermute | solution.py:67
  74.0 0.9 bitcast_dynamic-update-slice_fusion.6
  74.9 1.3 %collective-permute-start.16 = (bf16[128,512]{1,0:T(8,128)(2,1)S(1)}, bf16[128,512]{1,0:T(8,128)(2,1)S(1)}, u32[]{:S(2)}, u32[]{:S(2)}) collective-permute-start(bf16[128,512]{1,0:T(8,128)(2,1)S(1)} %bitcast.114), channel_id=1, source_target_pairs={{0,28},{1,29},{2,30},{3,31}} | collective-permute-start | bytes 393224 | tf_op jit(solution)/shard_map/ppermute | solution.py:67
  76.3 0.3 collective-permute-done.15
  76.7 2.0 %collective-permute-done.16 = bf16[128,512]{1,0:T(8,128)(2,1)S(1)} collective-permute-done((bf16[128,512]{1,0:T(8,128)(2,1)S(1)}, bf16[128,512]{1,0:T(8,128)(2,1)S(1)}, u32[]{:S(2)}, u32[]{:S(2)}) %collective-permute-start.16) | collective-permute-done | bytes 131104 | tf_op jit(solution)/shard_map/ppermute | solution.py:67
  78.8 0.7 gather_fusion.3
  79.5 0.2 broadcast_select_fusion.1
  79.7 0.3 reshape.220
  80.0 0.7 copy-done.1
  80.7 2.2 %multiply_reduce_fusion = (f32[128,4]{0,1:T(4,128)S(1)}, f32[128,4,128]{0,2,1:T(8,128)S(1)}) fusion(f32[1024,128]{1,0:T(8,128)S(1)} %copy-done.1, f32[4]{0:T(128)S(1)} %copy-done.25, f32[1024,128]{1,0:T(8,128)} %get-tuple-element.36, f32[4]{0:T(128)S(1)} %copy-done.26, f32[1024,128]{1,0:T(8,128)} %get-tuple-element.37, f32[4]{0:T(128)S(1)} %copy-done.27, ...), kind=kOutput, calls=%fused_computation.55 | convolution fusion | flops 138542592 | bytes 3409984 | tf_op jit(solution)/shard_map/hki,khd->ihd/dot_general | solution.py:199
  82.9 0.1 multiply_convert_fusion
  83.1 0.2 constant_dynamic-slice_fusion.3
  83.4 2.0 %collective-permute-start.20 = (bf16[32,512]{1,0:T(8,128)(2,1)S(1)}, bf16[32,512]{1,0:T(8,128)(2,1)S(1)}, u32[]{:S(2)}, u32[]{:S(2)}) collective-permute-start(bf16[32,512]{1,0:T(8,128)(2,1)S(1)} %copy.80), channel_id=1, source_target_pairs={{0,3},{1,0},{2,1},{3,2},{4,7},{5,4},{6,5},{7,6},{8,11},{9,8},{10,9... | collective-permute-start | bytes 98312 | tf_op jit(solution)/shard_map/ppermute | solution.py:34
  85.5 0.4 collective-permute-start.19
  86.0 2.1 %collective-permute-start.18 = (bf16[32,512]{1,0:T(8,128)(2,1)S(1)}, bf16[32,512]{1,0:T(8,128)(2,1)S(1)}, u32[]{:S(2)}, u32[]{:S(2)}) collective-permute-start(bf16[32,512]{1,0:T(8,128)(2,1)S(1)} %copy.78), channel_id=1, source_target_pairs={{0,1},{1,2},{2,3},{3,0},{4,5},{5,6},{6,7},{7,4},{8,9},{9,10},{10,1... | collective-permute-start | bytes 98312 | tf_op jit(solution)/shard_map/ppermute | solution.py:34
  88.1 2.2 %collective-permute-done.19 = bf16[32,512]{1,0:T(8,128)(2,1)S(1)} collective-permute-done((bf16[32,512]{1,0:T(8,128)(2,1)S(1)}, bf16[32,512]{1,0:T(8,128)(2,1)S(1)}, u32[]{:S(2)}, u32[]{:S(2)}) %collective-permute-start.19) | collective-permute-done | bytes 32800 | tf_op jit(solution)/shard_map/ppermute | solution.py:34
  90.3 1.4 %collective-permute-done.18 = bf16[32,512]{1,0:T(8,128)(2,1)S(1)} collective-permute-done((bf16[32,512]{1,0:T(8,128)(2,1)S(1)}, bf16[32,512]{1,0:T(8,128)(2,1)S(1)}, u32[]{:S(2)}, u32[]{:S(2)}) %collective-permute-start.18) | collective-permute-done | bytes 32800 | tf_op jit(solution)/shard_map/ppermute | solution.py:34
  91.7 0.7 gather_fusion.1
  92.5 0.7 copy.82
  (129 shorter events, 2.4 us)
Async XLA Ops:
  0.0 7.3 %copy-start.2 = (f32[4,6,11]{2,0,1:T(4,128)S(1)}, f32[4,6,11]{2,0,1:T(4,128)}, u32[]{:S(2)}) copy-start(f32[4,6,11]{2,0,1:T(4,128)} %param.11) | copy-start | bytes 3172
  0.0 10.8 %copy-start.3 = (f32[4,4]{1,0:T(4,128)S(1)}, f32[4,4]{1,0:T(4,128)}, u32[]{:S(2)}) copy-start(f32[4,4]{1,0:T(4,128)} %param.12) | copy-start | bytes 196
  1.2 11.0 %collective-permute-start.2 = (bf16[3,32,512]{2,1,0:T(8,128)(2,1)S(1)}, bf16[3,32,512]{2,1,0:T(8,128)(2,1)S(1)}, u32[]{:S(2)}, u32[]{:S(2)}) collective-permute-start(bf16[3,32,512]{2,1,0:T(8,128)(2,1)S(1)} %get-tuple-element.42), channel_id=1, source_target_pairs={{0,3},{1,0},{2,1},{3,2},{4,7},{5,4},{6,5},{7,6},{8,11},{9,8},{10,9... | collective-permute-start | bytes 294920 | tf_op jit(solution)/shard_map/ppermute | solution.py:34
  6.3 8.7 %collective-permute-start.1 = (bf16[3,32,512]{2,1,0:T(8,128)(2,1)S(1)}, bf16[3,32,512]{2,1,0:T(8,128)(2,1)S(1)}, u32[]{:S(2)}, u32[]{:S(2)}) collective-permute-start(bf16[3,32,512]{2,1,0:T(8,128)(2,1)S(1)} %get-tuple-element.43), channel_id=1, source_target_pairs={{0,2},{1,3},{2,0},{3,1},{4,6},{5,7},{6,4},{7,5},{8,10},{9,11},{10,... | collective-permute-start | bytes 294920 | tf_op jit(solution)/shard_map/ppermute | solution.py:34
  6.3 8.7 %collective-permute-start = (bf16[3,32,512]{2,1,0:T(8,128)(2,1)S(1)}, bf16[3,32,512]{2,1,0:T(8,128)(2,1)S(1)}, u32[]{:S(2)}, u32[]{:S(2)}) collective-permute-start(bf16[3,32,512]{2,1,0:T(8,128)(2,1)S(1)} %get-tuple-element.44), channel_id=1, source_target_pairs={{0,1},{1,2},{2,3},{3,0},{4,5},{5,6},{6,7},{7,4},{8,9},{9,10},{10,1... | collective-permute-start | bytes 294920 | tf_op jit(solution)/shard_map/ppermute | solution.py:34
  7.3 8.3 %copy-start.22 = (pred[4]{0:T(512)(128)(4,1)}, pred[4]{0:T(512)(128)(4,1)S(1)}, u32[]{:S(2)}) copy-start(pred[4]{0:T(512)(128)(4,1)S(1)} %compare_and_fusion.1) | copy-start | bytes 16
  9.0 6.6 %copy-start.10 = (s32[1024]{0:T(1024)}, s32[1024]{0:T(1024)S(1)}, u32[]{:S(2)}) copy-start(s32[1024]{0:T(1024)S(1)} %pad_clamp_fusion.1) | copy-start | bytes 12292
  15.8 16.5 %collective-permute-start.3 = (bf16[128,512]{1,0:T(8,128)(2,1)S(1)}, bf16[128,512]{1,0:T(8,128)(2,1)}, u32[]{:S(2)}, u32[]{:S(2)}) collective-permute-start(bf16[128,512]{1,0:T(8,128)(2,1)S(1)} %bitcast.115), channel_id=1, source_target_pairs={{0,4},{4,8},{8,12},{12,16},{16,20},{20,24},{24,28},{1,5},{5,9},{9,... | collective-permute-start | bytes 393224 | tf_op jit(solution)/shard_map/ppermute | solution.py:67
  17.9 17.1 %collective-permute-start.4 = (bf16[128,512]{1,0:T(8,128)(2,1)S(1)}, bf16[128,512]{1,0:T(8,128)(2,1)}, u32[]{:S(2)}, u32[]{:S(2)}) collective-permute-start(bf16[128,512]{1,0:T(8,128)(2,1)S(1)} %bitcast.116), channel_id=1, source_target_pairs={{0,8},{4,12},{8,16},{12,20},{16,24},{20,28},{1,9},{5,13},{9,17},{1... | collective-permute-start | bytes 393224 | tf_op jit(solution)/shard_map/ppermute | solution.py:67
  21.8 15.4 %collective-permute-start.5 = (bf16[128,512]{1,0:T(8,128)(2,1)S(1)}, bf16[128,512]{1,0:T(8,128)(2,1)S(1)}, u32[]{:S(2)}, u32[]{:S(2)}) collective-permute-start(bf16[128,512]{1,0:T(8,128)(2,1)S(1)} %bitcast.117), channel_id=1, source_target_pairs={{0,12},{4,16},{8,20},{12,24},{16,28},{1,13},{5,17},{9,21},{13,25},... | collective-permute-start | bytes 393224 | tf_op jit(solution)/shard_map/ppermute | solution.py:67
  25.5 11.8 %collective-permute-start.6 = (bf16[128,512]{1,0:T(8,128)(2,1)S(1)}, bf16[128,512]{1,0:T(8,128)(2,1)S(1)}, u32[]{:S(2)}, u32[]{:S(2)}) collective-permute-start(bf16[128,512]{1,0:T(8,128)(2,1)S(1)} %bitcast.118), channel_id=1, source_target_pairs={{0,16},{4,20},{8,24},{12,28},{1,17},{5,21},{9,25},{13,29},{2,18},{... | collective-permute-start | bytes 393224 | tf_op jit(solution)/shard_map/ppermute | solution.py:67
  27.0 2.1 %collective-permute-start.17 = (bf16[5,512]{1,0:T(8,128)(2,1)S(1)}, bf16[5,512]{1,0:T(8,128)(2,1)S(1)}, u32[]{:S(2)}, u32[]{:S(2)}) collective-permute-start(bf16[5,512]{1,0:T(8,128)(2,1)S(1)} %slice.274), channel_id=1, source_target_pairs={{0,4},{4,8},{8,12},{12,16},{16,20},{20,24},{24,28},{1,5},{5,9},{9,... | collective-permute-start | bytes 15368 | tf_op jit(solution)/shard_map/ppermute | solution.py:24
  29.1 8.2 %collective-permute-start.7 = (bf16[128,512]{1,0:T(8,128)(2,1)S(1)}, bf16[128,512]{1,0:T(8,128)(2,1)}, u32[]{:S(2)}, u32[]{:S(2)}) collective-permute-start(bf16[128,512]{1,0:T(8,128)(2,1)S(1)} %bitcast.120), channel_id=1, source_target_pairs={{0,20},{4,24},{8,28},{1,21},{5,25},{9,29},{2,22},{6,26},{10,30},{3... | collective-permute-start | bytes 393224 | tf_op jit(solution)/shard_map/ppermute | solution.py:67
  32.3 7.8 %copy-start = (bf16[128,4,6,128]{0,3,2,1:T(8,128)(2,1)}, bf16[128,4,6,128]{0,3,2,1:T(8,128)(2,1)S(1)}, u32[]{:S(2)}) copy-start(bf16[128,4,6,128]{0,3,2,1:T(8,128)(2,1)S(1)} %constant_dynamic-update-slice_fusion.1) | copy-start | bytes 2359300
  32.3 5.9 %collective-permute-start.8 = (bf16[128,512]{1,0:T(8,128)(2,1)S(1)}, bf16[128,512]{1,0:T(8,128)(2,1)S(1)}, u32[]{:S(2)}, u32[]{:S(2)}) collective-permute-start(bf16[128,512]{1,0:T(8,128)(2,1)S(1)} %bitcast.121), channel_id=1, source_target_pairs={{0,24},{4,28},{1,25},{5,29},{2,26},{6,30},{3,27},{7,31}} | collective-permute-start | bytes 393224 | tf_op jit(solution)/shard_map/ppermute | solution.py:67
  35.0 4.3 %collective-permute-start.9 = (bf16[128,512]{1,0:T(8,128)(2,1)S(1)}, bf16[128,512]{1,0:T(8,128)(2,1)S(1)}, u32[]{:S(2)}, u32[]{:S(2)}) collective-permute-start(bf16[128,512]{1,0:T(8,128)(2,1)S(1)} %bitcast.122), channel_id=1, source_target_pairs={{0,28},{1,29},{2,30},{3,31}} | collective-permute-start | bytes 393224 | tf_op jit(solution)/shard_map/ppermute | solution.py:67
  39.3 0.8 copy-start.16
  40.3 32.4 %collective-permute-start.10 = (bf16[128,512]{1,0:T(8,128)(2,1)S(1)}, bf16[128,512]{1,0:T(8,128)(2,1)}, u32[]{:S(2)}, u32[]{:S(2)}) collective-permute-start(bf16[128,512]{1,0:T(8,128)(2,1)S(1)} %bitcast.107), channel_id=1, source_target_pairs={{0,4},{4,8},{8,12},{12,16},{16,20},{20,24},{24,28},{1,5},{5,9},{9,... | collective-permute-start | bytes 393224 | tf_op jit(solution)/shard_map/ppermute | solution.py:67
  42.2 32.7 %collective-permute-start.11 = (bf16[128,512]{1,0:T(8,128)(2,1)S(1)}, bf16[128,512]{1,0:T(8,128)(2,1)S(1)}, u32[]{:S(2)}, u32[]{:S(2)}) collective-permute-start(bf16[128,512]{1,0:T(8,128)(2,1)S(1)} %bitcast.108), channel_id=1, source_target_pairs={{0,8},{4,12},{8,16},{12,20},{16,24},{20,28},{1,9},{5,13},{9,17},{1... | collective-permute-start | bytes 393224 | tf_op jit(solution)/shard_map/ppermute | solution.py:67
  44.2 32.1 %collective-permute-start.12 = (bf16[128,512]{1,0:T(8,128)(2,1)S(1)}, bf16[128,512]{1,0:T(8,128)(2,1)S(1)}, u32[]{:S(2)}, u32[]{:S(2)}) collective-permute-start(bf16[128,512]{1,0:T(8,128)(2,1)S(1)} %bitcast.109), channel_id=1, source_target_pairs={{0,12},{4,16},{8,20},{12,24},{16,28},{1,13},{5,17},{9,21},{13,25},... | collective-permute-start | bytes 393224 | tf_op jit(solution)/shard_map/ppermute | solution.py:67
  49.4 26.8 %collective-permute-start.13 = (bf16[128,512]{1,0:T(8,128)(2,1)S(1)}, bf16[128,512]{1,0:T(8,128)(2,1)S(1)}, u32[]{:S(2)}, u32[]{:S(2)}) collective-permute-start(bf16[128,512]{1,0:T(8,128)(2,1)S(1)} %bitcast.110), channel_id=1, source_target_pairs={{0,16},{4,20},{8,24},{12,28},{1,17},{5,21},{9,25},{13,29},{2,18},{... | collective-permute-start | bytes 393224 | tf_op jit(solution)/shard_map/ppermute | solution.py:67
  51.7 24.6 %collective-permute-start.14 = (bf16[128,512]{1,0:T(8,128)(2,1)S(1)}, bf16[128,512]{1,0:T(8,128)(2,1)S(1)}, u32[]{:S(2)}, u32[]{:S(2)}) collective-permute-start(bf16[128,512]{1,0:T(8,128)(2,1)S(1)} %bitcast.111), channel_id=1, source_target_pairs={{0,20},{4,24},{8,28},{1,21},{5,25},{9,29},{2,22},{6,26},{10,30},{3... | collective-permute-start | bytes 393224 | tf_op jit(solution)/shard_map/ppermute | solution.py:67
  56.2 11.0 %copy-start.4 = (f32[4]{0:T(128)S(1)}, f32[4]{0:T(128)}, u32[]{:S(2)}) copy-start(f32[4]{0:T(128)} %get-tuple-element.16) | copy-start | bytes 52
  56.2 11.0 %copy-start.5 = (f32[4]{0:T(128)S(1)}, f32[4]{0:T(128)}, u32[]{:S(2)}) copy-start(f32[4]{0:T(128)} %get-tuple-element.17) | copy-start | bytes 52
  56.2 11.0 %copy-start.6 = (f32[4]{0:T(128)S(1)}, f32[4]{0:T(128)}, u32[]{:S(2)}) copy-start(f32[4]{0:T(128)} %get-tuple-element.18) | copy-start | bytes 52
  56.2 11.0 %copy-start.7 = (f32[4]{0:T(128)S(1)}, f32[4]{0:T(128)}, u32[]{:S(2)}) copy-start(f32[4]{0:T(128)} %get-tuple-element.21) | copy-start | bytes 52
  56.2 11.0 %copy-start.8 = (f32[4]{0:T(128)S(1)}, f32[4]{0:T(128)}, u32[]{:S(2)}) copy-start(f32[4]{0:T(128)} %get-tuple-element.22) | copy-start | bytes 52
  56.2 11.0 %copy-start.9 = (f32[4]{0:T(128)S(1)}, f32[4]{0:T(128)}, u32[]{:S(2)}) copy-start(f32[4]{0:T(128)} %get-tuple-element.25) | copy-start | bytes 52
  56.2 11.1 %copy-start.11 = (f32[4]{0:T(128)S(1)}, f32[4]{0:T(128)}, u32[]{:S(2)}) copy-start(f32[4]{0:T(128)} %get-tuple-element.20) | copy-start | bytes 52
  56.2 11.1 %copy-start.12 = (f32[4]{0:T(128)S(1)}, f32[4]{0:T(128)}, u32[]{:S(2)}) copy-start(f32[4]{0:T(128)} %get-tuple-element.24) | copy-start | bytes 52
  56.3 11.1 %copy-start.13 = (f32[4]{0:T(128)S(1)}, f32[4]{0:T(128)}, u32[]{:S(2)}) copy-start(f32[4]{0:T(128)} %get-tuple-element.27) | copy-start | bytes 52
  56.3 11.1 %copy-start.14 = (f32[4]{0:T(128)S(1)}, f32[4]{0:T(128)}, u32[]{:S(2)}) copy-start(f32[4]{0:T(128)} %get-tuple-element.29) | copy-start | bytes 52
  56.3 11.2 %copy-start.17 = (f32[4]{0:T(128)S(1)}, f32[4]{0:T(128)}, u32[]{:S(2)}) copy-start(f32[4]{0:T(128)} %get-tuple-element.15) | copy-start | bytes 52
  56.3 11.2 %copy-start.18 = (f32[4]{0:T(128)S(1)}, f32[4]{0:T(128)}, u32[]{:S(2)}) copy-start(f32[4]{0:T(128)} %get-tuple-element.19) | copy-start | bytes 52
  56.3 11.2 %copy-start.19 = (f32[4]{0:T(128)S(1)}, f32[4]{0:T(128)}, u32[]{:S(2)}) copy-start(f32[4]{0:T(128)} %get-tuple-element.23) | copy-start | bytes 52
  56.3 11.2 %copy-start.20 = (f32[4]{0:T(128)S(1)}, f32[4]{0:T(128)}, u32[]{:S(2)}) copy-start(f32[4]{0:T(128)} %get-tuple-element.26) | copy-start | bytes 52
  56.3 11.2 %copy-start.21 = (f32[4]{0:T(128)S(1)}, f32[4]{0:T(128)}, u32[]{:S(2)}) copy-start(f32[4]{0:T(128)} %get-tuple-element.28) | copy-start | bytes 52
  72.7 4.0 %collective-permute-start.15 = (bf16[128,512]{1,0:T(8,128)(2,1)S(1)}, bf16[128,512]{1,0:T(8,128)(2,1)S(1)}, u32[]{:S(2)}, u32[]{:S(2)}) collective-permute-start(bf16[128,512]{1,0:T(8,128)(2,1)S(1)} %bitcast.113), channel_id=1, source_target_pairs={{0,24},{4,28},{1,25},{5,29},{2,26},{6,30},{3,27},{7,31}} | collective-permute-start | bytes 393224 | tf_op jit(solution)/shard_map/ppermute | solution.py:67
  74.9 3.8 %collective-permute-start.16 = (bf16[128,512]{1,0:T(8,128)(2,1)S(1)}, bf16[128,512]{1,0:T(8,128)(2,1)S(1)}, u32[]{:S(2)}, u32[]{:S(2)}) collective-permute-start(bf16[128,512]{1,0:T(8,128)(2,1)S(1)} %bitcast.114), channel_id=1, source_target_pairs={{0,28},{1,29},{2,30},{3,31}} | collective-permute-start | bytes 393224 | tf_op jit(solution)/shard_map/ppermute | solution.py:67
  79.7 1.0 %copy-start.1 = (f32[1024,128]{1,0:T(8,128)S(1)}, f32[1024,128]{1,0:T(8,128)}, u32[]{:S(2)}) copy-start(f32[1024,128]{1,0:T(8,128)} %get-tuple-element.35) | copy-start | bytes 1572868
  79.7 1.0 %copy-start.24 = (f32[4]{0:T(128)S(1)}, f32[4]{0:T(128)}, u32[]{:S(2)}) copy-start(f32[4]{0:T(128)} %get-tuple-element.30) | copy-start | bytes 52
  79.7 1.0 %copy-start.25 = (f32[4]{0:T(128)S(1)}, f32[4]{0:T(128)}, u32[]{:S(2)}) copy-start(f32[4]{0:T(128)} %get-tuple-element.31) | copy-start | bytes 52
  79.7 1.0 %copy-start.26 = (f32[4]{0:T(128)S(1)}, f32[4]{0:T(128)}, u32[]{:S(2)}) copy-start(f32[4]{0:T(128)} %get-tuple-element.32) | copy-start | bytes 52
  79.7 1.0 %copy-start.27 = (f32[4]{0:T(128)S(1)}, f32[4]{0:T(128)}, u32[]{:S(2)}) copy-start(f32[4]{0:T(128)} %get-tuple-element.33) | copy-start | bytes 52
  80.7 2.2 %copy-start.15 = (f32[512]{0:T(512)S(1)}, f32[512]{0:T(512)}, u32[]{:S(2)}) copy-start(f32[512]{0:T(512)} %param.13) | copy-start | bytes 6148
  83.1 9.4 %copy-start.23 = (pred[4]{0:T(512)(128)(4,1)S(1)}, pred[4]{0:T(512)(128)(4,1)}, u32[]{:S(2)}) copy-start(pred[4]{0:T(512)(128)(4,1)} %copy-done.22) | copy-start | bytes 16
  83.4 4.7 %collective-permute-start.20 = (bf16[32,512]{1,0:T(8,128)(2,1)S(1)}, bf16[32,512]{1,0:T(8,128)(2,1)S(1)}, u32[]{:S(2)}, u32[]{:S(2)}) collective-permute-start(bf16[32,512]{1,0:T(8,128)(2,1)S(1)} %copy.80), channel_id=1, source_target_pairs={{0,3},{1,0},{2,1},{3,2},{4,7},{5,4},{6,5},{7,6},{8,11},{9,8},{10,9... | collective-permute-start | bytes 98312 | tf_op jit(solution)/shard_map/ppermute | solution.py:34
  85.5 4.9 %collective-permute-start.19 = (bf16[32,512]{1,0:T(8,128)(2,1)S(1)}, bf16[32,512]{1,0:T(8,128)(2,1)S(1)}, u32[]{:S(2)}, u32[]{:S(2)}) collective-permute-start(bf16[32,512]{1,0:T(8,128)(2,1)S(1)} %copy.79), channel_id=1, source_target_pairs={{0,2},{1,3},{2,0},{3,1},{4,6},{5,7},{6,4},{7,5},{8,10},{9,11},{10,... | collective-permute-start | bytes 98312 | tf_op jit(solution)/shard_map/ppermute | solution.py:34
  86.0 5.8 %collective-permute-start.18 = (bf16[32,512]{1,0:T(8,128)(2,1)S(1)}, bf16[32,512]{1,0:T(8,128)(2,1)S(1)}, u32[]{:S(2)}, u32[]{:S(2)}) collective-permute-start(bf16[32,512]{1,0:T(8,128)(2,1)S(1)} %copy.78), channel_id=1, source_target_pairs={{0,1},{1,2},{2,3},{3,0},{4,5},{5,6},{6,7},{7,4},{8,9},{9,10},{10,1... | collective-permute-start | bytes 98312 | tf_op jit(solution)/shard_map/ppermute | solution.py:34

commit v11 on v9

--- a/solution.py
+++ b/solution.py
@@ -38,11 +38,15 @@
 def gathered(shard, axis):
     peers = lax.axis_size(axis)
     place = lax.axis_index(axis)
-    if peers & (peers - 1):
+    if peers & (peers - 1) or peers < 4:
         return lax.all_gather(shard, axis, axis=0, tiled=False)
     bits = peers.bit_length() - 1
-    held = shard[None]
-    for level in reversed(range(bits)):
+    received = [shard] + [
+        lax.ppermute(shard, axis, [(i, i ^ flip) for i in range(peers)]) for flip in range(1, 4)
+    ]
+    order = (place & 3) ^ jnp.arange(4, dtype=jnp.int32)
+    held = jnp.take(jnp.stack(received), order, axis=0)
+    for level in reversed(range(2, bits)):
         bit = 1 << level
         incoming = lax.ppermute(held, axis, [(i, i ^ bit) for i in range(peers)])
         upper = (place & bit) != 0
@@ -51,8 +55,11 @@
             jnp.concatenate([incoming, held], axis=0),
             jnp.concatenate([held, incoming], axis=0),
         )
-    held = held.reshape((2,) * bits + shard.shape)
-    return jnp.transpose(held, tuple(reversed(range(bits))) + tuple(range(bits, held.ndim)))
+    held = held.reshape((2,) * (bits - 2) + (4,) + shard.shape)
+    low_first = tuple(reversed(range(bits - 2))) + (bits - 2,)
+    return jnp.transpose(held, low_first + tuple(range(bits - 1, held.ndim))).reshape(
+        (peers,) + shard.shape
+    )
 
 
 def logits_kernel(taps_ref, query_ref, keys_ref, out_ref, high_ref, low_ref, conv_ref):

time: 72.4 us -> 84.9 us (1.17)
  waiting for transfers between devices: 16.3 us -> 28.7 us
  other arithmetic: 8.36 us -> 9.71 us
  local copies, waits for them, and re-layouts: 12.9 us -> 12 us
    ppermute x6 -> x2, waiting for transfers between devices: 9.5 us -> 18.6 us  [gathered(): incoming = lax.ppermute(held, axis, [(i, i ^ bit) for i in range(peers)])]
    ppermute x0 -> x6, starting transfers between devices: none -> 3.85 us  [gathered(): lax.ppermute(shard, axis, [(i, i ^ flip) for i in range(peers)])]
    ppermute x6 -> x2, starting transfers between devices: 7.42 us -> 3.98 us  [gathered(): incoming = lax.ppermute(held, axis, [(i, i ^ bit) for i in range(peers)])]
    ppermute x0 -> x6, waiting for transfers between devices: none -> 2.87 us  [gathered(): lax.ppermute(shard, axis, [(i, i ^ flip) for i in range(peers)])]
    ppermute x6, starting transfers between devices: 12.2 us -> 10.6 us  [exchanged(): received.append(lax.ppermute(outgoing, axis, pairs))]
    gather x0 -> x2, local copies, waits for them, and re-layouts: none -> 1.16 us  [gathered(): held = jnp.take(jnp.stack(received), order, axis=0)]
    transpose x2 -> x0, local copies, waits for them, and re-layouts: 1.04 us -> none  [gathered(): jnp.transpose(held, tuple(reversed(range(bits))) + tuple(range(bits, held...]
  transfers between devices with their start and end apart: 13 -> 15, of which waited for: 9 -> 7; matrix products, arithmetic and copies ran while one was open for 17% -> 18% of each run, Pallas kernels for 15% -> 13%
where the time goes in v11:
time: 84.9 us; the launch traced here: 84.5 us
  waiting for transfers between devices  28.7 us (34%)
  starting transfers between devices  20.5 us (24%)
  local copies, waits for them, and re-layouts  12 us (14%)
  Pallas kernels  10.9 us (13%)
  other arithmetic  9.71 us (11%)
  matrix products  2.17 us (3%)
    ppermute x2, waiting for transfers between devices, gathered(): incoming = lax.ppermute(held, axis, [(i, i ^ bit) for i in range(peers)])  18.6 us
    pallas_call x1, Pallas kernels, conv_logits(): pl.pallas_call(logits_kernel, grid=(heads, seq_len // span), in_specs=[pl...  10.9 us
    ppermute x6, starting transfers between devices, exchanged(): received.append(lax.ppermute(outgoing, axis, pairs))  10.6 us
    ppermute x6, waiting for transfers between devices, exchanged(): received.append(lax.ppermute(outgoing, axis, pairs))  6.55 us
    ppermute x2, starting transfers between devices, gathered(): incoming = lax.ppermute(held, axis, [(i, i ^ bit) for i in range(peers)])  3.98 us
    ppermute x6, starting transfers between devices, gathered(): lax.ppermute(shard, axis, [(i, i ^ flip) for i in range(peers)])  3.85 us
    div x1, other arithmetic, attend_chunk(): probabilities = expd / jnp.sum(expd, axis=1, keepdims=True)  3.74 us
    ppermute x6, waiting for transfers between devices, gathered(): lax.ppermute(shard, axis, [(i, i ^ flip) for i in range(peers)])  2.87 us
  transfers between devices with their start and end apart: 15, of which 7 were waited for; matrix products, arithmetic and copies ran while one was open for 18% of the time, Pallas kernels for 13%

profile of v11, /device:TPU:0, one launch (start us, length us, event | category | flops | bytes accessed | tf_op | source)
XLA Modules:
  0.0 84.5 jit_solution(14517357993134212244)
XLA Ops:
  0.0 1.1 %pad_maximum_fusion.2 = bf16[3,32,2048]{2,1,0:T(8,128)(2,1)S(1)} fusion(bf16[1,32,2048]{2,1,0:T(8,128)(2,1)} %bitcast.92, bf16[1,32,2048]{2,1,0:T(8,128)(2,1)} %bitcast.93, bf16[1,32,2048]{2,1,0:T(8,128)(2,1)} %bitcast.94), kind=kLoop, calls=%fused_computation.45 | loop fusion | flops 393216 | bytes 786432 | tf_op jit(solution)/shard_map/stack | solution.py:204
  1.1 5.1 %collective-permute-start.2 = (bf16[3,32,512]{2,1,0:T(8,128)(2,1)S(1)}, bf16[3,32,512]{2,1,0:T(8,128)(2,1)S(1)}, u32[]{:S(2)}, u32[]{:S(2)}) collective-permute-start(bf16[3,32,512]{2,1,0:T(8,128)(2,1)S(1)} %get-tuple-element.42), channel_id=1, source_target_pairs={{0,3},{1,0},{2,1},{3,2},{4,7},{5,4},{6,5},{7,6},{8,11},{9,8},{10,9... | collective-permute-start | bytes 294920 | tf_op jit(solution)/shard_map/ppermute | solution.py:33
  6.2 1.0 %collective-permute-start = (bf16[3,32,512]{2,1,0:T(8,128)(2,1)S(1)}, bf16[3,32,512]{2,1,0:T(8,128)(2,1)S(1)}, u32[]{:S(2)}, u32[]{:S(2)}) collective-permute-start(bf16[3,32,512]{2,1,0:T(8,128)(2,1)S(1)} %get-tuple-element.44), channel_id=1, source_target_pairs={{0,1},{1,2},{2,3},{3,0},{4,5},{5,6},{6,7},{7,4},{8,9},{9,10},{10,1... | collective-permute-start | bytes 294920 | tf_op jit(solution)/shard_map/ppermute | solution.py:33
  7.3 0.7 broadcast_multiply_fusion
  8.0 1.3 %slice_reduce_fusion.17 = (f32[4]{0:T(128)S(1)}, f32[4]{0:T(128)S(1)}, f32[4]{0:T(128)S(1)}, f32[4]{0:T(128)S(1)}, f32[4]{0:T(128)S(1)}, /*index=5*/f32[4]{0:T(1...) fusion(f32[4,6,11]{2,0,1:T(4,128)} %param.11), kind=kLoop, calls=%fused_computation.140 | loop fusion | bytes 480 | tf_op jit(solution)/shard_map/slice | solution.py:164
  9.4 0.7 reshape.181.taps_ref
  10.1 1.1 %fusion.16 = (pred[1024,128]{1,0:T(8,128)(4,1)S(1)}, pred[1024,128]{1,0:T(8,128)(4,1)S(1)}, pred[1024,128]{1,0:T(8,128)(4,1)S(1)}, pred[1024,128]{1,0:T(8,128)(4...) fusion(s32[128]{0:T(128)S(1)} %iota_add_fusion), kind=kLoop, calls=%fused_computation.42 | loop fusion | flops 917504 | bytes 786944 | tf_op jit(solution)/shard_map/ge | solution.py:180
  11.2 0.8 slice_reduce_fusion.18
  12.1 2.9 %collective-permute-done.1 = bf16[3,32,512]{2,1,0:T(8,128)(2,1)S(1)} collective-permute-done((bf16[3,32,512]{2,1,0:T(8,128)(2,1)S(1)}, bf16[3,32,512]{2,1,0:T(8,128)(2,1)S(1)}, u32[]{:S(2)}, u32[]{:S(2)}) %collective-permute-start.1) | collective-permute-done | bytes 98336 | tf_op jit(solution)/shard_map/ppermute | solution.py:33
  15.1 0.6 gather_fusion
  15.6 0.1 select_bitcast_fusion
  15.8 0.7 collective-permute-start.5
  16.5 0.9 %collective-permute-start.4 = (bf16[128,512]{1,0:T(8,128)(2,1)S(1)}, bf16[128,512]{1,0:T(8,128)(2,1)S(1)}, u32[]{:S(2)}, u32[]{:S(2)}) collective-permute-start(bf16[128,512]{1,0:T(8,128)(2,1)S(1)} %bitcast.89), channel_id=1, source_target_pairs={{0,8},{4,12},{8,0},{12,4},{16,24},{20,28},{24,16},{28,20},{1,9},{5... | collective-permute-start | bytes 393224 | tf_op jit(solution)/shard_map/ppermute | solution.py:45
  17.4 0.3 collective-permute-start.3
  17.7 0.1 copy.66
  17.9 2.1 %collective-permute-start.11 = (bf16[5,512]{1,0:T(8,128)(2,1)S(1)}, bf16[5,512]{1,0:T(8,128)(2,1)S(1)}, u32[]{:S(2)}, u32[]{:S(2)}) collective-permute-start(bf16[5,512]{1,0:T(8,128)(2,1)S(1)} %slice.274), channel_id=1, source_target_pairs={{0,4},{4,8},{8,12},{12,16},{16,20},{20,24},{24,28},{1,5},{5,9},{9,... | collective-permute-start | bytes 15368 | tf_op jit(solution)/shard_map/ppermute | solution.py:23
  20.1 0.8 collective-permute-done.11
  20.8 0.1 pad_maximum_fusion.5
  21.0 0.1 copy.61
  21.1 0.1 copy.62
  21.2 0.1 copy.63
  21.3 0.1 copy.64
  21.5 0.1 copy.65
  21.6 2.9 %collective-permute-done.4 = bf16[128,512]{1,0:T(8,128)(2,1)S(1)} collective-permute-done((bf16[128,512]{1,0:T(8,128)(2,1)S(1)}, bf16[128,512]{1,0:T(8,128)(2,1)S(1)}, u32[]{:S(2)}, u32[]{:S(2)}) %collective-permute-start.4) | collective-permute-done | bytes 131104 | tf_op jit(solution)/shard_map/ppermute | solution.py:45
  24.6 0.6 gather_fusion.2
  25.2 0.1 broadcast_select_fusion
  25.3 2.4 %collective-permute-start.6 = (bf16[4,128,512]{2,1,0:T(8,128)(2,1)S(1)}, bf16[4,128,512]{2,1,0:T(8,128)(2,1)S(1)}, u32[]{:S(2)}, u32[]{:S(2)}) collective-permute-start(bf16[4,128,512]{2,1,0:T(8,128)(2,1)S(1)} %broadcast_select_fusion), channel_id=1, source_target_pairs={{0,16},{4,20},{8,24},{12,28},{16,0},{20,4},{24,8},{28,12},{1,17},{... | collective-permute-start | bytes 1572872 | tf_op jit(solution)/shard_map/ppermute | solution.py:51
  27.8 11.4 %collective-permute-done.6 = bf16[4,128,512]{2,1,0:T(8,128)(2,1)S(1)} collective-permute-done((bf16[4,128,512]{2,1,0:T(8,128)(2,1)S(1)}, bf16[4,128,512]{2,1,0:T(8,128)(2,1)S(1)}, u32[]{:S(2)}, u32[]{:S(2)}) %collective-permute-start.6) | collective-permute-done | bytes 524320 | tf_op jit(solution)/shard_map/ppermute | solution.py:51
  39.2 0.2 maximum_select_fusion
  39.4 1.0 %collective-permute-start.8 = (bf16[128,512]{1,0:T(8,128)(2,1)S(1)}, bf16[128,512]{1,0:T(8,128)(2,1)S(1)}, u32[]{:S(2)}, u32[]{:S(2)}) collective-permute-start(bf16[128,512]{1,0:T(8,128)(2,1)S(1)} %bitcast.85), channel_id=1, source_target_pairs={{0,8},{4,12},{8,0},{12,4},{16,24},{20,28},{24,16},{28,20},{1,9},{5... | collective-permute-start | bytes 393224 | tf_op jit(solution)/shard_map/ppermute | solution.py:45
  40.5 0.8 collective-permute-start.7
  41.3 1.1 %concatenate.33.keys_ref = bf16[1152,512]{1,0:T(8,128)(2,1)} pad(bf16[1024,512]{1,0:T(8,128)(2,1)S(1)} %bitcast.73, bf16[]{:T(256)} %constant.116.clone.1), padding=128_0x0_0 | pad | bytes 2228226 | tf_op jit(solution)/shard_map/concatenate | solution.py:227
  42.4 0.1 fusion.25
  42.5 0.1 fusion.57
  42.6 0.1 slice.249
  42.7 0.1 slice.239
  42.9 0.1 slice.231
  43.0 0.1 slice.225
  43.1 0.1 slice.221
  43.2 0.8 fusion.22
  44.0 0.1 copy.68
  44.4 10.9 %shard_map.64 = f32[4,1024,128]{2,1,0:T(8,128)} custom-call(f32[264]{0:T(512)} %reshape.181.taps_ref, bf16[4,768,128]{2,1,0:T(8,128)(2,1)} %bitcast.78, bf16[1152,512]{1,0:T(8,128)(2,1)} %concatenate.33.keys_ref), custom_call_target="tpu_custom_call" | custom-call | tf_op jit(solution)/shard_map/pallas_call | solution.py:127
  55.3 0.7 subtract_bitcast_fusion.2
  55.9 0.1 fusion.45
  56.2 0.6 gather_fusion.3
  56.8 0.1 broadcast_select_fusion.1
  56.9 1.6 %collective-permute-start.10 = (bf16[4,128,512]{2,1,0:T(8,128)(2,1)S(1)}, bf16[4,128,512]{2,1,0:T(8,128)(2,1)S(1)}, u32[]{:S(2)}, u32[]{:S(2)}) collective-permute-start(bf16[4,128,512]{2,1,0:T(8,128)(2,1)S(1)} %broadcast_select_fusion.1), channel_id=1, source_target_pairs={{0,16},{4,20},{8,24},{12,28},{16,0},{20,4},{24,8},{28,12},{1,17},{... | collective-permute-start | bytes 1572872 | tf_op jit(solution)/shard_map/ppermute | solution.py:51
  58.5 3.7 %divide_bitcast_fusion = f32[1,4,1024,128]{3,2,1,0:T(8,128)S(1)} fusion(f32[4,1024,128]{2,1,0:T(8,128)} %shard_map.64, f32[4,128]{1,0:T(4,128)} %get-tuple-element.61, f32[4,128]{1,0:T(4,128)} %get-tuple-element.60, f32[4,128]{1,0:T(4,128)} %get-tuple-element.59, f32[4,128]{1,0:T(4,128)S(1)} %subtract_bitcast_fusion.3, f32[4,128]{1,0:T(4,128)S(1)} %fusion.45, ...), kind=kOutput, calls=%fused_computation.7 | output fusion | flops 6818814 | bytes 4990976 | tf_op jit(solution)/shard_map/div | solution.py:183
  62.3 1.4 %slice_bitcast_fusion.3 = (f32[1024,128]{1,0:T(8,128)}, f32[1024,128]{1,0:T(8,128)}, f32[1024,128]{1,0:T(8,128)}, f32[1024,128]{1,0:T(8,128)}) fusion(f32[1,4,1024,128]{3,2,1,0:T(8,128)S(1)} %divide_bitcast_fusion), kind=kLoop, calls=%fused_computation.33 | loop fusion | bytes 4194304 | tf_op jit(solution)/shard_map/mul | solution.py:188
  63.7 7.2 %collective-permute-done.10 = bf16[4,128,512]{2,1,0:T(8,128)(2,1)S(1)} collective-permute-done((bf16[4,128,512]{2,1,0:T(8,128)(2,1)S(1)}, bf16[4,128,512]{2,1,0:T(8,128)(2,1)S(1)}, u32[]{:S(2)}, u32[]{:S(2)}) %collective-permute-start.10) | collective-permute-done | bytes 524320 | tf_op jit(solution)/shard_map/ppermute | solution.py:51
  70.9 0.2 maximum_select_fusion.1
  71.0 0.3 reshape.224
  71.4 0.7 copy-done.1
  72.1 0.2 copy-done.2
  72.2 2.2 %multiply_reduce_fusion = (f32[128,4]{0,1:T(4,128)S(1)}, f32[128,4,128]{0,2,1:T(8,128)S(1)}) fusion(f32[1024,128]{1,0:T(8,128)S(1)} %copy-done.2, f32[4]{0:T(128)S(1)} %copy-done.6, f32[1024,128]{1,0:T(8,128)} %get-tuple-element.36, f32[4]{0:T(128)S(1)} %copy-done.7, f32[1024,128]{1,0:T(8,128)} %get-tuple-element.37, f32[4]{0:T(128)S(1)} %copy-done.8, ...), kind=kOutput, calls=%fused_computation.59 | convolution fusion | flops 138542592 | bytes 3409984 | tf_op jit(solution)/shard_map/hki,khd->ihd/dot_general | solution.py:190
  74.4 0.1 multiply_convert_fusion
  74.6 0.2 constant_dynamic-slice_fusion.3
  74.9 2.0 %collective-permute-start.14 = (bf16[32,512]{1,0:T(8,128)(2,1)S(1)}, bf16[32,512]{1,0:T(8,128)(2,1)S(1)}, u32[]{:S(2)}, u32[]{:S(2)}) collective-permute-start(bf16[32,512]{1,0:T(8,128)(2,1)S(1)} %copy.80), channel_id=1, source_target_pairs={{0,3},{1,0},{2,1},{3,2},{4,7},{5,4},{6,5},{7,6},{8,11},{9,8},{10,9... | collective-permute-start | bytes 98312 | tf_op jit(solution)/shard_map/ppermute | solution.py:33
  76.9 0.4 collective-permute-start.13
  77.4 2.1 %collective-permute-start.12 = (bf16[32,512]{1,0:T(8,128)(2,1)S(1)}, bf16[32,512]{1,0:T(8,128)(2,1)S(1)}, u32[]{:S(2)}, u32[]{:S(2)}) collective-permute-start(bf16[32,512]{1,0:T(8,128)(2,1)S(1)} %copy.78), channel_id=1, source_target_pairs={{0,1},{1,2},{2,3},{3,0},{4,5},{5,6},{6,7},{7,4},{8,9},{9,10},{10,1... | collective-permute-start | bytes 98312 | tf_op jit(solution)/shard_map/ppermute | solution.py:33
  79.6 2.2 %collective-permute-done.13 = bf16[32,512]{1,0:T(8,128)(2,1)S(1)} collective-permute-done((bf16[32,512]{1,0:T(8,128)(2,1)S(1)}, bf16[32,512]{1,0:T(8,128)(2,1)S(1)}, u32[]{:S(2)}, u32[]{:S(2)}) %collective-permute-start.13) | collective-permute-done | bytes 32800 | tf_op jit(solution)/shard_map/ppermute | solution.py:33
  81.8 1.4 %collective-permute-done.12 = bf16[32,512]{1,0:T(8,128)(2,1)S(1)} collective-permute-done((bf16[32,512]{1,0:T(8,128)(2,1)S(1)}, bf16[32,512]{1,0:T(8,128)(2,1)S(1)}, u32[]{:S(2)}, u32[]{:S(2)}) %collective-permute-start.12) | collective-permute-done | bytes 32800 | tf_op jit(solution)/shard_map/ppermute | solution.py:33
  83.2 0.6 gather_fusion.1
  83.9 0.7 copy.82
  (66 shorter events, 1.5 us)
Async XLA Ops:
  0.0 11.2 %copy-start.3 = (f32[4,4]{1,0:T(4,128)S(1)}, f32[4,4]{1,0:T(4,128)}, u32[]{:S(2)}) copy-start(f32[4,4]{1,0:T(4,128)} %param.12) | copy-start | bytes 196
  1.1 10.9 %collective-permute-start.2 = (bf16[3,32,512]{2,1,0:T(8,128)(2,1)S(1)}, bf16[3,32,512]{2,1,0:T(8,128)(2,1)S(1)}, u32[]{:S(2)}, u32[]{:S(2)}) collective-permute-start(bf16[3,32,512]{2,1,0:T(8,128)(2,1)S(1)} %get-tuple-element.42), channel_id=1, source_target_pairs={{0,3},{1,0},{2,1},{3,2},{4,7},{5,4},{6,5},{7,6},{8,11},{9,8},{10,9... | collective-permute-start | bytes 294920 | tf_op jit(solution)/shard_map/ppermute | solution.py:33
  6.2 8.7 %collective-permute-start.1 = (bf16[3,32,512]{2,1,0:T(8,128)(2,1)S(1)}, bf16[3,32,512]{2,1,0:T(8,128)(2,1)S(1)}, u32[]{:S(2)}, u32[]{:S(2)}) collective-permute-start(bf16[3,32,512]{2,1,0:T(8,128)(2,1)S(1)} %get-tuple-element.43), channel_id=1, source_target_pairs={{0,2},{1,3},{2,0},{3,1},{4,6},{5,7},{6,4},{7,5},{8,10},{9,11},{10,... | collective-permute-start | bytes 294920 | tf_op jit(solution)/shard_map/ppermute | solution.py:33
  6.2 8.7 %collective-permute-start = (bf16[3,32,512]{2,1,0:T(8,128)(2,1)S(1)}, bf16[3,32,512]{2,1,0:T(8,128)(2,1)S(1)}, u32[]{:S(2)}, u32[]{:S(2)}) collective-permute-start(bf16[3,32,512]{2,1,0:T(8,128)(2,1)S(1)} %get-tuple-element.44), channel_id=1, source_target_pairs={{0,1},{1,2},{2,3},{3,0},{4,5},{5,6},{6,7},{7,4},{8,9},{9,10},{10,1... | collective-permute-start | bytes 294920 | tf_op jit(solution)/shard_map/ppermute | solution.py:33
  15.8 5.9 %collective-permute-start.5 = (bf16[128,512]{1,0:T(8,128)(2,1)S(1)}, bf16[128,512]{1,0:T(8,128)(2,1)S(1)}, u32[]{:S(2)}, u32[]{:S(2)}) collective-permute-start(bf16[128,512]{1,0:T(8,128)(2,1)S(1)} %bitcast.88), channel_id=1, source_target_pairs={{0,12},{4,8},{8,4},{12,0},{16,28},{20,24},{24,20},{28,16},{1,13},{... | collective-permute-start | bytes 393224 | tf_op jit(solution)/shard_map/ppermute | solution.py:45
  16.5 8.0 %collective-permute-start.4 = (bf16[128,512]{1,0:T(8,128)(2,1)S(1)}, bf16[128,512]{1,0:T(8,128)(2,1)S(1)}, u32[]{:S(2)}, u32[]{:S(2)}) collective-permute-start(bf16[128,512]{1,0:T(8,128)(2,1)S(1)} %bitcast.89), channel_id=1, source_target_pairs={{0,8},{4,12},{8,0},{12,4},{16,24},{20,28},{24,16},{28,20},{1,9},{5... | collective-permute-start | bytes 393224 | tf_op jit(solution)/shard_map/ppermute | solution.py:45
  17.4 7.1 %collective-permute-start.3 = (bf16[128,512]{1,0:T(8,128)(2,1)S(1)}, bf16[128,512]{1,0:T(8,128)(2,1)S(1)}, u32[]{:S(2)}, u32[]{:S(2)}) collective-permute-start(bf16[128,512]{1,0:T(8,128)(2,1)S(1)} %bitcast.90), channel_id=1, source_target_pairs={{0,4},{4,0},{8,12},{12,8},{16,20},{20,16},{24,28},{28,24},{1,5},{5... | collective-permute-start | bytes 393224 | tf_op jit(solution)/shard_map/ppermute | solution.py:45
  17.9 2.9 %collective-permute-start.11 = (bf16[5,512]{1,0:T(8,128)(2,1)S(1)}, bf16[5,512]{1,0:T(8,128)(2,1)S(1)}, u32[]{:S(2)}, u32[]{:S(2)}) collective-permute-start(bf16[5,512]{1,0:T(8,128)(2,1)S(1)} %slice.274), channel_id=1, source_target_pairs={{0,4},{4,8},{8,12},{12,16},{16,20},{20,24},{24,28},{1,5},{5,9},{9,... | collective-permute-start | bytes 15368 | tf_op jit(solution)/shard_map/ppermute | solution.py:23
  25.3 13.9 %collective-permute-start.6 = (bf16[4,128,512]{2,1,0:T(8,128)(2,1)S(1)}, bf16[4,128,512]{2,1,0:T(8,128)(2,1)S(1)}, u32[]{:S(2)}, u32[]{:S(2)}) collective-permute-start(bf16[4,128,512]{2,1,0:T(8,128)(2,1)S(1)} %broadcast_select_fusion), channel_id=1, source_target_pairs={{0,16},{4,20},{8,24},{12,28},{16,0},{20,4},{24,8},{28,12},{1,17},{... | collective-permute-start | bytes 1572872 | tf_op jit(solution)/shard_map/ppermute | solution.py:51
  27.8 14.6 %copy-start = (bf16[128,4,6,128]{0,3,2,1:T(8,128)(2,1)}, bf16[128,4,6,128]{0,3,2,1:T(8,128)(2,1)S(1)}, u32[]{:S(2)}) copy-start(bf16[128,4,6,128]{0,3,2,1:T(8,128)(2,1)S(1)} %constant_dynamic-update-slice_fusion) | copy-start | bytes 2359300
  39.4 16.8 %collective-permute-start.9 = (bf16[128,512]{1,0:T(8,128)(2,1)S(1)}, bf16[128,512]{1,0:T(8,128)(2,1)S(1)}, u32[]{:S(2)}, u32[]{:S(2)}) collective-permute-start(bf16[128,512]{1,0:T(8,128)(2,1)S(1)} %bitcast.84), channel_id=1, source_target_pairs={{0,12},{4,8},{8,4},{12,0},{16,28},{20,24},{24,20},{28,16},{1,13},{... | collective-permute-start | bytes 393224 | tf_op jit(solution)/shard_map/ppermute | solution.py:45
  39.4 16.7 %collective-permute-start.8 = (bf16[128,512]{1,0:T(8,128)(2,1)S(1)}, bf16[128,512]{1,0:T(8,128)(2,1)S(1)}, u32[]{:S(2)}, u32[]{:S(2)}) collective-permute-start(bf16[128,512]{1,0:T(8,128)(2,1)S(1)} %bitcast.85), channel_id=1, source_target_pairs={{0,8},{4,12},{8,0},{12,4},{16,24},{20,28},{24,16},{28,20},{1,9},{5... | collective-permute-start | bytes 393224 | tf_op jit(solution)/shard_map/ppermute | solution.py:45
  40.5 15.7 %collective-permute-start.7 = (bf16[128,512]{1,0:T(8,128)(2,1)S(1)}, bf16[128,512]{1,0:T(8,128)(2,1)S(1)}, u32[]{:S(2)}, u32[]{:S(2)}) collective-permute-start(bf16[128,512]{1,0:T(8,128)(2,1)S(1)} %bitcast.86), channel_id=1, source_target_pairs={{0,4},{4,0},{8,12},{12,8},{16,20},{20,16},{24,28},{28,24},{1,5},{5... | collective-permute-start | bytes 393224 | tf_op jit(solution)/shard_map/ppermute | solution.py:45
  56.9 13.9 %collective-permute-start.10 = (bf16[4,128,512]{2,1,0:T(8,128)(2,1)S(1)}, bf16[4,128,512]{2,1,0:T(8,128)(2,1)S(1)}, u32[]{:S(2)}, u32[]{:S(2)}) collective-permute-start(bf16[4,128,512]{2,1,0:T(8,128)(2,1)S(1)} %broadcast_select_fusion.1), channel_id=1, source_target_pairs={{0,16},{4,20},{8,24},{12,28},{16,0},{20,4},{24,8},{28,12},{1,17},{... | collective-permute-start | bytes 1572872 | tf_op jit(solution)/shard_map/ppermute | solution.py:51
  63.7 7.7 %copy-start.5 = (f32[4]{0:T(128)S(1)}, f32[4]{0:T(128)}, u32[]{:S(2)}) copy-start(f32[4]{0:T(128)} %get-tuple-element.30) | copy-start | bytes 52
  63.7 7.7 %copy-start.6 = (f32[4]{0:T(128)S(1)}, f32[4]{0:T(128)}, u32[]{:S(2)}) copy-start(f32[4]{0:T(128)} %get-tuple-element.31) | copy-start | bytes 52
  63.7 7.7 %copy-start.7 = (f32[4]{0:T(128)S(1)}, f32[4]{0:T(128)}, u32[]{:S(2)}) copy-start(f32[4]{0:T(128)} %get-tuple-element.32) | copy-start | bytes 52
  63.7 7.7 %copy-start.8 = (f32[4]{0:T(128)S(1)}, f32[4]{0:T(128)}, u32[]{:S(2)}) copy-start(f32[4]{0:T(128)} %get-tuple-element.33) | copy-start | bytes 52
  71.0 1.0 %copy-start.1 = (f32[1024,128]{1,0:T(8,128)S(1)}, f32[1024,128]{1,0:T(8,128)}, u32[]{:S(2)}) copy-start(f32[1024,128]{1,0:T(8,128)} %get-tuple-element.34) | copy-start | bytes 1572868
  71.0 1.2 %copy-start.2 = (f32[1024,128]{1,0:T(8,128)S(1)}, f32[1024,128]{1,0:T(8,128)}, u32[]{:S(2)}) copy-start(f32[1024,128]{1,0:T(8,128)} %get-tuple-element.35) | copy-start | bytes 1572868
  72.2 2.2 %copy-start.4 = (f32[512]{0:T(512)S(1)}, f32[512]{0:T(512)}, u32[]{:S(2)}) copy-start(f32[512]{0:T(512)} %param.13) | copy-start | bytes 6148
  74.9 4.7 %collective-permute-start.14 = (bf16[32,512]{1,0:T(8,128)(2,1)S(1)}, bf16[32,512]{1,0:T(8,128)(2,1)S(1)}, u32[]{:S(2)}, u32[]{:S(2)}) collective-permute-start(bf16[32,512]{1,0:T(8,128)(2,1)S(1)} %copy.80), channel_id=1, source_target_pairs={{0,3},{1,0},{2,1},{3,2},{4,7},{5,4},{6,5},{7,6},{8,11},{9,8},{10,9... | collective-permute-start | bytes 98312 | tf_op jit(solution)/shard_map/ppermute | solution.py:33
  76.9 4.9 %collective-permute-start.13 = (bf16[32,512]{1,0:T(8,128)(2,1)S(1)}, bf16[32,512]{1,0:T(8,128)(2,1)S(1)}, u32[]{:S(2)}, u32[]{:S(2)}) collective-permute-start(bf16[32,512]{1,0:T(8,128)(2,1)S(1)} %copy.79), channel_id=1, source_target_pairs={{0,2},{1,3},{2,0},{3,1},{4,6},{5,7},{6,4},{7,5},{8,10},{9,11},{10,... | collective-permute-start | bytes 98312 | tf_op jit(solution)/shard_map/ppermute | solution.py:33
  77.4 5.8 %collective-permute-start.12 = (bf16[32,512]{1,0:T(8,128)(2,1)S(1)}, bf16[32,512]{1,0:T(8,128)(2,1)S(1)}, u32[]{:S(2)}, u32[]{:S(2)}) collective-permute-start(bf16[32,512]{1,0:T(8,128)(2,1)S(1)} %copy.78), channel_id=1, source_target_pairs={{0,1},{1,2},{2,3},{3,0},{4,5},{5,6},{6,7},{7,4},{8,9},{9,10},{10,1... | collective-permute-start | bytes 98312 | tf_op jit(solution)/shard_map/ppermute | solution.py:33

commit v12 on v8

--- a/solution.py
+++ b/solution.py
@@ -213,8 +213,10 @@
     query_first = ctx_place * shard_rows
     earlier = passed_along(query_local[shard_rows - row_lead :], "ctx", 1)
     query_ext = jnp.concatenate([earlier, query_local], axis=0)
-    key_all = gathered(key_local, "ctx").reshape((-1, width))
-    value_all = gathered(value_local, "ctx").reshape((-1, width))
+    both = gathered(jnp.stack([key_local, value_local]), "ctx")
+    both = both.reshape((-1,) + both.shape[-3:])
+    key_all = both[:, 0].reshape((-1, width))
+    value_all = both[:, 1].reshape((-1, width))
     seq_len = key_all.shape[0]
     key_pad = jnp.concatenate(
         [jnp.zeros((KEY_BLOCK, width), key_all.dtype), key_all], axis=0

time: 74.6 us -> 81.7 us (1.095)
  waiting for transfers between devices: 18.7 us -> 23.4 us
  local copies, waits for them, and re-layouts: 13.3 us -> 16.4 us
  starting transfers between devices: 18.9 us -> 18 us
    ppermute x6, waiting for transfers between devices: 4.52 us -> 7.93 us  [exchanged(): received.append(lax.ppermute(outgoing, axis, pairs))]
    unnamed x65 -> x63, local copies, waits for them, and re-layouts: 0.98 us -> 3.96 us
    slice x5, local copies, waits for them, and re-layouts: 0.6 us -> 2.78 us  [shards(): query_heads[row_lead - lag:row_lead - lag + shard_rows]]
    ppermute x6 -> x3, starting transfers between devices: 5.33 us -> 3.21 us  [gathered(): incoming = lax.ppermute(held, axis, [(i, i ^ bit) for i in range(peers)])]
    ppermute x6 -> x3, waiting for transfers between devices: 14.2 us -> 15.5 us  [gathered(): incoming = lax.ppermute(held, axis, [(i, i ^ bit) for i in range(peers)])]
    transpose x2 -> x0, local copies, waits for them, and re-layouts: 1.01 us -> none  [gathered(): jnp.transpose(held, tuple(reversed(range(bits))) + tuple(range(bits, held...]
    slice x1, local copies, waits for them, and re-layouts: 1.89 us -> 0.94 us  [band_terms(): score_kernel[None, :, row_lag, col_lag]]
    ppermute x1, starting transfers between devices: 1.51 us -> 2.4 us  [passed_along(): return lax.ppermute(shard, axis, pairs)]
  transfers between devices with their start and end apart: 13 -> 10, of which waited for: 6 -> 6; matrix products, arithmetic and copies ran while one was open for 22% -> 13% of each run, Pallas kernels for 15% -> 0%
where the time goes in v12:
time: 81.7 us; the launch traced here: 80.7 us
  waiting for transfers between devices  23.4 us (29%)
  starting transfers between devices  18 us (22%)
  local copies, waits for them, and re-layouts  16.4 us (20%)
  Pallas kernels  10.9 us (13%)
  other arithmetic  9.17 us (11%)
  matrix products  2.17 us (3%)
    ppermute x3, waiting for transfers between devices, gathered(): incoming = lax.ppermute(held, axis, [(i, i ^ bit) for i in range(peers)])  15.5 us
    ppermute x6, starting transfers between devices, exchanged(): received.append(lax.ppermute(outgoing, axis, pairs))  12.4 us
    pallas_call x1, Pallas kernels, conv_logits(): pl.pallas_call(logits_kernel, grid=(heads, seq_len // span), in_specs=[pl...  10.9 us
    ppermute x6, waiting for transfers between devices, exchanged(): received.append(lax.ppermute(outgoing, axis, pairs))  7.93 us
    unnamed x63, local copies, waits for them, and re-layouts  3.96 us
    div x1, other arithmetic, attend_chunk(): probabilities = expd / jnp.sum(expd, axis=1, keepdims=True)  3.88 us
    ppermute x3, starting transfers between devices, gathered(): incoming = lax.ppermute(held, axis, [(i, i ^ bit) for i in range(peers)])  3.21 us
    slice x5, local copies, waits for them, and re-layouts, shards(): query_heads[row_lead - lag:row_lead - lag + shard_rows]  2.78 us
  transfers between devices with their start and end apart: 10, of which 6 were waited for; matrix products, arithmetic and copies ran while one was open for 13% of the time, Pallas kernels for 0%

profile of v12, /device:TPU:0, one launch (start us, length us, event | category | flops | bytes accessed | tf_op | source)
XLA Modules:
  0.0 80.7 jit_solution(8029632211462670442)
XLA Ops:
  0.0 1.1 %pad_maximum_fusion = bf16[3,32,2048]{2,1,0:T(8,128)(2,1)S(1)} fusion(bf16[1,32,2048]{2,1,0:T(8,128)(2,1)} %bitcast.90, bf16[1,32,2048]{2,1,0:T(8,128)(2,1)} %bitcast.91, bf16[1,32,2048]{2,1,0:T(8,128)(2,1)} %bitcast.92), kind=kLoop, calls=%fused_computation.40 | loop fusion | flops 393216 | bytes 786432 | tf_op jit(solution)/shard_map/stack | solution.py:197
  1.1 3.1 %collective-permute-start = (bf16[3,32,512]{2,1,0:T(8,128)(2,1)S(1)}, bf16[3,32,512]{2,1,0:T(8,128)(2,1)S(1)}, u32[]{:S(2)}, u32[]{:S(2)}) collective-permute-start(bf16[3,32,512]{2,1,0:T(8,128)(2,1)S(1)} %get-tuple-element.41), channel_id=1, source_target_pairs={{0,1},{1,2},{2,3},{3,0},{4,5},{5,6},{6,7},{7,4},{8,9},{9,10},{10,1... | collective-permute-start | bytes 294920 | tf_op jit(solution)/shard_map/ppermute | solution.py:33
  4.2 2.6 %collective-permute-start.1 = (bf16[3,32,512]{2,1,0:T(8,128)(2,1)S(1)}, bf16[3,32,512]{2,1,0:T(8,128)(2,1)S(1)}, u32[]{:S(2)}, u32[]{:S(2)}) collective-permute-start(bf16[3,32,512]{2,1,0:T(8,128)(2,1)S(1)} %get-tuple-element.40), channel_id=1, source_target_pairs={{0,2},{1,3},{2,0},{3,1},{4,6},{5,7},{6,4},{7,5},{8,10},{9,11},{10,... | collective-permute-start | bytes 294920 | tf_op jit(solution)/shard_map/ppermute | solution.py:33
  6.8 1.3 %collective-permute-start.2 = (bf16[3,32,512]{2,1,0:T(8,128)(2,1)S(1)}, bf16[3,32,512]{2,1,0:T(8,128)(2,1)S(1)}, u32[]{:S(2)}, u32[]{:S(2)}) collective-permute-start(bf16[3,32,512]{2,1,0:T(8,128)(2,1)S(1)} %get-tuple-element.39), channel_id=1, source_target_pairs={{0,3},{1,0},{2,1},{3,2},{4,7},{5,4},{6,5},{7,6},{8,11},{9,8},{10,9... | collective-permute-start | bytes 294920 | tf_op jit(solution)/shard_map/ppermute | solution.py:33
  8.2 1.7 %collective-permute-done = bf16[3,32,512]{2,1,0:T(8,128)(2,1)S(1)} collective-permute-done((bf16[3,32,512]{2,1,0:T(8,128)(2,1)S(1)}, bf16[3,32,512]{2,1,0:T(8,128)(2,1)S(1)}, u32[]{:S(2)}, u32[]{:S(2)}) %collective-permute-start) | collective-permute-done | bytes 98336 | tf_op jit(solution)/shard_map/ppermute | solution.py:33
  9.9 3.5 %collective-permute-done.1 = bf16[3,32,512]{2,1,0:T(8,128)(2,1)S(1)} collective-permute-done((bf16[3,32,512]{2,1,0:T(8,128)(2,1)S(1)}, bf16[3,32,512]{2,1,0:T(8,128)(2,1)S(1)}, u32[]{:S(2)}, u32[]{:S(2)}) %collective-permute-start.1) | collective-permute-done | bytes 98336 | tf_op jit(solution)/shard_map/ppermute | solution.py:33
  13.5 0.6 gather_fusion
  14.1 0.1 select_bitcast_fusion
  14.3 1.6 %collective-permute-start.3 = (bf16[1,2,128,512]{3,2,1,0:T(8,128)(2,1)S(1)}, bf16[1,2,128,512]{3,2,1,0:T(8,128)(2,1)S(1)}, u32[]{:S(2)}, u32[]{:S(2)}) collective-permute-start(bf16[1,2,128,512]{3,2,1,0:T(8,128)(2,1)S(1)} %maximum_bitcast_fusion), channel_id=1, source_target_pairs={{0,16},{4,20},{8,24},{12,28},{16,0},{20,4},{24,8},{28,12},{1,17},{... | collective-permute-start | bytes 786440 | tf_op jit(solution)/shard_map/ppermute | solution.py:47
  15.8 6.6 %collective-permute-done.3 = bf16[1,2,128,512]{3,2,1,0:T(8,128)(2,1)S(1)} collective-permute-done((bf16[1,2,128,512]{3,2,1,0:T(8,128)(2,1)S(1)}, bf16[1,2,128,512]{3,2,1,0:T(8,128)(2,1)S(1)}, u32[]{:S(2)}, u32[]{:S(2)}) %collective-permute-start.3) | collective-permute-done | bytes 262176 | tf_op jit(solution)/shard_map/ppermute | solution.py:47
  22.5 1.6 %collective-permute-start.4 = (bf16[2,2,128,512]{3,2,1,0:T(8,128)(2,1)S(1)}, bf16[2,2,128,512]{3,2,1,0:T(8,128)(2,1)S(1)}, u32[]{:S(2)}, u32[]{:S(2)}) collective-permute-start(bf16[2,2,128,512]{3,2,1,0:T(8,128)(2,1)S(1)} %maximum_select_fusion.2), channel_id=1, source_target_pairs={{0,8},{4,12},{8,0},{12,4},{16,24},{20,28},{24,16},{28,20},{1,9},{5... | collective-permute-start | bytes 1572872 | tf_op jit(solution)/shard_map/ppermute | solution.py:47
  24.1 0.7 reshape.175.taps_ref
  24.8 0.8 %slice_reduce_fusion.18 = (f32[4]{0:T(128)}, f32[4]{0:T(128)}, f32[4]{0:T(128)}, f32[4]{0:T(128)}) fusion(f32[1,4,4]{2,1,0:T(4,128)S(1)} %bitcast.97), kind=kLoop, calls=%fused_computation.135 | loop fusion | bytes 128 | tf_op jit(solution)/shard_map/slice | solution.py:181
  25.6 0.9 %slice_reduce_fusion.17 = (f32[4]{0:T(128)}, f32[4]{0:T(128)S(1)}, f32[4]{0:T(128)S(1)}, f32[4]{0:T(128)}, f32[4]{0:T(128)}, /*index=5*/f32[4]{0:T(128)}, f32[4]...) fusion(f32[4,6,11]{2,0,1:T(4,128)S(1)} %copy-done.4), kind=kLoop, calls=%fused_computation.134 | loop fusion | bytes 480 | tf_op jit(solution)/shard_map/slice | solution.py:157
  26.5 8.9 %collective-permute-done.4 = bf16[2,2,128,512]{3,2,1,0:T(8,128)(2,1)S(1)} collective-permute-done((bf16[2,2,128,512]{3,2,1,0:T(8,128)(2,1)S(1)}, bf16[2,2,128,512]{3,2,1,0:T(8,128)(2,1)S(1)}, u32[]{:S(2)}, u32[]{:S(2)}) %collective-permute-start.4) | collective-permute-done | bytes 524320 | tf_op jit(solution)/shard_map/ppermute | solution.py:47
  35.4 0.2 maximum_select_fusion.1
  35.7 1.3 %fusion.16 = (pred[1024,128]{1,0:T(8,128)(4,1)}, pred[1024,128]{1,0:T(8,128)(4,1)}, pred[1024,128]{1,0:T(8,128)(4,1)}, pred[1024,128]{1,0:T(8,128)(4,1)}, pred[1...) fusion(s32[128]{0:T(128)S(1)} %iota_add_fusion), kind=kLoop, calls=%fused_computation.39 | loop fusion | flops 917504 | bytes 786944 | tf_op jit(solution)/shard_map/ge | solution.py:173
  37.0 2.4 %collective-permute-start.6 = (bf16[5,512]{1,0:T(8,128)(2,1)S(1)}, bf16[5,512]{1,0:T(8,128)(2,1)S(1)}, u32[]{:S(2)}, u32[]{:S(2)}) collective-permute-start(bf16[5,512]{1,0:T(8,128)(2,1)S(1)} %slice.279), channel_id=1, source_target_pairs={{0,4},{4,8},{8,12},{12,16},{16,20},{20,24},{24,28},{1,5},{5,9},{9,... | collective-permute-start | bytes 15368 | tf_op jit(solution)/shard_map/ppermute | solution.py:23
  39.4 0.1 copy.71
  39.6 0.7 concatenate.43
  40.2 0.8 pad_maximum_fusion.3
  41.0 1.7 %copy.66 = bf16[128,512]{0,1:T(8,128)(2,1)} copy(bf16[128,512]{1,0:T(8,128)(2,1)} %get-tuple-element.48) | data formatting | bytes 262144 | tf_op jit(solution)/shard_map/slice | solution.py:229
  42.7 0.8 copy.67
  43.4 0.1 copy.68
  43.6 0.1 copy.69
  43.7 0.1 copy.70
  43.8 0.9 %constant_dynamic-update-slice_fusion.4 = bf16[128,4,6,128]{0,3,2,1:T(8,128)(2,1)S(1)} fusion(bf16[128,4,6,128]{0,3,2,1:T(8,128)(2,1)S(1)} %constant_dynamic-update-slice_fusion.5, bf16[128,4,1,128]{0,3,2,1:T(8,128)(2,1)} %bitcast.86), kind=kLoop, calls=%fused_computation.72 | loop fusion | bytes 262144
  44.8 0.9 %constant_dynamic-update-slice_fusion.3 = bf16[128,4,6,128]{0,3,2,1:T(8,128)(2,1)S(1)} fusion(bf16[128,4,6,128]{0,3,2,1:T(8,128)(2,1)S(1)} %constant_dynamic-update-slice_fusion.4, bf16[128,4,1,128]{0,3,2,1:T(8,128)(2,1)} %bitcast.87), kind=kLoop, calls=%fused_computation.71 | loop fusion | bytes 262144
  45.8 0.3 maximum_select_fusion
  46.1 0.5 copy-done
  46.6 0.1 copy.63
  46.8 0.2 fusion.56
  47.0 1.1 %concatenate.41.keys_ref = bf16[1152,512]{1,0:T(8,128)(2,1)} pad(bf16[1024,512]{1,0:T(8,128)(2,1)S(1)} %bitcast.75, bf16[]{:T(256)} %constant.106.clone.1), padding=128_0x0_0 | pad | bytes 2228226 | tf_op jit(solution)/shard_map/concatenate | solution.py:221
  48.1 0.1 fusion.25
  48.2 0.1 fusion.58
  48.3 0.1 slice.229
  48.4 0.1 slice.233
  48.5 0.1 slice.239
  48.6 0.1 slice.247
  48.7 0.1 slice.257
  48.9 0.3 copy-done.1
  49.1 0.8 fusion.22
  50.0 0.1 copy.72
  50.1 0.1 copy.75
  50.2 0.1 copy.73
  50.4 10.9 %shard_map.64 = f32[4,1024,128]{2,1,0:T(8,128)} custom-call(f32[264]{0:T(512)} %reshape.175.taps_ref, bf16[4,768,128]{2,1,0:T(8,128)(2,1)} %bitcast.82, bf16[1152,512]{1,0:T(8,128)(2,1)} %concatenate.41.keys_ref), custom_call_target="tpu_custom_call" | custom-call | tf_op jit(solution)/shard_map/pallas_call | solution.py:120
  61.5 0.1 subtract_bitcast_fusion.3
  61.6 0.1 fusion.45
  61.7 3.9 %divide_bitcast_fusion = f32[1,4,1024,128]{3,2,1,0:T(8,128)S(1)} fusion(f32[4,1024,128]{2,1,0:T(8,128)} %shard_map.64, f32[4,128]{1,0:T(4,128)S(1)} %get-tuple-element.58, f32[4,128]{1,0:T(4,128)S(1)} %get-tuple-element.57, f32[4,128]{1,0:T(4,128)S(1)} %get-tuple-element.56, f32[4,128]{1,0:T(4,128)S(1)} %subtract_bitcast_fusion.3, f32[4,128]{1,0:T(4,128)S(1)} %fusion.45, ...), kind=kOutput, calls=%fused_computation.6 | output fusion | flops 6818814 | bytes 4990976 | tf_op jit(solution)/shard_map/div | solution.py:176
  65.6 1.4 %slice_bitcast_fusion.3 = (f32[1024,128]{1,0:T(8,128)}, f32[1024,128]{1,0:T(8,128)}, f32[1024,128]{1,0:T(8,128)}, f32[1024,128]{1,0:T(8,128)}) fusion(f32[1,4,1024,128]{3,2,1,0:T(8,128)S(1)} %divide_bitcast_fusion), kind=kLoop, calls=%fused_computation.31 | loop fusion | bytes 4194304 | tf_op jit(solution)/shard_map/mul | solution.py:181
  67.0 0.3 reshape.196
  67.3 0.7 copy-done.2
  68.0 0.2 copy-done.3
  68.2 2.2 %multiply_reduce_fusion = (f32[128,4]{0,1:T(4,128)S(1)}, f32[128,4,128]{0,2,1:T(8,128)S(1)}) fusion(f32[1024,128]{1,0:T(8,128)S(1)} %copy-done.3, f32[4]{0:T(128)S(1)} %copy-done.24, f32[1024,128]{1,0:T(8,128)} %get-tuple-element.31, f32[4]{0:T(128)S(1)} %copy-done.25, f32[1024,128]{1,0:T(8,128)} %get-tuple-element.32, f32[4]{0:T(128)S(1)} %copy-done.26, ...), kind=kOutput, calls=%fused_computation.55 | convolution fusion | flops 138542592 | bytes 3409984 | tf_op jit(solution)/shard_map/hki,khd->ihd/dot_general | solution.py:183
  70.4 0.1 multiply_convert_fusion
  70.5 0.2 constant_dynamic-slice_fusion.3
  70.8 0.1 copy.83
  70.8 2.9 %collective-permute-start.7 = (bf16[32,512]{1,0:T(8,128)(2,1)S(1)}, bf16[32,512]{1,0:T(8,128)(2,1)S(1)}, u32[]{:S(2)}, u32[]{:S(2)}) collective-permute-start(bf16[32,512]{1,0:T(8,128)(2,1)S(1)} %copy.83), channel_id=1, source_target_pairs={{0,1},{1,2},{2,3},{3,0},{4,5},{5,6},{6,7},{7,4},{8,9},{9,10},{10,1... | collective-permute-start | bytes 98312 | tf_op jit(solution)/shard_map/ppermute | solution.py:33
  74.0 2.4 %collective-permute-start.9 = (bf16[32,512]{1,0:T(8,128)(2,1)S(1)}, bf16[32,512]{1,0:T(8,128)(2,1)S(1)}, u32[]{:S(2)}, u32[]{:S(2)}) collective-permute-start(bf16[32,512]{1,0:T(8,128)(2,1)S(1)} %copy.85), channel_id=1, source_target_pairs={{0,3},{1,0},{2,1},{3,2},{4,7},{5,4},{6,5},{7,6},{8,11},{9,8},{10,9... | collective-permute-start | bytes 98312 | tf_op jit(solution)/shard_map/ppermute | solution.py:33
  76.5 0.3 collective-permute-done.7
  76.8 2.4 %collective-permute-done.8 = bf16[32,512]{1,0:T(8,128)(2,1)S(1)} collective-permute-done((bf16[32,512]{1,0:T(8,128)(2,1)S(1)}, bf16[32,512]{1,0:T(8,128)(2,1)S(1)}, u32[]{:S(2)}, u32[]{:S(2)}) %collective-permute-start.8) | collective-permute-done | bytes 32800 | tf_op jit(solution)/shard_map/ppermute | solution.py:33
  79.2 0.7 gather_fusion.1
  79.9 0.1 select_bitcast_fusion.1
  80.0 0.7 copy.87
  (86 shorter events, 1.2 us)
Async XLA Ops:
  1.1 8.8 %collective-permute-start = (bf16[3,32,512]{2,1,0:T(8,128)(2,1)S(1)}, bf16[3,32,512]{2,1,0:T(8,128)(2,1)S(1)}, u32[]{:S(2)}, u32[]{:S(2)}) collective-permute-start(bf16[3,32,512]{2,1,0:T(8,128)(2,1)S(1)} %get-tuple-element.41), channel_id=1, source_target_pairs={{0,1},{1,2},{2,3},{3,0},{4,5},{5,6},{6,7},{7,4},{8,9},{9,10},{10,1... | collective-permute-start | bytes 294920 | tf_op jit(solution)/shard_map/ppermute | solution.py:33
  4.2 9.2 %collective-permute-start.1 = (bf16[3,32,512]{2,1,0:T(8,128)(2,1)S(1)}, bf16[3,32,512]{2,1,0:T(8,128)(2,1)S(1)}, u32[]{:S(2)}, u32[]{:S(2)}) collective-permute-start(bf16[3,32,512]{2,1,0:T(8,128)(2,1)S(1)} %get-tuple-element.40), channel_id=1, source_target_pairs={{0,2},{1,3},{2,0},{3,1},{4,6},{5,7},{6,4},{7,5},{8,10},{9,11},{10,... | collective-permute-start | bytes 294920 | tf_op jit(solution)/shard_map/ppermute | solution.py:33
  6.8 6.6 %collective-permute-start.2 = (bf16[3,32,512]{2,1,0:T(8,128)(2,1)S(1)}, bf16[3,32,512]{2,1,0:T(8,128)(2,1)S(1)}, u32[]{:S(2)}, u32[]{:S(2)}) collective-permute-start(bf16[3,32,512]{2,1,0:T(8,128)(2,1)S(1)} %get-tuple-element.39), channel_id=1, source_target_pairs={{0,3},{1,0},{2,1},{3,2},{4,7},{5,4},{6,5},{7,6},{8,11},{9,8},{10,9... | collective-permute-start | bytes 294920 | tf_op jit(solution)/shard_map/ppermute | solution.py:33
  8.2 14.3 %copy-start.10 = (s32[1024]{0:T(1024)}, s32[1024]{0:T(1024)S(1)}, u32[]{:S(2)}) copy-start(s32[1024]{0:T(1024)S(1)} %pad_clamp_fusion) | copy-start | bytes 12292
  8.2 14.3 %copy-start.21 = (pred[4]{0:T(512)(128)(4,1)}, pred[4]{0:T(512)(128)(4,1)S(1)}, u32[]{:S(2)}) copy-start(pred[4]{0:T(512)(128)(4,1)S(1)} %compare_and_fusion) | copy-start | bytes 16
  13.5 10.6 %copy-start.4 = (f32[4,6,11]{2,0,1:T(4,128)S(1)}, f32[4,6,11]{2,0,1:T(4,128)}, u32[]{:S(2)}) copy-start(f32[4,6,11]{2,0,1:T(4,128)} %param.9) | copy-start | bytes 3172
  13.5 11.3 %copy-start.5 = (f32[4,4]{1,0:T(4,128)S(1)}, f32[4,4]{1,0:T(4,128)}, u32[]{:S(2)}) copy-start(f32[4,4]{1,0:T(4,128)} %param.10) | copy-start | bytes 196
  14.3 8.2 %collective-permute-start.3 = (bf16[1,2,128,512]{3,2,1,0:T(8,128)(2,1)S(1)}, bf16[1,2,128,512]{3,2,1,0:T(8,128)(2,1)S(1)}, u32[]{:S(2)}, u32[]{:S(2)}) collective-permute-start(bf16[1,2,128,512]{3,2,1,0:T(8,128)(2,1)S(1)} %maximum_bitcast_fusion), channel_id=1, source_target_pairs={{0,16},{4,20},{8,24},{12,28},{16,0},{20,4},{24,8},{28,12},{1,17},{... | collective-permute-start | bytes 786440 | tf_op jit(solution)/shard_map/ppermute | solution.py:47
  22.5 12.9 %collective-permute-start.4 = (bf16[2,2,128,512]{3,2,1,0:T(8,128)(2,1)S(1)}, bf16[2,2,128,512]{3,2,1,0:T(8,128)(2,1)S(1)}, u32[]{:S(2)}, u32[]{:S(2)}) collective-permute-start(bf16[2,2,128,512]{3,2,1,0:T(8,128)(2,1)S(1)} %maximum_select_fusion.2), channel_id=1, source_target_pairs={{0,8},{4,12},{8,0},{12,4},{16,24},{20,28},{24,16},{28,20},{1,9},{5... | collective-permute-start | bytes 1572872 | tf_op jit(solution)/shard_map/ppermute | solution.py:47
  35.6 10.2 %collective-permute-start.5 = (bf16[4,2,128,512]{3,2,1,0:T(8,128)(2,1)S(1)}, bf16[4,2,128,512]{3,2,1,0:T(8,128)(2,1)S(1)}, u32[]{:S(2)}, u32[]{:S(2)}) collective-permute-start(bf16[4,2,128,512]{3,2,1,0:T(8,128)(2,1)S(1)} %maximum_select_fusion.1), channel_id=1, source_target_pairs={{0,4},{4,0},{8,12},{12,8},{16,20},{20,16},{24,28},{28,24},{1,5},{5... | collective-permute-start | bytes 3145736 | tf_op jit(solution)/shard_map/ppermute | solution.py:47
  37.0 3.2 %collective-permute-start.6 = (bf16[5,512]{1,0:T(8,128)(2,1)S(1)}, bf16[5,512]{1,0:T(8,128)(2,1)S(1)}, u32[]{:S(2)}, u32[]{:S(2)}) collective-permute-start(bf16[5,512]{1,0:T(8,128)(2,1)S(1)} %slice.279), channel_id=1, source_target_pairs={{0,4},{4,8},{8,12},{12,16},{16,20},{20,24},{24,28},{1,5},{5,9},{9,... | collective-permute-start | bytes 15368 | tf_op jit(solution)/shard_map/ppermute | solution.py:23
  45.8 0.9 %copy-start = (bf16[128,4,6,128]{0,3,2,1:T(8,128)(2,1)}, bf16[128,4,6,128]{0,3,2,1:T(8,128)(2,1)S(1)}, u32[]{:S(2)}) copy-start(bf16[128,4,6,128]{0,3,2,1:T(8,128)(2,1)S(1)} %constant_dynamic-update-slice_fusion) | copy-start | bytes 2359300
  48.2 0.9 %copy-start.1 = (bf16[128,4,128]{2,1,0:T(4,128)(2,1)S(1)}, bf16[128,4,128]{2,1,0:T(4,128)(2,1)}, u32[]{:S(2)}) copy-start(bf16[128,4,128]{2,1,0:T(4,128)(2,1)} %concatenate.43) | copy-start | bytes 393220
  50.3 11.1 %copy-start.6 = (f32[4]{0:T(128)S(1)}, f32[4]{0:T(128)}, u32[]{:S(2)}) copy-start(f32[4]{0:T(128)} %get-tuple-element.13) | copy-start | bytes 52
  50.3 11.1 %copy-start.7 = (f32[4]{0:T(128)S(1)}, f32[4]{0:T(128)}, u32[]{:S(2)}) copy-start(f32[4]{0:T(128)} %get-tuple-element.16) | copy-start | bytes 52
  50.3 11.1 %copy-start.8 = (f32[4]{0:T(128)S(1)}, f32[4]{0:T(128)}, u32[]{:S(2)}) copy-start(f32[4]{0:T(128)} %get-tuple-element.17) | copy-start | bytes 52
  50.3 11.1 %copy-start.9 = (f32[4]{0:T(128)S(1)}, f32[4]{0:T(128)}, u32[]{:S(2)}) copy-start(f32[4]{0:T(128)} %get-tuple-element.20) | copy-start | bytes 52
  50.3 11.1 %copy-start.11 = (f32[4]{0:T(128)S(1)}, f32[4]{0:T(128)}, u32[]{:S(2)}) copy-start(f32[4]{0:T(128)} %get-tuple-element.15) | copy-start | bytes 52
  50.3 11.1 %copy-start.12 = (f32[4]{0:T(128)S(1)}, f32[4]{0:T(128)}, u32[]{:S(2)}) copy-start(f32[4]{0:T(128)} %get-tuple-element.19) | copy-start | bytes 52
  50.3 11.1 %copy-start.13 = (f32[4]{0:T(128)S(1)}, f32[4]{0:T(128)}, u32[]{:S(2)}) copy-start(f32[4]{0:T(128)} %get-tuple-element.22) | copy-start | bytes 52
  50.3 11.1 %copy-start.14 = (f32[4]{0:T(128)S(1)}, f32[4]{0:T(128)}, u32[]{:S(2)}) copy-start(f32[4]{0:T(128)} %get-tuple-element.24) | copy-start | bytes 52
  50.4 11.2 %copy-start.16 = (f32[4]{0:T(128)S(1)}, f32[4]{0:T(128)}, u32[]{:S(2)}) copy-start(f32[4]{0:T(128)} %get-tuple-element.10) | copy-start | bytes 52
  50.4 11.2 %copy-start.17 = (f32[4]{0:T(128)S(1)}, f32[4]{0:T(128)}, u32[]{:S(2)}) copy-start(f32[4]{0:T(128)} %get-tuple-element.14) | copy-start | bytes 52
  50.4 11.2 %copy-start.18 = (f32[4]{0:T(128)S(1)}, f32[4]{0:T(128)}, u32[]{:S(2)}) copy-start(f32[4]{0:T(128)} %get-tuple-element.18) | copy-start | bytes 52
  50.4 11.2 %copy-start.19 = (f32[4]{0:T(128)S(1)}, f32[4]{0:T(128)}, u32[]{:S(2)}) copy-start(f32[4]{0:T(128)} %get-tuple-element.21) | copy-start | bytes 52
  50.4 11.2 %copy-start.20 = (f32[4]{0:T(128)S(1)}, f32[4]{0:T(128)}, u32[]{:S(2)}) copy-start(f32[4]{0:T(128)} %get-tuple-element.23) | copy-start | bytes 52
  67.0 1.0 %copy-start.2 = (f32[1024,128]{1,0:T(8,128)S(1)}, f32[1024,128]{1,0:T(8,128)}, u32[]{:S(2)}) copy-start(f32[1024,128]{1,0:T(8,128)} %get-tuple-element.29) | copy-start | bytes 1572868
  67.0 1.2 %copy-start.3 = (f32[1024,128]{1,0:T(8,128)S(1)}, f32[1024,128]{1,0:T(8,128)}, u32[]{:S(2)}) copy-start(f32[1024,128]{1,0:T(8,128)} %get-tuple-element.30) | copy-start | bytes 1572868
  67.0 1.2 %copy-start.23 = (f32[4]{0:T(128)S(1)}, f32[4]{0:T(128)}, u32[]{:S(2)}) copy-start(f32[4]{0:T(128)} %get-tuple-element.25) | copy-start | bytes 52
  67.0 1.2 %copy-start.24 = (f32[4]{0:T(128)S(1)}, f32[4]{0:T(128)}, u32[]{:S(2)}) copy-start(f32[4]{0:T(128)} %get-tuple-element.26) | copy-start | bytes 52
  67.0 1.2 %copy-start.25 = (f32[4]{0:T(128)S(1)}, f32[4]{0:T(128)}, u32[]{:S(2)}) copy-start(f32[4]{0:T(128)} %get-tuple-element.27) | copy-start | bytes 52
  67.0 1.2 %copy-start.26 = (f32[4]{0:T(128)S(1)}, f32[4]{0:T(128)}, u32[]{:S(2)}) copy-start(f32[4]{0:T(128)} %get-tuple-element.28) | copy-start | bytes 52
  68.2 2.2 %copy-start.15 = (f32[512]{0:T(512)S(1)}, f32[512]{0:T(512)}, u32[]{:S(2)}) copy-start(f32[512]{0:T(512)} %param.11) | copy-start | bytes 6148
  70.4 9.5 %copy-start.22 = (pred[4]{0:T(512)(128)(4,1)S(1)}, pred[4]{0:T(512)(128)(4,1)}, u32[]{:S(2)}) copy-start(pred[4]{0:T(512)(128)(4,1)} %copy-done.21) | copy-start | bytes 16
  70.8 6.0 %collective-permute-start.7 = (bf16[32,512]{1,0:T(8,128)(2,1)S(1)}, bf16[32,512]{1,0:T(8,128)(2,1)S(1)}, u32[]{:S(2)}, u32[]{:S(2)}) collective-permute-start(bf16[32,512]{1,0:T(8,128)(2,1)S(1)} %copy.83), channel_id=1, source_target_pairs={{0,1},{1,2},{2,3},{3,0},{4,5},{5,6},{6,7},{7,4},{8,9},{9,10},{10,1... | collective-permute-start | bytes 98312 | tf_op jit(solution)/shard_map/ppermute | solution.py:33
  73.8 5.4 %collective-permute-start.8 = (bf16[32,512]{1,0:T(8,128)(2,1)S(1)}, bf16[32,512]{1,0:T(8,128)(2,1)S(1)}, u32[]{:S(2)}, u32[]{:S(2)}) collective-permute-start(bf16[32,512]{1,0:T(8,128)(2,1)S(1)} %copy.84), channel_id=1, source_target_pairs={{0,2},{1,3},{2,0},{3,1},{4,6},{5,7},{6,4},{7,5},{8,10},{9,11},{10,... | collective-permute-start | bytes 98312 | tf_op jit(solution)/shard_map/ppermute | solution.py:33
  74.0 5.2 %collective-permute-start.9 = (bf16[32,512]{1,0:T(8,128)(2,1)S(1)}, bf16[32,512]{1,0:T(8,128)(2,1)S(1)}, u32[]{:S(2)}, u32[]{:S(2)}) collective-permute-start(bf16[32,512]{1,0:T(8,128)(2,1)S(1)} %copy.85), channel_id=1, source_target_pairs={{0,3},{1,0},{2,1},{3,2},{4,7},{5,4},{6,5},{7,6},{8,11},{9,8},{10,9... | collective-permute-start | bytes 98312 | tf_op jit(solution)/shard_map/ppermute | solution.py:33

commit v13 on v9

--- a/solution.py
+++ b/solution.py
@@ -195,10 +195,10 @@
 def shards(query_states, key_states, value_states, score_kernel, head_mixing, head_gain):
     groups = lax.axis_size("uly")
     stacked = jnp.stack([query_states, key_states, value_states])
-    group_width = stacked.shape[2] // groups
+    stacked = stacked.reshape(stacked.shape[:2] + (groups, -1))
+    stacked = jnp.transpose(stacked, (2, 0, 1, 3))
     pieces = exchanged(
-        lambda group: lax.dynamic_slice_in_dim(stacked, group * group_width, group_width, 2),
-        "uly",
+        lambda group: lax.dynamic_index_in_dim(stacked, group, 0, keepdims=False), "uly"
     )
     pieces = jnp.moveaxis(pieces, 0, 1)
     query_local, key_local, value_local = pieces.reshape(

time: 72.4 us -> 74.1 us (1.023)
  local copies, waits for them, and re-layouts: 12.9 us -> 16.4 us
  other arithmetic: 8.36 us -> 7.24 us
    another operation x1 -> x5, local copies, waits for them, and re-layouts: 0.04 us -> 3.93 us  [the longest x4 3.01 us: shards(): stacked = jnp.stack([query_states, key_states, value_states])]
    transpose x0 -> x1, local copies, waits for them, and re-layouts: none -> 1.29 us  [attend_chunk(): jnp.transpose(shifted, (1, 2, 3, 0)).reshape((heads, -1, row_count))]
    ppermute x6, waiting for transfers between devices: 9.5 us -> 8.34 us  [gathered(): incoming = lax.ppermute(held, axis, [(i, i ^ bit) for i in range(peers)])]
    another operation x1 -> x0, other arithmetic: 1.07 us -> none  [shards(): stacked = jnp.stack([query_states, key_states, value_states])]
    transpose x2 -> x1, local copies, waits for them, and re-layouts: 1.04 us -> 0.1 us  [gathered(): jnp.transpose(held, tuple(reversed(range(bits))) + tuple(range(bits, held...]
    another operation x1 -> x2, local copies, waits for them, and re-layouts: 0.76 us -> 1.7 us  [shards(): value_heads = value_all.reshape(seq_len, heads, head_dim)]
  transfers between devices with their start and end apart: 13 -> 13, of which waited for: 9 -> 11; matrix products, arithmetic and copies ran while one was open for 17% -> 17% of each run, Pallas kernels for 15% -> 15%
where the time goes in v13:
time: 74.1 us; the launch traced here: 73.8 us
  starting transfers between devices  20.9 us (28%)
  local copies, waits for them, and re-layouts  16.4 us (22%)
  waiting for transfers between devices  15.6 us (21%)
  Pallas kernels  10.9 us (15%)
  other arithmetic  7.24 us (10%)
  matrix products  2.13 us (3%)
    ppermute x6, starting transfers between devices, exchanged(): received.append(lax.ppermute(outgoing, axis, pairs))  12.3 us
    pallas_call x1, Pallas kernels, conv_logits(): pl.pallas_call(logits_kernel, grid=(heads, seq_len // span), in_specs=[pl...  10.9 us
    ppermute x6, waiting for transfers between devices, gathered(): incoming = lax.ppermute(held, axis, [(i, i ^ bit) for i in range(peers)])  8.34 us
    ppermute x6, starting transfers between devices, gathered(): incoming = lax.ppermute(held, axis, [(i, i ^ bit) for i in range(peers)])  7.09 us
    ppermute x6, waiting for transfers between devices, exchanged(): received.append(lax.ppermute(outgoing, axis, pairs))  6.77 us
    div x1, other arithmetic, attend_chunk(): probabilities = expd / jnp.sum(expd, axis=1, keepdims=True)  3.81 us
    another operation x4, local copies, waits for them, and re-layouts, shards(): stacked = jnp.stack([query_states, key_states, value_states])  3.01 us
    dot_general x1, matrix products, attend_chunk(): jnp.einsum('hki,khd->ihd', mixed_probs, value_heads, preferred_element_ty...  2.13 us
  transfers between devices with their start and end apart: 13, of which 11 were waited for; matrix products, arithmetic and copies ran while one was open for 17% of the time, Pallas kernels for 15%

profile of v13, /device:TPU:0, one launch (start us, length us, event | category | flops | bytes accessed | tf_op | source)
XLA Modules:
  0.0 73.8 jit_solution(2347484620871092123)
XLA Ops:
  0.0 1.0 %stack.61 = bf16[1,32,4,512]{3,2,1,0:T(4,128)(2,1)S(1)} reshape(bf16[32,2048]{1,0:T(8,128)(2,1)} %param.6) | data formatting | bytes 262144 | tf_op jit(solution)/shard_map/stack | solution.py:197
  1.0 1.0 %stack.62 = bf16[1,32,4,512]{3,2,1,0:T(4,128)(2,1)S(1)} reshape(bf16[32,2048]{1,0:T(8,128)(2,1)} %param.7) | data formatting | bytes 262144 | tf_op jit(solution)/shard_map/stack | solution.py:197
  2.0 1.0 %stack.63 = bf16[1,32,4,512]{3,2,1,0:T(4,128)(2,1)S(1)} reshape(bf16[32,2048]{1,0:T(8,128)(2,1)} %param.8) | data formatting | bytes 262144 | tf_op jit(solution)/shard_map/stack | solution.py:197
  3.2 0.9 %constant_dynamic-slice_fusion.7 = (bf16[3,32,1,512]{3,2,1,0:T(2,128)(2,1)S(1)}, bf16[3,32,1,512]{3,2,1,0:T(2,128)(2,1)S(1)}, bf16[3,32,1,512]{3,2,1,0:T(2,128)(2,1)S(1)}, bf16[3,32,1,512]{3,2,1,0:T(2,128)(2,1)S(1)}) fusion(bf16[3,32,4,512]{3,2,1,0:T(4,128)(2,1)S(1)} %constant_dynamic-update-slice_fusion, s32[]{:T(128)S(6)} %select_n.171, s32[]{:T(128)S(6)} %select_n.177, ...), kind=kLoop, calls=%fused_computation.91 | loop fusion | bytes 786448 | tf_op jit(solution)/shard_map/dynamic-slice
  4.1 3.1 %collective-permute-start = (bf16[3,32,512]{2,1,0:T(8,128)(2,1)S(1)}, bf16[3,32,512]{2,1,0:T(8,128)(2,1)S(1)}, u32[]{:S(2)}, u32[]{:S(2)}) collective-permute-start(bf16[3,32,512]{2,1,0:T(8,128)(2,1)S(1)} %bitcast.94), channel_id=1, source_target_pairs={{0,1},{1,2},{2,3},{3,0},{4,5},{5,6},{6,7},{7,4},{8,9},{9,10},{10,1... | collective-permute-start | bytes 294920 | tf_op jit(solution)/shard_map/ppermute | solution.py:33
  7.2 2.7 %collective-permute-start.1 = (bf16[3,32,512]{2,1,0:T(8,128)(2,1)S(1)}, bf16[3,32,512]{2,1,0:T(8,128)(2,1)S(1)}, u32[]{:S(2)}, u32[]{:S(2)}) collective-permute-start(bf16[3,32,512]{2,1,0:T(8,128)(2,1)S(1)} %bitcast.95), channel_id=1, source_target_pairs={{0,2},{1,3},{2,0},{3,1},{4,6},{5,7},{6,4},{7,5},{8,10},{9,11},{10,... | collective-permute-start | bytes 294920 | tf_op jit(solution)/shard_map/ppermute | solution.py:33
  9.9 1.4 %collective-permute-start.2 = (bf16[3,32,512]{2,1,0:T(8,128)(2,1)S(1)}, bf16[3,32,512]{2,1,0:T(8,128)(2,1)S(1)}, u32[]{:S(2)}, u32[]{:S(2)}) collective-permute-start(bf16[3,32,512]{2,1,0:T(8,128)(2,1)S(1)} %bitcast.96), channel_id=1, source_target_pairs={{0,3},{1,0},{2,1},{3,2},{4,7},{5,4},{6,5},{7,6},{8,11},{9,8},{10,9... | collective-permute-start | bytes 294920 | tf_op jit(solution)/shard_map/ppermute | solution.py:33
  11.4 1.2 %fusion.15 = (pred[1024,128]{1,0:T(8,128)(4,1)S(1)}, pred[1024,128]{1,0:T(8,128)(4,1)S(1)}, pred[1024,128]{1,0:T(8,128)(4,1)}, pred[1024,128]{1,0:T(8,128)(4,1)}...) fusion(s32[128]{0:T(128)S(1)} %iota_add_fusion), kind=kLoop, calls=%fused_computation.39 | loop fusion | flops 917504 | bytes 786944 | tf_op jit(solution)/shard_map/ge | solution.py:173
  12.6 0.3 collective-permute-done
  12.8 3.5 %collective-permute-done.1 = bf16[3,32,512]{2,1,0:T(8,128)(2,1)S(1)} collective-permute-done((bf16[3,32,512]{2,1,0:T(8,128)(2,1)S(1)}, bf16[3,32,512]{2,1,0:T(8,128)(2,1)S(1)}, u32[]{:S(2)}, u32[]{:S(2)}) %collective-permute-start.1) | collective-permute-done | bytes 98336 | tf_op jit(solution)/shard_map/ppermute | solution.py:33
  16.4 0.2 collective-permute-done.2
  16.6 0.6 gather_fusion
  17.2 0.1 select_bitcast_fusion
  17.3 1.6 %collective-permute-start.3 = (bf16[1,128,512]{2,1,0:T(8,128)(2,1)S(1)}, bf16[1,128,512]{2,1,0:T(8,128)(2,1)S(1)}, u32[]{:S(2)}, u32[]{:S(2)}) collective-permute-start(bf16[1,128,512]{2,1,0:T(8,128)(2,1)S(1)} %bitcast.87), channel_id=1, source_target_pairs={{0,16},{4,20},{8,24},{12,28},{16,0},{20,4},{24,8},{28,12},{1,17},{... | collective-permute-start | bytes 393224 | tf_op jit(solution)/shard_map/ppermute | solution.py:47
  18.9 0.9 %slice_reduce_fusion.17 = (f32[4]{0:T(128)}, f32[4]{0:T(128)S(1)}, f32[4]{0:T(128)S(1)}, f32[4]{0:T(128)S(1)}, f32[4]{0:T(128)}, /*index=5*/f32[4]{0:T(128)S(1)}...) fusion(f32[4,6,11]{2,0,1:T(4,128)S(1)} %copy-done.2), kind=kLoop, calls=%fused_computation.141 | loop fusion | bytes 480 | tf_op jit(solution)/shard_map/slice | solution.py:157
  19.9 2.7 %collective-permute-done.3 = bf16[1,128,512]{2,1,0:T(8,128)(2,1)S(1)} collective-permute-done((bf16[1,128,512]{2,1,0:T(8,128)(2,1)S(1)}, bf16[1,128,512]{2,1,0:T(8,128)(2,1)S(1)}, u32[]{:S(2)}, u32[]{:S(2)}) %collective-permute-start.3) | collective-permute-done | bytes 131104 | tf_op jit(solution)/shard_map/ppermute | solution.py:47
  22.6 1.6 %collective-permute-start.4 = (bf16[2,128,512]{2,1,0:T(8,128)(2,1)S(1)}, bf16[2,128,512]{2,1,0:T(8,128)(2,1)S(1)}, u32[]{:S(2)}, u32[]{:S(2)}) collective-permute-start(bf16[2,128,512]{2,1,0:T(8,128)(2,1)S(1)} %maximum_select_fusion.4), channel_id=1, source_target_pairs={{0,8},{4,12},{8,0},{12,4},{16,24},{20,28},{24,16},{28,20},{1,9},{5... | collective-permute-start | bytes 786440 | tf_op jit(solution)/shard_map/ppermute | solution.py:47
  24.1 0.8 %slice_reduce_fusion.18 = (f32[4]{0:T(128)}, f32[4]{0:T(128)}, f32[4]{0:T(128)}, f32[4]{0:T(128)}) fusion(f32[1,4,4]{2,1,0:T(4,128)S(1)} %bitcast.97), kind=kLoop, calls=%fused_computation.142 | loop fusion | bytes 128 | tf_op jit(solution)/shard_map/slice | solution.py:181
  24.9 0.7 reshape.195.taps_ref
  25.7 1.5 %collective-permute-start.9 = (bf16[5,512]{1,0:T(8,128)(2,1)S(1)}, bf16[5,512]{1,0:T(8,128)(2,1)S(1)}, u32[]{:S(2)}, u32[]{:S(2)}) collective-permute-start(bf16[5,512]{1,0:T(8,128)(2,1)S(1)} %slice.270), channel_id=1, source_target_pairs={{0,4},{4,8},{8,12},{12,16},{16,20},{20,24},{24,28},{1,5},{5,9},{9,... | collective-permute-start | bytes 15368 | tf_op jit(solution)/shard_map/ppermute | solution.py:23
  27.2 0.5 collective-permute-done.9
  27.8 0.1 pad_maximum_fusion.2
  28.1 1.6 %collective-permute-done.4 = bf16[2,128,512]{2,1,0:T(8,128)(2,1)S(1)} collective-permute-done((bf16[2,128,512]{2,1,0:T(8,128)(2,1)S(1)}, bf16[2,128,512]{2,1,0:T(8,128)(2,1)S(1)}, u32[]{:S(2)}, u32[]{:S(2)}) %collective-permute-start.4) | collective-permute-done | bytes 262176 | tf_op jit(solution)/shard_map/ppermute | solution.py:47
  29.7 0.1 maximum_select_fusion.2
  30.2 1.3 %copy.56 = bf16[4,6,128,128]{3,2,1,0:T(8,128)(2,1)} copy(bf16[4,6,128,128]{2,0,3,1:T(4,128)(2,1)S(1)} %bitcast.84) | data formatting | bytes 1572864 | tf_op jit(solution)/shard_map/transpose | solution.py:167
  31.5 0.3 collective-permute-done.5
  31.8 0.2 maximum_select_fusion
  31.9 0.1 copy.53
  32.0 0.1 fusion.24
  32.1 0.1 fusion.56
  32.3 0.1 slice.221
  32.4 0.1 slice.225
  32.5 0.1 slice.231
  32.6 0.1 slice.239
  32.7 0.1 slice.249
  32.8 0.8 %fusion.21 = (f32[133,4]{1,0:T(8,128)S(1)}, f32[133,4]{1,0:T(8,128)S(1)}, f32[133,4]{1,0:T(8,128)S(1)}, f32[133,4]{1,0:T(8,128)S(1)}, f32[133,4]{1,0:T(8,128)S(1)}) fusion(f32[133,4,128]{2,1,0:T(4,128)S(1)} %slice.249, bf16[128,4,128]{2,1,0:T(4,128)(2,1)S(1)} %concatenate.68, bf16[5,4,128]{2,1,0:T(4,128)(2,1)S(1)} %concatenate.67, ...), kind=kLoop, calls=%fused_computation.51 | loop fusion | flops 814492 | bytes 1508752 | tf_op jit(solution)/shard_map/reduce_sum | solution.py:148
  33.7 0.1 copy.60
  33.8 0.1 copy.58
  33.8 0.1 copy.59
  33.9 3.7 %collective-permute-start.6 = (bf16[1,128,512]{2,1,0:T(8,128)(2,1)S(1)}, bf16[1,128,512]{2,1,0:T(8,128)(2,1)S(1)}, u32[]{:S(2)}, u32[]{:S(2)}) collective-permute-start(bf16[1,128,512]{2,1,0:T(8,128)(2,1)S(1)} %bitcast.85), channel_id=1, source_target_pairs={{0,16},{4,20},{8,24},{12,28},{16,0},{20,4},{24,8},{28,12},{1,17},{... | collective-permute-start | bytes 393224 | tf_op jit(solution)/shard_map/ppermute | solution.py:47
  37.8 3.8 %collective-permute-done.6 = bf16[1,128,512]{2,1,0:T(8,128)(2,1)S(1)} collective-permute-done((bf16[1,128,512]{2,1,0:T(8,128)(2,1)S(1)}, bf16[1,128,512]{2,1,0:T(8,128)(2,1)S(1)}, u32[]{:S(2)}, u32[]{:S(2)}) %collective-permute-start.6) | collective-permute-done | bytes 131104 | tf_op jit(solution)/shard_map/ppermute | solution.py:47
  41.7 0.1 subtract_bitcast_fusion.3
  41.8 1.1 %concatenate.66.keys_ref = bf16[1152,512]{1,0:T(8,128)(2,1)} pad(bf16[1024,512]{1,0:T(8,128)(2,1)S(1)} %bitcast.77, bf16[]{:T(256)} %constant.112.clone.1), padding=128_0x0_0 | pad | bytes 2228226 | tf_op jit(solution)/shard_map/concatenate | solution.py:220
  43.0 10.9 %shard_map.64 = f32[4,1024,128]{2,1,0:T(8,128)} custom-call(f32[264]{0:T(512)} %reshape.195.taps_ref, bf16[4,768,128]{2,1,0:T(8,128)(2,1)} %bitcast.81, bf16[1152,512]{1,0:T(8,128)(2,1)} %concatenate.66.keys_ref), custom_call_target="tpu_custom_call" | custom-call | tf_op jit(solution)/shard_map/pallas_call | solution.py:120
  53.9 0.1 fusion.44
  54.1 0.1 maximum_select_fusion.3
  54.2 3.8 %divide_bitcast_fusion = f32[1,4,1024,128]{3,2,1,0:T(8,128)S(1)} fusion(f32[4,1024,128]{2,1,0:T(8,128)} %shard_map.64, f32[4,128]{1,0:T(4,128)S(1)} %get-tuple-element.60, f32[4,128]{1,0:T(4,128)S(1)} %get-tuple-element.59, f32[4,128]{1,0:T(4,128)S(1)} %get-tuple-element.58, f32[4,128]{1,0:T(4,128)S(1)} %subtract_bitcast_fusion.3, f32[4,128]{1,0:T(4,128)S(1)} %fusion.44, ...), kind=kOutput, calls=%fused_computation.5 | output fusion | flops 6818814 | bytes 4990976 | tf_op jit(solution)/shard_map/div | solution.py:176
  58.0 1.4 %slice_bitcast_fusion.3 = (f32[1024,128]{1,0:T(8,128)}, f32[1024,128]{1,0:T(8,128)}, f32[1024,128]{1,0:T(8,128)}, f32[1024,128]{1,0:T(8,128)}) fusion(f32[1,4,1024,128]{3,2,1,0:T(8,128)S(1)} %divide_bitcast_fusion), kind=kLoop, calls=%fused_computation.30 | loop fusion | bytes 4194304 | tf_op jit(solution)/shard_map/mul | solution.py:181
  59.4 0.2 maximum_select_fusion.1
  59.6 0.9 %copy.68 = bf16[2,2,2,128,512]{3,2,1,0,4:T(2,128)(2,1)S(1)} copy(bf16[2,2,2,128,512]{4,3,0,1,2:T(8,128)(2,1)S(1)} %bitcast.78) | data formatting | bytes 2097152 | tf_op jit(solution)/shard_map/reshape;reshape | solution.py:230
  60.6 0.8 %reshape.216 = bf16[1024,4,128]{0,2,1:T(8,128)(2,1)S(1)} reshape(bf16[2,2,2,128,512]{3,2,1,0,4:T(2,128)(2,1)S(1)} %copy.68) | data formatting | bytes 2097152 | tf_op jit(solution)/shard_map/reshape;reshape | solution.py:230
  61.4 0.2 copy-done.1
  61.6 2.1 %multiply_reduce_fusion = (f32[128,4]{0,1:T(4,128)S(1)}, f32[128,4,128]{0,2,1:T(8,128)S(1)}) fusion(bf16[1024,4,128]{0,2,1:T(8,128)(2,1)S(1)} %reshape.216, f32[1024,128]{1,0:T(8,128)S(1)} %copy-done.1, f32[4]{0:T(128)S(1)} %copy-done.16, f32[1024,128]{1,0:T(8,128)} %get-tuple-element.35, f32[4]{0:T(128)S(1)} %copy-done.17, ...), kind=kOutput, calls=%fused_computation.55 | convolution fusion | flops 138542592 | bytes 3409984 | tf_op jit(solution)/shard_map/hki,khd->ihd/dot_general | solution.py:183
  63.8 0.1 multiply_convert_fusion
  63.9 0.2 constant_dynamic-slice_fusion.3
  64.2 2.7 %collective-permute-start.10 = (bf16[32,512]{1,0:T(8,128)(2,1)S(1)}, bf16[32,512]{1,0:T(8,128)(2,1)S(1)}, u32[]{:S(2)}, u32[]{:S(2)}) collective-permute-start(bf16[32,512]{1,0:T(8,128)(2,1)S(1)} %copy.74), channel_id=1, source_target_pairs={{0,1},{1,2},{2,3},{3,0},{4,5},{5,6},{6,7},{7,4},{8,9},{9,10},{10,1... | collective-permute-start | bytes 98312 | tf_op jit(solution)/shard_map/ppermute | solution.py:33
  67.0 1.3 %collective-permute-start.11 = (bf16[32,512]{1,0:T(8,128)(2,1)S(1)}, bf16[32,512]{1,0:T(8,128)(2,1)S(1)}, u32[]{:S(2)}, u32[]{:S(2)}) collective-permute-start(bf16[32,512]{1,0:T(8,128)(2,1)S(1)} %copy.75), channel_id=1, source_target_pairs={{0,2},{1,3},{2,0},{3,1},{4,6},{5,7},{6,4},{7,5},{8,10},{9,11},{10,... | collective-permute-start | bytes 98312 | tf_op jit(solution)/shard_map/ppermute | solution.py:33
  68.4 1.2 %collective-permute-start.12 = (bf16[32,512]{1,0:T(8,128)(2,1)S(1)}, bf16[32,512]{1,0:T(8,128)(2,1)S(1)}, u32[]{:S(2)}, u32[]{:S(2)}) collective-permute-start(bf16[32,512]{1,0:T(8,128)(2,1)S(1)} %copy.76), channel_id=1, source_target_pairs={{0,3},{1,0},{2,1},{3,2},{4,7},{5,4},{6,5},{7,6},{8,11},{9,8},{10,9... | collective-permute-start | bytes 98312 | tf_op jit(solution)/shard_map/ppermute | solution.py:33
  69.7 0.3 collective-permute-done.10
  70.0 2.3 %collective-permute-done.11 = bf16[32,512]{1,0:T(8,128)(2,1)S(1)} collective-permute-done((bf16[32,512]{1,0:T(8,128)(2,1)S(1)}, bf16[32,512]{1,0:T(8,128)(2,1)S(1)}, u32[]{:S(2)}, u32[]{:S(2)}) %collective-permute-start.11) | collective-permute-done | bytes 32800 | tf_op jit(solution)/shard_map/ppermute | solution.py:33
  72.3 0.2 collective-permute-done.12
  72.5 0.6 gather_fusion.1
  73.1 0.1 select_bitcast_fusion.1
  73.2 0.7 copy.78
  (87 shorter events, 1.9 us)
Async XLA Ops:
  4.1 8.7 %collective-permute-start = (bf16[3,32,512]{2,1,0:T(8,128)(2,1)S(1)}, bf16[3,32,512]{2,1,0:T(8,128)(2,1)S(1)}, u32[]{:S(2)}, u32[]{:S(2)}) collective-permute-start(bf16[3,32,512]{2,1,0:T(8,128)(2,1)S(1)} %bitcast.94), channel_id=1, source_target_pairs={{0,1},{1,2},{2,3},{3,0},{4,5},{5,6},{6,7},{7,4},{8,9},{9,10},{10,1... | collective-permute-start | bytes 294920 | tf_op jit(solution)/shard_map/ppermute | solution.py:33
  7.2 9.2 %collective-permute-start.1 = (bf16[3,32,512]{2,1,0:T(8,128)(2,1)S(1)}, bf16[3,32,512]{2,1,0:T(8,128)(2,1)S(1)}, u32[]{:S(2)}, u32[]{:S(2)}) collective-permute-start(bf16[3,32,512]{2,1,0:T(8,128)(2,1)S(1)} %bitcast.95), channel_id=1, source_target_pairs={{0,2},{1,3},{2,0},{3,1},{4,6},{5,7},{6,4},{7,5},{8,10},{9,11},{10,... | collective-permute-start | bytes 294920 | tf_op jit(solution)/shard_map/ppermute | solution.py:33
  9.9 6.7 %collective-permute-start.2 = (bf16[3,32,512]{2,1,0:T(8,128)(2,1)S(1)}, bf16[3,32,512]{2,1,0:T(8,128)(2,1)S(1)}, u32[]{:S(2)}, u32[]{:S(2)}) collective-permute-start(bf16[3,32,512]{2,1,0:T(8,128)(2,1)S(1)} %bitcast.96), channel_id=1, source_target_pairs={{0,3},{1,0},{2,1},{3,2},{4,7},{5,4},{6,5},{7,6},{8,11},{9,8},{10,9... | collective-permute-start | bytes 294920 | tf_op jit(solution)/shard_map/ppermute | solution.py:33
  11.3 7.6 %copy-start.2 = (f32[4,6,11]{2,0,1:T(4,128)S(1)}, f32[4,6,11]{2,0,1:T(4,128)}, u32[]{:S(2)}) copy-start(f32[4,6,11]{2,0,1:T(4,128)} %param.9) | copy-start | bytes 3172
  11.4 12.8 %copy-start.3 = (f32[4,4]{1,0:T(4,128)S(1)}, f32[4,4]{1,0:T(4,128)}, u32[]{:S(2)}) copy-start(f32[4,4]{1,0:T(4,128)} %param.10) | copy-start | bytes 196
  12.6 4.6 %copy-start.13 = (pred[4]{0:T(512)(128)(4,1)}, pred[4]{0:T(512)(128)(4,1)S(1)}, u32[]{:S(2)}) copy-start(pred[4]{0:T(512)(128)(4,1)S(1)} %compare_and_fusion) | copy-start | bytes 16
  17.3 5.2 %collective-permute-start.3 = (bf16[1,128,512]{2,1,0:T(8,128)(2,1)S(1)}, bf16[1,128,512]{2,1,0:T(8,128)(2,1)S(1)}, u32[]{:S(2)}, u32[]{:S(2)}) collective-permute-start(bf16[1,128,512]{2,1,0:T(8,128)(2,1)S(1)} %bitcast.87), channel_id=1, source_target_pairs={{0,16},{4,20},{8,24},{12,28},{16,0},{20,4},{24,8},{28,12},{1,17},{... | collective-permute-start | bytes 393224 | tf_op jit(solution)/shard_map/ppermute | solution.py:47
  22.6 7.1 %collective-permute-start.4 = (bf16[2,128,512]{2,1,0:T(8,128)(2,1)S(1)}, bf16[2,128,512]{2,1,0:T(8,128)(2,1)S(1)}, u32[]{:S(2)}, u32[]{:S(2)}) collective-permute-start(bf16[2,128,512]{2,1,0:T(8,128)(2,1)S(1)} %maximum_select_fusion.4), channel_id=1, source_target_pairs={{0,8},{4,12},{8,0},{12,4},{16,24},{20,28},{24,16},{28,20},{1,9},{5... | collective-permute-start | bytes 786440 | tf_op jit(solution)/shard_map/ppermute | solution.py:47
  25.7 2.1 %collective-permute-start.9 = (bf16[5,512]{1,0:T(8,128)(2,1)S(1)}, bf16[5,512]{1,0:T(8,128)(2,1)S(1)}, u32[]{:S(2)}, u32[]{:S(2)}) collective-permute-start(bf16[5,512]{1,0:T(8,128)(2,1)S(1)} %slice.270), channel_id=1, source_target_pairs={{0,4},{4,8},{8,12},{12,16},{16,20},{20,24},{24,28},{1,5},{5,9},{9,... | collective-permute-start | bytes 15368 | tf_op jit(solution)/shard_map/ppermute | solution.py:23
  29.8 2.0 %collective-permute-start.5 = (bf16[4,128,512]{2,1,0:T(8,128)(2,1)S(1)}, bf16[4,128,512]{2,1,0:T(8,128)(2,1)S(1)}, u32[]{:S(2)}, u32[]{:S(2)}) collective-permute-start(bf16[4,128,512]{2,1,0:T(8,128)(2,1)S(1)} %maximum_select_fusion.2), channel_id=1, source_target_pairs={{0,4},{4,0},{8,12},{12,8},{16,20},{20,16},{24,28},{28,24},{1,5},{5... | collective-permute-start | bytes 1572872 | tf_op jit(solution)/shard_map/ppermute | solution.py:47
  32.5 9.2 %copy-start.4 = (f32[4]{0:T(128)S(1)}, f32[4]{0:T(128)}, u32[]{:S(2)}) copy-start(f32[4]{0:T(128)} %get-tuple-element.23) | copy-start | bytes 52
  32.5 9.2 %copy-start.5 = (f32[4]{0:T(128)S(1)}, f32[4]{0:T(128)}, u32[]{:S(2)}) copy-start(f32[4]{0:T(128)} %get-tuple-element.26) | copy-start | bytes 52
  32.6 9.1 %copy-start.6 = (f32[4]{0:T(128)S(1)}, f32[4]{0:T(128)}, u32[]{:S(2)}) copy-start(f32[4]{0:T(128)} %get-tuple-element.28) | copy-start | bytes 52
  33.9 7.7 %collective-permute-start.6 = (bf16[1,128,512]{2,1,0:T(8,128)(2,1)S(1)}, bf16[1,128,512]{2,1,0:T(8,128)(2,1)S(1)}, u32[]{:S(2)}, u32[]{:S(2)}) collective-permute-start(bf16[1,128,512]{2,1,0:T(8,128)(2,1)S(1)} %bitcast.85), channel_id=1, source_target_pairs={{0,16},{4,20},{8,24},{12,28},{16,0},{20,4},{24,8},{28,12},{1,17},{... | collective-permute-start | bytes 393224 | tf_op jit(solution)/shard_map/ppermute | solution.py:47
  41.6 12.4 %collective-permute-start.7 = (bf16[2,128,512]{2,1,0:T(8,128)(2,1)S(1)}, bf16[2,128,512]{2,1,0:T(8,128)(2,1)S(1)}, u32[]{:S(2)}, u32[]{:S(2)}) collective-permute-start(bf16[2,128,512]{2,1,0:T(8,128)(2,1)S(1)} %maximum_select_fusion.5), channel_id=1, source_target_pairs={{0,8},{4,12},{8,0},{12,4},{16,24},{20,28},{24,16},{28,20},{1,9},{5... | collective-permute-start | bytes 786440 | tf_op jit(solution)/shard_map/ppermute | solution.py:47
  42.9 11.0 %copy-start.8 = (f32[4]{0:T(128)S(1)}, f32[4]{0:T(128)}, u32[]{:S(2)}) copy-start(f32[4]{0:T(128)} %get-tuple-element.14) | copy-start | bytes 52
  42.9 11.0 %copy-start.9 = (f32[4]{0:T(128)S(1)}, f32[4]{0:T(128)}, u32[]{:S(2)}) copy-start(f32[4]{0:T(128)} %get-tuple-element.18) | copy-start | bytes 52
  42.9 11.0 %copy-start.10 = (f32[4]{0:T(128)S(1)}, f32[4]{0:T(128)}, u32[]{:S(2)}) copy-start(f32[4]{0:T(128)} %get-tuple-element.22) | copy-start | bytes 52
  43.0 11.0 %copy-start.11 = (f32[4]{0:T(128)S(1)}, f32[4]{0:T(128)}, u32[]{:S(2)}) copy-start(f32[4]{0:T(128)} %get-tuple-element.25) | copy-start | bytes 52
  43.0 11.0 %copy-start.12 = (f32[4]{0:T(128)S(1)}, f32[4]{0:T(128)}, u32[]{:S(2)}) copy-start(f32[4]{0:T(128)} %get-tuple-element.27) | copy-start | bytes 52
  54.1 5.3 %collective-permute-start.8 = (bf16[4,128,512]{2,1,0:T(8,128)(2,1)S(1)}, bf16[4,128,512]{2,1,0:T(8,128)(2,1)S(1)}, u32[]{:S(2)}, u32[]{:S(2)}) collective-permute-start(bf16[4,128,512]{2,1,0:T(8,128)(2,1)S(1)} %maximum_select_fusion.3), channel_id=1, source_target_pairs={{0,4},{4,0},{8,12},{12,8},{16,20},{20,16},{24,28},{28,24},{1,5},{5... | collective-permute-start | bytes 1572872 | tf_op jit(solution)/shard_map/ppermute | solution.py:47
  59.6 1.8 %copy-start = (f32[1024,128]{1,0:T(8,128)S(1)}, f32[1024,128]{1,0:T(8,128)}, u32[]{:S(2)}) copy-start(f32[1024,128]{1,0:T(8,128)} %get-tuple-element.33) | copy-start | bytes 1572868
  59.6 1.8 %copy-start.15 = (f32[4]{0:T(128)S(1)}, f32[4]{0:T(128)}, u32[]{:S(2)}) copy-start(f32[4]{0:T(128)} %get-tuple-element.29) | copy-start | bytes 52
  59.6 1.8 %copy-start.16 = (f32[4]{0:T(128)S(1)}, f32[4]{0:T(128)}, u32[]{:S(2)}) copy-start(f32[4]{0:T(128)} %get-tuple-element.30) | copy-start | bytes 52
  59.6 1.8 %copy-start.17 = (f32[4]{0:T(128)S(1)}, f32[4]{0:T(128)}, u32[]{:S(2)}) copy-start(f32[4]{0:T(128)} %get-tuple-element.31) | copy-start | bytes 52
  59.6 1.8 %copy-start.18 = (f32[4]{0:T(128)S(1)}, f32[4]{0:T(128)}, u32[]{:S(2)}) copy-start(f32[4]{0:T(128)} %get-tuple-element.32) | copy-start | bytes 52
  60.6 1.1 %copy-start.1 = (f32[1024,128]{1,0:T(8,128)S(1)}, f32[1024,128]{1,0:T(8,128)}, u32[]{:S(2)}) copy-start(f32[1024,128]{1,0:T(8,128)} %get-tuple-element.34) | copy-start | bytes 1572868
  61.6 2.2 %copy-start.7 = (f32[512]{0:T(512)S(1)}, f32[512]{0:T(512)}, u32[]{:S(2)}) copy-start(f32[512]{0:T(512)} %param.11) | copy-start | bytes 6148
  63.8 9.3 %copy-start.14 = (pred[4]{0:T(512)(128)(4,1)S(1)}, pred[4]{0:T(512)(128)(4,1)}, u32[]{:S(2)}) copy-start(pred[4]{0:T(512)(128)(4,1)} %copy-done.13) | copy-start | bytes 16
  64.2 5.8 %collective-permute-start.10 = (bf16[32,512]{1,0:T(8,128)(2,1)S(1)}, bf16[32,512]{1,0:T(8,128)(2,1)S(1)}, u32[]{:S(2)}, u32[]{:S(2)}) collective-permute-start(bf16[32,512]{1,0:T(8,128)(2,1)S(1)} %copy.74), channel_id=1, source_target_pairs={{0,1},{1,2},{2,3},{3,0},{4,5},{5,6},{6,7},{7,4},{8,9},{9,10},{10,1... | collective-permute-start | bytes 98312 | tf_op jit(solution)/shard_map/ppermute | solution.py:33
  67.0 5.2 %collective-permute-start.11 = (bf16[32,512]{1,0:T(8,128)(2,1)S(1)}, bf16[32,512]{1,0:T(8,128)(2,1)S(1)}, u32[]{:S(2)}, u32[]{:S(2)}) collective-permute-start(bf16[32,512]{1,0:T(8,128)(2,1)S(1)} %copy.75), channel_id=1, source_target_pairs={{0,2},{1,3},{2,0},{3,1},{4,6},{5,7},{6,4},{7,5},{8,10},{9,11},{10,... | collective-permute-start | bytes 98312 | tf_op jit(solution)/shard_map/ppermute | solution.py:33
  68.4 4.1 %collective-permute-start.12 = (bf16[32,512]{1,0:T(8,128)(2,1)S(1)}, bf16[32,512]{1,0:T(8,128)(2,1)S(1)}, u32[]{:S(2)}, u32[]{:S(2)}) collective-permute-start(bf16[32,512]{1,0:T(8,128)(2,1)S(1)} %copy.76), channel_id=1, source_target_pairs={{0,3},{1,0},{2,1},{3,2},{4,7},{5,4},{6,5},{7,6},{8,11},{9,8},{10,9... | collective-permute-start | bytes 98312 | tf_op jit(solution)/shard_map/ppermute | solution.py:33

commit v14 on v9

--- a/solution.py
+++ b/solution.py
@@ -135,6 +135,53 @@
     )(taps, shifted_t, key_pad)
 
 
+def post_kernel(first_ref, mix_ref, logits_ref, band_ref, values_ref, out_ref, probs_ref):
+    heads, seq_len, rows = logits_ref.shape
+    head_dim = out_ref.shape[1]
+    gap = (
+        first_ref[0]
+        + lax.broadcasted_iota(jnp.int32, (seq_len, rows), 1)
+        - lax.broadcasted_iota(jnp.int32, (seq_len, rows), 0)
+    )
+    for head in range(heads):
+        convolved = logits_ref[head]
+        for lag in range(QCONV - 1):
+            convolved = convolved + jnp.where(gap == lag, band_ref[head, lag : lag + 1, :], 0.0)
+        logits = jnp.where(gap >= 0, convolved, lowest)
+        peak = jnp.max(logits, axis=0, keepdims=True)
+        expd = jnp.exp(logits - peak)
+        probs_ref[head] = expd / jnp.sum(expd, axis=0, keepdims=True)
+    for head in range(heads):
+        first_head = head // GROUP * GROUP
+        mixed = jnp.zeros((seq_len, rows), jnp.float32)
+        for source in range(GROUP):
+            mixed = mixed + mix_ref[head * GROUP + source] * probs_ref[first_head + source]
+        out_ref[head] = jnp.dot(
+            values_ref[head * head_dim : (head + 1) * head_dim, :],
+            mixed.astype(jnp.bfloat16),
+            preferred_element_type=jnp.float32,
+        )
+
+
+def post_attend(convolved, band, query_first, values_t, head_mixing):
+    heads, seq_len, row_count = convolved.shape
+    head_dim = values_t.shape[0] // heads
+    first = jnp.reshape(query_first, (1,)).astype(jnp.int32)
+    return pl.pallas_call(
+        post_kernel,
+        in_specs=[
+            pl.BlockSpec(memory_space=pltpu.SMEM),
+            pl.BlockSpec(memory_space=pltpu.SMEM),
+            pl.BlockSpec(memory_space=pltpu.VMEM),
+            pl.BlockSpec(memory_space=pltpu.VMEM),
+            pl.BlockSpec(memory_space=pltpu.VMEM),
+        ],
+        out_specs=pl.BlockSpec(memory_space=pltpu.VMEM),
+        out_shape=jax.ShapeDtypeStruct((heads, head_dim, row_count), jnp.float32),
+        scratch_shapes=[pltpu.VMEM((heads, seq_len, row_count), jnp.float32)],
+    )(first, head_mixing.reshape(-1), convolved, jnp.transpose(band, (1, 0, 2)), values_t)
+
+
 def band_terms(query_rows, query_first, key_flat, score_kernel):
     row_lead = QCONV - 1
     heads = score_kernel.shape[0]
@@ -163,26 +210,10 @@
 
 def attend_chunk(shifted, band, query_first, key_pad, score_kernel, value_heads, head_mixing):
     row_count, heads = shifted.shape[:2]
-    seq_len = value_heads.shape[0]
     shifted_t = jnp.transpose(shifted, (1, 2, 3, 0)).reshape((heads, -1, row_count))
     convolved = conv_logits(shifted_t, score_kernel, key_pad)
-    query_pos = query_first + lax.iota(jnp.int32, row_count)
-    gap = query_pos[None, :] - lax.iota(jnp.int32, seq_len)[:, None]
-    for lag in range(QCONV - 1):
-        convolved = convolved + jnp.where(gap == lag, band[lag][:, None, :], 0.0)
-    logits = jnp.where(gap >= 0, convolved, lowest)
-    peak = jnp.max(logits, axis=1, keepdims=True)
-    expd = jnp.exp(logits - peak)
-    probabilities = expd / jnp.sum(expd, axis=1, keepdims=True)
-    grouped = probabilities.reshape(heads // GROUP, GROUP, seq_len, row_count)
-    weights = head_mixing.reshape(heads // GROUP, GROUP, GROUP)
-    mixed_probs = jnp.zeros_like(grouped)
-    for source in range(GROUP):
-        mixed_probs = mixed_probs + weights[:, :, source, None, None] * grouped[:, source, None]
-    mixed_probs = mixed_probs.reshape(heads, seq_len, row_count).astype(jnp.bfloat16)
-    return jnp.einsum(
-        "hki,khd->ihd", mixed_probs, value_heads, preferred_element_type=jnp.float32
-    )
+    weighted_t = post_attend(convolved, band, query_first, value_heads, head_mixing)
+    return jnp.transpose(weighted_t, (2, 0, 1))
 
 
 def normalize(weighted, gain_local):
@@ -227,7 +258,7 @@
     shifted = jnp.stack(
         [query_heads[row_lead - lag : row_lead - lag + shard_rows] for lag in range(QCONV)], axis=2
     )
-    value_heads = value_all.reshape(seq_len, heads, head_dim)
+    value_heads = value_all.T
     chunk = min(ROW_CHUNK * KEY_BLOCK * 8 // seq_len, shard_rows)
     if chunk == shard_rows:
         weighted = attend_chunk(

time: 72.4 us -> 81.2 us (1.12)
  waiting for transfers between devices: 16.3 us -> 23 us
  Pallas kernels: 10.9 us -> 16.3 us
  matrix products: 2.13 us -> 0 us
  other arithmetic: 8.36 us -> 6.24 us
  starting transfers between devices: 21 us -> 22 us
    ppermute x6, waiting for transfers between devices: 9.5 us -> 15.1 us  [gathered(): incoming = lax.ppermute(held, axis, [(i, i ^ bit) for i in range(peers)])]
    pallas_call x0 -> x1, Pallas kernels: none -> 5.42 us  [post_attend(): pl.pallas_call(post_kernel, in_specs=[pl.BlockSpec(memory_space=pltpu.SME...]
    div x1 -> x0, other arithmetic: 3.81 us -> none  [attend_chunk(): probabilities = expd / jnp.sum(expd, axis=1, keepdims=True)]
    reshape x0 -> x2, local copies, waits for them, and re-layouts: none -> 2.22 us  [the longest x1 1.57 us: shards(): value_all = gathered(value_local, 'ctx').reshape((-1, width))]
    dot_general x1 -> x0, matrix products: 2.13 us -> none  [attend_chunk(): jnp.einsum('hki,khd->ihd', mixed_probs, value_heads, preferred_element_ty...]
    mul x1 -> x0, local copies, waits for them, and re-layouts: 1.37 us -> none  [attend_chunk(): weights[:, :, source, None, None] * grouped[:, source, None]]
    ppermute x6, waiting for transfers between devices: 6.75 us -> 7.97 us  [exchanged(): received.append(lax.ppermute(outgoing, axis, pairs))]
    ge x1 -> x0, other arithmetic: 1.22 us -> none  [attend_chunk(): logits = jnp.where(gap >= 0, convolved, lowest)]
  transfers between devices with their start and end apart: 13 -> 13, of which waited for: 9 -> 10; matrix products, arithmetic and copies ran while one was open for 17% -> 10% of each run, Pallas kernels for 15% -> 13%
where the time goes in v14:
time: 81.2 us; the launch traced here: 80.9 us
  waiting for transfers between devices  23 us (28%)
  starting transfers between devices  22 us (27%)
  Pallas kernels  16.3 us (20%)
  local copies, waits for them, and re-layouts  12.8 us (16%)
  other arithmetic  6.24 us (8%)
    ppermute x6, waiting for transfers between devices, gathered(): incoming = lax.ppermute(held, axis, [(i, i ^ bit) for i in range(peers)])  15.1 us
    ppermute x6, starting transfers between devices, exchanged(): received.append(lax.ppermute(outgoing, axis, pairs))  12.2 us
    pallas_call x1, Pallas kernels, conv_logits(): pl.pallas_call(logits_kernel, grid=(heads, seq_len // span), in_specs=[pl...  10.9 us
    ppermute x6, starting transfers between devices, gathered(): incoming = lax.ppermute(held, axis, [(i, i ^ bit) for i in range(peers)])  8.53 us
    ppermute x6, waiting for transfers between devices, exchanged(): received.append(lax.ppermute(outgoing, axis, pairs))  7.97 us
    pallas_call x1, Pallas kernels, post_attend(): pl.pallas_call(post_kernel, in_specs=[pl.BlockSpec(memory_space=pltpu.SME...  5.42 us
  transfers between devices with their start and end apart: 13, of which 10 were waited for; matrix products, arithmetic and copies ran while one was open for 10% of the time, Pallas kernels for 13%

profile of v14, /device:TPU:0, one launch (start us, length us, event | category | flops | bytes accessed | tf_op | source)
XLA Modules:
  0.0 80.9 jit_solution(9916982805756658228)
XLA Ops:
  0.0 1.1 %pad_maximum_fusion = bf16[3,32,2048]{2,1,0:T(8,128)(2,1)S(1)} fusion(bf16[1,32,2048]{2,1,0:T(8,128)(2,1)} %bitcast.102, bf16[1,32,2048]{2,1,0:T(8,128)(2,1)} %bitcast.103, bf16[1,32,2048]{2,1,0:T(8,128)(2,1)} %bitcast.104), kind=kLoop, calls=%fused_computation.14 | loop fusion | flops 393216 | bytes 786432 | tf_op jit(solution)/shard_map/stack | solution.py:228
  1.1 3.1 %collective-permute-start = (bf16[3,32,512]{2,1,0:T(8,128)(2,1)S(1)}, bf16[3,32,512]{2,1,0:T(8,128)(2,1)S(1)}, u32[]{:S(2)}, u32[]{:S(2)}) collective-permute-start(bf16[3,32,512]{2,1,0:T(8,128)(2,1)S(1)} %get-tuple-element.35), channel_id=1, source_target_pairs={{0,1},{1,2},{2,3},{3,0},{4,5},{5,6},{6,7},{7,4},{8,9},{9,10},{10,1... | collective-permute-start | bytes 294920 | tf_op jit(solution)/shard_map/ppermute | solution.py:33
  4.2 2.6 %collective-permute-start.1 = (bf16[3,32,512]{2,1,0:T(8,128)(2,1)S(1)}, bf16[3,32,512]{2,1,0:T(8,128)(2,1)S(1)}, u32[]{:S(2)}, u32[]{:S(2)}) collective-permute-start(bf16[3,32,512]{2,1,0:T(8,128)(2,1)S(1)} %get-tuple-element.34), channel_id=1, source_target_pairs={{0,2},{1,3},{2,0},{3,1},{4,6},{5,7},{6,4},{7,5},{8,10},{9,11},{10,... | collective-permute-start | bytes 294920 | tf_op jit(solution)/shard_map/ppermute | solution.py:33
  6.8 1.3 %collective-permute-start.2 = (bf16[3,32,512]{2,1,0:T(8,128)(2,1)S(1)}, bf16[3,32,512]{2,1,0:T(8,128)(2,1)S(1)}, u32[]{:S(2)}, u32[]{:S(2)}) collective-permute-start(bf16[3,32,512]{2,1,0:T(8,128)(2,1)S(1)} %get-tuple-element.33), channel_id=1, source_target_pairs={{0,3},{1,0},{2,1},{3,2},{4,7},{5,4},{6,5},{7,6},{8,11},{9,8},{10,9... | collective-permute-start | bytes 294920 | tf_op jit(solution)/shard_map/ppermute | solution.py:33
  8.2 1.7 %collective-permute-done = bf16[3,32,512]{2,1,0:T(8,128)(2,1)S(1)} collective-permute-done((bf16[3,32,512]{2,1,0:T(8,128)(2,1)S(1)}, bf16[3,32,512]{2,1,0:T(8,128)(2,1)S(1)}, u32[]{:S(2)}, u32[]{:S(2)}) %collective-permute-start) | collective-permute-done | bytes 98336 | tf_op jit(solution)/shard_map/ppermute | solution.py:33
  9.9 3.5 %collective-permute-done.1 = bf16[3,32,512]{2,1,0:T(8,128)(2,1)S(1)} collective-permute-done((bf16[3,32,512]{2,1,0:T(8,128)(2,1)S(1)}, bf16[3,32,512]{2,1,0:T(8,128)(2,1)S(1)}, u32[]{:S(2)}, u32[]{:S(2)}) %collective-permute-start.1) | collective-permute-done | bytes 98336 | tf_op jit(solution)/shard_map/ppermute | solution.py:33
  13.5 0.6 gather_fusion
  14.1 0.1 select_bitcast_fusion
  14.2 0.7 fusion.33
  14.9 1.5 %collective-permute-start.4 = (bf16[1,128,512]{2,1,0:T(8,128)(2,1)S(1)}, bf16[1,128,512]{2,1,0:T(8,128)(2,1)S(1)}, u32[]{:S(2)}, u32[]{:S(2)}) collective-permute-start(bf16[1,128,512]{2,1,0:T(8,128)(2,1)S(1)} %bitcast.100), channel_id=1, source_target_pairs={{0,16},{4,20},{8,24},{12,28},{16,0},{20,4},{24,8},{28,12},{1,17},{... | collective-permute-start | bytes 393224 | tf_op jit(solution)/shard_map/ppermute | solution.py:47
  16.4 3.8 %collective-permute-done.4 = bf16[1,128,512]{2,1,0:T(8,128)(2,1)S(1)} collective-permute-done((bf16[1,128,512]{2,1,0:T(8,128)(2,1)S(1)}, bf16[1,128,512]{2,1,0:T(8,128)(2,1)S(1)}, u32[]{:S(2)}, u32[]{:S(2)}) %collective-permute-start.4) | collective-permute-done | bytes 131104 | tf_op jit(solution)/shard_map/ppermute | solution.py:47
  20.2 1.6 %collective-permute-start.5 = (bf16[2,128,512]{2,1,0:T(8,128)(2,1)S(1)}, bf16[2,128,512]{2,1,0:T(8,128)(2,1)S(1)}, u32[]{:S(2)}, u32[]{:S(2)}) collective-permute-start(bf16[2,128,512]{2,1,0:T(8,128)(2,1)S(1)} %maximum_select_fusion.4), channel_id=1, source_target_pairs={{0,8},{4,12},{8,0},{12,4},{16,24},{20,28},{24,16},{28,20},{1,9},{5... | collective-permute-start | bytes 786440 | tf_op jit(solution)/shard_map/ppermute | solution.py:47
  21.8 0.9 %slice_reduce_fusion.14 = (f32[4]{0:T(128)}, f32[4]{0:T(128)S(1)}, f32[4]{0:T(128)S(1)}, f32[4]{0:T(128)S(1)}, f32[4]{0:T(128)}, /*index=5*/f32[4]{0:T(128)S(1)}...) fusion(f32[4,6,11]{2,0,1:T(4,128)S(1)} %copy-done.2), kind=kLoop, calls=%fused_computation.108 | loop fusion | bytes 480 | tf_op jit(solution)/shard_map/slice | solution.py:204
  22.6 0.7 reshape.145.taps_ref
  23.3 0.7 reshape.144.mix_ref
  24.0 1.3 %collective-permute-start.3 = (bf16[5,512]{1,0:T(8,128)(2,1)S(1)}, bf16[5,512]{1,0:T(8,128)(2,1)S(1)}, u32[]{:S(2)}, u32[]{:S(2)}) collective-permute-start(bf16[5,512]{1,0:T(8,128)(2,1)S(1)} %slice.238), channel_id=1, source_target_pairs={{0,4},{4,8},{8,12},{12,16},{16,20},{20,24},{24,28},{1,5},{5,9},{9,... | collective-permute-start | bytes 15368 | tf_op jit(solution)/shard_map/ppermute | solution.py:23
  25.3 0.1 copy.60
  25.5 0.7 concatenate.61
  26.2 0.1 pad_maximum_fusion.3
  26.3 0.1 copy.55
  26.4 0.1 copy.56
  26.6 0.1 copy.57
  26.7 0.1 copy.58
  26.8 0.1 copy.59
  27.0 0.5 collective-permute-done.5
  27.6 0.8 %collective-permute-start.6 = (bf16[4,128,512]{2,1,0:T(8,128)(2,1)S(1)}, bf16[4,128,512]{2,1,0:T(8,128)(2,1)S(1)}, u32[]{:S(2)}, u32[]{:S(2)}) collective-permute-start(bf16[4,128,512]{2,1,0:T(8,128)(2,1)S(1)} %maximum_select_fusion.2), channel_id=1, source_target_pairs={{0,4},{4,0},{8,12},{12,8},{16,20},{20,16},{24,28},{28,24},{1,5},{5... | collective-permute-start | bytes 1572872 | tf_op jit(solution)/shard_map/ppermute | solution.py:47
  28.5 1.4 %collective-permute-done.6 = bf16[4,128,512]{2,1,0:T(8,128)(2,1)S(1)} collective-permute-done((bf16[4,128,512]{2,1,0:T(8,128)(2,1)S(1)}, bf16[4,128,512]{2,1,0:T(8,128)(2,1)S(1)}, u32[]{:S(2)}, u32[]{:S(2)}) %collective-permute-start.6) | collective-permute-done | bytes 524320 | tf_op jit(solution)/shard_map/ppermute | solution.py:47
  29.9 0.2 maximum_select_fusion
  30.1 0.1 copy.61
  30.2 4.4 %collective-permute-start.7 = (bf16[1,128,512]{2,1,0:T(8,128)(2,1)}, bf16[1,128,512]{2,1,0:T(8,128)(2,1)S(1)}, u32[]{:S(2)}, u32[]{:S(2)}) collective-permute-start(bf16[1,128,512]{2,1,0:T(8,128)(2,1)} %bitcast.38), channel_id=1, source_target_pairs={{0,16},{4,20},{8,24},{12,28},{16,0},{20,4},{24,8},{28,12},{1,17},{... | collective-permute-start | bytes 393224 | tf_op jit(solution)/shard_map/ppermute | solution.py:47
  34.6 0.1 fusion.10
  34.7 0.1 fusion.34
  34.9 0.1 slice.196
  35.0 0.1 slice.200
  35.1 0.1 slice.206
  35.2 0.1 slice.214
  35.3 0.1 slice.224
  35.4 0.5 copy-done.1
  35.9 0.8 fusion.4
  36.8 0.1 copy.63
  36.9 1.8 %collective-permute-done.7 = bf16[1,128,512]{2,1,0:T(8,128)(2,1)S(1)} collective-permute-done((bf16[1,128,512]{2,1,0:T(8,128)(2,1)}, bf16[1,128,512]{2,1,0:T(8,128)(2,1)S(1)}, u32[]{:S(2)}, u32[]{:S(2)}) %collective-permute-start.7) | collective-permute-done | bytes 131104 | tf_op jit(solution)/shard_map/ppermute | solution.py:47
  38.7 1.0 %maximum_select_fusion.5 = bf16[2,128,512]{2,1,0:T(8,128)(2,1)S(1)} fusion(bf16[1,128,512]{2,1,0:T(8,128)(2,1)} %bitcast.38, bf16[1,128,512]{2,1,0:T(8,128)(2,1)S(1)} %collective-permute-done.7, pred[]{:T(512)S(6)} %ne.70), kind=kLoop, calls=%fused_computation.27 | loop fusion | flops 393216 | bytes 524289 | tf_op jit(solution)/shard_map/jit(_where)/select_n | solution.py:49
  39.7 0.1 collective-permute-start.8
  39.9 0.1 copy.65
  40.0 7.6 %collective-permute-done.8 = bf16[2,128,512]{2,1,0:T(8,128)(2,1)S(1)} collective-permute-done((bf16[2,128,512]{2,1,0:T(8,128)(2,1)S(1)}, bf16[2,128,512]{2,1,0:T(8,128)(2,1)S(1)}, u32[]{:S(2)}, u32[]{:S(2)}) %collective-permute-start.8) | collective-permute-done | bytes 262176 | tf_op jit(solution)/shard_map/ppermute | solution.py:47
  47.8 1.1 %concatenate.59.keys_ref = bf16[1152,512]{1,0:T(8,128)(2,1)} pad(bf16[1024,512]{1,0:T(8,128)(2,1)S(1)} %bitcast.87, bf16[]{:T(256)} %constant.99.clone.1), padding=128_0x0_0 | pad | bytes 2228226 | tf_op jit(solution)/shard_map/concatenate | solution.py:251
  49.0 10.9 %shard_map.64.logits_ref = f32[4,1024,128]{2,1,0:T(8,128)} custom-call(f32[264]{0:T(512)} %reshape.145.taps_ref, bf16[4,768,128]{2,1,0:T(8,128)(2,1)} %bitcast.94, bf16[1152,512]{1,0:T(8,128)(2,1)} %concatenate.59.keys_ref), custom_call_target="tpu_custom_call" | custom-call | tf_op jit(solution)/shard_map/pallas_call | solution.py:120
  60.1 0.1 fusion.23
  60.2 0.6 stack.102
  60.8 0.2 maximum_select_fusion.1
  61.0 0.9 %copy.71 = bf16[2,2,2,128,512]{3,2,1,0,4:T(2,128)(2,1)S(1)} copy(bf16[2,2,2,128,512]{4,3,0,1,2:T(8,128)(2,1)S(1)} %bitcast.88) | data formatting | bytes 2097152 | tf_op jit(solution)/shard_map/transpose | solution.py:55
  61.9 1.6 %reshape.148 = bf16[1024,512]{0,1:T(8,128)(2,1)} reshape(bf16[2,2,2,128,512]{3,2,1,0,4:T(2,128)(2,1)S(1)} %copy.71) | data formatting | bytes 2097152 | tf_op jit(solution)/shard_map/reshape | solution.py:249
  63.5 5.4 %shard_map.65 = f32[4,128,128]{2,1,0:T(8,128)} custom-call(s32[1]{0:T(128)} %bitcast.first_ref, f32[16]{0:T(128)} %reshape.144.mix_ref, f32[4,1024,128]{2,1,0:T(8,128)} %shard_map.64.logits_ref, f32[4,5,128]{2,1,0:T(8,128)} %bitcast.109, bf16[512,1024]{1,0:T(8,128)(2,1)} %bitcast.90), custom_call_target="tpu_custom_call" | custom-call | tf_op jit(solution)/shard_map/pallas_call | solution.py:170
  68.9 1.0 %fusion.5 = f32[128,4]{0,1:T(4,128)S(1)} fusion(f32[4,128,128]{2,1,0:T(8,128)} %shard_map.65), kind=kLoop, calls=%fused_computation.30 | loop fusion | flops 130560 | bytes 264192 | tf_op jit(solution)/shard_map/reduce_sum | solution.py:220
  69.9 1.1 %fusion.7 = bf16[128,4,128]{0,2,1:T(8,128)(2,1)S(1)} fusion(f32[4,128,128]{2,1,0:T(8,128)} %shard_map.65, f32[4,128]{1,0:T(4,128)S(1)} %bitcast.118, f32[128,4]{0,1:T(4,128)S(1)} %add_rsqrt_fusion), kind=kLoop, calls=%fused_computation.32 | loop fusion | flops 196608 | bytes 397312 | tf_op jit(solution)/shard_map/convert_element_type | solution.py:222
  71.0 0.2 constant_dynamic-slice_fusion.3
  71.3 2.7 %collective-permute-start.10 = (bf16[32,512]{1,0:T(8,128)(2,1)S(1)}, bf16[32,512]{1,0:T(8,128)(2,1)S(1)}, u32[]{:S(2)}, u32[]{:S(2)}) collective-permute-start(bf16[32,512]{1,0:T(8,128)(2,1)S(1)} %copy.77), channel_id=1, source_target_pairs={{0,1},{1,2},{2,3},{3,0},{4,5},{5,6},{6,7},{7,4},{8,9},{9,10},{10,1... | collective-permute-start | bytes 98312 | tf_op jit(solution)/shard_map/ppermute | solution.py:33
  74.1 1.2 %collective-permute-start.11 = (bf16[32,512]{1,0:T(8,128)(2,1)S(1)}, bf16[32,512]{1,0:T(8,128)(2,1)S(1)}, u32[]{:S(2)}, u32[]{:S(2)}) collective-permute-start(bf16[32,512]{1,0:T(8,128)(2,1)S(1)} %copy.78), channel_id=1, source_target_pairs={{0,2},{1,3},{2,0},{3,1},{4,6},{5,7},{6,4},{7,5},{8,10},{9,11},{10,... | collective-permute-start | bytes 98312 | tf_op jit(solution)/shard_map/ppermute | solution.py:33
  75.4 1.3 %collective-permute-start.12 = (bf16[32,512]{1,0:T(8,128)(2,1)S(1)}, bf16[32,512]{1,0:T(8,128)(2,1)S(1)}, u32[]{:S(2)}, u32[]{:S(2)}) collective-permute-start(bf16[32,512]{1,0:T(8,128)(2,1)S(1)} %copy.79), channel_id=1, source_target_pairs={{0,3},{1,0},{2,1},{3,2},{4,7},{5,4},{6,5},{7,6},{8,11},{9,8},{10,9... | collective-permute-start | bytes 98312 | tf_op jit(solution)/shard_map/ppermute | solution.py:33
  76.8 0.3 collective-permute-done.10
  77.1 2.3 %collective-permute-done.11 = bf16[32,512]{1,0:T(8,128)(2,1)S(1)} collective-permute-done((bf16[32,512]{1,0:T(8,128)(2,1)S(1)}, bf16[32,512]{1,0:T(8,128)(2,1)S(1)}, u32[]{:S(2)}, u32[]{:S(2)}) %collective-permute-start.11) | collective-permute-done | bytes 32800 | tf_op jit(solution)/shard_map/ppermute | solution.py:33
  79.3 0.2 collective-permute-done.12
  79.6 0.6 gather_fusion.1
  80.2 0.7 copy.81
  (62 shorter events, 1.5 us)
Async XLA Ops:
  1.1 8.8 %collective-permute-start = (bf16[3,32,512]{2,1,0:T(8,128)(2,1)S(1)}, bf16[3,32,512]{2,1,0:T(8,128)(2,1)S(1)}, u32[]{:S(2)}, u32[]{:S(2)}) collective-permute-start(bf16[3,32,512]{2,1,0:T(8,128)(2,1)S(1)} %get-tuple-element.35), channel_id=1, source_target_pairs={{0,1},{1,2},{2,3},{3,0},{4,5},{5,6},{6,7},{7,4},{8,9},{9,10},{10,1... | collective-permute-start | bytes 294920 | tf_op jit(solution)/shard_map/ppermute | solution.py:33
  4.2 9.2 %collective-permute-start.1 = (bf16[3,32,512]{2,1,0:T(8,128)(2,1)S(1)}, bf16[3,32,512]{2,1,0:T(8,128)(2,1)S(1)}, u32[]{:S(2)}, u32[]{:S(2)}) collective-permute-start(bf16[3,32,512]{2,1,0:T(8,128)(2,1)S(1)} %get-tuple-element.34), channel_id=1, source_target_pairs={{0,2},{1,3},{2,0},{3,1},{4,6},{5,7},{6,4},{7,5},{8,10},{9,11},{10,... | collective-permute-start | bytes 294920 | tf_op jit(solution)/shard_map/ppermute | solution.py:33
  6.8 6.6 %collective-permute-start.2 = (bf16[3,32,512]{2,1,0:T(8,128)(2,1)S(1)}, bf16[3,32,512]{2,1,0:T(8,128)(2,1)S(1)}, u32[]{:S(2)}, u32[]{:S(2)}) collective-permute-start(bf16[3,32,512]{2,1,0:T(8,128)(2,1)S(1)} %get-tuple-element.33), channel_id=1, source_target_pairs={{0,3},{1,0},{2,1},{3,2},{4,7},{5,4},{6,5},{7,6},{8,11},{9,8},{10,9... | collective-permute-start | bytes 294920 | tf_op jit(solution)/shard_map/ppermute | solution.py:33
  8.2 6.0 %copy-start.10 = (pred[4]{0:T(512)(128)(4,1)}, pred[4]{0:T(512)(128)(4,1)S(1)}, u32[]{:S(2)}) copy-start(pred[4]{0:T(512)(128)(4,1)S(1)} %compare_and_fusion) | copy-start | bytes 16
  13.5 2.9 %copy-start.2 = (f32[4,6,11]{2,0,1:T(4,128)S(1)}, f32[4,6,11]{2,0,1:T(4,128)}, u32[]{:S(2)}) copy-start(f32[4,6,11]{2,0,1:T(4,128)} %param.9) | copy-start | bytes 3172
  14.1 9.3 %copy-start.9 = (f32[4,4]{1,0:T(4,128)S(1)}, f32[4,4]{1,0:T(4,128)}, u32[]{:S(2)}) copy-start(f32[4,4]{1,0:T(4,128)} %param.10) | copy-start | bytes 196
  14.9 5.3 %collective-permute-start.4 = (bf16[1,128,512]{2,1,0:T(8,128)(2,1)S(1)}, bf16[1,128,512]{2,1,0:T(8,128)(2,1)S(1)}, u32[]{:S(2)}, u32[]{:S(2)}) collective-permute-start(bf16[1,128,512]{2,1,0:T(8,128)(2,1)S(1)} %bitcast.100), channel_id=1, source_target_pairs={{0,16},{4,20},{8,24},{12,28},{16,0},{20,4},{24,8},{28,12},{1,17},{... | collective-permute-start | bytes 393224 | tf_op jit(solution)/shard_map/ppermute | solution.py:47
  20.2 7.3 %collective-permute-start.5 = (bf16[2,128,512]{2,1,0:T(8,128)(2,1)S(1)}, bf16[2,128,512]{2,1,0:T(8,128)(2,1)S(1)}, u32[]{:S(2)}, u32[]{:S(2)}) collective-permute-start(bf16[2,128,512]{2,1,0:T(8,128)(2,1)S(1)} %maximum_select_fusion.4), channel_id=1, source_target_pairs={{0,8},{4,12},{8,0},{12,4},{16,24},{20,28},{24,16},{28,20},{1,9},{5... | collective-permute-start | bytes 786440 | tf_op jit(solution)/shard_map/ppermute | solution.py:47
  24.0 2.1 %collective-permute-start.3 = (bf16[5,512]{1,0:T(8,128)(2,1)S(1)}, bf16[5,512]{1,0:T(8,128)(2,1)S(1)}, u32[]{:S(2)}, u32[]{:S(2)}) collective-permute-start(bf16[5,512]{1,0:T(8,128)(2,1)S(1)} %slice.238), channel_id=1, source_target_pairs={{0,4},{4,8},{8,12},{12,16},{16,20},{20,24},{24,28},{1,5},{5,9},{9,... | collective-permute-start | bytes 15368 | tf_op jit(solution)/shard_map/ppermute | solution.py:23
  27.6 2.4 %collective-permute-start.6 = (bf16[4,128,512]{2,1,0:T(8,128)(2,1)S(1)}, bf16[4,128,512]{2,1,0:T(8,128)(2,1)S(1)}, u32[]{:S(2)}, u32[]{:S(2)}) collective-permute-start(bf16[4,128,512]{2,1,0:T(8,128)(2,1)S(1)} %maximum_select_fusion.2), channel_id=1, source_target_pairs={{0,4},{4,0},{8,12},{12,8},{16,20},{20,16},{24,28},{28,24},{1,5},{5... | collective-permute-start | bytes 1572872 | tf_op jit(solution)/shard_map/ppermute | solution.py:47
  28.5 1.7 %copy-start = (bf16[128,4,6,128]{0,3,2,1:T(8,128)(2,1)}, bf16[128,4,6,128]{0,3,2,1:T(8,128)(2,1)S(1)}, u32[]{:S(2)}) copy-start(bf16[128,4,6,128]{0,3,2,1:T(8,128)(2,1)S(1)} %constant_dynamic-update-slice_fusion) | copy-start | bytes 2359300
  30.2 8.4 %collective-permute-start.7 = (bf16[1,128,512]{2,1,0:T(8,128)(2,1)}, bf16[1,128,512]{2,1,0:T(8,128)(2,1)S(1)}, u32[]{:S(2)}, u32[]{:S(2)}) collective-permute-start(bf16[1,128,512]{2,1,0:T(8,128)(2,1)} %bitcast.38), channel_id=1, source_target_pairs={{0,16},{4,20},{8,24},{12,28},{16,0},{20,4},{24,8},{28,12},{1,17},{... | collective-permute-start | bytes 393224 | tf_op jit(solution)/shard_map/ppermute | solution.py:47
  35.0 0.9 %copy-start.1 = (bf16[128,4,128]{2,1,0:T(4,128)(2,1)S(1)}, bf16[128,4,128]{2,1,0:T(4,128)(2,1)}, u32[]{:S(2)}) copy-start(bf16[128,4,128]{2,1,0:T(4,128)(2,1)} %concatenate.61) | copy-start | bytes 393220
  39.7 7.9 %collective-permute-start.8 = (bf16[2,128,512]{2,1,0:T(8,128)(2,1)S(1)}, bf16[2,128,512]{2,1,0:T(8,128)(2,1)S(1)}, u32[]{:S(2)}, u32[]{:S(2)}) collective-permute-start(bf16[2,128,512]{2,1,0:T(8,128)(2,1)S(1)} %maximum_select_fusion.5), channel_id=1, source_target_pairs={{0,8},{4,12},{8,0},{12,4},{16,24},{20,28},{24,16},{28,20},{1,9},{5... | collective-permute-start | bytes 786440 | tf_op jit(solution)/shard_map/ppermute | solution.py:47
  47.7 13.1 %collective-permute-start.9 = (bf16[4,128,512]{2,1,0:T(8,128)(2,1)S(1)}, bf16[4,128,512]{2,1,0:T(8,128)(2,1)S(1)}, u32[]{:S(2)}, u32[]{:S(2)}) collective-permute-start(bf16[4,128,512]{2,1,0:T(8,128)(2,1)S(1)} %maximum_select_fusion.3), channel_id=1, source_target_pairs={{0,4},{4,0},{8,12},{12,8},{16,20},{20,16},{24,28},{28,24},{1,5},{5... | collective-permute-start | bytes 1572872 | tf_op jit(solution)/shard_map/ppermute | solution.py:47
  49.0 11.0 %copy-start.4 = (f32[4]{0:T(128)S(1)}, f32[4]{0:T(128)}, u32[]{:S(2)}) copy-start(f32[4]{0:T(128)} %get-tuple-element.14) | copy-start | bytes 52
  49.0 11.0 %copy-start.5 = (f32[4]{0:T(128)S(1)}, f32[4]{0:T(128)}, u32[]{:S(2)}) copy-start(f32[4]{0:T(128)} %get-tuple-element.18) | copy-start | bytes 52
  49.0 11.0 %copy-start.6 = (f32[4]{0:T(128)S(1)}, f32[4]{0:T(128)}, u32[]{:S(2)}) copy-start(f32[4]{0:T(128)} %get-tuple-element.22) | copy-start | bytes 52
  49.0 11.0 %copy-start.7 = (f32[4]{0:T(128)S(1)}, f32[4]{0:T(128)}, u32[]{:S(2)}) copy-start(f32[4]{0:T(128)} %get-tuple-element.25) | copy-start | bytes 52
  49.0 11.0 %copy-start.8 = (f32[4]{0:T(128)S(1)}, f32[4]{0:T(128)}, u32[]{:S(2)}) copy-start(f32[4]{0:T(128)} %get-tuple-element.27) | copy-start | bytes 52
  63.5 6.4 %copy-start.3 = (f32[512]{0:T(512)S(1)}, f32[512]{0:T(512)}, u32[]{:S(2)}) copy-start(f32[512]{0:T(512)} %param.11) | copy-start | bytes 6148
  71.0 9.1 %copy-start.11 = (pred[4]{0:T(512)(128)(4,1)S(1)}, pred[4]{0:T(512)(128)(4,1)}, u32[]{:S(2)}) copy-start(pred[4]{0:T(512)(128)(4,1)} %copy-done.10) | copy-start | bytes 16
  71.3 5.8 %collective-permute-start.10 = (bf16[32,512]{1,0:T(8,128)(2,1)S(1)}, bf16[32,512]{1,0:T(8,128)(2,1)S(1)}, u32[]{:S(2)}, u32[]{:S(2)}) collective-permute-start(bf16[32,512]{1,0:T(8,128)(2,1)S(1)} %copy.77), channel_id=1, source_target_pairs={{0,1},{1,2},{2,3},{3,0},{4,5},{5,6},{6,7},{7,4},{8,9},{9,10},{10,1... | collective-permute-start | bytes 98312 | tf_op jit(solution)/shard_map/ppermute | solution.py:33
  74.1 5.2 %collective-permute-start.11 = (bf16[32,512]{1,0:T(8,128)(2,1)S(1)}, bf16[32,512]{1,0:T(8,128)(2,1)S(1)}, u32[]{:S(2)}, u32[]{:S(2)}) collective-permute-start(bf16[32,512]{1,0:T(8,128)(2,1)S(1)} %copy.78), channel_id=1, source_target_pairs={{0,2},{1,3},{2,0},{3,1},{4,6},{5,7},{6,4},{7,5},{8,10},{9,11},{10,... | collective-permute-start | bytes 98312 | tf_op jit(solution)/shard_map/ppermute | solution.py:33
  75.4 4.1 %collective-permute-start.12 = (bf16[32,512]{1,0:T(8,128)(2,1)S(1)}, bf16[32,512]{1,0:T(8,128)(2,1)S(1)}, u32[]{:S(2)}, u32[]{:S(2)}) collective-permute-start(bf16[32,512]{1,0:T(8,128)(2,1)S(1)} %copy.79), channel_id=1, source_target_pairs={{0,3},{1,0},{2,1},{3,2},{4,7},{5,4},{6,5},{7,6},{8,11},{9,8},{10,9... | collective-permute-start | bytes 98312 | tf_op jit(solution)/shard_map/ppermute | solution.py:33

commit v15 on v9

--- a/solution.py
+++ b/solution.py
@@ -83,8 +83,10 @@
     body = QCONV * KEY_BLOCK
     for block in range(blocks):
         start = pl.multiple_of((group * blocks + block) * KEY_BLOCK, KEY_BLOCK)
-        before = keys_ref[pl.ds(start, KEY_BLOCK), :]
-        current = keys_ref[pl.ds(start + KEY_BLOCK, KEY_BLOCK), :]
+        before_start = pl.multiple_of(jnp.maximum(start - KEY_BLOCK, 0), KEY_BLOCK)
+        before = keys_ref[pl.ds(before_start, KEY_BLOCK), :]
+        before = jnp.where(start > 0, before, jnp.zeros(before.shape, before.dtype))
+        current = keys_ref[pl.ds(start, KEY_BLOCK), :]
         conv_body = jnp.dot(
             high_ref[:body], current, preferred_element_type=jnp.float32
         ) + jnp.dot(low_ref[:body], current, preferred_element_type=jnp.float32)
@@ -113,7 +115,7 @@
 
 def conv_logits(shifted_t, score_kernel, key_pad):
     heads, contract, row_count = shifted_t.shape
-    seq_len = key_pad.shape[0] - KEY_BLOCK
+    seq_len = key_pad.shape[0]
     head_dim = key_pad.shape[1] // heads
     span = min(seq_len, KEY_SPAN)
     taps = (score_kernel * head_dim ** (-0.5)).reshape(-1)
@@ -217,9 +219,7 @@
     key_all, value_local = lax.optimization_barrier((key_all, value_local))
     value_all = gathered(value_local, "ctx").reshape((-1, width))
     seq_len = key_all.shape[0]
-    key_pad = jnp.concatenate(
-        [jnp.zeros((KEY_BLOCK, width), key_all.dtype), key_all], axis=0
-    )
+    key_pad = key_all
     edge = jnp.zeros((8, width), key_all.dtype)
     key_flat = jnp.concatenate([edge, key_all, edge], axis=0)
     band = band_terms(query_ext, query_first, key_flat, score_kernel)

time: 72.4 us -> 71.6 us (0.989)
  local copies, waits for them, and re-layouts: 12.9 us -> 11.6 us
    concatenate x1 -> x0, local copies, waits for them, and re-layouts: 1.12 us -> none  [shards(): jnp.concatenate([jnp.zeros((KEY_BLOCK, width), key_all.dtype), key_all],...]
  transfers between devices with their start and end apart: 13 -> 13, of which waited for: 9 -> 9; matrix products, arithmetic and copies ran while one was open for 17% -> 15% of each run, Pallas kernels for 15% -> 15%
where the time goes in v15:
time: 71.6 us; the launch traced here: 71.3 us
  starting transfers between devices  20.9 us (29%)
  waiting for transfers between devices  16.8 us (23%)
  local copies, waits for them, and re-layouts  11.6 us (16%)
  Pallas kernels  10.9 us (15%)
  other arithmetic  8.44 us (12%)
  matrix products  2.13 us (3%)
    ppermute x6, starting transfers between devices, exchanged(): received.append(lax.ppermute(outgoing, axis, pairs))  12.2 us
    pallas_call x1, Pallas kernels, conv_logits(): pl.pallas_call(logits_kernel, grid=(heads, seq_len // span), in_specs=[pl...  10.9 us
    ppermute x6, waiting for transfers between devices, gathered(): incoming = lax.ppermute(held, axis, [(i, i ^ bit) for i in range(peers)])  10.1 us
    ppermute x6, starting transfers between devices, gathered(): incoming = lax.ppermute(held, axis, [(i, i ^ bit) for i in range(peers)])  7.37 us
    ppermute x6, waiting for transfers between devices, exchanged(): received.append(lax.ppermute(outgoing, axis, pairs))  6.73 us
    div x1, other arithmetic, attend_chunk(): probabilities = expd / jnp.sum(expd, axis=1, keepdims=True)  3.88 us
    dot_general x1, matrix products, attend_chunk(): jnp.einsum('hki,khd->ihd', mixed_probs, value_heads, preferred_element_ty...  2.13 us
  transfers between devices with their start and end apart: 13, of which 9 were waited for; matrix products, arithmetic and copies ran while one was open for 15% of the time, Pallas kernels for 15%

profile of v15, /device:TPU:0, one launch (start us, length us, event | category | flops | bytes accessed | tf_op | source)
XLA Modules:
  0.0 71.3 jit_solution(6459244838579514571)
XLA Ops:
  0.0 1.1 %pad_maximum_fusion = bf16[3,32,2048]{2,1,0:T(8,128)(2,1)S(1)} fusion(bf16[1,32,2048]{2,1,0:T(8,128)(2,1)} %bitcast.92, bf16[1,32,2048]{2,1,0:T(8,128)(2,1)} %bitcast.93, bf16[1,32,2048]{2,1,0:T(8,128)(2,1)} %bitcast.94), kind=kLoop, calls=%fused_computation.40 | loop fusion | flops 393216 | bytes 786432 | tf_op jit(solution)/shard_map/stack | solution.py:199
  1.1 3.1 %collective-permute-start = (bf16[3,32,512]{2,1,0:T(8,128)(2,1)S(1)}, bf16[3,32,512]{2,1,0:T(8,128)(2,1)S(1)}, u32[]{:S(2)}, u32[]{:S(2)}) collective-permute-start(bf16[3,32,512]{2,1,0:T(8,128)(2,1)S(1)} %get-tuple-element.43), channel_id=1, source_target_pairs={{0,1},{1,2},{2,3},{3,0},{4,5},{5,6},{6,7},{7,4},{8,9},{9,10},{10,1... | collective-permute-start | bytes 294920 | tf_op jit(solution)/shard_map/ppermute | solution.py:33
  4.2 2.6 %collective-permute-start.1 = (bf16[3,32,512]{2,1,0:T(8,128)(2,1)S(1)}, bf16[3,32,512]{2,1,0:T(8,128)(2,1)S(1)}, u32[]{:S(2)}, u32[]{:S(2)}) collective-permute-start(bf16[3,32,512]{2,1,0:T(8,128)(2,1)S(1)} %get-tuple-element.42), channel_id=1, source_target_pairs={{0,2},{1,3},{2,0},{3,1},{4,6},{5,7},{6,4},{7,5},{8,10},{9,11},{10,... | collective-permute-start | bytes 294920 | tf_op jit(solution)/shard_map/ppermute | solution.py:33
  6.8 1.3 %collective-permute-start.2 = (bf16[3,32,512]{2,1,0:T(8,128)(2,1)S(1)}, bf16[3,32,512]{2,1,0:T(8,128)(2,1)S(1)}, u32[]{:S(2)}, u32[]{:S(2)}) collective-permute-start(bf16[3,32,512]{2,1,0:T(8,128)(2,1)S(1)} %get-tuple-element.41), channel_id=1, source_target_pairs={{0,3},{1,0},{2,1},{3,2},{4,7},{5,4},{6,5},{7,6},{8,11},{9,8},{10,9... | collective-permute-start | bytes 294920 | tf_op jit(solution)/shard_map/ppermute | solution.py:33
  8.2 1.2 %fusion.15 = (pred[1024,128]{1,0:T(8,128)(4,1)}, pred[1024,128]{1,0:T(8,128)(4,1)}, pred[1024,128]{1,0:T(8,128)(4,1)}, pred[1024,128]{1,0:T(8,128)(4,1)}, pred[1...) fusion(s32[128]{0:T(128)S(1)} %iota_add_fusion), kind=kLoop, calls=%fused_computation.39 | loop fusion | flops 917504 | bytes 786944 | tf_op jit(solution)/shard_map/ge | solution.py:175
  9.5 0.4 collective-permute-done
  9.9 3.5 %collective-permute-done.1 = bf16[3,32,512]{2,1,0:T(8,128)(2,1)S(1)} collective-permute-done((bf16[3,32,512]{2,1,0:T(8,128)(2,1)S(1)}, bf16[3,32,512]{2,1,0:T(8,128)(2,1)S(1)}, u32[]{:S(2)}, u32[]{:S(2)}) %collective-permute-start.1) | collective-permute-done | bytes 98336 | tf_op jit(solution)/shard_map/ppermute | solution.py:33
  13.5 0.6 gather_fusion
  14.1 0.1 select_bitcast_fusion
  14.2 0.7 fusion.55
  14.9 1.5 %collective-permute-start.3 = (bf16[1,128,512]{2,1,0:T(8,128)(2,1)S(1)}, bf16[1,128,512]{2,1,0:T(8,128)(2,1)S(1)}, u32[]{:S(2)}, u32[]{:S(2)}) collective-permute-start(bf16[1,128,512]{2,1,0:T(8,128)(2,1)S(1)} %bitcast.85), channel_id=1, source_target_pairs={{0,16},{4,20},{8,24},{12,28},{16,0},{20,4},{24,8},{28,12},{1,17},{... | collective-permute-start | bytes 393224 | tf_op jit(solution)/shard_map/ppermute | solution.py:47
  16.4 0.4 slice_reduce_fusion.17
  16.8 3.4 %collective-permute-done.3 = bf16[1,128,512]{2,1,0:T(8,128)(2,1)S(1)} collective-permute-done((bf16[1,128,512]{2,1,0:T(8,128)(2,1)S(1)}, bf16[1,128,512]{2,1,0:T(8,128)(2,1)S(1)}, u32[]{:S(2)}, u32[]{:S(2)}) %collective-permute-start.3) | collective-permute-done | bytes 131104 | tf_op jit(solution)/shard_map/ppermute | solution.py:47
  20.2 1.6 %collective-permute-start.4 = (bf16[2,128,512]{2,1,0:T(8,128)(2,1)S(1)}, bf16[2,128,512]{2,1,0:T(8,128)(2,1)S(1)}, u32[]{:S(2)}, u32[]{:S(2)}) collective-permute-start(bf16[2,128,512]{2,1,0:T(8,128)(2,1)S(1)} %maximum_select_fusion.4), channel_id=1, source_target_pairs={{0,8},{4,12},{8,0},{12,4},{16,24},{20,28},{24,16},{28,20},{1,9},{5... | collective-permute-start | bytes 786440 | tf_op jit(solution)/shard_map/ppermute | solution.py:47
  21.7 0.8 %slice_reduce_fusion.18 = (f32[4]{0:T(128)}, f32[4]{0:T(128)}, f32[4]{0:T(128)}, f32[4]{0:T(128)}) fusion(f32[1,4,4]{2,1,0:T(4,128)S(1)} %bitcast.99), kind=kLoop, calls=%fused_computation.136 | loop fusion | bytes 128 | tf_op jit(solution)/shard_map/slice | solution.py:183
  22.5 0.7 reshape.181.taps_ref
  23.2 1.3 %collective-permute-start.9 = (bf16[5,512]{1,0:T(8,128)(2,1)S(1)}, bf16[5,512]{1,0:T(8,128)(2,1)S(1)}, u32[]{:S(2)}, u32[]{:S(2)}) collective-permute-start(bf16[5,512]{1,0:T(8,128)(2,1)S(1)} %slice.270), channel_id=1, source_target_pairs={{0,4},{4,8},{8,12},{12,16},{16,20},{20,24},{24,28},{1,5},{5,9},{9,... | collective-permute-start | bytes 15368 | tf_op jit(solution)/shard_map/ppermute | solution.py:23
  24.6 0.1 copy.70
  24.7 0.7 concatenate.63
  25.4 0.1 pad_maximum_fusion.3
  25.5 0.1 copy.65
  25.6 0.1 copy.66
  25.8 0.1 copy.67
  25.9 0.1 copy.68
  26.0 0.1 copy.69
  26.2 1.3 %collective-permute-done.4 = bf16[2,128,512]{2,1,0:T(8,128)(2,1)S(1)} collective-permute-done((bf16[2,128,512]{2,1,0:T(8,128)(2,1)S(1)}, bf16[2,128,512]{2,1,0:T(8,128)(2,1)S(1)}, u32[]{:S(2)}, u32[]{:S(2)}) %collective-permute-start.4) | collective-permute-done | bytes 262176 | tf_op jit(solution)/shard_map/ppermute | solution.py:47
  27.8 1.8 %collective-permute-done.5 = bf16[4,128,512]{2,1,0:T(8,128)(2,1)S(1)} collective-permute-done((bf16[4,128,512]{2,1,0:T(8,128)(2,1)S(1)}, bf16[4,128,512]{2,1,0:T(8,128)(2,1)S(1)}, u32[]{:S(2)}, u32[]{:S(2)}) %collective-permute-start.5) | collective-permute-done | bytes 524320 | tf_op jit(solution)/shard_map/ppermute | solution.py:47
  29.5 0.2 maximum_select_fusion
  29.7 0.1 copy.62
  29.8 0.1 fusion.24
  29.9 0.1 fusion.56
  30.1 0.1 slice.221
  30.2 0.6 copy-done
  30.8 0.1 slice.225
  30.9 0.1 slice.231
  31.0 0.1 slice.239
  31.1 0.1 slice.249
  31.2 0.8 %fusion.21 = (f32[133,4]{1,0:T(8,128)S(1)}, f32[133,4]{1,0:T(8,128)S(1)}, f32[133,4]{1,0:T(8,128)S(1)}, f32[133,4]{1,0:T(8,128)S(1)}, f32[133,4]{1,0:T(8,128)S(1)}) fusion(f32[133,4,128]{2,1,0:T(4,128)S(1)} %slice.249, bf16[128,4,128]{2,1,0:T(4,128)(2,1)S(1)} %copy-done.3, bf16[5,4,128]{2,1,0:T(4,128)(2,1)S(1)} %concatenate.62, ...), kind=kLoop, calls=%fused_computation.52 | loop fusion | flops 814492 | bytes 1508752 | tf_op jit(solution)/shard_map/reduce_sum | solution.py:150
  32.1 0.1 copy.74
  32.2 0.1 copy.72
  32.3 0.1 copy.73
  32.4 4.0 %collective-permute-start.6 = (bf16[1,128,512]{2,1,0:T(8,128)(2,1)S(1)}, bf16[1,128,512]{2,1,0:T(8,128)(2,1)S(1)}, u32[]{:S(2)}, u32[]{:S(2)}) collective-permute-start(bf16[1,128,512]{2,1,0:T(8,128)(2,1)S(1)} %bitcast.83), channel_id=1, source_target_pairs={{0,16},{4,20},{8,24},{12,28},{16,0},{20,4},{24,8},{28,12},{1,17},{... | collective-permute-start | bytes 393224 | tf_op jit(solution)/shard_map/ppermute | solution.py:47
  36.4 3.7 %collective-permute-done.6 = bf16[1,128,512]{2,1,0:T(8,128)(2,1)S(1)} collective-permute-done((bf16[1,128,512]{2,1,0:T(8,128)(2,1)S(1)}, bf16[1,128,512]{2,1,0:T(8,128)(2,1)S(1)}, u32[]{:S(2)}, u32[]{:S(2)}) %collective-permute-start.6) | collective-permute-done | bytes 131104 | tf_op jit(solution)/shard_map/ppermute | solution.py:47
  40.2 0.1 collective-permute-start.7
  40.5 10.9 %shard_map.64 = f32[4,1024,128]{2,1,0:T(8,128)} custom-call(f32[264]{0:T(512)} %reshape.181.taps_ref, bf16[4,768,128]{2,1,0:T(8,128)(2,1)} %bitcast.82, bf16[1024,512]{1,0:T(8,128)(2,1)} %bitcast.76), custom_call_target="tpu_custom_call" | custom-call | tf_op jit(solution)/shard_map/pallas_call | solution.py:122
  51.4 0.1 fusion.44
  51.5 0.1 maximum_select_fusion.3
  51.6 3.9 %divide_bitcast_fusion = f32[1,4,1024,128]{3,2,1,0:T(8,128)S(1)} fusion(f32[4,1024,128]{2,1,0:T(8,128)} %shard_map.64, f32[4,128]{1,0:T(4,128)S(1)} %get-tuple-element.60, f32[4,128]{1,0:T(4,128)S(1)} %get-tuple-element.59, f32[4,128]{1,0:T(4,128)S(1)} %get-tuple-element.58, f32[4,128]{1,0:T(4,128)S(1)} %subtract_bitcast_fusion.3, f32[4,128]{1,0:T(4,128)S(1)} %fusion.44, ...), kind=kOutput, calls=%fused_computation.5 | output fusion | flops 6818814 | bytes 4990976 | tf_op jit(solution)/shard_map/div | solution.py:178
  55.5 1.4 %slice_bitcast_fusion.3 = (f32[1024,128]{1,0:T(8,128)}, f32[1024,128]{1,0:T(8,128)}, f32[1024,128]{1,0:T(8,128)}, f32[1024,128]{1,0:T(8,128)}) fusion(f32[1,4,1024,128]{3,2,1,0:T(8,128)S(1)} %divide_bitcast_fusion), kind=kLoop, calls=%fused_computation.30 | loop fusion | bytes 4194304 | tf_op jit(solution)/shard_map/mul | solution.py:183
  56.9 0.2 maximum_select_fusion.1
  57.1 0.9 %copy.63 = bf16[2,2,2,128,512]{3,2,1,0,4:T(2,128)(2,1)S(1)} copy(bf16[2,2,2,128,512]{4,3,0,1,2:T(8,128)(2,1)S(1)} %bitcast.77) | data formatting | bytes 2097152 | tf_op jit(solution)/shard_map/transpose | solution.py:55
  58.1 0.8 %reshape_reshape.3 = bf16[1024,4,128]{0,2,1:T(8,128)(2,1)S(1)} reshape(bf16[2,2,2,128,512]{3,2,1,0,4:T(2,128)(2,1)S(1)} %copy.63) | data formatting | bytes 2097152 | tf_op jit(solution)/shard_map/reshape;reshape | solution.py:230
  58.9 0.2 copy-done.5
  59.1 2.1 %multiply_reduce_fusion = (f32[128,4]{0,1:T(4,128)S(1)}, f32[128,4,128]{0,2,1:T(8,128)S(1)}) fusion(bf16[1024,4,128]{0,2,1:T(8,128)(2,1)S(1)} %reshape_reshape.3, f32[1024,128]{1,0:T(8,128)S(1)} %copy-done.5, f32[4]{0:T(128)S(1)} %copy-done.12, f32[1024,128]{1,0:T(8,128)} %get-tuple-element.35, f32[4]{0:T(128)S(1)} %copy-done.13, ...), kind=kOutput, calls=%fused_computation.56 | convolution fusion | flops 138542592 | bytes 3409984 | tf_op jit(solution)/shard_map/hki,khd->ihd/dot_general | solution.py:185
  61.3 0.1 multiply_convert_fusion
  61.4 0.2 constant_dynamic-slice_fusion.3
  61.8 2.7 %collective-permute-start.10 = (bf16[32,512]{1,0:T(8,128)(2,1)S(1)}, bf16[32,512]{1,0:T(8,128)(2,1)S(1)}, u32[]{:S(2)}, u32[]{:S(2)}) collective-permute-start(bf16[32,512]{1,0:T(8,128)(2,1)S(1)} %copy.81), channel_id=1, source_target_pairs={{0,1},{1,2},{2,3},{3,0},{4,5},{5,6},{6,7},{7,4},{8,9},{9,10},{10,1... | collective-permute-start | bytes 98312 | tf_op jit(solution)/shard_map/ppermute | solution.py:33
  64.6 1.2 %collective-permute-start.11 = (bf16[32,512]{1,0:T(8,128)(2,1)S(1)}, bf16[32,512]{1,0:T(8,128)(2,1)S(1)}, u32[]{:S(2)}, u32[]{:S(2)}) collective-permute-start(bf16[32,512]{1,0:T(8,128)(2,1)S(1)} %copy.82), channel_id=1, source_target_pairs={{0,2},{1,3},{2,0},{3,1},{4,6},{5,7},{6,4},{7,5},{8,10},{9,11},{10,... | collective-permute-start | bytes 98312 | tf_op jit(solution)/shard_map/ppermute | solution.py:33
  65.9 1.3 %collective-permute-start.12 = (bf16[32,512]{1,0:T(8,128)(2,1)S(1)}, bf16[32,512]{1,0:T(8,128)(2,1)S(1)}, u32[]{:S(2)}, u32[]{:S(2)}) collective-permute-start(bf16[32,512]{1,0:T(8,128)(2,1)S(1)} %copy.83), channel_id=1, source_target_pairs={{0,3},{1,0},{2,1},{3,2},{4,7},{5,4},{6,5},{7,6},{8,11},{9,8},{10,9... | collective-permute-start | bytes 98312 | tf_op jit(solution)/shard_map/ppermute | solution.py:33
  67.2 0.3 collective-permute-done.10
  67.5 2.3 %collective-permute-done.11 = bf16[32,512]{1,0:T(8,128)(2,1)S(1)} collective-permute-done((bf16[32,512]{1,0:T(8,128)(2,1)S(1)}, bf16[32,512]{1,0:T(8,128)(2,1)S(1)}, u32[]{:S(2)}, u32[]{:S(2)}) %collective-permute-start.11) | collective-permute-done | bytes 32800 | tf_op jit(solution)/shard_map/ppermute | solution.py:33
  69.8 0.2 collective-permute-done.12
  70.0 0.6 gather_fusion.1
  70.7 0.7 copy.85
  (69 shorter events, 1.4 us)
Async XLA Ops:
  1.1 15.3 %copy-start.6 = (f32[4,6,11]{2,0,1:T(4,128)S(1)}, f32[4,6,11]{2,0,1:T(4,128)}, u32[]{:S(2)}) copy-start(f32[4,6,11]{2,0,1:T(4,128)} %param.9) | copy-start | bytes 3172
  1.1 8.8 %collective-permute-start = (bf16[3,32,512]{2,1,0:T(8,128)(2,1)S(1)}, bf16[3,32,512]{2,1,0:T(8,128)(2,1)S(1)}, u32[]{:S(2)}, u32[]{:S(2)}) collective-permute-start(bf16[3,32,512]{2,1,0:T(8,128)(2,1)S(1)} %get-tuple-element.43), channel_id=1, source_target_pairs={{0,1},{1,2},{2,3},{3,0},{4,5},{5,6},{6,7},{7,4},{8,9},{9,10},{10,1... | collective-permute-start | bytes 294920 | tf_op jit(solution)/shard_map/ppermute | solution.py:33
  4.2 9.2 %collective-permute-start.1 = (bf16[3,32,512]{2,1,0:T(8,128)(2,1)S(1)}, bf16[3,32,512]{2,1,0:T(8,128)(2,1)S(1)}, u32[]{:S(2)}, u32[]{:S(2)}) collective-permute-start(bf16[3,32,512]{2,1,0:T(8,128)(2,1)S(1)} %get-tuple-element.42), channel_id=1, source_target_pairs={{0,2},{1,3},{2,0},{3,1},{4,6},{5,7},{6,4},{7,5},{8,10},{9,11},{10,... | collective-permute-start | bytes 294920 | tf_op jit(solution)/shard_map/ppermute | solution.py:33
  6.8 6.6 %collective-permute-start.2 = (bf16[3,32,512]{2,1,0:T(8,128)(2,1)S(1)}, bf16[3,32,512]{2,1,0:T(8,128)(2,1)S(1)}, u32[]{:S(2)}, u32[]{:S(2)}) collective-permute-start(bf16[3,32,512]{2,1,0:T(8,128)(2,1)S(1)} %get-tuple-element.41), channel_id=1, source_target_pairs={{0,3},{1,0},{2,1},{3,2},{4,7},{5,4},{6,5},{7,6},{8,11},{9,8},{10,9... | collective-permute-start | bytes 294920 | tf_op jit(solution)/shard_map/ppermute | solution.py:33
  8.2 13.5 %copy-start.7 = (f32[4,4]{1,0:T(4,128)S(1)}, f32[4,4]{1,0:T(4,128)}, u32[]{:S(2)}) copy-start(f32[4,4]{1,0:T(4,128)} %param.10) | copy-start | bytes 196
  9.5 15.1 %copy-start.9 = (pred[4]{0:T(512)(128)(4,1)}, pred[4]{0:T(512)(128)(4,1)S(1)}, u32[]{:S(2)}) copy-start(pred[4]{0:T(512)(128)(4,1)S(1)} %compare_and_fusion) | copy-start | bytes 16
  14.9 5.3 %collective-permute-start.3 = (bf16[1,128,512]{2,1,0:T(8,128)(2,1)S(1)}, bf16[1,128,512]{2,1,0:T(8,128)(2,1)S(1)}, u32[]{:S(2)}, u32[]{:S(2)}) collective-permute-start(bf16[1,128,512]{2,1,0:T(8,128)(2,1)S(1)} %bitcast.85), channel_id=1, source_target_pairs={{0,16},{4,20},{8,24},{12,28},{16,0},{20,4},{24,8},{28,12},{1,17},{... | collective-permute-start | bytes 393224 | tf_op jit(solution)/shard_map/ppermute | solution.py:47
  20.2 7.3 %collective-permute-start.4 = (bf16[2,128,512]{2,1,0:T(8,128)(2,1)S(1)}, bf16[2,128,512]{2,1,0:T(8,128)(2,1)S(1)}, u32[]{:S(2)}, u32[]{:S(2)}) collective-permute-start(bf16[2,128,512]{2,1,0:T(8,128)(2,1)S(1)} %maximum_select_fusion.4), channel_id=1, source_target_pairs={{0,8},{4,12},{8,0},{12,4},{16,24},{20,28},{24,16},{28,20},{1,9},{5... | collective-permute-start | bytes 786440 | tf_op jit(solution)/shard_map/ppermute | solution.py:47
  23.2 2.1 %collective-permute-start.9 = (bf16[5,512]{1,0:T(8,128)(2,1)S(1)}, bf16[5,512]{1,0:T(8,128)(2,1)S(1)}, u32[]{:S(2)}, u32[]{:S(2)}) collective-permute-start(bf16[5,512]{1,0:T(8,128)(2,1)S(1)} %slice.270), channel_id=1, source_target_pairs={{0,4},{4,8},{8,12},{12,16},{16,20},{20,24},{24,28},{1,5},{5,9},{9,... | collective-permute-start | bytes 15368 | tf_op jit(solution)/shard_map/ppermute | solution.py:23
  27.5 2.0 %collective-permute-start.5 = (bf16[4,128,512]{2,1,0:T(8,128)(2,1)S(1)}, bf16[4,128,512]{2,1,0:T(8,128)(2,1)S(1)}, u32[]{:S(2)}, u32[]{:S(2)}) collective-permute-start(bf16[4,128,512]{2,1,0:T(8,128)(2,1)S(1)} %maximum_select_fusion.2), channel_id=1, source_target_pairs={{0,4},{4,0},{8,12},{12,8},{16,20},{20,16},{24,28},{28,24},{1,5},{5... | collective-permute-start | bytes 1572872 | tf_op jit(solution)/shard_map/ppermute | solution.py:47
  27.8 2.0 %copy-start.1 = (bf16[128,4,6,128]{0,3,2,1:T(8,128)(2,1)}, bf16[128,4,6,128]{0,3,2,1:T(8,128)(2,1)S(1)}, u32[]{:S(2)}) copy-start(bf16[128,4,6,128]{0,3,2,1:T(8,128)(2,1)S(1)} %constant_dynamic-update-slice_fusion) | copy-start | bytes 2359300
  29.8 1.0 %copy-start = (bf16[2,2,2,128,512]{4,3,2,1,0:T(8,128)(2,1)}, bf16[2,2,2,128,512]{4,3,2,1,0:T(8,128)(2,1)S(1)}, u32[]{:S(2)}) copy-start(bf16[2,2,2,128,512]{4,3,2,1,0:T(8,128)(2,1)S(1)} %copy.62) | copy-start | bytes 3145732
  29.9 1.3 %copy-start.3 = (bf16[128,4,128]{2,1,0:T(4,128)(2,1)S(1)}, bf16[128,4,128]{2,1,0:T(4,128)(2,1)}, u32[]{:S(2)}) copy-start(bf16[128,4,128]{2,1,0:T(4,128)(2,1)} %concatenate.63) | copy-start | bytes 393220
  30.8 1.6 %copy-start.2 = (bf16[1,4,32,512]{3,2,0,1:T(8,128)(2,1)S(1)}, bf16[1,4,32,512]{3,2,0,1:T(8,128)(2,1)}, u32[]{:S(2)}) copy-start(bf16[1,4,32,512]{3,2,0,1:T(8,128)(2,1)} %get-tuple-element.38) | copy-start | bytes 393220
  32.4 7.8 %collective-permute-start.6 = (bf16[1,128,512]{2,1,0:T(8,128)(2,1)S(1)}, bf16[1,128,512]{2,1,0:T(8,128)(2,1)S(1)}, u32[]{:S(2)}, u32[]{:S(2)}) collective-permute-start(bf16[1,128,512]{2,1,0:T(8,128)(2,1)S(1)} %bitcast.83), channel_id=1, source_target_pairs={{0,16},{4,20},{8,24},{12,28},{16,0},{20,4},{24,8},{28,12},{1,17},{... | collective-permute-start | bytes 393224 | tf_op jit(solution)/shard_map/ppermute | solution.py:47
  40.2 11.3 %collective-permute-start.7 = (bf16[2,128,512]{2,1,0:T(8,128)(2,1)S(1)}, bf16[2,128,512]{2,1,0:T(8,128)(2,1)S(1)}, u32[]{:S(2)}, u32[]{:S(2)}) collective-permute-start(bf16[2,128,512]{2,1,0:T(8,128)(2,1)S(1)} %maximum_select_fusion.5), channel_id=1, source_target_pairs={{0,8},{4,12},{8,0},{12,4},{16,24},{20,28},{24,16},{28,20},{1,9},{5... | collective-permute-start | bytes 786440 | tf_op jit(solution)/shard_map/ppermute | solution.py:47
  51.6 5.4 %collective-permute-start.8 = (bf16[4,128,512]{2,1,0:T(8,128)(2,1)S(1)}, bf16[4,128,512]{2,1,0:T(8,128)(2,1)S(1)}, u32[]{:S(2)}, u32[]{:S(2)}) collective-permute-start(bf16[4,128,512]{2,1,0:T(8,128)(2,1)S(1)} %maximum_select_fusion.3), channel_id=1, source_target_pairs={{0,4},{4,0},{8,12},{12,8},{16,20},{20,16},{24,28},{28,24},{1,5},{5... | collective-permute-start | bytes 1572872 | tf_op jit(solution)/shard_map/ppermute | solution.py:47
  57.1 1.8 %copy-start.4 = (f32[1024,128]{1,0:T(8,128)S(1)}, f32[1024,128]{1,0:T(8,128)}, u32[]{:S(2)}) copy-start(f32[1024,128]{1,0:T(8,128)} %get-tuple-element.33) | copy-start | bytes 1572868
  57.1 1.8 %copy-start.11 = (f32[4]{0:T(128)S(1)}, f32[4]{0:T(128)}, u32[]{:S(2)}) copy-start(f32[4]{0:T(128)} %get-tuple-element.29) | copy-start | bytes 52
  57.1 1.8 %copy-start.12 = (f32[4]{0:T(128)S(1)}, f32[4]{0:T(128)}, u32[]{:S(2)}) copy-start(f32[4]{0:T(128)} %get-tuple-element.30) | copy-start | bytes 52
  57.1 1.8 %copy-start.13 = (f32[4]{0:T(128)S(1)}, f32[4]{0:T(128)}, u32[]{:S(2)}) copy-start(f32[4]{0:T(128)} %get-tuple-element.31) | copy-start | bytes 52
  58.1 1.1 %copy-start.5 = (f32[1024,128]{1,0:T(8,128)S(1)}, f32[1024,128]{1,0:T(8,128)}, u32[]{:S(2)}) copy-start(f32[1024,128]{1,0:T(8,128)} %get-tuple-element.34) | copy-start | bytes 1572868
  58.1 1.0 %copy-start.14 = (f32[4]{0:T(128)S(1)}, f32[4]{0:T(128)}, u32[]{:S(2)}) copy-start(f32[4]{0:T(128)} %get-tuple-element.32) | copy-start | bytes 52
  59.1 2.2 %copy-start.8 = (f32[512]{0:T(512)S(1)}, f32[512]{0:T(512)}, u32[]{:S(2)}) copy-start(f32[512]{0:T(512)} %param.11) | copy-start | bytes 6148
  61.3 9.3 %copy-start.10 = (pred[4]{0:T(512)(128)(4,1)S(1)}, pred[4]{0:T(512)(128)(4,1)}, u32[]{:S(2)}) copy-start(pred[4]{0:T(512)(128)(4,1)} %copy-done.9) | copy-start | bytes 16
  61.8 5.8 %collective-permute-start.10 = (bf16[32,512]{1,0:T(8,128)(2,1)S(1)}, bf16[32,512]{1,0:T(8,128)(2,1)S(1)}, u32[]{:S(2)}, u32[]{:S(2)}) collective-permute-start(bf16[32,512]{1,0:T(8,128)(2,1)S(1)} %copy.81), channel_id=1, source_target_pairs={{0,1},{1,2},{2,3},{3,0},{4,5},{5,6},{6,7},{7,4},{8,9},{9,10},{10,1... | collective-permute-start | bytes 98312 | tf_op jit(solution)/shard_map/ppermute | solution.py:33
  64.6 5.2 %collective-permute-start.11 = (bf16[32,512]{1,0:T(8,128)(2,1)S(1)}, bf16[32,512]{1,0:T(8,128)(2,1)S(1)}, u32[]{:S(2)}, u32[]{:S(2)}) collective-permute-start(bf16[32,512]{1,0:T(8,128)(2,1)S(1)} %copy.82), channel_id=1, source_target_pairs={{0,2},{1,3},{2,0},{3,1},{4,6},{5,7},{6,4},{7,5},{8,10},{9,11},{10,... | collective-permute-start | bytes 98312 | tf_op jit(solution)/shard_map/ppermute | solution.py:33
  65.9 4.1 %collective-permute-start.12 = (bf16[32,512]{1,0:T(8,128)(2,1)S(1)}, bf16[32,512]{1,0:T(8,128)(2,1)S(1)}, u32[]{:S(2)}, u32[]{:S(2)}) collective-permute-start(bf16[32,512]{1,0:T(8,128)(2,1)S(1)} %copy.83), channel_id=1, source_target_pairs={{0,3},{1,0},{2,1},{3,2},{4,7},{5,4},{6,5},{7,6},{8,11},{9,8},{10,9... | collective-permute-start | bytes 98312 | tf_op jit(solution)/shard_map/ppermute | solution.py:33

commit v16 on v15

--- a/solution.py
+++ b/solution.py
@@ -42,7 +42,7 @@
         return lax.all_gather(shard, axis, axis=0, tiled=False)
     bits = peers.bit_length() - 1
     held = shard[None]
-    for level in reversed(range(bits)):
+    for level in range(bits):
         bit = 1 << level
         incoming = lax.ppermute(held, axis, [(i, i ^ bit) for i in range(peers)])
         upper = (place & bit) != 0
@@ -51,8 +51,7 @@
             jnp.concatenate([incoming, held], axis=0),
             jnp.concatenate([held, incoming], axis=0),
         )
-    held = held.reshape((2,) * bits + shard.shape)
-    return jnp.transpose(held, tuple(reversed(range(bits))) + tuple(range(bits, held.ndim)))
+    return held.reshape((peers,) + shard.shape)
 
 
 def logits_kernel(taps_ref, query_ref, keys_ref, out_ref, high_ref, low_ref, conv_ref):

time: 71.6 us -> 85.7 us (1.20)
  waiting for transfers between devices: 16.8 us -> 31.1 us
  other arithmetic: 8.44 us -> 9.36 us
    ppermute x6, waiting for transfers between devices: 10.1 us -> 21 us  [gathered(): incoming = lax.ppermute(held, axis, [(i, i ^ bit) for i in range(peers)])]
    ppermute x6, waiting for transfers between devices: 6.73 us -> 10 us  [exchanged(): received.append(lax.ppermute(outgoing, axis, pairs))]
    ppermute x6, starting transfers between devices: 12.2 us -> 10.6 us  [exchanged(): received.append(lax.ppermute(outgoing, axis, pairs))]
    transpose x2 -> x0, local copies, waits for them, and re-layouts: 1.04 us -> none  [gathered(): jnp.transpose(held, tuple(reversed(range(bits))) + tuple(range(bits, held...]
    reduce_sum x1, other arithmetic: 0.79 us -> 1.71 us  [band_terms(): jnp.sum(query_heads * near_heads[lag - 1:lag - 1 + ext_count], axis=2)]
    unnamed x39 -> x47, local copies, waits for them, and re-layouts: 1.28 us -> 1.89 us
  transfers between devices with their start and end apart: 13 -> 13, of which waited for: 9 -> 10; matrix products, arithmetic and copies ran while one was open for 15% -> 13% of each run, Pallas kernels for 15% -> 13%
where the time goes in v16:
time: 85.7 us; the launch traced here: 85.5 us
  waiting for transfers between devices  31.1 us (36%)
  starting transfers between devices  20.1 us (23%)
  local copies, waits for them, and re-layouts  11.2 us (13%)
  Pallas kernels  10.9 us (13%)
  other arithmetic  9.36 us (11%)
  matrix products  2.17 us (3%)
    ppermute x6, waiting for transfers between devices, gathered(): incoming = lax.ppermute(held, axis, [(i, i ^ bit) for i in range(peers)])  21 us
    pallas_call x1, Pallas kernels, conv_logits(): pl.pallas_call(logits_kernel, grid=(heads, seq_len // span), in_specs=[pl...  10.9 us
    ppermute x6, starting transfers between devices, exchanged(): received.append(lax.ppermute(outgoing, axis, pairs))  10.6 us
    ppermute x6, waiting for transfers between devices, exchanged(): received.append(lax.ppermute(outgoing, axis, pairs))  10 us
    ppermute x6, starting transfers between devices, gathered(): incoming = lax.ppermute(held, axis, [(i, i ^ bit) for i in range(peers)])  7.78 us
    div x1, other arithmetic, attend_chunk(): probabilities = expd / jnp.sum(expd, axis=1, keepdims=True)  3.87 us
    dot_general x1, matrix products, attend_chunk(): jnp.einsum('hki,khd->ihd', mixed_probs, value_heads, preferred_element_ty...  2.17 us
    unnamed x47, local copies, waits for them, and re-layouts  1.89 us
  transfers between devices with their start and end apart: 13, of which 10 were waited for; matrix products, arithmetic and copies ran while one was open for 13% of the time, Pallas kernels for 13%

profile of v16, /device:TPU:0, one launch (start us, length us, event | category | flops | bytes accessed | tf_op | source)
XLA Modules:
  0.0 85.5 jit_solution(10046941251570754412)
XLA Ops:
  0.0 1.1 %pad_maximum_fusion = bf16[3,32,2048]{2,1,0:T(8,128)(2,1)S(1)} fusion(bf16[1,32,2048]{2,1,0:T(8,128)(2,1)} %bitcast.81, bf16[1,32,2048]{2,1,0:T(8,128)(2,1)} %bitcast.82, bf16[1,32,2048]{2,1,0:T(8,128)(2,1)} %bitcast.83), kind=kLoop, calls=%fused_computation.41 | loop fusion | flops 393216 | bytes 786432 | tf_op jit(solution)/shard_map/stack | solution.py:198
  1.1 5.1 %collective-permute-start.2 = (bf16[3,32,512]{2,1,0:T(8,128)(2,1)S(1)}, bf16[3,32,512]{2,1,0:T(8,128)(2,1)S(1)}, u32[]{:S(2)}, u32[]{:S(2)}) collective-permute-start(bf16[3,32,512]{2,1,0:T(8,128)(2,1)S(1)} %get-tuple-element.41), channel_id=1, source_target_pairs={{0,3},{1,0},{2,1},{3,2},{4,7},{5,4},{6,5},{7,6},{8,11},{9,8},{10,9... | collective-permute-start | bytes 294920 | tf_op jit(solution)/shard_map/ppermute | solution.py:33
  6.2 1.0 %collective-permute-start = (bf16[3,32,512]{2,1,0:T(8,128)(2,1)S(1)}, bf16[3,32,512]{2,1,0:T(8,128)(2,1)S(1)}, u32[]{:S(2)}, u32[]{:S(2)}) collective-permute-start(bf16[3,32,512]{2,1,0:T(8,128)(2,1)S(1)} %get-tuple-element.43), channel_id=1, source_target_pairs={{0,1},{1,2},{2,3},{3,0},{4,5},{5,6},{6,7},{7,4},{8,9},{9,10},{10,1... | collective-permute-start | bytes 294920 | tf_op jit(solution)/shard_map/ppermute | solution.py:33
  7.3 1.2 %fusion.16 = (pred[1024,128]{1,0:T(8,128)(4,1)}, pred[1024,128]{1,0:T(8,128)(4,1)}, pred[1024,128]{1,0:T(8,128)(4,1)}, pred[1024,128]{1,0:T(8,128)(4,1)}, pred[1...) fusion(s32[128]{0:T(128)S(1)} %iota_add_fusion), kind=kLoop, calls=%fused_computation.40 | loop fusion | flops 917504 | bytes 786944 | tf_op jit(solution)/shard_map/ge | solution.py:174
  8.6 0.9 %collective-permute-done.2 = bf16[3,32,512]{2,1,0:T(8,128)(2,1)S(1)} collective-permute-done((bf16[3,32,512]{2,1,0:T(8,128)(2,1)S(1)}, bf16[3,32,512]{2,1,0:T(8,128)(2,1)S(1)}, u32[]{:S(2)}, u32[]{:S(2)}) %collective-permute-start.2) | collective-permute-done | bytes 98336 | tf_op jit(solution)/shard_map/ppermute | solution.py:33
  9.4 5.5 %collective-permute-done.1 = bf16[3,32,512]{2,1,0:T(8,128)(2,1)S(1)} collective-permute-done((bf16[3,32,512]{2,1,0:T(8,128)(2,1)S(1)}, bf16[3,32,512]{2,1,0:T(8,128)(2,1)S(1)}, u32[]{:S(2)}, u32[]{:S(2)}) %collective-permute-start.1) | collective-permute-done | bytes 98336 | tf_op jit(solution)/shard_map/ppermute | solution.py:33
  15.0 0.6 gather_fusion
  15.6 0.1 select_bitcast_fusion
  15.7 0.7 fusion.56
  16.4 0.9 %slice_reduce_fusion.17 = (f32[4]{0:T(128)}, f32[4]{0:T(128)S(1)}, f32[4]{0:T(128)S(1)}, f32[4]{0:T(128)S(1)}, f32[4]{0:T(128)}, /*index=5*/f32[4]{0:T(128)S(1)}...) fusion(f32[4,6,11]{2,0,1:T(4,128)S(1)} %copy-done.5), kind=kLoop, calls=%fused_computation.136 | loop fusion | bytes 480 | tf_op jit(solution)/shard_map/slice | solution.py:158
  17.4 0.4 collective-permute-done.3
  17.8 1.6 %collective-permute-start.4 = (bf16[2,128,512]{2,1,0:T(8,128)(2,1)S(1)}, bf16[2,128,512]{2,1,0:T(8,128)(2,1)S(1)}, u32[]{:S(2)}, u32[]{:S(2)}) collective-permute-start(bf16[2,128,512]{2,1,0:T(8,128)(2,1)S(1)} %maximum_select_fusion.4), channel_id=1, source_target_pairs={{0,8},{4,12},{8,0},{12,4},{16,24},{20,28},{24,16},{28,20},{1,9},{5... | collective-permute-start | bytes 786440 | tf_op jit(solution)/shard_map/ppermute | solution.py:47
  19.4 0.8 slice_reduce_fusion.18
  20.1 0.7 reshape.176.taps_ref
  20.8 0.1 copy.66
  21.0 1.8 %collective-permute-start.9 = (bf16[5,512]{1,0:T(8,128)(2,1)S(1)}, bf16[5,512]{1,0:T(8,128)(2,1)S(1)}, u32[]{:S(2)}, u32[]{:S(2)}) collective-permute-start(bf16[5,512]{1,0:T(8,128)(2,1)S(1)} %slice.270), channel_id=1, source_target_pairs={{0,4},{4,8},{8,12},{12,16},{16,20},{20,24},{24,28},{1,5},{5,9},{9,... | collective-permute-start | bytes 15368 | tf_op jit(solution)/shard_map/ppermute | solution.py:23
  22.8 0.7 concatenate.63
  23.5 0.1 collective-permute-done.9
  23.6 0.1 pad_maximum_fusion.3
  23.7 0.1 copy.61
  23.9 0.1 copy.62
  24.0 0.1 copy.63
  24.1 0.1 copy.64
  24.2 0.1 copy.65
  24.4 1.8 %collective-permute-done.4 = bf16[2,128,512]{2,1,0:T(8,128)(2,1)S(1)} collective-permute-done((bf16[2,128,512]{2,1,0:T(8,128)(2,1)S(1)}, bf16[2,128,512]{2,1,0:T(8,128)(2,1)S(1)}, u32[]{:S(2)}, u32[]{:S(2)}) %collective-permute-start.4) | collective-permute-done | bytes 262176 | tf_op jit(solution)/shard_map/ppermute | solution.py:47
  26.3 3.0 %collective-permute-start.5 = (bf16[4,128,512]{2,1,0:T(8,128)(2,1)S(1)}, bf16[4,128,512]{2,1,0:T(8,128)(2,1)S(1)}, u32[]{:S(2)}, u32[]{:S(2)}) collective-permute-start(bf16[4,128,512]{2,1,0:T(8,128)(2,1)S(1)} %maximum_select_fusion.2), channel_id=1, source_target_pairs={{0,16},{4,20},{8,24},{12,28},{16,0},{20,4},{24,8},{28,12},{1,17},{... | collective-permute-start | bytes 1572872 | tf_op jit(solution)/shard_map/ppermute | solution.py:47
  29.5 10.0 %collective-permute-done.5 = bf16[4,128,512]{2,1,0:T(8,128)(2,1)S(1)} collective-permute-done((bf16[4,128,512]{2,1,0:T(8,128)(2,1)S(1)}, bf16[4,128,512]{2,1,0:T(8,128)(2,1)S(1)}, u32[]{:S(2)}, u32[]{:S(2)}) %collective-permute-start.5) | collective-permute-done | bytes 524320 | tf_op jit(solution)/shard_map/ppermute | solution.py:47
  39.5 0.2 maximum_select_fusion
  39.7 0.1 fusion.25
  39.8 0.1 fusion.57
  40.0 0.1 slice.249
  40.1 0.6 copy-done
  40.7 0.1 slice.239
  40.8 0.1 slice.231
  40.9 0.1 slice.225
  41.0 0.1 slice.221
  41.1 1.7 %fusion.22 = (f32[133,4]{1,0:T(8,128)S(1)}, f32[133,4]{1,0:T(8,128)S(1)}, f32[133,4]{1,0:T(8,128)S(1)}, f32[133,4]{1,0:T(8,128)S(1)}, f32[133,4]{1,0:T(8,128)S(1)}) fusion(f32[133,4,128]{2,1,0:T(4,128)S(1)} %slice.249, bf16[128,4,128]{2,1,0:T(4,128)(2,1)} %concatenate.63, bf16[5,4,128]{2,1,0:T(4,128)(2,1)S(1)} %concatenate.62, ...), kind=kLoop, calls=%fused_computation.53 | loop fusion | flops 814492 | bytes 1508752 | tf_op jit(solution)/shard_map/reduce_sum | solution.py:149
  42.9 0.1 copy.68
  43.0 0.1 copy.70
  43.0 0.1 copy.67
  43.3 1.2 %collective-permute-done.6 = bf16[1,128,512]{2,1,0:T(8,128)(2,1)S(1)} collective-permute-done((bf16[1,128,512]{2,1,0:T(8,128)(2,1)S(1)}, bf16[1,128,512]{2,1,0:T(8,128)(2,1)S(1)}, u32[]{:S(2)}, u32[]{:S(2)}) %collective-permute-start.6) | collective-permute-done | bytes 131104 | tf_op jit(solution)/shard_map/ppermute | solution.py:47
  44.6 2.1 %collective-permute-start.7 = (bf16[2,128,512]{2,1,0:T(8,128)(2,1)S(1)}, bf16[2,128,512]{2,1,0:T(8,128)(2,1)S(1)}, u32[]{:S(2)}, u32[]{:S(2)}) collective-permute-start(bf16[2,128,512]{2,1,0:T(8,128)(2,1)S(1)} %maximum_select_fusion.5), channel_id=1, source_target_pairs={{0,8},{4,12},{8,0},{12,4},{16,24},{20,28},{24,16},{28,20},{1,9},{5... | collective-permute-start | bytes 786440 | tf_op jit(solution)/shard_map/ppermute | solution.py:47
  46.9 10.9 %shard_map.64 = f32[4,1024,128]{2,1,0:T(8,128)} custom-call(f32[264]{0:T(512)} %reshape.176.taps_ref, bf16[4,768,128]{2,1,0:T(8,128)(2,1)} %bitcast.71, bf16[1024,512]{1,0:T(8,128)(2,1)} %bitcast.67), custom_call_target="tpu_custom_call" | custom-call | tf_op jit(solution)/shard_map/pallas_call | solution.py:121
  57.8 0.1 fusion.45
  57.9 0.1 maximum_select_fusion.3
  58.0 1.0 %collective-permute-start.8 = (bf16[4,128,512]{2,1,0:T(8,128)(2,1)S(1)}, bf16[4,128,512]{2,1,0:T(8,128)(2,1)S(1)}, u32[]{:S(2)}, u32[]{:S(2)}) collective-permute-start(bf16[4,128,512]{2,1,0:T(8,128)(2,1)S(1)} %maximum_select_fusion.3), channel_id=1, source_target_pairs={{0,16},{4,20},{8,24},{12,28},{16,0},{20,4},{24,8},{28,12},{1,17},{... | collective-permute-start | bytes 1572872 | tf_op jit(solution)/shard_map/ppermute | solution.py:47
  59.0 3.9 %divide_bitcast_fusion = f32[1,4,1024,128]{3,2,1,0:T(8,128)S(1)} fusion(f32[4,1024,128]{2,1,0:T(8,128)} %shard_map.64, f32[4,128]{1,0:T(4,128)S(1)} %get-tuple-element.60, f32[4,128]{1,0:T(4,128)S(1)} %get-tuple-element.59, f32[4,128]{1,0:T(4,128)S(1)} %get-tuple-element.58, f32[4,128]{1,0:T(4,128)S(1)} %subtract_bitcast_fusion.3, f32[4,128]{1,0:T(4,128)S(1)} %fusion.45, ...), kind=kOutput, calls=%fused_computation.5 | output fusion | flops 6818814 | bytes 4990976 | tf_op jit(solution)/shard_map/div | solution.py:177
  62.9 1.4 %slice_bitcast_fusion.3 = (f32[1024,128]{1,0:T(8,128)}, f32[1024,128]{1,0:T(8,128)}, f32[1024,128]{1,0:T(8,128)}, f32[1024,128]{1,0:T(8,128)}) fusion(f32[1,4,1024,128]{3,2,1,0:T(8,128)S(1)} %divide_bitcast_fusion), kind=kLoop, calls=%fused_computation.31 | loop fusion | bytes 4194304 | tf_op jit(solution)/shard_map/mul | solution.py:182
  64.3 7.5 %collective-permute-done.8 = bf16[4,128,512]{2,1,0:T(8,128)(2,1)S(1)} collective-permute-done((bf16[4,128,512]{2,1,0:T(8,128)(2,1)S(1)}, bf16[4,128,512]{2,1,0:T(8,128)(2,1)S(1)}, u32[]{:S(2)}, u32[]{:S(2)}) %collective-permute-start.8) | collective-permute-done | bytes 524320 | tf_op jit(solution)/shard_map/ppermute | solution.py:47
  71.8 0.2 maximum_select_fusion.1
  71.9 0.3 reshape.197
  72.3 0.7 copy-done.3
  73.0 0.2 copy-done.4
  73.1 2.2 %multiply_reduce_fusion = (f32[128,4]{0,1:T(4,128)S(1)}, f32[128,4,128]{0,2,1:T(8,128)S(1)}) fusion(f32[1024,128]{1,0:T(8,128)S(1)} %copy-done.4, f32[4]{0:T(128)S(1)} %copy-done.16, f32[1024,128]{1,0:T(8,128)} %get-tuple-element.35, f32[4]{0:T(128)S(1)} %copy-done.17, f32[1024,128]{1,0:T(8,128)} %get-tuple-element.36, f32[4]{0:T(128)S(1)} %copy-done.18, ...), kind=kOutput, calls=%fused_computation.57 | convolution fusion | flops 138542592 | bytes 3409984 | tf_op jit(solution)/shard_map/hki,khd->ihd/dot_general | solution.py:184
  75.3 0.1 multiply_convert_fusion
  75.5 0.2 constant_dynamic-slice_fusion.3
  75.8 2.0 %collective-permute-start.12 = (bf16[32,512]{1,0:T(8,128)(2,1)S(1)}, bf16[32,512]{1,0:T(8,128)(2,1)S(1)}, u32[]{:S(2)}, u32[]{:S(2)}) collective-permute-start(bf16[32,512]{1,0:T(8,128)(2,1)S(1)} %copy.80), channel_id=1, source_target_pairs={{0,3},{1,0},{2,1},{3,2},{4,7},{5,4},{6,5},{7,6},{8,11},{9,8},{10,9... | collective-permute-start | bytes 98312 | tf_op jit(solution)/shard_map/ppermute | solution.py:33
  77.9 0.4 collective-permute-start.11
  78.3 2.1 %collective-permute-start.10 = (bf16[32,512]{1,0:T(8,128)(2,1)S(1)}, bf16[32,512]{1,0:T(8,128)(2,1)S(1)}, u32[]{:S(2)}, u32[]{:S(2)}) collective-permute-start(bf16[32,512]{1,0:T(8,128)(2,1)S(1)} %copy.78), channel_id=1, source_target_pairs={{0,1},{1,2},{2,3},{3,0},{4,5},{5,6},{6,7},{7,4},{8,9},{9,10},{10,1... | collective-permute-start | bytes 98312 | tf_op jit(solution)/shard_map/ppermute | solution.py:33
  80.5 2.2 %collective-permute-done.11 = bf16[32,512]{1,0:T(8,128)(2,1)S(1)} collective-permute-done((bf16[32,512]{1,0:T(8,128)(2,1)S(1)}, bf16[32,512]{1,0:T(8,128)(2,1)S(1)}, u32[]{:S(2)}, u32[]{:S(2)}) %collective-permute-start.11) | collective-permute-done | bytes 32800 | tf_op jit(solution)/shard_map/ppermute | solution.py:33
  82.7 1.4 %collective-permute-done.10 = bf16[32,512]{1,0:T(8,128)(2,1)S(1)} collective-permute-done((bf16[32,512]{1,0:T(8,128)(2,1)S(1)}, bf16[32,512]{1,0:T(8,128)(2,1)S(1)}, u32[]{:S(2)}, u32[]{:S(2)}) %collective-permute-start.10) | collective-permute-done | bytes 32800 | tf_op jit(solution)/shard_map/ppermute | solution.py:33
  84.1 0.6 gather_fusion.1
  84.7 0.1 select_bitcast_fusion.1
  84.8 0.7 copy.82
  (75 shorter events, 1.2 us)
Async XLA Ops:
  1.1 15.3 %copy-start.5 = (f32[4,6,11]{2,0,1:T(4,128)S(1)}, f32[4,6,11]{2,0,1:T(4,128)}, u32[]{:S(2)}) copy-start(f32[4,6,11]{2,0,1:T(4,128)} %param.9) | copy-start | bytes 3172
  1.1 8.3 %collective-permute-start.2 = (bf16[3,32,512]{2,1,0:T(8,128)(2,1)S(1)}, bf16[3,32,512]{2,1,0:T(8,128)(2,1)S(1)}, u32[]{:S(2)}, u32[]{:S(2)}) collective-permute-start(bf16[3,32,512]{2,1,0:T(8,128)(2,1)S(1)} %get-tuple-element.41), channel_id=1, source_target_pairs={{0,3},{1,0},{2,1},{3,2},{4,7},{5,4},{6,5},{7,6},{8,11},{9,8},{10,9... | collective-permute-start | bytes 294920 | tf_op jit(solution)/shard_map/ppermute | solution.py:33
  6.2 8.7 %collective-permute-start.1 = (bf16[3,32,512]{2,1,0:T(8,128)(2,1)S(1)}, bf16[3,32,512]{2,1,0:T(8,128)(2,1)S(1)}, u32[]{:S(2)}, u32[]{:S(2)}) collective-permute-start(bf16[3,32,512]{2,1,0:T(8,128)(2,1)S(1)} %get-tuple-element.42), channel_id=1, source_target_pairs={{0,2},{1,3},{2,0},{3,1},{4,6},{5,7},{6,4},{7,5},{8,10},{9,11},{10,... | collective-permute-start | bytes 294920 | tf_op jit(solution)/shard_map/ppermute | solution.py:33
  6.2 8.7 %collective-permute-start = (bf16[3,32,512]{2,1,0:T(8,128)(2,1)S(1)}, bf16[3,32,512]{2,1,0:T(8,128)(2,1)S(1)}, u32[]{:S(2)}, u32[]{:S(2)}) collective-permute-start(bf16[3,32,512]{2,1,0:T(8,128)(2,1)S(1)} %get-tuple-element.43), channel_id=1, source_target_pairs={{0,1},{1,2},{2,3},{3,0},{4,5},{5,6},{6,7},{7,4},{8,9},{9,10},{10,1... | collective-permute-start | bytes 294920 | tf_op jit(solution)/shard_map/ppermute | solution.py:33
  7.3 12.1 %copy-start.6 = (f32[4,4]{1,0:T(4,128)S(1)}, f32[4,4]{1,0:T(4,128)}, u32[]{:S(2)}) copy-start(f32[4,4]{1,0:T(4,128)} %param.10) | copy-start | bytes 196
  8.6 12.4 %copy-start.13 = (pred[4]{0:T(512)(128)(4,1)}, pred[4]{0:T(512)(128)(4,1)S(1)}, u32[]{:S(2)}) copy-start(pred[4]{0:T(512)(128)(4,1)S(1)} %compare_and_fusion) | copy-start | bytes 16
  16.4 1.3 %collective-permute-start.3 = (bf16[1,128,512]{2,1,0:T(8,128)(2,1)S(1)}, bf16[1,128,512]{2,1,0:T(8,128)(2,1)S(1)}, u32[]{:S(2)}, u32[]{:S(2)}) collective-permute-start(bf16[1,128,512]{2,1,0:T(8,128)(2,1)S(1)} %bitcast.74), channel_id=1, source_target_pairs={{0,4},{4,0},{8,12},{12,8},{16,20},{20,16},{24,28},{28,24},{1,5},{5... | collective-permute-start | bytes 393224 | tf_op jit(solution)/shard_map/ppermute | solution.py:47
  17.8 8.4 %collective-permute-start.4 = (bf16[2,128,512]{2,1,0:T(8,128)(2,1)S(1)}, bf16[2,128,512]{2,1,0:T(8,128)(2,1)S(1)}, u32[]{:S(2)}, u32[]{:S(2)}) collective-permute-start(bf16[2,128,512]{2,1,0:T(8,128)(2,1)S(1)} %maximum_select_fusion.4), channel_id=1, source_target_pairs={{0,8},{4,12},{8,0},{12,4},{16,24},{20,28},{24,16},{28,20},{1,9},{5... | collective-permute-start | bytes 786440 | tf_op jit(solution)/shard_map/ppermute | solution.py:47
  21.0 2.6 %collective-permute-start.9 = (bf16[5,512]{1,0:T(8,128)(2,1)S(1)}, bf16[5,512]{1,0:T(8,128)(2,1)S(1)}, u32[]{:S(2)}, u32[]{:S(2)}) collective-permute-start(bf16[5,512]{1,0:T(8,128)(2,1)S(1)} %slice.270), channel_id=1, source_target_pairs={{0,4},{4,8},{8,12},{12,16},{16,20},{20,24},{24,28},{1,5},{5,9},{9,... | collective-permute-start | bytes 15368 | tf_op jit(solution)/shard_map/ppermute | solution.py:23
  26.3 13.2 %collective-permute-start.5 = (bf16[4,128,512]{2,1,0:T(8,128)(2,1)S(1)}, bf16[4,128,512]{2,1,0:T(8,128)(2,1)S(1)}, u32[]{:S(2)}, u32[]{:S(2)}) collective-permute-start(bf16[4,128,512]{2,1,0:T(8,128)(2,1)S(1)} %maximum_select_fusion.2), channel_id=1, source_target_pairs={{0,16},{4,20},{8,24},{12,28},{16,0},{20,4},{24,8},{28,12},{1,17},{... | collective-permute-start | bytes 1572872 | tf_op jit(solution)/shard_map/ppermute | solution.py:47
  29.5 10.5 %copy-start.1 = (bf16[128,4,6,128]{0,3,2,1:T(8,128)(2,1)}, bf16[128,4,6,128]{0,3,2,1:T(8,128)(2,1)S(1)}, u32[]{:S(2)}) copy-start(bf16[128,4,6,128]{0,3,2,1:T(8,128)(2,1)S(1)} %constant_dynamic-update-slice_fusion) | copy-start | bytes 2359300
  39.7 1.0 %copy-start = (bf16[8,128,512]{2,1,0:T(8,128)(2,1)}, bf16[8,128,512]{2,1,0:T(8,128)(2,1)S(1)}, u32[]{:S(2)}) copy-start(bf16[8,128,512]{2,1,0:T(8,128)(2,1)S(1)} %maximum_select_fusion) | copy-start | bytes 3145732
  40.7 2.5 %copy-start.2 = (bf16[1,4,32,512]{3,2,0,1:T(8,128)(2,1)S(1)}, bf16[1,4,32,512]{3,2,0,1:T(8,128)(2,1)}, u32[]{:S(2)}) copy-start(bf16[1,4,32,512]{3,2,0,1:T(8,128)(2,1)} %get-tuple-element.38) | copy-start | bytes 393220
  43.1 1.4 %collective-permute-start.6 = (bf16[1,128,512]{2,1,0:T(8,128)(2,1)S(1)}, bf16[1,128,512]{2,1,0:T(8,128)(2,1)S(1)}, u32[]{:S(2)}, u32[]{:S(2)}) collective-permute-start(bf16[1,128,512]{2,1,0:T(8,128)(2,1)S(1)} %bitcast.72), channel_id=1, source_target_pairs={{0,4},{4,0},{8,12},{12,8},{16,20},{20,16},{24,28},{28,24},{1,5},{5... | collective-permute-start | bytes 393224 | tf_op jit(solution)/shard_map/ppermute | solution.py:47
  44.6 13.2 %copy-start.8 = (f32[4]{0:T(128)S(1)}, f32[4]{0:T(128)}, u32[]{:S(2)}) copy-start(f32[4]{0:T(128)} %get-tuple-element.14) | copy-start | bytes 52
  44.6 13.2 %copy-start.9 = (f32[4]{0:T(128)S(1)}, f32[4]{0:T(128)}, u32[]{:S(2)}) copy-start(f32[4]{0:T(128)} %get-tuple-element.18) | copy-start | bytes 52
  44.6 13.2 %copy-start.10 = (f32[4]{0:T(128)S(1)}, f32[4]{0:T(128)}, u32[]{:S(2)}) copy-start(f32[4]{0:T(128)} %get-tuple-element.22) | copy-start | bytes 52
  44.6 13.2 %copy-start.11 = (f32[4]{0:T(128)S(1)}, f32[4]{0:T(128)}, u32[]{:S(2)}) copy-start(f32[4]{0:T(128)} %get-tuple-element.25) | copy-start | bytes 52
  44.6 13.2 %copy-start.12 = (f32[4]{0:T(128)S(1)}, f32[4]{0:T(128)}, u32[]{:S(2)}) copy-start(f32[4]{0:T(128)} %get-tuple-element.27) | copy-start | bytes 52
  44.6 13.3 %collective-permute-start.7 = (bf16[2,128,512]{2,1,0:T(8,128)(2,1)S(1)}, bf16[2,128,512]{2,1,0:T(8,128)(2,1)S(1)}, u32[]{:S(2)}, u32[]{:S(2)}) collective-permute-start(bf16[2,128,512]{2,1,0:T(8,128)(2,1)S(1)} %maximum_select_fusion.5), channel_id=1, source_target_pairs={{0,8},{4,12},{8,0},{12,4},{16,24},{20,28},{24,16},{28,20},{1,9},{5... | collective-permute-start | bytes 786440 | tf_op jit(solution)/shard_map/ppermute | solution.py:47
  58.0 13.8 %collective-permute-start.8 = (bf16[4,128,512]{2,1,0:T(8,128)(2,1)S(1)}, bf16[4,128,512]{2,1,0:T(8,128)(2,1)S(1)}, u32[]{:S(2)}, u32[]{:S(2)}) collective-permute-start(bf16[4,128,512]{2,1,0:T(8,128)(2,1)S(1)} %maximum_select_fusion.3), channel_id=1, source_target_pairs={{0,16},{4,20},{8,24},{12,28},{16,0},{20,4},{24,8},{28,12},{1,17},{... | collective-permute-start | bytes 1572872 | tf_op jit(solution)/shard_map/ppermute | solution.py:47
  64.3 8.0 %copy-start.15 = (f32[4]{0:T(128)S(1)}, f32[4]{0:T(128)}, u32[]{:S(2)}) copy-start(f32[4]{0:T(128)} %get-tuple-element.29) | copy-start | bytes 52
  64.3 8.0 %copy-start.16 = (f32[4]{0:T(128)S(1)}, f32[4]{0:T(128)}, u32[]{:S(2)}) copy-start(f32[4]{0:T(128)} %get-tuple-element.30) | copy-start | bytes 52
  64.3 8.0 %copy-start.17 = (f32[4]{0:T(128)S(1)}, f32[4]{0:T(128)}, u32[]{:S(2)}) copy-start(f32[4]{0:T(128)} %get-tuple-element.31) | copy-start | bytes 52
  64.3 8.0 %copy-start.18 = (f32[4]{0:T(128)S(1)}, f32[4]{0:T(128)}, u32[]{:S(2)}) copy-start(f32[4]{0:T(128)} %get-tuple-element.32) | copy-start | bytes 52
  71.9 1.0 %copy-start.3 = (f32[1024,128]{1,0:T(8,128)S(1)}, f32[1024,128]{1,0:T(8,128)}, u32[]{:S(2)}) copy-start(f32[1024,128]{1,0:T(8,128)} %get-tuple-element.33) | copy-start | bytes 1572868
  71.9 1.2 %copy-start.4 = (f32[1024,128]{1,0:T(8,128)S(1)}, f32[1024,128]{1,0:T(8,128)}, u32[]{:S(2)}) copy-start(f32[1024,128]{1,0:T(8,128)} %get-tuple-element.34) | copy-start | bytes 1572868
  73.1 2.2 %copy-start.7 = (f32[512]{0:T(512)S(1)}, f32[512]{0:T(512)}, u32[]{:S(2)}) copy-start(f32[512]{0:T(512)} %param.11) | copy-start | bytes 6148
  75.3 9.4 %copy-start.14 = (pred[4]{0:T(512)(128)(4,1)S(1)}, pred[4]{0:T(512)(128)(4,1)}, u32[]{:S(2)}) copy-start(pred[4]{0:T(512)(128)(4,1)} %copy-done.13) | copy-start | bytes 16
  75.8 4.7 %collective-permute-start.12 = (bf16[32,512]{1,0:T(8,128)(2,1)S(1)}, bf16[32,512]{1,0:T(8,128)(2,1)S(1)}, u32[]{:S(2)}, u32[]{:S(2)}) collective-permute-start(bf16[32,512]{1,0:T(8,128)(2,1)S(1)} %copy.80), channel_id=1, source_target_pairs={{0,3},{1,0},{2,1},{3,2},{4,7},{5,4},{6,5},{7,6},{8,11},{9,8},{10,9... | collective-permute-start | bytes 98312 | tf_op jit(solution)/shard_map/ppermute | solution.py:33
  77.9 4.9 %collective-permute-start.11 = (bf16[32,512]{1,0:T(8,128)(2,1)S(1)}, bf16[32,512]{1,0:T(8,128)(2,1)S(1)}, u32[]{:S(2)}, u32[]{:S(2)}) collective-permute-start(bf16[32,512]{1,0:T(8,128)(2,1)S(1)} %copy.79), channel_id=1, source_target_pairs={{0,2},{1,3},{2,0},{3,1},{4,6},{5,7},{6,4},{7,5},{8,10},{9,11},{10,... | collective-permute-start | bytes 98312 | tf_op jit(solution)/shard_map/ppermute | solution.py:33
  78.3 5.8 %collective-permute-start.10 = (bf16[32,512]{1,0:T(8,128)(2,1)S(1)}, bf16[32,512]{1,0:T(8,128)(2,1)S(1)}, u32[]{:S(2)}, u32[]{:S(2)}) collective-permute-start(bf16[32,512]{1,0:T(8,128)(2,1)S(1)} %copy.78), channel_id=1, source_target_pairs={{0,1},{1,2},{2,3},{3,0},{4,5},{5,6},{6,7},{7,4},{8,9},{9,10},{10,1... | collective-permute-start | bytes 98312 | tf_op jit(solution)/shard_map/ppermute | solution.py:33

commit v17 on v15

--- a/solution.py
+++ b/solution.py
@@ -108,13 +108,14 @@
                 conv_ref[0, rows, cols] = part_high
                 conv_ref[1, rows, cols] = part_low
     query = query_ref[0]
-    out_ref[0] = jnp.dot(conv_ref[0], query, preferred_element_type=jnp.float32) + jnp.dot(
-        conv_ref[1], query, preferred_element_type=jnp.float32
-    )
+    dims = (((1,), (1,)), ((), ()))
+    out_ref[0] = lax.dot_general(
+        query, conv_ref[0], dims, preferred_element_type=jnp.float32
+    ) + lax.dot_general(query, conv_ref[1], dims, preferred_element_type=jnp.float32)
 
 
 def conv_logits(shifted_t, score_kernel, key_pad):
-    heads, contract, row_count = shifted_t.shape
+    heads, row_count, contract = shifted_t.shape
     seq_len = key_pad.shape[0]
     head_dim = key_pad.shape[1] // heads
     span = min(seq_len, KEY_SPAN)
@@ -124,11 +125,11 @@
         grid=(heads, seq_len // span),
         in_specs=[
             pl.BlockSpec(memory_space=pltpu.SMEM),
-            pl.BlockSpec((1, contract, row_count), lambda h, g: (h, 0, 0)),
+            pl.BlockSpec((1, row_count, contract), lambda h, g: (h, 0, 0)),
             pl.BlockSpec((key_pad.shape[0], head_dim), lambda h, g: (0, h)),
         ],
-        out_specs=pl.BlockSpec((1, span, row_count), lambda h, g: (h, g, 0)),
-        out_shape=jax.ShapeDtypeStruct((heads, seq_len, row_count), jnp.float32),
+        out_specs=pl.BlockSpec((1, row_count, span), lambda h, g: (h, 0, g)),
+        out_shape=jax.ShapeDtypeStruct((heads, row_count, seq_len), jnp.float32),
         scratch_shapes=[
             pltpu.VMEM((QCONV * (KEY_BLOCK + 16), KEY_BLOCK), jnp.bfloat16),
             pltpu.VMEM((QCONV * (KEY_BLOCK + 16), KEY_BLOCK), jnp.bfloat16),
@@ -166,24 +167,24 @@
 def attend_chunk(shifted, band, query_first, key_pad, score_kernel, value_heads, head_mixing):
     row_count, heads = shifted.shape[:2]
     seq_len = value_heads.shape[0]
-    shifted_t = jnp.transpose(shifted, (1, 2, 3, 0)).reshape((heads, -1, row_count))
+    shifted_t = jnp.transpose(shifted, (1, 0, 2, 3)).reshape((heads, row_count, -1))
     convolved = conv_logits(shifted_t, score_kernel, key_pad)
     query_pos = query_first + lax.iota(jnp.int32, row_count)
-    gap = query_pos[None, :] - lax.iota(jnp.int32, seq_len)[:, None]
+    gap = query_pos[:, None] - lax.iota(jnp.int32, seq_len)[None, :]
     for lag in range(QCONV - 1):
-        convolved = convolved + jnp.where(gap == lag, band[lag][:, None, :], 0.0)
+        convolved = convolved + jnp.where(gap == lag, band[lag][:, :, None], 0.0)
     logits = jnp.where(gap >= 0, convolved, lowest)
-    peak = jnp.max(logits, axis=1, keepdims=True)
+    peak = jnp.max(logits, axis=2, keepdims=True)
     expd = jnp.exp(logits - peak)
-    probabilities = expd / jnp.sum(expd, axis=1, keepdims=True)
-    grouped = probabilities.reshape(heads // GROUP, GROUP, seq_len, row_count)
+    probabilities = expd / jnp.sum(expd, axis=2, keepdims=True)
+    grouped = probabilities.reshape(heads // GROUP, GROUP, row_count, seq_len)
     weights = head_mixing.reshape(heads // GROUP, GROUP, GROUP)
     mixed_probs = jnp.zeros_like(grouped)
     for source in range(GROUP):
         mixed_probs = mixed_probs + weights[:, :, source, None, None] * grouped[:, source, None]
-    mixed_probs = mixed_probs.reshape(heads, seq_len, row_count).astype(jnp.bfloat16)
+    mixed_probs = mixed_probs.reshape(heads, row_count, seq_len).astype(jnp.bfloat16)
     return jnp.einsum(
-        "hki,khd->ihd", mixed_probs, value_heads, preferred_element_type=jnp.float32
+        "hik,khd->ihd", mixed_probs, value_heads, preferred_element_type=jnp.float32
     )
 
 

time: 71.6 us -> 75.7 us (1.057)
  other arithmetic: 8.44 us -> 12.6 us
  waiting for transfers between devices: 16.8 us -> 14.3 us
  local copies, waits for them, and re-layouts: 11.6 us -> 13.5 us
    ppermute x6, waiting for transfers between devices: 10.1 us -> 6.83 us  [gathered(): incoming = lax.ppermute(held, axis, [(i, i ^ bit) for i in range(peers)])]
    div x1, other arithmetic: 3.88 us -> 6.26 us  [attend_chunk(): probabilities = expd / jnp.sum(expd, axis=2, keepdims=True)]
    transpose x3, other arithmetic: 0.25 us -> 2.06 us  [band_terms(): band.append(acc.T)]
    reshape x0 -> x1, local copies, waits for them, and re-layouts: none -> 1.16 us  [attend_chunk(): jnp.transpose(shifted, (1, 0, 2, 3)).reshape((heads, row_count, -1))]
  transfers between devices with their start and end apart: 13 -> 13, of which waited for: 9 -> 9; matrix products, arithmetic and copies ran while one was open for 15% -> 23% of each run, Pallas kernels for 15% -> 14%
where the time goes in v17:
time: 75.7 us; the launch traced here: 75.4 us
  starting transfers between devices  21.6 us (29%)
  waiting for transfers between devices  14.3 us (19%)
  local copies, waits for them, and re-layouts  13.5 us (18%)
  other arithmetic  12.6 us (17%)
  Pallas kernels  10.7 us (14%)
  matrix products  2.01 us (3%)
    ppermute x6, starting transfers between devices, exchanged(): received.append(lax.ppermute(outgoing, axis, pairs))  12.2 us
    pallas_call x1, Pallas kernels, conv_logits(): pl.pallas_call(logits_kernel, grid=(heads, seq_len // span), in_specs=[pl...  10.7 us
    ppermute x6, starting transfers between devices, gathered(): incoming = lax.ppermute(held, axis, [(i, i ^ bit) for i in range(peers)])  8.09 us
    ppermute x6, waiting for transfers between devices, gathered(): incoming = lax.ppermute(held, axis, [(i, i ^ bit) for i in range(peers)])  6.83 us
    ppermute x6, waiting for transfers between devices, exchanged(): received.append(lax.ppermute(outgoing, axis, pairs))  6.73 us
    div x1, other arithmetic, attend_chunk(): probabilities = expd / jnp.sum(expd, axis=2, keepdims=True)  6.26 us
    transpose x3, other arithmetic, band_terms(): band.append(acc.T)  2.06 us
    dot_general x1, matrix products, attend_chunk(): jnp.einsum('hik,khd->ihd', mixed_probs, value_heads, preferred_element_ty...  2.01 us
  transfers between devices with their start and end apart: 13, of which 9 were waited for; matrix products, arithmetic and copies ran while one was open for 23% of the time, Pallas kernels for 14%

profile of v17, /device:TPU:0, one launch (start us, length us, event | category | flops | bytes accessed | tf_op | source)
XLA Modules:
  0.0 75.4 jit_solution(16330560216854126821)
XLA Ops:
  0.0 1.1 %pad_maximum_fusion = bf16[3,32,2048]{2,1,0:T(8,128)(2,1)S(1)} fusion(bf16[1,32,2048]{2,1,0:T(8,128)(2,1)} %bitcast.92, bf16[1,32,2048]{2,1,0:T(8,128)(2,1)} %bitcast.93, bf16[1,32,2048]{2,1,0:T(8,128)(2,1)} %bitcast.94), kind=kLoop, calls=%fused_computation.40 | loop fusion | flops 393216 | bytes 786432 | tf_op jit(solution)/shard_map/stack | solution.py:200
  1.1 3.1 %collective-permute-start = (bf16[3,32,512]{2,1,0:T(8,128)(2,1)S(1)}, bf16[3,32,512]{2,1,0:T(8,128)(2,1)S(1)}, u32[]{:S(2)}, u32[]{:S(2)}) collective-permute-start(bf16[3,32,512]{2,1,0:T(8,128)(2,1)S(1)} %get-tuple-element.43), channel_id=1, source_target_pairs={{0,1},{1,2},{2,3},{3,0},{4,5},{5,6},{6,7},{7,4},{8,9},{9,10},{10,1... | collective-permute-start | bytes 294920 | tf_op jit(solution)/shard_map/ppermute | solution.py:33
  4.2 2.6 %collective-permute-start.1 = (bf16[3,32,512]{2,1,0:T(8,128)(2,1)S(1)}, bf16[3,32,512]{2,1,0:T(8,128)(2,1)S(1)}, u32[]{:S(2)}, u32[]{:S(2)}) collective-permute-start(bf16[3,32,512]{2,1,0:T(8,128)(2,1)S(1)} %get-tuple-element.42), channel_id=1, source_target_pairs={{0,2},{1,3},{2,0},{3,1},{4,6},{5,7},{6,4},{7,5},{8,10},{9,11},{10,... | collective-permute-start | bytes 294920 | tf_op jit(solution)/shard_map/ppermute | solution.py:33
  6.8 1.3 %collective-permute-start.2 = (bf16[3,32,512]{2,1,0:T(8,128)(2,1)S(1)}, bf16[3,32,512]{2,1,0:T(8,128)(2,1)S(1)}, u32[]{:S(2)}, u32[]{:S(2)}) collective-permute-start(bf16[3,32,512]{2,1,0:T(8,128)(2,1)S(1)} %get-tuple-element.41), channel_id=1, source_target_pairs={{0,3},{1,0},{2,1},{3,2},{4,7},{5,4},{6,5},{7,6},{8,11},{9,8},{10,9... | collective-permute-start | bytes 294920 | tf_op jit(solution)/shard_map/ppermute | solution.py:33
  8.2 1.2 %fusion.15 = (pred[128,1024]{1,0:T(8,128)(4,1)S(1)}, pred[128,1024]{1,0:T(8,128)(4,1)S(1)}, pred[128,1024]{1,0:T(8,128)(4,1)S(1)}, pred[128,1024]{1,0:T(8,128)(4...) fusion(s32[128]{0:T(128)S(1)} %iota_add_fusion), kind=kLoop, calls=%fused_computation.39 | loop fusion | flops 917504 | bytes 786944 | tf_op jit(solution)/shard_map/ge | solution.py:176
  9.5 0.4 collective-permute-done
  9.9 3.5 %collective-permute-done.1 = bf16[3,32,512]{2,1,0:T(8,128)(2,1)S(1)} collective-permute-done((bf16[3,32,512]{2,1,0:T(8,128)(2,1)S(1)}, bf16[3,32,512]{2,1,0:T(8,128)(2,1)S(1)}, u32[]{:S(2)}, u32[]{:S(2)}) %collective-permute-start.1) | collective-permute-done | bytes 98336 | tf_op jit(solution)/shard_map/ppermute | solution.py:33
  13.5 0.6 gather_fusion
  14.1 0.1 select_bitcast_fusion
  14.2 1.6 %collective-permute-start.3 = (bf16[1,128,512]{2,1,0:T(8,128)(2,1)S(1)}, bf16[1,128,512]{2,1,0:T(8,128)(2,1)S(1)}, u32[]{:S(2)}, u32[]{:S(2)}) collective-permute-start(bf16[1,128,512]{2,1,0:T(8,128)(2,1)S(1)} %bitcast.85), channel_id=1, source_target_pairs={{0,16},{4,20},{8,24},{12,28},{16,0},{20,4},{24,8},{28,12},{1,17},{... | collective-permute-start | bytes 393224 | tf_op jit(solution)/shard_map/ppermute | solution.py:47
  15.8 1.0 %slice_reduce_fusion.17 = (f32[4]{0:T(128)}, f32[4]{0:T(128)S(1)}, f32[4]{0:T(128)S(1)}, f32[4]{0:T(128)S(1)}, f32[4]{0:T(128)}, /*index=5*/f32[4]{0:T(128)S(1)}...) fusion(f32[4,6,11]{2,0,1:T(4,128)S(1)} %copy-done.3), kind=kLoop, calls=%fused_computation.135 | loop fusion | bytes 480 | tf_op jit(solution)/shard_map/slice | solution.py:160
  16.8 2.8 %collective-permute-done.3 = bf16[1,128,512]{2,1,0:T(8,128)(2,1)S(1)} collective-permute-done((bf16[1,128,512]{2,1,0:T(8,128)(2,1)S(1)}, bf16[1,128,512]{2,1,0:T(8,128)(2,1)S(1)}, u32[]{:S(2)}, u32[]{:S(2)}) %collective-permute-start.3) | collective-permute-done | bytes 131104 | tf_op jit(solution)/shard_map/ppermute | solution.py:47
  19.6 1.6 %collective-permute-start.4 = (bf16[2,128,512]{2,1,0:T(8,128)(2,1)S(1)}, bf16[2,128,512]{2,1,0:T(8,128)(2,1)S(1)}, u32[]{:S(2)}, u32[]{:S(2)}) collective-permute-start(bf16[2,128,512]{2,1,0:T(8,128)(2,1)S(1)} %maximum_select_fusion.4), channel_id=1, source_target_pairs={{0,8},{4,12},{8,0},{12,4},{16,24},{20,28},{24,16},{28,20},{1,9},{5... | collective-permute-start | bytes 786440 | tf_op jit(solution)/shard_map/ppermute | solution.py:47
  21.1 0.8 %slice_reduce_fusion.18 = (f32[4]{0:T(128)}, f32[4]{0:T(128)}, f32[4]{0:T(128)}, f32[4]{0:T(128)}) fusion(f32[1,4,4]{2,1,0:T(4,128)S(1)} %bitcast.99), kind=kLoop, calls=%fused_computation.136 | loop fusion | bytes 128 | tf_op jit(solution)/shard_map/slice | solution.py:184
  21.9 0.7 reshape.181.taps_ref
  22.6 1.3 %collective-permute-start.9 = (bf16[5,512]{1,0:T(8,128)(2,1)S(1)}, bf16[5,512]{1,0:T(8,128)(2,1)S(1)}, u32[]{:S(2)}, u32[]{:S(2)}) collective-permute-start(bf16[5,512]{1,0:T(8,128)(2,1)S(1)} %slice.270), channel_id=1, source_target_pairs={{0,4},{4,8},{8,12},{12,16},{16,20},{20,24},{24,28},{1,5},{5,9},{9,... | collective-permute-start | bytes 15368 | tf_op jit(solution)/shard_map/ppermute | solution.py:23
  24.0 0.7 collective-permute-done.9
  24.8 0.1 pad_maximum_fusion.3
  24.9 0.1 copy.103
  25.0 0.1 copy.108
  25.2 0.1 copy.104
  25.3 0.1 copy.109
  25.4 0.1 copy.105
  25.6 0.1 copy.110
  25.7 0.1 copy.106
  25.8 0.1 copy.111
  26.0 0.1 copy.107
  26.1 0.1 copy.112
  26.3 0.6 collective-permute-done.4
  27.0 0.7 collective-permute-start.5
  28.0 0.6 copy.113
  28.6 1.2 %copy.114.query_ref = bf16[4,128,768]{2,1,0:T(8,128)(2,1)} copy(bf16[4,128,768]{1,2,0:T(8,128)(2,1)S(1)} %bitcast.79) | data formatting | bytes 1572864 | tf_op jit(solution)/shard_map/reshape | solution.py:170
  29.8 0.2 maximum_select_fusion
  30.0 0.1 copy.100
  30.2 0.1 fusion.51
  30.4 0.1 slice.221
  30.5 0.6 copy-done
  31.2 0.1 slice.231
  31.3 0.1 slice.239
  31.4 0.1 slice.249
  31.5 0.8 %fusion.21 = (f32[133,4]{1,0:T(8,128)S(1)}, f32[133,4]{1,0:T(8,128)S(1)}, f32[133,4]{1,0:T(8,128)S(1)}, f32[133,4]{1,0:T(8,128)S(1)}, f32[133,4]{1,0:T(8,128)S(1)}) fusion(f32[133,4,128]{2,1,0:T(4,128)S(1)} %slice.249, bf16[128,4,128]{2,1,0:T(4,128)(2,1)S(1)} %concatenate.63, bf16[5,4,128]{2,1,0:T(4,128)(2,1)S(1)} %concatenate.62, ...), kind=kLoop, calls=%fused_computation.52 | loop fusion | flops 814492 | bytes 1508752 | tf_op jit(solution)/shard_map/reduce_sum | solution.py:151
  32.7 4.1 %collective-permute-start.6 = (bf16[1,128,512]{2,1,0:T(8,128)(2,1)S(1)}, bf16[1,128,512]{2,1,0:T(8,128)(2,1)S(1)}, u32[]{:S(2)}, u32[]{:S(2)}) collective-permute-start(bf16[1,128,512]{2,1,0:T(8,128)(2,1)S(1)} %bitcast.83), channel_id=1, source_target_pairs={{0,16},{4,20},{8,24},{12,28},{16,0},{20,4},{24,8},{28,12},{1,17},{... | collective-permute-start | bytes 393224 | tf_op jit(solution)/shard_map/ppermute | solution.py:47
  36.8 0.7 subtract_bitcast_fusion.2
  37.5 3.5 %collective-permute-done.6 = bf16[1,128,512]{2,1,0:T(8,128)(2,1)S(1)} collective-permute-done((bf16[1,128,512]{2,1,0:T(8,128)(2,1)S(1)}, bf16[1,128,512]{2,1,0:T(8,128)(2,1)S(1)}, u32[]{:S(2)}, u32[]{:S(2)}) %collective-permute-start.6) | collective-permute-done | bytes 131104 | tf_op jit(solution)/shard_map/ppermute | solution.py:47
  41.1 0.7 subtract_bitcast_fusion.3
  41.8 10.7 %shard_map.64 = f32[4,128,1024]{2,1,0:T(8,128)} custom-call(f32[264]{0:T(512)} %reshape.181.taps_ref, bf16[4,128,768]{2,1,0:T(8,128)(2,1)} %copy.114.query_ref, bf16[1024,512]{1,0:T(8,128)(2,1)} %bitcast.75), custom_call_target="tpu_custom_call" | custom-call | tf_op jit(solution)/shard_map/pallas_call | solution.py:123
  52.6 0.7 fusion.44
  53.5 6.3 %divide_bitcast_fusion = f32[1,4,128,1024]{3,2,1,0:T(8,128)S(1)} fusion(f32[4,128,1024]{2,1,0:T(8,128)} %shard_map.64, f32[4,128]{1,0:T(4,128)} %get-tuple-element.60, f32[4,128]{1,0:T(4,128)} %get-tuple-element.59, f32[4,128]{1,0:T(4,128)} %get-tuple-element.58, f32[4,128]{1,0:T(4,128)} %subtract_bitcast_fusion.3, f32[4,128]{1,0:T(4,128)} %fusion.44, ...), kind=kOutput, calls=%fused_computation.5 | output fusion | flops 6818814 | bytes 4990976 | tf_op jit(solution)/shard_map/div | solution.py:179
  59.7 1.4 %slice_bitcast_fusion.3 = (f32[128,1024]{1,0:T(8,128)}, f32[128,1024]{1,0:T(8,128)}, f32[128,1024]{1,0:T(8,128)}, f32[128,1024]{1,0:T(8,128)}) fusion(f32[1,4,128,1024]{3,2,1,0:T(8,128)S(1)} %divide_bitcast_fusion), kind=kLoop, calls=%fused_computation.30 | loop fusion | bytes 4194304 | tf_op jit(solution)/shard_map/mul | solution.py:184
  61.1 0.2 maximum_select_fusion.1
  61.3 0.9 %copy.101 = bf16[2,2,2,128,512]{3,2,1,0,4:T(2,128)(2,1)S(1)} copy(bf16[2,2,2,128,512]{4,3,0,1,2:T(8,128)(2,1)S(1)} %bitcast.76) | data formatting | bytes 2097152 | tf_op jit(solution)/shard_map/transpose | solution.py:55
  62.3 0.8 %reshape_reshape.3 = bf16[1024,4,128]{0,2,1:T(8,128)(2,1)S(1)} reshape(bf16[2,2,2,128,512]{3,2,1,0,4:T(2,128)(2,1)S(1)} %copy.101) | data formatting | bytes 2097152 | tf_op jit(solution)/shard_map/reshape;reshape | solution.py:231
  63.1 0.2 copy-done.2
  63.3 2.0 %multiply_reduce_fusion = (f32[128,4]{0,1:T(4,128)S(1)}, f32[128,4,128]{0,2,1:T(8,128)S(1)}) fusion(bf16[1024,4,128]{0,2,1:T(8,128)(2,1)S(1)} %reshape_reshape.3, f32[128,1024]{1,0:T(8,128)S(1)} %copy-done.2, f32[4]{0:T(128)S(1)} %copy-done.16, f32[128,1024]{1,0:T(8,128)} %get-tuple-element.35, f32[4]{0:T(128)S(1)} %copy-done.17, ...), kind=kOutput, calls=%fused_computation.56 | convolution fusion | flops 138542592 | bytes 3409984 | tf_op jit(solution)/shard_map/hik,khd->ihd/dot_general | solution.py:186
  65.4 0.1 multiply_convert_fusion
  65.5 0.2 constant_dynamic-slice_fusion.3
  65.8 2.7 %collective-permute-start.10 = (bf16[32,512]{1,0:T(8,128)(2,1)S(1)}, bf16[32,512]{1,0:T(8,128)(2,1)S(1)}, u32[]{:S(2)}, u32[]{:S(2)}) collective-permute-start(bf16[32,512]{1,0:T(8,128)(2,1)S(1)} %copy.125), channel_id=1, source_target_pairs={{0,1},{1,2},{2,3},{3,0},{4,5},{5,6},{6,7},{7,4},{8,9},{9,10},{10,1... | collective-permute-start | bytes 98312 | tf_op jit(solution)/shard_map/ppermute | solution.py:33
  68.6 1.2 %collective-permute-start.11 = (bf16[32,512]{1,0:T(8,128)(2,1)S(1)}, bf16[32,512]{1,0:T(8,128)(2,1)S(1)}, u32[]{:S(2)}, u32[]{:S(2)}) collective-permute-start(bf16[32,512]{1,0:T(8,128)(2,1)S(1)} %copy.126), channel_id=1, source_target_pairs={{0,2},{1,3},{2,0},{3,1},{4,6},{5,7},{6,4},{7,5},{8,10},{9,11},{10,... | collective-permute-start | bytes 98312 | tf_op jit(solution)/shard_map/ppermute | solution.py:33
  70.0 1.3 %collective-permute-start.12 = (bf16[32,512]{1,0:T(8,128)(2,1)S(1)}, bf16[32,512]{1,0:T(8,128)(2,1)S(1)}, u32[]{:S(2)}, u32[]{:S(2)}) collective-permute-start(bf16[32,512]{1,0:T(8,128)(2,1)S(1)} %copy.127), channel_id=1, source_target_pairs={{0,3},{1,0},{2,1},{3,2},{4,7},{5,4},{6,5},{7,6},{8,11},{9,8},{10,9... | collective-permute-start | bytes 98312 | tf_op jit(solution)/shard_map/ppermute | solution.py:33
  71.3 0.3 collective-permute-done.10
  71.6 2.3 %collective-permute-done.11 = bf16[32,512]{1,0:T(8,128)(2,1)S(1)} collective-permute-done((bf16[32,512]{1,0:T(8,128)(2,1)S(1)}, bf16[32,512]{1,0:T(8,128)(2,1)S(1)}, u32[]{:S(2)}, u32[]{:S(2)}) %collective-permute-start.11) | collective-permute-done | bytes 32800 | tf_op jit(solution)/shard_map/ppermute | solution.py:33
  73.9 0.2 collective-permute-done.12
  74.1 0.6 gather_fusion.1
  74.8 0.7 copy.129
  (83 shorter events, 2.1 us)
Async XLA Ops:
  1.1 14.7 %copy-start.3 = (f32[4,6,11]{2,0,1:T(4,128)S(1)}, f32[4,6,11]{2,0,1:T(4,128)}, u32[]{:S(2)}) copy-start(f32[4,6,11]{2,0,1:T(4,128)} %param.9) | copy-start | bytes 3172
  1.1 8.8 %collective-permute-start = (bf16[3,32,512]{2,1,0:T(8,128)(2,1)S(1)}, bf16[3,32,512]{2,1,0:T(8,128)(2,1)S(1)}, u32[]{:S(2)}, u32[]{:S(2)}) collective-permute-start(bf16[3,32,512]{2,1,0:T(8,128)(2,1)S(1)} %get-tuple-element.43), channel_id=1, source_target_pairs={{0,1},{1,2},{2,3},{3,0},{4,5},{5,6},{6,7},{7,4},{8,9},{9,10},{10,1... | collective-permute-start | bytes 294920 | tf_op jit(solution)/shard_map/ppermute | solution.py:33
  4.2 9.2 %collective-permute-start.1 = (bf16[3,32,512]{2,1,0:T(8,128)(2,1)S(1)}, bf16[3,32,512]{2,1,0:T(8,128)(2,1)S(1)}, u32[]{:S(2)}, u32[]{:S(2)}) collective-permute-start(bf16[3,32,512]{2,1,0:T(8,128)(2,1)S(1)} %get-tuple-element.42), channel_id=1, source_target_pairs={{0,2},{1,3},{2,0},{3,1},{4,6},{5,7},{6,4},{7,5},{8,10},{9,11},{10,... | collective-permute-start | bytes 294920 | tf_op jit(solution)/shard_map/ppermute | solution.py:33
  6.8 6.6 %collective-permute-start.2 = (bf16[3,32,512]{2,1,0:T(8,128)(2,1)S(1)}, bf16[3,32,512]{2,1,0:T(8,128)(2,1)S(1)}, u32[]{:S(2)}, u32[]{:S(2)}) collective-permute-start(bf16[3,32,512]{2,1,0:T(8,128)(2,1)S(1)} %get-tuple-element.41), channel_id=1, source_target_pairs={{0,3},{1,0},{2,1},{3,2},{4,7},{5,4},{6,5},{7,6},{8,11},{9,8},{10,9... | collective-permute-start | bytes 294920 | tf_op jit(solution)/shard_map/ppermute | solution.py:33
  8.2 13.0 %copy-start.4 = (f32[4,4]{1,0:T(4,128)S(1)}, f32[4,4]{1,0:T(4,128)}, u32[]{:S(2)}) copy-start(f32[4,4]{1,0:T(4,128)} %param.10) | copy-start | bytes 196
  9.5 6.4 %copy-start.13 = (pred[4]{0:T(512)(128)(4,1)}, pred[4]{0:T(512)(128)(4,1)S(1)}, u32[]{:S(2)}) copy-start(pred[4]{0:T(512)(128)(4,1)S(1)} %compare_and_fusion) | copy-start | bytes 16
  14.2 5.3 %collective-permute-start.3 = (bf16[1,128,512]{2,1,0:T(8,128)(2,1)S(1)}, bf16[1,128,512]{2,1,0:T(8,128)(2,1)S(1)}, u32[]{:S(2)}, u32[]{:S(2)}) collective-permute-start(bf16[1,128,512]{2,1,0:T(8,128)(2,1)S(1)} %bitcast.85), channel_id=1, source_target_pairs={{0,16},{4,20},{8,24},{12,28},{16,0},{20,4},{24,8},{28,12},{1,17},{... | collective-permute-start | bytes 393224 | tf_op jit(solution)/shard_map/ppermute | solution.py:47
  19.6 7.3 %collective-permute-start.4 = (bf16[2,128,512]{2,1,0:T(8,128)(2,1)S(1)}, bf16[2,128,512]{2,1,0:T(8,128)(2,1)S(1)}, u32[]{:S(2)}, u32[]{:S(2)}) collective-permute-start(bf16[2,128,512]{2,1,0:T(8,128)(2,1)S(1)} %maximum_select_fusion.4), channel_id=1, source_target_pairs={{0,8},{4,12},{8,0},{12,4},{16,24},{20,28},{24,16},{28,20},{1,9},{5... | collective-permute-start | bytes 786440 | tf_op jit(solution)/shard_map/ppermute | solution.py:47
  22.6 2.1 %collective-permute-start.9 = (bf16[5,512]{1,0:T(8,128)(2,1)S(1)}, bf16[5,512]{1,0:T(8,128)(2,1)S(1)}, u32[]{:S(2)}, u32[]{:S(2)}) collective-permute-start(bf16[5,512]{1,0:T(8,128)(2,1)S(1)} %slice.270), channel_id=1, source_target_pairs={{0,4},{4,8},{8,12},{12,16},{16,20},{20,24},{24,28},{1,5},{5,9},{9,... | collective-permute-start | bytes 15368 | tf_op jit(solution)/shard_map/ppermute | solution.py:23
  27.0 2.9 %collective-permute-start.5 = (bf16[4,128,512]{2,1,0:T(8,128)(2,1)S(1)}, bf16[4,128,512]{2,1,0:T(8,128)(2,1)S(1)}, u32[]{:S(2)}, u32[]{:S(2)}) collective-permute-start(bf16[4,128,512]{2,1,0:T(8,128)(2,1)S(1)} %maximum_select_fusion.2), channel_id=1, source_target_pairs={{0,4},{4,0},{8,12},{12,8},{16,20},{20,16},{24,28},{28,24},{1,5},{5... | collective-permute-start | bytes 1572872 | tf_op jit(solution)/shard_map/ppermute | solution.py:47
  30.1 1.0 %copy-start = (bf16[2,2,2,128,512]{4,3,2,1,0:T(8,128)(2,1)}, bf16[2,2,2,128,512]{4,3,2,1,0:T(8,128)(2,1)S(1)}, u32[]{:S(2)}) copy-start(bf16[2,2,2,128,512]{4,3,2,1,0:T(8,128)(2,1)S(1)} %copy.100) | copy-start | bytes 3145732
  31.2 9.9 %copy-start.5 = (f32[4]{0:T(128)S(1)}, f32[4]{0:T(128)}, u32[]{:S(2)}) copy-start(f32[4]{0:T(128)} %get-tuple-element.26) | copy-start | bytes 52
  31.2 9.9 %copy-start.6 = (f32[4]{0:T(128)S(1)}, f32[4]{0:T(128)}, u32[]{:S(2)}) copy-start(f32[4]{0:T(128)} %get-tuple-element.28) | copy-start | bytes 52
  32.7 8.3 %collective-permute-start.6 = (bf16[1,128,512]{2,1,0:T(8,128)(2,1)S(1)}, bf16[1,128,512]{2,1,0:T(8,128)(2,1)S(1)}, u32[]{:S(2)}, u32[]{:S(2)}) collective-permute-start(bf16[1,128,512]{2,1,0:T(8,128)(2,1)S(1)} %bitcast.83), channel_id=1, source_target_pairs={{0,16},{4,20},{8,24},{12,28},{16,0},{20,4},{24,8},{28,12},{1,17},{... | collective-permute-start | bytes 393224 | tf_op jit(solution)/shard_map/ppermute | solution.py:47
  40.9 11.6 %copy-start.8 = (f32[4]{0:T(128)S(1)}, f32[4]{0:T(128)}, u32[]{:S(2)}) copy-start(f32[4]{0:T(128)} %get-tuple-element.14) | copy-start | bytes 52
  41.0 11.6 %copy-start.9 = (f32[4]{0:T(128)S(1)}, f32[4]{0:T(128)}, u32[]{:S(2)}) copy-start(f32[4]{0:T(128)} %get-tuple-element.18) | copy-start | bytes 52
  41.0 11.6 %copy-start.10 = (f32[4]{0:T(128)S(1)}, f32[4]{0:T(128)}, u32[]{:S(2)}) copy-start(f32[4]{0:T(128)} %get-tuple-element.22) | copy-start | bytes 52
  41.0 11.6 %copy-start.11 = (f32[4]{0:T(128)S(1)}, f32[4]{0:T(128)}, u32[]{:S(2)}) copy-start(f32[4]{0:T(128)} %get-tuple-element.25) | copy-start | bytes 52
  41.0 11.6 %copy-start.12 = (f32[4]{0:T(128)S(1)}, f32[4]{0:T(128)}, u32[]{:S(2)}) copy-start(f32[4]{0:T(128)} %get-tuple-element.27) | copy-start | bytes 52
  41.0 12.3 %collective-permute-start.7 = (bf16[2,128,512]{2,1,0:T(8,128)(2,1)S(1)}, bf16[2,128,512]{2,1,0:T(8,128)(2,1)S(1)}, u32[]{:S(2)}, u32[]{:S(2)}) collective-permute-start(bf16[2,128,512]{2,1,0:T(8,128)(2,1)S(1)} %maximum_select_fusion.5), channel_id=1, source_target_pairs={{0,8},{4,12},{8,0},{12,4},{16,24},{20,28},{24,16},{28,20},{1,9},{5... | collective-permute-start | bytes 786440 | tf_op jit(solution)/shard_map/ppermute | solution.py:47
  53.4 7.7 %collective-permute-start.8 = (bf16[4,128,512]{2,1,0:T(8,128)(2,1)S(1)}, bf16[4,128,512]{2,1,0:T(8,128)(2,1)S(1)}, u32[]{:S(2)}, u32[]{:S(2)}) collective-permute-start(bf16[4,128,512]{2,1,0:T(8,128)(2,1)S(1)} %maximum_select_fusion.3), channel_id=1, source_target_pairs={{0,4},{4,0},{8,12},{12,8},{16,20},{20,16},{24,28},{28,24},{1,5},{5... | collective-permute-start | bytes 1572872 | tf_op jit(solution)/shard_map/ppermute | solution.py:47
  61.3 1.8 %copy-start.1 = (f32[128,1024]{1,0:T(8,128)S(1)}, f32[128,1024]{1,0:T(8,128)}, u32[]{:S(2)}) copy-start(f32[128,1024]{1,0:T(8,128)} %get-tuple-element.33) | copy-start | bytes 1572868
  61.3 1.8 %copy-start.15 = (f32[4]{0:T(128)S(1)}, f32[4]{0:T(128)}, u32[]{:S(2)}) copy-start(f32[4]{0:T(128)} %get-tuple-element.29) | copy-start | bytes 52
  61.3 1.8 %copy-start.16 = (f32[4]{0:T(128)S(1)}, f32[4]{0:T(128)}, u32[]{:S(2)}) copy-start(f32[4]{0:T(128)} %get-tuple-element.30) | copy-start | bytes 52
  61.3 1.8 %copy-start.17 = (f32[4]{0:T(128)S(1)}, f32[4]{0:T(128)}, u32[]{:S(2)}) copy-start(f32[4]{0:T(128)} %get-tuple-element.31) | copy-start | bytes 52
  61.3 1.8 %copy-start.18 = (f32[4]{0:T(128)S(1)}, f32[4]{0:T(128)}, u32[]{:S(2)}) copy-start(f32[4]{0:T(128)} %get-tuple-element.32) | copy-start | bytes 52
  62.3 1.1 %copy-start.2 = (f32[128,1024]{1,0:T(8,128)S(1)}, f32[128,1024]{1,0:T(8,128)}, u32[]{:S(2)}) copy-start(f32[128,1024]{1,0:T(8,128)} %get-tuple-element.34) | copy-start | bytes 1572868
  63.3 2.0 %copy-start.7 = (f32[512]{0:T(512)S(1)}, f32[512]{0:T(512)}, u32[]{:S(2)}) copy-start(f32[512]{0:T(512)} %param.11) | copy-start | bytes 6148
  65.3 9.3 %copy-start.14 = (pred[4]{0:T(512)(128)(4,1)S(1)}, pred[4]{0:T(512)(128)(4,1)}, u32[]{:S(2)}) copy-start(pred[4]{0:T(512)(128)(4,1)} %copy-done.13) | copy-start | bytes 16
  65.8 5.8 %collective-permute-start.10 = (bf16[32,512]{1,0:T(8,128)(2,1)S(1)}, bf16[32,512]{1,0:T(8,128)(2,1)S(1)}, u32[]{:S(2)}, u32[]{:S(2)}) collective-permute-start(bf16[32,512]{1,0:T(8,128)(2,1)S(1)} %copy.125), channel_id=1, source_target_pairs={{0,1},{1,2},{2,3},{3,0},{4,5},{5,6},{6,7},{7,4},{8,9},{9,10},{10,1... | collective-permute-start | bytes 98312 | tf_op jit(solution)/shard_map/ppermute | solution.py:33
  68.6 5.2 %collective-permute-start.11 = (bf16[32,512]{1,0:T(8,128)(2,1)S(1)}, bf16[32,512]{1,0:T(8,128)(2,1)S(1)}, u32[]{:S(2)}, u32[]{:S(2)}) collective-permute-start(bf16[32,512]{1,0:T(8,128)(2,1)S(1)} %copy.126), channel_id=1, source_target_pairs={{0,2},{1,3},{2,0},{3,1},{4,6},{5,7},{6,4},{7,5},{8,10},{9,11},{10,... | collective-permute-start | bytes 98312 | tf_op jit(solution)/shard_map/ppermute | solution.py:33
  70.0 4.1 %collective-permute-start.12 = (bf16[32,512]{1,0:T(8,128)(2,1)S(1)}, bf16[32,512]{1,0:T(8,128)(2,1)S(1)}, u32[]{:S(2)}, u32[]{:S(2)}) collective-permute-start(bf16[32,512]{1,0:T(8,128)(2,1)S(1)} %copy.127), channel_id=1, source_target_pairs={{0,3},{1,0},{2,1},{3,2},{4,7},{5,4},{6,5},{7,6},{8,11},{9,8},{10,9... | collective-permute-start | bytes 98312 | tf_op jit(solution)/shard_map/ppermute | solution.py:33

commit v18 on v15

--- a/solution.py
+++ b/solution.py
@@ -79,7 +79,7 @@
             high_ref[top : top + edge] = high[:edge, :KEY_BLOCK]
             low_ref[top : top + edge] = low[:edge, :KEY_BLOCK]
 
-    blocks = conv_ref.shape[1] // KEY_BLOCK
+    blocks = conv_ref.shape[0] // KEY_BLOCK
     body = QCONV * KEY_BLOCK
     for block in range(blocks):
         start = pl.multiple_of((group * blocks + block) * KEY_BLOCK, KEY_BLOCK)
@@ -105,12 +105,10 @@
                                (rest_rows, slice(base + edge, base + KEY_BLOCK))):
                 part_high = part.astype(jnp.bfloat16)
                 part_low = (part - part_high.astype(jnp.float32)).astype(jnp.bfloat16)
-                conv_ref[0, rows, cols] = part_high
-                conv_ref[1, rows, cols] = part_low
-    query = query_ref[0]
-    out_ref[0] = jnp.dot(conv_ref[0], query, preferred_element_type=jnp.float32) + jnp.dot(
-        conv_ref[1], query, preferred_element_type=jnp.float32
-    )
+                low_cols = slice(body + cols.start, body + cols.stop)
+                conv_ref[rows, cols] = part_high
+                conv_ref[rows, low_cols] = part_low
+    out_ref[0] = jnp.dot(conv_ref[...], query_ref[0], preferred_element_type=jnp.float32)
 
 
 def conv_logits(shifted_t, score_kernel, key_pad):
@@ -124,7 +122,7 @@
         grid=(heads, seq_len // span),
         in_specs=[
             pl.BlockSpec(memory_space=pltpu.SMEM),
-            pl.BlockSpec((1, contract, row_count), lambda h, g: (h, 0, 0)),
+            pl.BlockSpec((1, 2 * contract, row_count), lambda h, g: (h, 0, 0)),
             pl.BlockSpec((key_pad.shape[0], head_dim), lambda h, g: (0, h)),
         ],
         out_specs=pl.BlockSpec((1, span, row_count), lambda h, g: (h, g, 0)),
@@ -132,9 +130,9 @@
         scratch_shapes=[
             pltpu.VMEM((QCONV * (KEY_BLOCK + 16), KEY_BLOCK), jnp.bfloat16),
             pltpu.VMEM((QCONV * (KEY_BLOCK + 16), KEY_BLOCK), jnp.bfloat16),
-            pltpu.VMEM((2, span, QCONV * head_dim), jnp.bfloat16),
+            pltpu.VMEM((span, 2 * QCONV * head_dim), jnp.bfloat16),
         ],
-    )(taps, shifted_t, key_pad)
+    )(taps, jnp.concatenate([shifted_t, shifted_t], axis=1), key_pad)
 
 
 def band_terms(query_rows, query_first, key_flat, score_kernel):

time: 71.6 us -> 71.9 us (level)
  other arithmetic: 8.44 us -> 10.4 us
  starting transfers between devices: 20.9 us -> 20.1 us
    ppermute x6, waiting for transfers between devices: 6.73 us -> 4.99 us  [exchanged(): received.append(lax.ppermute(outgoing, axis, pairs))]
    concatenate x0 -> x1, other arithmetic: none -> 1.25 us  [conv_logits(): jnp.concatenate([shifted_t, shifted_t], axis=1)]
    ppermute x6, waiting for transfers between devices: 10.1 us -> 11.4 us  [gathered(): incoming = lax.ppermute(held, axis, [(i, i ^ bit) for i in range(peers)])]
    slice x1, local copies, waits for them, and re-layouts: 0.4 us -> 1.35 us  [band_terms(): score_kernel[None, :, row_lag, col_lag]]
    ppermute x6, starting transfers between devices: 7.37 us -> 6.49 us  [gathered(): incoming = lax.ppermute(held, axis, [(i, i ^ bit) for i in range(peers)])]
  transfers between devices with their start and end apart: 13 -> 13, of which waited for: 9 -> 7; matrix products, arithmetic and copies ran while one was open for 15% -> 18% of each run, Pallas kernels for 15% -> 15%
where the time goes in v18:
time: 71.9 us; the launch traced here: 71.6 us
  starting transfers between devices  20.1 us (28%)
  waiting for transfers between devices  16.4 us (23%)
  local copies, waits for them, and re-layouts  11.2 us (16%)
  Pallas kernels  10.9 us (15%)
  other arithmetic  10.4 us (14%)
  matrix products  2.13 us (3%)
    ppermute x6, starting transfers between devices, exchanged(): received.append(lax.ppermute(outgoing, axis, pairs))  12.1 us
    ppermute x6, waiting for transfers between devices, gathered(): incoming = lax.ppermute(held, axis, [(i, i ^ bit) for i in range(peers)])  11.4 us
    pallas_call x1, Pallas kernels, conv_logits(): pl.pallas_call(logits_kernel, grid=(heads, seq_len // span), in_specs=[pl...  10.9 us
    ppermute x6, starting transfers between devices, gathered(): incoming = lax.ppermute(held, axis, [(i, i ^ bit) for i in range(peers)])  6.49 us
    ppermute x6, waiting for transfers between devices, exchanged(): received.append(lax.ppermute(outgoing, axis, pairs))  4.99 us
    div x1, other arithmetic, attend_chunk(): probabilities = expd / jnp.sum(expd, axis=1, keepdims=True)  3.88 us
    dot_general x1, matrix products, attend_chunk(): jnp.einsum('hki,khd->ihd', mixed_probs, value_heads, preferred_element_ty...  2.13 us
    ppermute x1, starting transfers between devices, passed_along(): return lax.ppermute(shard, axis, pairs)  1.51 us
  transfers between devices with their start and end apart: 13, of which 7 were waited for; matrix products, arithmetic and copies ran while one was open for 18% of the time, Pallas kernels for 15%

profile of v18, /device:TPU:0, one launch (start us, length us, event | category | flops | bytes accessed | tf_op | source)
XLA Modules:
  0.0 71.6 jit_solution(10420143740415785615)
XLA Ops:
  0.0 1.1 %pad_maximum_fusion.1 = bf16[3,32,2048]{2,1,0:T(8,128)(2,1)S(1)} fusion(bf16[1,32,2048]{2,1,0:T(8,128)(2,1)} %bitcast.92, bf16[1,32,2048]{2,1,0:T(8,128)(2,1)} %bitcast.93, bf16[1,32,2048]{2,1,0:T(8,128)(2,1)} %bitcast.94), kind=kLoop, calls=%fused_computation.41 | loop fusion | flops 393216 | bytes 786432 | tf_op jit(solution)/shard_map/stack | solution.py:197
  1.1 3.1 %collective-permute-start = (bf16[3,32,512]{2,1,0:T(8,128)(2,1)S(1)}, bf16[3,32,512]{2,1,0:T(8,128)(2,1)S(1)}, u32[]{:S(2)}, u32[]{:S(2)}) collective-permute-start(bf16[3,32,512]{2,1,0:T(8,128)(2,1)S(1)} %get-tuple-element.43), channel_id=1, source_target_pairs={{0,1},{1,2},{2,3},{3,0},{4,5},{5,6},{6,7},{7,4},{8,9},{9,10},{10,1... | collective-permute-start | bytes 294920 | tf_op jit(solution)/shard_map/ppermute | solution.py:33
  4.2 2.6 %collective-permute-start.1 = (bf16[3,32,512]{2,1,0:T(8,128)(2,1)S(1)}, bf16[3,32,512]{2,1,0:T(8,128)(2,1)S(1)}, u32[]{:S(2)}, u32[]{:S(2)}) collective-permute-start(bf16[3,32,512]{2,1,0:T(8,128)(2,1)S(1)} %get-tuple-element.42), channel_id=1, source_target_pairs={{0,2},{1,3},{2,0},{3,1},{4,6},{5,7},{6,4},{7,5},{8,10},{9,11},{10,... | collective-permute-start | bytes 294920 | tf_op jit(solution)/shard_map/ppermute | solution.py:33
  6.8 1.3 %collective-permute-start.2 = (bf16[3,32,512]{2,1,0:T(8,128)(2,1)S(1)}, bf16[3,32,512]{2,1,0:T(8,128)(2,1)S(1)}, u32[]{:S(2)}, u32[]{:S(2)}) collective-permute-start(bf16[3,32,512]{2,1,0:T(8,128)(2,1)S(1)} %get-tuple-element.41), channel_id=1, source_target_pairs={{0,3},{1,0},{2,1},{3,2},{4,7},{5,4},{6,5},{7,6},{8,11},{9,8},{10,9... | collective-permute-start | bytes 294920 | tf_op jit(solution)/shard_map/ppermute | solution.py:33
  8.2 1.4 %slice_reduce_fusion.17 = (f32[4]{0:T(128)S(1)}, f32[4]{0:T(128)S(1)}, f32[4]{0:T(128)S(1)}, f32[4]{0:T(128)S(1)}, f32[4]{0:T(128)S(1)}, /*index=5*/f32[4]{0:T(1...) fusion(f32[4,6,11]{2,0,1:T(4,128)} %param.9), kind=kLoop, calls=%fused_computation.136 | loop fusion | bytes 480 | tf_op jit(solution)/shard_map/slice | solution.py:157
  9.5 0.7 %broadcast_multiply_fusion = f32[4,6,11]{2,0,1:T(4,128)S(1)} fusion(f32[4,6,11]{2,0,1:T(4,128)} %param.9), kind=kLoop, calls=%fused_computation.76 | loop fusion | flops 264 | bytes 2112 | tf_op jit(solution)/shard_map/mul | solution.py:119
  10.3 1.2 %fusion.15 = (pred[1024,128]{1,0:T(8,128)(4,1)}, pred[1024,128]{1,0:T(8,128)(4,1)}, pred[1024,128]{1,0:T(8,128)(4,1)}, pred[1024,128]{1,0:T(8,128)(4,1)}, pred[1...) fusion(s32[128]{0:T(128)S(1)} %iota_add_fusion), kind=kLoop, calls=%fused_computation.40 | loop fusion | flops 917504 | bytes 786944 | tf_op jit(solution)/shard_map/ge | solution.py:173
  11.5 1.9 %collective-permute-done.1 = bf16[3,32,512]{2,1,0:T(8,128)(2,1)S(1)} collective-permute-done((bf16[3,32,512]{2,1,0:T(8,128)(2,1)S(1)}, bf16[3,32,512]{2,1,0:T(8,128)(2,1)S(1)}, u32[]{:S(2)}, u32[]{:S(2)}) %collective-permute-start.1) | collective-permute-done | bytes 98336 | tf_op jit(solution)/shard_map/ppermute | solution.py:33
  13.5 0.6 gather_fusion
  14.1 0.1 select_bitcast_fusion
  14.2 1.6 %collective-permute-start.3 = (bf16[1,128,512]{2,1,0:T(8,128)(2,1)S(1)}, bf16[1,128,512]{2,1,0:T(8,128)(2,1)S(1)}, u32[]{:S(2)}, u32[]{:S(2)}) collective-permute-start(bf16[1,128,512]{2,1,0:T(8,128)(2,1)S(1)} %bitcast.85), channel_id=1, source_target_pairs={{0,16},{4,20},{8,24},{12,28},{16,0},{20,4},{24,8},{28,12},{1,17},{... | collective-permute-start | bytes 393224 | tf_op jit(solution)/shard_map/ppermute | solution.py:47
  15.8 0.8 %slice_reduce_fusion.18 = (f32[4]{0:T(128)}, f32[4]{0:T(128)}, f32[4]{0:T(128)}, f32[4]{0:T(128)}) fusion(f32[1,4,4]{2,1,0:T(4,128)S(1)} %bitcast.99), kind=kLoop, calls=%fused_computation.137 | loop fusion | bytes 128 | tf_op jit(solution)/shard_map/slice | solution.py:181
  16.6 0.7 reshape.181.taps_ref
  17.3 1.5 %collective-permute-start.9 = (bf16[5,512]{1,0:T(8,128)(2,1)S(1)}, bf16[5,512]{1,0:T(8,128)(2,1)S(1)}, u32[]{:S(2)}, u32[]{:S(2)}) collective-permute-start(bf16[5,512]{1,0:T(8,128)(2,1)S(1)} %slice.270), channel_id=1, source_target_pairs={{0,4},{4,8},{8,12},{12,16},{16,20},{20,24},{24,28},{1,5},{5,9},{9,... | collective-permute-start | bytes 15368 | tf_op jit(solution)/shard_map/ppermute | solution.py:23
  18.9 0.1 copy.70
  19.0 0.5 collective-permute-done.3
  19.6 1.6 %collective-permute-start.4 = (bf16[2,128,512]{2,1,0:T(8,128)(2,1)S(1)}, bf16[2,128,512]{2,1,0:T(8,128)(2,1)S(1)}, u32[]{:S(2)}, u32[]{:S(2)}) collective-permute-start(bf16[2,128,512]{2,1,0:T(8,128)(2,1)S(1)} %maximum_select_fusion.4), channel_id=1, source_target_pairs={{0,8},{4,12},{8,0},{12,4},{16,24},{20,28},{24,16},{28,20},{1,9},{5... | collective-permute-start | bytes 786440 | tf_op jit(solution)/shard_map/ppermute | solution.py:47
  21.1 0.1 pad_maximum_fusion.4
  21.3 0.1 copy.65
  21.4 0.1 copy.66
  21.5 0.1 copy.67
  21.7 6.7 %collective-permute-done.4 = bf16[2,128,512]{2,1,0:T(8,128)(2,1)S(1)} collective-permute-done((bf16[2,128,512]{2,1,0:T(8,128)(2,1)S(1)}, bf16[2,128,512]{2,1,0:T(8,128)(2,1)S(1)}, u32[]{:S(2)}, u32[]{:S(2)}) %collective-permute-start.4) | collective-permute-done | bytes 262176 | tf_op jit(solution)/shard_map/ppermute | solution.py:47
  28.5 0.3 collective-permute-start.5
  28.8 0.1 copy.68
  29.0 0.1 copy.69
  29.2 1.3 %pad_maximum_fusion.query_ref = bf16[4,1536,128]{2,1,0:T(8,128)(2,1)} fusion(bf16[4,768,128]{2,1,0:T(8,128)(2,1)S(1)} %bitcast.82), kind=kLoop, calls=%fused_computation.8 | loop fusion | flops 3145728 | bytes 2359296 | tf_op jit(solution)/shard_map/concatenate | solution.py:135
  30.4 0.2 maximum_select_fusion
  30.6 0.1 copy.62
  30.7 0.1 fusion.24
  30.9 0.1 fusion.56
  31.0 0.1 slice.221
  31.1 0.6 copy-done
  31.7 0.1 slice.225
  31.8 0.1 slice.231
  31.9 0.1 slice.239
  32.0 0.1 slice.249
  32.1 0.8 %fusion.21 = (f32[133,4]{1,0:T(8,128)S(1)}, f32[133,4]{1,0:T(8,128)S(1)}, f32[133,4]{1,0:T(8,128)S(1)}, f32[133,4]{1,0:T(8,128)S(1)}, f32[133,4]{1,0:T(8,128)S(1)}) fusion(f32[133,4,128]{2,1,0:T(4,128)S(1)} %slice.249, bf16[128,4,128]{2,1,0:T(4,128)(2,1)S(1)} %concatenate.67, bf16[5,4,128]{2,1,0:T(4,128)(2,1)S(1)} %concatenate.66, ...), kind=kLoop, calls=%fused_computation.53 | loop fusion | flops 814492 | bytes 1508752 | tf_op jit(solution)/shard_map/reduce_sum | solution.py:148
  33.0 0.1 copy.74
  33.1 0.1 copy.72
  33.1 0.1 copy.73
  33.2 1.5 %collective-permute-start.6 = (bf16[1,128,512]{2,1,0:T(8,128)(2,1)S(1)}, bf16[1,128,512]{2,1,0:T(8,128)(2,1)S(1)}, u32[]{:S(2)}, u32[]{:S(2)}) collective-permute-start(bf16[1,128,512]{2,1,0:T(8,128)(2,1)S(1)} %bitcast.83), channel_id=1, source_target_pairs={{0,16},{4,20},{8,24},{12,28},{16,0},{20,4},{24,8},{28,12},{1,17},{... | collective-permute-start | bytes 393224 | tf_op jit(solution)/shard_map/ppermute | solution.py:47
  34.8 4.1 %collective-permute-done.6 = bf16[1,128,512]{2,1,0:T(8,128)(2,1)S(1)} collective-permute-done((bf16[1,128,512]{2,1,0:T(8,128)(2,1)S(1)}, bf16[1,128,512]{2,1,0:T(8,128)(2,1)S(1)}, u32[]{:S(2)}, u32[]{:S(2)}) %collective-permute-start.6) | collective-permute-done | bytes 131104 | tf_op jit(solution)/shard_map/ppermute | solution.py:47
  39.0 1.4 %collective-permute-start.7 = (bf16[2,128,512]{2,1,0:T(8,128)(2,1)S(1)}, bf16[2,128,512]{2,1,0:T(8,128)(2,1)S(1)}, u32[]{:S(2)}, u32[]{:S(2)}) collective-permute-start(bf16[2,128,512]{2,1,0:T(8,128)(2,1)S(1)} %maximum_select_fusion.5), channel_id=1, source_target_pairs={{0,8},{4,12},{8,0},{12,4},{16,24},{20,28},{24,16},{28,20},{1,9},{5... | collective-permute-start | bytes 786440 | tf_op jit(solution)/shard_map/ppermute | solution.py:47
  40.6 10.9 %shard_map.64 = f32[4,1024,128]{2,1,0:T(8,128)} custom-call(f32[264]{0:T(512)} %reshape.181.taps_ref, bf16[4,1536,128]{2,1,0:T(8,128)(2,1)} %pad_maximum_fusion.query_ref, bf16[1024,512]{1,0:T(8,128)(2,1)} %bitcast.76), custom_call_target="tpu_custom_call" | custom-call | tf_op jit(solution)/shard_map/pallas_call | solution.py:120
  51.4 0.1 fusion.44
  51.5 0.1 maximum_select_fusion.3
  51.7 3.9 %divide_bitcast_fusion = f32[1,4,1024,128]{3,2,1,0:T(8,128)S(1)} fusion(f32[4,1024,128]{2,1,0:T(8,128)} %shard_map.64, f32[4,128]{1,0:T(4,128)S(1)} %get-tuple-element.60, f32[4,128]{1,0:T(4,128)S(1)} %get-tuple-element.59, f32[4,128]{1,0:T(4,128)S(1)} %get-tuple-element.58, f32[4,128]{1,0:T(4,128)S(1)} %subtract_bitcast_fusion.3, f32[4,128]{1,0:T(4,128)S(1)} %fusion.44, ...), kind=kOutput, calls=%fused_computation.5 | output fusion | flops 6818814 | bytes 4990976 | tf_op jit(solution)/shard_map/div | solution.py:176
  55.6 1.4 %slice_bitcast_fusion.3 = (f32[1024,128]{1,0:T(8,128)}, f32[1024,128]{1,0:T(8,128)}, f32[1024,128]{1,0:T(8,128)}, f32[1024,128]{1,0:T(8,128)}) fusion(f32[1,4,1024,128]{3,2,1,0:T(8,128)S(1)} %divide_bitcast_fusion), kind=kLoop, calls=%fused_computation.31 | loop fusion | bytes 4194304 | tf_op jit(solution)/shard_map/mul | solution.py:181
  57.0 0.2 maximum_select_fusion.1
  57.2 0.9 %copy.63 = bf16[2,2,2,128,512]{3,2,1,0,4:T(2,128)(2,1)S(1)} copy(bf16[2,2,2,128,512]{4,3,0,1,2:T(8,128)(2,1)S(1)} %bitcast.77) | data formatting | bytes 2097152 | tf_op jit(solution)/shard_map/transpose | solution.py:55
  58.2 0.8 %reshape_reshape.3 = bf16[1024,4,128]{0,2,1:T(8,128)(2,1)S(1)} reshape(bf16[2,2,2,128,512]{3,2,1,0,4:T(2,128)(2,1)S(1)} %copy.63) | data formatting | bytes 2097152 | tf_op jit(solution)/shard_map/reshape;reshape | solution.py:228
  59.0 0.2 copy-done.2
  59.2 2.1 %multiply_reduce_fusion = (f32[128,4]{0,1:T(4,128)S(1)}, f32[128,4,128]{0,2,1:T(8,128)S(1)}) fusion(bf16[1024,4,128]{0,2,1:T(8,128)(2,1)S(1)} %reshape_reshape.3, f32[1024,128]{1,0:T(8,128)S(1)} %copy-done.2, f32[4]{0:T(128)S(1)} %copy-done.8, f32[1024,128]{1,0:T(8,128)} %get-tuple-element.35, f32[4]{0:T(128)S(1)} %copy-done.9, ...), kind=kOutput, calls=%fused_computation.57 | convolution fusion | flops 138542592 | bytes 3409984 | tf_op jit(solution)/shard_map/hki,khd->ihd/dot_general | solution.py:183
  61.4 0.1 multiply_convert_fusion
  61.5 0.2 constant_dynamic-slice_fusion.3
  61.8 2.6 %collective-permute-start.10 = (bf16[32,512]{1,0:T(8,128)(2,1)S(1)}, bf16[32,512]{1,0:T(8,128)(2,1)S(1)}, u32[]{:S(2)}, u32[]{:S(2)}) collective-permute-start(bf16[32,512]{1,0:T(8,128)(2,1)S(1)} %copy.81), channel_id=1, source_target_pairs={{0,1},{1,2},{2,3},{3,0},{4,5},{5,6},{6,7},{7,4},{8,9},{9,10},{10,1... | collective-permute-start | bytes 98312 | tf_op jit(solution)/shard_map/ppermute | solution.py:33
  64.5 1.7 %collective-permute-start.11 = (bf16[32,512]{1,0:T(8,128)(2,1)S(1)}, bf16[32,512]{1,0:T(8,128)(2,1)S(1)}, u32[]{:S(2)}, u32[]{:S(2)}) collective-permute-start(bf16[32,512]{1,0:T(8,128)(2,1)S(1)} %copy.82), channel_id=1, source_target_pairs={{0,2},{1,3},{2,0},{3,1},{4,6},{5,7},{6,4},{7,5},{8,10},{9,11},{10,... | collective-permute-start | bytes 98312 | tf_op jit(solution)/shard_map/ppermute | solution.py:33
  66.3 0.8 %collective-permute-start.12 = (bf16[32,512]{1,0:T(8,128)(2,1)S(1)}, bf16[32,512]{1,0:T(8,128)(2,1)S(1)}, u32[]{:S(2)}, u32[]{:S(2)}) collective-permute-start(bf16[32,512]{1,0:T(8,128)(2,1)S(1)} %copy.83), channel_id=1, source_target_pairs={{0,3},{1,0},{2,1},{3,2},{4,7},{5,4},{6,5},{7,6},{8,11},{9,8},{10,9... | collective-permute-start | bytes 98312 | tf_op jit(solution)/shard_map/ppermute | solution.py:33
  67.2 0.4 collective-permute-done.10
  67.6 2.1 %collective-permute-done.11 = bf16[32,512]{1,0:T(8,128)(2,1)S(1)} collective-permute-done((bf16[32,512]{1,0:T(8,128)(2,1)S(1)}, bf16[32,512]{1,0:T(8,128)(2,1)S(1)}, u32[]{:S(2)}, u32[]{:S(2)}) %collective-permute-start.11) | collective-permute-done | bytes 32800 | tf_op jit(solution)/shard_map/ppermute | solution.py:33
  69.7 0.5 collective-permute-done.12
  70.3 0.6 gather_fusion.1
  70.9 0.1 select_bitcast_fusion.1
  70.9 0.7 copy.85
  (62 shorter events, 1.4 us)
Async XLA Ops:
  1.1 14.7 %copy-start.3 = (f32[4,4]{1,0:T(4,128)S(1)}, f32[4,4]{1,0:T(4,128)}, u32[]{:S(2)}) copy-start(f32[4,4]{1,0:T(4,128)} %param.10) | copy-start | bytes 196
  1.1 10.4 %collective-permute-start = (bf16[3,32,512]{2,1,0:T(8,128)(2,1)S(1)}, bf16[3,32,512]{2,1,0:T(8,128)(2,1)S(1)}, u32[]{:S(2)}, u32[]{:S(2)}) collective-permute-start(bf16[3,32,512]{2,1,0:T(8,128)(2,1)S(1)} %get-tuple-element.43), channel_id=1, source_target_pairs={{0,1},{1,2},{2,3},{3,0},{4,5},{5,6},{6,7},{7,4},{8,9},{9,10},{10,1... | collective-permute-start | bytes 294920 | tf_op jit(solution)/shard_map/ppermute | solution.py:33
  4.2 9.2 %collective-permute-start.1 = (bf16[3,32,512]{2,1,0:T(8,128)(2,1)S(1)}, bf16[3,32,512]{2,1,0:T(8,128)(2,1)S(1)}, u32[]{:S(2)}, u32[]{:S(2)}) collective-permute-start(bf16[3,32,512]{2,1,0:T(8,128)(2,1)S(1)} %get-tuple-element.42), channel_id=1, source_target_pairs={{0,2},{1,3},{2,0},{3,1},{4,6},{5,7},{6,4},{7,5},{8,10},{9,11},{10,... | collective-permute-start | bytes 294920 | tf_op jit(solution)/shard_map/ppermute | solution.py:33
  6.8 6.6 %collective-permute-start.2 = (bf16[3,32,512]{2,1,0:T(8,128)(2,1)S(1)}, bf16[3,32,512]{2,1,0:T(8,128)(2,1)S(1)}, u32[]{:S(2)}, u32[]{:S(2)}) collective-permute-start(bf16[3,32,512]{2,1,0:T(8,128)(2,1)S(1)} %get-tuple-element.41), channel_id=1, source_target_pairs={{0,3},{1,0},{2,1},{3,2},{4,7},{5,4},{6,5},{7,6},{8,11},{9,8},{10,9... | collective-permute-start | bytes 294920 | tf_op jit(solution)/shard_map/ppermute | solution.py:33
  11.5 7.5 %copy-start.5 = (pred[4]{0:T(512)(128)(4,1)}, pred[4]{0:T(512)(128)(4,1)S(1)}, u32[]{:S(2)}) copy-start(pred[4]{0:T(512)(128)(4,1)S(1)} %compare_and_fusion) | copy-start | bytes 16
  14.2 5.3 %collective-permute-start.3 = (bf16[1,128,512]{2,1,0:T(8,128)(2,1)S(1)}, bf16[1,128,512]{2,1,0:T(8,128)(2,1)S(1)}, u32[]{:S(2)}, u32[]{:S(2)}) collective-permute-start(bf16[1,128,512]{2,1,0:T(8,128)(2,1)S(1)} %bitcast.85), channel_id=1, source_target_pairs={{0,16},{4,20},{8,24},{12,28},{16,0},{20,4},{24,8},{28,12},{1,17},{... | collective-permute-start | bytes 393224 | tf_op jit(solution)/shard_map/ppermute | solution.py:47
  17.3 3.8 %collective-permute-start.9 = (bf16[5,512]{1,0:T(8,128)(2,1)S(1)}, bf16[5,512]{1,0:T(8,128)(2,1)S(1)}, u32[]{:S(2)}, u32[]{:S(2)}) collective-permute-start(bf16[5,512]{1,0:T(8,128)(2,1)S(1)} %slice.270), channel_id=1, source_target_pairs={{0,4},{4,8},{8,12},{12,16},{16,20},{20,24},{24,28},{1,5},{5,9},{9,... | collective-permute-start | bytes 15368 | tf_op jit(solution)/shard_map/ppermute | solution.py:23
  19.6 8.8 %collective-permute-start.4 = (bf16[2,128,512]{2,1,0:T(8,128)(2,1)S(1)}, bf16[2,128,512]{2,1,0:T(8,128)(2,1)S(1)}, u32[]{:S(2)}, u32[]{:S(2)}) collective-permute-start(bf16[2,128,512]{2,1,0:T(8,128)(2,1)S(1)} %maximum_select_fusion.4), channel_id=1, source_target_pairs={{0,8},{4,12},{8,0},{12,4},{16,24},{20,28},{24,16},{28,20},{1,9},{5... | collective-permute-start | bytes 786440 | tf_op jit(solution)/shard_map/ppermute | solution.py:47
  28.5 2.0 %collective-permute-start.5 = (bf16[4,128,512]{2,1,0:T(8,128)(2,1)S(1)}, bf16[4,128,512]{2,1,0:T(8,128)(2,1)S(1)}, u32[]{:S(2)}, u32[]{:S(2)}) collective-permute-start(bf16[4,128,512]{2,1,0:T(8,128)(2,1)S(1)} %maximum_select_fusion.2), channel_id=1, source_target_pairs={{0,4},{4,0},{8,12},{12,8},{16,20},{20,16},{24,28},{28,24},{1,5},{5... | collective-permute-start | bytes 1572872 | tf_op jit(solution)/shard_map/ppermute | solution.py:47
  30.7 1.0 %copy-start = (bf16[2,2,2,128,512]{4,3,2,1,0:T(8,128)(2,1)}, bf16[2,2,2,128,512]{4,3,2,1,0:T(8,128)(2,1)S(1)}, u32[]{:S(2)}) copy-start(bf16[2,2,2,128,512]{4,3,2,1,0:T(8,128)(2,1)S(1)} %copy.62) | copy-start | bytes 3145732
  33.2 5.7 %collective-permute-start.6 = (bf16[1,128,512]{2,1,0:T(8,128)(2,1)S(1)}, bf16[1,128,512]{2,1,0:T(8,128)(2,1)S(1)}, u32[]{:S(2)}, u32[]{:S(2)}) collective-permute-start(bf16[1,128,512]{2,1,0:T(8,128)(2,1)S(1)} %bitcast.83), channel_id=1, source_target_pairs={{0,16},{4,20},{8,24},{12,28},{16,0},{20,4},{24,8},{28,12},{1,17},{... | collective-permute-start | bytes 393224 | tf_op jit(solution)/shard_map/ppermute | solution.py:47
  39.0 12.6 %collective-permute-start.7 = (bf16[2,128,512]{2,1,0:T(8,128)(2,1)S(1)}, bf16[2,128,512]{2,1,0:T(8,128)(2,1)S(1)}, u32[]{:S(2)}, u32[]{:S(2)}) collective-permute-start(bf16[2,128,512]{2,1,0:T(8,128)(2,1)S(1)} %maximum_select_fusion.5), channel_id=1, source_target_pairs={{0,8},{4,12},{8,0},{12,4},{16,24},{20,28},{24,16},{28,20},{1,9},{5... | collective-permute-start | bytes 786440 | tf_op jit(solution)/shard_map/ppermute | solution.py:47
  51.6 5.4 %collective-permute-start.8 = (bf16[4,128,512]{2,1,0:T(8,128)(2,1)S(1)}, bf16[4,128,512]{2,1,0:T(8,128)(2,1)S(1)}, u32[]{:S(2)}, u32[]{:S(2)}) collective-permute-start(bf16[4,128,512]{2,1,0:T(8,128)(2,1)S(1)} %maximum_select_fusion.3), channel_id=1, source_target_pairs={{0,4},{4,0},{8,12},{12,8},{16,20},{20,16},{24,28},{28,24},{1,5},{5... | collective-permute-start | bytes 1572872 | tf_op jit(solution)/shard_map/ppermute | solution.py:47
  57.2 1.8 %copy-start.1 = (f32[1024,128]{1,0:T(8,128)S(1)}, f32[1024,128]{1,0:T(8,128)}, u32[]{:S(2)}) copy-start(f32[1024,128]{1,0:T(8,128)} %get-tuple-element.33) | copy-start | bytes 1572868
  57.2 1.8 %copy-start.7 = (f32[4]{0:T(128)S(1)}, f32[4]{0:T(128)}, u32[]{:S(2)}) copy-start(f32[4]{0:T(128)} %get-tuple-element.29) | copy-start | bytes 52
  57.2 1.8 %copy-start.8 = (f32[4]{0:T(128)S(1)}, f32[4]{0:T(128)}, u32[]{:S(2)}) copy-start(f32[4]{0:T(128)} %get-tuple-element.30) | copy-start | bytes 52
  57.2 1.8 %copy-start.9 = (f32[4]{0:T(128)S(1)}, f32[4]{0:T(128)}, u32[]{:S(2)}) copy-start(f32[4]{0:T(128)} %get-tuple-element.31) | copy-start | bytes 52
  58.2 1.1 %copy-start.2 = (f32[1024,128]{1,0:T(8,128)S(1)}, f32[1024,128]{1,0:T(8,128)}, u32[]{:S(2)}) copy-start(f32[1024,128]{1,0:T(8,128)} %get-tuple-element.34) | copy-start | bytes 1572868
  58.2 1.0 %copy-start.10 = (f32[4]{0:T(128)S(1)}, f32[4]{0:T(128)}, u32[]{:S(2)}) copy-start(f32[4]{0:T(128)} %get-tuple-element.32) | copy-start | bytes 52
  59.2 2.2 %copy-start.4 = (f32[512]{0:T(512)S(1)}, f32[512]{0:T(512)}, u32[]{:S(2)}) copy-start(f32[512]{0:T(512)} %param.11) | copy-start | bytes 6148
  61.4 9.5 %copy-start.6 = (pred[4]{0:T(512)(128)(4,1)S(1)}, pred[4]{0:T(512)(128)(4,1)}, u32[]{:S(2)}) copy-start(pred[4]{0:T(512)(128)(4,1)} %copy-done.5) | copy-start | bytes 16
  61.8 5.8 %collective-permute-start.10 = (bf16[32,512]{1,0:T(8,128)(2,1)S(1)}, bf16[32,512]{1,0:T(8,128)(2,1)S(1)}, u32[]{:S(2)}, u32[]{:S(2)}) collective-permute-start(bf16[32,512]{1,0:T(8,128)(2,1)S(1)} %copy.81), channel_id=1, source_target_pairs={{0,1},{1,2},{2,3},{3,0},{4,5},{5,6},{6,7},{7,4},{8,9},{9,10},{10,1... | collective-permute-start | bytes 98312 | tf_op jit(solution)/shard_map/ppermute | solution.py:33
  64.5 5.2 %collective-permute-start.11 = (bf16[32,512]{1,0:T(8,128)(2,1)S(1)}, bf16[32,512]{1,0:T(8,128)(2,1)S(1)}, u32[]{:S(2)}, u32[]{:S(2)}) collective-permute-start(bf16[32,512]{1,0:T(8,128)(2,1)S(1)} %copy.82), channel_id=1, source_target_pairs={{0,2},{1,3},{2,0},{3,1},{4,6},{5,7},{6,4},{7,5},{8,10},{9,11},{10,... | collective-permute-start | bytes 98312 | tf_op jit(solution)/shard_map/ppermute | solution.py:33
  66.3 4.0 %collective-permute-start.12 = (bf16[32,512]{1,0:T(8,128)(2,1)S(1)}, bf16[32,512]{1,0:T(8,128)(2,1)S(1)}, u32[]{:S(2)}, u32[]{:S(2)}) collective-permute-start(bf16[32,512]{1,0:T(8,128)(2,1)S(1)} %copy.83), channel_id=1, source_target_pairs={{0,3},{1,0},{2,1},{3,2},{4,7},{5,4},{6,5},{7,6},{8,11},{9,8},{10,9... | collective-permute-start | bytes 98312 | tf_op jit(solution)/shard_map/ppermute | solution.py:33

commit v19 on v15

--- a/solution.py
+++ b/solution.py
@@ -215,9 +215,8 @@
     query_first = ctx_place * shard_rows
     earlier = passed_along(query_local[shard_rows - row_lead :], "ctx", 1)
     query_ext = jnp.concatenate([earlier, query_local], axis=0)
+    value_all = lax.all_gather(value_local, "ctx", axis=0, tiled=True)
     key_all = gathered(key_local, "ctx").reshape((-1, width))
-    key_all, value_local = lax.optimization_barrier((key_all, value_local))
-    value_all = gathered(value_local, "ctx").reshape((-1, width))
     seq_len = key_all.shape[0]
     key_pad = key_all
     edge = jnp.zeros((8, width), key_all.dtype)

time: 71.6 us -> 77.2 us (1.078)
  between operations: 0.59 us -> 13.8 us
  starting transfers between devices: 20.9 us -> 17.8 us
  waiting for transfers between devices: 16.8 us -> 14.4 us
  local copies, waits for them, and re-layouts: 11.6 us -> 9.51 us
    ppermute x6 -> x3, waiting for transfers between devices: 10.1 us -> 5.25 us  [gathered(): incoming = lax.ppermute(held, axis, [(i, i ^ bit) for i in range(peers)])]
    ppermute x6 -> x3, starting transfers between devices: 7.37 us -> 4 us  [gathered(): incoming = lax.ppermute(held, axis, [(i, i ^ bit) for i in range(peers)])]
    all_gather x0 -> x1, waiting for transfers between devices: none -> 2.73 us  [shards(): value_all = lax.all_gather(value_local, 'ctx', axis=0, tiled=True)]
    transpose x2 -> x1, local copies, waits for them, and re-layouts: 1.04 us -> 0.1 us  [gathered(): jnp.transpose(held, tuple(reversed(range(bits))) + tuple(range(bits, held...]
  transfers between devices with their start and end apart: 13 -> 11, of which waited for: 9 -> 9; matrix products, arithmetic and copies ran while one was open for 15% -> 17% of each run, Pallas kernels for 15% -> 14%
where the time goes in v19:
time: 77.2 us; the launch traced here: 77 us
  starting transfers between devices  17.8 us (23%)
  waiting for transfers between devices  14.4 us (19%)
  between operations  13.8 us (18%)
  Pallas kernels  10.8 us (14%)
  local copies, waits for them, and re-layouts  9.51 us (12%)
  other arithmetic  8.11 us (11%)
  matrix products  2.44 us (3%)
    ppermute x6, starting transfers between devices, exchanged(): received.append(lax.ppermute(outgoing, axis, pairs))  12.5 us
    pallas_call x1, Pallas kernels, conv_logits(): pl.pallas_call(logits_kernel, grid=(heads, seq_len // span), in_specs=[pl...  10.8 us
    ppermute x6, waiting for transfers between devices, exchanged(): received.append(lax.ppermute(outgoing, axis, pairs))  6.44 us
    ppermute x3, waiting for transfers between devices, gathered(): incoming = lax.ppermute(held, axis, [(i, i ^ bit) for i in range(peers)])  5.25 us
    ppermute x3, starting transfers between devices, gathered(): incoming = lax.ppermute(held, axis, [(i, i ^ bit) for i in range(peers)])  4 us
    div x1, other arithmetic, attend_chunk(): probabilities = expd / jnp.sum(expd, axis=1, keepdims=True)  3.88 us
    all_gather x1, waiting for transfers between devices, shards(): value_all = lax.all_gather(value_local, 'ctx', axis=0, tiled=True)  2.73 us
    dot_general x1, matrix products, attend_chunk(): jnp.einsum('hki,khd->ihd', mixed_probs, value_heads, preferred_element_ty...  2.44 us
  transfers between devices with their start and end apart: 11, of which 9 were waited for; matrix products, arithmetic and copies ran while one was open for 17% of the time, Pallas kernels for 14%

profile of v19, /device:TPU:0, one launch (start us, length us, event | category | flops | bytes accessed | tf_op | source)
XLA Modules:
  0.0 77.0 jit_solution(10273753870866150420)
XLA Ops:
  6.5 1.1 %pad_maximum_fusion = bf16[3,32,2048]{2,1,0:T(8,128)(2,1)S(1)} fusion(bf16[1,32,2048]{2,1,0:T(8,128)(2,1)} %bitcast.85, bf16[1,32,2048]{2,1,0:T(8,128)(2,1)} %bitcast.86, bf16[1,32,2048]{2,1,0:T(8,128)(2,1)} %bitcast.87), kind=kLoop, calls=%fused_computation.38 | loop fusion | flops 393216 | bytes 786432 | tf_op jit(solution)/shard_map/stack | solution.py:199
  7.7 3.1 %collective-permute-start = (bf16[3,32,512]{2,1,0:T(8,128)(2,1)S(1)}, bf16[3,32,512]{2,1,0:T(8,128)(2,1)S(1)}, u32[]{:S(2)}, u32[]{:S(2)}) collective-permute-start(bf16[3,32,512]{2,1,0:T(8,128)(2,1)S(1)} %get-tuple-element.39), channel_id=1, source_target_pairs={{0,1},{1,2},{2,3},{3,0},{4,5},{5,6},{6,7},{7,4},{8,9},{9,10},{10,1... | collective-permute-start | bytes 294920 | tf_op jit(solution)/shard_map/ppermute | solution.py:33
  10.8 2.6 %collective-permute-start.1 = (bf16[3,32,512]{2,1,0:T(8,128)(2,1)S(1)}, bf16[3,32,512]{2,1,0:T(8,128)(2,1)S(1)}, u32[]{:S(2)}, u32[]{:S(2)}) collective-permute-start(bf16[3,32,512]{2,1,0:T(8,128)(2,1)S(1)} %get-tuple-element.38), channel_id=1, source_target_pairs={{0,2},{1,3},{2,0},{3,1},{4,6},{5,7},{6,4},{7,5},{8,10},{9,11},{10,... | collective-permute-start | bytes 294920 | tf_op jit(solution)/shard_map/ppermute | solution.py:33
  13.3 1.3 %collective-permute-start.2 = (bf16[3,32,512]{2,1,0:T(8,128)(2,1)S(1)}, bf16[3,32,512]{2,1,0:T(8,128)(2,1)S(1)}, u32[]{:S(2)}, u32[]{:S(2)}) collective-permute-start(bf16[3,32,512]{2,1,0:T(8,128)(2,1)S(1)} %get-tuple-element.37), channel_id=1, source_target_pairs={{0,3},{1,0},{2,1},{3,2},{4,7},{5,4},{6,5},{7,6},{8,11},{9,8},{10,9... | collective-permute-start | bytes 294920 | tf_op jit(solution)/shard_map/ppermute | solution.py:33
  14.7 1.2 %fusion.15 = (pred[1024,128]{1,0:T(8,128)(4,1)S(1)}, pred[1024,128]{1,0:T(8,128)(4,1)S(1)}, pred[1024,128]{1,0:T(8,128)(4,1)S(1)}, pred[1024,128]{1,0:T(8,128)(4...) fusion(s32[128]{0:T(128)S(1)} %iota_add_fusion), kind=kLoop, calls=%fused_computation.37 | loop fusion | flops 917504 | bytes 786944 | tf_op jit(solution)/shard_map/ge | solution.py:175
  15.9 0.5 collective-permute-done
  16.4 3.5 %collective-permute-done.1 = bf16[3,32,512]{2,1,0:T(8,128)(2,1)S(1)} collective-permute-done((bf16[3,32,512]{2,1,0:T(8,128)(2,1)S(1)}, bf16[3,32,512]{2,1,0:T(8,128)(2,1)S(1)}, u32[]{:S(2)}, u32[]{:S(2)}) %collective-permute-start.1) | collective-permute-done | bytes 98336 | tf_op jit(solution)/shard_map/ppermute | solution.py:33
  20.0 0.6 gather_fusion
  20.6 0.1 select_bitcast_fusion
  20.7 1.6 %collective-permute-start.4 = (bf16[1,128,512]{2,1,0:T(8,128)(2,1)S(1)}, bf16[1,128,512]{2,1,0:T(8,128)(2,1)S(1)}, u32[]{:S(2)}, u32[]{:S(2)}) collective-permute-start(bf16[1,128,512]{2,1,0:T(8,128)(2,1)S(1)} %bitcast.77), channel_id=1, source_target_pairs={{0,16},{4,20},{8,24},{12,28},{16,0},{20,4},{24,8},{28,12},{1,17},{... | collective-permute-start | bytes 393224 | tf_op jit(solution)/shard_map/ppermute | solution.py:47
  22.3 0.4 slice_reduce_fusion.17
  22.7 3.4 %collective-permute-done.4 = bf16[1,128,512]{2,1,0:T(8,128)(2,1)S(1)} collective-permute-done((bf16[1,128,512]{2,1,0:T(8,128)(2,1)S(1)}, bf16[1,128,512]{2,1,0:T(8,128)(2,1)S(1)}, u32[]{:S(2)}, u32[]{:S(2)}) %collective-permute-start.4) | collective-permute-done | bytes 131104 | tf_op jit(solution)/shard_map/ppermute | solution.py:47
  26.1 1.6 %collective-permute-start.5 = (bf16[2,128,512]{2,1,0:T(8,128)(2,1)S(1)}, bf16[2,128,512]{2,1,0:T(8,128)(2,1)S(1)}, u32[]{:S(2)}, u32[]{:S(2)}) collective-permute-start(bf16[2,128,512]{2,1,0:T(8,128)(2,1)S(1)} %maximum_select_fusion.2), channel_id=1, source_target_pairs={{0,8},{4,12},{8,0},{12,4},{16,24},{20,28},{24,16},{28,20},{1,9},{5... | collective-permute-start | bytes 786440 | tf_op jit(solution)/shard_map/ppermute | solution.py:47
  27.7 0.8 %slice_reduce_fusion.18 = (f32[4]{0:T(128)S(1)}, f32[4]{0:T(128)S(1)}, f32[4]{0:T(128)}, f32[4]{0:T(128)}) fusion(f32[1,4,4]{2,1,0:T(4,128)S(1)} %bitcast.92), kind=kLoop, calls=%fused_computation.133 | loop fusion | bytes 128 | tf_op jit(solution)/shard_map/slice | solution.py:183
  28.5 0.7 reshape.179.taps_ref
  29.2 1.3 %collective-permute-start.3 = (bf16[5,512]{1,0:T(8,128)(2,1)S(1)}, bf16[5,512]{1,0:T(8,128)(2,1)S(1)}, u32[]{:S(2)}, u32[]{:S(2)}) collective-permute-start(bf16[5,512]{1,0:T(8,128)(2,1)S(1)} %slice.270), channel_id=1, source_target_pairs={{0,4},{4,8},{8,12},{12,16},{16,20},{20,24},{24,28},{1,5},{5,9},{9,... | collective-permute-start | bytes 15368 | tf_op jit(solution)/shard_map/ppermute | solution.py:23
  30.5 0.1 copy.69
  30.7 0.7 concatenate.39
  31.3 0.8 copy.62
  32.1 0.1 pad_maximum_fusion.3
  32.3 0.1 copy.64
  32.4 0.1 copy.65
  32.5 0.1 copy.66
  32.6 0.1 copy.67
  32.8 0.1 copy.68
  32.9 0.5 collective-permute-done.5
  33.4 0.1 maximum_select_fusion.1
  33.5 0.9 %collective-permute-start.6 = (bf16[4,128,512]{2,1,0:T(8,128)(2,1)S(1)}, bf16[4,128,512]{2,1,0:T(8,128)(2,1)S(1)}, u32[]{:S(2)}, u32[]{:S(2)}) collective-permute-start(bf16[4,128,512]{2,1,0:T(8,128)(2,1)S(1)} %maximum_select_fusion.1), channel_id=1, source_target_pairs={{0,4},{4,0},{8,12},{12,8},{16,20},{20,16},{24,28},{28,24},{1,5},{5... | collective-permute-start | bytes 1572872 | tf_op jit(solution)/shard_map/ppermute | solution.py:47
  34.5 1.4 %collective-permute-done.6 = bf16[4,128,512]{2,1,0:T(8,128)(2,1)S(1)} collective-permute-done((bf16[4,128,512]{2,1,0:T(8,128)(2,1)S(1)}, bf16[4,128,512]{2,1,0:T(8,128)(2,1)S(1)}, u32[]{:S(2)}, u32[]{:S(2)}) %collective-permute-start.6) | collective-permute-done | bytes 524320 | tf_op jit(solution)/shard_map/ppermute | solution.py:47
  35.9 0.2 maximum_select_fusion
  36.1 0.1 copy.70
  36.2 0.1 fusion.24
  36.3 0.1 fusion.56
  36.5 0.1 slice.221
  36.6 0.6 copy-done
  37.2 0.1 slice.225
  37.3 0.1 slice.231
  37.4 0.1 slice.239
  37.5 0.1 slice.249
  37.6 0.8 %fusion.21 = (f32[133,4]{1,0:T(8,128)S(1)}, f32[133,4]{1,0:T(8,128)S(1)}, f32[133,4]{1,0:T(8,128)S(1)}, f32[133,4]{1,0:T(8,128)S(1)}, f32[133,4]{1,0:T(8,128)S(1)}) fusion(f32[133,4,128]{2,1,0:T(4,128)S(1)} %slice.249, bf16[128,4,128]{2,1,0:T(4,128)(2,1)S(1)} %copy-done.2, bf16[5,4,128]{2,1,0:T(4,128)(2,1)S(1)} %concatenate.38, ...), kind=kLoop, calls=%fused_computation.50 | loop fusion | flops 814492 | bytes 1508752 | tf_op jit(solution)/shard_map/reduce_sum | solution.py:150
  38.4 0.1 copy.84
  38.6 0.1 copy.74
  38.6 0.1 copy.72
  38.7 0.1 copy.73
  38.8 10.8 %shard_map.64 = f32[4,1024,128]{2,1,0:T(8,128)} custom-call(f32[264]{0:T(512)} %reshape.179.taps_ref, bf16[4,768,128]{2,1,0:T(8,128)(2,1)} %bitcast.76, bf16[1024,512]{1,0:T(8,128)(2,1)} %bitcast.71), custom_call_target="tpu_custom_call" | custom-call | tf_op jit(solution)/shard_map/pallas_call | solution.py:122
  49.7 0.1 subtract_bitcast_fusion.2
  49.8 0.1 subtract_bitcast_fusion.3
  49.9 0.1 fusion.44
  50.0 3.9 %divide_bitcast_fusion = f32[1,4,1024,128]{3,2,1,0:T(8,128)S(1)} fusion(f32[4,1024,128]{2,1,0:T(8,128)} %shard_map.64, f32[4,128]{1,0:T(4,128)S(1)} %get-tuple-element.56, f32[4,128]{1,0:T(4,128)S(1)} %get-tuple-element.55, f32[4,128]{1,0:T(4,128)S(1)} %get-tuple-element.54, f32[4,128]{1,0:T(4,128)S(1)} %subtract_bitcast_fusion.3, f32[4,128]{1,0:T(4,128)S(1)} %fusion.44, ...), kind=kOutput, calls=%fused_computation.5 | output fusion | flops 6818814 | bytes 4990976 | tf_op jit(solution)/shard_map/div | solution.py:178
  53.9 1.1 %slice_bitcast_fusion.3 = (f32[1024,128]{1,0:T(8,128)S(1)}, f32[1024,128]{1,0:T(8,128)S(1)}, f32[1024,128]{1,0:T(8,128)}, f32[1024,128]{1,0:T(8,128)}) fusion(f32[1,4,1024,128]{3,2,1,0:T(8,128)S(1)} %divide_bitcast_fusion), kind=kLoop, calls=%fused_computation.29 | loop fusion | bytes 4194304 | tf_op jit(solution)/shard_map/mul | solution.py:183
  55.0 2.7 %all-gather.2.cloned.1.call-done = bf16[1024,512]{0,1:T(8,128)(2,1)} async-done(((bf16[128,512]{0,1:T(8,128)(2,1)}), bf16[1024,512]{0,1:T(8,128)(2,1)}) %all-gather.2.cloned.1.call-update) | async-done | bytes 1048592 | tf_op jit(solution)/shard_map/all_gather | solution.py:218
  57.7 2.4 %multiply_reduce_fusion = (f32[128,4]{0,1:T(4,128)S(1)}, f32[128,4,128]{0,2,1:T(8,128)S(1)}) fusion(bf16[1024,4,128]{0,2,1:T(8,128)(2,1)} %bitcast.97, f32[1024,128]{1,0:T(8,128)S(1)} %get-tuple-element.30, f32[4]{0:T(128)S(1)} %get-tuple-element.26, f32[1024,128]{1,0:T(8,128)} %get-tuple-element.31, f32[4]{0:T(128)S(1)} %copy-done.6, ...), kind=kOutput, calls=%fused_computation.53 | convolution fusion | flops 138542592 | bytes 3409984 | tf_op jit(solution)/shard_map/hki,khd->ihd/dot_general | solution.py:185
  60.2 0.1 multiply_convert_fusion
  60.3 0.2 constant_dynamic-slice_fusion.3
  60.6 0.1 copy.81
  60.6 1.5 %collective-permute-start.7 = (bf16[32,512]{1,0:T(8,128)(2,1)S(1)}, bf16[32,512]{1,0:T(8,128)(2,1)S(1)}, u32[]{:S(2)}, u32[]{:S(2)}) collective-permute-start(bf16[32,512]{1,0:T(8,128)(2,1)S(1)} %copy.81), channel_id=1, source_target_pairs={{0,1},{1,2},{2,3},{3,0},{4,5},{5,6},{6,7},{7,4},{8,9},{9,10},{10,1... | collective-permute-start | bytes 98312 | tf_op jit(solution)/shard_map/ppermute | solution.py:33
  62.3 2.5 %collective-permute-start.8 = (bf16[32,512]{1,0:T(8,128)(2,1)S(1)}, bf16[32,512]{1,0:T(8,128)(2,1)S(1)}, u32[]{:S(2)}, u32[]{:S(2)}) collective-permute-start(bf16[32,512]{1,0:T(8,128)(2,1)S(1)} %copy.82), channel_id=1, source_target_pairs={{0,2},{1,3},{2,0},{3,1},{4,6},{5,7},{6,4},{7,5},{8,10},{9,11},{10,... | collective-permute-start | bytes 98312 | tf_op jit(solution)/shard_map/ppermute | solution.py:33
  64.8 1.5 %collective-permute-start.9 = (bf16[32,512]{1,0:T(8,128)(2,1)S(1)}, bf16[32,512]{1,0:T(8,128)(2,1)S(1)}, u32[]{:S(2)}, u32[]{:S(2)}) collective-permute-start(bf16[32,512]{1,0:T(8,128)(2,1)S(1)} %copy.83), channel_id=1, source_target_pairs={{0,3},{1,0},{2,1},{3,2},{4,7},{5,4},{6,5},{7,6},{8,11},{9,8},{10,9... | collective-permute-start | bytes 98312 | tf_op jit(solution)/shard_map/ppermute | solution.py:33
  66.4 0.1 collective-permute-done.7
  66.5 1.3 %collective-permute-done.8 = bf16[32,512]{1,0:T(8,128)(2,1)S(1)} collective-permute-done((bf16[32,512]{1,0:T(8,128)(2,1)S(1)}, bf16[32,512]{1,0:T(8,128)(2,1)S(1)}, u32[]{:S(2)}, u32[]{:S(2)}) %collective-permute-start.8) | collective-permute-done | bytes 32800 | tf_op jit(solution)/shard_map/ppermute | solution.py:33
  67.8 1.0 %collective-permute-done.9 = bf16[32,512]{1,0:T(8,128)(2,1)S(1)} collective-permute-done((bf16[32,512]{1,0:T(8,128)(2,1)S(1)}, bf16[32,512]{1,0:T(8,128)(2,1)S(1)}, u32[]{:S(2)}, u32[]{:S(2)}) %collective-permute-start.9) | collective-permute-done | bytes 32800 | tf_op jit(solution)/shard_map/ppermute | solution.py:33
  68.8 0.6 gather_fusion.1
  69.4 0.1 select_bitcast_fusion.1
  69.5 0.7 copy.85
  (48 shorter events, 0.8 us)
Async XLA Ops:
  6.5 51.2 %all-gather.2.cloned.1.call-start = ((), (), s32[]{:S(2)}) async-start(), calls=%async_computation | async-start | bytes 1179648 | tf_op jit(solution)/shard_map/all_gather | solution.py:218
  7.7 14.7 %copy-start.3 = (f32[4,6,11]{2,0,1:T(4,128)S(1)}, f32[4,6,11]{2,0,1:T(4,128)}, u32[]{:S(2)}) copy-start(f32[4,6,11]{2,0,1:T(4,128)} %param.9) | copy-start | bytes 3172
  7.7 8.8 %collective-permute-start = (bf16[3,32,512]{2,1,0:T(8,128)(2,1)S(1)}, bf16[3,32,512]{2,1,0:T(8,128)(2,1)S(1)}, u32[]{:S(2)}, u32[]{:S(2)}) collective-permute-start(bf16[3,32,512]{2,1,0:T(8,128)(2,1)S(1)} %get-tuple-element.39), channel_id=1, source_target_pairs={{0,1},{1,2},{2,3},{3,0},{4,5},{5,6},{6,7},{7,4},{8,9},{9,10},{10,1... | collective-permute-start | bytes 294920 | tf_op jit(solution)/shard_map/ppermute | solution.py:33
  10.8 9.2 %collective-permute-start.1 = (bf16[3,32,512]{2,1,0:T(8,128)(2,1)S(1)}, bf16[3,32,512]{2,1,0:T(8,128)(2,1)S(1)}, u32[]{:S(2)}, u32[]{:S(2)}) collective-permute-start(bf16[3,32,512]{2,1,0:T(8,128)(2,1)S(1)} %get-tuple-element.38), channel_id=1, source_target_pairs={{0,2},{1,3},{2,0},{3,1},{4,6},{5,7},{6,4},{7,5},{8,10},{9,11},{10,... | collective-permute-start | bytes 294920 | tf_op jit(solution)/shard_map/ppermute | solution.py:33
  13.3 6.6 %collective-permute-start.2 = (bf16[3,32,512]{2,1,0:T(8,128)(2,1)S(1)}, bf16[3,32,512]{2,1,0:T(8,128)(2,1)S(1)}, u32[]{:S(2)}, u32[]{:S(2)}) collective-permute-start(bf16[3,32,512]{2,1,0:T(8,128)(2,1)S(1)} %get-tuple-element.37), channel_id=1, source_target_pairs={{0,3},{1,0},{2,1},{3,2},{4,7},{5,4},{6,5},{7,6},{8,11},{9,8},{10,9... | collective-permute-start | bytes 294920 | tf_op jit(solution)/shard_map/ppermute | solution.py:33
  14.7 13.0 %copy-start.4 = (f32[4,4]{1,0:T(4,128)S(1)}, f32[4,4]{1,0:T(4,128)}, u32[]{:S(2)}) copy-start(f32[4,4]{1,0:T(4,128)} %param.10) | copy-start | bytes 196
  20.7 5.3 %collective-permute-start.4 = (bf16[1,128,512]{2,1,0:T(8,128)(2,1)S(1)}, bf16[1,128,512]{2,1,0:T(8,128)(2,1)S(1)}, u32[]{:S(2)}, u32[]{:S(2)}) collective-permute-start(bf16[1,128,512]{2,1,0:T(8,128)(2,1)S(1)} %bitcast.77), channel_id=1, source_target_pairs={{0,16},{4,20},{8,24},{12,28},{16,0},{20,4},{24,8},{28,12},{1,17},{... | collective-permute-start | bytes 393224 | tf_op jit(solution)/shard_map/ppermute | solution.py:47
  26.1 7.3 %collective-permute-start.5 = (bf16[2,128,512]{2,1,0:T(8,128)(2,1)S(1)}, bf16[2,128,512]{2,1,0:T(8,128)(2,1)S(1)}, u32[]{:S(2)}, u32[]{:S(2)}) collective-permute-start(bf16[2,128,512]{2,1,0:T(8,128)(2,1)S(1)} %maximum_select_fusion.2), channel_id=1, source_target_pairs={{0,8},{4,12},{8,0},{12,4},{16,24},{20,28},{24,16},{28,20},{1,9},{5... | collective-permute-start | bytes 786440 | tf_op jit(solution)/shard_map/ppermute | solution.py:47
  29.2 2.9 %collective-permute-start.3 = (bf16[5,512]{1,0:T(8,128)(2,1)S(1)}, bf16[5,512]{1,0:T(8,128)(2,1)S(1)}, u32[]{:S(2)}, u32[]{:S(2)}) collective-permute-start(bf16[5,512]{1,0:T(8,128)(2,1)S(1)} %slice.270), channel_id=1, source_target_pairs={{0,4},{4,8},{8,12},{12,16},{16,20},{20,24},{24,28},{1,5},{5,9},{9,... | collective-permute-start | bytes 15368 | tf_op jit(solution)/shard_map/ppermute | solution.py:23
  33.5 2.4 %collective-permute-start.6 = (bf16[4,128,512]{2,1,0:T(8,128)(2,1)S(1)}, bf16[4,128,512]{2,1,0:T(8,128)(2,1)S(1)}, u32[]{:S(2)}, u32[]{:S(2)}) collective-permute-start(bf16[4,128,512]{2,1,0:T(8,128)(2,1)S(1)} %maximum_select_fusion.1), channel_id=1, source_target_pairs={{0,4},{4,0},{8,12},{12,8},{16,20},{20,16},{24,28},{28,24},{1,5},{5... | collective-permute-start | bytes 1572872 | tf_op jit(solution)/shard_map/ppermute | solution.py:47
  34.5 1.7 %copy-start.1 = (bf16[128,4,6,128]{0,3,2,1:T(8,128)(2,1)}, bf16[128,4,6,128]{0,3,2,1:T(8,128)(2,1)S(1)}, u32[]{:S(2)}) copy-start(bf16[128,4,6,128]{0,3,2,1:T(8,128)(2,1)S(1)} %constant_dynamic-update-slice_fusion) | copy-start | bytes 2359300
  36.2 1.0 %copy-start = (bf16[2,2,2,128,512]{4,3,2,1,0:T(8,128)(2,1)}, bf16[2,2,2,128,512]{4,3,2,1,0:T(8,128)(2,1)S(1)}, u32[]{:S(2)}) copy-start(bf16[2,2,2,128,512]{4,3,2,1,0:T(8,128)(2,1)S(1)} %copy.70) | copy-start | bytes 3145732
  36.3 1.3 %copy-start.2 = (bf16[128,4,128]{2,1,0:T(4,128)(2,1)S(1)}, bf16[128,4,128]{2,1,0:T(4,128)(2,1)}, u32[]{:S(2)}) copy-start(bf16[128,4,128]{2,1,0:T(4,128)(2,1)} %concatenate.39) | copy-start | bytes 393220
  53.8 3.9 %copy-start.6 = (f32[4]{0:T(128)S(1)}, f32[4]{0:T(128)}, u32[]{:S(2)}) copy-start(f32[4]{0:T(128)} %get-tuple-element.27) | copy-start | bytes 52
  53.8 3.9 %copy-start.7 = (f32[4]{0:T(128)S(1)}, f32[4]{0:T(128)}, u32[]{:S(2)}) copy-start(f32[4]{0:T(128)} %get-tuple-element.28) | copy-start | bytes 52
  57.7 2.5 %copy-start.5 = (f32[512]{0:T(512)S(1)}, f32[512]{0:T(512)}, u32[]{:S(2)}) copy-start(f32[512]{0:T(512)} %param.11) | copy-start | bytes 6148
  60.6 5.9 %collective-permute-start.7 = (bf16[32,512]{1,0:T(8,128)(2,1)S(1)}, bf16[32,512]{1,0:T(8,128)(2,1)S(1)}, u32[]{:S(2)}, u32[]{:S(2)}) collective-permute-start(bf16[32,512]{1,0:T(8,128)(2,1)S(1)} %copy.81), channel_id=1, source_target_pairs={{0,1},{1,2},{2,3},{3,0},{4,5},{5,6},{6,7},{7,4},{8,9},{9,10},{10,1... | collective-permute-start | bytes 98312 | tf_op jit(solution)/shard_map/ppermute | solution.py:33
  62.3 5.5 %collective-permute-start.8 = (bf16[32,512]{1,0:T(8,128)(2,1)S(1)}, bf16[32,512]{1,0:T(8,128)(2,1)S(1)}, u32[]{:S(2)}, u32[]{:S(2)}) collective-permute-start(bf16[32,512]{1,0:T(8,128)(2,1)S(1)} %copy.82), channel_id=1, source_target_pairs={{0,2},{1,3},{2,0},{3,1},{4,6},{5,7},{6,4},{7,5},{8,10},{9,11},{10,... | collective-permute-start | bytes 98312 | tf_op jit(solution)/shard_map/ppermute | solution.py:33
  64.8 4.0 %collective-permute-start.9 = (bf16[32,512]{1,0:T(8,128)(2,1)S(1)}, bf16[32,512]{1,0:T(8,128)(2,1)S(1)}, u32[]{:S(2)}, u32[]{:S(2)}) collective-permute-start(bf16[32,512]{1,0:T(8,128)(2,1)S(1)} %copy.83), channel_id=1, source_target_pairs={{0,3},{1,0},{2,1},{3,2},{4,7},{5,4},{6,5},{7,6},{8,11},{9,8},{10,9... | collective-permute-start | bytes 98312 | tf_op jit(solution)/shard_map/ppermute | solution.py:33
Sparse Core Ops, SparseCore 0:
  32.2 25.4 all-gather.1

commit v20 on v15

--- a/solution.py
+++ b/solution.py
@@ -1,3 +1,5 @@
+import functools
+
 import jax
 import jax.numpy as jnp
 from jax import lax
@@ -55,8 +57,8 @@
     return jnp.transpose(held, tuple(reversed(range(bits))) + tuple(range(bits, held.ndim)))
 
 
-def logits_kernel(taps_ref, query_ref, keys_ref, out_ref, high_ref, low_ref, conv_ref):
-    head = pl.program_id(0)
+def logits_kernel(first_head, taps_ref, query_ref, keys_ref, out_ref, high_ref, low_ref, conv_ref):
+    head = pl.program_id(0) + first_head
     group = pl.program_id(1)
     edge = 16
 
@@ -113,19 +115,19 @@
     )
 
 
-def conv_logits(shifted_t, score_kernel, key_pad):
+def conv_logits(shifted_t, score_kernel, key_pad, first_head):
     heads, contract, row_count = shifted_t.shape
     seq_len = key_pad.shape[0]
-    head_dim = key_pad.shape[1] // heads
+    head_dim = key_pad.shape[1] // score_kernel.shape[0]
     span = min(seq_len, KEY_SPAN)
     taps = (score_kernel * head_dim ** (-0.5)).reshape(-1)
     return pl.pallas_call(
-        logits_kernel,
+        functools.partial(logits_kernel, first_head),
         grid=(heads, seq_len // span),
         in_specs=[
             pl.BlockSpec(memory_space=pltpu.SMEM),
             pl.BlockSpec((1, contract, row_count), lambda h, g: (h, 0, 0)),
-            pl.BlockSpec((key_pad.shape[0], head_dim), lambda h, g: (0, h)),
+            pl.BlockSpec((key_pad.shape[0], head_dim), lambda h, g: (0, h + first_head)),
         ],
         out_specs=pl.BlockSpec((1, span, row_count), lambda h, g: (h, g, 0)),
         out_shape=jax.ShapeDtypeStruct((heads, seq_len, row_count), jnp.float32),
@@ -167,7 +169,14 @@
     row_count, heads = shifted.shape[:2]
     seq_len = value_heads.shape[0]
     shifted_t = jnp.transpose(shifted, (1, 2, 3, 0)).reshape((heads, -1, row_count))
-    convolved = conv_logits(shifted_t, score_kernel, key_pad)
+    half = heads // 2
+    convolved = jnp.concatenate(
+        [
+            conv_logits(shifted_t[:half], score_kernel, key_pad, 0),
+            conv_logits(shifted_t[half:], score_kernel, key_pad, half),
+        ],
+        axis=0,
+    )
     query_pos = query_first + lax.iota(jnp.int32, row_count)
     gap = query_pos[None, :] - lax.iota(jnp.int32, seq_len)[:, None]
     for lag in range(QCONV - 1):

time: 71.6 us -> 79.5 us (1.11)
  local copies, waits for them, and re-layouts: 11.6 us -> 14.3 us
  Pallas kernels: 10.9 us -> 13 us
  other arithmetic: 8.44 us -> 10.2 us
  starting transfers between devices: 20.9 us -> 21.8 us
    div x1, other arithmetic: 3.88 us -> 1.24 us  [attend_chunk(): probabilities = expd / jnp.sum(expd, axis=1, keepdims=True)]
    reduce_max x0 -> x1, other arithmetic: none -> 2.28 us  [attend_chunk(): peak = jnp.max(logits, axis=1, keepdims=True)]
    pallas_call x1 -> x2, Pallas kernels: 10.9 us -> 13 us  [conv_logits(): pl.pallas_call(functools.partial(logits_kernel, first_head), grid=(heads,...]
    ppermute x6, waiting for transfers between devices: 10.1 us -> 12.2 us  [gathered(): incoming = lax.ppermute(held, axis, [(i, i ^ bit) for i in range(peers)])]
    ppermute x6, waiting for transfers between devices: 6.73 us -> 4.96 us  [exchanged(): received.append(lax.ppermute(outgoing, axis, pairs))]
    slice x1, local copies, waits for them, and re-layouts: 0.4 us -> 1.9 us  [band_terms(): score_kernel[None, :, row_lag, col_lag]]
    reduce_sum x0 -> x1, other arithmetic: none -> 1.25 us  [attend_chunk(): probabilities = expd / jnp.sum(expd, axis=1, keepdims=True)]
    slice x0 -> x1, local copies, waits for them, and re-layouts: none -> 0.92 us  [attend_chunk(): shifted_t[:half]]
  transfers between devices with their start and end apart: 13 -> 13, of which waited for: 9 -> 8; matrix products, arithmetic and copies ran while one was open for 15% -> 17% of each run, Pallas kernels for 15% -> 0%
where the time goes in v20:
time: 79.5 us; the launch traced here: 79.1 us
  starting transfers between devices  21.8 us (27%)
  waiting for transfers between devices  17.1 us (22%)
  local copies, waits for them, and re-layouts  14.3 us (18%)
  Pallas kernels  13 us (16%)
  other arithmetic  10.2 us (13%)
  matrix products  2.12 us (3%)
    pallas_call x2, Pallas kernels, conv_logits(): pl.pallas_call(functools.partial(logits_kernel, first_head), grid=(heads,...  13 us
    ppermute x6, starting transfers between devices, exchanged(): received.append(lax.ppermute(outgoing, axis, pairs))  12.2 us
    ppermute x6, waiting for transfers between devices, gathered(): incoming = lax.ppermute(held, axis, [(i, i ^ bit) for i in range(peers)])  12.2 us
    ppermute x6, starting transfers between devices, gathered(): incoming = lax.ppermute(held, axis, [(i, i ^ bit) for i in range(peers)])  8.05 us
    ppermute x6, waiting for transfers between devices, exchanged(): received.append(lax.ppermute(outgoing, axis, pairs))  4.96 us
    reduce_max x1, other arithmetic, attend_chunk(): peak = jnp.max(logits, axis=1, keepdims=True)  2.28 us
    dot_general x1, matrix products, attend_chunk(): jnp.einsum('hki,khd->ihd', mixed_probs, value_heads, preferred_element_ty...  2.12 us
    slice x1, local copies, waits for them, and re-layouts, band_terms(): score_kernel[None, :, row_lag, col_lag]  1.9 us
  transfers between devices with their start and end apart: 13, of which 8 were waited for; matrix products, arithmetic and copies ran while one was open for 17% of the time, Pallas kernels for 0%

profile of v20, /device:TPU:0, one launch (start us, length us, event | category | flops | bytes accessed | tf_op | source)
XLA Modules:
  0.0 79.1 jit_solution(7821453253892365904)
XLA Ops:
  0.0 1.1 %pad_maximum_fusion = bf16[3,32,2048]{2,1,0:T(8,128)(2,1)S(1)} fusion(bf16[1,32,2048]{2,1,0:T(8,128)(2,1)} %bitcast.97, bf16[1,32,2048]{2,1,0:T(8,128)(2,1)} %bitcast.98, bf16[1,32,2048]{2,1,0:T(8,128)(2,1)} %bitcast.99), kind=kLoop, calls=%fused_computation.51 | loop fusion | flops 393216 | bytes 786432 | tf_op jit(solution)/shard_map/stack | solution.py:208
  1.1 3.1 %collective-permute-start = (bf16[3,32,512]{2,1,0:T(8,128)(2,1)S(1)}, bf16[3,32,512]{2,1,0:T(8,128)(2,1)S(1)}, u32[]{:S(2)}, u32[]{:S(2)}) collective-permute-start(bf16[3,32,512]{2,1,0:T(8,128)(2,1)S(1)} %get-tuple-element.45), channel_id=1, source_target_pairs={{0,1},{1,2},{2,3},{3,0},{4,5},{5,6},{6,7},{7,4},{8,9},{9,10},{10,1... | collective-permute-start | bytes 294920 | tf_op jit(solution)/shard_map/ppermute | solution.py:35
  4.2 2.6 %collective-permute-start.1 = (bf16[3,32,512]{2,1,0:T(8,128)(2,1)S(1)}, bf16[3,32,512]{2,1,0:T(8,128)(2,1)S(1)}, u32[]{:S(2)}, u32[]{:S(2)}) collective-permute-start(bf16[3,32,512]{2,1,0:T(8,128)(2,1)S(1)} %get-tuple-element.44), channel_id=1, source_target_pairs={{0,2},{1,3},{2,0},{3,1},{4,6},{5,7},{6,4},{7,5},{8,10},{9,11},{10,... | collective-permute-start | bytes 294920 | tf_op jit(solution)/shard_map/ppermute | solution.py:35
  6.8 1.3 %collective-permute-start.2 = (bf16[3,32,512]{2,1,0:T(8,128)(2,1)S(1)}, bf16[3,32,512]{2,1,0:T(8,128)(2,1)S(1)}, u32[]{:S(2)}, u32[]{:S(2)}) collective-permute-start(bf16[3,32,512]{2,1,0:T(8,128)(2,1)S(1)} %get-tuple-element.43), channel_id=1, source_target_pairs={{0,3},{1,0},{2,1},{3,2},{4,7},{5,4},{6,5},{7,6},{8,11},{9,8},{10,9... | collective-permute-start | bytes 294920 | tf_op jit(solution)/shard_map/ppermute | solution.py:35
  8.2 1.9 %slice_reduce_fusion.17 = (f32[4]{0:T(128)}, f32[4]{0:T(128)S(1)}, f32[4]{0:T(128)S(1)}, f32[4]{0:T(128)S(1)}, f32[4]{0:T(128)}, /*index=5*/f32[4]{0:T(128)S(1)}...) fusion(f32[4,6,11]{2,0,1:T(4,128)} %param.9), kind=kLoop, calls=%fused_computation.145 | loop fusion | bytes 480 | tf_op jit(solution)/shard_map/slice | solution.py:161
  10.1 0.7 broadcast_multiply_fusion
  10.8 0.5 fusion.26
  11.3 2.0 %collective-permute-done.1 = bf16[3,32,512]{2,1,0:T(8,128)(2,1)S(1)} collective-permute-done((bf16[3,32,512]{2,1,0:T(8,128)(2,1)S(1)}, bf16[3,32,512]{2,1,0:T(8,128)(2,1)S(1)}, u32[]{:S(2)}, u32[]{:S(2)}) %collective-permute-start.1) | collective-permute-done | bytes 98336 | tf_op jit(solution)/shard_map/ppermute | solution.py:35
  13.5 0.6 gather_fusion
  14.1 0.1 select_bitcast_fusion
  14.2 0.7 fusion.60
  14.9 1.5 %collective-permute-start.3 = (bf16[1,128,512]{2,1,0:T(8,128)(2,1)S(1)}, bf16[1,128,512]{2,1,0:T(8,128)(2,1)S(1)}, u32[]{:S(2)}, u32[]{:S(2)}) collective-permute-start(bf16[1,128,512]{2,1,0:T(8,128)(2,1)S(1)} %bitcast.90), channel_id=1, source_target_pairs={{0,16},{4,20},{8,24},{12,28},{16,0},{20,4},{24,8},{28,12},{1,17},{... | collective-permute-start | bytes 393224 | tf_op jit(solution)/shard_map/ppermute | solution.py:49
  16.4 0.8 %slice_reduce_fusion.18 = (f32[4]{0:T(128)}, f32[4]{0:T(128)}, f32[4]{0:T(128)}, f32[4]{0:T(128)}) fusion(f32[1,4,4]{2,1,0:T(4,128)S(1)} %bitcast.104), kind=kLoop, calls=%fused_computation.146 | loop fusion | bytes 128 | tf_op jit(solution)/shard_map/slice | solution.py:192
  17.2 0.7 reshape.263.taps_ref
  17.9 0.7 concatenate.82
  18.6 1.5 %collective-permute-start.9 = (bf16[5,512]{1,0:T(8,128)(2,1)S(1)}, bf16[5,512]{1,0:T(8,128)(2,1)S(1)}, u32[]{:S(2)}, u32[]{:S(2)}) collective-permute-start(bf16[5,512]{1,0:T(8,128)(2,1)S(1)} %slice.286), channel_id=1, source_target_pairs={{0,4},{4,8},{8,12},{12,16},{16,20},{20,24},{24,28},{1,5},{5,9},{9,... | collective-permute-start | bytes 15368 | tf_op jit(solution)/shard_map/ppermute | solution.py:25
  20.1 0.1 copy.80
  20.4 2.0 %collective-permute-start.4 = (bf16[2,128,512]{2,1,0:T(8,128)(2,1)S(1)}, bf16[2,128,512]{2,1,0:T(8,128)(2,1)S(1)}, u32[]{:S(2)}, u32[]{:S(2)}) collective-permute-start(bf16[2,128,512]{2,1,0:T(8,128)(2,1)S(1)} %maximum_select_fusion.4), channel_id=1, source_target_pairs={{0,8},{4,12},{8,0},{12,4},{16,24},{20,28},{24,16},{28,20},{1,9},{5... | collective-permute-start | bytes 786440 | tf_op jit(solution)/shard_map/ppermute | solution.py:49
  22.3 0.1 pad_maximum_fusion.3
  22.5 0.1 copy.75
  22.6 0.1 copy.76
  22.7 0.1 copy.77
  22.9 5.7 %collective-permute-done.4 = bf16[2,128,512]{2,1,0:T(8,128)(2,1)S(1)} collective-permute-done((bf16[2,128,512]{2,1,0:T(8,128)(2,1)S(1)}, bf16[2,128,512]{2,1,0:T(8,128)(2,1)S(1)}, u32[]{:S(2)}, u32[]{:S(2)}) %collective-permute-start.4) | collective-permute-done | bytes 262176 | tf_op jit(solution)/shard_map/ppermute | solution.py:49
  28.7 0.9 %collective-permute-start.5 = (bf16[4,128,512]{2,1,0:T(8,128)(2,1)S(1)}, bf16[4,128,512]{2,1,0:T(8,128)(2,1)S(1)}, u32[]{:S(2)}, u32[]{:S(2)}) collective-permute-start(bf16[4,128,512]{2,1,0:T(8,128)(2,1)S(1)} %maximum_select_fusion.2), channel_id=1, source_target_pairs={{0,4},{4,0},{8,12},{12,8},{16,20},{20,16},{24,28},{28,24},{1,5},{5... | collective-permute-start | bytes 1572872 | tf_op jit(solution)/shard_map/ppermute | solution.py:49
  29.6 0.1 copy.78
  29.7 0.1 copy.79
  29.9 0.9 %fusion.59 = (bf16[2,6,128,128]{3,2,1,0:T(8,128)(2,1)}, bf16[2,6,128,128]{3,2,1,0:T(8,128)(2,1)}) fusion(bf16[4,6,128,128]{3,2,1,0:T(8,128)(2,1)S(1)} %bitcast.87), kind=kLoop, calls=%fused_computation.156 | loop fusion | bytes 1572864 | tf_op jit(solution)/shard_map/slice | solution.py:175
  30.8 0.3 collective-permute-done.5
  31.1 0.2 maximum_select_fusion
  31.3 0.1 copy.72
  31.4 0.1 fusion.34
  31.5 0.1 fusion.61
  31.6 0.9 %slice.237 = f32[133,4,128]{2,1,0:T(4,128)} reshape(f32[133,512]{1,0:T(8,128)S(1)} %get-tuple-element.46) | data formatting | bytes 544768 | tf_op jit(solution)/shard_map/slice | solution.py:152
  32.5 0.1 slice.241
  32.6 0.1 slice.247
  32.7 0.1 slice.255
  32.8 0.1 slice.265
  32.9 0.5 copy-done.3
  33.4 1.7 %fusion.31 = (f32[133,4]{1,0:T(8,128)S(1)}, f32[133,4]{1,0:T(8,128)S(1)}, f32[133,4]{1,0:T(8,128)S(1)}, f32[133,4]{1,0:T(8,128)S(1)}, f32[133,4]{1,0:T(8,128)S(1)}) fusion(f32[133,4,128]{2,1,0:T(4,128)S(1)} %slice.265, bf16[128,4,128]{2,1,0:T(4,128)(2,1)} %concatenate.82, bf16[5,4,128]{2,1,0:T(4,128)(2,1)S(1)} %concatenate.81, ...), kind=kLoop, calls=%fused_computation.62 | loop fusion | flops 814492 | bytes 1508752 | tf_op jit(solution)/shard_map/reduce_sum | solution.py:152
  35.6 6.5 %shard_map.64 = f32[2,1024,128]{2,1,0:T(8,128)} custom-call(f32[264]{0:T(512)} %reshape.263.taps_ref, bf16[2,768,128]{2,1,0:T(8,128)(2,1)} %bitcast.86, bf16[1024,512]{1,0:T(8,128)(2,1)} %bitcast.78), custom_call_target="tpu_custom_call" | custom-call | tf_op jit(solution)/shard_map/pallas_call | solution.py:124
  42.2 6.4 %shard_map.65 = f32[2,1024,128]{2,1,0:T(8,128)} custom-call(f32[264]{0:T(512)} %reshape.263.taps_ref, bf16[2,768,128]{2,1,0:T(8,128)(2,1)} %bitcast.85, bf16[1024,512]{1,0:T(8,128)(2,1)} %bitcast.79), custom_call_target="tpu_custom_call" | custom-call | tf_op jit(solution)/shard_map/pallas_call | solution.py:124
  48.6 1.7 %collective-permute-start.6 = (bf16[1,128,512]{2,1,0:T(8,128)(2,1)S(1)}, bf16[1,128,512]{2,1,0:T(8,128)(2,1)S(1)}, u32[]{:S(2)}, u32[]{:S(2)}) collective-permute-start(bf16[1,128,512]{2,1,0:T(8,128)(2,1)S(1)} %bitcast.88), channel_id=1, source_target_pairs={{0,16},{4,20},{8,24},{12,28},{16,0},{20,4},{24,8},{28,12},{1,17},{... | collective-permute-start | bytes 393224 | tf_op jit(solution)/shard_map/ppermute | solution.py:49
  50.6 0.1 fusion.54
  50.7 2.3 %fusion.58 = f32[4,128]{1,0:T(4,128)S(1)} fusion(f32[4,128]{1,0:T(4,128)S(1)} %get-tuple-element.62, pred[1024,128]{1,0:T(8,128)(4,1)S(1)} %get-tuple-element.64, f32[4,128]{1,0:T(4,128)S(1)} %get-tuple-element.61, pred[1024,128]{1,0:T(8,128)(4,1)S(1)} %get-tuple-element.65, f32[4,128]{1,0:T(4,128)S(1)} %get-tuple-element.60, ...), kind=kLoop, calls=%fused_computation.155 | loop fusion | flops 6815232 | bytes 2895872 | tf_op jit(solution)/shard_map/reduce_max | solution.py:185
  53.0 1.5 %collective-permute-done.6 = bf16[1,128,512]{2,1,0:T(8,128)(2,1)S(1)} collective-permute-done((bf16[1,128,512]{2,1,0:T(8,128)(2,1)S(1)}, bf16[1,128,512]{2,1,0:T(8,128)(2,1)S(1)}, u32[]{:S(2)}, u32[]{:S(2)}) %collective-permute-start.6) | collective-permute-done | bytes 131104 | tf_op jit(solution)/shard_map/ppermute | solution.py:49
  54.5 1.9 %collective-permute-start.7 = (bf16[2,128,512]{2,1,0:T(8,128)(2,1)S(1)}, bf16[2,128,512]{2,1,0:T(8,128)(2,1)S(1)}, u32[]{:S(2)}, u32[]{:S(2)}) collective-permute-start(bf16[2,128,512]{2,1,0:T(8,128)(2,1)S(1)} %maximum_select_fusion.5), channel_id=1, source_target_pairs={{0,8},{4,12},{8,0},{12,4},{16,24},{20,28},{24,16},{28,20},{1,9},{5... | collective-permute-start | bytes 786440 | tf_op jit(solution)/shard_map/ppermute | solution.py:49
  56.4 1.2 %exponential_reduce_fusion = f32[4,128]{1,0:T(4,128)S(1)} fusion(f32[4,128]{1,0:T(4,128)S(1)} %fusion.58, f32[4,128]{1,0:T(4,128)S(1)} %get-tuple-element.62, pred[1024,128]{1,0:T(8,128)(4,1)S(1)} %get-tuple-element.64, f32[4,128]{1,0:T(4,128)S(1)} %get-tuple-element.61, pred[1024,128]{1,0:T(8,128)(4,1)S(1)} %get-tuple-element.65, ...), kind=kLoop, calls=%fused_computation.18 | loop fusion | flops 7339520 | bytes 2897920 | tf_op jit(solution)/shard_map/reduce_sum | solution.py:187
  57.6 4.7 %collective-permute-done.7 = bf16[2,128,512]{2,1,0:T(8,128)(2,1)S(1)} collective-permute-done((bf16[2,128,512]{2,1,0:T(8,128)(2,1)S(1)}, bf16[2,128,512]{2,1,0:T(8,128)(2,1)S(1)}, u32[]{:S(2)}, u32[]{:S(2)}) %collective-permute-start.7) | collective-permute-done | bytes 262176 | tf_op jit(solution)/shard_map/ppermute | solution.py:49
  62.5 1.2 %fusion.7 = f32[1,4,1024,128]{3,2,1,0:T(8,128)S(1)} fusion(f32[1,2,1024,128]{3,2,1,0:T(8,128)S(1)} %bitcast.76, f32[1,2,1024,128]{3,2,1,0:T(8,128)S(1)} %bitcast.75, f32[4,128]{1,0:T(4,128)S(1)} %exponential_reduce_fusion, f32[4,128]{1,0:T(4,128)S(1)} %fusion.58, f32[4,128]{1,0:T(4,128)S(1)} %get-tuple-element.62, f32[4,128]{1,0:T(4,128)S(1)} %get-tuple-element.61, ...), kind=kLoop, calls=%fused_computation.10 | loop fusion | flops 7340032 | bytes 4995072 | tf_op jit(solution)/shard_map/div | solution.py:187
  63.7 1.1 %slice_bitcast_fusion.3 = (f32[1024,128]{1,0:T(8,128)S(1)}, f32[1024,128]{1,0:T(8,128)S(1)}, f32[1024,128]{1,0:T(8,128)}, f32[1024,128]{1,0:T(8,128)}) fusion(f32[1,4,1024,128]{3,2,1,0:T(8,128)S(1)} %fusion.7), kind=kLoop, calls=%fused_computation.41 | loop fusion | bytes 4194304 | tf_op jit(solution)/shard_map/mul | solution.py:192
  64.8 0.2 maximum_select_fusion.1
  65.1 0.9 %copy.73 = bf16[2,2,2,128,512]{3,2,1,0,4:T(2,128)(2,1)S(1)} copy(bf16[2,2,2,128,512]{4,3,0,1,2:T(8,128)(2,1)S(1)} %bitcast.80) | data formatting | bytes 2097152 | tf_op jit(solution)/shard_map/transpose | solution.py:57
  66.0 0.8 reshape_reshape.3
  66.8 2.1 %multiply_reduce_fusion = (f32[128,4]{0,1:T(4,128)S(1)}, f32[128,4,128]{0,2,1:T(8,128)S(1)}) fusion(bf16[1024,4,128]{0,2,1:T(8,128)(2,1)S(1)} %reshape_reshape.3, f32[1024,128]{1,0:T(8,128)S(1)} %get-tuple-element.34, f32[4]{0:T(128)S(1)} %copy-done.15, f32[1024,128]{1,0:T(8,128)} %get-tuple-element.35, f32[4]{0:T(128)S(1)} %copy-done.16, ...), kind=kOutput, calls=%fused_computation.66 | convolution fusion | flops 138542592 | bytes 3409984 | tf_op jit(solution)/shard_map/hki,khd->ihd/dot_general | solution.py:194
  69.0 0.1 multiply_convert_fusion
  69.1 0.2 constant_dynamic-slice_fusion.3
  69.4 2.7 %collective-permute-start.10 = (bf16[32,512]{1,0:T(8,128)(2,1)S(1)}, bf16[32,512]{1,0:T(8,128)(2,1)S(1)}, u32[]{:S(2)}, u32[]{:S(2)}) collective-permute-start(bf16[32,512]{1,0:T(8,128)(2,1)S(1)} %copy.91), channel_id=1, source_target_pairs={{0,1},{1,2},{2,3},{3,0},{4,5},{5,6},{6,7},{7,4},{8,9},{9,10},{10,1... | collective-permute-start | bytes 98312 | tf_op jit(solution)/shard_map/ppermute | solution.py:35
  72.2 1.4 %collective-permute-start.11 = (bf16[32,512]{1,0:T(8,128)(2,1)S(1)}, bf16[32,512]{1,0:T(8,128)(2,1)S(1)}, u32[]{:S(2)}, u32[]{:S(2)}) collective-permute-start(bf16[32,512]{1,0:T(8,128)(2,1)S(1)} %copy.92), channel_id=1, source_target_pairs={{0,2},{1,3},{2,0},{3,1},{4,6},{5,7},{6,4},{7,5},{8,10},{9,11},{10,... | collective-permute-start | bytes 98312 | tf_op jit(solution)/shard_map/ppermute | solution.py:35
  73.8 1.1 %collective-permute-start.12 = (bf16[32,512]{1,0:T(8,128)(2,1)S(1)}, bf16[32,512]{1,0:T(8,128)(2,1)S(1)}, u32[]{:S(2)}, u32[]{:S(2)}) collective-permute-start(bf16[32,512]{1,0:T(8,128)(2,1)S(1)} %copy.93), channel_id=1, source_target_pairs={{0,3},{1,0},{2,1},{3,2},{4,7},{5,4},{6,5},{7,6},{8,11},{9,8},{10,9... | collective-permute-start | bytes 98312 | tf_op jit(solution)/shard_map/ppermute | solution.py:35
  74.9 0.3 collective-permute-done.10
  75.2 2.3 %collective-permute-done.11 = bf16[32,512]{1,0:T(8,128)(2,1)S(1)} collective-permute-done((bf16[32,512]{1,0:T(8,128)(2,1)S(1)}, bf16[32,512]{1,0:T(8,128)(2,1)S(1)}, u32[]{:S(2)}, u32[]{:S(2)}) %collective-permute-start.11) | collective-permute-done | bytes 32800 | tf_op jit(solution)/shard_map/ppermute | solution.py:35
  77.5 0.3 collective-permute-done.12
  77.8 0.6 gather_fusion.1
  78.5 0.7 copy.95
  (79 shorter events, 1.7 us)
Async XLA Ops:
  1.1 15.3 %copy-start.5 = (f32[4,4]{1,0:T(4,128)S(1)}, f32[4,4]{1,0:T(4,128)}, u32[]{:S(2)}) copy-start(f32[4,4]{1,0:T(4,128)} %param.10) | copy-start | bytes 196
  1.1 10.2 %collective-permute-start = (bf16[3,32,512]{2,1,0:T(8,128)(2,1)S(1)}, bf16[3,32,512]{2,1,0:T(8,128)(2,1)S(1)}, u32[]{:S(2)}, u32[]{:S(2)}) collective-permute-start(bf16[3,32,512]{2,1,0:T(8,128)(2,1)S(1)} %get-tuple-element.45), channel_id=1, source_target_pairs={{0,1},{1,2},{2,3},{3,0},{4,5},{5,6},{6,7},{7,4},{8,9},{9,10},{10,1... | collective-permute-start | bytes 294920 | tf_op jit(solution)/shard_map/ppermute | solution.py:35
  4.2 9.2 %collective-permute-start.1 = (bf16[3,32,512]{2,1,0:T(8,128)(2,1)S(1)}, bf16[3,32,512]{2,1,0:T(8,128)(2,1)S(1)}, u32[]{:S(2)}, u32[]{:S(2)}) collective-permute-start(bf16[3,32,512]{2,1,0:T(8,128)(2,1)S(1)} %get-tuple-element.44), channel_id=1, source_target_pairs={{0,2},{1,3},{2,0},{3,1},{4,6},{5,7},{6,4},{7,5},{8,10},{9,11},{10,... | collective-permute-start | bytes 294920 | tf_op jit(solution)/shard_map/ppermute | solution.py:35
  6.8 6.6 %collective-permute-start.2 = (bf16[3,32,512]{2,1,0:T(8,128)(2,1)S(1)}, bf16[3,32,512]{2,1,0:T(8,128)(2,1)S(1)}, u32[]{:S(2)}, u32[]{:S(2)}) collective-permute-start(bf16[3,32,512]{2,1,0:T(8,128)(2,1)S(1)} %get-tuple-element.43), channel_id=1, source_target_pairs={{0,3},{1,0},{2,1},{3,2},{4,7},{5,4},{6,5},{7,6},{8,11},{9,8},{10,9... | collective-permute-start | bytes 294920 | tf_op jit(solution)/shard_map/ppermute | solution.py:35
  11.3 8.8 %copy-start.12 = (pred[4]{0:T(512)(128)(4,1)}, pred[4]{0:T(512)(128)(4,1)S(1)}, u32[]{:S(2)}) copy-start(pred[4]{0:T(512)(128)(4,1)S(1)} %compare_and_fusion) | copy-start | bytes 16
  14.9 5.4 %collective-permute-start.3 = (bf16[1,128,512]{2,1,0:T(8,128)(2,1)S(1)}, bf16[1,128,512]{2,1,0:T(8,128)(2,1)S(1)}, u32[]{:S(2)}, u32[]{:S(2)}) collective-permute-start(bf16[1,128,512]{2,1,0:T(8,128)(2,1)S(1)} %bitcast.90), channel_id=1, source_target_pairs={{0,16},{4,20},{8,24},{12,28},{16,0},{20,4},{24,8},{28,12},{1,17},{... | collective-permute-start | bytes 393224 | tf_op jit(solution)/shard_map/ppermute | solution.py:49
  18.6 3.7 %collective-permute-start.9 = (bf16[5,512]{1,0:T(8,128)(2,1)S(1)}, bf16[5,512]{1,0:T(8,128)(2,1)S(1)}, u32[]{:S(2)}, u32[]{:S(2)}) collective-permute-start(bf16[5,512]{1,0:T(8,128)(2,1)S(1)} %slice.286), channel_id=1, source_target_pairs={{0,4},{4,8},{8,12},{12,16},{16,20},{20,24},{24,28},{1,5},{5,9},{9,... | collective-permute-start | bytes 15368 | tf_op jit(solution)/shard_map/ppermute | solution.py:25
  20.4 8.3 %collective-permute-start.4 = (bf16[2,128,512]{2,1,0:T(8,128)(2,1)S(1)}, bf16[2,128,512]{2,1,0:T(8,128)(2,1)S(1)}, u32[]{:S(2)}, u32[]{:S(2)}) collective-permute-start(bf16[2,128,512]{2,1,0:T(8,128)(2,1)S(1)} %maximum_select_fusion.4), channel_id=1, source_target_pairs={{0,8},{4,12},{8,0},{12,4},{16,24},{20,28},{24,16},{28,20},{1,9},{5... | collective-permute-start | bytes 786440 | tf_op jit(solution)/shard_map/ppermute | solution.py:49
  28.7 2.4 %collective-permute-start.5 = (bf16[4,128,512]{2,1,0:T(8,128)(2,1)S(1)}, bf16[4,128,512]{2,1,0:T(8,128)(2,1)S(1)}, u32[]{:S(2)}, u32[]{:S(2)}) collective-permute-start(bf16[4,128,512]{2,1,0:T(8,128)(2,1)S(1)} %maximum_select_fusion.2), channel_id=1, source_target_pairs={{0,4},{4,0},{8,12},{12,8},{16,20},{20,16},{24,28},{28,24},{1,5},{5... | collective-permute-start | bytes 1572872 | tf_op jit(solution)/shard_map/ppermute | solution.py:49
  31.4 1.1 %copy-start.2 = (bf16[2,2,2,128,512]{4,3,2,1,0:T(8,128)(2,1)}, bf16[2,2,2,128,512]{4,3,2,1,0:T(8,128)(2,1)S(1)}, u32[]{:S(2)}) copy-start(bf16[2,2,2,128,512]{4,3,2,1,0:T(8,128)(2,1)S(1)} %copy.72) | copy-start | bytes 3145732
  32.5 1.0 %copy-start.3 = (f32[133,4,128]{2,1,0:T(4,128)S(1)}, f32[133,4,128]{2,1,0:T(4,128)}, u32[]{:S(2)}) copy-start(f32[133,4,128]{2,1,0:T(4,128)} %slice.237) | copy-start | bytes 817156
  35.6 13.0 %copy-start.4 = (bf16[1,4,32,512]{3,2,0,1:T(8,128)(2,1)S(1)}, bf16[1,4,32,512]{3,2,0,1:T(8,128)(2,1)}, u32[]{:S(2)}) copy-start(bf16[1,4,32,512]{3,2,0,1:T(8,128)(2,1)} %get-tuple-element.40) | copy-start | bytes 393220
  35.6 14.9 %copy-start.7 = (f32[4]{0:T(128)S(1)}, f32[4]{0:T(128)}, u32[]{:S(2)}) copy-start(f32[4]{0:T(128)} %get-tuple-element.14) | copy-start | bytes 52
  35.6 15.0 %copy-start.8 = (f32[4]{0:T(128)S(1)}, f32[4]{0:T(128)}, u32[]{:S(2)}) copy-start(f32[4]{0:T(128)} %get-tuple-element.18) | copy-start | bytes 52
  35.6 15.0 %copy-start.9 = (f32[4]{0:T(128)S(1)}, f32[4]{0:T(128)}, u32[]{:S(2)}) copy-start(f32[4]{0:T(128)} %get-tuple-element.22) | copy-start | bytes 52
  35.6 15.0 %copy-start.10 = (f32[4]{0:T(128)S(1)}, f32[4]{0:T(128)}, u32[]{:S(2)}) copy-start(f32[4]{0:T(128)} %get-tuple-element.25) | copy-start | bytes 52
  35.6 15.0 %copy-start.11 = (f32[4]{0:T(128)S(1)}, f32[4]{0:T(128)}, u32[]{:S(2)}) copy-start(f32[4]{0:T(128)} %get-tuple-element.27) | copy-start | bytes 52
  42.2 8.5 %copy-start = (f32[2,1024,128]{2,1,0:T(8,128)S(1)}, f32[2,1024,128]{2,1,0:T(8,128)}, u32[]{:S(2)}) copy-start(f32[2,1024,128]{2,1,0:T(8,128)} %shard_map.64) | copy-start | bytes 3145732
  48.6 7.8 %copy-start.1 = (f32[2,1024,128]{2,1,0:T(8,128)S(1)}, f32[2,1024,128]{2,1,0:T(8,128)}, u32[]{:S(2)}) copy-start(f32[2,1024,128]{2,1,0:T(8,128)} %shard_map.65) | copy-start | bytes 3145732
  48.6 5.8 %collective-permute-start.6 = (bf16[1,128,512]{2,1,0:T(8,128)(2,1)S(1)}, bf16[1,128,512]{2,1,0:T(8,128)(2,1)S(1)}, u32[]{:S(2)}, u32[]{:S(2)}) collective-permute-start(bf16[1,128,512]{2,1,0:T(8,128)(2,1)S(1)} %bitcast.88), channel_id=1, source_target_pairs={{0,16},{4,20},{8,24},{12,28},{16,0},{20,4},{24,8},{28,12},{1,17},{... | collective-permute-start | bytes 393224 | tf_op jit(solution)/shard_map/ppermute | solution.py:49
  54.5 7.8 %collective-permute-start.7 = (bf16[2,128,512]{2,1,0:T(8,128)(2,1)S(1)}, bf16[2,128,512]{2,1,0:T(8,128)(2,1)S(1)}, u32[]{:S(2)}, u32[]{:S(2)}) collective-permute-start(bf16[2,128,512]{2,1,0:T(8,128)(2,1)S(1)} %maximum_select_fusion.5), channel_id=1, source_target_pairs={{0,8},{4,12},{8,0},{12,4},{16,24},{20,28},{24,16},{28,20},{1,9},{5... | collective-permute-start | bytes 786440 | tf_op jit(solution)/shard_map/ppermute | solution.py:49
  62.4 2.4 %collective-permute-start.8 = (bf16[4,128,512]{2,1,0:T(8,128)(2,1)S(1)}, bf16[4,128,512]{2,1,0:T(8,128)(2,1)S(1)}, u32[]{:S(2)}, u32[]{:S(2)}) collective-permute-start(bf16[4,128,512]{2,1,0:T(8,128)(2,1)S(1)} %maximum_select_fusion.3), channel_id=1, source_target_pairs={{0,4},{4,0},{8,12},{12,8},{16,20},{20,16},{24,28},{28,24},{1,5},{5... | collective-permute-start | bytes 1572872 | tf_op jit(solution)/shard_map/ppermute | solution.py:49
  65.0 1.8 %copy-start.14 = (f32[4]{0:T(128)S(1)}, f32[4]{0:T(128)}, u32[]{:S(2)}) copy-start(f32[4]{0:T(128)} %get-tuple-element.29) | copy-start | bytes 52
  65.0 1.8 %copy-start.15 = (f32[4]{0:T(128)S(1)}, f32[4]{0:T(128)}, u32[]{:S(2)}) copy-start(f32[4]{0:T(128)} %get-tuple-element.30) | copy-start | bytes 52
  65.0 1.8 %copy-start.16 = (f32[4]{0:T(128)S(1)}, f32[4]{0:T(128)}, u32[]{:S(2)}) copy-start(f32[4]{0:T(128)} %get-tuple-element.31) | copy-start | bytes 52
  65.0 1.8 %copy-start.17 = (f32[4]{0:T(128)S(1)}, f32[4]{0:T(128)}, u32[]{:S(2)}) copy-start(f32[4]{0:T(128)} %get-tuple-element.32) | copy-start | bytes 52
  66.8 2.2 %copy-start.6 = (f32[512]{0:T(512)S(1)}, f32[512]{0:T(512)}, u32[]{:S(2)}) copy-start(f32[512]{0:T(512)} %param.11) | copy-start | bytes 6148
  68.9 9.4 %copy-start.13 = (pred[4]{0:T(512)(128)(4,1)S(1)}, pred[4]{0:T(512)(128)(4,1)}, u32[]{:S(2)}) copy-start(pred[4]{0:T(512)(128)(4,1)} %copy-done.12) | copy-start | bytes 16
  69.4 5.8 %collective-permute-start.10 = (bf16[32,512]{1,0:T(8,128)(2,1)S(1)}, bf16[32,512]{1,0:T(8,128)(2,1)S(1)}, u32[]{:S(2)}, u32[]{:S(2)}) collective-permute-start(bf16[32,512]{1,0:T(8,128)(2,1)S(1)} %copy.91), channel_id=1, source_target_pairs={{0,1},{1,2},{2,3},{3,0},{4,5},{5,6},{6,7},{7,4},{8,9},{9,10},{10,1... | collective-permute-start | bytes 98312 | tf_op jit(solution)/shard_map/ppermute | solution.py:35
  72.2 5.2 %collective-permute-start.11 = (bf16[32,512]{1,0:T(8,128)(2,1)S(1)}, bf16[32,512]{1,0:T(8,128)(2,1)S(1)}, u32[]{:S(2)}, u32[]{:S(2)}) collective-permute-start(bf16[32,512]{1,0:T(8,128)(2,1)S(1)} %copy.92), channel_id=1, source_target_pairs={{0,2},{1,3},{2,0},{3,1},{4,6},{5,7},{6,4},{7,5},{8,10},{9,11},{10,... | collective-permute-start | bytes 98312 | tf_op jit(solution)/shard_map/ppermute | solution.py:35
  73.8 4.0 %collective-permute-start.12 = (bf16[32,512]{1,0:T(8,128)(2,1)S(1)}, bf16[32,512]{1,0:T(8,128)(2,1)S(1)}, u32[]{:S(2)}, u32[]{:S(2)}) collective-permute-start(bf16[32,512]{1,0:T(8,128)(2,1)S(1)} %copy.93), channel_id=1, source_target_pairs={{0,3},{1,0},{2,1},{3,2},{4,7},{5,4},{6,5},{7,6},{8,11},{9,8},{10,9... | collective-permute-start | bytes 98312 | tf_op jit(solution)/shard_map/ppermute | solution.py:35

commit v21 on v19

--- a/solution.py
+++ b/solution.py
@@ -53,6 +53,38 @@
         )
     held = held.reshape((2,) * bits + shard.shape)
     return jnp.transpose(held, tuple(reversed(range(bits))) + tuple(range(bits, held.ndim)))
+
+
+def doubling_step(held, axis, bit):
+    peers = lax.axis_size(axis)
+    place = lax.axis_index(axis)
+    incoming = lax.ppermute(held, axis, [(i, i ^ bit) for i in range(peers)])
+    return jnp.where(
+        (place & bit) != 0,
+        jnp.concatenate([incoming, held], axis=0),
+        jnp.concatenate([held, incoming], axis=0),
+    )
+
+
+def doubling_done(held, peers, shard_shape):
+    bits = peers.bit_length() - 1
+    held = held.reshape((2,) * bits + shard_shape)
+    return jnp.transpose(held, tuple(reversed(range(bits))) + tuple(range(bits, held.ndim)))
+
+
+def gathered_pair(first, second, axis):
+    peers = lax.axis_size(axis)
+    if peers & (peers - 1) or peers < 4:
+        return gathered(first, axis), gathered(second, axis)
+    levels = list(reversed(range(peers.bit_length() - 1)))
+    held = first[None]
+    for level in levels[:-1]:
+        held = doubling_step(held, axis, 1 << level)
+    held, later = lax.optimization_barrier((held, second[None]))
+    held = doubling_step(held, axis, 1 << levels[-1])
+    for level in levels:
+        later = doubling_step(later, axis, 1 << level)
+    return doubling_done(held, peers, first.shape), doubling_done(later, peers, second.shape)
 
 
 def logits_kernel(taps_ref, query_ref, keys_ref, out_ref, high_ref, low_ref, conv_ref):
@@ -215,8 +247,9 @@
     query_first = ctx_place * shard_rows
     earlier = passed_along(query_local[shard_rows - row_lead :], "ctx", 1)
     query_ext = jnp.concatenate([earlier, query_local], axis=0)
-    value_all = lax.all_gather(value_local, "ctx", axis=0, tiled=True)
-    key_all = gathered(key_local, "ctx").reshape((-1, width))
+    key_all, value_all = gathered_pair(key_local, value_local, "ctx")
+    key_all = key_all.reshape((-1, width))
+    value_all = value_all.reshape((-1, width))
     seq_len = key_all.shape[0]
     key_pad = key_all
     edge = jnp.zeros((8, width), key_all.dtype)

time: 77.2 us -> 75.5 us (0.978)
  between operations: 13.8 us -> 0.63 us
  waiting for transfers between devices: 14.4 us -> 20.1 us
  starting transfers between devices: 17.8 us -> 21.3 us
  other arithmetic: 8.11 us -> 9.58 us
  local copies, waits for them, and re-layouts: 9.51 us -> 10.6 us
    ppermute x3 -> x6, waiting for transfers between devices: 5.25 us -> 12.6 us  [doubling_step(): incoming = lax.ppermute(held, axis, [(i, i ^ bit) for i in range(peers)])]
    ppermute x3 -> x6, starting transfers between devices: 4 us -> 7.74 us  [doubling_step(): incoming = lax.ppermute(held, axis, [(i, i ^ bit) for i in range(peers)])]
    all_gather x1 -> x0, waiting for transfers between devices: 2.73 us -> none  [shards(): value_all = lax.all_gather(value_local, 'ctx', axis=0, tiled=True)]
    select_n x3 -> x6, other arithmetic: 0.27 us -> 1.79 us  [doubling_step(): jnp.where(place & bit != 0, jnp.concatenate([incoming, held], axis=0), jn...]
    transpose x1 -> x2, local copies, waits for them, and re-layouts: 0.1 us -> 1.01 us  [doubling_done(): jnp.transpose(held, tuple(reversed(range(bits))) + tuple(range(bits, held...]
  transfers between devices with their start and end apart: 11 -> 13, of which waited for: 9 -> 10; matrix products, arithmetic and copies ran while one was open for 17% -> 17% of each run, Pallas kernels for 14% -> 14%
where the time goes in v21:
time: 75.5 us; the launch traced here: 75.2 us
  starting transfers between devices  21.3 us (28%)
  waiting for transfers between devices  20.1 us (27%)
  Pallas kernels  10.9 us (14%)
  local copies, waits for them, and re-layouts  10.6 us (14%)
  other arithmetic  9.58 us (13%)
  matrix products  2.13 us (3%)
    ppermute x6, waiting for transfers between devices, doubling_step(): incoming = lax.ppermute(held, axis, [(i, i ^ bit) for i in range(peers)])  12.6 us
    ppermute x6, starting transfers between devices, exchanged(): received.append(lax.ppermute(outgoing, axis, pairs))  12.2 us
    pallas_call x1, Pallas kernels, conv_logits(): pl.pallas_call(logits_kernel, grid=(heads, seq_len // span), in_specs=[pl...  10.9 us
    ppermute x6, starting transfers between devices, doubling_step(): incoming = lax.ppermute(held, axis, [(i, i ^ bit) for i in range(peers)])  7.74 us
    ppermute x6, waiting for transfers between devices, exchanged(): received.append(lax.ppermute(outgoing, axis, pairs))  6.87 us
    div x1, other arithmetic, attend_chunk(): probabilities = expd / jnp.sum(expd, axis=1, keepdims=True)  3.81 us
    dot_general x1, matrix products, attend_chunk(): jnp.einsum('hki,khd->ihd', mixed_probs, value_heads, preferred_element_ty...  2.13 us
    select_n x6, other arithmetic, doubling_step(): jnp.where(place & bit != 0, jnp.concatenate([incoming, held], axis=0), jn...  1.79 us
  transfers between devices with their start and end apart: 13, of which 10 were waited for; matrix products, arithmetic and copies ran while one was open for 17% of the time, Pallas kernels for 14%

profile of v21, /device:TPU:0, one launch (start us, length us, event | category | flops | bytes accessed | tf_op | source)
XLA Modules:
  0.0 75.2 jit_solution(15654380380160907825)
XLA Ops:
  0.0 1.1 %pad_maximum_fusion = bf16[3,32,2048]{2,1,0:T(8,128)(2,1)S(1)} fusion(bf16[1,32,2048]{2,1,0:T(8,128)(2,1)} %bitcast.91, bf16[1,32,2048]{2,1,0:T(8,128)(2,1)} %bitcast.92, bf16[1,32,2048]{2,1,0:T(8,128)(2,1)} %bitcast.93), kind=kLoop, calls=%fused_computation.40 | loop fusion | flops 393216 | bytes 786432 | tf_op jit(solution)/shard_map/stack | solution.py:231
  1.1 3.1 %collective-permute-start = (bf16[3,32,512]{2,1,0:T(8,128)(2,1)S(1)}, bf16[3,32,512]{2,1,0:T(8,128)(2,1)S(1)}, u32[]{:S(2)}, u32[]{:S(2)}) collective-permute-start(bf16[3,32,512]{2,1,0:T(8,128)(2,1)S(1)} %get-tuple-element.43), channel_id=1, source_target_pairs={{0,1},{1,2},{2,3},{3,0},{4,5},{5,6},{6,7},{7,4},{8,9},{9,10},{10,1... | collective-permute-start | bytes 294920 | tf_op jit(solution)/shard_map/ppermute | solution.py:33
  4.2 2.6 %collective-permute-start.1 = (bf16[3,32,512]{2,1,0:T(8,128)(2,1)S(1)}, bf16[3,32,512]{2,1,0:T(8,128)(2,1)S(1)}, u32[]{:S(2)}, u32[]{:S(2)}) collective-permute-start(bf16[3,32,512]{2,1,0:T(8,128)(2,1)S(1)} %get-tuple-element.42), channel_id=1, source_target_pairs={{0,2},{1,3},{2,0},{3,1},{4,6},{5,7},{6,4},{7,5},{8,10},{9,11},{10,... | collective-permute-start | bytes 294920 | tf_op jit(solution)/shard_map/ppermute | solution.py:33
  6.8 1.3 %collective-permute-start.2 = (bf16[3,32,512]{2,1,0:T(8,128)(2,1)S(1)}, bf16[3,32,512]{2,1,0:T(8,128)(2,1)S(1)}, u32[]{:S(2)}, u32[]{:S(2)}) collective-permute-start(bf16[3,32,512]{2,1,0:T(8,128)(2,1)S(1)} %get-tuple-element.41), channel_id=1, source_target_pairs={{0,3},{1,0},{2,1},{3,2},{4,7},{5,4},{6,5},{7,6},{8,11},{9,8},{10,9... | collective-permute-start | bytes 294920 | tf_op jit(solution)/shard_map/ppermute | solution.py:33
  8.2 1.2 %fusion.15 = (pred[1024,128]{1,0:T(8,128)(4,1)S(1)}, pred[1024,128]{1,0:T(8,128)(4,1)}, pred[1024,128]{1,0:T(8,128)(4,1)}, pred[1024,128]{1,0:T(8,128)(4,1)}, pr...) fusion(s32[128]{0:T(128)S(1)} %iota_add_fusion), kind=kLoop, calls=%fused_computation.39 | loop fusion | flops 917504 | bytes 786944 | tf_op jit(solution)/shard_map/ge | solution.py:207
  9.4 0.5 collective-permute-done
  9.9 3.5 %collective-permute-done.1 = bf16[3,32,512]{2,1,0:T(8,128)(2,1)S(1)} collective-permute-done((bf16[3,32,512]{2,1,0:T(8,128)(2,1)S(1)}, bf16[3,32,512]{2,1,0:T(8,128)(2,1)S(1)}, u32[]{:S(2)}, u32[]{:S(2)}) %collective-permute-start.1) | collective-permute-done | bytes 98336 | tf_op jit(solution)/shard_map/ppermute | solution.py:33
  13.5 0.6 gather_fusion
  14.1 0.1 select_bitcast_fusion
  14.2 1.6 %collective-permute-start.3 = (bf16[1,128,512]{2,1,0:T(8,128)(2,1)S(1)}, bf16[1,128,512]{2,1,0:T(8,128)(2,1)S(1)}, u32[]{:S(2)}, u32[]{:S(2)}) collective-permute-start(bf16[1,128,512]{2,1,0:T(8,128)(2,1)S(1)} %bitcast.84), channel_id=1, source_target_pairs={{0,16},{4,20},{8,24},{12,28},{16,0},{20,4},{24,8},{28,12},{1,17},{... | collective-permute-start | bytes 393224 | tf_op jit(solution)/shard_map/ppermute | solution.py:61
  15.8 0.9 %slice_reduce_fusion.17 = (f32[4]{0:T(128)}, f32[4]{0:T(128)S(1)}, f32[4]{0:T(128)S(1)}, f32[4]{0:T(128)S(1)}, f32[4]{0:T(128)}, /*index=5*/f32[4]{0:T(128)S(1)}...) fusion(f32[4,6,11]{2,0,1:T(4,128)S(1)} %copy-done.3), kind=kLoop, calls=%fused_computation.135 | loop fusion | bytes 480 | tf_op jit(solution)/shard_map/slice | solution.py:191
  16.7 2.8 %collective-permute-done.3 = bf16[1,128,512]{2,1,0:T(8,128)(2,1)S(1)} collective-permute-done((bf16[1,128,512]{2,1,0:T(8,128)(2,1)S(1)}, bf16[1,128,512]{2,1,0:T(8,128)(2,1)S(1)}, u32[]{:S(2)}, u32[]{:S(2)}) %collective-permute-start.3) | collective-permute-done | bytes 131104 | tf_op jit(solution)/shard_map/ppermute | solution.py:61
  19.6 1.6 %collective-permute-start.4 = (bf16[2,128,512]{2,1,0:T(8,128)(2,1)S(1)}, bf16[2,128,512]{2,1,0:T(8,128)(2,1)S(1)}, u32[]{:S(2)}, u32[]{:S(2)}) collective-permute-start(bf16[2,128,512]{2,1,0:T(8,128)(2,1)S(1)} %maximum_select_fusion.4), channel_id=1, source_target_pairs={{0,8},{4,12},{8,0},{12,4},{16,24},{20,28},{24,16},{28,20},{1,9},{5... | collective-permute-start | bytes 786440 | tf_op jit(solution)/shard_map/ppermute | solution.py:61
  21.1 0.8 %slice_reduce_fusion.18 = (f32[4]{0:T(128)}, f32[4]{0:T(128)}, f32[4]{0:T(128)}, f32[4]{0:T(128)}) fusion(f32[1,4,4]{2,1,0:T(4,128)S(1)} %bitcast.98), kind=kLoop, calls=%fused_computation.136 | loop fusion | bytes 128 | tf_op jit(solution)/shard_map/slice | solution.py:215
  22.0 0.7 reshape.179.taps_ref
  22.7 1.3 %collective-permute-start.8 = (bf16[5,512]{1,0:T(8,128)(2,1)S(1)}, bf16[5,512]{1,0:T(8,128)(2,1)S(1)}, u32[]{:S(2)}, u32[]{:S(2)}) collective-permute-start(bf16[5,512]{1,0:T(8,128)(2,1)S(1)} %slice.270), channel_id=1, source_target_pairs={{0,4},{4,8},{8,12},{12,16},{16,20},{20,24},{24,28},{1,5},{5,9},{9,... | collective-permute-start | bytes 15368 | tf_op jit(solution)/shard_map/ppermute | solution.py:23
  24.0 0.1 copy.69
  24.2 0.6 collective-permute-done.8
  24.8 0.1 pad_maximum_fusion.3
  24.9 0.1 copy.64
  25.1 1.8 %collective-permute-done.4 = bf16[2,128,512]{2,1,0:T(8,128)(2,1)S(1)} collective-permute-done((bf16[2,128,512]{2,1,0:T(8,128)(2,1)S(1)}, bf16[2,128,512]{2,1,0:T(8,128)(2,1)S(1)}, u32[]{:S(2)}, u32[]{:S(2)}) %collective-permute-start.4) | collective-permute-done | bytes 262176 | tf_op jit(solution)/shard_map/ppermute | solution.py:61
  26.9 0.1 maximum_select_fusion.2
  27.0 3.5 %collective-permute-start.5 = (bf16[1,128,512]{2,1,0:T(8,128)(2,1)S(1)}, bf16[1,128,512]{2,1,0:T(8,128)(2,1)S(1)}, u32[]{:S(2)}, u32[]{:S(2)}) collective-permute-start(bf16[1,128,512]{2,1,0:T(8,128)(2,1)S(1)} %bitcast.82), channel_id=1, source_target_pairs={{0,16},{4,20},{8,24},{12,28},{16,0},{20,4},{24,8},{28,12},{1,17},{... | collective-permute-start | bytes 393224 | tf_op jit(solution)/shard_map/ppermute | solution.py:61
  30.5 0.1 copy.65
  30.7 0.1 copy.66
  30.9 2.6 %collective-permute-done.5 = bf16[1,128,512]{2,1,0:T(8,128)(2,1)S(1)} collective-permute-done((bf16[1,128,512]{2,1,0:T(8,128)(2,1)S(1)}, bf16[1,128,512]{2,1,0:T(8,128)(2,1)S(1)}, u32[]{:S(2)}, u32[]{:S(2)}) %collective-permute-start.5) | collective-permute-done | bytes 131104 | tf_op jit(solution)/shard_map/ppermute | solution.py:61
  33.5 0.9 %collective-permute-start.6 = (bf16[2,128,512]{2,1,0:T(8,128)(2,1)S(1)}, bf16[2,128,512]{2,1,0:T(8,128)(2,1)S(1)}, u32[]{:S(2)}, u32[]{:S(2)}) collective-permute-start(bf16[2,128,512]{2,1,0:T(8,128)(2,1)S(1)} %maximum_select_fusion.5), channel_id=1, source_target_pairs={{0,8},{4,12},{8,0},{12,4},{16,24},{20,28},{24,16},{28,20},{1,9},{5... | collective-permute-start | bytes 786440 | tf_op jit(solution)/shard_map/ppermute | solution.py:61
  34.4 0.1 copy.67
  34.5 0.1 copy.68
  34.8 5.4 %collective-permute-done.6 = bf16[2,128,512]{2,1,0:T(8,128)(2,1)S(1)} collective-permute-done((bf16[2,128,512]{2,1,0:T(8,128)(2,1)S(1)}, bf16[2,128,512]{2,1,0:T(8,128)(2,1)S(1)}, u32[]{:S(2)}, u32[]{:S(2)}) %collective-permute-start.6) | collective-permute-done | bytes 262176 | tf_op jit(solution)/shard_map/ppermute | solution.py:61
  40.3 0.2 maximum_select_fusion.1
  40.6 0.1 fusion.24
  40.7 0.1 fusion.56
  40.9 0.1 slice.221
  41.0 0.6 copy-done
  41.6 0.1 slice.225
  41.7 0.1 slice.231
  41.8 0.1 slice.239
  41.9 0.1 slice.249
  42.0 0.8 %fusion.21 = (f32[133,4]{1,0:T(8,128)S(1)}, f32[133,4]{1,0:T(8,128)S(1)}, f32[133,4]{1,0:T(8,128)S(1)}, f32[133,4]{1,0:T(8,128)S(1)}, f32[133,4]{1,0:T(8,128)S(1)}) fusion(f32[133,4,128]{2,1,0:T(4,128)S(1)} %slice.249, bf16[128,4,128]{2,1,0:T(4,128)(2,1)S(1)} %concatenate.63, bf16[5,4,128]{2,1,0:T(4,128)(2,1)S(1)} %concatenate.62, ...), kind=kLoop, calls=%fused_computation.52 | loop fusion | flops 814492 | bytes 1508752 | tf_op jit(solution)/shard_map/reduce_sum | solution.py:182
  42.9 0.1 copy.71
  43.0 0.1 copy.74
  43.2 0.1 copy.73
  43.3 10.9 %shard_map.64 = f32[4,1024,128]{2,1,0:T(8,128)} custom-call(f32[264]{0:T(512)} %reshape.179.taps_ref, bf16[4,768,128]{2,1,0:T(8,128)(2,1)} %bitcast.81, bf16[1024,512]{1,0:T(8,128)(2,1)} %bitcast.75), custom_call_target="tpu_custom_call" | custom-call | tf_op jit(solution)/shard_map/pallas_call | solution.py:154
  54.2 0.1 subtract_bitcast_fusion.3
  54.3 0.1 fusion.44
  54.4 3.8 %divide_bitcast_fusion = f32[1,4,1024,128]{3,2,1,0:T(8,128)S(1)} fusion(f32[4,1024,128]{2,1,0:T(8,128)} %shard_map.64, f32[4,128]{1,0:T(4,128)S(1)} %get-tuple-element.60, f32[4,128]{1,0:T(4,128)S(1)} %get-tuple-element.59, f32[4,128]{1,0:T(4,128)S(1)} %get-tuple-element.58, f32[4,128]{1,0:T(4,128)S(1)} %subtract_bitcast_fusion.3, f32[4,128]{1,0:T(4,128)S(1)} %fusion.44, ...), kind=kOutput, calls=%fused_computation.5 | output fusion | flops 6818814 | bytes 4990976 | tf_op jit(solution)/shard_map/div | solution.py:210
  58.3 1.2 %slice_bitcast_fusion.3 = (f32[1024,128]{1,0:T(8,128)S(1)}, f32[1024,128]{1,0:T(8,128)}, f32[1024,128]{1,0:T(8,128)}, f32[1024,128]{1,0:T(8,128)}) fusion(f32[1,4,1024,128]{3,2,1,0:T(8,128)S(1)} %divide_bitcast_fusion), kind=kLoop, calls=%fused_computation.30 | loop fusion | bytes 4194304 | tf_op jit(solution)/shard_map/mul | solution.py:215
  59.5 1.4 %maximum_select_fusion = bf16[8,128,512]{2,1,0:T(8,128)(2,1)S(1)} fusion(bf16[4,128,512]{2,1,0:T(8,128)(2,1)S(1)} %maximum_select_fusion.3, bf16[4,128,512]{2,1,0:T(8,128)(2,1)} %collective-permute-done.7, pred[]{:T(512)S(6)} %ne.64), kind=kLoop, calls=%fused_computation.12 | loop fusion | flops 1572864 | bytes 2097153 | tf_op jit(solution)/shard_map/jit(_where)/select_n | solution.py:62
  60.9 0.9 %copy.62 = bf16[2,2,2,128,512]{3,2,1,0,4:T(2,128)(2,1)S(1)} copy(bf16[2,2,2,128,512]{4,3,0,1,2:T(8,128)(2,1)S(1)} %bitcast.76) | data formatting | bytes 2097152 | tf_op jit(solution)/shard_map/transpose | solution.py:72
  61.9 0.8 %reshape_reshape.3 = bf16[1024,4,128]{0,2,1:T(8,128)(2,1)S(1)} reshape(bf16[2,2,2,128,512]{3,2,1,0,4:T(2,128)(2,1)S(1)} %copy.62) | data formatting | bytes 2097152 | tf_op jit(solution)/shard_map/reshape;reshape | solution.py:262
  62.7 0.2 copy-done.2
  62.9 2.1 %multiply_reduce_fusion = (f32[128,4]{0,1:T(4,128)S(1)}, f32[128,4,128]{0,2,1:T(8,128)S(1)}) fusion(bf16[1024,4,128]{0,2,1:T(8,128)(2,1)S(1)} %reshape_reshape.3, f32[1024,128]{1,0:T(8,128)S(1)} %copy-done.2, f32[4]{0:T(128)S(1)} %copy-done.14, f32[1024,128]{1,0:T(8,128)} %get-tuple-element.35, f32[4]{0:T(128)S(1)} %copy-done.15, ...), kind=kOutput, calls=%fused_computation.56 | convolution fusion | flops 138542592 | bytes 3409984 | tf_op jit(solution)/shard_map/hki,khd->ihd/dot_general | solution.py:217
  65.1 0.1 multiply_convert_fusion
  65.2 0.2 constant_dynamic-slice_fusion.3
  65.5 2.7 %collective-permute-start.10 = (bf16[32,512]{1,0:T(8,128)(2,1)S(1)}, bf16[32,512]{1,0:T(8,128)(2,1)S(1)}, u32[]{:S(2)}, u32[]{:S(2)}) collective-permute-start(bf16[32,512]{1,0:T(8,128)(2,1)S(1)} %copy.81), channel_id=1, source_target_pairs={{0,1},{1,2},{2,3},{3,0},{4,5},{5,6},{6,7},{7,4},{8,9},{9,10},{10,1... | collective-permute-start | bytes 98312 | tf_op jit(solution)/shard_map/ppermute | solution.py:33
  68.3 1.4 %collective-permute-start.11 = (bf16[32,512]{1,0:T(8,128)(2,1)S(1)}, bf16[32,512]{1,0:T(8,128)(2,1)S(1)}, u32[]{:S(2)}, u32[]{:S(2)}) collective-permute-start(bf16[32,512]{1,0:T(8,128)(2,1)S(1)} %copy.82), channel_id=1, source_target_pairs={{0,2},{1,3},{2,0},{3,1},{4,6},{5,7},{6,4},{7,5},{8,10},{9,11},{10,... | collective-permute-start | bytes 98312 | tf_op jit(solution)/shard_map/ppermute | solution.py:33
  69.8 1.1 %collective-permute-start.12 = (bf16[32,512]{1,0:T(8,128)(2,1)S(1)}, bf16[32,512]{1,0:T(8,128)(2,1)S(1)}, u32[]{:S(2)}, u32[]{:S(2)}) collective-permute-start(bf16[32,512]{1,0:T(8,128)(2,1)S(1)} %copy.83), channel_id=1, source_target_pairs={{0,3},{1,0},{2,1},{3,2},{4,7},{5,4},{6,5},{7,6},{8,11},{9,8},{10,9... | collective-permute-start | bytes 98312 | tf_op jit(solution)/shard_map/ppermute | solution.py:33
  71.0 0.3 collective-permute-done.10
  71.3 2.3 %collective-permute-done.11 = bf16[32,512]{1,0:T(8,128)(2,1)S(1)} collective-permute-done((bf16[32,512]{1,0:T(8,128)(2,1)S(1)}, bf16[32,512]{1,0:T(8,128)(2,1)S(1)}, u32[]{:S(2)}, u32[]{:S(2)}) %collective-permute-start.11) | collective-permute-done | bytes 32800 | tf_op jit(solution)/shard_map/ppermute | solution.py:33
  73.5 0.3 collective-permute-done.12
  73.9 0.6 gather_fusion.1
  74.4 0.1 select_bitcast_fusion.1
  74.5 0.7 copy.85
  (73 shorter events, 1.4 us)
Async XLA Ops:
  1.1 14.7 %copy-start.3 = (f32[4,6,11]{2,0,1:T(4,128)S(1)}, f32[4,6,11]{2,0,1:T(4,128)}, u32[]{:S(2)}) copy-start(f32[4,6,11]{2,0,1:T(4,128)} %param.9) | copy-start | bytes 3172
  1.1 8.8 %collective-permute-start = (bf16[3,32,512]{2,1,0:T(8,128)(2,1)S(1)}, bf16[3,32,512]{2,1,0:T(8,128)(2,1)S(1)}, u32[]{:S(2)}, u32[]{:S(2)}) collective-permute-start(bf16[3,32,512]{2,1,0:T(8,128)(2,1)S(1)} %get-tuple-element.43), channel_id=1, source_target_pairs={{0,1},{1,2},{2,3},{3,0},{4,5},{5,6},{6,7},{7,4},{8,9},{9,10},{10,1... | collective-permute-start | bytes 294920 | tf_op jit(solution)/shard_map/ppermute | solution.py:33
  4.2 9.2 %collective-permute-start.1 = (bf16[3,32,512]{2,1,0:T(8,128)(2,1)S(1)}, bf16[3,32,512]{2,1,0:T(8,128)(2,1)S(1)}, u32[]{:S(2)}, u32[]{:S(2)}) collective-permute-start(bf16[3,32,512]{2,1,0:T(8,128)(2,1)S(1)} %get-tuple-element.42), channel_id=1, source_target_pairs={{0,2},{1,3},{2,0},{3,1},{4,6},{5,7},{6,4},{7,5},{8,10},{9,11},{10,... | collective-permute-start | bytes 294920 | tf_op jit(solution)/shard_map/ppermute | solution.py:33
  6.8 6.6 %collective-permute-start.2 = (bf16[3,32,512]{2,1,0:T(8,128)(2,1)S(1)}, bf16[3,32,512]{2,1,0:T(8,128)(2,1)S(1)}, u32[]{:S(2)}, u32[]{:S(2)}) collective-permute-start(bf16[3,32,512]{2,1,0:T(8,128)(2,1)S(1)} %get-tuple-element.41), channel_id=1, source_target_pairs={{0,3},{1,0},{2,1},{3,2},{4,7},{5,4},{6,5},{7,6},{8,11},{9,8},{10,9... | collective-permute-start | bytes 294920 | tf_op jit(solution)/shard_map/ppermute | solution.py:33
  8.2 13.0 %copy-start.4 = (f32[4,4]{1,0:T(4,128)S(1)}, f32[4,4]{1,0:T(4,128)}, u32[]{:S(2)}) copy-start(f32[4,4]{1,0:T(4,128)} %param.10) | copy-start | bytes 196
  9.4 13.3 %copy-start.11 = (pred[4]{0:T(512)(128)(4,1)}, pred[4]{0:T(512)(128)(4,1)S(1)}, u32[]{:S(2)}) copy-start(pred[4]{0:T(512)(128)(4,1)S(1)} %compare_and_fusion) | copy-start | bytes 16
  14.2 5.3 %collective-permute-start.3 = (bf16[1,128,512]{2,1,0:T(8,128)(2,1)S(1)}, bf16[1,128,512]{2,1,0:T(8,128)(2,1)S(1)}, u32[]{:S(2)}, u32[]{:S(2)}) collective-permute-start(bf16[1,128,512]{2,1,0:T(8,128)(2,1)S(1)} %bitcast.84), channel_id=1, source_target_pairs={{0,16},{4,20},{8,24},{12,28},{16,0},{20,4},{24,8},{28,12},{1,17},{... | collective-permute-start | bytes 393224 | tf_op jit(solution)/shard_map/ppermute | solution.py:61
  19.6 7.3 %collective-permute-start.4 = (bf16[2,128,512]{2,1,0:T(8,128)(2,1)S(1)}, bf16[2,128,512]{2,1,0:T(8,128)(2,1)S(1)}, u32[]{:S(2)}, u32[]{:S(2)}) collective-permute-start(bf16[2,128,512]{2,1,0:T(8,128)(2,1)S(1)} %maximum_select_fusion.4), channel_id=1, source_target_pairs={{0,8},{4,12},{8,0},{12,4},{16,24},{20,28},{24,16},{28,20},{1,9},{5... | collective-permute-start | bytes 786440 | tf_op jit(solution)/shard_map/ppermute | solution.py:61
  22.7 2.1 %collective-permute-start.8 = (bf16[5,512]{1,0:T(8,128)(2,1)S(1)}, bf16[5,512]{1,0:T(8,128)(2,1)S(1)}, u32[]{:S(2)}, u32[]{:S(2)}) collective-permute-start(bf16[5,512]{1,0:T(8,128)(2,1)S(1)} %slice.270), channel_id=1, source_target_pairs={{0,4},{4,8},{8,12},{12,16},{16,20},{20,24},{24,28},{1,5},{5,9},{9,... | collective-permute-start | bytes 15368 | tf_op jit(solution)/shard_map/ppermute | solution.py:23
  27.0 6.5 %collective-permute-start.5 = (bf16[1,128,512]{2,1,0:T(8,128)(2,1)S(1)}, bf16[1,128,512]{2,1,0:T(8,128)(2,1)S(1)}, u32[]{:S(2)}, u32[]{:S(2)}) collective-permute-start(bf16[1,128,512]{2,1,0:T(8,128)(2,1)S(1)} %bitcast.82), channel_id=1, source_target_pairs={{0,16},{4,20},{8,24},{12,28},{16,0},{20,4},{24,8},{28,12},{1,17},{... | collective-permute-start | bytes 393224 | tf_op jit(solution)/shard_map/ppermute | solution.py:61
  30.8 9.5 %collective-permute-start.9 = (bf16[4,128,512]{2,1,0:T(8,128)(2,1)S(1)}, bf16[4,128,512]{2,1,0:T(8,128)(2,1)S(1)}, u32[]{:S(2)}, u32[]{:S(2)}) collective-permute-start(bf16[4,128,512]{2,1,0:T(8,128)(2,1)S(1)} %maximum_select_fusion.2), channel_id=1, source_target_pairs={{0,4},{4,0},{8,12},{12,8},{16,20},{20,16},{24,28},{28,24},{1,5},{5... | collective-permute-start | bytes 1572872 | tf_op jit(solution)/shard_map/ppermute | solution.py:61
  33.5 6.7 %collective-permute-start.6 = (bf16[2,128,512]{2,1,0:T(8,128)(2,1)S(1)}, bf16[2,128,512]{2,1,0:T(8,128)(2,1)S(1)}, u32[]{:S(2)}, u32[]{:S(2)}) collective-permute-start(bf16[2,128,512]{2,1,0:T(8,128)(2,1)S(1)} %maximum_select_fusion.5), channel_id=1, source_target_pairs={{0,8},{4,12},{8,0},{12,4},{16,24},{20,28},{24,16},{28,20},{1,9},{5... | collective-permute-start | bytes 786440 | tf_op jit(solution)/shard_map/ppermute | solution.py:61
  34.7 5.8 %copy-start.1 = (bf16[128,4,6,128]{0,3,2,1:T(8,128)(2,1)}, bf16[128,4,6,128]{0,3,2,1:T(8,128)(2,1)S(1)}, u32[]{:S(2)}) copy-start(bf16[128,4,6,128]{0,3,2,1:T(8,128)(2,1)S(1)} %constant_dynamic-update-slice_fusion) | copy-start | bytes 2359300
  40.2 19.2 %collective-permute-start.7 = (bf16[4,128,512]{2,1,0:T(8,128)(2,1)S(1)}, bf16[4,128,512]{2,1,0:T(8,128)(2,1)}, u32[]{:S(2)}, u32[]{:S(2)}) collective-permute-start(bf16[4,128,512]{2,1,0:T(8,128)(2,1)S(1)} %maximum_select_fusion.3), channel_id=1, source_target_pairs={{0,4},{4,0},{8,12},{12,8},{16,20},{20,16},{24,28},{28,24},{1,5},{5... | collective-permute-start | bytes 1572872 | tf_op jit(solution)/shard_map/ppermute | solution.py:61
  40.6 1.0 %copy-start = (bf16[2,2,2,128,512]{4,3,2,1,0:T(8,128)(2,1)}, bf16[2,2,2,128,512]{4,3,2,1,0:T(8,128)(2,1)S(1)}, u32[]{:S(2)}) copy-start(bf16[2,2,2,128,512]{4,3,2,1,0:T(8,128)(2,1)S(1)} %copy.70) | copy-start | bytes 3145732
  43.0 11.2 %copy-start.6 = (f32[4]{0:T(128)S(1)}, f32[4]{0:T(128)}, u32[]{:S(2)}) copy-start(f32[4]{0:T(128)} %get-tuple-element.14) | copy-start | bytes 52
  43.0 11.3 %copy-start.7 = (f32[4]{0:T(128)S(1)}, f32[4]{0:T(128)}, u32[]{:S(2)}) copy-start(f32[4]{0:T(128)} %get-tuple-element.18) | copy-start | bytes 52
  43.1 11.3 %copy-start.8 = (f32[4]{0:T(128)S(1)}, f32[4]{0:T(128)}, u32[]{:S(2)}) copy-start(f32[4]{0:T(128)} %get-tuple-element.22) | copy-start | bytes 52
  43.1 11.3 %copy-start.9 = (f32[4]{0:T(128)S(1)}, f32[4]{0:T(128)}, u32[]{:S(2)}) copy-start(f32[4]{0:T(128)} %get-tuple-element.25) | copy-start | bytes 52
  43.1 11.3 %copy-start.10 = (f32[4]{0:T(128)S(1)}, f32[4]{0:T(128)}, u32[]{:S(2)}) copy-start(f32[4]{0:T(128)} %get-tuple-element.27) | copy-start | bytes 52
  60.9 1.8 %copy-start.13 = (f32[4]{0:T(128)S(1)}, f32[4]{0:T(128)}, u32[]{:S(2)}) copy-start(f32[4]{0:T(128)} %get-tuple-element.29) | copy-start | bytes 52
  60.9 1.8 %copy-start.14 = (f32[4]{0:T(128)S(1)}, f32[4]{0:T(128)}, u32[]{:S(2)}) copy-start(f32[4]{0:T(128)} %get-tuple-element.30) | copy-start | bytes 52
  60.9 1.8 %copy-start.15 = (f32[4]{0:T(128)S(1)}, f32[4]{0:T(128)}, u32[]{:S(2)}) copy-start(f32[4]{0:T(128)} %get-tuple-element.31) | copy-start | bytes 52
  60.9 1.8 %copy-start.16 = (f32[4]{0:T(128)S(1)}, f32[4]{0:T(128)}, u32[]{:S(2)}) copy-start(f32[4]{0:T(128)} %get-tuple-element.32) | copy-start | bytes 52
  61.9 1.0 %copy-start.2 = (f32[1024,128]{1,0:T(8,128)S(1)}, f32[1024,128]{1,0:T(8,128)}, u32[]{:S(2)}) copy-start(f32[1024,128]{1,0:T(8,128)} %get-tuple-element.34) | copy-start | bytes 1572868
  62.9 2.2 %copy-start.5 = (f32[512]{0:T(512)S(1)}, f32[512]{0:T(512)}, u32[]{:S(2)}) copy-start(f32[512]{0:T(512)} %param.11) | copy-start | bytes 6148
  65.0 9.4 %copy-start.12 = (pred[4]{0:T(512)(128)(4,1)S(1)}, pred[4]{0:T(512)(128)(4,1)}, u32[]{:S(2)}) copy-start(pred[4]{0:T(512)(128)(4,1)} %copy-done.11) | copy-start | bytes 16
  65.5 5.8 %collective-permute-start.10 = (bf16[32,512]{1,0:T(8,128)(2,1)S(1)}, bf16[32,512]{1,0:T(8,128)(2,1)S(1)}, u32[]{:S(2)}, u32[]{:S(2)}) collective-permute-start(bf16[32,512]{1,0:T(8,128)(2,1)S(1)} %copy.81), channel_id=1, source_target_pairs={{0,1},{1,2},{2,3},{3,0},{4,5},{5,6},{6,7},{7,4},{8,9},{9,10},{10,1... | collective-permute-start | bytes 98312 | tf_op jit(solution)/shard_map/ppermute | solution.py:33
  68.3 5.2 %collective-permute-start.11 = (bf16[32,512]{1,0:T(8,128)(2,1)S(1)}, bf16[32,512]{1,0:T(8,128)(2,1)S(1)}, u32[]{:S(2)}, u32[]{:S(2)}) collective-permute-start(bf16[32,512]{1,0:T(8,128)(2,1)S(1)} %copy.82), channel_id=1, source_target_pairs={{0,2},{1,3},{2,0},{3,1},{4,6},{5,7},{6,4},{7,5},{8,10},{9,11},{10,... | collective-permute-start | bytes 98312 | tf_op jit(solution)/shard_map/ppermute | solution.py:33
  69.8 4.0 %collective-permute-start.12 = (bf16[32,512]{1,0:T(8,128)(2,1)S(1)}, bf16[32,512]{1,0:T(8,128)(2,1)S(1)}, u32[]{:S(2)}, u32[]{:S(2)}) collective-permute-start(bf16[32,512]{1,0:T(8,128)(2,1)S(1)} %copy.83), channel_id=1, source_target_pairs={{0,3},{1,0},{2,1},{3,2},{4,7},{5,4},{6,5},{7,6},{8,11},{9,8},{10,9... | collective-permute-start | bytes 98312 | tf_op jit(solution)/shard_map/ppermute | solution.py:33

commit v22 on v15

--- a/solution.py
+++ b/solution.py
@@ -175,7 +175,7 @@
     logits = jnp.where(gap >= 0, convolved, lowest)
     peak = jnp.max(logits, axis=1, keepdims=True)
     expd = jnp.exp(logits - peak)
-    probabilities = expd / jnp.sum(expd, axis=1, keepdims=True)
+    probabilities = expd * (1.0 / jnp.sum(expd, axis=1, keepdims=True))
     grouped = probabilities.reshape(heads // GROUP, GROUP, seq_len, row_count)
     weights = head_mixing.reshape(heads // GROUP, GROUP, GROUP)
     mixed_probs = jnp.zeros_like(grouped)

time: 71.6 us -> 71.5 us (level)
  waiting for transfers between devices: 16.8 us -> 18.5 us
  local copies, waits for them, and re-layouts: 11.6 us -> 10.5 us
    div x1, other arithmetic: 3.88 us -> 0.01 us  [attend_chunk(): probabilities = expd * (1.0 / jnp.sum(expd, axis=1, keepdims=True))]
    sub x0 -> x1, other arithmetic: none -> 3.73 us  [attend_chunk(): expd = jnp.exp(logits - peak)]
    ppermute x6, waiting for transfers between devices: 10.1 us -> 11.9 us  [gathered(): incoming = lax.ppermute(held, axis, [(i, i ^ bit) for i in range(peers)])]
  transfers between devices with their start and end apart: 13 -> 13, of which waited for: 9 -> 10; matrix products, arithmetic and copies ran while one was open for 15% -> 14% of each run, Pallas kernels for 15% -> 15%
where the time goes in v22:
time: 71.5 us; the launch traced here: 71.3 us
  starting transfers between devices  20.3 us (28%)
  waiting for transfers between devices  18.5 us (26%)
  Pallas kernels  10.9 us (15%)
  local copies, waits for them, and re-layouts  10.5 us (15%)
  other arithmetic  8.36 us (12%)
  matrix products  2.12 us (3%)
    ppermute x6, starting transfers between devices, exchanged(): received.append(lax.ppermute(outgoing, axis, pairs))  12.2 us
    ppermute x6, waiting for transfers between devices, gathered(): incoming = lax.ppermute(held, axis, [(i, i ^ bit) for i in range(peers)])  11.9 us
    pallas_call x1, Pallas kernels, conv_logits(): pl.pallas_call(logits_kernel, grid=(heads, seq_len // span), in_specs=[pl...  10.9 us
    ppermute x6, starting transfers between devices, gathered(): incoming = lax.ppermute(held, axis, [(i, i ^ bit) for i in range(peers)])  6.76 us
    ppermute x6, waiting for transfers between devices, exchanged(): received.append(lax.ppermute(outgoing, axis, pairs))  6.69 us
    sub x1, other arithmetic, attend_chunk(): expd = jnp.exp(logits - peak)  3.73 us
    dot_general x1, matrix products, attend_chunk(): jnp.einsum('hki,khd->ihd', mixed_probs, value_heads, preferred_element_ty...  2.12 us
  transfers between devices with their start and end apart: 13, of which 10 were waited for; matrix products, arithmetic and copies ran while one was open for 14% of the time, Pallas kernels for 15%

profile of v22, /device:TPU:0, one launch (start us, length us, event | category | flops | bytes accessed | tf_op | source)
XLA Modules:
  0.0 71.3 jit_solution(3618231545724094734)
XLA Ops:
  0.0 1.1 %pad_maximum_fusion = bf16[3,32,2048]{2,1,0:T(8,128)(2,1)S(1)} fusion(bf16[1,32,2048]{2,1,0:T(8,128)(2,1)} %bitcast.92, bf16[1,32,2048]{2,1,0:T(8,128)(2,1)} %bitcast.93, bf16[1,32,2048]{2,1,0:T(8,128)(2,1)} %bitcast.94), kind=kLoop, calls=%fused_computation.39 | loop fusion | flops 393216 | bytes 786432 | tf_op jit(solution)/shard_map/stack | solution.py:199
  1.1 3.1 %collective-permute-start = (bf16[3,32,512]{2,1,0:T(8,128)(2,1)S(1)}, bf16[3,32,512]{2,1,0:T(8,128)(2,1)S(1)}, u32[]{:S(2)}, u32[]{:S(2)}) collective-permute-start(bf16[3,32,512]{2,1,0:T(8,128)(2,1)S(1)} %get-tuple-element.43), channel_id=1, source_target_pairs={{0,1},{1,2},{2,3},{3,0},{4,5},{5,6},{6,7},{7,4},{8,9},{9,10},{10,1... | collective-permute-start | bytes 294920 | tf_op jit(solution)/shard_map/ppermute | solution.py:33
  4.2 2.6 %collective-permute-start.1 = (bf16[3,32,512]{2,1,0:T(8,128)(2,1)S(1)}, bf16[3,32,512]{2,1,0:T(8,128)(2,1)S(1)}, u32[]{:S(2)}, u32[]{:S(2)}) collective-permute-start(bf16[3,32,512]{2,1,0:T(8,128)(2,1)S(1)} %get-tuple-element.42), channel_id=1, source_target_pairs={{0,2},{1,3},{2,0},{3,1},{4,6},{5,7},{6,4},{7,5},{8,10},{9,11},{10,... | collective-permute-start | bytes 294920 | tf_op jit(solution)/shard_map/ppermute | solution.py:33
  6.8 1.3 %collective-permute-start.2 = (bf16[3,32,512]{2,1,0:T(8,128)(2,1)S(1)}, bf16[3,32,512]{2,1,0:T(8,128)(2,1)S(1)}, u32[]{:S(2)}, u32[]{:S(2)}) collective-permute-start(bf16[3,32,512]{2,1,0:T(8,128)(2,1)S(1)} %get-tuple-element.41), channel_id=1, source_target_pairs={{0,3},{1,0},{2,1},{3,2},{4,7},{5,4},{6,5},{7,6},{8,11},{9,8},{10,9... | collective-permute-start | bytes 294920 | tf_op jit(solution)/shard_map/ppermute | solution.py:33
  8.2 1.1 %fusion.14 = (pred[1024,128]{1,0:T(8,128)(4,1)S(1)}, pred[1024,128]{1,0:T(8,128)(4,1)S(1)}, pred[1024,128]{1,0:T(8,128)(4,1)S(1)}, pred[1024,128]{1,0:T(8,128)(4...) fusion(s32[128]{0:T(128)S(1)} %iota_add_fusion), kind=kLoop, calls=%fused_computation.38 | loop fusion | flops 917504 | bytes 786944 | tf_op jit(solution)/shard_map/ge | solution.py:175
  9.4 0.5 collective-permute-done
  9.9 3.5 %collective-permute-done.1 = bf16[3,32,512]{2,1,0:T(8,128)(2,1)S(1)} collective-permute-done((bf16[3,32,512]{2,1,0:T(8,128)(2,1)S(1)}, bf16[3,32,512]{2,1,0:T(8,128)(2,1)S(1)}, u32[]{:S(2)}, u32[]{:S(2)}) %collective-permute-start.1) | collective-permute-done | bytes 98336 | tf_op jit(solution)/shard_map/ppermute | solution.py:33
  13.5 0.6 gather_fusion
  14.1 0.1 select_bitcast_fusion
  14.2 0.7 fusion.49
  14.9 1.5 %collective-permute-start.3 = (bf16[1,128,512]{2,1,0:T(8,128)(2,1)S(1)}, bf16[1,128,512]{2,1,0:T(8,128)(2,1)S(1)}, u32[]{:S(2)}, u32[]{:S(2)}) collective-permute-start(bf16[1,128,512]{2,1,0:T(8,128)(2,1)S(1)} %bitcast.85), channel_id=1, source_target_pairs={{0,16},{4,20},{8,24},{12,28},{16,0},{20,4},{24,8},{28,12},{1,17},{... | collective-permute-start | bytes 393224 | tf_op jit(solution)/shard_map/ppermute | solution.py:47
  16.4 0.4 slice_reduce_fusion.17
  16.8 3.4 %collective-permute-done.3 = bf16[1,128,512]{2,1,0:T(8,128)(2,1)S(1)} collective-permute-done((bf16[1,128,512]{2,1,0:T(8,128)(2,1)S(1)}, bf16[1,128,512]{2,1,0:T(8,128)(2,1)S(1)}, u32[]{:S(2)}, u32[]{:S(2)}) %collective-permute-start.3) | collective-permute-done | bytes 131104 | tf_op jit(solution)/shard_map/ppermute | solution.py:47
  20.2 1.6 %collective-permute-start.4 = (bf16[2,128,512]{2,1,0:T(8,128)(2,1)S(1)}, bf16[2,128,512]{2,1,0:T(8,128)(2,1)S(1)}, u32[]{:S(2)}, u32[]{:S(2)}) collective-permute-start(bf16[2,128,512]{2,1,0:T(8,128)(2,1)S(1)} %maximum_select_fusion.4), channel_id=1, source_target_pairs={{0,8},{4,12},{8,0},{12,4},{16,24},{20,28},{24,16},{28,20},{1,9},{5... | collective-permute-start | bytes 786440 | tf_op jit(solution)/shard_map/ppermute | solution.py:47
  21.7 0.2 slice_reduce_fusion.18
  22.0 0.7 reshape.184.taps_ref
  22.7 1.3 %collective-permute-start.9 = (bf16[5,512]{1,0:T(8,128)(2,1)S(1)}, bf16[5,512]{1,0:T(8,128)(2,1)S(1)}, u32[]{:S(2)}, u32[]{:S(2)}) collective-permute-start(bf16[5,512]{1,0:T(8,128)(2,1)S(1)} %slice.270), channel_id=1, source_target_pairs={{0,4},{4,8},{8,12},{12,16},{16,20},{20,24},{24,28},{1,5},{5,9},{9,... | collective-permute-start | bytes 15368 | tf_op jit(solution)/shard_map/ppermute | solution.py:23
  24.0 0.1 copy.70
  24.2 0.7 concatenate.63
  24.8 0.1 pad_maximum_fusion.3
  25.0 0.1 copy.65
  25.1 0.1 copy.66
  25.2 0.1 copy.67
  25.4 0.1 copy.68
  25.5 0.1 copy.69
  25.6 1.8 %collective-permute-done.4 = bf16[2,128,512]{2,1,0:T(8,128)(2,1)S(1)} collective-permute-done((bf16[2,128,512]{2,1,0:T(8,128)(2,1)S(1)}, bf16[2,128,512]{2,1,0:T(8,128)(2,1)S(1)}, u32[]{:S(2)}, u32[]{:S(2)}) %collective-permute-start.4) | collective-permute-done | bytes 262176 | tf_op jit(solution)/shard_map/ppermute | solution.py:47
  27.8 1.8 %collective-permute-done.5 = bf16[4,128,512]{2,1,0:T(8,128)(2,1)S(1)} collective-permute-done((bf16[4,128,512]{2,1,0:T(8,128)(2,1)S(1)}, bf16[4,128,512]{2,1,0:T(8,128)(2,1)S(1)}, u32[]{:S(2)}, u32[]{:S(2)}) %collective-permute-start.5) | collective-permute-done | bytes 524320 | tf_op jit(solution)/shard_map/ppermute | solution.py:47
  29.5 0.2 maximum_select_fusion
  29.7 0.1 copy.62
  29.8 0.1 fusion.23
  29.9 0.1 fusion.50
  30.1 0.1 slice.221
  30.2 0.6 copy-done
  30.8 0.1 slice.225
  30.9 0.1 slice.231
  31.0 0.1 slice.239
  31.1 0.1 slice.249
  31.2 0.8 %fusion.20 = (f32[133,4]{1,0:T(8,128)S(1)}, f32[133,4]{1,0:T(8,128)S(1)}, f32[133,4]{1,0:T(8,128)S(1)}, f32[133,4]{1,0:T(8,128)S(1)}, f32[133,4]{1,0:T(8,128)S(1)}) fusion(f32[133,4,128]{2,1,0:T(4,128)S(1)} %slice.249, bf16[128,4,128]{2,1,0:T(4,128)(2,1)S(1)} %copy-done.3, bf16[5,4,128]{2,1,0:T(4,128)(2,1)S(1)} %concatenate.62, ...), kind=kLoop, calls=%fused_computation.51 | loop fusion | flops 814492 | bytes 1508752 | tf_op jit(solution)/shard_map/reduce_sum | solution.py:150
  32.1 0.1 copy.71
  32.2 0.1 copy.74
  32.3 0.1 copy.72
  32.4 0.1 copy.73
  32.5 3.5 %collective-permute-start.6 = (bf16[1,128,512]{2,1,0:T(8,128)(2,1)S(1)}, bf16[1,128,512]{2,1,0:T(8,128)(2,1)S(1)}, u32[]{:S(2)}, u32[]{:S(2)}) collective-permute-start(bf16[1,128,512]{2,1,0:T(8,128)(2,1)S(1)} %bitcast.83), channel_id=1, source_target_pairs={{0,16},{4,20},{8,24},{12,28},{16,0},{20,4},{24,8},{28,12},{1,17},{... | collective-permute-start | bytes 393224 | tf_op jit(solution)/shard_map/ppermute | solution.py:47
  36.0 10.9 %shard_map.64 = f32[4,1024,128]{2,1,0:T(8,128)} custom-call(f32[264]{0:T(512)} %reshape.184.taps_ref, bf16[4,768,128]{2,1,0:T(8,128)(2,1)} %bitcast.82, bf16[1024,512]{1,0:T(8,128)(2,1)} %bitcast.76), custom_call_target="tpu_custom_call" | custom-call | tf_op jit(solution)/shard_map/pallas_call | solution.py:122
  47.0 0.1 fusion.43
  47.3 3.7 %fusion.51 = (f32[4,128]{1,0:T(4,128)S(1)}, f32[4,1024,128]{2,1,0:T(8,128)S(1)}) fusion(f32[4,1024,128]{2,1,0:T(8,128)} %shard_map.64, f32[4,128]{1,0:T(4,128)S(1)} %get-tuple-element.60, f32[4,128]{1,0:T(4,128)S(1)} %get-tuple-element.59, f32[4,128]{1,0:T(4,128)S(1)} %get-tuple-element.58, f32[4,128]{1,0:T(4,128)S(1)} %subtract_bitcast_fusion.3, ...), kind=kOutput, calls=%fused_computation.149 | output fusion | flops 6816767 | bytes 4993024 | tf_op jit(solution)/shard_map/sub | solution.py:177
  51.0 4.3 %collective-permute-done.7 = bf16[2,128,512]{2,1,0:T(8,128)(2,1)S(1)} collective-permute-done((bf16[2,128,512]{2,1,0:T(8,128)(2,1)S(1)}, bf16[2,128,512]{2,1,0:T(8,128)(2,1)S(1)}, u32[]{:S(2)}, u32[]{:S(2)}) %collective-permute-start.7) | collective-permute-done | bytes 262176 | tf_op jit(solution)/shard_map/ppermute | solution.py:47
  55.5 0.1 multiply_bitcast_fusion
  55.6 1.1 %slice_bitcast_fusion.3 = (f32[1024,128]{1,0:T(8,128)S(1)}, f32[1024,128]{1,0:T(8,128)S(1)}, f32[1024,128]{1,0:T(8,128)}, f32[1024,128]{1,0:T(8,128)}) fusion(f32[1,4,1024,128]{3,2,1,0:T(8,128)S(1)} %multiply_bitcast_fusion), kind=kLoop, calls=%fused_computation.29 | loop fusion | bytes 4194304 | tf_op jit(solution)/shard_map/mul | solution.py:183
  56.8 0.6 collective-permute-done.8
  57.4 0.2 maximum_select_fusion.1
  57.6 0.9 %copy.63 = bf16[2,2,2,128,512]{3,2,1,0,4:T(2,128)(2,1)S(1)} copy(bf16[2,2,2,128,512]{4,3,0,1,2:T(8,128)(2,1)S(1)} %bitcast.77) | data formatting | bytes 2097152 | tf_op jit(solution)/shard_map/transpose | solution.py:55
  58.5 0.8 %reshape_reshape.3 = bf16[1024,4,128]{0,2,1:T(8,128)(2,1)S(1)} reshape(bf16[2,2,2,128,512]{3,2,1,0,4:T(2,128)(2,1)S(1)} %copy.63) | data formatting | bytes 2097152 | tf_op jit(solution)/shard_map/reshape;reshape | solution.py:230
  59.3 2.1 %multiply_reduce_fusion = (f32[128,4]{0,1:T(4,128)S(1)}, f32[128,4,128]{0,2,1:T(8,128)S(1)}) fusion(bf16[1024,4,128]{0,2,1:T(8,128)(2,1)S(1)} %reshape_reshape.3, f32[1024,128]{1,0:T(8,128)S(1)} %get-tuple-element.34, f32[4]{0:T(128)S(1)} %get-tuple-element.30, f32[1024,128]{1,0:T(8,128)} %get-tuple-element.35, f32[4]{0:T(128)S(1)} %get-tuple-element.31, ...), kind=kOutput, calls=%fused_computation.55 | convolution fusion | flops 138542592 | bytes 3409984 | tf_op jit(solution)/shard_map/hki,khd->ihd/dot_general | solution.py:185
  61.4 0.1 multiply_convert_fusion
  61.6 0.2 constant_dynamic-slice_fusion.3
  61.9 2.7 %collective-permute-start.10 = (bf16[32,512]{1,0:T(8,128)(2,1)S(1)}, bf16[32,512]{1,0:T(8,128)(2,1)S(1)}, u32[]{:S(2)}, u32[]{:S(2)}) collective-permute-start(bf16[32,512]{1,0:T(8,128)(2,1)S(1)} %copy.81), channel_id=1, source_target_pairs={{0,1},{1,2},{2,3},{3,0},{4,5},{5,6},{6,7},{7,4},{8,9},{9,10},{10,1... | collective-permute-start | bytes 98312 | tf_op jit(solution)/shard_map/ppermute | solution.py:33
  64.7 1.2 %collective-permute-start.11 = (bf16[32,512]{1,0:T(8,128)(2,1)S(1)}, bf16[32,512]{1,0:T(8,128)(2,1)S(1)}, u32[]{:S(2)}, u32[]{:S(2)}) collective-permute-start(bf16[32,512]{1,0:T(8,128)(2,1)S(1)} %copy.82), channel_id=1, source_target_pairs={{0,2},{1,3},{2,0},{3,1},{4,6},{5,7},{6,4},{7,5},{8,10},{9,11},{10,... | collective-permute-start | bytes 98312 | tf_op jit(solution)/shard_map/ppermute | solution.py:33
  66.0 1.3 %collective-permute-start.12 = (bf16[32,512]{1,0:T(8,128)(2,1)S(1)}, bf16[32,512]{1,0:T(8,128)(2,1)S(1)}, u32[]{:S(2)}, u32[]{:S(2)}) collective-permute-start(bf16[32,512]{1,0:T(8,128)(2,1)S(1)} %copy.83), channel_id=1, source_target_pairs={{0,3},{1,0},{2,1},{3,2},{4,7},{5,4},{6,5},{7,6},{8,11},{9,8},{10,9... | collective-permute-start | bytes 98312 | tf_op jit(solution)/shard_map/ppermute | solution.py:33
  67.4 0.3 collective-permute-done.10
  67.7 1.9 %collective-permute-done.11 = bf16[32,512]{1,0:T(8,128)(2,1)S(1)} collective-permute-done((bf16[32,512]{1,0:T(8,128)(2,1)S(1)}, bf16[32,512]{1,0:T(8,128)(2,1)S(1)}, u32[]{:S(2)}, u32[]{:S(2)}) %collective-permute-start.11) | collective-permute-done | bytes 32800 | tf_op jit(solution)/shard_map/ppermute | solution.py:33
  69.6 0.4 collective-permute-done.12
  70.0 0.6 gather_fusion.1
  70.7 0.7 copy.85
  (61 shorter events, 1.5 us)
Async XLA Ops:
  1.1 15.3 %copy-start.4 = (f32[4,6,11]{2,0,1:T(4,128)S(1)}, f32[4,6,11]{2,0,1:T(4,128)}, u32[]{:S(2)}) copy-start(f32[4,6,11]{2,0,1:T(4,128)} %param.9) | copy-start | bytes 3172
  1.1 8.8 %collective-permute-start = (bf16[3,32,512]{2,1,0:T(8,128)(2,1)S(1)}, bf16[3,32,512]{2,1,0:T(8,128)(2,1)S(1)}, u32[]{:S(2)}, u32[]{:S(2)}) collective-permute-start(bf16[3,32,512]{2,1,0:T(8,128)(2,1)S(1)} %get-tuple-element.43), channel_id=1, source_target_pairs={{0,1},{1,2},{2,3},{3,0},{4,5},{5,6},{6,7},{7,4},{8,9},{9,10},{10,1... | collective-permute-start | bytes 294920 | tf_op jit(solution)/shard_map/ppermute | solution.py:33
  4.2 9.2 %collective-permute-start.1 = (bf16[3,32,512]{2,1,0:T(8,128)(2,1)S(1)}, bf16[3,32,512]{2,1,0:T(8,128)(2,1)S(1)}, u32[]{:S(2)}, u32[]{:S(2)}) collective-permute-start(bf16[3,32,512]{2,1,0:T(8,128)(2,1)S(1)} %get-tuple-element.42), channel_id=1, source_target_pairs={{0,2},{1,3},{2,0},{3,1},{4,6},{5,7},{6,4},{7,5},{8,10},{9,11},{10,... | collective-permute-start | bytes 294920 | tf_op jit(solution)/shard_map/ppermute | solution.py:33
  6.8 6.6 %collective-permute-start.2 = (bf16[3,32,512]{2,1,0:T(8,128)(2,1)S(1)}, bf16[3,32,512]{2,1,0:T(8,128)(2,1)S(1)}, u32[]{:S(2)}, u32[]{:S(2)}) collective-permute-start(bf16[3,32,512]{2,1,0:T(8,128)(2,1)S(1)} %get-tuple-element.41), channel_id=1, source_target_pairs={{0,3},{1,0},{2,1},{3,2},{4,7},{5,4},{6,5},{7,6},{8,11},{9,8},{10,9... | collective-permute-start | bytes 294920 | tf_op jit(solution)/shard_map/ppermute | solution.py:33
  8.2 13.5 %copy-start.8 = (f32[4,4]{1,0:T(4,128)S(1)}, f32[4,4]{1,0:T(4,128)}, u32[]{:S(2)}) copy-start(f32[4,4]{1,0:T(4,128)} %param.10) | copy-start | bytes 196
  14.9 5.3 %collective-permute-start.3 = (bf16[1,128,512]{2,1,0:T(8,128)(2,1)S(1)}, bf16[1,128,512]{2,1,0:T(8,128)(2,1)S(1)}, u32[]{:S(2)}, u32[]{:S(2)}) collective-permute-start(bf16[1,128,512]{2,1,0:T(8,128)(2,1)S(1)} %bitcast.85), channel_id=1, source_target_pairs={{0,16},{4,20},{8,24},{12,28},{16,0},{20,4},{24,8},{28,12},{1,17},{... | collective-permute-start | bytes 393224 | tf_op jit(solution)/shard_map/ppermute | solution.py:47
  20.2 7.3 %collective-permute-start.4 = (bf16[2,128,512]{2,1,0:T(8,128)(2,1)S(1)}, bf16[2,128,512]{2,1,0:T(8,128)(2,1)S(1)}, u32[]{:S(2)}, u32[]{:S(2)}) collective-permute-start(bf16[2,128,512]{2,1,0:T(8,128)(2,1)S(1)} %maximum_select_fusion.4), channel_id=1, source_target_pairs={{0,8},{4,12},{8,0},{12,4},{16,24},{20,28},{24,16},{28,20},{1,9},{5... | collective-permute-start | bytes 786440 | tf_op jit(solution)/shard_map/ppermute | solution.py:47
  22.7 2.1 %collective-permute-start.9 = (bf16[5,512]{1,0:T(8,128)(2,1)S(1)}, bf16[5,512]{1,0:T(8,128)(2,1)S(1)}, u32[]{:S(2)}, u32[]{:S(2)}) collective-permute-start(bf16[5,512]{1,0:T(8,128)(2,1)S(1)} %slice.270), channel_id=1, source_target_pairs={{0,4},{4,8},{8,12},{12,16},{16,20},{20,24},{24,28},{1,5},{5,9},{9,... | collective-permute-start | bytes 15368 | tf_op jit(solution)/shard_map/ppermute | solution.py:23
  27.5 2.0 %collective-permute-start.5 = (bf16[4,128,512]{2,1,0:T(8,128)(2,1)S(1)}, bf16[4,128,512]{2,1,0:T(8,128)(2,1)S(1)}, u32[]{:S(2)}, u32[]{:S(2)}) collective-permute-start(bf16[4,128,512]{2,1,0:T(8,128)(2,1)S(1)} %maximum_select_fusion.2), channel_id=1, source_target_pairs={{0,4},{4,0},{8,12},{12,8},{16,20},{20,16},{24,28},{28,24},{1,5},{5... | collective-permute-start | bytes 1572872 | tf_op jit(solution)/shard_map/ppermute | solution.py:47
  27.8 2.0 %copy-start.1 = (bf16[128,4,6,128]{0,3,2,1:T(8,128)(2,1)}, bf16[128,4,6,128]{0,3,2,1:T(8,128)(2,1)S(1)}, u32[]{:S(2)}) copy-start(bf16[128,4,6,128]{0,3,2,1:T(8,128)(2,1)S(1)} %constant_dynamic-update-slice_fusion) | copy-start | bytes 2359300
  29.8 1.0 %copy-start = (bf16[2,2,2,128,512]{4,3,2,1,0:T(8,128)(2,1)}, bf16[2,2,2,128,512]{4,3,2,1,0:T(8,128)(2,1)S(1)}, u32[]{:S(2)}) copy-start(bf16[2,2,2,128,512]{4,3,2,1,0:T(8,128)(2,1)S(1)} %copy.62) | copy-start | bytes 3145732
  29.9 1.3 %copy-start.3 = (bf16[128,4,128]{2,1,0:T(4,128)(2,1)S(1)}, bf16[128,4,128]{2,1,0:T(4,128)(2,1)}, u32[]{:S(2)}) copy-start(bf16[128,4,128]{2,1,0:T(4,128)(2,1)} %concatenate.63) | copy-start | bytes 393220
  30.9 1.6 %copy-start.2 = (bf16[1,4,32,512]{3,2,0,1:T(8,128)(2,1)S(1)}, bf16[1,4,32,512]{3,2,0,1:T(8,128)(2,1)}, u32[]{:S(2)}) copy-start(bf16[1,4,32,512]{3,2,0,1:T(8,128)(2,1)} %get-tuple-element.38) | copy-start | bytes 393220
  32.5 14.7 %collective-permute-start.6 = (bf16[1,128,512]{2,1,0:T(8,128)(2,1)S(1)}, bf16[1,128,512]{2,1,0:T(8,128)(2,1)S(1)}, u32[]{:S(2)}, u32[]{:S(2)}) collective-permute-start(bf16[1,128,512]{2,1,0:T(8,128)(2,1)S(1)} %bitcast.83), channel_id=1, source_target_pairs={{0,16},{4,20},{8,24},{12,28},{16,0},{20,4},{24,8},{28,12},{1,17},{... | collective-permute-start | bytes 393224 | tf_op jit(solution)/shard_map/ppermute | solution.py:47
  35.9 11.3 %copy-start.5 = (pred[1024,128]{1,0:T(8,128)(4,1)S(1)}, pred[1024,128]{1,0:T(8,128)(4,1)}, u32[]{:S(2)}) copy-start(pred[1024,128]{1,0:T(8,128)(4,1)} %get-tuple-element.64) | copy-start | bytes 393220
  35.9 11.3 %copy-start.6 = (pred[1024,128]{1,0:T(8,128)(4,1)S(1)}, pred[1024,128]{1,0:T(8,128)(4,1)}, u32[]{:S(2)}) copy-start(pred[1024,128]{1,0:T(8,128)(4,1)} %get-tuple-element.65) | copy-start | bytes 393220
  36.0 11.3 %copy-start.7 = (pred[1024,128]{1,0:T(8,128)(4,1)S(1)}, pred[1024,128]{1,0:T(8,128)(4,1)}, u32[]{:S(2)}) copy-start(pred[1024,128]{1,0:T(8,128)(4,1)} %get-tuple-element.66) | copy-start | bytes 393220
  47.2 8.1 %collective-permute-start.7 = (bf16[2,128,512]{2,1,0:T(8,128)(2,1)S(1)}, bf16[2,128,512]{2,1,0:T(8,128)(2,1)S(1)}, u32[]{:S(2)}, u32[]{:S(2)}) collective-permute-start(bf16[2,128,512]{2,1,0:T(8,128)(2,1)S(1)} %maximum_select_fusion.5), channel_id=1, source_target_pairs={{0,8},{4,12},{8,0},{12,4},{16,24},{20,28},{24,16},{28,20},{1,9},{5... | collective-permute-start | bytes 786440 | tf_op jit(solution)/shard_map/ppermute | solution.py:47
  55.4 2.0 %collective-permute-start.8 = (bf16[4,128,512]{2,1,0:T(8,128)(2,1)S(1)}, bf16[4,128,512]{2,1,0:T(8,128)(2,1)S(1)}, u32[]{:S(2)}, u32[]{:S(2)}) collective-permute-start(bf16[4,128,512]{2,1,0:T(8,128)(2,1)S(1)} %maximum_select_fusion.3), channel_id=1, source_target_pairs={{0,4},{4,0},{8,12},{12,8},{16,20},{20,16},{24,28},{28,24},{1,5},{5... | collective-permute-start | bytes 1572872 | tf_op jit(solution)/shard_map/ppermute | solution.py:47
  59.3 2.1 %copy-start.9 = (f32[512]{0:T(512)S(1)}, f32[512]{0:T(512)}, u32[]{:S(2)}) copy-start(f32[512]{0:T(512)} %param.11) | copy-start | bytes 6148
  61.9 5.8 %collective-permute-start.10 = (bf16[32,512]{1,0:T(8,128)(2,1)S(1)}, bf16[32,512]{1,0:T(8,128)(2,1)S(1)}, u32[]{:S(2)}, u32[]{:S(2)}) collective-permute-start(bf16[32,512]{1,0:T(8,128)(2,1)S(1)} %copy.81), channel_id=1, source_target_pairs={{0,1},{1,2},{2,3},{3,0},{4,5},{5,6},{6,7},{7,4},{8,9},{9,10},{10,1... | collective-permute-start | bytes 98312 | tf_op jit(solution)/shard_map/ppermute | solution.py:33
  64.7 4.9 %collective-permute-start.11 = (bf16[32,512]{1,0:T(8,128)(2,1)S(1)}, bf16[32,512]{1,0:T(8,128)(2,1)S(1)}, u32[]{:S(2)}, u32[]{:S(2)}) collective-permute-start(bf16[32,512]{1,0:T(8,128)(2,1)S(1)} %copy.82), channel_id=1, source_target_pairs={{0,2},{1,3},{2,0},{3,1},{4,6},{5,7},{6,4},{7,5},{8,10},{9,11},{10,... | collective-permute-start | bytes 98312 | tf_op jit(solution)/shard_map/ppermute | solution.py:33
  66.0 4.0 %collective-permute-start.12 = (bf16[32,512]{1,0:T(8,128)(2,1)S(1)}, bf16[32,512]{1,0:T(8,128)(2,1)S(1)}, u32[]{:S(2)}, u32[]{:S(2)}) collective-permute-start(bf16[32,512]{1,0:T(8,128)(2,1)S(1)} %copy.83), channel_id=1, source_target_pairs={{0,3},{1,0},{2,1},{3,2},{4,7},{5,4},{6,5},{7,6},{8,11},{9,8},{10,9... | collective-permute-start | bytes 98312 | tf_op jit(solution)/shard_map/ppermute | solution.py:33

commit v23 on v15

--- a/solution.py
+++ b/solution.py
@@ -253,9 +253,9 @@
     gain_local = head_gain.reshape(heads, head_dim)
     attended = normalize(weighted, gain_local)
     block_rows = shard_rows // groups
+    attended = attended.reshape((groups, block_rows, -1))
     returned = exchanged(
-        lambda group: lax.dynamic_slice_in_dim(attended, group * block_rows, block_rows, 0),
-        "uly",
+        lambda group: lax.dynamic_index_in_dim(attended, group, 0, keepdims=False), "uly"
     )
     return jnp.moveaxis(returned, 0, 1).reshape((block_rows, -1))
 

time: 71.6 us -> 71.3 us (level)
  no operation moved by 1% of the time
where the time goes in v23:
time: 71.3 us; the launch traced here: 71.1 us
  starting transfers between devices  20.8 us (29%)
  waiting for transfers between devices  16.9 us (24%)
  local copies, waits for them, and re-layouts  11.3 us (16%)
  Pallas kernels  10.9 us (15%)
  other arithmetic  8.44 us (12%)
  matrix products  2.13 us (3%)
    ppermute x6, starting transfers between devices, exchanged(): received.append(lax.ppermute(outgoing, axis, pairs))  12.2 us
    pallas_call x1, Pallas kernels, conv_logits(): pl.pallas_call(logits_kernel, grid=(heads, seq_len // span), in_specs=[pl...  10.9 us
    ppermute x6, waiting for transfers between devices, gathered(): incoming = lax.ppermute(held, axis, [(i, i ^ bit) for i in range(peers)])  10.1 us
    ppermute x6, starting transfers between devices, gathered(): incoming = lax.ppermute(held, axis, [(i, i ^ bit) for i in range(peers)])  7.37 us
    ppermute x6, waiting for transfers between devices, exchanged(): received.append(lax.ppermute(outgoing, axis, pairs))  6.83 us
    div x1, other arithmetic, attend_chunk(): probabilities = expd / jnp.sum(expd, axis=1, keepdims=True)  3.88 us
    dot_general x1, matrix products, attend_chunk(): jnp.einsum('hki,khd->ihd', mixed_probs, value_heads, preferred_element_ty...  2.13 us
  transfers between devices with their start and end apart: 13, of which 9 were waited for; matrix products, arithmetic and copies ran while one was open for 15% of the time, Pallas kernels for 15%

profile of v23, /device:TPU:0, one launch (start us, length us, event | category | flops | bytes accessed | tf_op | source)
XLA Modules:
  0.0 71.1 jit_solution(11543477713862076411)
XLA Ops:
  0.0 1.1 %pad_maximum_fusion = bf16[3,32,2048]{2,1,0:T(8,128)(2,1)S(1)} fusion(bf16[1,32,2048]{2,1,0:T(8,128)(2,1)} %bitcast.95, bf16[1,32,2048]{2,1,0:T(8,128)(2,1)} %bitcast.96, bf16[1,32,2048]{2,1,0:T(8,128)(2,1)} %bitcast.97), kind=kLoop, calls=%fused_computation.40 | loop fusion | flops 393216 | bytes 786432 | tf_op jit(solution)/shard_map/stack | solution.py:199
  1.1 3.1 %collective-permute-start = (bf16[3,32,512]{2,1,0:T(8,128)(2,1)S(1)}, bf16[3,32,512]{2,1,0:T(8,128)(2,1)S(1)}, u32[]{:S(2)}, u32[]{:S(2)}) collective-permute-start(bf16[3,32,512]{2,1,0:T(8,128)(2,1)S(1)} %get-tuple-element.43), channel_id=1, source_target_pairs={{0,1},{1,2},{2,3},{3,0},{4,5},{5,6},{6,7},{7,4},{8,9},{9,10},{10,1... | collective-permute-start | bytes 294920 | tf_op jit(solution)/shard_map/ppermute | solution.py:33
  4.2 2.6 %collective-permute-start.1 = (bf16[3,32,512]{2,1,0:T(8,128)(2,1)S(1)}, bf16[3,32,512]{2,1,0:T(8,128)(2,1)S(1)}, u32[]{:S(2)}, u32[]{:S(2)}) collective-permute-start(bf16[3,32,512]{2,1,0:T(8,128)(2,1)S(1)} %get-tuple-element.42), channel_id=1, source_target_pairs={{0,2},{1,3},{2,0},{3,1},{4,6},{5,7},{6,4},{7,5},{8,10},{9,11},{10,... | collective-permute-start | bytes 294920 | tf_op jit(solution)/shard_map/ppermute | solution.py:33
  6.8 1.3 %collective-permute-start.2 = (bf16[3,32,512]{2,1,0:T(8,128)(2,1)S(1)}, bf16[3,32,512]{2,1,0:T(8,128)(2,1)S(1)}, u32[]{:S(2)}, u32[]{:S(2)}) collective-permute-start(bf16[3,32,512]{2,1,0:T(8,128)(2,1)S(1)} %get-tuple-element.41), channel_id=1, source_target_pairs={{0,3},{1,0},{2,1},{3,2},{4,7},{5,4},{6,5},{7,6},{8,11},{9,8},{10,9... | collective-permute-start | bytes 294920 | tf_op jit(solution)/shard_map/ppermute | solution.py:33
  8.2 1.2 %fusion.15 = (pred[1024,128]{1,0:T(8,128)(4,1)}, pred[1024,128]{1,0:T(8,128)(4,1)}, pred[1024,128]{1,0:T(8,128)(4,1)}, pred[1024,128]{1,0:T(8,128)(4,1)}, pred[1...) fusion(s32[128]{0:T(128)S(1)} %iota_add_fusion), kind=kLoop, calls=%fused_computation.39 | loop fusion | flops 917504 | bytes 786944 | tf_op jit(solution)/shard_map/ge | solution.py:175
  9.5 0.4 collective-permute-done
  9.9 3.5 %collective-permute-done.1 = bf16[3,32,512]{2,1,0:T(8,128)(2,1)S(1)} collective-permute-done((bf16[3,32,512]{2,1,0:T(8,128)(2,1)S(1)}, bf16[3,32,512]{2,1,0:T(8,128)(2,1)S(1)}, u32[]{:S(2)}, u32[]{:S(2)}) %collective-permute-start.1) | collective-permute-done | bytes 98336 | tf_op jit(solution)/shard_map/ppermute | solution.py:33
  13.5 0.6 gather_fusion
  14.1 0.1 select_bitcast_fusion
  14.2 0.7 fusion.55
  14.9 1.5 %collective-permute-start.3 = (bf16[1,128,512]{2,1,0:T(8,128)(2,1)S(1)}, bf16[1,128,512]{2,1,0:T(8,128)(2,1)S(1)}, u32[]{:S(2)}, u32[]{:S(2)}) collective-permute-start(bf16[1,128,512]{2,1,0:T(8,128)(2,1)S(1)} %bitcast.88), channel_id=1, source_target_pairs={{0,16},{4,20},{8,24},{12,28},{16,0},{20,4},{24,8},{28,12},{1,17},{... | collective-permute-start | bytes 393224 | tf_op jit(solution)/shard_map/ppermute | solution.py:47
  16.4 0.4 slice_reduce_fusion.17
  16.8 3.4 %collective-permute-done.3 = bf16[1,128,512]{2,1,0:T(8,128)(2,1)S(1)} collective-permute-done((bf16[1,128,512]{2,1,0:T(8,128)(2,1)S(1)}, bf16[1,128,512]{2,1,0:T(8,128)(2,1)S(1)}, u32[]{:S(2)}, u32[]{:S(2)}) %collective-permute-start.3) | collective-permute-done | bytes 131104 | tf_op jit(solution)/shard_map/ppermute | solution.py:47
  20.2 1.6 %collective-permute-start.4 = (bf16[2,128,512]{2,1,0:T(8,128)(2,1)S(1)}, bf16[2,128,512]{2,1,0:T(8,128)(2,1)S(1)}, u32[]{:S(2)}, u32[]{:S(2)}) collective-permute-start(bf16[2,128,512]{2,1,0:T(8,128)(2,1)S(1)} %maximum_select_fusion.4), channel_id=1, source_target_pairs={{0,8},{4,12},{8,0},{12,4},{16,24},{20,28},{24,16},{28,20},{1,9},{5... | collective-permute-start | bytes 786440 | tf_op jit(solution)/shard_map/ppermute | solution.py:47
  21.7 0.8 %slice_reduce_fusion.18 = (f32[4]{0:T(128)}, f32[4]{0:T(128)}, f32[4]{0:T(128)}, f32[4]{0:T(128)}) fusion(f32[1,4,4]{2,1,0:T(4,128)S(1)} %bitcast.101), kind=kLoop, calls=%fused_computation.136 | loop fusion | bytes 128 | tf_op jit(solution)/shard_map/slice | solution.py:183
  22.5 0.7 reshape.178.taps_ref
  23.2 1.3 %collective-permute-start.9 = (bf16[5,512]{1,0:T(8,128)(2,1)S(1)}, bf16[5,512]{1,0:T(8,128)(2,1)S(1)}, u32[]{:S(2)}, u32[]{:S(2)}) collective-permute-start(bf16[5,512]{1,0:T(8,128)(2,1)S(1)} %slice.270), channel_id=1, source_target_pairs={{0,4},{4,8},{8,12},{12,16},{16,20},{20,24},{24,28},{1,5},{5,9},{9,... | collective-permute-start | bytes 15368 | tf_op jit(solution)/shard_map/ppermute | solution.py:23
  24.6 0.1 copy.60
  24.7 0.7 concatenate.63
  25.4 0.1 pad_maximum_fusion.3
  25.5 0.1 copy.55
  25.6 0.1 copy.56
  25.8 0.1 copy.57
  25.9 0.1 copy.58
  26.0 0.1 copy.59
  26.2 1.3 %collective-permute-done.4 = bf16[2,128,512]{2,1,0:T(8,128)(2,1)S(1)} collective-permute-done((bf16[2,128,512]{2,1,0:T(8,128)(2,1)S(1)}, bf16[2,128,512]{2,1,0:T(8,128)(2,1)S(1)}, u32[]{:S(2)}, u32[]{:S(2)}) %collective-permute-start.4) | collective-permute-done | bytes 262176 | tf_op jit(solution)/shard_map/ppermute | solution.py:47
  27.8 1.8 %collective-permute-done.5 = bf16[4,128,512]{2,1,0:T(8,128)(2,1)S(1)} collective-permute-done((bf16[4,128,512]{2,1,0:T(8,128)(2,1)S(1)}, bf16[4,128,512]{2,1,0:T(8,128)(2,1)S(1)}, u32[]{:S(2)}, u32[]{:S(2)}) %collective-permute-start.5) | collective-permute-done | bytes 524320 | tf_op jit(solution)/shard_map/ppermute | solution.py:47
  29.5 0.2 maximum_select_fusion
  29.7 0.1 copy.52
  29.8 0.1 fusion.24
  29.9 0.1 fusion.56
  30.1 0.1 slice.221
  30.2 0.6 copy-done
  30.8 0.1 slice.225
  30.9 0.1 slice.231
  31.0 0.1 slice.239
  31.1 0.1 slice.249
  31.2 0.8 %fusion.21 = (f32[133,4]{1,0:T(8,128)S(1)}, f32[133,4]{1,0:T(8,128)S(1)}, f32[133,4]{1,0:T(8,128)S(1)}, f32[133,4]{1,0:T(8,128)S(1)}, f32[133,4]{1,0:T(8,128)S(1)}) fusion(f32[133,4,128]{2,1,0:T(4,128)S(1)} %slice.249, bf16[128,4,128]{2,1,0:T(4,128)(2,1)S(1)} %copy-done.3, bf16[5,4,128]{2,1,0:T(4,128)(2,1)S(1)} %concatenate.62, ...), kind=kLoop, calls=%fused_computation.52 | loop fusion | flops 814492 | bytes 1508752 | tf_op jit(solution)/shard_map/reduce_sum | solution.py:150
  32.1 0.1 copy.64
  32.2 0.1 copy.62
  32.3 0.1 copy.63
  32.4 4.0 %collective-permute-start.6 = (bf16[1,128,512]{2,1,0:T(8,128)(2,1)S(1)}, bf16[1,128,512]{2,1,0:T(8,128)(2,1)S(1)}, u32[]{:S(2)}, u32[]{:S(2)}) collective-permute-start(bf16[1,128,512]{2,1,0:T(8,128)(2,1)S(1)} %bitcast.86), channel_id=1, source_target_pairs={{0,16},{4,20},{8,24},{12,28},{16,0},{20,4},{24,8},{28,12},{1,17},{... | collective-permute-start | bytes 393224 | tf_op jit(solution)/shard_map/ppermute | solution.py:47
  36.4 3.7 %collective-permute-done.6 = bf16[1,128,512]{2,1,0:T(8,128)(2,1)S(1)} collective-permute-done((bf16[1,128,512]{2,1,0:T(8,128)(2,1)S(1)}, bf16[1,128,512]{2,1,0:T(8,128)(2,1)S(1)}, u32[]{:S(2)}, u32[]{:S(2)}) %collective-permute-start.6) | collective-permute-done | bytes 131104 | tf_op jit(solution)/shard_map/ppermute | solution.py:47
  40.2 0.1 collective-permute-start.7
  40.5 10.9 %shard_map.64 = f32[4,1024,128]{2,1,0:T(8,128)} custom-call(f32[264]{0:T(512)} %reshape.178.taps_ref, bf16[4,768,128]{2,1,0:T(8,128)(2,1)} %bitcast.85, bf16[1024,512]{1,0:T(8,128)(2,1)} %bitcast.80), custom_call_target="tpu_custom_call" | custom-call | tf_op jit(solution)/shard_map/pallas_call | solution.py:122
  51.4 0.1 fusion.44
  51.5 0.1 maximum_select_fusion.3
  51.6 3.9 %divide_bitcast_fusion = f32[1,4,1024,128]{3,2,1,0:T(8,128)S(1)} fusion(f32[4,1024,128]{2,1,0:T(8,128)} %shard_map.64, f32[4,128]{1,0:T(4,128)S(1)} %get-tuple-element.60, f32[4,128]{1,0:T(4,128)S(1)} %get-tuple-element.59, f32[4,128]{1,0:T(4,128)S(1)} %get-tuple-element.58, f32[4,128]{1,0:T(4,128)S(1)} %subtract_bitcast_fusion.3, f32[4,128]{1,0:T(4,128)S(1)} %fusion.44, ...), kind=kOutput, calls=%fused_computation.5 | output fusion | flops 6818814 | bytes 4990976 | tf_op jit(solution)/shard_map/div | solution.py:178
  55.5 1.4 %slice_bitcast_fusion.3 = (f32[1024,128]{1,0:T(8,128)}, f32[1024,128]{1,0:T(8,128)}, f32[1024,128]{1,0:T(8,128)}, f32[1024,128]{1,0:T(8,128)}) fusion(f32[1,4,1024,128]{3,2,1,0:T(8,128)S(1)} %divide_bitcast_fusion), kind=kLoop, calls=%fused_computation.30 | loop fusion | bytes 4194304 | tf_op jit(solution)/shard_map/mul | solution.py:183
  56.9 0.2 maximum_select_fusion.1
  57.1 0.9 %copy.53 = bf16[2,2,2,128,512]{3,2,1,0,4:T(2,128)(2,1)S(1)} copy(bf16[2,2,2,128,512]{4,3,0,1,2:T(8,128)(2,1)S(1)} %bitcast.81) | data formatting | bytes 2097152 | tf_op jit(solution)/shard_map/transpose | solution.py:55
  58.1 0.8 %reshape_reshape.6 = bf16[1024,4,128]{0,2,1:T(8,128)(2,1)S(1)} reshape(bf16[2,2,2,128,512]{3,2,1,0,4:T(2,128)(2,1)S(1)} %copy.53) | data formatting | bytes 2097152 | tf_op jit(solution)/shard_map/reshape;reshape | solution.py:230
  58.9 0.2 copy-done.5
  59.1 2.1 %multiply_reduce_fusion = (f32[128,4]{0,1:T(4,128)S(1)}, f32[128,4,128]{0,2,1:T(8,128)S(1)}) fusion(bf16[1024,4,128]{0,2,1:T(8,128)(2,1)S(1)} %reshape_reshape.6, f32[1024,128]{1,0:T(8,128)S(1)} %copy-done.5, f32[4]{0:T(128)S(1)} %copy-done.12, f32[1024,128]{1,0:T(8,128)} %get-tuple-element.35, f32[4]{0:T(128)S(1)} %copy-done.13, ...), kind=kOutput, calls=%fused_computation.56 | convolution fusion | flops 138542592 | bytes 3409984 | tf_op jit(solution)/shard_map/hki,khd->ihd/dot_general | solution.py:185
  61.3 0.1 multiply_convert_fusion
  61.4 0.1 copy.66
  61.7 2.7 %collective-permute-start.10 = (bf16[32,512]{1,0:T(8,128)(2,1)S(1)}, bf16[32,512]{1,0:T(8,128)(2,1)S(1)}, u32[]{:S(2)}, u32[]{:S(2)}) collective-permute-start(bf16[32,512]{1,0:T(8,128)(2,1)S(1)} %get-tuple-element.57), channel_id=1, source_target_pairs={{0,1},{1,2},{2,3},{3,0},{4,5},{5,6},{6,7},{7,4},{8,9},{9,10},{10,1... | collective-permute-start | bytes 98312 | tf_op jit(solution)/shard_map/ppermute | solution.py:33
  64.4 1.2 %collective-permute-start.11 = (bf16[32,512]{1,0:T(8,128)(2,1)S(1)}, bf16[32,512]{1,0:T(8,128)(2,1)S(1)}, u32[]{:S(2)}, u32[]{:S(2)}) collective-permute-start(bf16[32,512]{1,0:T(8,128)(2,1)S(1)} %get-tuple-element.56), channel_id=1, source_target_pairs={{0,2},{1,3},{2,0},{3,1},{4,6},{5,7},{6,4},{7,5},{8,10},{9,11},{10,... | collective-permute-start | bytes 98312 | tf_op jit(solution)/shard_map/ppermute | solution.py:33
  65.6 1.3 %collective-permute-start.12 = (bf16[32,512]{1,0:T(8,128)(2,1)S(1)}, bf16[32,512]{1,0:T(8,128)(2,1)S(1)}, u32[]{:S(2)}, u32[]{:S(2)}) collective-permute-start(bf16[32,512]{1,0:T(8,128)(2,1)S(1)} %get-tuple-element.55), channel_id=1, source_target_pairs={{0,3},{1,0},{2,1},{3,2},{4,7},{5,4},{6,5},{7,6},{8,11},{9,8},{10,9... | collective-permute-start | bytes 98312 | tf_op jit(solution)/shard_map/ppermute | solution.py:33
  66.8 0.6 collective-permute-done.10
  67.4 2.1 %collective-permute-done.11 = bf16[32,512]{1,0:T(8,128)(2,1)S(1)} collective-permute-done((bf16[32,512]{1,0:T(8,128)(2,1)S(1)}, bf16[32,512]{1,0:T(8,128)(2,1)S(1)}, u32[]{:S(2)}, u32[]{:S(2)}) %collective-permute-start.11) | collective-permute-done | bytes 32800 | tf_op jit(solution)/shard_map/ppermute | solution.py:33
  69.6 0.1 collective-permute-done.12
  69.7 0.6 gather_fusion.1
  70.4 0.7 copy.69
  (67 shorter events, 1.2 us)
Async XLA Ops:
  1.1 15.3 %copy-start.6 = (f32[4,6,11]{2,0,1:T(4,128)S(1)}, f32[4,6,11]{2,0,1:T(4,128)}, u32[]{:S(2)}) copy-start(f32[4,6,11]{2,0,1:T(4,128)} %param.9) | copy-start | bytes 3172
  1.1 8.8 %collective-permute-start = (bf16[3,32,512]{2,1,0:T(8,128)(2,1)S(1)}, bf16[3,32,512]{2,1,0:T(8,128)(2,1)S(1)}, u32[]{:S(2)}, u32[]{:S(2)}) collective-permute-start(bf16[3,32,512]{2,1,0:T(8,128)(2,1)S(1)} %get-tuple-element.43), channel_id=1, source_target_pairs={{0,1},{1,2},{2,3},{3,0},{4,5},{5,6},{6,7},{7,4},{8,9},{9,10},{10,1... | collective-permute-start | bytes 294920 | tf_op jit(solution)/shard_map/ppermute | solution.py:33
  4.2 9.2 %collective-permute-start.1 = (bf16[3,32,512]{2,1,0:T(8,128)(2,1)S(1)}, bf16[3,32,512]{2,1,0:T(8,128)(2,1)S(1)}, u32[]{:S(2)}, u32[]{:S(2)}) collective-permute-start(bf16[3,32,512]{2,1,0:T(8,128)(2,1)S(1)} %get-tuple-element.42), channel_id=1, source_target_pairs={{0,2},{1,3},{2,0},{3,1},{4,6},{5,7},{6,4},{7,5},{8,10},{9,11},{10,... | collective-permute-start | bytes 294920 | tf_op jit(solution)/shard_map/ppermute | solution.py:33
  6.8 6.6 %collective-permute-start.2 = (bf16[3,32,512]{2,1,0:T(8,128)(2,1)S(1)}, bf16[3,32,512]{2,1,0:T(8,128)(2,1)S(1)}, u32[]{:S(2)}, u32[]{:S(2)}) collective-permute-start(bf16[3,32,512]{2,1,0:T(8,128)(2,1)S(1)} %get-tuple-element.41), channel_id=1, source_target_pairs={{0,3},{1,0},{2,1},{3,2},{4,7},{5,4},{6,5},{7,6},{8,11},{9,8},{10,9... | collective-permute-start | bytes 294920 | tf_op jit(solution)/shard_map/ppermute | solution.py:33
  8.2 13.5 %copy-start.7 = (f32[4,4]{1,0:T(4,128)S(1)}, f32[4,4]{1,0:T(4,128)}, u32[]{:S(2)}) copy-start(f32[4,4]{1,0:T(4,128)} %param.10) | copy-start | bytes 196
  9.5 15.1 %copy-start.9 = (pred[4]{0:T(512)(128)(4,1)}, pred[4]{0:T(512)(128)(4,1)S(1)}, u32[]{:S(2)}) copy-start(pred[4]{0:T(512)(128)(4,1)S(1)} %compare_and_fusion) | copy-start | bytes 16
  14.9 5.3 %collective-permute-start.3 = (bf16[1,128,512]{2,1,0:T(8,128)(2,1)S(1)}, bf16[1,128,512]{2,1,0:T(8,128)(2,1)S(1)}, u32[]{:S(2)}, u32[]{:S(2)}) collective-permute-start(bf16[1,128,512]{2,1,0:T(8,128)(2,1)S(1)} %bitcast.88), channel_id=1, source_target_pairs={{0,16},{4,20},{8,24},{12,28},{16,0},{20,4},{24,8},{28,12},{1,17},{... | collective-permute-start | bytes 393224 | tf_op jit(solution)/shard_map/ppermute | solution.py:47
  20.2 7.3 %collective-permute-start.4 = (bf16[2,128,512]{2,1,0:T(8,128)(2,1)S(1)}, bf16[2,128,512]{2,1,0:T(8,128)(2,1)S(1)}, u32[]{:S(2)}, u32[]{:S(2)}) collective-permute-start(bf16[2,128,512]{2,1,0:T(8,128)(2,1)S(1)} %maximum_select_fusion.4), channel_id=1, source_target_pairs={{0,8},{4,12},{8,0},{12,4},{16,24},{20,28},{24,16},{28,20},{1,9},{5... | collective-permute-start | bytes 786440 | tf_op jit(solution)/shard_map/ppermute | solution.py:47
  23.2 2.1 %collective-permute-start.9 = (bf16[5,512]{1,0:T(8,128)(2,1)S(1)}, bf16[5,512]{1,0:T(8,128)(2,1)S(1)}, u32[]{:S(2)}, u32[]{:S(2)}) collective-permute-start(bf16[5,512]{1,0:T(8,128)(2,1)S(1)} %slice.270), channel_id=1, source_target_pairs={{0,4},{4,8},{8,12},{12,16},{16,20},{20,24},{24,28},{1,5},{5,9},{9,... | collective-permute-start | bytes 15368 | tf_op jit(solution)/shard_map/ppermute | solution.py:23
  27.5 2.0 %collective-permute-start.5 = (bf16[4,128,512]{2,1,0:T(8,128)(2,1)S(1)}, bf16[4,128,512]{2,1,0:T(8,128)(2,1)S(1)}, u32[]{:S(2)}, u32[]{:S(2)}) collective-permute-start(bf16[4,128,512]{2,1,0:T(8,128)(2,1)S(1)} %maximum_select_fusion.2), channel_id=1, source_target_pairs={{0,4},{4,0},{8,12},{12,8},{16,20},{20,16},{24,28},{28,24},{1,5},{5... | collective-permute-start | bytes 1572872 | tf_op jit(solution)/shard_map/ppermute | solution.py:47
  27.8 2.0 %copy-start.1 = (bf16[128,4,6,128]{0,3,2,1:T(8,128)(2,1)}, bf16[128,4,6,128]{0,3,2,1:T(8,128)(2,1)S(1)}, u32[]{:S(2)}) copy-start(bf16[128,4,6,128]{0,3,2,1:T(8,128)(2,1)S(1)} %constant_dynamic-update-slice_fusion) | copy-start | bytes 2359300
  29.8 1.0 %copy-start = (bf16[2,2,2,128,512]{4,3,2,1,0:T(8,128)(2,1)}, bf16[2,2,2,128,512]{4,3,2,1,0:T(8,128)(2,1)S(1)}, u32[]{:S(2)}) copy-start(bf16[2,2,2,128,512]{4,3,2,1,0:T(8,128)(2,1)S(1)} %copy.52) | copy-start | bytes 3145732
  29.9 1.3 %copy-start.3 = (bf16[128,4,128]{2,1,0:T(4,128)(2,1)S(1)}, bf16[128,4,128]{2,1,0:T(4,128)(2,1)}, u32[]{:S(2)}) copy-start(bf16[128,4,128]{2,1,0:T(4,128)(2,1)} %concatenate.63) | copy-start | bytes 393220
  30.8 1.6 %copy-start.2 = (bf16[1,4,32,512]{3,2,0,1:T(8,128)(2,1)S(1)}, bf16[1,4,32,512]{3,2,0,1:T(8,128)(2,1)}, u32[]{:S(2)}) copy-start(bf16[1,4,32,512]{3,2,0,1:T(8,128)(2,1)} %get-tuple-element.38) | copy-start | bytes 393220
  32.4 7.8 %collective-permute-start.6 = (bf16[1,128,512]{2,1,0:T(8,128)(2,1)S(1)}, bf16[1,128,512]{2,1,0:T(8,128)(2,1)S(1)}, u32[]{:S(2)}, u32[]{:S(2)}) collective-permute-start(bf16[1,128,512]{2,1,0:T(8,128)(2,1)S(1)} %bitcast.86), channel_id=1, source_target_pairs={{0,16},{4,20},{8,24},{12,28},{16,0},{20,4},{24,8},{28,12},{1,17},{... | collective-permute-start | bytes 393224 | tf_op jit(solution)/shard_map/ppermute | solution.py:47
  40.2 11.3 %collective-permute-start.7 = (bf16[2,128,512]{2,1,0:T(8,128)(2,1)S(1)}, bf16[2,128,512]{2,1,0:T(8,128)(2,1)S(1)}, u32[]{:S(2)}, u32[]{:S(2)}) collective-permute-start(bf16[2,128,512]{2,1,0:T(8,128)(2,1)S(1)} %maximum_select_fusion.5), channel_id=1, source_target_pairs={{0,8},{4,12},{8,0},{12,4},{16,24},{20,28},{24,16},{28,20},{1,9},{5... | collective-permute-start | bytes 786440 | tf_op jit(solution)/shard_map/ppermute | solution.py:47
  51.6 5.4 %collective-permute-start.8 = (bf16[4,128,512]{2,1,0:T(8,128)(2,1)S(1)}, bf16[4,128,512]{2,1,0:T(8,128)(2,1)S(1)}, u32[]{:S(2)}, u32[]{:S(2)}) collective-permute-start(bf16[4,128,512]{2,1,0:T(8,128)(2,1)S(1)} %maximum_select_fusion.3), channel_id=1, source_target_pairs={{0,4},{4,0},{8,12},{12,8},{16,20},{20,16},{24,28},{28,24},{1,5},{5... | collective-permute-start | bytes 1572872 | tf_op jit(solution)/shard_map/ppermute | solution.py:47
  57.1 1.8 %copy-start.4 = (f32[1024,128]{1,0:T(8,128)S(1)}, f32[1024,128]{1,0:T(8,128)}, u32[]{:S(2)}) copy-start(f32[1024,128]{1,0:T(8,128)} %get-tuple-element.33) | copy-start | bytes 1572868
  57.1 1.8 %copy-start.11 = (f32[4]{0:T(128)S(1)}, f32[4]{0:T(128)}, u32[]{:S(2)}) copy-start(f32[4]{0:T(128)} %get-tuple-element.29) | copy-start | bytes 52
  57.1 1.8 %copy-start.12 = (f32[4]{0:T(128)S(1)}, f32[4]{0:T(128)}, u32[]{:S(2)}) copy-start(f32[4]{0:T(128)} %get-tuple-element.30) | copy-start | bytes 52
  57.1 1.8 %copy-start.13 = (f32[4]{0:T(128)S(1)}, f32[4]{0:T(128)}, u32[]{:S(2)}) copy-start(f32[4]{0:T(128)} %get-tuple-element.31) | copy-start | bytes 52
  58.1 1.1 %copy-start.5 = (f32[1024,128]{1,0:T(8,128)S(1)}, f32[1024,128]{1,0:T(8,128)}, u32[]{:S(2)}) copy-start(f32[1024,128]{1,0:T(8,128)} %get-tuple-element.34) | copy-start | bytes 1572868
  58.1 1.0 %copy-start.14 = (f32[4]{0:T(128)S(1)}, f32[4]{0:T(128)}, u32[]{:S(2)}) copy-start(f32[4]{0:T(128)} %get-tuple-element.32) | copy-start | bytes 52
  59.1 2.1 %copy-start.8 = (f32[512]{0:T(512)S(1)}, f32[512]{0:T(512)}, u32[]{:S(2)}) copy-start(f32[512]{0:T(512)} %param.11) | copy-start | bytes 6148
  59.1 11.1 %copy-start.10 = (pred[4]{0:T(512)(128)(4,1)S(1)}, pred[4]{0:T(512)(128)(4,1)}, u32[]{:S(2)}) copy-start(pred[4]{0:T(512)(128)(4,1)} %copy-done.9) | copy-start | bytes 16
  61.7 5.8 %collective-permute-start.10 = (bf16[32,512]{1,0:T(8,128)(2,1)S(1)}, bf16[32,512]{1,0:T(8,128)(2,1)S(1)}, u32[]{:S(2)}, u32[]{:S(2)}) collective-permute-start(bf16[32,512]{1,0:T(8,128)(2,1)S(1)} %get-tuple-element.57), channel_id=1, source_target_pairs={{0,1},{1,2},{2,3},{3,0},{4,5},{5,6},{6,7},{7,4},{8,9},{9,10},{10,1... | collective-permute-start | bytes 98312 | tf_op jit(solution)/shard_map/ppermute | solution.py:33
  64.4 5.2 %collective-permute-start.11 = (bf16[32,512]{1,0:T(8,128)(2,1)S(1)}, bf16[32,512]{1,0:T(8,128)(2,1)S(1)}, u32[]{:S(2)}, u32[]{:S(2)}) collective-permute-start(bf16[32,512]{1,0:T(8,128)(2,1)S(1)} %get-tuple-element.56), channel_id=1, source_target_pairs={{0,2},{1,3},{2,0},{3,1},{4,6},{5,7},{6,4},{7,5},{8,10},{9,11},{10,... | collective-permute-start | bytes 98312 | tf_op jit(solution)/shard_map/ppermute | solution.py:33
  65.6 4.1 %collective-permute-start.12 = (bf16[32,512]{1,0:T(8,128)(2,1)S(1)}, bf16[32,512]{1,0:T(8,128)(2,1)S(1)}, u32[]{:S(2)}, u32[]{:S(2)}) collective-permute-start(bf16[32,512]{1,0:T(8,128)(2,1)S(1)} %get-tuple-element.55), channel_id=1, source_target_pairs={{0,3},{1,0},{2,1},{3,2},{4,7},{5,4},{6,5},{7,6},{8,11},{9,8},{10,9... | collective-permute-start | bytes 98312 | tf_op jit(solution)/shard_map/ppermute | solution.py:33
